TPU v7x, 32 devices: a whole 2x2x4 slice. The times are simulated.
32 devices in a mesh: cohort: 2 (over x), row: 16 (over z, y, core).
Axes of the slice: x: 2, y: 2, z: 4, core: 2. Of those that a mesh axis runs over, the one named last changes fastest.
Arguments:
- embeddings: bfloat16 [192, 16384], P(None, ('cohort', 'row')), parts along dimension 1, may hold values from -0.4375 to 0.4375
- local_scale: bfloat16 [16384], P(('cohort', 'row')), parts along dimension 0, may hold values from 0.69921875 to 2
- degree_scale: float32 [16384], P(('cohort', 'row')), parts along dimension 0, may hold values from 0.5 to 2
- lanczos_block: float32 [16, 16384], P(None, ('cohort', 'row')), parts along dimension 1, may hold values from -25 to 25
- previous_block: float32 [16, 16384], P(None, ('cohort', 'row')), parts along dimension 1, may hold values from -6 to 6
- previous_coupling: float32 [32, 16], P('cohort'), parts along dimension 0, may hold values from -1.5 to 1.5
- tile_plan: int32 [128, 2], P(('cohort', 'row')), parts along dimension 0, may hold values from 0 to 7, as said below
- tile_counts: int32 [32], P(('cohort', 'row')), parts along dimension 0, may hold values from 0 to 4, as said below
Outputs:
- result: float32 [16, 16384], P(None, ('cohort', 'row')), parts along dimension 1
- coupling: float32 [32, 16], P('cohort'), parts along dimension 0
There are 2 independent parts, one for each index of `cohort`. A program takes and returns all parts, laid end to end along the dimension named above; each array names one. Nothing has to cross between parts.
Inputs may be any that keep to these rules, and one draw needn't show every extreme that they name: Device d's rows of tile_plan (rows d * 4 to d * 4 + 3) start with tile_counts[d] live block pairs, each with row block no larger than column block; all live pairs over all devices are distinct; every other row holds one and the same pair, with row block no larger than column block, that is live on no device. `tile_counts`: the counts sum to 27; some device holds exactly 4.
All inputs are finite; a program needn't handle non-finite values.
Results may differ from a plain program's by a relative error of at most 0.002.
Values may be sent and summed in bfloat16 or wider, within the bound.
No kernel may reach another device: no remote copies, remote signals or barrier semaphores. Data moves between devices by JAX's collectives and lax.ppermute only.
A program may use at most 64 MiB of HBM per device.

v0:
```python
import math

import jax
import jax.numpy as jnp
from jax import lax
from jax.sharding import PartitionSpec as P

LANCZOS = 16
BLK = 1024


HIGHEST = lax.Precision.HIGHEST


def affinity(left_x, left_width, right_x, right_width):
    inner_prod = lax.dot_general(
        left_x, right_x, (((0,), (0,)), ((), ())), preferred_element_type=jnp.float32
    )
    left_norm = jnp.sum(jnp.square(left_x.astype(jnp.float32)), axis=0)
    right_norm = jnp.sum(jnp.square(right_x.astype(jnp.float32)), axis=0)
    distance = left_norm[:, None] + right_norm[None, :] - 2.0 * inner_prod
    spread = left_width.astype(jnp.float32)[:, None] * right_width.astype(jnp.float32)[None, :]
    return jnp.exp(-distance / spread).astype(jnp.bfloat16)


def tile_terms(totals, all_x, all_width, all_lanes, row_block, col_block):
    row_start = row_block * BLK
    col_start = col_block * BLK
    left_x = lax.dynamic_slice_in_dim(all_x, row_start, BLK, 1)
    right_x = lax.dynamic_slice_in_dim(all_x, col_start, BLK, 1)
    left_width = lax.dynamic_slice_in_dim(all_width, row_start, BLK, 0)
    right_width = lax.dynamic_slice_in_dim(all_width, col_start, BLK, 0)
    left_lanes = lax.dynamic_slice_in_dim(all_lanes, row_start, BLK, 1)
    right_lanes = lax.dynamic_slice_in_dim(all_lanes, col_start, BLK, 1)
    weights = affinity(left_x, left_width, right_x, right_width)
    to_rows = lax.dot_general(
        right_lanes, weights, (((1,), (1,)), ((), ())), preferred_element_type=jnp.float32
    )
    to_cols = lax.dot_general(
        left_lanes, weights, (((1,), (0,)), ((), ())), preferred_element_type=jnp.float32
    )
    apart = (row_block != col_block).astype(jnp.float32)
    current = lax.dynamic_slice_in_dim(totals, row_start, BLK, 1)
    totals = lax.dynamic_update_slice_in_dim(totals, current + to_rows, row_start, 1)
    current = lax.dynamic_slice_in_dim(totals, col_start, BLK, 1)
    return lax.dynamic_update_slice_in_dim(totals, current + apart * to_cols, col_start, 1)


def shards(
    embeddings,
    local_scale,
    degree_scale,
    lanczos_block,
    previous_block,
    previous_coupling,
    tile_plan,
    tile_counts,
):
    own_rows = embeddings.shape[1]
    devices = lax.axis_size("row")
    total_rows = devices * own_rows
    weighted = (degree_scale[None, :] * lanczos_block).astype(jnp.bfloat16)
    all_x, all_width, all_lanes = (
        lax.all_gather(embeddings, "row", axis=1, tiled=True),
        lax.all_gather(local_scale, "row", axis=0, tiled=True),
        lax.all_gather(weighted, "row", axis=1, tiled=True),
    )
    totals = jnp.zeros((LANCZOS, all_x.shape[1]), jnp.float32)

    def own_step(turn, inner):
        entry = lax.dynamic_slice_in_dim(tile_plan, turn, 1, 0)[0]
        return tile_terms(inner, all_x, all_width, all_lanes, entry[0], entry[1])

    totals = lax.fori_loop(0, tile_counts[0], own_step, totals)
    summed = lax.psum_scatter(totals, "row", scatter_dimension=1, tiled=True)
    scaled = summed * (degree_scale[None, :] / math.sqrt(total_rows))
    partial_value = lax.dot_general(
        lanczos_block, scaled, (((1,), (1,)), ((), ())), precision=HIGHEST
    )
    coupling = lax.psum(partial_value, "row") / total_rows
    projected = lax.dot_general(
        coupling, lanczos_block, (((0,), (0,)), ((), ())), precision=HIGHEST
    )
    result = scaled - projected - jnp.dot(previous_coupling, previous_block, precision=HIGHEST)
    return (result, coupling)


def solution(mesh):
    in_specs = (
        P(None, ("cohort", "row")),
        P(("cohort", "row")),
        P(("cohort", "row")),
        P(None, ("cohort", "row")),
        P(None, ("cohort", "row")),
        P("cohort", None),
        P(("cohort", "row"), None),
        P(("cohort", "row")),
    )
    out_specs = (P(None, ("cohort", "row")), P("cohort", None))
    return jax.shard_map(shards, mesh=mesh, in_specs=in_specs, out_specs=out_specs, check_vma=False)
```

profile of v0, /device:TPU:0, one launch (start us, length us, event | category | flops | bytes accessed | tf_op | source)
XLA Modules:
  0.0 195.9 jit_solution(14362163972466927057)
XLA Ops:
  7.2 0.0 copy-start
  7.2 0.0 all-gather.3.cloned.1.call-start
  7.2 0.7 all-gather.3.cloned.1.call-update
  7.9 0.0 reduce-scatter.2.cloned.1.call-start
  8.0 0.7 reshape.23
  8.6 23.2 %all-gather = bf16[16,1,512]{2,1,0:T(2,128)(2,1)S(1)} all-gather(bf16[1,1,512]{2,1,0:T(2,128)(2,1)S(1)} %reshape.23), channel_id=1, replica_groups=mesh['cohort'=2,'row'=16] {'row'}, dimensions={0}, use_global_device_ids=true | all-gather | bytes 17408 | tf_op jit(solution)/shard_map/all_gather | solution.py:65
  31.8 0.1 reduce
  31.9 0.8 multiply_convert_fusion
  32.7 18.7 %all_gather.9 = bf16[16,8192]{1,0:T(8,128)(2,1)S(1)} all-gather(bf16[16,512]{1,0:T(8,128)(2,1)S(1)} %multiply_convert_fusion), channel_id=1, replica_groups=mesh['cohort'=2,'row'=16] {'row'}, dimensions={1}, use_global_device_ids=true | all-gather | bytes 278528 | tf_op jit(solution)/shard_map/all_gather | solution.py:66
  51.4 9.9 %all-gather.3.cloned.1.call-done = bf16[192,8192]{1,0:T(8,128)(2,1)} async-done(((bf16[192,512]{1,0:T(8,128)(2,1)}), bf16[192,8192]{1,0:T(8,128)(2,1)}) %all-gather.3.cloned.1.call-update) | async-done | bytes 3145744 | tf_op jit(solution)/shard_map/all_gather | solution.py:64
  61.3 0.0 copy-start.3
  61.3 0.0 copy-start.2
  61.3 0.0 copy-start.4
  61.3 39.4 %while.10 = (s32[]{:T(128)}, f32[16,8192]{1,0:T(8,128)S(1)}, s32[]{:T(128)}, s32[4,2]{0,1:T(2,128)}, bf16[16,8192]{1,0:T(8,128)(2,1)S(1)}, /*index=5*/bf16[192,8...) while((s32[]{:T(128)}, f32[16,8192]{1,0:T(8,128)S(1)}, ...), condition=%wide.region_3.0_spmd, body=%wide.region_0.0_spmd.sunk | while | flops 478330880 | bytes 8229201 | solution.py:74
  62.0 0.8 constant_dynamic-slice_fusion.2
  62.8 0.5 fusion.34
  64.6 1.3 multiply_reduce_fusion.3
  65.9 2.8 %exponential_convert_fusion.2 = bf16[1024,1024]{1,0:T(8,128)(2,1)S(1)} fusion(f32[1024]{0:T(1024)S(1)} %get-tuple-element.119, f32[1024]{0:T(1024)S(1)} %get-tuple-element.120, f32[1024]{0:T(1024)S(1)} %get-tuple-element.121, f32[1024]{0:T(1024)S(1)} %get-tuple-element.122, bf16[192,8192]{1,0:T(8,128)(2,1)} %get-tuple-element.152, s32[]{:T(128)S(6)} %select_n.22, ...), kind=kOutput, calls=%fused_computation.clone.1 | convolution fusion | flops 409993216 | bytes 2899976 | tf_op jit(solution)/shard_map/while/body/dot_general | solution.py:16
  68.7 0.7 fusion.35
  70.7 0.4 fusion.36
  71.7 0.8 constant_dynamic-slice_fusion.2
  72.5 0.5 fusion.34
  74.3 1.3 multiply_reduce_fusion.3
  75.6 2.8 %exponential_convert_fusion.2 = bf16[1024,1024]{1,0:T(8,128)(2,1)S(1)} fusion(f32[1024]{0:T(1024)S(1)} %get-tuple-element.119, f32[1024]{0:T(1024)S(1)} %get-tuple-element.120, f32[1024]{0:T(1024)S(1)} %get-tuple-element.121, f32[1024]{0:T(1024)S(1)} %get-tuple-element.122, bf16[192,8192]{1,0:T(8,128)(2,1)} %get-tuple-element.152, s32[]{:T(128)S(6)} %select_n.22, ...), kind=kOutput, calls=%fused_computation.clone.1 | convolution fusion | flops 409993216 | bytes 2899976 | tf_op jit(solution)/shard_map/while/body/dot_general | solution.py:16
  78.4 0.7 fusion.35
  80.3 0.4 fusion.36
  81.4 0.8 constant_dynamic-slice_fusion.2
  82.2 0.5 fusion.34
  84.0 1.3 multiply_reduce_fusion.3
  85.3 2.8 %exponential_convert_fusion.2 = bf16[1024,1024]{1,0:T(8,128)(2,1)S(1)} fusion(f32[1024]{0:T(1024)S(1)} %get-tuple-element.119, f32[1024]{0:T(1024)S(1)} %get-tuple-element.120, f32[1024]{0:T(1024)S(1)} %get-tuple-element.121, f32[1024]{0:T(1024)S(1)} %get-tuple-element.122, bf16[192,8192]{1,0:T(8,128)(2,1)} %get-tuple-element.152, s32[]{:T(128)S(6)} %select_n.22, ...), kind=kOutput, calls=%fused_computation.clone.1 | convolution fusion | flops 409993216 | bytes 2899976 | tf_op jit(solution)/shard_map/while/body/dot_general | solution.py:16
  88.1 0.7 fusion.35
  90.0 0.4 fusion.36
  91.1 0.8 constant_dynamic-slice_fusion.2
  91.8 0.5 fusion.34
  93.6 1.3 multiply_reduce_fusion.3
  94.9 2.8 %exponential_convert_fusion.2 = bf16[1024,1024]{1,0:T(8,128)(2,1)S(1)} fusion(f32[1024]{0:T(1024)S(1)} %get-tuple-element.119, f32[1024]{0:T(1024)S(1)} %get-tuple-element.120, f32[1024]{0:T(1024)S(1)} %get-tuple-element.121, f32[1024]{0:T(1024)S(1)} %get-tuple-element.122, bf16[192,8192]{1,0:T(8,128)(2,1)} %get-tuple-element.152, s32[]{:T(128)S(6)} %select_n.22, ...), kind=kOutput, calls=%fused_computation.clone.1 | convolution fusion | flops 409993216 | bytes 2899976 | tf_op jit(solution)/shard_map/while/body/dot_general | solution.py:16
  97.8 0.7 fusion.35
  99.7 0.4 fusion.36
  100.7 0.0 copy-start.1
  100.8 0.8 copy-done.1
  101.5 0.0 reduce-scatter.2.cloned.1.call-update
  101.6 54.1 %reduce-scatter.2.cloned.1.call-done = f32[16,512]{1,0:T(8,128)} async-done(((f32[16,8192]{1,0:T(8,128)}), f32[16,512]{1,0:T(8,128)}) %reduce-scatter.2.cloned.1.call-update) | async-done | bytes 32784 | tf_op jit(solution)/shard_map/reduce_scatter | solution.py:75
  155.6 0.0 copy-done.2
  155.6 0.9 convolution_bitcast_fusion
  156.5 30.1 %psum.7 = f32[16,16]{0,1:T(8,128)S(1)} all-reduce(f32[16,16]{0,1:T(8,128)S(1)} %convolution_bitcast_fusion), channel_id=1, replica_groups=mesh['cohort'=2,'row'=16] {'row'}, use_global_device_ids=true, to_apply=%region_5.0 | all-reduce | flops 256 | bytes 2048 | tf_op jit(solution)/shard_map/psum | solution.py:80
  186.7 0.7 copy.12
  187.3 0.9 convolution_subtract_fusion.1
  188.3 0.8 convolution_subtract_fusion
  (11 shorter events, 0.1 us)
Async XLA Ops:
  7.2 181.1 %copy-start = (f32[16,512]{1,0:T(8,128)S(1)}, f32[16,512]{1,0:T(8,128)}, u32[]{:S(2)}) copy-start(f32[16,512]{1,0:T(8,128)} %param.14) | copy-start | bytes 98308
  7.2 54.1 %all-gather.3.cloned.1.call-start = ((), (), s32[]{:S(2)}) async-start(), calls=%async_computation.1 | async-start | bytes 3342336 | tf_op jit(solution)/shard_map/all_gather | solution.py:64
  7.9 147.7 %reduce-scatter.2.cloned.1.call-start = ((), (), s32[]{:S(2)}) async-start(), calls=%async_computation.2 | async-start | bytes 557056 | tf_op jit(solution)/shard_map/reduce_scatter | solution.py:75
  61.3 40.3 %copy-start.3 = (f32[512]{0:T(512)S(1)}, f32[512]{0:T(512)}, u32[]{:S(2)}) copy-start(f32[512]{0:T(512)} %param.12) | copy-start | bytes 6148
  61.3 94.3 %copy-start.2 = (f32[16,512]{1,0:T(8,128)S(1)}, f32[16,512]{1,0:T(8,128)}, u32[]{:S(2)}) copy-start(f32[16,512]{1,0:T(8,128)} %param.13) | copy-start | bytes 98308
  61.3 127.0 %copy-start.4 = (f32[16,16]{1,0:T(8,128)S(1)}, f32[16,16]{1,0:T(8,128)}, u32[]{:S(2)}) copy-start(f32[16,16]{1,0:T(8,128)} %param.15) | copy-start | bytes 3076
  100.7 0.8 copy-start.1
Sparse Core Ops, SparseCore 0:
  10.2 51.0 all-gather.2
  101.7 53.9 reduce-scatter.1
where the time goes:
time: 196 us
  blocking collectives  72 us (37%)
  waiting for transfers between devices  64.7 us (33%)
  matrix products  17.9 us (9%)
  between operations  14.1 us (7%)
  loops' own time  13.7 us (7%)
  local copies, waits for them, and re-layouts  7.33 us (4%)
  other arithmetic  6.14 us (3%)
    reduce_scatter x1, waiting for transfers between devices, shards(): summed = lax.psum_scatter(totals, 'row', scatter_dimension=1, tiled=True)  54.1 us
    psum x1, blocking collectives, shards(): coupling = lax.psum(partial_value, 'row') / total_rows  30.1 us
    all_gather x1, blocking collectives, shards(): lax.all_gather(local_scale, 'row', axis=0, tiled=True)  23.2 us
    all_gather x1, blocking collectives, shards(): lax.all_gather(weighted, 'row', axis=1, tiled=True)  18.7 us
    another operation x1, loops' own time, shards(): totals = lax.fori_loop(0, tile_counts[0], own_step, totals)  13.7 us
    dot_general x4, matrix products, affinity(): lax.dot_general(left_x, right_x, (((0,), (0,)), ((), ())), preferred_elem...  11.1 us
    all_gather x1, waiting for transfers between devices, shards(): lax.all_gather(embeddings, 'row', axis=1, tiled=True)  9.9 us
    reduce_sum x4, other arithmetic, affinity(): left_norm = jnp.sum(jnp.square(left_x.astype(jnp.float32)), axis=0)  5.23 us
  transfers between devices with their start and end apart: 2, of which 2 were waited for; matrix products, arithmetic and copies ran while one was open for 1% of the time, Pallas kernels for 0%

commit v1 on v0

v1 whole, which is shorter than its diff:
```python
import math

import jax
import jax.numpy as jnp
from jax import lax
from jax.experimental import pallas as pl
from jax.experimental.pallas import tpu as pltpu
from jax.sharding import PartitionSpec as P

LANCZOS = 16
BLK = 1024


HIGHEST = lax.Precision.HIGHEST


def affinity_kernel(mask_ref, xo_ref, no_ref, ro_ref, xc_ref, nc_ref, rc_ref, wc_ref, out_ref):
    c = pl.program_id(0)

    @pl.when(c == 0)
    def _():
        out_ref[...] = jnp.zeros_like(out_ref)

    @pl.when(mask_ref[c] != 0)
    def _():
        inner = jnp.dot(xo_ref[...], xc_ref[...], preferred_element_type=jnp.float32)
        distance = (no_ref[...] + nc_ref[...]) - 2.0 * inner
        weights = jnp.exp(-distance * (ro_ref[...] * rc_ref[...])).astype(jnp.bfloat16)
        out_ref[...] += lax.dot_general(
            wc_ref[...], weights, (((1,), (1,)), ((), ())), preferred_element_type=jnp.float32
        )


def own_rows_product(mask_row, x_own, norm_own, recip_own, gathered, norm_all, recip_all, width):
    own = x_own.shape[1]
    total = gathered.shape[1]
    lanes_row = width // LANCZOS
    grid_spec = pltpu.PrefetchScalarGridSpec(
        num_scalar_prefetch=1,
        grid=(total // BLK,),
        in_specs=[
            pl.BlockSpec((own, width), lambda c, m: (0, 0)),
            pl.BlockSpec((own, 1), lambda c, m: (0, 0)),
            pl.BlockSpec((own, 1), lambda c, m: (0, 0)),
            pl.BlockSpec((width, BLK), lambda c, m: (0, c)),
            pl.BlockSpec((1, BLK), lambda c, m: (0, c)),
            pl.BlockSpec((1, BLK), lambda c, m: (0, c)),
            pl.BlockSpec((LANCZOS, BLK), lambda c, m: (lanes_row, c)),
        ],
        out_specs=pl.BlockSpec((LANCZOS, own), lambda c, m: (0, 0)),
    )
    return pl.pallas_call(
        affinity_kernel,
        grid_spec=grid_spec,
        out_shape=jax.ShapeDtypeStruct((LANCZOS, own), jnp.float32),
    )(mask_row, x_own.T, norm_own, recip_own, gathered, norm_all, recip_all, gathered)


def shards(
    embeddings,
    local_scale,
    degree_scale,
    lanczos_block,
    previous_block,
    previous_coupling,
    tile_plan,
    tile_counts,
):
    width, own = embeddings.shape
    devices = lax.axis_size("row")
    total_rows = devices * own
    slots = tile_plan.shape[0]
    weighted = (degree_scale[None, :] * lanczos_block).astype(jnp.bfloat16)
    plan_row = jnp.concatenate([tile_plan.reshape(-1), tile_counts]).astype(jnp.bfloat16)
    plan_row = jnp.pad(plan_row, (0, own - plan_row.shape[0]))
    packed = jnp.concatenate(
        [embeddings, weighted, local_scale[None, :], plan_row[None, :]], axis=0
    )
    gathered = lax.all_gather(packed, "row", axis=1, tiled=True)

    plans = gathered[width + LANCZOS + 1].reshape(devices, own)[:, : 2 * slots + 1]
    plans = plans.astype(jnp.int32)
    counts = plans[:, 2 * slots]
    pairs = plans[:, : 2 * slots].reshape(devices, slots, 2)
    live = jnp.arange(slots, dtype=jnp.int32)[None, :] < counts[:, None]
    row_block = pairs[..., 0].reshape(-1)
    col_block = pairs[..., 1].reshape(-1)
    live = live.reshape(-1)
    my_block = (lax.axis_index("row") * own) // BLK
    block_ids = jnp.arange(total_rows // BLK, dtype=jnp.int32)
    hit = live[:, None] & (
        ((row_block[:, None] == my_block) & (col_block[:, None] == block_ids[None, :]))
        | ((col_block[:, None] == my_block) & (row_block[:, None] == block_ids[None, :]))
    )
    mask_row = jnp.any(hit, axis=0).astype(jnp.int32)

    x_all = gathered[:width]
    norm_all = jnp.sum(jnp.square(x_all.astype(jnp.float32)), axis=0)[None, :]
    recip_all = (1.0 / gathered[width + LANCZOS].astype(jnp.float32))[None, :]
    norm_own = jnp.sum(jnp.square(embeddings.astype(jnp.float32)), axis=0)[:, None]
    recip_own = (1.0 / local_scale.astype(jnp.float32))[:, None]

    summed = own_rows_product(
        mask_row, embeddings, norm_own, recip_own, gathered, norm_all, recip_all, width
    )
    scaled = summed * (degree_scale[None, :] / math.sqrt(total_rows))
    partial_value = lax.dot_general(
        lanczos_block, scaled, (((1,), (1,)), ((), ())), precision=HIGHEST
    )
    coupling = lax.psum(partial_value, "row") / total_rows
    projected = lax.dot_general(
        coupling, lanczos_block, (((0,), (0,)), ((), ())), precision=HIGHEST
    )
    result = scaled - projected - jnp.dot(previous_coupling, previous_block, precision=HIGHEST)
    return (result, coupling)


def solution(mesh):
    in_specs = (
        P(None, ("cohort", "row")),
        P(("cohort", "row")),
        P(("cohort", "row")),
        P(None, ("cohort", "row")),
        P(None, ("cohort", "row")),
        P("cohort", None),
        P(("cohort", "row"), None),
        P(("cohort", "row")),
    )
    out_specs = (P(None, ("cohort", "row")), P("cohort", None))
    return jax.shard_map(shards, mesh=mesh, in_specs=in_specs, out_specs=out_specs, check_vma=False)
```

time: 196 us -> 123 us (0.63)
  blocking collectives: 72 us -> 30.5 us
  waiting for transfers between devices: 64.7 us -> 46.3 us
  matrix products: 17.9 us -> 2.6 us
  loops' own time: 13.7 us -> 0 us
  Pallas kernels: 0 us -> 9.59 us
  other arithmetic: 6.14 us -> 11 us
    reduce_scatter x1 -> x0, waiting for transfers between devices: 54.1 us -> none  [shards(): summed = lax.psum_scatter(totals, 'row', scatter_dimension=1, tiled=True)]
    all_gather x2 -> x0, blocking collectives: 41.8 us -> none  [the longest x1 23.2 us: shards(): lax.all_gather(local_scale, 'row', axis=0, tiled=True)]
    all_gather x1, waiting for transfers between devices: 9.9 us -> 46.3 us  [shards(): gathered = lax.all_gather(packed, 'row', axis=1, tiled=True)]
    dot_general x12 -> x0, matrix products: 15.3 us -> none  [the longest x4 11.1 us: affinity(): lax.dot_general(left_x, right_x, (((0,), (0,)), ((), ())), preferred_elem...]
    another operation x1 -> x0, loops' own time: 13.7 us -> none  [shards(): totals = lax.fori_loop(0, tile_counts[0], own_step, totals)]
    pallas_call x0 -> x1, Pallas kernels: none -> 9.59 us  [own_rows_product(): pl.pallas_call(affinity_kernel, grid_spec=grid_spec, out_shape=jax.ShapeD...]
    dynamic_slice x4 -> x0, local copies, waits for them, and re-layouts: 3.02 us -> none  [own_step(): entry = lax.dynamic_slice_in_dim(tile_plan, turn, 1, 0)[0]]
    broadcast_in_dim x1 -> x4, local copies, waits for them, and re-layouts: 0.03 us -> 2.39 us  [the longest x1 0.85 us: shards(): jnp.sum(jnp.square(embeddings.astype(jnp.float32)), axis=0)[:, None]]
  transfers between devices with their start and end apart: 2 -> 1, of which waited for: 2 -> 1; matrix products, arithmetic and copies ran while one was open for 1% -> 5% of each run, Pallas kernels for 0% -> 0%
where the time goes in v1:
time: 123 us; the launch traced here: 121 us
  waiting for transfers between devices  46.3 us (38%)
  blocking collectives  30.5 us (25%)
  between operations  14.8 us (12%)
  other arithmetic  11 us (9%)
  Pallas kernels  9.59 us (8%)
  local copies, waits for them, and re-layouts  6.6 us (5%)
  matrix products  2.6 us (2%)
    all_gather x1, waiting for transfers between devices, shards(): gathered = lax.all_gather(packed, 'row', axis=1, tiled=True)  46.3 us
    psum x1, blocking collectives, shards(): coupling = lax.psum(partial_value, 'row') / total_rows  30.5 us
    pallas_call x1, Pallas kernels, own_rows_product(): pl.pallas_call(affinity_kernel, grid_spec=grid_spec, out_shape=jax.ShapeD...  9.59 us
    reduce_sum x1, other arithmetic, shards(): norm_all = jnp.sum(jnp.square(x_all.astype(jnp.float32)), axis=0)[None, :]  3.17 us
    unnamed x9, local copies, waits for them, and re-layouts  2.52 us
  transfers between devices with their start and end apart: 1, of which 1 were waited for; matrix products, arithmetic and copies ran while one was open for 5% of the time, Pallas kernels for 0%

profile of v1, /device:TPU:0, one launch (start us, length us, event | category | flops | bytes accessed | tf_op | source)
XLA Modules:
  0.0 121.4 jit_solution(4164901910263598889)
XLA Ops:
  7.2 0.0 copy-start
  7.2 0.0 all-gather.2.cloned.1.call-start
  7.2 0.7 convert.7
  7.9 0.1 copy.24
  8.0 0.1 reshape.44
  8.8 0.1 fusion.10
  8.8 0.7 broadcast_in_dim.10
  9.5 0.8 multiply_convert_fusion
  10.3 1.6 %pad_maximum_fusion = bf16[210,512]{1,0:T(8,128)(2,1)} fusion(bf16[1,512]{1,0:T(2,128)(2,1)S(1)} %broadcast_in_dim.22, bf16[1,512]{1,0:T(2,128)(2,1)S(1)} %broadcast_in_dim.10, bf16[16,512]{1,0:T(8,128)(2,1)S(1)} %multiply_convert_fusion, bf16[192,512]{1,0:T(8,128)(2,1)} %param.8), kind=kLoop, calls=%fused_computation.5 | loop fusion | flops 860160 | bytes 430080 | tf_op jit(solution)/shard_map/concatenate | solution.py:76
  11.9 0.0 all-gather.2.cloned.1.call-update
  12.0 1.8 %copy.28 = bf16[192,512]{0,1:T(8,128)(2,1)} copy(bf16[192,512]{1,0:T(8,128)(2,1)} %param.8) | data formatting | bytes 393216 | tf_op args[0]
  13.7 1.0 multiply_reduce_fusion.1
  14.7 0.9 copy.29.no_ref
  15.6 0.7 convert_divide_fusion
  16.2 0.8 copy.30.ro_ref
  17.1 0.7 broadcast_multiply_fusion.1
  17.8 46.3 %all-gather.2.cloned.1.call-done.xc_ref.wc_ref = bf16[210,8192]{1,0:T(8,128)(2,1)} async-done(((bf16[210,512]{1,0:T(8,128)(2,1)}), bf16[210,8192]{1,0:T(8,128)(2,1)}) %all-gather.2.cloned.1.call-update) | async-done | bytes 3440656 | tf_op jit(solution)/shard_map/all_gather | solution.py:79
  64.1 1.0 slice_reduce_fusion
  65.1 0.1 copy.32
  65.2 0.1 copy.26
  65.3 0.1 broadcast_in_dim_reshape_squeeze.2
  65.4 0.1 copy.27
  65.5 0.1 eq.50
  65.6 0.1 iota_compare_fusion
  65.7 0.1 lt.26
  65.8 0.1 fusion.7
  65.9 0.5 convert_element_type.27.mask_ref
  66.4 3.2 %multiply_reduce_fusion = f32[8192]{0:T(1024)} fusion(bf16[210,8192]{1,0:T(8,128)(2,1)} %all-gather.2.cloned.1.call-done.xc_ref.wc_ref), kind=kLoop, calls=%fused_computation | loop fusion | flops 4710400 | bytes 3178496 | tf_op jit(solution)/shard_map/reduce_sum | solution.py:98
  69.6 1.5 %fusion.rc_ref = f32[1,8192]{1,0:T(1,128)} fusion(bf16[210,8192]{1,0:T(8,128)(2,1)} %all-gather.2.cloned.1.call-done.xc_ref.wc_ref), kind=kLoop, calls=%fused_computation.7 | loop fusion | flops 16384 | bytes 49152 | tf_op jit(solution)/shard_map/div | solution.py:99
  71.1 0.0 copy-start.1
  71.1 0.0 copy-start.2
  71.1 9.6 %shard_map.95 = f32[16,512]{1,0:T(8,128)} custom-call(s32[8]{0:T(128)} %convert_element_type.27.mask_ref, bf16[512,192]{1,0:T(8,128)(2,1)} %bitcast.17, f32[512,1]{1,0:T(8,128)} %copy.29.no_ref, f32[512,1]{1,0:T(8,128)} %copy.30.ro_ref, bf16[210,8192]{1,0:T(8,128)(2,1)} %all-gather.2.cloned.1.call-done.xc_ref.wc_ref, f32[1,8192]{1,0:T(1,128)} %bitcast.18, ...), custom_call_target="tpu_custom_call" | custom-call | tf_op jit(solution)/shard_map/pallas_call | solution.py:52
  80.7 0.0 copy-done.1
  80.7 0.9 convolution_bitcast_fusion
  81.6 30.5 %psum.7 = f32[16,16]{0,1:T(8,128)S(1)} all-reduce(f32[16,16]{0,1:T(8,128)S(1)} %convolution_bitcast_fusion), channel_id=1, replica_groups=mesh['cohort'=2,'row'=16] {'row'}, use_global_device_ids=true, to_apply=%region_3.4 | all-reduce | flops 256 | bytes 2048 | tf_op jit(solution)/shard_map/psum | solution.py:110
  112.1 0.9 convolution_subtract_fusion.1
  113.1 0.7 copy.31
  113.7 0.0 copy-done
  113.7 0.0 copy-done.2
  113.7 0.8 convolution_subtract_fusion
  (9 shorter events, 0.1 us)
Async XLA Ops:
  7.2 106.6 %copy-start = (f32[16,512]{1,0:T(8,128)S(1)}, f32[16,512]{1,0:T(8,128)}, u32[]{:S(2)}) copy-start(f32[16,512]{1,0:T(8,128)} %param.12) | copy-start | bytes 98308
  7.2 56.9 %all-gather.2.cloned.1.call-start = ((), (), s32[]{:S(2)}) async-start(), calls=%async_computation | async-start | bytes 3760128 | tf_op jit(solution)/shard_map/all_gather | solution.py:79
  71.1 9.6 %copy-start.1 = (f32[16,512]{1,0:T(8,128)S(1)}, f32[16,512]{1,0:T(8,128)}, u32[]{:S(2)}) copy-start(f32[16,512]{1,0:T(8,128)} %param.11) | copy-start | bytes 98308
  71.1 42.6 %copy-start.2 = (f32[16,16]{1,0:T(8,128)S(1)}, f32[16,16]{1,0:T(8,128)}, u32[]{:S(2)}) copy-start(f32[16,16]{1,0:T(8,128)} %param.13) | copy-start | bytes 3076
Sparse Core Ops, SparseCore 0:
  12.1 51.9 all-gather.1

commit v2 on v1

--- a/solution.py
+++ b/solution.py
@@ -56,6 +56,17 @@
     )(mask_row, x_own.T, norm_own, recip_own, gathered, norm_all, recip_all, gathered)
 
 
+def sum_over_rows(value):
+    devices = lax.axis_size("row")
+    if devices & (devices - 1):
+        return lax.psum(value, "row")
+    stride = 1
+    while stride < devices:
+        value = value + lax.ppermute(value, "row", [(i, i ^ stride) for i in range(devices)])
+        stride *= 2
+    return value
+
+
 def shards(
     embeddings,
     local_scale,
@@ -107,7 +118,7 @@
     partial_value = lax.dot_general(
         lanczos_block, scaled, (((1,), (1,)), ((), ())), precision=HIGHEST
     )
-    coupling = lax.psum(partial_value, "row") / total_rows
+    coupling = sum_over_rows(partial_value) / total_rows
     projected = lax.dot_general(
         coupling, lanczos_block, (((0,), (0,)), ((), ())), precision=HIGHEST
     )

time: 123 us -> 105 us (0.85); the launches traced: 121 us -> 105 us
  blocking collectives: 30.5 us -> 0 us
  waiting for transfers between devices: 46.3 us -> 56.1 us
  starting transfers between devices: 0.04 us -> 3.17 us
    psum x1 -> x0, blocking collectives: 30.5 us -> none  [shards(): coupling = lax.psum(partial_value, 'row') / total_rows]
    ppermute x0 -> x4, waiting for transfers between devices: none -> 9.77 us  [sum_over_rows(): lax.ppermute(value, 'row', [(i, i ^ stride) for i in range(devices)])]
    ppermute x0 -> x4, starting transfers between devices: none -> 3.14 us  [sum_over_rows(): lax.ppermute(value, 'row', [(i, i ^ stride) for i in range(devices)])]
  transfers between devices with their start and end apart: 1 -> 5, of which waited for: 1 -> 5; matrix products, arithmetic and copies ran while one was open for 5% -> 6% of each run, Pallas kernels for 0% -> 0%
where the time goes in v2:
time: 105 us
  waiting for transfers between devices  56.1 us (53%)
  between operations  14.8 us (14%)
  other arithmetic  11 us (10%)
  Pallas kernels  10.5 us (10%)
  local copies, waits for them, and re-layouts  6.64 us (6%)
  starting transfers between devices  3.17 us (3%)
  matrix products  2.58 us (2%)
    all_gather x1, waiting for transfers between devices, shards(): gathered = lax.all_gather(packed, 'row', axis=1, tiled=True)  46.3 us
    pallas_call x1, Pallas kernels, own_rows_product(): pl.pallas_call(affinity_kernel, grid_spec=grid_spec, out_shape=jax.ShapeD...  10.5 us
    ppermute x4, waiting for transfers between devices, sum_over_rows(): lax.ppermute(value, 'row', [(i, i ^ stride) for i in range(devices)])  9.77 us
    reduce_sum x1, other arithmetic, shards(): norm_all = jnp.sum(jnp.square(x_all.astype(jnp.float32)), axis=0)[None, :]  3.17 us
    ppermute x4, starting transfers between devices, sum_over_rows(): lax.ppermute(value, 'row', [(i, i ^ stride) for i in range(devices)])  3.14 us
    unnamed x9, local copies, waits for them, and re-layouts  2.55 us
  transfers between devices with their start and end apart: 5, of which 5 were waited for; matrix products, arithmetic and copies ran while one was open for 6% of the time, Pallas kernels for 0%

profile of v2, /device:TPU:0, one launch (start us, length us, event | category | flops | bytes accessed | tf_op | source)
XLA Modules:
  0.0 104.6 jit_solution(6914279455936797668)
XLA Ops:
  7.2 0.0 copy-start
  7.2 0.0 all-gather.2.cloned.1.call-start
  7.2 0.7 convert.7
  7.9 0.1 copy.24
  8.0 0.1 reshape.44
  8.8 0.1 fusion.11
  8.8 0.7 broadcast_in_dim.10
  9.5 0.8 multiply_convert_fusion
  10.3 1.6 %pad_maximum_fusion = bf16[210,512]{1,0:T(8,128)(2,1)} fusion(bf16[1,512]{1,0:T(2,128)(2,1)S(1)} %broadcast_in_dim.22, bf16[1,512]{1,0:T(2,128)(2,1)S(1)} %broadcast_in_dim.10, bf16[16,512]{1,0:T(8,128)(2,1)S(1)} %multiply_convert_fusion, bf16[192,512]{1,0:T(8,128)(2,1)} %param.8), kind=kLoop, calls=%fused_computation.5 | loop fusion | flops 860160 | bytes 430080 | tf_op jit(solution)/shard_map/concatenate | solution.py:87
  11.9 0.0 all-gather.2.cloned.1.call-update
  12.0 1.8 %copy.28 = bf16[192,512]{0,1:T(8,128)(2,1)} copy(bf16[192,512]{1,0:T(8,128)(2,1)} %param.8) | data formatting | bytes 393216 | tf_op args[0]
  13.7 1.0 multiply_reduce_fusion.1
  14.7 0.8 copy.29.no_ref
  15.6 0.7 convert_divide_fusion
  16.3 0.9 copy.30.ro_ref
  17.1 0.7 broadcast_multiply_fusion
  17.8 46.3 %all-gather.2.cloned.1.call-done.xc_ref.wc_ref = bf16[210,8192]{1,0:T(8,128)(2,1)} async-done(((bf16[210,512]{1,0:T(8,128)(2,1)}), bf16[210,8192]{1,0:T(8,128)(2,1)}) %all-gather.2.cloned.1.call-update) | async-done | bytes 3440656 | tf_op jit(solution)/shard_map/all_gather | solution.py:90
  64.1 1.0 slice_reduce_fusion
  65.1 0.1 copy.32
  65.2 0.1 copy.26
  65.3 0.1 broadcast_in_dim_reshape_squeeze.2
  65.4 0.1 copy.27
  65.5 0.1 eq.50
  65.6 0.1 iota_compare_fusion
  65.7 0.1 lt.26
  65.8 0.1 fusion.8
  65.9 0.5 convert_element_type.27.mask_ref
  66.4 3.2 %multiply_reduce_fusion = f32[8192]{0:T(1024)} fusion(bf16[210,8192]{1,0:T(8,128)(2,1)} %all-gather.2.cloned.1.call-done.xc_ref.wc_ref), kind=kLoop, calls=%fused_computation | loop fusion | flops 4710400 | bytes 3178496 | tf_op jit(solution)/shard_map/reduce_sum | solution.py:109
  69.6 1.6 %fusion.1.rc_ref = f32[1,8192]{1,0:T(1,128)} fusion(bf16[210,8192]{1,0:T(8,128)(2,1)} %all-gather.2.cloned.1.call-done.xc_ref.wc_ref), kind=kLoop, calls=%fused_computation.7 | loop fusion | flops 16384 | bytes 49152 | tf_op jit(solution)/shard_map/div | solution.py:110
  71.1 0.0 copy-start.1
  71.1 0.0 copy-start.2
  71.2 10.5 %shard_map.95 = f32[16,512]{1,0:T(8,128)} custom-call(s32[8]{0:T(128)} %convert_element_type.27.mask_ref, bf16[512,192]{1,0:T(8,128)(2,1)} %bitcast.18, f32[512,1]{1,0:T(8,128)} %copy.29.no_ref, f32[512,1]{1,0:T(8,128)} %copy.30.ro_ref, bf16[210,8192]{1,0:T(8,128)(2,1)} %all-gather.2.cloned.1.call-done.xc_ref.wc_ref, f32[1,8192]{1,0:T(1,128)} %bitcast.19, ...), custom_call_target="tpu_custom_call" | custom-call | tf_op jit(solution)/shard_map/pallas_call | solution.py:52
  81.6 0.0 copy-done.1
  81.6 0.9 convolution_bitcast_fusion
  82.5 0.3 collective-permute-start
  82.8 0.9 collective-permute-done
  83.7 1.4 %collective-permute-start.1 = (f32[16,16]{0,1:T(8,128)S(1)}, f32[16,16]{0,1:T(8,128)S(1)}, u32[]{:S(2)}, u32[]{:S(2)}) collective-permute-start(f32[16,16]{0,1:T(8,128)S(1)} %add.15), channel_id=1, source_target_pairs={{0,2},{1,3},{2,0},{3,1},{4,6},{5,7},{6,4},{7,5},{8,10},{9,11},{10,... | collective-permute-start | bytes 3080 | tf_op jit(solution)/shard_map/ppermute | solution.py:65
  85.1 2.3 %collective-permute-done.1 = f32[16,16]{0,1:T(8,128)S(1)} collective-permute-done((f32[16,16]{0,1:T(8,128)S(1)}, f32[16,16]{0,1:T(8,128)S(1)}, u32[]{:S(2)}, u32[]{:S(2)}) %collective-permute-start.1) | collective-permute-done | bytes 1056 | tf_op jit(solution)/shard_map/ppermute | solution.py:65
  87.4 0.0 collective-permute-start.2
  87.4 3.6 %collective-permute-done.2 = f32[16,16]{0,1:T(8,128)S(1)} collective-permute-done((f32[16,16]{0,1:T(8,128)S(1)}, f32[16,16]{0,1:T(8,128)S(1)}, u32[]{:S(2)}, u32[]{:S(2)}) %collective-permute-start.2) | collective-permute-done | bytes 1056 | tf_op jit(solution)/shard_map/ppermute | solution.py:65
  91.0 1.5 %collective-permute-start.3 = (f32[16,16]{0,1:T(8,128)S(1)}, f32[16,16]{0,1:T(8,128)S(1)}, u32[]{:S(2)}, u32[]{:S(2)}) collective-permute-start(f32[16,16]{0,1:T(8,128)S(1)} %add.17), channel_id=1, source_target_pairs={{0,8},{1,9},{2,10},{3,11},{4,12},{5,13},{6,14},{7,15},{8,0},{9,1},... | collective-permute-start | bytes 3080 | tf_op jit(solution)/shard_map/ppermute | solution.py:65
  92.5 0.0 copy-done
  92.5 0.0 copy-done.2
  92.5 0.1 fusion.13
  92.6 2.9 %collective-permute-done.3 = f32[16,16]{0,1:T(8,128)S(1)} collective-permute-done((f32[16,16]{0,1:T(8,128)S(1)}, f32[16,16]{0,1:T(8,128)S(1)}, u32[]{:S(2)}, u32[]{:S(2)}) %collective-permute-start.3) | collective-permute-done | bytes 1056 | tf_op jit(solution)/shard_map/ppermute | solution.py:65
  95.6 0.7 copy.31
  96.3 1.5 %fusion = f32[16,512]{1,0:T(8,128)} fusion(f32[16,512]{1,0:T(8,128)S(1)} %fusion.13, f32[16,16]{0,1:T(8,128)S(1)} %add_multiply_fusion, f32[16,512]{1,0:T(8,128)S(1)} %copy-done.1, f32[16,512]{1,0:T(8,128)} %shard_map.95, f32[512]{0:T(512)S(1)} %broadcast_multiply_fusion), kind=kOutput, calls=%fused_computation.2 | convolution fusion | flops 1597440 | bytes 134144 | tf_op jit(solution)/shard_map/dot_general | solution.py:122
  (12 shorter events, 0.1 us)
Async XLA Ops:
  7.2 85.3 %copy-start = (f32[16,512]{1,0:T(8,128)S(1)}, f32[16,512]{1,0:T(8,128)}, u32[]{:S(2)}) copy-start(f32[16,512]{1,0:T(8,128)} %param.12) | copy-start | bytes 98308
  7.2 56.9 %all-gather.2.cloned.1.call-start = ((), (), s32[]{:S(2)}) async-start(), calls=%async_computation | async-start | bytes 3760128 | tf_op jit(solution)/shard_map/all_gather | solution.py:90
  71.1 10.5 %copy-start.1 = (f32[16,512]{1,0:T(8,128)S(1)}, f32[16,512]{1,0:T(8,128)}, u32[]{:S(2)}) copy-start(f32[16,512]{1,0:T(8,128)} %param.11) | copy-start | bytes 98308
  71.1 21.3 %copy-start.2 = (f32[16,16]{1,0:T(8,128)S(1)}, f32[16,16]{1,0:T(8,128)}, u32[]{:S(2)}) copy-start(f32[16,16]{1,0:T(8,128)} %param.13) | copy-start | bytes 3076
  82.5 1.2 %collective-permute-start = (f32[16,16]{0,1:T(8,128)S(1)}, f32[16,16]{0,1:T(8,128)S(1)}, u32[]{:S(2)}, u32[]{:S(2)}) collective-permute-start(f32[16,16]{0,1:T(8,128)S(1)} %convolution_bitcast_fusion), channel_id=1, source_target_pairs={{0,1},{1,0},{2,3},{3,2},{4,5},{5,4},{6,7},{7,6},{8,9},{9,8},{10,11... | collective-permute-start | bytes 3080 | tf_op jit(solution)/shard_map/ppermute | solution.py:65
  83.7 3.7 %collective-permute-start.1 = (f32[16,16]{0,1:T(8,128)S(1)}, f32[16,16]{0,1:T(8,128)S(1)}, u32[]{:S(2)}, u32[]{:S(2)}) collective-permute-start(f32[16,16]{0,1:T(8,128)S(1)} %add.15), channel_id=1, source_target_pairs={{0,2},{1,3},{2,0},{3,1},{4,6},{5,7},{6,4},{7,5},{8,10},{9,11},{10,... | collective-permute-start | bytes 3080 | tf_op jit(solution)/shard_map/ppermute | solution.py:65
  87.4 3.7 %collective-permute-start.2 = (f32[16,16]{0,1:T(8,128)S(1)}, f32[16,16]{0,1:T(8,128)S(1)}, u32[]{:S(2)}, u32[]{:S(2)}) collective-permute-start(f32[16,16]{0,1:T(8,128)S(1)} %add.16), channel_id=1, source_target_pairs={{0,4},{1,5},{2,6},{3,7},{4,0},{5,1},{6,2},{7,3},{8,12},{9,13},{10,... | collective-permute-start | bytes 3080 | tf_op jit(solution)/shard_map/ppermute | solution.py:65
  91.0 4.5 %collective-permute-start.3 = (f32[16,16]{0,1:T(8,128)S(1)}, f32[16,16]{0,1:T(8,128)S(1)}, u32[]{:S(2)}, u32[]{:S(2)}) collective-permute-start(f32[16,16]{0,1:T(8,128)S(1)} %add.17), channel_id=1, source_target_pairs={{0,8},{1,9},{2,10},{3,11},{4,12},{5,13},{6,14},{7,15},{8,0},{9,1},... | collective-permute-start | bytes 3080 | tf_op jit(solution)/shard_map/ppermute | solution.py:65
Sparse Core Ops, SparseCore 0:
  12.1 51.9 all-gather.1

commit v3 on v2

--- a/solution.py
+++ b/solution.py
@@ -14,46 +14,93 @@
 HIGHEST = lax.Precision.HIGHEST
 
 
-def affinity_kernel(mask_ref, xo_ref, no_ref, ro_ref, xc_ref, nc_ref, rc_ref, wc_ref, out_ref):
-    c = pl.program_id(0)
+def affinity_kernel(flag_ref, xo_ref, no_ref, ro_ref, xc_ref, nc_ref, rc_ref, wc_ref, out_ref):
+    s = pl.program_id(0)
 
-    @pl.when(c == 0)
+    @pl.when(s == 0)
     def _():
         out_ref[...] = jnp.zeros_like(out_ref)
 
-    @pl.when(mask_ref[c] != 0)
+    @pl.when(flag_ref[s] != 0)
     def _():
-        inner = jnp.dot(xo_ref[...], xc_ref[...], preferred_element_type=jnp.float32)
-        distance = (no_ref[...] + nc_ref[...]) - 2.0 * inner
-        weights = jnp.exp(-distance * (ro_ref[...] * rc_ref[...])).astype(jnp.bfloat16)
+        inner = jnp.dot(xo_ref[...], xc_ref[0], preferred_element_type=jnp.float32)
+        distance = (no_ref[...] + nc_ref[0]) - 2.0 * inner
+        weights = jnp.exp(-distance * (ro_ref[...] * rc_ref[0])).astype(jnp.bfloat16)
         out_ref[...] += lax.dot_general(
-            wc_ref[...], weights, (((1,), (1,)), ((), ())), preferred_element_type=jnp.float32
+            wc_ref[0], weights, (((1,), (1,)), ((), ())), preferred_element_type=jnp.float32
         )
 
 
-def own_rows_product(mask_row, x_own, norm_own, recip_own, gathered, norm_all, recip_all, width):
+def own_rows_product(flags, x_own, norm_own, recip_own, pieces, norm_all, recip_all, width):
     own = x_own.shape[1]
-    total = gathered.shape[1]
+    slots = pieces.shape[0]
     lanes_row = width // LANCZOS
     grid_spec = pltpu.PrefetchScalarGridSpec(
         num_scalar_prefetch=1,
-        grid=(total // BLK,),
+        grid=(slots,),
         in_specs=[
-            pl.BlockSpec((own, width), lambda c, m: (0, 0)),
-            pl.BlockSpec((own, 1), lambda c, m: (0, 0)),
-            pl.BlockSpec((own, 1), lambda c, m: (0, 0)),
-            pl.BlockSpec((width, BLK), lambda c, m: (0, c)),
-            pl.BlockSpec((1, BLK), lambda c, m: (0, c)),
-            pl.BlockSpec((1, BLK), lambda c, m: (0, c)),
-            pl.BlockSpec((LANCZOS, BLK), lambda c, m: (lanes_row, c)),
+            pl.BlockSpec((own, width), lambda s, m: (0, 0)),
+            pl.BlockSpec((own, 1), lambda s, m: (0, 0)),
+            pl.BlockSpec((own, 1), lambda s, m: (0, 0)),
+            pl.BlockSpec((1, width, own), lambda s, m: (s, 0, 0)),
+            pl.BlockSpec((1, 1, own), lambda s, m: (s, 0, 0)),
+            pl.BlockSpec((1, 1, own), lambda s, m: (s, 0, 0)),
+            pl.BlockSpec((1, LANCZOS, own), lambda s, m: (s, lanes_row, 0)),
         ],
-        out_specs=pl.BlockSpec((LANCZOS, own), lambda c, m: (0, 0)),
+        out_specs=pl.BlockSpec((LANCZOS, own), lambda s, m: (0, 0)),
     )
     return pl.pallas_call(
         affinity_kernel,
         grid_spec=grid_spec,
         out_shape=jax.ShapeDtypeStruct((LANCZOS, own), jnp.float32),
-    )(mask_row, x_own.T, norm_own, recip_own, gathered, norm_all, recip_all, gathered)
+    )(flags, x_own.T, norm_own, recip_own, pieces, norm_all, recip_all, pieces)
+
+
+def gather_pieces(packed):
+    devices = lax.axis_size("row")
+    me = lax.axis_index("row")
+    if devices != 16:
+        pieces = lax.all_gather(packed, "row", axis=0, tiled=False)
+        return pieces, jnp.arange(devices, dtype=jnp.int32)
+    up = [(r, r + 4) for r in range(12)]
+    down = [(r, r - 4) for r in range(4, 16)]
+    across = [(r, r ^ 2) for r in range(16)]
+    twin = [(r, r ^ 1) for r in range(16)]
+    z = me // 4
+    partner = me ^ 2
+
+    up1 = lax.ppermute(packed, "row", up)
+    down1 = lax.ppermute(packed, "row", down)
+    across1 = lax.ppermute(packed, "row", across)
+    up2 = lax.ppermute(up1, "row", up)
+    down2 = lax.ppermute(down1, "row", down)
+    across2 = lax.ppermute(jnp.stack([up1, down1]), "row", across)
+    pick2 = jnp.where(z >= 2, up2, down2)
+    up3 = lax.ppermute(up2, "row", up)
+    down3 = lax.ppermute(down2, "row", down)
+    across3 = lax.ppermute(pick2, "row", across)
+    pick3 = jnp.where(z == 3, up3, down3)
+    across4 = lax.ppermute(pick3, "row", across)
+
+    ends = (z == 0) | (z == 3)
+    line1 = jnp.where(z >= 1, up1, down1)
+    line2 = jnp.where(z >= 2, up2, jnp.where(z == 1, down1, down2))
+    line3 = jnp.where(z == 3, up3, jnp.where(z == 2, down1, jnp.where(z == 1, down2, down3)))
+    other2 = jnp.where(z >= 1, across2[0], across2[1])
+    other3 = jnp.where(ends, across4, across2[1])
+    mine = jnp.stack([packed, line1, line2, line3, across1, across3, other2, other3])
+    origin = jnp.stack([
+        me,
+        jnp.where(z >= 1, me - 4, me + 4),
+        jnp.where(z >= 2, me - 8, jnp.where(z == 1, me + 4, me + 8)),
+        jnp.where(z == 3, me - 12, jnp.where(z == 2, me + 4, jnp.where(z == 1, me + 8, me + 12))),
+        partner,
+        jnp.where(z >= 2, partner - 8, partner + 8),
+        jnp.where(z >= 1, partner - 4, partner + 4),
+        jnp.where(z == 3, partner - 12, jnp.where(z == 0, partner + 12, partner + 4)),
+    ]).astype(jnp.int32)
+    theirs = lax.ppermute(mine, "row", twin)
+    return jnp.concatenate([mine, theirs]), jnp.concatenate([origin, origin ^ 1])
 
 
 def sum_over_rows(value):
@@ -87,10 +134,9 @@
     packed = jnp.concatenate(
         [embeddings, weighted, local_scale[None, :], plan_row[None, :]], axis=0
     )
-    gathered = lax.all_gather(packed, "row", axis=1, tiled=True)
+    pieces, origin = gather_pieces(packed)
 
-    plans = gathered[width + LANCZOS + 1].reshape(devices, own)[:, : 2 * slots + 1]
-    plans = plans.astype(jnp.int32)
+    plans = pieces[:, width + LANCZOS + 1, : 2 * slots + 1].astype(jnp.int32)
     counts = plans[:, 2 * slots]
     pairs = plans[:, : 2 * slots].reshape(devices, slots, 2)
     live = jnp.arange(slots, dtype=jnp.int32)[None, :] < counts[:, None]
@@ -104,15 +150,15 @@
         | ((col_block[:, None] == my_block) & (row_block[:, None] == block_ids[None, :]))
     )
     mask_row = jnp.any(hit, axis=0).astype(jnp.int32)
+    flags = mask_row[(origin * own) // BLK]
 
-    x_all = gathered[:width]
-    norm_all = jnp.sum(jnp.square(x_all.astype(jnp.float32)), axis=0)[None, :]
-    recip_all = (1.0 / gathered[width + LANCZOS].astype(jnp.float32))[None, :]
+    norm_all = jnp.sum(jnp.square(pieces[:, :width].astype(jnp.float32)), axis=1)[:, None, :]
+    recip_all = (1.0 / pieces[:, width + LANCZOS].astype(jnp.float32))[:, None, :]
     norm_own = jnp.sum(jnp.square(embeddings.astype(jnp.float32)), axis=0)[:, None]
     recip_own = (1.0 / local_scale.astype(jnp.float32))[:, None]
 
     summed = own_rows_product(
-        mask_row, embeddings, norm_own, recip_own, gathered, norm_all, recip_all, width
+        flags, embeddings, norm_own, recip_own, pieces, norm_all, recip_all, width
     )
     scaled = summed * (degree_scale[None, :] / math.sqrt(total_rows))
     partial_value = lax.dot_general(

time: 105 us -> 93 us (0.89)
  waiting for transfers between devices: 56.1 us -> 15.6 us
  starting transfers between devices: 3.17 us -> 32.1 us
  between operations: 14.8 us -> 1.45 us
  local copies, waits for them, and re-layouts: 6.64 us -> 13.2 us
  Pallas kernels: 10.5 us -> 15.1 us
    all_gather x1 -> x0, waiting for transfers between devices: 46.3 us -> none  [shards(): gathered = lax.all_gather(packed, 'row', axis=1, tiled=True)]
    ppermute x0 -> x11, starting transfers between devices: none -> 25.4 us  [the longest x1 5.57 us: gather_pieces(): up1 = lax.ppermute(packed, 'row', up)]
    ppermute x0 -> x11, waiting for transfers between devices: none -> 8.54 us  [the longest x1 1.46 us: gather_pieces(): up3 = lax.ppermute(up2, 'row', up)]
    pallas_call x1, Pallas kernels: 10.5 us -> 15.1 us  [own_rows_product(): pl.pallas_call(affinity_kernel, grid_spec=grid_spec, out_shape=jax.ShapeD...]
    ppermute x4, starting transfers between devices: 3.14 us -> 6.72 us  [sum_over_rows(): lax.ppermute(value, 'row', [(i, i ^ stride) for i in range(devices)])]
    unnamed x0 -> x5, other arithmetic: none -> 3.34 us
    ppermute x4, waiting for transfers between devices: 9.77 us -> 7.09 us  [sum_over_rows(): lax.ppermute(value, 'row', [(i, i ^ stride) for i in range(devices)])]
    concatenate x0 -> x2, local copies, waits for them, and re-layouts: none -> 1.88 us  [the longest x1 1.77 us: gather_pieces(): jnp.concatenate([mine, theirs])]
  transfers between devices with their start and end apart: 5 -> 15, of which waited for: 5 -> 11; matrix products, arithmetic and copies ran while one was open for 6% -> 10% of each run, Pallas kernels for 0% -> 0%
where the time goes in v3:
time: 93 us; the launch traced here: 92 us
  starting transfers between devices  32.1 us (35%)
  waiting for transfers between devices  15.6 us (17%)
  Pallas kernels  15.1 us (16%)
  local copies, waits for them, and re-layouts  13.2 us (14%)
  other arithmetic  11.9 us (13%)
  matrix products  2.58 us (3%)
  between operations  1.45 us (2%)
    pallas_call x1, Pallas kernels, own_rows_product(): pl.pallas_call(affinity_kernel, grid_spec=grid_spec, out_shape=jax.ShapeD...  15.1 us
    ppermute x4, waiting for transfers between devices, sum_over_rows(): lax.ppermute(value, 'row', [(i, i ^ stride) for i in range(devices)])  7.09 us
    ppermute x4, starting transfers between devices, sum_over_rows(): lax.ppermute(value, 'row', [(i, i ^ stride) for i in range(devices)])  6.72 us
    ppermute x1, starting transfers between devices, gather_pieces(): up1 = lax.ppermute(packed, 'row', up)  5.57 us
    ppermute x1, starting transfers between devices, gather_pieces(): up3 = lax.ppermute(up2, 'row', up)  5.03 us
    ppermute x1, starting transfers between devices, gather_pieces(): up2 = lax.ppermute(up1, 'row', up)  5.03 us
    unnamed x18, local copies, waits for them, and re-layouts  4.38 us
    unnamed x5, other arithmetic  3.34 us
  transfers between devices with their start and end apart: 15, of which 11 were waited for; matrix products, arithmetic and copies ran while one was open for 10% of the time, Pallas kernels for 0%

profile of v3, /device:TPU:0, one launch (start us, length us, event | category | flops | bytes accessed | tf_op | source)
XLA Modules:
  0.0 92.0 jit_solution(11062280234339684698)
XLA Ops:
  0.6 0.7 convert.8
  2.3 0.7 broadcast_in_dim.10
  3.0 0.8 multiply_convert_fusion
  3.7 0.9 %pad_maximum_fusion.1 = bf16[210,512]{1,0:T(8,128)(2,1)S(1)} fusion(bf16[1,512]{1,0:T(2,128)(2,1)S(1)} %broadcast_in_dim.11, bf16[1,512]{1,0:T(2,128)(2,1)S(1)} %broadcast_in_dim.10, bf16[16,512]{1,0:T(8,128)(2,1)S(1)} %multiply_convert_fusion, bf16[192,512]{1,0:T(8,128)(2,1)} %param.8), kind=kLoop, calls=%fused_computation.9 | loop fusion | flops 860160 | bytes 430080 | tf_op jit(solution)/shard_map/concatenate | solution.py:134
  4.7 1.3 %collective-permute-start.1 = (bf16[210,512]{1,0:T(8,128)(2,1)S(1)}, bf16[210,512]{1,0:T(8,128)(2,1)S(1)}, u32[]{:S(2)}, u32[]{:S(2)}) collective-permute-start(bf16[210,512]{1,0:T(8,128)(2,1)S(1)} %pad_maximum_fusion.1), channel_id=1, source_target_pairs={{4,0},{5,1},{6,2},{7,3},{8,4},{9,5},{10,6},{11,7},{12,8},{13,9},{1... | collective-permute-start | bytes 645128 | tf_op jit(solution)/shard_map/ppermute | solution.py:73
  6.0 5.6 %collective-permute-start = (bf16[210,512]{1,0:T(8,128)(2,1)S(1)}, bf16[210,512]{1,0:T(8,128)(2,1)S(1)}, u32[]{:S(2)}, u32[]{:S(2)}) collective-permute-start(bf16[210,512]{1,0:T(8,128)(2,1)S(1)} %pad_maximum_fusion.1), channel_id=1, source_target_pairs={{0,4},{1,5},{2,6},{3,7},{4,8},{5,9},{6,10},{7,11},{8,12},{9,13},{1... | collective-permute-start | bytes 645128 | tf_op jit(solution)/shard_map/ppermute | solution.py:72
  11.5 2.0 %collective-permute-start.6 = (bf16[210,512]{1,0:T(8,128)(2,1)S(1)}, bf16[210,512]{1,0:T(8,128)(2,1)S(1)}, u32[]{:S(2)}, u32[]{:S(2)}) collective-permute-start(bf16[210,512]{1,0:T(8,128)(2,1)S(1)} %pad_maximum_fusion.1), channel_id=1, source_target_pairs={{0,2},{1,3},{2,0},{3,1},{4,6},{5,7},{6,4},{7,5},{8,10},{9,11},{10,... | collective-permute-start | bytes 645128 | tf_op jit(solution)/shard_map/ppermute | solution.py:74
  13.6 1.6 %bitcast_dynamic-update-slice_fusion.13 = (bf16[8,210,512]{2,1,0:T(8,128)(2,1)S(1)}, bf16[16,210,512]{2,1,0:T(8,128)(2,1)}) fusion(bf16[1,512]{1,0:T(2,128)(2,1)S(1)} %broadcast_in_dim.11, bf16[1,512]{1,0:T(2,128)(2,1)S(1)} %broadcast_in_dim.10, bf16[16,512]{1,0:T(8,128)(2,1)S(1)} %multiply_convert_fusion, bf16[192,512]{1,0:T(8,128)(2,1)} %param.8), kind=kLoop, calls=%fused_computation.24 | loop fusion | flops 860158 | bytes 657408
  15.2 1.0 %collective-permute-done = bf16[210,512]{1,0:T(8,128)(2,1)S(1)} collective-permute-done((bf16[210,512]{1,0:T(8,128)(2,1)S(1)}, bf16[210,512]{1,0:T(8,128)(2,1)S(1)}, u32[]{:S(2)}, u32[]{:S(2)}) %collective-permute-start) | collective-permute-done | bytes 215072 | tf_op jit(solution)/shard_map/ppermute | solution.py:72
  16.2 1.7 %collective-permute-start.8 = (bf16[2,210,512]{2,1,0:T(8,128)(2,1)S(1)}, bf16[2,210,512]{2,1,0:T(8,128)(2,1)S(1)}, u32[]{:S(2)}, u32[]{:S(2)}) collective-permute-start(bf16[2,210,512]{2,1,0:T(8,128)(2,1)S(1)} %pad_maximum_fusion), channel_id=1, source_target_pairs={{0,2},{1,3},{2,0},{3,1},{4,6},{5,7},{6,4},{7,5},{8,10},{9,11},{10,... | collective-permute-start | bytes 1290248 | tf_op jit(solution)/shard_map/ppermute | solution.py:77
  18.0 1.3 %collective-permute-start.3 = (bf16[210,512]{1,0:T(8,128)(2,1)S(1)}, bf16[210,512]{1,0:T(8,128)(2,1)S(1)}, u32[]{:S(2)}, u32[]{:S(2)}) collective-permute-start(bf16[210,512]{1,0:T(8,128)(2,1)S(1)} %collective-permute-done.1), channel_id=1, source_target_pairs={{4,0},{5,1},{6,2},{7,3},{8,4},{9,5},{10,6},{11,7},{12,8},{13,9},{1... | collective-permute-start | bytes 645128 | tf_op jit(solution)/shard_map/ppermute | solution.py:76
  19.3 5.0 %collective-permute-start.2 = (bf16[210,512]{1,0:T(8,128)(2,1)S(1)}, bf16[210,512]{1,0:T(8,128)(2,1)S(1)}, u32[]{:S(2)}, u32[]{:S(2)}) collective-permute-start(bf16[210,512]{1,0:T(8,128)(2,1)S(1)} %collective-permute-done), channel_id=1, source_target_pairs={{0,4},{1,5},{2,6},{3,7},{4,8},{5,9},{6,10},{7,11},{8,12},{9,13},{1... | collective-permute-start | bytes 645128 | tf_op jit(solution)/shard_map/ppermute | solution.py:75
  24.3 0.8 bitcast_dynamic-update-slice_fusion.11
  25.1 1.2 %collective-permute-done.3 = bf16[210,512]{1,0:T(8,128)(2,1)S(1)} collective-permute-done((bf16[210,512]{1,0:T(8,128)(2,1)S(1)}, bf16[210,512]{1,0:T(8,128)(2,1)S(1)}, u32[]{:S(2)}, u32[]{:S(2)}) %collective-permute-start.3) | collective-permute-done | bytes 215072 | tf_op jit(solution)/shard_map/ppermute | solution.py:76
  26.3 1.4 %collective-permute-done.2 = bf16[210,512]{1,0:T(8,128)(2,1)S(1)} collective-permute-done((bf16[210,512]{1,0:T(8,128)(2,1)S(1)}, bf16[210,512]{1,0:T(8,128)(2,1)S(1)}, u32[]{:S(2)}, u32[]{:S(2)}) %collective-permute-start.2) | collective-permute-done | bytes 215072 | tf_op jit(solution)/shard_map/ppermute | solution.py:75
  28.3 1.3 %collective-permute-start.5 = (bf16[210,512]{1,0:T(8,128)(2,1)S(1)}, bf16[210,512]{1,0:T(8,128)(2,1)S(1)}, u32[]{:S(2)}, u32[]{:S(2)}) collective-permute-start(bf16[210,512]{1,0:T(8,128)(2,1)S(1)} %collective-permute-done.3), channel_id=1, source_target_pairs={{4,0},{5,1},{6,2},{7,3},{8,4},{9,5},{10,6},{11,7},{12,8},{13,9},{1... | collective-permute-start | bytes 645128 | tf_op jit(solution)/shard_map/ppermute | solution.py:80
  29.6 5.0 %collective-permute-start.4 = (bf16[210,512]{1,0:T(8,128)(2,1)S(1)}, bf16[210,512]{1,0:T(8,128)(2,1)S(1)}, u32[]{:S(2)}, u32[]{:S(2)}) collective-permute-start(bf16[210,512]{1,0:T(8,128)(2,1)S(1)} %collective-permute-done.2), channel_id=1, source_target_pairs={{0,4},{1,5},{2,6},{3,7},{4,8},{5,9},{6,10},{7,11},{8,12},{9,13},{1... | collective-permute-start | bytes 645128 | tf_op jit(solution)/shard_map/ppermute | solution.py:79
  34.7 0.7 bitcast_dynamic-update-slice_fusion.8
  35.4 1.2 %collective-permute-done.5 = bf16[210,512]{1,0:T(8,128)(2,1)S(1)} collective-permute-done((bf16[210,512]{1,0:T(8,128)(2,1)S(1)}, bf16[210,512]{1,0:T(8,128)(2,1)S(1)}, u32[]{:S(2)}, u32[]{:S(2)}) %collective-permute-start.5) | collective-permute-done | bytes 215072 | tf_op jit(solution)/shard_map/ppermute | solution.py:80
  36.5 1.5 %collective-permute-done.4 = bf16[210,512]{1,0:T(8,128)(2,1)S(1)} collective-permute-done((bf16[210,512]{1,0:T(8,128)(2,1)S(1)}, bf16[210,512]{1,0:T(8,128)(2,1)S(1)}, u32[]{:S(2)}, u32[]{:S(2)}) %collective-permute-start.4) | collective-permute-done | bytes 215072 | tf_op jit(solution)/shard_map/ppermute | solution.py:79
  38.0 1.7 %collective-permute-start.9 = (bf16[210,512]{1,0:T(8,128)(2,1)S(1)}, bf16[210,512]{1,0:T(8,128)(2,1)S(1)}, u32[]{:S(2)}, u32[]{:S(2)}) collective-permute-start(bf16[210,512]{1,0:T(8,128)(2,1)S(1)} %broadcast_select_fusion), channel_id=1, source_target_pairs={{0,2},{1,3},{2,0},{3,1},{4,6},{5,7},{6,4},{7,5},{8,10},{9,11},{10,... | collective-permute-start | bytes 645128 | tf_op jit(solution)/shard_map/ppermute | solution.py:83
  39.8 0.7 bitcast_dynamic-update-slice_fusion.6
  40.5 0.7 bitcast_dynamic-update-slice_fusion.5
  41.3 0.7 bitcast_dynamic-update-slice_fusion.3
  42.0 0.7 constant_dynamic-update-slice_fusion
  42.7 1.3 %collective-permute-done.9 = bf16[210,512]{1,0:T(8,128)(2,1)S(1)} collective-permute-done((bf16[210,512]{1,0:T(8,128)(2,1)S(1)}, bf16[210,512]{1,0:T(8,128)(2,1)S(1)}, u32[]{:S(2)}, u32[]{:S(2)}) %collective-permute-start.9) | collective-permute-done | bytes 215072 | tf_op jit(solution)/shard_map/ppermute | solution.py:83
  44.0 0.8 bitcast_dynamic-update-slice_fusion.1
  44.8 1.7 %copy.35 = bf16[8,210,512]{2,0,1:T(8,128)(2,1)} copy(bf16[8,210,512]{2,1,0:T(8,128)(2,1)S(1)} %get-tuple-element.14) | data formatting | bytes 3440640 | tf_op jit(solution)/shard_map/stack | solution.py:91
  46.5 0.8 copy.40
  47.5 0.9 copy.41.no_ref
  48.3 0.9 copy.42.ro_ref
  49.4 0.9 %collective-permute-done.10 = bf16[8,210,512]{2,0,1:T(8,128)(2,1)S(1)} collective-permute-done((bf16[8,210,512]{2,0,1:T(8,128)(2,1)}, bf16[8,210,512]{2,0,1:T(8,128)(2,1)S(1)}, u32[]{:S(2)}, u32[]{:S(2)}) %collective-permute-start.10) | collective-permute-done | bytes 1720352 | tf_op jit(solution)/shard_map/ppermute | solution.py:102
  50.4 1.8 %copy_dynamic-update-slice_fusion.xc_ref.wc_ref = bf16[16,210,512]{2,1,0:T(8,128)(2,1)} fusion(bf16[16,210,512]{2,1,0:T(8,128)(2,1)} %get-tuple-element.15, bf16[8,210,512]{2,0,1:T(8,128)(2,1)S(1)} %collective-permute-done.10), kind=kLoop, calls=%fused_computation.2 | loop fusion | bytes 3489792 | tf_op jit(solution)/shard_map/concatenate | solution.py:103
  52.1 0.8 slice_convert_fusion.1
  52.9 2.6 %multiply_reduce_fusion = f32[16,512]{1,0:T(8,128)S(1)} fusion(bf16[16,210,512]{2,1,0:T(8,128)(2,1)} %copy_dynamic-update-slice_fusion.xc_ref.wc_ref), kind=kLoop, calls=%fused_computation.1 | loop fusion | flops 4710400 | bytes 3178496 | tf_op jit(solution)/shard_map/reduce_sum | solution.py:155
  55.5 1.5 %fusion.1.rc_ref = f32[16,1,512]{2,1,0:T(1,128)} fusion(bf16[16,210,512]{2,1,0:T(8,128)(2,1)} %copy_dynamic-update-slice_fusion.xc_ref.wc_ref), kind=kLoop, calls=%fused_computation.33 | loop fusion | flops 16384 | bytes 49152 | tf_op jit(solution)/shard_map/div | solution.py:156
  58.6 1.2 %gather_fusion = s32[16]{0:T(128)} fusion(s32[8]{0:T(128)S(1)} %convert_element_type.31, s32[1024]{0:T(1024)S(1)} %pad_clamp_fusion), kind=kCustom, calls=%fused_computation | custom fusion | bytes 192 | tf_op jit(solution)/shard_map/gather | solution.py:153
  59.8 15.1 %shard_map.95 = f32[16,512]{1,0:T(8,128)} custom-call(s32[16]{0:T(128)} %gather_fusion, bf16[512,192]{1,0:T(8,128)(2,1)} %bitcast.67, f32[512,1]{1,0:T(8,128)} %copy.41.no_ref, f32[512,1]{1,0:T(8,128)} %copy.42.ro_ref, bf16[16,210,512]{2,1,0:T(8,128)(2,1)} %copy_dynamic-update-slice_fusion.xc_ref.wc_ref, f32[16,1,512]{2,1,0:T(1,128)} %broadcast_in_dim.26.nc_ref, ...), custom_call_target="tpu_custom_call" | custom-call | tf_op jit(solution)/shard_map/pallas_call | solution.py:52
  74.9 0.9 convolution_bitcast_fusion
  75.9 1.0 %collective-permute-done.11 = f32[16,16]{0,1:T(8,128)S(1)} collective-permute-done((f32[16,16]{0,1:T(8,128)S(1)}, f32[16,16]{0,1:T(8,128)S(1)}, u32[]{:S(2)}, u32[]{:S(2)}) %collective-permute-start.11) | collective-permute-done | bytes 1056 | tf_op jit(solution)/shard_map/ppermute | solution.py:112
  77.0 0.7 collective-permute-start.12
  77.7 2.9 %collective-permute-done.12 = f32[16,16]{0,1:T(8,128)S(1)} collective-permute-done((f32[16,16]{0,1:T(8,128)S(1)}, f32[16,16]{0,1:T(8,128)S(1)}, u32[]{:S(2)}, u32[]{:S(2)}) %collective-permute-start.12) | collective-permute-done | bytes 1056 | tf_op jit(solution)/shard_map/ppermute | solution.py:112
  80.6 2.0 %collective-permute-start.13 = (f32[16,16]{0,1:T(8,128)S(1)}, f32[16,16]{0,1:T(8,128)S(1)}, u32[]{:S(2)}, u32[]{:S(2)}) collective-permute-start(f32[16,16]{0,1:T(8,128)S(1)} %add.70), channel_id=1, source_target_pairs={{0,4},{1,5},{2,6},{3,7},{4,0},{5,1},{6,2},{7,3},{8,12},{9,13},{10,... | collective-permute-start | bytes 3080 | tf_op jit(solution)/shard_map/ppermute | solution.py:112
  82.7 1.6 %collective-permute-done.13 = f32[16,16]{0,1:T(8,128)S(1)} collective-permute-done((f32[16,16]{0,1:T(8,128)S(1)}, f32[16,16]{0,1:T(8,128)S(1)}, u32[]{:S(2)}, u32[]{:S(2)}) %collective-permute-start.13) | collective-permute-done | bytes 1056 | tf_op jit(solution)/shard_map/ppermute | solution.py:112
  84.3 3.8 %collective-permute-start.14 = (f32[16,16]{0,1:T(8,128)S(1)}, f32[16,16]{0,1:T(8,128)S(1)}, u32[]{:S(2)}, u32[]{:S(2)}) collective-permute-start(f32[16,16]{0,1:T(8,128)S(1)} %add.71), channel_id=1, source_target_pairs={{0,8},{1,9},{2,10},{3,11},{4,12},{5,13},{6,14},{7,15},{8,0},{9,1},... | collective-permute-start | bytes 3080 | tf_op jit(solution)/shard_map/ppermute | solution.py:112
  88.3 1.5 %collective-permute-done.14 = f32[16,16]{0,1:T(8,128)S(1)} collective-permute-done((f32[16,16]{0,1:T(8,128)S(1)}, f32[16,16]{0,1:T(8,128)S(1)}, u32[]{:S(2)}, u32[]{:S(2)}) %collective-permute-start.14) | collective-permute-done | bytes 1056 | tf_op jit(solution)/shard_map/ppermute | solution.py:112
  89.7 0.7 copy.43
  90.4 1.5 %fusion = f32[16,512]{1,0:T(8,128)} fusion(f32[16,512]{1,0:T(8,128)S(1)} %fusion.14, f32[16,16]{0,1:T(8,128)S(1)} %add_multiply_fusion, f32[16,512]{1,0:T(8,128)S(1)} %copy-done.2, f32[16,512]{1,0:T(8,128)} %shard_map.95, f32[512]{0:T(512)S(1)} %broadcast_multiply_fusion), kind=kOutput, calls=%fused_computation.4 | convolution fusion | flops 1597440 | bytes 134144 | tf_op jit(solution)/shard_map/dot_general | solution.py:168
  (54 shorter events, 3.3 us)
Async XLA Ops:
  0.6 87.5 %copy-start = (f32[16,512]{1,0:T(8,128)S(1)}, f32[16,512]{1,0:T(8,128)}, u32[]{:S(2)}) copy-start(f32[16,512]{1,0:T(8,128)} %param.12) | copy-start | bytes 98308
  4.7 10.5 %collective-permute-start.1 = (bf16[210,512]{1,0:T(8,128)(2,1)S(1)}, bf16[210,512]{1,0:T(8,128)(2,1)S(1)}, u32[]{:S(2)}, u32[]{:S(2)}) collective-permute-start(bf16[210,512]{1,0:T(8,128)(2,1)S(1)} %pad_maximum_fusion.1), channel_id=1, source_target_pairs={{4,0},{5,1},{6,2},{7,3},{8,4},{9,5},{10,6},{11,7},{12,8},{13,9},{1... | collective-permute-start | bytes 645128 | tf_op jit(solution)/shard_map/ppermute | solution.py:73
  6.0 10.2 %collective-permute-start = (bf16[210,512]{1,0:T(8,128)(2,1)S(1)}, bf16[210,512]{1,0:T(8,128)(2,1)S(1)}, u32[]{:S(2)}, u32[]{:S(2)}) collective-permute-start(bf16[210,512]{1,0:T(8,128)(2,1)S(1)} %pad_maximum_fusion.1), channel_id=1, source_target_pairs={{0,4},{1,5},{2,6},{3,7},{4,8},{5,9},{6,10},{7,11},{8,12},{9,13},{1... | collective-permute-start | bytes 645128 | tf_op jit(solution)/shard_map/ppermute | solution.py:72
  11.5 29.0 %collective-permute-start.6 = (bf16[210,512]{1,0:T(8,128)(2,1)S(1)}, bf16[210,512]{1,0:T(8,128)(2,1)S(1)}, u32[]{:S(2)}, u32[]{:S(2)}) collective-permute-start(bf16[210,512]{1,0:T(8,128)(2,1)S(1)} %pad_maximum_fusion.1), channel_id=1, source_target_pairs={{0,2},{1,3},{2,0},{3,1},{4,6},{5,7},{6,4},{7,5},{8,10},{9,11},{10,... | collective-permute-start | bytes 645128 | tf_op jit(solution)/shard_map/ppermute | solution.py:74
  16.2 25.7 %collective-permute-start.8 = (bf16[2,210,512]{2,1,0:T(8,128)(2,1)S(1)}, bf16[2,210,512]{2,1,0:T(8,128)(2,1)S(1)}, u32[]{:S(2)}, u32[]{:S(2)}) collective-permute-start(bf16[2,210,512]{2,1,0:T(8,128)(2,1)S(1)} %pad_maximum_fusion), channel_id=1, source_target_pairs={{0,2},{1,3},{2,0},{3,1},{4,6},{5,7},{6,4},{7,5},{8,10},{9,11},{10,... | collective-permute-start | bytes 1290248 | tf_op jit(solution)/shard_map/ppermute | solution.py:77
  18.0 8.3 %collective-permute-start.3 = (bf16[210,512]{1,0:T(8,128)(2,1)S(1)}, bf16[210,512]{1,0:T(8,128)(2,1)S(1)}, u32[]{:S(2)}, u32[]{:S(2)}) collective-permute-start(bf16[210,512]{1,0:T(8,128)(2,1)S(1)} %collective-permute-done.1), channel_id=1, source_target_pairs={{4,0},{5,1},{6,2},{7,3},{8,4},{9,5},{10,6},{11,7},{12,8},{13,9},{1... | collective-permute-start | bytes 645128 | tf_op jit(solution)/shard_map/ppermute | solution.py:76
  19.3 8.5 %collective-permute-start.2 = (bf16[210,512]{1,0:T(8,128)(2,1)S(1)}, bf16[210,512]{1,0:T(8,128)(2,1)S(1)}, u32[]{:S(2)}, u32[]{:S(2)}) collective-permute-start(bf16[210,512]{1,0:T(8,128)(2,1)S(1)} %collective-permute-done), channel_id=1, source_target_pairs={{0,4},{1,5},{2,6},{3,7},{4,8},{5,9},{6,10},{7,11},{8,12},{9,13},{1... | collective-permute-start | bytes 645128 | tf_op jit(solution)/shard_map/ppermute | solution.py:75
  27.8 13.5 %collective-permute-start.7 = (bf16[210,512]{1,0:T(8,128)(2,1)S(1)}, bf16[210,512]{1,0:T(8,128)(2,1)S(1)}, u32[]{:S(2)}, u32[]{:S(2)}) collective-permute-start(bf16[210,512]{1,0:T(8,128)(2,1)S(1)} %broadcast_select_fusion.1), channel_id=1, source_target_pairs={{0,2},{1,3},{2,0},{3,1},{4,6},{5,7},{6,4},{7,5},{8,10},{9,11},{10,... | collective-permute-start | bytes 645128 | tf_op jit(solution)/shard_map/ppermute | solution.py:81
  28.3 8.3 %collective-permute-start.5 = (bf16[210,512]{1,0:T(8,128)(2,1)S(1)}, bf16[210,512]{1,0:T(8,128)(2,1)S(1)}, u32[]{:S(2)}, u32[]{:S(2)}) collective-permute-start(bf16[210,512]{1,0:T(8,128)(2,1)S(1)} %collective-permute-done.3), channel_id=1, source_target_pairs={{4,0},{5,1},{6,2},{7,3},{8,4},{9,5},{10,6},{11,7},{12,8},{13,9},{1... | collective-permute-start | bytes 645128 | tf_op jit(solution)/shard_map/ppermute | solution.py:80
  29.6 8.5 %collective-permute-start.4 = (bf16[210,512]{1,0:T(8,128)(2,1)S(1)}, bf16[210,512]{1,0:T(8,128)(2,1)S(1)}, u32[]{:S(2)}, u32[]{:S(2)}) collective-permute-start(bf16[210,512]{1,0:T(8,128)(2,1)S(1)} %collective-permute-done.2), channel_id=1, source_target_pairs={{0,4},{1,5},{2,6},{3,7},{4,8},{5,9},{6,10},{7,11},{8,12},{9,13},{1... | collective-permute-start | bytes 645128 | tf_op jit(solution)/shard_map/ppermute | solution.py:79
  38.0 6.0 %collective-permute-start.9 = (bf16[210,512]{1,0:T(8,128)(2,1)S(1)}, bf16[210,512]{1,0:T(8,128)(2,1)S(1)}, u32[]{:S(2)}, u32[]{:S(2)}) collective-permute-start(bf16[210,512]{1,0:T(8,128)(2,1)S(1)} %broadcast_select_fusion), channel_id=1, source_target_pairs={{0,2},{1,3},{2,0},{3,1},{4,6},{5,7},{6,4},{7,5},{8,10},{9,11},{10,... | collective-permute-start | bytes 645128 | tf_op jit(solution)/shard_map/ppermute | solution.py:83
  39.8 6.7 %copy-start.1 = (bf16[192,512]{1,0:T(8,128)(2,1)S(1)}, bf16[192,512]{1,0:T(8,128)(2,1)}, u32[]{:S(2)}) copy-start(bf16[192,512]{1,0:T(8,128)(2,1)} %param.8) | copy-start | bytes 589828
  41.2 7.1 %copy-start.5 = (bf16[512]{0:T(512)(128)(2,1)S(1)}, bf16[512]{0:T(512)(128)(2,1)}, u32[]{:S(2)}) copy-start(bf16[512]{0:T(512)(128)(2,1)} %param.9) | copy-start | bytes 3076
  41.3 8.2 %copy-start.4 = (f32[512]{0:T(512)S(1)}, f32[512]{0:T(512)}, u32[]{:S(2)}) copy-start(f32[512]{0:T(512)} %param.10) | copy-start | bytes 6148
  46.5 3.8 %collective-permute-start.10 = (bf16[8,210,512]{2,0,1:T(8,128)(2,1)}, bf16[8,210,512]{2,0,1:T(8,128)(2,1)S(1)}, u32[]{:S(2)}, u32[]{:S(2)}) collective-permute-start(bf16[8,210,512]{2,0,1:T(8,128)(2,1)} %copy.35), channel_id=1, source_target_pairs={{0,1},{1,0},{2,3},{3,2},{4,5},{5,4},{6,7},{7,6},{8,9},{9,8},{10,11... | collective-permute-start | bytes 5160968 | tf_op jit(solution)/shard_map/ppermute | solution.py:102
  59.8 15.1 %copy-start.2 = (f32[16,512]{1,0:T(8,128)S(1)}, f32[16,512]{1,0:T(8,128)}, u32[]{:S(2)}) copy-start(f32[16,512]{1,0:T(8,128)} %param.11) | copy-start | bytes 98308
  59.8 28.3 %copy-start.3 = (f32[16,16]{1,0:T(8,128)S(1)}, f32[16,16]{1,0:T(8,128)}, u32[]{:S(2)}) copy-start(f32[16,16]{1,0:T(8,128)} %param.13) | copy-start | bytes 3076
  75.8 1.2 %collective-permute-start.11 = (f32[16,16]{0,1:T(8,128)S(1)}, f32[16,16]{0,1:T(8,128)S(1)}, u32[]{:S(2)}, u32[]{:S(2)}) collective-permute-start(f32[16,16]{0,1:T(8,128)S(1)} %convolution_bitcast_fusion), channel_id=1, source_target_pairs={{0,1},{1,0},{2,3},{3,2},{4,5},{5,4},{6,7},{7,6},{8,9},{9,8},{10,11... | collective-permute-start | bytes 3080 | tf_op jit(solution)/shard_map/ppermute | solution.py:112
  77.0 3.7 %collective-permute-start.12 = (f32[16,16]{0,1:T(8,128)S(1)}, f32[16,16]{0,1:T(8,128)S(1)}, u32[]{:S(2)}, u32[]{:S(2)}) collective-permute-start(f32[16,16]{0,1:T(8,128)S(1)} %add.69), channel_id=1, source_target_pairs={{0,2},{1,3},{2,0},{3,1},{4,6},{5,7},{6,4},{7,5},{8,10},{9,11},{10,... | collective-permute-start | bytes 3080 | tf_op jit(solution)/shard_map/ppermute | solution.py:112
  80.6 3.7 %collective-permute-start.13 = (f32[16,16]{0,1:T(8,128)S(1)}, f32[16,16]{0,1:T(8,128)S(1)}, u32[]{:S(2)}, u32[]{:S(2)}) collective-permute-start(f32[16,16]{0,1:T(8,128)S(1)} %add.70), channel_id=1, source_target_pairs={{0,4},{1,5},{2,6},{3,7},{4,0},{5,1},{6,2},{7,3},{8,12},{9,13},{10,... | collective-permute-start | bytes 3080 | tf_op jit(solution)/shard_map/ppermute | solution.py:112
  84.3 5.4 %collective-permute-start.14 = (f32[16,16]{0,1:T(8,128)S(1)}, f32[16,16]{0,1:T(8,128)S(1)}, u32[]{:S(2)}, u32[]{:S(2)}) collective-permute-start(f32[16,16]{0,1:T(8,128)S(1)} %add.71), channel_id=1, source_target_pairs={{0,8},{1,9},{2,10},{3,11},{4,12},{5,13},{6,14},{7,15},{8,0},{9,1},... | collective-permute-start | bytes 3080 | tf_op jit(solution)/shard_map/ppermute | solution.py:112

commit v4 on v3

v4 whole, which is shorter than its diff:
```python
import functools
import math

import jax
import jax.numpy as jnp
from jax import lax
from jax.experimental import pallas as pl
from jax.experimental.pallas import tpu as pltpu
from jax.sharding import PartitionSpec as P

LANCZOS = 16
BLK = 1024


HIGHEST = lax.Precision.HIGHEST


def piece_kernel(width, rows, shapes, sel_ref, xo_ref, no_ref, ro_ref, *refs):
    out_ref = refs[-1]
    views = []
    for ref, shape in zip(refs[:-1], shapes):
        views += [ref.at[i * rows : (i + 1) * rows, :] for i in range(shape[0] // rows)]
    for slot, piece in enumerate(views):

        @pl.when(sel_ref[slot] != 0)
        def _():
            x_cols = piece[:width, :]
            x_wide = x_cols.astype(jnp.float32)
            norm_cols = jnp.sum(x_wide * x_wide, axis=0, keepdims=True)
            recip_cols = 1.0 / piece[width + LANCZOS : width + LANCZOS + 1, :].astype(jnp.float32)
            inner = jnp.dot(xo_ref[...], x_cols, preferred_element_type=jnp.float32)
            distance = (no_ref[...] + norm_cols) - 2.0 * inner
            weights = jnp.exp(-distance * (ro_ref[...] * recip_cols)).astype(jnp.bfloat16)
            out_ref[slot] = lax.dot_general(
                piece[width : width + LANCZOS, :],
                weights,
                (((1,), (1,)), ((), ())),
                preferred_element_type=jnp.float32,
            )

        @pl.when(sel_ref[slot] == 0)
        def _():
            out_ref[slot] = jnp.zeros(out_ref.shape[1:], jnp.float32)


def piece_products(sel, own_terms, pieces, width, rows):
    x_own_t, norm_own, recip_own = own_terms
    own = x_own_t.shape[0]
    shapes = [p.shape for p in pieces]
    slots = sum(sh[0] // rows for sh in shapes)
    vmem = pl.BlockSpec(memory_space=pltpu.VMEM)
    return pl.pallas_call(
        functools.partial(piece_kernel, width, rows, shapes),
        in_specs=[pl.BlockSpec(memory_space=pltpu.SMEM)] + [vmem] * (3 + len(pieces)),
        out_specs=vmem,
        out_shape=jax.ShapeDtypeStruct((slots, LANCZOS, own), jnp.float32),
    )(sel.astype(jnp.int32), x_own_t, norm_own, recip_own, *pieces)


def gather_products(packed, own_terms, width):
    devices = lax.axis_size("row")
    me = lax.axis_index("row")
    rows = packed.shape[0]
    if devices != 16:
        pieces = lax.all_gather(packed, "row", axis=0, tiled=True)
        sel = jnp.ones((devices,), jnp.int32)
        parts = piece_products(sel, own_terms, [pieces], width, rows)
        return [parts], [jnp.arange(devices, dtype=jnp.int32)], [sel], [pieces]
    up = [(r, r + 4) for r in range(12)]
    down = [(r, r - 4) for r in range(4, 16)]
    across = [(r, r ^ 2) for r in range(16)]
    twin = [(r, r ^ 1) for r in range(16)]
    z = me // 4
    partner = me ^ 2
    ends = (z == 0) | (z == 3)
    one = jnp.ones((), bool)

    def run(pieces, sel, origin):
        sel = jnp.stack(sel).astype(jnp.int32)
        return piece_products(sel, own_terms, pieces, width, rows), jnp.stack(origin).astype(jnp.int32), sel

    results = [run([packed], [one], [me])]
    up1 = lax.ppermute(packed, "row", up)
    down1 = lax.ppermute(packed, "row", down)
    across1 = lax.ppermute(packed, "row", across)
    results.append(run([up1, down1, across1], [z >= 1, z <= 2, one], [me - 4, me + 4, partner]))
    up2 = lax.ppermute(up1, "row", up)
    down2 = lax.ppermute(down1, "row", down)
    across2 = lax.ppermute(jnp.concatenate([up1, down1]), "row", across)
    results.append(run(
        [up2, down2, across2],
        [z >= 2, z <= 1, z >= 1, z <= 2],
        [me - 8, me + 8, partner - 4, partner + 4],
    ))
    pick2 = jnp.where(z >= 2, up2, down2)
    up3 = lax.ppermute(up2, "row", up)
    down3 = lax.ppermute(down2, "row", down)
    across3 = lax.ppermute(pick2, "row", across)
    results.append(run(
        [up3, down3, across3],
        [z == 3, z == 0, one],
        [me - 12, me + 12, jnp.where(z >= 2, partner - 8, partner + 8)],
    ))
    pick3 = jnp.where(z == 3, up3, down3)
    across4 = lax.ppermute(pick3, "row", across)
    results.append(run([across4], [ends], [jnp.where(z == 3, partner - 12, partner + 12)]))

    line1 = jnp.where(z >= 1, up1, down1)
    line2 = jnp.where(z >= 2, up2, jnp.where(z == 1, down1, down2))
    line3 = jnp.where(z == 3, up3, jnp.where(z == 2, down1, jnp.where(z == 1, down2, down3)))
    other2 = jnp.where(z >= 1, across2[:rows], across2[rows:])
    other3 = jnp.where(ends, across4, across2[rows:])
    mine = jnp.concatenate([packed, line1, line2, line3, across1, across3, other2, other3])
    origin = jnp.stack([
        me,
        jnp.where(z >= 1, me - 4, me + 4),
        jnp.where(z >= 2, me - 8, jnp.where(z == 1, me + 4, me + 8)),
        jnp.where(z == 3, me - 12, jnp.where(z == 2, me + 4, jnp.where(z == 1, me + 8, me + 12))),
        partner,
        jnp.where(z >= 2, partner - 8, partner + 8),
        jnp.where(z >= 1, partner - 4, partner + 4),
        jnp.where(z == 3, partner - 12, jnp.where(z == 0, partner + 12, partner + 4)),
    ]).astype(jnp.int32)
    theirs = lax.ppermute(mine, "row", twin)
    results.append(run([theirs], [one] * 8, list(origin ^ 1)))
    parts, origins, sels = zip(*results)
    return list(parts), list(origins), list(sels), [mine, theirs]


def sum_over_rows(value):
    devices = lax.axis_size("row")
    if devices & (devices - 1):
        return lax.psum(value, "row")
    stride = 1
    while stride < devices:
        value = value + lax.ppermute(value, "row", [(i, i ^ stride) for i in range(devices)])
        stride *= 2
    return value


def shards(
    embeddings,
    local_scale,
    degree_scale,
    lanczos_block,
    previous_block,
    previous_coupling,
    tile_plan,
    tile_counts,
):
    width, own = embeddings.shape
    devices = lax.axis_size("row")
    total_rows = devices * own
    slots = tile_plan.shape[0]
    weighted = (degree_scale[None, :] * lanczos_block).astype(jnp.bfloat16)
    plan_row = jnp.concatenate([tile_plan.reshape(-1), tile_counts]).astype(jnp.bfloat16)
    plan_row = jnp.pad(plan_row, (0, own - plan_row.shape[0]))
    packed = jnp.concatenate(
        [embeddings, weighted, local_scale[None, :], plan_row[None, :]], axis=0
    )
    packed = jnp.pad(packed, ((0, -packed.shape[0] % 16), (0, 0)))
    x_own_t = embeddings.T
    norm_own = jnp.sum(jnp.square(embeddings.astype(jnp.float32)), axis=0)[:, None]
    recip_own = (1.0 / local_scale.astype(jnp.float32))[:, None]
    parts, origins, sels, pieces = gather_products(packed, (x_own_t, norm_own, recip_own), width)

    plans = jnp.concatenate(
        [p.reshape(-1, packed.shape[0], own)[:, width + LANCZOS + 1, : 2 * slots + 1] for p in pieces]
    ).astype(jnp.int32)
    counts = plans[:, 2 * slots]
    pairs = plans[:, : 2 * slots].reshape(devices, slots, 2)
    live = jnp.arange(slots, dtype=jnp.int32)[None, :] < counts[:, None]
    row_block = pairs[..., 0].reshape(-1)
    col_block = pairs[..., 1].reshape(-1)
    live = live.reshape(-1)
    my_block = (lax.axis_index("row") * own) // BLK
    block_ids = jnp.arange(total_rows // BLK, dtype=jnp.int32)
    hit = live[:, None] & (
        ((row_block[:, None] == my_block) & (col_block[:, None] == block_ids[None, :]))
        | ((col_block[:, None] == my_block) & (row_block[:, None] == block_ids[None, :]))
    )
    mask_row = jnp.any(hit, axis=0)

    summed = jnp.zeros((LANCZOS, own), jnp.float32)
    for part, origin, sel in zip(parts, origins, sels):
        source = jnp.clip(origin, 0, devices - 1)
        keep = (sel != 0) & mask_row[(source * own) // BLK]
        summed = summed + jnp.sum(jnp.where(keep[:, None, None], part, 0.0), axis=0)
    scaled = summed * (degree_scale[None, :] / math.sqrt(total_rows))
    partial_value = lax.dot_general(
        lanczos_block, scaled, (((1,), (1,)), ((), ())), precision=HIGHEST
    )
    coupling = sum_over_rows(partial_value) / total_rows
    projected = lax.dot_general(
        coupling, lanczos_block, (((0,), (0,)), ((), ())), precision=HIGHEST
    )
    result = scaled - projected - jnp.dot(previous_coupling, previous_block, precision=HIGHEST)
    return (result, coupling)


def solution(mesh):
    in_specs = (
        P(None, ("cohort", "row")),
        P(("cohort", "row")),
        P(("cohort", "row")),
        P(None, ("cohort", "row")),
        P(None, ("cohort", "row")),
        P("cohort", None),
        P(("cohort", "row"), None),
        P(("cohort", "row")),
    )
    out_specs = (P(None, ("cohort", "row")), P("cohort", None))
    return jax.shard_map(shards, mesh=mesh, in_specs=in_specs, out_specs=out_specs, check_vma=False)
```

time: 93 us -> 99.6 us (1.071)
  Pallas kernels: 15.1 us -> 22.5 us
  other arithmetic: 11.9 us -> 14.2 us
  local copies, waits for them, and re-layouts: 13.2 us -> 11.1 us
  matrix products: 2.58 us -> 1.06 us
    pallas_call x1 -> x6, Pallas kernels: 15.1 us -> 22.5 us  [piece_products(): pl.pallas_call(functools.partial(piece_kernel, width, rows, shapes), in_s...]
    gather x1 -> x5, local copies, waits for them, and re-layouts: 1.17 us -> 3.24 us  [shards(): keep = (sel != 0) & mask_row[source * own // BLK]]
    concatenate x2 -> x0, local copies, waits for them, and re-layouts: 1.88 us -> none  [the longest x1 1.77 us: gather_pieces(): jnp.concatenate([mine, theirs])]
    unnamed x5 -> x2, other arithmetic: 3.34 us -> 1.5 us
    select_n x3 -> x6, other arithmetic: 0.08 us -> 1.91 us  [the longest x1 0.83 us: gather_products(): pick3 = jnp.where(z == 3, up3, down3)]
    and x0 -> x3, other arithmetic: none -> 1.77 us  [shards(): keep = (sel != 0) & mask_row[source * own // BLK]]
    div x1 -> x0, other arithmetic: 1.55 us -> none  [shards(): 1.0 / pieces[:, width + LANCZOS].astype(jnp.float32)]
    reduce_sum x1 -> x4, other arithmetic: 2.56 us -> 4 us  [shards(): summed = summed + jnp.sum(jnp.where(keep[:, None, None], part, 0.0), axis=0)]
  transfers between devices with their start and end apart: 15 -> 15, of which waited for: 11 -> 11; matrix products, arithmetic and copies ran while one was open for 10% -> 9% of each run, Pallas kernels for 0% -> 5%
where the time goes in v4:
time: 99.6 us; the launch traced here: 98.8 us
  starting transfers between devices  31.3 us (31%)
  Pallas kernels  22.5 us (23%)
  waiting for transfers between devices  16.5 us (17%)
  other arithmetic  14.2 us (14%)
  local copies, waits for them, and re-layouts  11.1 us (11%)
  between operations  2.22 us (2%)
  matrix products  1.06 us (1%)
    pallas_call x6, Pallas kernels, piece_products(): pl.pallas_call(functools.partial(piece_kernel, width, rows, shapes), in_s...  22.5 us
    ppermute x4, starting transfers between devices, sum_over_rows(): lax.ppermute(value, 'row', [(i, i ^ stride) for i in range(devices)])  7.14 us
    ppermute x4, waiting for transfers between devices, sum_over_rows(): lax.ppermute(value, 'row', [(i, i ^ stride) for i in range(devices)])  6.55 us
    ppermute x1, starting transfers between devices, gather_products(): up1 = lax.ppermute(packed, 'row', up)  5.57 us
    ppermute x1, starting transfers between devices, gather_products(): up2 = lax.ppermute(up1, 'row', up)  5.03 us
    ppermute x1, starting transfers between devices, gather_products(): up3 = lax.ppermute(up2, 'row', up)  4.54 us
    reduce_sum x4, other arithmetic, shards(): summed = summed + jnp.sum(jnp.where(keep[:, None, None], part, 0.0), axis=0)  4 us
    gather x5, local copies, waits for them, and re-layouts, shards(): keep = (sel != 0) & mask_row[source * own // BLK]  3.24 us
  transfers between devices with their start and end apart: 15, of which 11 were waited for; matrix products, arithmetic and copies ran while one was open for 9% of the time, Pallas kernels for 5%

profile of v4, /device:TPU:0, one launch (start us, length us, event | category | flops | bytes accessed | tf_op | source)
XLA Modules:
  0.0 98.8 jit_solution(17861646430828550527)
XLA Ops:
  0.6 0.7 convert.8
  3.0 0.8 multiply_convert_fusion
  3.7 1.6 %fusion.7 = (bf16[224,512]{1,0:T(8,128)(2,1)S(1)}, bf16[1792,512]{1,0:T(8,128)(2,1)}) fusion(bf16[1,512]{1,0:T(2,128)(2,1)S(1)} %broadcast_in_dim.98, bf16[1,512]{1,0:T(2,128)(2,1)S(1)} %broadcast_in_dim.97, bf16[16,512]{1,0:T(8,128)(2,1)S(1)} %multiply_convert_fusion, bf16[192,512]{1,0:T(8,128)(2,1)} %param.8), kind=kLoop, calls=%fused_computation.17 | loop fusion | flops 1490943 | bytes 673792 | tf_op jit(solution)/shard_map/concatenate | solution.py:158
  5.4 1.3 %collective-permute-start.1 = (bf16[224,512]{1,0:T(8,128)(2,1)S(1)}, bf16[224,512]{1,0:T(8,128)(2,1)S(1)}, u32[]{:S(2)}, u32[]{:S(2)}) collective-permute-start(bf16[224,512]{1,0:T(8,128)(2,1)S(1)} %get-tuple-element.40.refs_0_), channel_id=1, source_target_pairs={{4,0},{5,1},{6,2},{7,3},{8,4},{9,5},{10,6},{11,7},{12,8},{13,9},{1... | collective-permute-start | bytes 688136 | tf_op jit(solution)/shard_map/ppermute | solution.py:84
  6.7 5.6 %collective-permute-start = (bf16[224,512]{1,0:T(8,128)(2,1)S(1)}, bf16[224,512]{1,0:T(8,128)(2,1)S(1)}, u32[]{:S(2)}, u32[]{:S(2)}) collective-permute-start(bf16[224,512]{1,0:T(8,128)(2,1)S(1)} %get-tuple-element.40.refs_0_), channel_id=1, source_target_pairs={{0,4},{1,5},{2,6},{3,7},{4,8},{5,9},{6,10},{7,11},{8,12},{9,13},{1... | collective-permute-start | bytes 688136 | tf_op jit(solution)/shard_map/ppermute | solution.py:83
  12.2 2.0 %collective-permute-start.6 = (bf16[224,512]{1,0:T(8,128)(2,1)S(1)}, bf16[224,512]{1,0:T(8,128)(2,1)S(1)}, u32[]{:S(2)}, u32[]{:S(2)}) collective-permute-start(bf16[224,512]{1,0:T(8,128)(2,1)S(1)} %get-tuple-element.40.refs_0_), channel_id=1, source_target_pairs={{0,2},{1,3},{2,0},{3,1},{4,6},{5,7},{6,4},{7,5},{8,10},{9,11},{10,... | collective-permute-start | bytes 688136 | tf_op jit(solution)/shard_map/ppermute | solution.py:85
  14.3 1.6 %collective-permute-done.1.refs_1_ = bf16[224,512]{1,0:T(8,128)(2,1)S(1)} collective-permute-done((bf16[224,512]{1,0:T(8,128)(2,1)S(1)}, bf16[224,512]{1,0:T(8,128)(2,1)S(1)}, u32[]{:S(2)}, u32[]{:S(2)}) %collective-permute-start.1) | collective-permute-done | bytes 229408 | tf_op jit(solution)/shard_map/ppermute | solution.py:84
  15.9 1.2 %collective-permute-done.refs_0_ = bf16[224,512]{1,0:T(8,128)(2,1)S(1)} collective-permute-done((bf16[224,512]{1,0:T(8,128)(2,1)S(1)}, bf16[224,512]{1,0:T(8,128)(2,1)S(1)}, u32[]{:S(2)}, u32[]{:S(2)}) %collective-permute-start) | collective-permute-done | bytes 229408 | tf_op jit(solution)/shard_map/ppermute | solution.py:83
  17.1 1.7 %collective-permute-start.8 = (bf16[448,512]{1,0:T(8,128)(2,1)S(1)}, bf16[448,512]{1,0:T(8,128)(2,1)S(1)}, u32[]{:S(2)}, u32[]{:S(2)}) collective-permute-start(bf16[448,512]{1,0:T(8,128)(2,1)S(1)} %pad_maximum_fusion), channel_id=1, source_target_pairs={{0,2},{1,3},{2,0},{3,1},{4,6},{5,7},{6,4},{7,5},{8,10},{9,11},{10,... | collective-permute-start | bytes 1376264 | tf_op jit(solution)/shard_map/ppermute | solution.py:89
  18.8 1.3 %collective-permute-start.3 = (bf16[224,512]{1,0:T(8,128)(2,1)S(1)}, bf16[224,512]{1,0:T(8,128)(2,1)S(1)}, u32[]{:S(2)}, u32[]{:S(2)}) collective-permute-start(bf16[224,512]{1,0:T(8,128)(2,1)S(1)} %collective-permute-done.1.refs_1_), channel_id=1, source_target_pairs={{4,0},{5,1},{6,2},{7,3},{8,4},{9,5},{10,6},{11,7},{12,8},{13,9},{1... | collective-permute-start | bytes 688136 | tf_op jit(solution)/shard_map/ppermute | solution.py:88
  20.1 5.0 %collective-permute-start.2 = (bf16[224,512]{1,0:T(8,128)(2,1)S(1)}, bf16[224,512]{1,0:T(8,128)(2,1)S(1)}, u32[]{:S(2)}, u32[]{:S(2)}) collective-permute-start(bf16[224,512]{1,0:T(8,128)(2,1)S(1)} %collective-permute-done.refs_0_), channel_id=1, source_target_pairs={{0,4},{1,5},{2,6},{3,7},{4,8},{5,9},{6,10},{7,11},{8,12},{9,13},{1... | collective-permute-start | bytes 688136 | tf_op jit(solution)/shard_map/ppermute | solution.py:87
  25.2 0.7 select_dynamic-update-slice_fusion.3
  25.9 1.4 %collective-permute-done.3.refs_1_ = bf16[224,512]{1,0:T(8,128)(2,1)S(1)} collective-permute-done((bf16[224,512]{1,0:T(8,128)(2,1)S(1)}, bf16[224,512]{1,0:T(8,128)(2,1)S(1)}, u32[]{:S(2)}, u32[]{:S(2)}) %collective-permute-start.3) | collective-permute-done | bytes 229408 | tf_op jit(solution)/shard_map/ppermute | solution.py:88
  27.4 1.3 %collective-permute-start.5 = (bf16[224,512]{1,0:T(8,128)(2,1)S(1)}, bf16[224,512]{1,0:T(8,128)(2,1)S(1)}, u32[]{:S(2)}, u32[]{:S(2)}) collective-permute-start(bf16[224,512]{1,0:T(8,128)(2,1)S(1)} %collective-permute-done.3.refs_1_), channel_id=1, source_target_pairs={{4,0},{5,1},{6,2},{7,3},{8,4},{9,5},{10,6},{11,7},{12,8},{13,9},{1... | collective-permute-start | bytes 688136 | tf_op jit(solution)/shard_map/ppermute | solution.py:97
  28.7 4.5 %collective-permute-start.4 = (bf16[224,512]{1,0:T(8,128)(2,1)S(1)}, bf16[224,512]{1,0:T(8,128)(2,1)S(1)}, u32[]{:S(2)}, u32[]{:S(2)}) collective-permute-start(bf16[224,512]{1,0:T(8,128)(2,1)S(1)} %collective-permute-done.2.refs_0_), channel_id=1, source_target_pairs={{0,4},{1,5},{2,6},{3,7},{4,8},{5,9},{6,10},{7,11},{8,12},{9,13},{1... | collective-permute-start | bytes 688136 | tf_op jit(solution)/shard_map/ppermute | solution.py:96
  33.2 0.8 broadcast_select_fusion.1
  35.3 1.5 %collective-permute-done.4.refs_0_ = bf16[224,512]{1,0:T(8,128)(2,1)S(1)} collective-permute-done((bf16[224,512]{1,0:T(8,128)(2,1)S(1)}, bf16[224,512]{1,0:T(8,128)(2,1)S(1)}, u32[]{:S(2)}, u32[]{:S(2)}) %collective-permute-start.4) | collective-permute-done | bytes 229408 | tf_op jit(solution)/shard_map/ppermute | solution.py:96
  36.7 0.8 broadcast_select_fusion
  37.6 0.7 collective-permute-start.9
  38.3 0.8 constant_dynamic-update-slice_fusion.1
  39.1 2.7 %collective-permute-done.7.refs_2_ = bf16[224,512]{1,0:T(8,128)(2,1)S(1)} collective-permute-done((bf16[224,512]{1,0:T(8,128)(2,1)S(1)}, bf16[224,512]{1,0:T(8,128)(2,1)S(1)}, u32[]{:S(2)}, u32[]{:S(2)}) %collective-permute-start.7) | collective-permute-done | bytes 229408 | tf_op jit(solution)/shard_map/ppermute | solution.py:98
  41.8 0.8 constant_dynamic-update-slice_fusion
  42.5 0.8 fusion.8
  43.3 0.9 collective-permute-done.9.refs_0_
  44.2 0.8 select_dynamic-update-slice_fusion
  45.0 0.8 copy.44
  45.9 0.9 copy.45.no_ref
  46.8 0.9 copy.46.ro_ref
  47.7 2.4 %shard_map.95 = f32[1,16,512]{2,1,0:T(8,128)} custom-call(s32[1]{0:T(128)} %constant.144.clone.1.sel_ref, bf16[512,192]{1,0:T(8,128)(2,1)} %bitcast.74, f32[512,1]{1,0:T(8,128)} %copy.45.no_ref, f32[512,1]{1,0:T(8,128)} %copy.46.ro_ref, bf16[224,512]{1,0:T(8,128)(2,1)} %copy-done.13), custom_call_target="tpu_custom_call" | custom-call | tf_op jit(solution)/shard_map/pallas_call | solution.py:52
  50.6 0.7 slice.54
  51.3 2.4 %shard_map.99 = f32[1,16,512]{2,1,0:T(8,128)} custom-call(s32[1]{0:T(128)} %bitcast.31.sel_ref, bf16[512,192]{1,0:T(8,128)(2,1)} %bitcast.75, f32[512,1]{1,0:T(8,128)} %copy.45.no_ref, f32[512,1]{1,0:T(8,128)} %copy.46.ro_ref, bf16[224,512]{1,0:T(8,128)(2,1)} %copy-done.9), custom_call_target="tpu_custom_call" | custom-call | tf_op jit(solution)/shard_map/pallas_call | solution.py:52
  59.2 3.3 %shard_map.96 = f32[3,16,512]{2,1,0:T(8,128)} custom-call(s32[3]{0:T(128)} %get-tuple-element.31.sel_ref, bf16[512,192]{1,0:T(8,128)(2,1)} %bitcast.76, f32[512,1]{1,0:T(8,128)} %copy.45.no_ref, f32[512,1]{1,0:T(8,128)} %copy.46.ro_ref, bf16[224,512]{1,0:T(8,128)(2,1)} %copy-done.3, bf16[224,512]{1,0:T(8,128)(2,1)} %copy-done.1, bf16[224,512]{1,0:T(8,128)(2,1)} %copy-done.7), custom_call_target="tpu_custom_call" | custom-call | tf_op jit(solution)/shard_map/pallas_call | solution.py:52
  62.5 1.0 select_reduce_fusion.3
  64.1 3.4 %shard_map.97 = f32[4,16,512]{2,1,0:T(8,128)} custom-call(s32[4]{0:T(128)} %get-tuple-element.33.sel_ref, bf16[512,192]{1,0:T(8,128)(2,1)} %bitcast.77, f32[512,1]{1,0:T(8,128)} %copy.45.no_ref, f32[512,1]{1,0:T(8,128)} %copy.46.ro_ref, bf16[224,512]{1,0:T(8,128)(2,1)} %copy-done.11, bf16[224,512]{1,0:T(8,128)(2,1)} %copy-done.4, bf16[448,512]{1,0:T(8,128)(2,1)} %copy-done.2), custom_call_target="tpu_custom_call" | custom-call | tf_op jit(solution)/shard_map/pallas_call | solution.py:52
  67.5 1.0 select_reduce_fusion.1
  69.1 3.3 %shard_map.98 = f32[3,16,512]{2,1,0:T(8,128)} custom-call(s32[3]{0:T(128)} %get-tuple-element.35.sel_ref, bf16[512,192]{1,0:T(8,128)(2,1)} %bitcast.78, f32[512,1]{1,0:T(8,128)} %copy.45.no_ref, f32[512,1]{1,0:T(8,128)} %copy.46.ro_ref, bf16[224,512]{1,0:T(8,128)(2,1)} %copy-done.12, bf16[224,512]{1,0:T(8,128)(2,1)} %copy-done.10, bf16[224,512]{1,0:T(8,128)(2,1)} %copy-done.8), custom_call_target="tpu_custom_call" | custom-call | tf_op jit(solution)/shard_map/pallas_call | solution.py:52
  72.4 1.0 %select_reduce_fusion.2 = f32[16,512]{1,0:T(8,128)S(1)} fusion(f32[3,16,512]{2,1,0:T(8,128)} %shard_map.98, pred[3]{0:T(512)(128)(4,1)S(1)} %get-tuple-element.34), kind=kLoop, calls=%fused_computation.27 | loop fusion | flops 40960 | bytes 131075 | tf_op jit(solution)/shard_map/reduce_sum | solution.py:188
  74.0 7.6 %shard_map.100 = f32[8,16,512]{2,1,0:T(8,128)} custom-call(s32[8]{0:T(128)} %broadcast_31_sel_ref.2.sel_ref, bf16[512,192]{1,0:T(8,128)(2,1)} %bitcast.79, f32[512,1]{1,0:T(8,128)} %copy.45.no_ref, f32[512,1]{1,0:T(8,128)} %copy.46.ro_ref, bf16[1792,512]{1,0:T(8,128)(2,1)} %copy-done.5), custom_call_target="tpu_custom_call" | custom-call | tf_op jit(solution)/shard_map/pallas_call | solution.py:52
  81.6 1.0 %select_reduce_fusion = f32[16,512]{1,0:T(8,128)S(1)} fusion(f32[8,16,512]{2,1,0:T(8,128)} %shard_map.100, pred[8]{0:T(512)(128)(4,1)S(1)} %gather_fusion.3), kind=kLoop, calls=%fused_computation.14 | loop fusion | flops 122880 | bytes 294920 | tf_op jit(solution)/shard_map/reduce_sum | solution.py:188
  82.6 0.7 fusion.10
  84.0 0.8 collective-permute-done.11
  84.8 1.0 %collective-permute-start.12 = (f32[16,16]{0,1:T(8,128)S(1)}, f32[16,16]{0,1:T(8,128)S(1)}, u32[]{:S(2)}, u32[]{:S(2)}) collective-permute-start(f32[16,16]{0,1:T(8,128)S(1)} %add.164), channel_id=1, source_target_pairs={{0,2},{1,3},{2,0},{3,1},{4,6},{5,7},{6,4},{7,5},{8,10},{9,11},{10,... | collective-permute-start | bytes 3080 | tf_op jit(solution)/shard_map/ppermute | solution.py:136
  85.8 2.6 %collective-permute-done.12 = f32[16,16]{0,1:T(8,128)S(1)} collective-permute-done((f32[16,16]{0,1:T(8,128)S(1)}, f32[16,16]{0,1:T(8,128)S(1)}, u32[]{:S(2)}, u32[]{:S(2)}) %collective-permute-start.12) | collective-permute-done | bytes 1056 | tf_op jit(solution)/shard_map/ppermute | solution.py:136
  88.5 2.5 %collective-permute-start.13 = (f32[16,16]{0,1:T(8,128)S(1)}, f32[16,16]{0,1:T(8,128)S(1)}, u32[]{:S(2)}, u32[]{:S(2)}) collective-permute-start(f32[16,16]{0,1:T(8,128)S(1)} %add.165), channel_id=1, source_target_pairs={{0,4},{1,5},{2,6},{3,7},{4,0},{5,1},{6,2},{7,3},{8,12},{9,13},{10,... | collective-permute-start | bytes 3080 | tf_op jit(solution)/shard_map/ppermute | solution.py:136
  90.9 1.6 %collective-permute-done.13 = f32[16,16]{0,1:T(8,128)S(1)} collective-permute-done((f32[16,16]{0,1:T(8,128)S(1)}, f32[16,16]{0,1:T(8,128)S(1)}, u32[]{:S(2)}, u32[]{:S(2)}) %collective-permute-start.13) | collective-permute-done | bytes 1056 | tf_op jit(solution)/shard_map/ppermute | solution.py:136
  92.5 3.1 %collective-permute-start.14 = (f32[16,16]{0,1:T(8,128)S(1)}, f32[16,16]{0,1:T(8,128)S(1)}, u32[]{:S(2)}, u32[]{:S(2)}) collective-permute-start(f32[16,16]{0,1:T(8,128)S(1)} %add.166), channel_id=1, source_target_pairs={{0,8},{1,9},{2,10},{3,11},{4,12},{5,13},{6,14},{7,15},{8,0},{9,1},... | collective-permute-start | bytes 3080 | tf_op jit(solution)/shard_map/ppermute | solution.py:136
  95.8 1.5 %collective-permute-done.14 = f32[16,16]{0,1:T(8,128)S(1)} collective-permute-done((f32[16,16]{0,1:T(8,128)S(1)}, f32[16,16]{0,1:T(8,128)S(1)}, u32[]{:S(2)}, u32[]{:S(2)}) %collective-permute-start.14) | collective-permute-done | bytes 1056 | tf_op jit(solution)/shard_map/ppermute | solution.py:136
  98.0 0.8 fusion
  (96 shorter events, 10.7 us)
Async XLA Ops:
  0.6 95.1 %copy-start = (f32[16,512]{1,0:T(8,128)S(1)}, f32[16,512]{1,0:T(8,128)}, u32[]{:S(2)}) copy-start(f32[16,512]{1,0:T(8,128)} %param.12) | copy-start | bytes 98308
  5.4 32.2 %copy-start.13 = (bf16[224,512]{1,0:T(8,128)(2,1)}, bf16[224,512]{1,0:T(8,128)(2,1)S(1)}, u32[]{:S(2)}) copy-start(bf16[224,512]{1,0:T(8,128)(2,1)S(1)} %get-tuple-element.40.refs_0_) | copy-start | bytes 688132
  5.4 10.5 %collective-permute-start.1 = (bf16[224,512]{1,0:T(8,128)(2,1)S(1)}, bf16[224,512]{1,0:T(8,128)(2,1)S(1)}, u32[]{:S(2)}, u32[]{:S(2)}) collective-permute-start(bf16[224,512]{1,0:T(8,128)(2,1)S(1)} %get-tuple-element.40.refs_0_), channel_id=1, source_target_pairs={{4,0},{5,1},{6,2},{7,3},{8,4},{9,5},{10,6},{11,7},{12,8},{13,9},{1... | collective-permute-start | bytes 688136 | tf_op jit(solution)/shard_map/ppermute | solution.py:84
  6.7 10.4 %collective-permute-start = (bf16[224,512]{1,0:T(8,128)(2,1)S(1)}, bf16[224,512]{1,0:T(8,128)(2,1)S(1)}, u32[]{:S(2)}, u32[]{:S(2)}) collective-permute-start(bf16[224,512]{1,0:T(8,128)(2,1)S(1)} %get-tuple-element.40.refs_0_), channel_id=1, source_target_pairs={{0,4},{1,5},{2,6},{3,7},{4,8},{5,9},{6,10},{7,11},{8,12},{9,13},{1... | collective-permute-start | bytes 688136 | tf_op jit(solution)/shard_map/ppermute | solution.py:83
  12.2 26.1 %collective-permute-start.6 = (bf16[224,512]{1,0:T(8,128)(2,1)S(1)}, bf16[224,512]{1,0:T(8,128)(2,1)S(1)}, u32[]{:S(2)}, u32[]{:S(2)}) collective-permute-start(bf16[224,512]{1,0:T(8,128)(2,1)S(1)} %get-tuple-element.40.refs_0_), channel_id=1, source_target_pairs={{0,2},{1,3},{2,0},{3,1},{4,6},{5,7},{6,4},{7,5},{8,10},{9,11},{10,... | collective-permute-start | bytes 688136 | tf_op jit(solution)/shard_map/ppermute | solution.py:85
  15.9 21.7 %copy-start.1 = (bf16[224,512]{1,0:T(8,128)(2,1)}, bf16[224,512]{1,0:T(8,128)(2,1)S(1)}, u32[]{:S(2)}) copy-start(bf16[224,512]{1,0:T(8,128)(2,1)S(1)} %collective-permute-done.1.refs_1_) | copy-start | bytes 688132
  17.1 20.5 %copy-start.3 = (bf16[224,512]{1,0:T(8,128)(2,1)}, bf16[224,512]{1,0:T(8,128)(2,1)S(1)}, u32[]{:S(2)}) copy-start(bf16[224,512]{1,0:T(8,128)(2,1)S(1)} %collective-permute-done.refs_0_) | copy-start | bytes 688132
  17.1 25.4 %collective-permute-start.8 = (bf16[448,512]{1,0:T(8,128)(2,1)S(1)}, bf16[448,512]{1,0:T(8,128)(2,1)S(1)}, u32[]{:S(2)}, u32[]{:S(2)}) collective-permute-start(bf16[448,512]{1,0:T(8,128)(2,1)S(1)} %pad_maximum_fusion), channel_id=1, source_target_pairs={{0,2},{1,3},{2,0},{3,1},{4,6},{5,7},{6,4},{7,5},{8,10},{9,11},{10,... | collective-permute-start | bytes 1376264 | tf_op jit(solution)/shard_map/ppermute | solution.py:89
  18.8 8.5 %collective-permute-start.3 = (bf16[224,512]{1,0:T(8,128)(2,1)S(1)}, bf16[224,512]{1,0:T(8,128)(2,1)S(1)}, u32[]{:S(2)}, u32[]{:S(2)}) collective-permute-start(bf16[224,512]{1,0:T(8,128)(2,1)S(1)} %collective-permute-done.1.refs_1_), channel_id=1, source_target_pairs={{4,0},{5,1},{6,2},{7,3},{8,4},{9,5},{10,6},{11,7},{12,8},{13,9},{1... | collective-permute-start | bytes 688136 | tf_op jit(solution)/shard_map/ppermute | solution.py:88
  20.1 8.5 %collective-permute-start.2 = (bf16[224,512]{1,0:T(8,128)(2,1)S(1)}, bf16[224,512]{1,0:T(8,128)(2,1)S(1)}, u32[]{:S(2)}, u32[]{:S(2)}) collective-permute-start(bf16[224,512]{1,0:T(8,128)(2,1)S(1)} %collective-permute-done.refs_0_), channel_id=1, source_target_pairs={{0,4},{1,5},{2,6},{3,7},{4,8},{5,9},{6,10},{7,11},{8,12},{9,13},{1... | collective-permute-start | bytes 688136 | tf_op jit(solution)/shard_map/ppermute | solution.py:87
  27.4 15.9 %copy-start.4 = (bf16[224,512]{1,0:T(8,128)(2,1)}, bf16[224,512]{1,0:T(8,128)(2,1)S(1)}, u32[]{:S(2)}) copy-start(bf16[224,512]{1,0:T(8,128)(2,1)S(1)} %collective-permute-done.3.refs_1_) | copy-start | bytes 688132
  27.4 7.9 %collective-permute-start.5 = (bf16[224,512]{1,0:T(8,128)(2,1)S(1)}, bf16[224,512]{1,0:T(8,128)(2,1)S(1)}, u32[]{:S(2)}, u32[]{:S(2)}) collective-permute-start(bf16[224,512]{1,0:T(8,128)(2,1)S(1)} %collective-permute-done.3.refs_1_), channel_id=1, source_target_pairs={{4,0},{5,1},{6,2},{7,3},{8,4},{9,5},{10,6},{11,7},{12,8},{13,9},{1... | collective-permute-start | bytes 688136 | tf_op jit(solution)/shard_map/ppermute | solution.py:97
  28.7 8.9 %copy-start.11 = (bf16[224,512]{1,0:T(8,128)(2,1)}, bf16[224,512]{1,0:T(8,128)(2,1)S(1)}, u32[]{:S(2)}) copy-start(bf16[224,512]{1,0:T(8,128)(2,1)S(1)} %collective-permute-done.2.refs_0_) | copy-start | bytes 688132
  28.7 8.1 %collective-permute-start.4 = (bf16[224,512]{1,0:T(8,128)(2,1)S(1)}, bf16[224,512]{1,0:T(8,128)(2,1)S(1)}, u32[]{:S(2)}, u32[]{:S(2)}) collective-permute-start(bf16[224,512]{1,0:T(8,128)(2,1)S(1)} %collective-permute-done.2.refs_0_), channel_id=1, source_target_pairs={{0,4},{1,5},{2,6},{3,7},{4,8},{5,9},{6,10},{7,11},{8,12},{9,13},{1... | collective-permute-start | bytes 688136 | tf_op jit(solution)/shard_map/ppermute | solution.py:96
  34.0 7.7 %collective-permute-start.7 = (bf16[224,512]{1,0:T(8,128)(2,1)S(1)}, bf16[224,512]{1,0:T(8,128)(2,1)S(1)}, u32[]{:S(2)}, u32[]{:S(2)}) collective-permute-start(bf16[224,512]{1,0:T(8,128)(2,1)S(1)} %get-tuple-element.38), channel_id=1, source_target_pairs={{0,2},{1,3},{2,0},{3,1},{4,6},{5,7},{6,4},{7,5},{8,10},{9,11},{10,... | collective-permute-start | bytes 688136 | tf_op jit(solution)/shard_map/ppermute | solution.py:98
  35.3 9.8 %copy-start.10 = (bf16[224,512]{1,0:T(8,128)(2,1)}, bf16[224,512]{1,0:T(8,128)(2,1)S(1)}, u32[]{:S(2)}) copy-start(bf16[224,512]{1,0:T(8,128)(2,1)S(1)} %collective-permute-done.5.refs_1_) | copy-start | bytes 688132
  36.7 7.5 %copy-start.12 = (bf16[224,512]{1,0:T(8,128)(2,1)}, bf16[224,512]{1,0:T(8,128)(2,1)S(1)}, u32[]{:S(2)}) copy-start(bf16[224,512]{1,0:T(8,128)(2,1)S(1)} %collective-permute-done.4.refs_0_) | copy-start | bytes 688132
  36.7 8.3 %copy-start.6 = (bf16[192,512]{1,0:T(8,128)(2,1)S(1)}, bf16[192,512]{1,0:T(8,128)(2,1)}, u32[]{:S(2)}) copy-start(bf16[192,512]{1,0:T(8,128)(2,1)} %param.8) | copy-start | bytes 589828
  37.6 9.2 %copy-start.19 = (bf16[512]{0:T(512)(128)(2,1)S(1)}, bf16[512]{0:T(512)(128)(2,1)}, u32[]{:S(2)}) copy-start(bf16[512]{0:T(512)(128)(2,1)} %param.9) | copy-start | bytes 3076
  37.6 6.6 %collective-permute-start.9 = (bf16[224,512]{1,0:T(8,128)(2,1)S(1)}, bf16[224,512]{1,0:T(8,128)(2,1)S(1)}, u32[]{:S(2)}, u32[]{:S(2)}) collective-permute-start(bf16[224,512]{1,0:T(8,128)(2,1)S(1)} %get-tuple-element.36), channel_id=1, source_target_pairs={{0,2},{1,3},{2,0},{3,1},{4,6},{5,7},{6,4},{7,5},{8,10},{9,11},{10,... | collective-permute-start | bytes 688136 | tf_op jit(solution)/shard_map/ppermute | solution.py:105
  38.3 11.8 %copy-start.7 = (bf16[224,512]{1,0:T(8,128)(2,1)}, bf16[224,512]{1,0:T(8,128)(2,1)S(1)}, u32[]{:S(2)}) copy-start(bf16[224,512]{1,0:T(8,128)(2,1)S(1)} %collective-permute-done.6.refs_2_) | copy-start | bytes 688132
  41.8 8.4 %copy-start.8 = (bf16[224,512]{1,0:T(8,128)(2,1)}, bf16[224,512]{1,0:T(8,128)(2,1)S(1)}, u32[]{:S(2)}) copy-start(bf16[224,512]{1,0:T(8,128)(2,1)S(1)} %collective-permute-done.7.refs_2_) | copy-start | bytes 688132
  42.5 8.1 %copy-start.18 = (f32[512]{0:T(512)S(1)}, f32[512]{0:T(512)}, u32[]{:S(2)}) copy-start(f32[512]{0:T(512)} %param.10) | copy-start | bytes 6148
  42.5 7.6 %copy-start.2 = (bf16[448,512]{1,0:T(8,128)(2,1)}, bf16[448,512]{1,0:T(8,128)(2,1)S(1)}, u32[]{:S(2)}) copy-start(bf16[448,512]{1,0:T(8,128)(2,1)S(1)} %collective-permute-done.8.refs_2_) | copy-start | bytes 1376260
  44.2 7.1 %copy-start.9 = (bf16[224,512]{1,0:T(8,128)(2,1)}, bf16[224,512]{1,0:T(8,128)(2,1)S(1)}, u32[]{:S(2)}) copy-start(bf16[224,512]{1,0:T(8,128)(2,1)S(1)} %collective-permute-done.9.refs_0_) | copy-start | bytes 688132
  45.0 8.8 %collective-permute-start.10 = (bf16[1792,512]{1,0:T(8,128)(2,1)}, bf16[1792,512]{1,0:T(8,128)(2,1)S(1)}, u32[]{:S(2)}, u32[]{:S(2)}) collective-permute-start(bf16[1792,512]{1,0:T(8,128)(2,1)} %select_dynamic-update-slice_fusion), channel_id=1, source_target_pairs={{0,1},{1,0},{2,3},{3,2},{4,5},{5,4},{6,7},{7,6},{8,9},{9,8},{10,11... | collective-permute-start | bytes 5505032 | tf_op jit(solution)/shard_map/ppermute | solution.py:124
  53.8 8.8 %copy-start.5 = (bf16[1792,512]{1,0:T(8,128)(2,1)}, bf16[1792,512]{1,0:T(8,128)(2,1)S(1)}, u32[]{:S(2)}) copy-start(bf16[1792,512]{1,0:T(8,128)(2,1)S(1)} %collective-permute-done.10.refs_0_) | copy-start | bytes 5505028
  72.4 10.2 %copy-start.15 = (f32[1,16,512]{2,1,0:T(8,128)S(1)}, f32[1,16,512]{2,1,0:T(8,128)}, u32[]{:S(2)}) copy-start(f32[1,16,512]{2,1,0:T(8,128)} %shard_map.95) | copy-start | bytes 98308
  72.4 10.2 %copy-start.16 = (f32[1,16,512]{2,1,0:T(8,128)S(1)}, f32[1,16,512]{2,1,0:T(8,128)}, u32[]{:S(2)}) copy-start(f32[1,16,512]{2,1,0:T(8,128)} %shard_map.99) | copy-start | bytes 98308
  72.4 10.9 %copy-start.14 = (f32[16,512]{1,0:T(8,128)S(1)}, f32[16,512]{1,0:T(8,128)}, u32[]{:S(2)}) copy-start(f32[16,512]{1,0:T(8,128)} %param.11) | copy-start | bytes 98308
  72.4 23.3 %copy-start.17 = (f32[16,16]{1,0:T(8,128)S(1)}, f32[16,16]{1,0:T(8,128)}, u32[]{:S(2)}) copy-start(f32[16,16]{1,0:T(8,128)} %param.13) | copy-start | bytes 3076
  83.5 1.3 %collective-permute-start.11 = (f32[16,16]{0,1:T(8,128)S(1)}, f32[16,16]{0,1:T(8,128)S(1)}, u32[]{:S(2)}, u32[]{:S(2)}) collective-permute-start(f32[16,16]{0,1:T(8,128)S(1)} %convolution_bitcast_fusion), channel_id=1, source_target_pairs={{0,1},{1,0},{2,3},{3,2},{4,5},{5,4},{6,7},{7,6},{8,9},{9,8},{10,11... | collective-permute-start | bytes 3080 | tf_op jit(solution)/shard_map/ppermute | solution.py:136
  84.8 3.7 %collective-permute-start.12 = (f32[16,16]{0,1:T(8,128)S(1)}, f32[16,16]{0,1:T(8,128)S(1)}, u32[]{:S(2)}, u32[]{:S(2)}) collective-permute-start(f32[16,16]{0,1:T(8,128)S(1)} %add.164), channel_id=1, source_target_pairs={{0,2},{1,3},{2,0},{3,1},{4,6},{5,7},{6,4},{7,5},{8,10},{9,11},{10,... | collective-permute-start | bytes 3080 | tf_op jit(solution)/shard_map/ppermute | solution.py:136
  88.5 4.1 %collective-permute-start.13 = (f32[16,16]{0,1:T(8,128)S(1)}, f32[16,16]{0,1:T(8,128)S(1)}, u32[]{:S(2)}, u32[]{:S(2)}) collective-permute-start(f32[16,16]{0,1:T(8,128)S(1)} %add.165), channel_id=1, source_target_pairs={{0,4},{1,5},{2,6},{3,7},{4,0},{5,1},{6,2},{7,3},{8,12},{9,13},{10,... | collective-permute-start | bytes 3080 | tf_op jit(solution)/shard_map/ppermute | solution.py:136
  92.5 4.8 %collective-permute-start.14 = (f32[16,16]{0,1:T(8,128)S(1)}, f32[16,16]{0,1:T(8,128)S(1)}, u32[]{:S(2)}, u32[]{:S(2)}) collective-permute-start(f32[16,16]{0,1:T(8,128)S(1)} %add.166), channel_id=1, source_target_pairs={{0,8},{1,9},{2,10},{3,11},{4,12},{5,13},{6,14},{7,15},{8,0},{9,1},... | collective-permute-start | bytes 3080 | tf_op jit(solution)/shard_map/ppermute | solution.py:136

commit v5 on v3

--- a/solution.py
+++ b/solution.py
@@ -1,3 +1,4 @@
+import functools
 import math
 
 import jax
@@ -14,46 +15,58 @@
 HIGHEST = lax.Precision.HIGHEST
 
 
-def affinity_kernel(flag_ref, xo_ref, no_ref, ro_ref, xc_ref, nc_ref, rc_ref, wc_ref, out_ref):
+def affinity_kernel(
+    width, flag_ref, xo_ref, no_ref, ro_ref, xa_ref, wa_ref, xb_ref, wb_ref, out_ref
+):
     s = pl.program_id(0)
+    halves = pl.num_programs(0)
 
     @pl.when(s == 0)
     def _():
         out_ref[...] = jnp.zeros_like(out_ref)
 
-    @pl.when(flag_ref[s] != 0)
-    def _():
-        inner = jnp.dot(xo_ref[...], xc_ref[0], preferred_element_type=jnp.float32)
-        distance = (no_ref[...] + nc_ref[0]) - 2.0 * inner
-        weights = jnp.exp(-distance * (ro_ref[...] * rc_ref[0])).astype(jnp.bfloat16)
-        out_ref[...] += lax.dot_general(
-            wc_ref[0], weights, (((1,), (1,)), ((), ())), preferred_element_type=jnp.float32
-        )
+    for slot, x_ref, w_ref in ((s, xa_ref, wa_ref), (s + halves, xb_ref, wb_ref)):
+
+        @pl.when(flag_ref[slot] != 0)
+        def _():
+            x_cols = x_ref[0, :width, :]
+            x_wide = x_cols.astype(jnp.float32)
+            norm_cols = jnp.sum(x_wide * x_wide, axis=0, keepdims=True)
+            recip_cols = 1.0 / w_ref[0, LANCZOS : LANCZOS + 1, :].astype(jnp.float32)
+            twice_inner = jnp.dot(xo_ref[...], x_cols, preferred_element_type=jnp.float32)
+            distance = (no_ref[...] + norm_cols) - twice_inner
+            weights = jnp.exp2(distance * (ro_ref[...] * recip_cols)).astype(jnp.bfloat16)
+            out_ref[...] += lax.dot_general(
+                w_ref[0, :LANCZOS, :], weights, (((1,), (1,)), ((), ())),
+                preferred_element_type=jnp.float32,
+            )
 
 
-def own_rows_product(flags, x_own, norm_own, recip_own, pieces, norm_all, recip_all, width):
+def own_rows_product(flags, x_own, norm_own, recip_own, mine, theirs, width):
     own = x_own.shape[1]
-    slots = pieces.shape[0]
+    rows = mine.shape[1]
+    half = mine.shape[0]
     lanes_row = width // LANCZOS
+    x_spec = pl.BlockSpec((1, rows, own), lambda s, m: (s, 0, 0))
+    w_spec = pl.BlockSpec((1, 2 * LANCZOS, own), lambda s, m: (s, lanes_row // 2, 0))
     grid_spec = pltpu.PrefetchScalarGridSpec(
         num_scalar_prefetch=1,
-        grid=(slots,),
+        grid=(half,),
         in_specs=[
             pl.BlockSpec((own, width), lambda s, m: (0, 0)),
             pl.BlockSpec((own, 1), lambda s, m: (0, 0)),
             pl.BlockSpec((own, 1), lambda s, m: (0, 0)),
-            pl.BlockSpec((1, width, own), lambda s, m: (s, 0, 0)),
-            pl.BlockSpec((1, 1, own), lambda s, m: (s, 0, 0)),
-            pl.BlockSpec((1, 1, own), lambda s, m: (s, 0, 0)),
-            pl.BlockSpec((1, LANCZOS, own), lambda s, m: (s, lanes_row, 0)),
+            x_spec, w_spec, x_spec, w_spec,
         ],
         out_specs=pl.BlockSpec((LANCZOS, own), lambda s, m: (0, 0)),
     )
+    twice_own_t = (x_own * 2).T
+    log2e = 1.0 / math.log(2.0)
     return pl.pallas_call(
-        affinity_kernel,
+        functools.partial(affinity_kernel, width),
         grid_spec=grid_spec,
         out_shape=jax.ShapeDtypeStruct((LANCZOS, own), jnp.float32),
-    )(flags, x_own.T, norm_own, recip_own, pieces, norm_all, recip_all, pieces)
+    )(flags, twice_own_t, norm_own, recip_own * -log2e, mine, mine, theirs, theirs)
 
 
 def gather_pieces(packed):
@@ -61,7 +74,7 @@
     me = lax.axis_index("row")
     if devices != 16:
         pieces = lax.all_gather(packed, "row", axis=0, tiled=False)
-        return pieces, jnp.arange(devices, dtype=jnp.int32)
+        return pieces[: devices // 2], pieces[devices // 2 :], jnp.arange(devices, dtype=jnp.int32)
     up = [(r, r + 4) for r in range(12)]
     down = [(r, r - 4) for r in range(4, 16)]
     across = [(r, r ^ 2) for r in range(16)]
@@ -100,7 +113,7 @@
         jnp.where(z == 3, partner - 12, jnp.where(z == 0, partner + 12, partner + 4)),
     ]).astype(jnp.int32)
     theirs = lax.ppermute(mine, "row", twin)
-    return jnp.concatenate([mine, theirs]), jnp.concatenate([origin, origin ^ 1])
+    return mine, theirs, jnp.concatenate([origin, origin ^ 1])
 
 
 def sum_over_rows(value):
@@ -134,9 +147,11 @@
     packed = jnp.concatenate(
         [embeddings, weighted, local_scale[None, :], plan_row[None, :]], axis=0
     )
-    pieces, origin = gather_pieces(packed)
+    packed = jnp.pad(packed, ((0, -packed.shape[0] % (2 * LANCZOS)), (0, 0)))
+    mine, theirs, origin = gather_pieces(packed)
 
-    plans = pieces[:, width + LANCZOS + 1, : 2 * slots + 1].astype(jnp.int32)
+    plans = jnp.concatenate([mine, theirs])[:, width + LANCZOS + 1, : 2 * slots + 1]
+    plans = plans.astype(jnp.int32)
     counts = plans[:, 2 * slots]
     pairs = plans[:, : 2 * slots].reshape(devices, slots, 2)
     live = jnp.arange(slots, dtype=jnp.int32)[None, :] < counts[:, None]
@@ -152,14 +167,10 @@
     mask_row = jnp.any(hit, axis=0).astype(jnp.int32)
     flags = mask_row[(origin * own) // BLK]
 
-    norm_all = jnp.sum(jnp.square(pieces[:, :width].astype(jnp.float32)), axis=1)[:, None, :]
-    recip_all = (1.0 / pieces[:, width + LANCZOS].astype(jnp.float32))[:, None, :]
     norm_own = jnp.sum(jnp.square(embeddings.astype(jnp.float32)), axis=0)[:, None]
     recip_own = (1.0 / local_scale.astype(jnp.float32))[:, None]
 
-    summed = own_rows_product(
-        flags, embeddings, norm_own, recip_own, pieces, norm_all, recip_all, width
-    )
+    summed = own_rows_product(flags, embeddings, norm_own, recip_own, mine, theirs, width)
     scaled = summed * (degree_scale[None, :] / math.sqrt(total_rows))
     partial_value = lax.dot_general(
         lanczos_block, scaled, (((1,), (1,)), ((), ())), precision=HIGHEST

time: 93 us -> 84.8 us (0.912)
  Pallas kernels: 15.1 us -> 11.6 us
  local copies, waits for them, and re-layouts: 13.2 us -> 10.4 us
  other arithmetic: 11.9 us -> 9.95 us
    pallas_call x1, Pallas kernels: 15.1 us -> 11.6 us  [own_rows_product(): pl.pallas_call(functools.partial(affinity_kernel, width), grid_spec=grid_...]
    reduce_sum x1 -> x0, other arithmetic: 2.56 us -> none  [shards(): jnp.sum(jnp.square(pieces[:, :width].astype(jnp.float32)), axis=1)]
    another operation x2 -> x1, local copies, waits for them, and re-layouts: 1.85 us -> 0.11 us  [the longest x1 1.74 us: gather_pieces(): jnp.stack([packed, line1, line2, line3, across1, across3, other2, other3])]
    div x2 -> x0, other arithmetic: 1.55 us -> none  [the longest x1 1.55 us: shards(): 1.0 / pieces[:, width + LANCZOS].astype(jnp.float32)]
    broadcast_in_dim x2 -> x0, local copies, waits for them, and re-layouts: 1.51 us -> none  [the longest x1 0.87 us: shards(): recip_own = (1.0 / local_scale.astype(jnp.float32))[:, None]]
    unnamed x5, other arithmetic: 3.34 us -> 4.75 us
    unnamed x18 -> x22, local copies, waits for them, and re-layouts: 4.38 us -> 4.12 us
  transfers between devices with their start and end apart: 15 -> 15, of which waited for: 11 -> 11; matrix products, arithmetic and copies ran while one was open for 10% -> 11% of each run, Pallas kernels for 0% -> 0%
where the time goes in v5:
time: 84.8 us; the launch traced here: 84.1 us
  starting transfers between devices  31.6 us (37%)
  waiting for transfers between devices  16.5 us (19%)
  Pallas kernels  11.6 us (14%)
  local copies, waits for them, and re-layouts  10.4 us (12%)
  other arithmetic  9.95 us (12%)
  matrix products  2.59 us (3%)
  between operations  1.51 us (2%)
    pallas_call x1, Pallas kernels, own_rows_product(): pl.pallas_call(functools.partial(affinity_kernel, width), grid_spec=grid_...  11.6 us
    ppermute x4, waiting for transfers between devices, sum_over_rows(): lax.ppermute(value, 'row', [(i, i ^ stride) for i in range(devices)])  7.49 us
    ppermute x4, starting transfers between devices, sum_over_rows(): lax.ppermute(value, 'row', [(i, i ^ stride) for i in range(devices)])  6.16 us
    ppermute x1, starting transfers between devices, gather_pieces(): up1 = lax.ppermute(packed, 'row', up)  5.57 us
    ppermute x1, starting transfers between devices, gather_pieces(): up3 = lax.ppermute(up2, 'row', up)  5.03 us
    ppermute x1, starting transfers between devices, gather_pieces(): up2 = lax.ppermute(up1, 'row', up)  5.03 us
    unnamed x5, other arithmetic  4.75 us
    unnamed x22, local copies, waits for them, and re-layouts  4.12 us
  transfers between devices with their start and end apart: 15, of which 11 were waited for; matrix products, arithmetic and copies ran while one was open for 11% of the time, Pallas kernels for 0%

profile of v5, /device:TPU:0, one launch (start us, length us, event | category | flops | bytes accessed | tf_op | source)
XLA Modules:
  0.0 84.1 jit_solution(12794983003487929909)
XLA Ops:
  0.6 0.7 convert.8
  2.3 0.7 broadcast_in_dim.6
  3.0 0.8 multiply_convert_fusion
  3.7 0.9 %fusion.7 = bf16[224,512]{1,0:T(8,128)(2,1)S(1)} fusion(bf16[1,512]{1,0:T(2,128)(2,1)S(1)} %broadcast_in_dim.7, bf16[1,512]{1,0:T(2,128)(2,1)S(1)} %broadcast_in_dim.6, bf16[16,512]{1,0:T(8,128)(2,1)S(1)} %multiply_convert_fusion, bf16[192,512]{1,0:T(8,128)(2,1)} %param.8), kind=kLoop, calls=%fused_computation.14 | loop fusion | flops 1490944 | bytes 444416 | tf_op jit(solution)/shard_map/concatenate | solution.py:147
  4.7 1.3 %collective-permute-start.1 = (bf16[224,512]{1,0:T(8,128)(2,1)S(1)}, bf16[224,512]{1,0:T(8,128)(2,1)S(1)}, u32[]{:S(2)}, u32[]{:S(2)}) collective-permute-start(bf16[224,512]{1,0:T(8,128)(2,1)S(1)} %fusion.7), channel_id=1, source_target_pairs={{4,0},{5,1},{6,2},{7,3},{8,4},{9,5},{10,6},{11,7},{12,8},{13,9},{1... | collective-permute-start | bytes 688136 | tf_op jit(solution)/shard_map/ppermute | solution.py:86
  6.0 5.6 %collective-permute-start = (bf16[224,512]{1,0:T(8,128)(2,1)S(1)}, bf16[224,512]{1,0:T(8,128)(2,1)S(1)}, u32[]{:S(2)}, u32[]{:S(2)}) collective-permute-start(bf16[224,512]{1,0:T(8,128)(2,1)S(1)} %fusion.7), channel_id=1, source_target_pairs={{0,4},{1,5},{2,6},{3,7},{4,8},{5,9},{6,10},{7,11},{8,12},{9,13},{1... | collective-permute-start | bytes 688136 | tf_op jit(solution)/shard_map/ppermute | solution.py:85
  11.5 2.0 %collective-permute-start.6 = (bf16[224,512]{1,0:T(8,128)(2,1)S(1)}, bf16[224,512]{1,0:T(8,128)(2,1)S(1)}, u32[]{:S(2)}, u32[]{:S(2)}) collective-permute-start(bf16[224,512]{1,0:T(8,128)(2,1)S(1)} %fusion.7), channel_id=1, source_target_pairs={{0,2},{1,3},{2,0},{3,1},{4,6},{5,7},{6,4},{7,5},{8,10},{9,11},{10,... | collective-permute-start | bytes 688136 | tf_op jit(solution)/shard_map/ppermute | solution.py:87
  13.6 1.6 %bitcast_dynamic-update-slice_fusion.13 = (bf16[8,224,512]{2,1,0:T(8,128)(2,1)}, bf16[16,224,512]{2,1,0:T(8,128)(2,1)S(1)}) fusion(bf16[1,512]{1,0:T(2,128)(2,1)S(1)} %broadcast_in_dim.7, bf16[1,512]{1,0:T(2,128)(2,1)S(1)} %broadcast_in_dim.6, bf16[16,512]{1,0:T(8,128)(2,1)S(1)} %multiply_convert_fusion, bf16[192,512]{1,0:T(8,128)(2,1)} %param.8), kind=kLoop, calls=%fused_computation.30 | loop fusion | flops 1490942 | bytes 673792
  15.2 1.2 %collective-permute-done = bf16[224,512]{1,0:T(8,128)(2,1)S(1)} collective-permute-done((bf16[224,512]{1,0:T(8,128)(2,1)S(1)}, bf16[224,512]{1,0:T(8,128)(2,1)S(1)}, u32[]{:S(2)}, u32[]{:S(2)}) %collective-permute-start) | collective-permute-done | bytes 229408 | tf_op jit(solution)/shard_map/ppermute | solution.py:85
  16.4 1.7 %collective-permute-start.8 = (bf16[2,224,512]{2,1,0:T(8,128)(2,1)S(1)}, bf16[2,224,512]{2,1,0:T(8,128)(2,1)S(1)}, u32[]{:S(2)}, u32[]{:S(2)}) collective-permute-start(bf16[2,224,512]{2,1,0:T(8,128)(2,1)S(1)} %pad_maximum_fusion), channel_id=1, source_target_pairs={{0,2},{1,3},{2,0},{3,1},{4,6},{5,7},{6,4},{7,5},{8,10},{9,11},{10,... | collective-permute-start | bytes 1376264 | tf_op jit(solution)/shard_map/ppermute | solution.py:90
  18.2 1.3 %collective-permute-start.3 = (bf16[224,512]{1,0:T(8,128)(2,1)S(1)}, bf16[224,512]{1,0:T(8,128)(2,1)S(1)}, u32[]{:S(2)}, u32[]{:S(2)}) collective-permute-start(bf16[224,512]{1,0:T(8,128)(2,1)S(1)} %collective-permute-done.1), channel_id=1, source_target_pairs={{4,0},{5,1},{6,2},{7,3},{8,4},{9,5},{10,6},{11,7},{12,8},{13,9},{1... | collective-permute-start | bytes 688136 | tf_op jit(solution)/shard_map/ppermute | solution.py:89
  19.5 5.0 %collective-permute-start.2 = (bf16[224,512]{1,0:T(8,128)(2,1)S(1)}, bf16[224,512]{1,0:T(8,128)(2,1)S(1)}, u32[]{:S(2)}, u32[]{:S(2)}) collective-permute-start(bf16[224,512]{1,0:T(8,128)(2,1)S(1)} %collective-permute-done), channel_id=1, source_target_pairs={{0,4},{1,5},{2,6},{3,7},{4,8},{5,9},{6,10},{7,11},{8,12},{9,13},{1... | collective-permute-start | bytes 688136 | tf_op jit(solution)/shard_map/ppermute | solution.py:88
  24.5 0.7 bitcast_dynamic-update-slice_fusion.11
  25.2 1.4 %collective-permute-done.3 = bf16[224,512]{1,0:T(8,128)(2,1)S(1)} collective-permute-done((bf16[224,512]{1,0:T(8,128)(2,1)S(1)}, bf16[224,512]{1,0:T(8,128)(2,1)S(1)}, u32[]{:S(2)}, u32[]{:S(2)}) %collective-permute-start.3) | collective-permute-done | bytes 229408 | tf_op jit(solution)/shard_map/ppermute | solution.py:89
  26.7 1.3 %collective-permute-done.2 = bf16[224,512]{1,0:T(8,128)(2,1)S(1)} collective-permute-done((bf16[224,512]{1,0:T(8,128)(2,1)S(1)}, bf16[224,512]{1,0:T(8,128)(2,1)S(1)}, u32[]{:S(2)}, u32[]{:S(2)}) %collective-permute-start.2) | collective-permute-done | bytes 229408 | tf_op jit(solution)/shard_map/ppermute | solution.py:88
  28.0 0.6 collective-permute-start.7
  28.6 1.3 %collective-permute-start.5 = (bf16[224,512]{1,0:T(8,128)(2,1)S(1)}, bf16[224,512]{1,0:T(8,128)(2,1)S(1)}, u32[]{:S(2)}, u32[]{:S(2)}) collective-permute-start(bf16[224,512]{1,0:T(8,128)(2,1)S(1)} %collective-permute-done.3), channel_id=1, source_target_pairs={{4,0},{5,1},{6,2},{7,3},{8,4},{9,5},{10,6},{11,7},{12,8},{13,9},{1... | collective-permute-start | bytes 688136 | tf_op jit(solution)/shard_map/ppermute | solution.py:93
  29.9 5.0 %collective-permute-start.4 = (bf16[224,512]{1,0:T(8,128)(2,1)S(1)}, bf16[224,512]{1,0:T(8,128)(2,1)S(1)}, u32[]{:S(2)}, u32[]{:S(2)}) collective-permute-start(bf16[224,512]{1,0:T(8,128)(2,1)S(1)} %collective-permute-done.2), channel_id=1, source_target_pairs={{0,4},{1,5},{2,6},{3,7},{4,8},{5,9},{6,10},{7,11},{8,12},{9,13},{1... | collective-permute-start | bytes 688136 | tf_op jit(solution)/shard_map/ppermute | solution.py:92
  35.0 0.8 bitcast_dynamic-update-slice_fusion.9
  35.8 1.2 %collective-permute-done.5 = bf16[224,512]{1,0:T(8,128)(2,1)S(1)} collective-permute-done((bf16[224,512]{1,0:T(8,128)(2,1)S(1)}, bf16[224,512]{1,0:T(8,128)(2,1)S(1)}, u32[]{:S(2)}, u32[]{:S(2)}) %collective-permute-start.5) | collective-permute-done | bytes 229408 | tf_op jit(solution)/shard_map/ppermute | solution.py:93
  37.0 1.5 %collective-permute-done.4 = bf16[224,512]{1,0:T(8,128)(2,1)S(1)} collective-permute-done((bf16[224,512]{1,0:T(8,128)(2,1)S(1)}, bf16[224,512]{1,0:T(8,128)(2,1)S(1)}, u32[]{:S(2)}, u32[]{:S(2)}) %collective-permute-start.4) | collective-permute-done | bytes 229408 | tf_op jit(solution)/shard_map/ppermute | solution.py:92
  38.5 1.6 %collective-permute-start.9 = (bf16[224,512]{1,0:T(8,128)(2,1)S(1)}, bf16[224,512]{1,0:T(8,128)(2,1)S(1)}, u32[]{:S(2)}, u32[]{:S(2)}) collective-permute-start(bf16[224,512]{1,0:T(8,128)(2,1)S(1)} %broadcast_select_fusion), channel_id=1, source_target_pairs={{0,2},{1,3},{2,0},{3,1},{4,6},{5,7},{6,4},{7,5},{8,10},{9,11},{10,... | collective-permute-start | bytes 688136 | tf_op jit(solution)/shard_map/ppermute | solution.py:96
  40.0 0.8 bitcast_dynamic-update-slice_fusion.7
  40.9 0.7 bitcast_dynamic-update-slice_fusion.5
  41.6 0.7 bitcast_dynamic-update-slice_fusion.3
  42.4 0.8 constant_dynamic-update-slice_fusion
  43.1 1.4 %collective-permute-done.9 = bf16[224,512]{1,0:T(8,128)(2,1)S(1)} collective-permute-done((bf16[224,512]{1,0:T(8,128)(2,1)S(1)}, bf16[224,512]{1,0:T(8,128)(2,1)S(1)}, u32[]{:S(2)}, u32[]{:S(2)}) %collective-permute-start.9) | collective-permute-done | bytes 229408 | tf_op jit(solution)/shard_map/ppermute | solution.py:96
  44.6 0.7 bitcast_dynamic-update-slice_fusion.1
  45.3 1.8 %copy-done.4 = bf16[16,224,512]{2,1,0:T(8,128)(2,1)} copy-done((bf16[16,224,512]{2,1,0:T(8,128)(2,1)}, bf16[16,224,512]{2,1,0:T(8,128)(2,1)S(1)}, u32[]{:S(2)}) %copy-start.4) | copy-done | bytes 3670040
  47.3 0.9 %copy.38.no_ref = f32[512,1]{1,0:T(8,128)} copy(f32[512,1]{0,1:T(1,128)S(1)} %bitcast.72) | data formatting | bytes 4096 | tf_op jit(solution)/shard_map/broadcast_in_dim | solution.py:170
  48.2 0.9 %copy.39.ro_ref = f32[512,1]{1,0:T(8,128)} copy(f32[512,1]{0,1:T(1,128)S(1)} %bitcast.73) | data formatting | bytes 4096 | tf_op jit(solution)/shard_map/mul | solution.py:69
  49.3 0.8 multiply_bitcast_fusion.xo_ref
  50.1 1.0 %collective-permute-done.10.xb_ref.wb_ref = bf16[8,224,512]{2,1,0:T(8,128)(2,1)S(1)} collective-permute-done((bf16[8,224,512]{2,1,0:T(8,128)(2,1)}, bf16[8,224,512]{2,1,0:T(8,128)(2,1)S(1)}, u32[]{:S(2)}, u32[]{:S(2)}) %collective-permute-start.10) | collective-permute-done | bytes 1835040 | tf_op jit(solution)/shard_map/ppermute | solution.py:115
  51.1 1.6 %constant_dynamic-update-slice_fusion.1 = bf16[16,224,512]{2,1,0:T(8,128)(2,1)} fusion(bf16[16,224,512]{2,1,0:T(8,128)(2,1)} %copy-done.4, bf16[8,224,512]{2,1,0:T(8,128)(2,1)S(1)} %collective-permute-done.10.xb_ref.wb_ref), kind=kLoop, calls=%fused_computation.37 | loop fusion | bytes 3670016 | tf_op jit(solution)/shard_map/concatenate | solution.py:153
  52.7 0.8 slice_convert_fusion
  53.5 0.2 slice_reduce_fusion
  54.4 1.2 %gather_fusion = s32[16]{0:T(128)} fusion(s32[8]{0:T(128)S(1)} %convert_element_type.26, s32[1024]{0:T(1024)S(1)} %pad_clamp_fusion), kind=kCustom, calls=%fused_computation | custom fusion | bytes 192 | tf_op jit(solution)/shard_map/gather | solution.py:168
  55.6 11.6 %shard_map.95 = f32[16,512]{1,0:T(8,128)} custom-call(s32[16]{0:T(128)} %gather_fusion, bf16[512,192]{1,0:T(8,128)(2,1)} %multiply_bitcast_fusion.xo_ref, f32[512,1]{1,0:T(8,128)} %copy.38.no_ref, f32[512,1]{1,0:T(8,128)} %copy.39.ro_ref, bf16[8,224,512]{2,1,0:T(8,128)(2,1)} %get-tuple-element.14.xa_ref.wa_ref, ...), custom_call_target="tpu_custom_call" | custom-call | tf_op jit(solution)/shard_map/pallas_call | solution.py:65
  67.2 0.9 %convolution_bitcast_fusion = f32[16,16]{0,1:T(8,128)S(1)} fusion(f32[16,512]{1,0:T(8,128)S(1)} %copy-done.3, f32[16,512]{1,0:T(8,128)} %shard_map.95, f32[512]{0:T(512)S(1)} %broadcast_multiply_fusion), kind=kOutput, calls=%fused_computation.3 | convolution fusion | flops 1581056 | bytes 68608 | tf_op jit(solution)/shard_map/dot_general | solution.py:175
  68.3 1.0 %collective-permute-done.11 = f32[16,16]{0,1:T(8,128)S(1)} collective-permute-done((f32[16,16]{0,1:T(8,128)S(1)}, f32[16,16]{0,1:T(8,128)S(1)}, u32[]{:S(2)}, u32[]{:S(2)}) %collective-permute-start.11) | collective-permute-done | bytes 1056 | tf_op jit(solution)/shard_map/ppermute | solution.py:125
  69.3 0.3 collective-permute-start.12
  69.6 3.3 %collective-permute-done.12 = f32[16,16]{0,1:T(8,128)S(1)} collective-permute-done((f32[16,16]{0,1:T(8,128)S(1)}, f32[16,16]{0,1:T(8,128)S(1)}, u32[]{:S(2)}, u32[]{:S(2)}) %collective-permute-start.12) | collective-permute-done | bytes 1056 | tf_op jit(solution)/shard_map/ppermute | solution.py:125
  73.0 2.5 %collective-permute-start.13 = (f32[16,16]{0,1:T(8,128)S(1)}, f32[16,16]{0,1:T(8,128)S(1)}, u32[]{:S(2)}, u32[]{:S(2)}) collective-permute-start(f32[16,16]{0,1:T(8,128)S(1)} %add.72), channel_id=1, source_target_pairs={{0,4},{1,5},{2,6},{3,7},{4,0},{5,1},{6,2},{7,3},{8,12},{9,13},{10,... | collective-permute-start | bytes 3080 | tf_op jit(solution)/shard_map/ppermute | solution.py:125
  75.4 1.6 %collective-permute-done.13 = f32[16,16]{0,1:T(8,128)S(1)} collective-permute-done((f32[16,16]{0,1:T(8,128)S(1)}, f32[16,16]{0,1:T(8,128)S(1)}, u32[]{:S(2)}, u32[]{:S(2)}) %collective-permute-start.13) | collective-permute-done | bytes 1056 | tf_op jit(solution)/shard_map/ppermute | solution.py:125
  77.1 3.2 %collective-permute-start.14 = (f32[16,16]{0,1:T(8,128)S(1)}, f32[16,16]{0,1:T(8,128)S(1)}, u32[]{:S(2)}, u32[]{:S(2)}) collective-permute-start(f32[16,16]{0,1:T(8,128)S(1)} %add.73), channel_id=1, source_target_pairs={{0,8},{1,9},{2,10},{3,11},{4,12},{5,13},{6,14},{7,15},{8,0},{9,1},... | collective-permute-start | bytes 3080 | tf_op jit(solution)/shard_map/ppermute | solution.py:125
  80.4 1.5 %collective-permute-done.14 = f32[16,16]{0,1:T(8,128)S(1)} collective-permute-done((f32[16,16]{0,1:T(8,128)S(1)}, f32[16,16]{0,1:T(8,128)S(1)}, u32[]{:S(2)}, u32[]{:S(2)}) %collective-permute-start.14) | collective-permute-done | bytes 1056 | tf_op jit(solution)/shard_map/ppermute | solution.py:125
  81.9 0.7 copy.40
  82.6 1.5 %fusion = f32[16,512]{1,0:T(8,128)} fusion(f32[16,512]{1,0:T(8,128)S(1)} %fusion.20, f32[16,16]{0,1:T(8,128)S(1)} %add_multiply_fusion, f32[16,512]{1,0:T(8,128)S(1)} %copy-done.3, f32[16,512]{1,0:T(8,128)} %shard_map.95, f32[512]{0:T(512)S(1)} %broadcast_multiply_fusion), kind=kOutput, calls=%fused_computation.2 | convolution fusion | flops 1597440 | bytes 134144 | tf_op jit(solution)/shard_map/dot_general | solution.py:179
  (55 shorter events, 1.9 us)
Async XLA Ops:
  0.6 79.7 %copy-start = (f32[16,512]{1,0:T(8,128)S(1)}, f32[16,512]{1,0:T(8,128)}, u32[]{:S(2)}) copy-start(f32[16,512]{1,0:T(8,128)} %param.12) | copy-start | bytes 98308
  4.7 10.6 %collective-permute-start.1 = (bf16[224,512]{1,0:T(8,128)(2,1)S(1)}, bf16[224,512]{1,0:T(8,128)(2,1)S(1)}, u32[]{:S(2)}, u32[]{:S(2)}) collective-permute-start(bf16[224,512]{1,0:T(8,128)(2,1)S(1)} %fusion.7), channel_id=1, source_target_pairs={{4,0},{5,1},{6,2},{7,3},{8,4},{9,5},{10,6},{11,7},{12,8},{13,9},{1... | collective-permute-start | bytes 688136 | tf_op jit(solution)/shard_map/ppermute | solution.py:86
  6.0 10.4 %collective-permute-start = (bf16[224,512]{1,0:T(8,128)(2,1)S(1)}, bf16[224,512]{1,0:T(8,128)(2,1)S(1)}, u32[]{:S(2)}, u32[]{:S(2)}) collective-permute-start(bf16[224,512]{1,0:T(8,128)(2,1)S(1)} %fusion.7), channel_id=1, source_target_pairs={{0,4},{1,5},{2,6},{3,7},{4,8},{5,9},{6,10},{7,11},{8,12},{9,13},{1... | collective-permute-start | bytes 688136 | tf_op jit(solution)/shard_map/ppermute | solution.py:85
  11.5 29.3 %collective-permute-start.6 = (bf16[224,512]{1,0:T(8,128)(2,1)S(1)}, bf16[224,512]{1,0:T(8,128)(2,1)S(1)}, u32[]{:S(2)}, u32[]{:S(2)}) collective-permute-start(bf16[224,512]{1,0:T(8,128)(2,1)S(1)} %fusion.7), channel_id=1, source_target_pairs={{0,2},{1,3},{2,0},{3,1},{4,6},{5,7},{6,4},{7,5},{8,10},{9,11},{10,... | collective-permute-start | bytes 688136 | tf_op jit(solution)/shard_map/ppermute | solution.py:87
  16.4 25.9 %collective-permute-start.8 = (bf16[2,224,512]{2,1,0:T(8,128)(2,1)S(1)}, bf16[2,224,512]{2,1,0:T(8,128)(2,1)S(1)}, u32[]{:S(2)}, u32[]{:S(2)}) collective-permute-start(bf16[2,224,512]{2,1,0:T(8,128)(2,1)S(1)} %pad_maximum_fusion), channel_id=1, source_target_pairs={{0,2},{1,3},{2,0},{3,1},{4,6},{5,7},{6,4},{7,5},{8,10},{9,11},{10,... | collective-permute-start | bytes 1376264 | tf_op jit(solution)/shard_map/ppermute | solution.py:90
  18.2 8.5 %collective-permute-start.3 = (bf16[224,512]{1,0:T(8,128)(2,1)S(1)}, bf16[224,512]{1,0:T(8,128)(2,1)S(1)}, u32[]{:S(2)}, u32[]{:S(2)}) collective-permute-start(bf16[224,512]{1,0:T(8,128)(2,1)S(1)} %collective-permute-done.1), channel_id=1, source_target_pairs={{4,0},{5,1},{6,2},{7,3},{8,4},{9,5},{10,6},{11,7},{12,8},{13,9},{1... | collective-permute-start | bytes 688136 | tf_op jit(solution)/shard_map/ppermute | solution.py:89
  19.5 8.5 %collective-permute-start.2 = (bf16[224,512]{1,0:T(8,128)(2,1)S(1)}, bf16[224,512]{1,0:T(8,128)(2,1)S(1)}, u32[]{:S(2)}, u32[]{:S(2)}) collective-permute-start(bf16[224,512]{1,0:T(8,128)(2,1)S(1)} %collective-permute-done), channel_id=1, source_target_pairs={{0,4},{1,5},{2,6},{3,7},{4,8},{5,9},{6,10},{7,11},{8,12},{9,13},{1... | collective-permute-start | bytes 688136 | tf_op jit(solution)/shard_map/ppermute | solution.py:88
  28.0 13.6 %collective-permute-start.7 = (bf16[224,512]{1,0:T(8,128)(2,1)S(1)}, bf16[224,512]{1,0:T(8,128)(2,1)S(1)}, u32[]{:S(2)}, u32[]{:S(2)}) collective-permute-start(bf16[224,512]{1,0:T(8,128)(2,1)S(1)} %broadcast_select_fusion.1), channel_id=1, source_target_pairs={{0,2},{1,3},{2,0},{3,1},{4,6},{5,7},{6,4},{7,5},{8,10},{9,11},{10,... | collective-permute-start | bytes 688136 | tf_op jit(solution)/shard_map/ppermute | solution.py:94
  28.6 8.4 %collective-permute-start.5 = (bf16[224,512]{1,0:T(8,128)(2,1)S(1)}, bf16[224,512]{1,0:T(8,128)(2,1)S(1)}, u32[]{:S(2)}, u32[]{:S(2)}) collective-permute-start(bf16[224,512]{1,0:T(8,128)(2,1)S(1)} %collective-permute-done.3), channel_id=1, source_target_pairs={{4,0},{5,1},{6,2},{7,3},{8,4},{9,5},{10,6},{11,7},{12,8},{13,9},{1... | collective-permute-start | bytes 688136 | tf_op jit(solution)/shard_map/ppermute | solution.py:93
  29.9 8.5 %collective-permute-start.4 = (bf16[224,512]{1,0:T(8,128)(2,1)S(1)}, bf16[224,512]{1,0:T(8,128)(2,1)S(1)}, u32[]{:S(2)}, u32[]{:S(2)}) collective-permute-start(bf16[224,512]{1,0:T(8,128)(2,1)S(1)} %collective-permute-done.2), channel_id=1, source_target_pairs={{0,4},{1,5},{2,6},{3,7},{4,8},{5,9},{6,10},{7,11},{8,12},{9,13},{1... | collective-permute-start | bytes 688136 | tf_op jit(solution)/shard_map/ppermute | solution.py:92
  34.9 12.2 %copy-start.2 = (bf16[192,512]{1,0:T(8,128)(2,1)S(1)}, bf16[192,512]{1,0:T(8,128)(2,1)}, u32[]{:S(2)}) copy-start(bf16[192,512]{1,0:T(8,128)(2,1)} %param.8) | copy-start | bytes 589828
  35.7 12.5 %copy-start.7 = (bf16[512]{0:T(512)(128)(2,1)S(1)}, bf16[512]{0:T(512)(128)(2,1)}, u32[]{:S(2)}) copy-start(bf16[512]{0:T(512)(128)(2,1)} %param.9) | copy-start | bytes 3076
  35.7 13.6 %copy-start.6 = (f32[512]{0:T(512)S(1)}, f32[512]{0:T(512)}, u32[]{:S(2)}) copy-start(f32[512]{0:T(512)} %param.10) | copy-start | bytes 6148
  38.5 6.1 %collective-permute-start.9 = (bf16[224,512]{1,0:T(8,128)(2,1)S(1)}, bf16[224,512]{1,0:T(8,128)(2,1)S(1)}, u32[]{:S(2)}, u32[]{:S(2)}) collective-permute-start(bf16[224,512]{1,0:T(8,128)(2,1)S(1)} %broadcast_select_fusion), channel_id=1, source_target_pairs={{0,2},{1,3},{2,0},{3,1},{4,6},{5,7},{6,4},{7,5},{8,10},{9,11},{10,... | collective-permute-start | bytes 688136 | tf_op jit(solution)/shard_map/ppermute | solution.py:96
  45.3 1.8 %copy-start.4 = (bf16[16,224,512]{2,1,0:T(8,128)(2,1)}, bf16[16,224,512]{2,1,0:T(8,128)(2,1)S(1)}, u32[]{:S(2)}) copy-start(bf16[16,224,512]{2,1,0:T(8,128)(2,1)S(1)} %get-tuple-element.15) | copy-start | bytes 11010052
  47.1 4.0 %collective-permute-start.10 = (bf16[8,224,512]{2,1,0:T(8,128)(2,1)}, bf16[8,224,512]{2,1,0:T(8,128)(2,1)S(1)}, u32[]{:S(2)}, u32[]{:S(2)}) collective-permute-start(bf16[8,224,512]{2,1,0:T(8,128)(2,1)} %get-tuple-element.14.xa_ref.wa_ref), channel_id=1, source_target_pairs={{0,1},{1,0},{2,3},{3,2},{4,5},{5,4},{6,7},{7,6},{8,9},{9,8},{10,11... | collective-permute-start | bytes 5505032 | tf_op jit(solution)/shard_map/ppermute | solution.py:115
  51.1 4.5 %copy-start.1 = (bf16[8,224,512]{2,1,0:T(8,128)(2,1)}, bf16[8,224,512]{2,1,0:T(8,128)(2,1)S(1)}, u32[]{:S(2)}) copy-start(bf16[8,224,512]{2,1,0:T(8,128)(2,1)S(1)} %collective-permute-done.10.xb_ref.wb_ref) | copy-start | bytes 5505028
  55.6 11.6 %copy-start.3 = (f32[16,512]{1,0:T(8,128)S(1)}, f32[16,512]{1,0:T(8,128)}, u32[]{:S(2)}) copy-start(f32[16,512]{1,0:T(8,128)} %param.11) | copy-start | bytes 98308
  55.6 24.7 %copy-start.5 = (f32[16,16]{1,0:T(8,128)S(1)}, f32[16,16]{1,0:T(8,128)}, u32[]{:S(2)}) copy-start(f32[16,16]{1,0:T(8,128)} %param.13) | copy-start | bytes 3076
  68.1 1.2 %collective-permute-start.11 = (f32[16,16]{0,1:T(8,128)S(1)}, f32[16,16]{0,1:T(8,128)S(1)}, u32[]{:S(2)}, u32[]{:S(2)}) collective-permute-start(f32[16,16]{0,1:T(8,128)S(1)} %convolution_bitcast_fusion), channel_id=1, source_target_pairs={{0,1},{1,0},{2,3},{3,2},{4,5},{5,4},{6,7},{7,6},{8,9},{9,8},{10,11... | collective-permute-start | bytes 3080 | tf_op jit(solution)/shard_map/ppermute | solution.py:125
  69.3 3.7 %collective-permute-start.12 = (f32[16,16]{0,1:T(8,128)S(1)}, f32[16,16]{0,1:T(8,128)S(1)}, u32[]{:S(2)}, u32[]{:S(2)}) collective-permute-start(f32[16,16]{0,1:T(8,128)S(1)} %add.71), channel_id=1, source_target_pairs={{0,2},{1,3},{2,0},{3,1},{4,6},{5,7},{6,4},{7,5},{8,10},{9,11},{10,... | collective-permute-start | bytes 3080 | tf_op jit(solution)/shard_map/ppermute | solution.py:125
  73.0 4.1 %collective-permute-start.13 = (f32[16,16]{0,1:T(8,128)S(1)}, f32[16,16]{0,1:T(8,128)S(1)}, u32[]{:S(2)}, u32[]{:S(2)}) collective-permute-start(f32[16,16]{0,1:T(8,128)S(1)} %add.72), channel_id=1, source_target_pairs={{0,4},{1,5},{2,6},{3,7},{4,0},{5,1},{6,2},{7,3},{8,12},{9,13},{10,... | collective-permute-start | bytes 3080 | tf_op jit(solution)/shard_map/ppermute | solution.py:125
  77.1 4.8 %collective-permute-start.14 = (f32[16,16]{0,1:T(8,128)S(1)}, f32[16,16]{0,1:T(8,128)S(1)}, u32[]{:S(2)}, u32[]{:S(2)}) collective-permute-start(f32[16,16]{0,1:T(8,128)S(1)} %add.73), channel_id=1, source_target_pairs={{0,8},{1,9},{2,10},{3,11},{4,12},{5,13},{6,14},{7,15},{8,0},{9,1},... | collective-permute-start | bytes 3080 | tf_op jit(solution)/shard_map/ppermute | solution.py:125

commit v6 on v5

--- a/solution.py
+++ b/solution.py
@@ -15,35 +15,31 @@
 HIGHEST = lax.Precision.HIGHEST
 
 
-def affinity_kernel(
-    width, flag_ref, xo_ref, no_ref, ro_ref, xa_ref, wa_ref, xb_ref, wb_ref, out_ref
-):
+def affinity_kernel(width, flag_ref, xo_ref, no_ref, ro_ref, x_ref, w_ref, out_ref):
     s = pl.program_id(0)
-    halves = pl.num_programs(0)
 
     @pl.when(s == 0)
     def _():
         out_ref[...] = jnp.zeros_like(out_ref)
 
-    for slot, x_ref, w_ref in ((s, xa_ref, wa_ref), (s + halves, xb_ref, wb_ref)):
-
-        @pl.when(flag_ref[slot] != 0)
-        def _():
-            x_cols = x_ref[0, :width, :]
-            x_wide = x_cols.astype(jnp.float32)
-            norm_cols = jnp.sum(x_wide * x_wide, axis=0, keepdims=True)
-            recip_cols = 1.0 / w_ref[0, LANCZOS : LANCZOS + 1, :].astype(jnp.float32)
-            twice_inner = jnp.dot(xo_ref[...], x_cols, preferred_element_type=jnp.float32)
-            distance = (no_ref[...] + norm_cols) - twice_inner
-            weights = jnp.exp2(distance * (ro_ref[...] * recip_cols)).astype(jnp.bfloat16)
-            out_ref[...] += lax.dot_general(
-                w_ref[0, :LANCZOS, :], weights, (((1,), (1,)), ((), ())),
-                preferred_element_type=jnp.float32,
-            )
-
-
-def own_rows_product(flags, x_own, norm_own, recip_own, mine, theirs, width):
-    own = x_own.shape[1]
+    @pl.when(flag_ref[s] != 0)
+    def _():
+        x_cols = x_ref[0, :width, :]
+        x_wide = x_cols.astype(jnp.float32)
+        norm_cols = jnp.sum(x_wide * x_wide, axis=0, keepdims=True)
+        recip_cols = 1.0 / w_ref[0, LANCZOS : LANCZOS + 1, :].astype(jnp.float32)
+        twice_inner = jnp.dot(xo_ref[...], x_cols, preferred_element_type=jnp.float32)
+        distance = (no_ref[...] + norm_cols) - twice_inner
+        weights = jnp.exp2(distance * (ro_ref[...] * recip_cols)).astype(jnp.bfloat16)
+        out_ref[...] += lax.dot_general(
+            w_ref[0, :LANCZOS, :], weights, (((1,), (1,)), ((), ())),
+            preferred_element_type=jnp.float32,
+        )
+
+
+def own_rows_product(flags, own_terms, mine, width):
+    twice_own_t, norm_own, recip_own = own_terms
+    own = twice_own_t.shape[0]
     rows = mine.shape[1]
     half = mine.shape[0]
     lanes_row = width // LANCZOS
@@ -56,17 +52,15 @@
             pl.BlockSpec((own, width), lambda s, m: (0, 0)),
             pl.BlockSpec((own, 1), lambda s, m: (0, 0)),
             pl.BlockSpec((own, 1), lambda s, m: (0, 0)),
-            x_spec, w_spec, x_spec, w_spec,
+            x_spec, w_spec,
         ],
         out_specs=pl.BlockSpec((LANCZOS, own), lambda s, m: (0, 0)),
     )
-    twice_own_t = (x_own * 2).T
-    log2e = 1.0 / math.log(2.0)
     return pl.pallas_call(
         functools.partial(affinity_kernel, width),
         grid_spec=grid_spec,
         out_shape=jax.ShapeDtypeStruct((LANCZOS, own), jnp.float32),
-    )(flags, twice_own_t, norm_own, recip_own * -log2e, mine, mine, theirs, theirs)
+    )(flags, twice_own_t, norm_own, recip_own, mine, mine)
 
 
 def gather_pieces(packed):
@@ -74,7 +68,7 @@
     me = lax.axis_index("row")
     if devices != 16:
         pieces = lax.all_gather(packed, "row", axis=0, tiled=False)
-        return pieces[: devices // 2], pieces[devices // 2 :], jnp.arange(devices, dtype=jnp.int32)
+        return pieces, None, jnp.arange(devices, dtype=jnp.int32), None
     up = [(r, r + 4) for r in range(12)]
     down = [(r, r - 4) for r in range(4, 16)]
     across = [(r, r ^ 2) for r in range(16)]
@@ -113,7 +107,7 @@
         jnp.where(z == 3, partner - 12, jnp.where(z == 0, partner + 12, partner + 4)),
     ]).astype(jnp.int32)
     theirs = lax.ppermute(mine, "row", twin)
-    return mine, theirs, jnp.concatenate([origin, origin ^ 1])
+    return mine, theirs, origin, origin ^ 1
 
 
 def sum_over_rows(value):
@@ -148,9 +142,13 @@
         [embeddings, weighted, local_scale[None, :], plan_row[None, :]], axis=0
     )
     packed = jnp.pad(packed, ((0, -packed.shape[0] % (2 * LANCZOS)), (0, 0)))
-    mine, theirs, origin = gather_pieces(packed)
-
-    plans = jnp.concatenate([mine, theirs])[:, width + LANCZOS + 1, : 2 * slots + 1]
+    mine, theirs, origin, their_origin = gather_pieces(packed)
+
+    plan_at = width + LANCZOS + 1
+    plans = mine[:, plan_at, : 2 * slots + 1]
+    if theirs is not None:
+        twin = [(r, r ^ 1) for r in range(devices)]
+        plans = jnp.concatenate([plans, lax.ppermute(plans, "row", twin)])
     plans = plans.astype(jnp.int32)
     counts = plans[:, 2 * slots]
     pairs = plans[:, : 2 * slots].reshape(devices, slots, 2)
@@ -165,12 +163,16 @@
         | ((col_block[:, None] == my_block) & (row_block[:, None] == block_ids[None, :]))
     )
     mask_row = jnp.any(hit, axis=0).astype(jnp.int32)
-    flags = mask_row[(origin * own) // BLK]
 
     norm_own = jnp.sum(jnp.square(embeddings.astype(jnp.float32)), axis=0)[:, None]
-    recip_own = (1.0 / local_scale.astype(jnp.float32))[:, None]
-
-    summed = own_rows_product(flags, embeddings, norm_own, recip_own, mine, theirs, width)
+    log2e = 1.0 / math.log(2.0)
+    recip_own = (-log2e / local_scale.astype(jnp.float32))[:, None]
+    own_terms = ((embeddings * 2).T, norm_own, recip_own)
+    summed = own_rows_product(mask_row[(origin * own) // BLK], own_terms, mine, width)
+    if theirs is not None:
+        summed = summed + own_rows_product(
+            mask_row[(their_origin * own) // BLK], own_terms, theirs, width
+        )
     scaled = summed * (degree_scale[None, :] / math.sqrt(total_rows))
     partial_value = lax.dot_general(
         lanczos_block, scaled, (((1,), (1,)), ((), ())), precision=HIGHEST

time: 84.8 us -> 87.1 us (1.027)
  waiting for transfers between devices: 16.5 us -> 22 us
  other arithmetic: 9.95 us -> 5.85 us
  Pallas kernels: 11.6 us -> 15.3 us
  local copies, waits for them, and re-layouts: 10.4 us -> 7.59 us
    unnamed x5, other arithmetic: 4.75 us -> 0.35 us
    ppermute x1, waiting for transfers between devices: 1.45 us -> 5.41 us  [gather_pieces(): across4 = lax.ppermute(pick3, 'row', across)]
    pallas_call x1 -> x2, Pallas kernels: 11.6 us -> 15.3 us  [own_rows_product(): pl.pallas_call(functools.partial(affinity_kernel, width), grid_spec=grid_...]
    ppermute x0 -> x1, waiting for transfers between devices: none -> 2.39 us  [shards(): plans = jnp.concatenate([plans, lax.ppermute(plans, 'row', twin)])]
    unnamed x22 -> x19, local copies, waits for them, and re-layouts: 4.12 us -> 1.8 us
    concatenate x2 -> x0, local copies, waits for them, and re-layouts: 1.71 us -> none  [the longest x1 1.6 us: shards(): jnp.concatenate([mine, theirs])[:, width + LANCZOS + 1, :2 * slots + 1]]
    ppermute x1, starting transfers between devices: 1.74 us -> 0.13 us  [gather_pieces(): across2 = lax.ppermute(jnp.stack([up1, down1]), 'row', across)]
    gather x1 -> x2, local copies, waits for them, and re-layouts: 1.17 us -> 2.37 us  [the longest x1 1.21 us: shards(): mask_row[their_origin * own // BLK]]
  transfers between devices with their start and end apart: 15 -> 16, of which waited for: 11 -> 10; matrix products, arithmetic and copies ran while one was open for 11% -> 11% of each run, Pallas kernels for 0% -> 9%
where the time goes in v6:
time: 87.1 us; the launch traced here: 86.2 us
  starting transfers between devices  31.2 us (36%)
  waiting for transfers between devices  22 us (25%)
  Pallas kernels  15.3 us (18%)
  local copies, waits for them, and re-layouts  7.59 us (9%)
  other arithmetic  5.85 us (7%)
  matrix products  2.58 us (3%)
  between operations  1.6 us (2%)
    pallas_call x2, Pallas kernels, own_rows_product(): pl.pallas_call(functools.partial(affinity_kernel, width), grid_spec=grid_...  15.3 us
    ppermute x4, waiting for transfers between devices, sum_over_rows(): lax.ppermute(value, 'row', [(i, i ^ stride) for i in range(devices)])  7.37 us
    ppermute x4, starting transfers between devices, sum_over_rows(): lax.ppermute(value, 'row', [(i, i ^ stride) for i in range(devices)])  7.14 us
    ppermute x1, starting transfers between devices, gather_pieces(): up1 = lax.ppermute(packed, 'row', up)  5.57 us
    ppermute x1, waiting for transfers between devices, gather_pieces(): across4 = lax.ppermute(pick3, 'row', across)  5.41 us
    ppermute x1, starting transfers between devices, gather_pieces(): up3 = lax.ppermute(up2, 'row', up)  5.03 us
    ppermute x1, starting transfers between devices, gather_pieces(): up2 = lax.ppermute(up1, 'row', up)  4.83 us
    ppermute x1, waiting for transfers between devices, shards(): plans = jnp.concatenate([plans, lax.ppermute(plans, 'row', twin)])  2.39 us
  transfers between devices with their start and end apart: 16, of which 10 were waited for; matrix products, arithmetic and copies ran while one was open for 11% of the time, Pallas kernels for 9%

profile of v6, /device:TPU:0, one launch (start us, length us, event | category | flops | bytes accessed | tf_op | source)
XLA Modules:
  0.0 86.2 jit_solution(5699784105804984442)
XLA Ops:
  0.7 0.7 convert.7
  1.4 0.1 copy.36
  2.3 0.7 broadcast_in_dim.8
  3.0 0.8 multiply_convert_fusion
  3.8 0.9 %fusion.7 = bf16[224,512]{1,0:T(8,128)(2,1)S(1)} fusion(bf16[1,512]{1,0:T(2,128)(2,1)S(1)} %broadcast_in_dim.9, bf16[1,512]{1,0:T(2,128)(2,1)S(1)} %broadcast_in_dim.8, bf16[16,512]{1,0:T(8,128)(2,1)S(1)} %multiply_convert_fusion, bf16[192,512]{1,0:T(8,128)(2,1)} %param.8), kind=kLoop, calls=%fused_computation.15 | loop fusion | flops 1490944 | bytes 444416 | tf_op jit(solution)/shard_map/concatenate | solution.py:141
  4.7 1.3 %collective-permute-start.1 = (bf16[224,512]{1,0:T(8,128)(2,1)S(1)}, bf16[224,512]{1,0:T(8,128)(2,1)S(1)}, u32[]{:S(2)}, u32[]{:S(2)}) collective-permute-start(bf16[224,512]{1,0:T(8,128)(2,1)S(1)} %fusion.7), channel_id=1, source_target_pairs={{4,0},{5,1},{6,2},{7,3},{8,4},{9,5},{10,6},{11,7},{12,8},{13,9},{1... | collective-permute-start | bytes 688136 | tf_op jit(solution)/shard_map/ppermute | solution.py:80
  6.0 5.6 %collective-permute-start = (bf16[224,512]{1,0:T(8,128)(2,1)S(1)}, bf16[224,512]{1,0:T(8,128)(2,1)S(1)}, u32[]{:S(2)}, u32[]{:S(2)}) collective-permute-start(bf16[224,512]{1,0:T(8,128)(2,1)S(1)} %fusion.7), channel_id=1, source_target_pairs={{0,4},{1,5},{2,6},{3,7},{4,8},{5,9},{6,10},{7,11},{8,12},{9,13},{1... | collective-permute-start | bytes 688136 | tf_op jit(solution)/shard_map/ppermute | solution.py:79
  11.6 2.0 %collective-permute-start.6 = (bf16[224,512]{1,0:T(8,128)(2,1)S(1)}, bf16[224,512]{1,0:T(8,128)(2,1)S(1)}, u32[]{:S(2)}, u32[]{:S(2)}) collective-permute-start(bf16[224,512]{1,0:T(8,128)(2,1)S(1)} %fusion.7), channel_id=1, source_target_pairs={{0,2},{1,3},{2,0},{3,1},{4,6},{5,7},{6,4},{7,5},{8,10},{9,11},{10,... | collective-permute-start | bytes 688136 | tf_op jit(solution)/shard_map/ppermute | solution.py:81
  13.6 1.1 %copy.40 = bf16[192,512]{0,1:T(8,128)(2,1)S(1)} copy(bf16[192,512]{1,0:T(8,128)(2,1)} %param.8) | data formatting | bytes 393216 | tf_op args[0]
  14.7 0.7 convert_divide_fusion
  15.4 1.0 %multiply_reduce_fusion = f32[512]{0:T(512)S(1)} fusion(bf16[192,512]{1,0:T(8,128)(2,1)} %param.8), kind=kLoop, calls=%fused_computation.11 | loop fusion | flops 294400 | bytes 198656 | tf_op jit(solution)/shard_map/reduce_sum | solution.py:167
  16.4 0.9 copy.42.no_ref
  17.2 0.9 copy.43.ro_ref
  18.3 0.1 collective-permute-start.8
  18.4 1.3 %collective-permute-start.3 = (bf16[224,512]{1,0:T(8,128)(2,1)S(1)}, bf16[224,512]{1,0:T(8,128)(2,1)S(1)}, u32[]{:S(2)}, u32[]{:S(2)}) collective-permute-start(bf16[224,512]{1,0:T(8,128)(2,1)S(1)} %collective-permute-done.1), channel_id=1, source_target_pairs={{4,0},{5,1},{6,2},{7,3},{8,4},{9,5},{10,6},{11,7},{12,8},{13,9},{1... | collective-permute-start | bytes 688136 | tf_op jit(solution)/shard_map/ppermute | solution.py:83
  19.7 4.8 %collective-permute-start.2 = (bf16[224,512]{1,0:T(8,128)(2,1)S(1)}, bf16[224,512]{1,0:T(8,128)(2,1)S(1)}, u32[]{:S(2)}, u32[]{:S(2)}) collective-permute-start(bf16[224,512]{1,0:T(8,128)(2,1)S(1)} %collective-permute-done), channel_id=1, source_target_pairs={{0,4},{1,5},{2,6},{3,7},{4,8},{5,9},{6,10},{7,11},{8,12},{9,13},{1... | collective-permute-start | bytes 688136 | tf_op jit(solution)/shard_map/ppermute | solution.py:82
  24.6 2.2 %collective-permute-done.3 = bf16[224,512]{1,0:T(8,128)(2,1)S(1)} collective-permute-done((bf16[224,512]{1,0:T(8,128)(2,1)S(1)}, bf16[224,512]{1,0:T(8,128)(2,1)S(1)}, u32[]{:S(2)}, u32[]{:S(2)}) %collective-permute-start.3) | collective-permute-done | bytes 229408 | tf_op jit(solution)/shard_map/ppermute | solution.py:83
  26.8 1.2 %collective-permute-done.2 = bf16[224,512]{1,0:T(8,128)(2,1)S(1)} collective-permute-done((bf16[224,512]{1,0:T(8,128)(2,1)S(1)}, bf16[224,512]{1,0:T(8,128)(2,1)S(1)}, u32[]{:S(2)}, u32[]{:S(2)}) %collective-permute-start.2) | collective-permute-done | bytes 229408 | tf_op jit(solution)/shard_map/ppermute | solution.py:82
  28.1 1.8 %collective-permute-start.7 = (bf16[224,512]{1,0:T(8,128)(2,1)S(1)}, bf16[224,512]{1,0:T(8,128)(2,1)S(1)}, u32[]{:S(2)}, u32[]{:S(2)}) collective-permute-start(bf16[224,512]{1,0:T(8,128)(2,1)S(1)} %broadcast_select_fusion.1), channel_id=1, source_target_pairs={{0,2},{1,3},{2,0},{3,1},{4,6},{5,7},{6,4},{7,5},{8,10},{9,11},{10,... | collective-permute-start | bytes 688136 | tf_op jit(solution)/shard_map/ppermute | solution.py:88
  29.8 1.3 %collective-permute-start.5 = (bf16[224,512]{1,0:T(8,128)(2,1)S(1)}, bf16[224,512]{1,0:T(8,128)(2,1)S(1)}, u32[]{:S(2)}, u32[]{:S(2)}) collective-permute-start(bf16[224,512]{1,0:T(8,128)(2,1)S(1)} %collective-permute-done.3), channel_id=1, source_target_pairs={{4,0},{5,1},{6,2},{7,3},{8,4},{9,5},{10,6},{11,7},{12,8},{13,9},{1... | collective-permute-start | bytes 688136 | tf_op jit(solution)/shard_map/ppermute | solution.py:87
  31.1 5.0 %collective-permute-start.4 = (bf16[224,512]{1,0:T(8,128)(2,1)S(1)}, bf16[224,512]{1,0:T(8,128)(2,1)S(1)}, u32[]{:S(2)}, u32[]{:S(2)}) collective-permute-start(bf16[224,512]{1,0:T(8,128)(2,1)S(1)} %collective-permute-done.2), channel_id=1, source_target_pairs={{0,4},{1,5},{2,6},{3,7},{4,8},{5,9},{6,10},{7,11},{8,12},{9,13},{1... | collective-permute-start | bytes 688136 | tf_op jit(solution)/shard_map/ppermute | solution.py:86
  36.2 1.9 %collective-permute-done.5 = bf16[224,512]{1,0:T(8,128)(2,1)S(1)} collective-permute-done((bf16[224,512]{1,0:T(8,128)(2,1)S(1)}, bf16[224,512]{1,0:T(8,128)(2,1)S(1)}, u32[]{:S(2)}, u32[]{:S(2)}) %collective-permute-start.5) | collective-permute-done | bytes 229408 | tf_op jit(solution)/shard_map/ppermute | solution.py:87
  38.2 1.5 %collective-permute-done.4 = bf16[224,512]{1,0:T(8,128)(2,1)S(1)} collective-permute-done((bf16[224,512]{1,0:T(8,128)(2,1)S(1)}, bf16[224,512]{1,0:T(8,128)(2,1)S(1)}, u32[]{:S(2)}, u32[]{:S(2)}) %collective-permute-start.4) | collective-permute-done | bytes 229408 | tf_op jit(solution)/shard_map/ppermute | solution.py:86
  39.7 0.4 collective-permute-start.9
  40.1 0.1 bitcast_dynamic-update-slice_fusion.3
  40.4 5.4 %collective-permute-done.9 = bf16[224,512]{1,0:T(8,128)(2,1)S(1)} collective-permute-done((bf16[224,512]{1,0:T(8,128)(2,1)S(1)}, bf16[224,512]{1,0:T(8,128)(2,1)S(1)}, u32[]{:S(2)}, u32[]{:S(2)}) %collective-permute-start.9) | collective-permute-done | bytes 229408 | tf_op jit(solution)/shard_map/ppermute | solution.py:90
  46.0 0.9 %multiply_bitcast_fusion.xo_ref = bf16[512,192]{1,0:T(8,128)(2,1)} fusion(bf16[192,512]{0,1:T(8,128)(2,1)S(1)} %copy.40), kind=kLoop, calls=%fused_computation.12 | loop fusion | flops 98304 | bytes 393216 | tf_op jit(solution)/shard_map/transpose | solution.py:170
  46.9 0.4 collective-permute-start.10
  47.3 2.4 %collective-permute-done.10 = bf16[8,9]{1,0:T(8,128)(2,1)S(1)} collective-permute-done((bf16[8,9]{1,0:T(8,128)(2,1)S(1)}, bf16[8,9]{1,0:T(8,128)(2,1)S(1)}, u32[]{:S(2)}, u32[]{:S(2)}) %collective-permute-start.10) | collective-permute-done | bytes 176 | tf_op jit(solution)/shard_map/ppermute | solution.py:151
  50.1 0.2 slice_reduce_fusion
  50.4 0.1 lt.46
  50.5 0.1 fusion.13
  50.7 1.2 %gather_fusion.1 = s32[8]{0:T(128)} fusion(s32[8]{0:T(128)S(1)} %convert_element_type.22, s32[1024]{0:T(1024)S(1)} %pad_clamp_fusion), kind=kCustom, calls=%fused_computation.1 | custom fusion | bytes 96 | tf_op jit(solution)/shard_map/gather | solution.py:174
  51.9 1.2 %gather_fusion = s32[8]{0:T(128)} fusion(s32[8]{0:T(128)S(1)} %convert_element_type.22, s32[1024]{0:T(1024)S(1)} %pad_clamp_fusion.1), kind=kCustom, calls=%fused_computation | custom fusion | bytes 96 | tf_op jit(solution)/shard_map/gather | solution.py:171
  53.0 7.6 %shard_map.95 = f32[16,512]{1,0:T(8,128)} custom-call(s32[8]{0:T(128)} %gather_fusion, bf16[512,192]{1,0:T(8,128)(2,1)} %multiply_bitcast_fusion.xo_ref, f32[512,1]{1,0:T(8,128)} %copy.42.no_ref, f32[512,1]{1,0:T(8,128)} %copy.43.ro_ref, bf16[8,224,512]{2,1,0:T(8,128)(2,1)} %copy-done.1, bf16[8,224,512]{2,1,0:T(8,128)(2,1)} %copy-done.1), custom_call_target="tpu_custom_call" | custom-call | tf_op jit(solution)/shard_map/pallas_call | solution.py:59
  60.6 7.7 %shard_map.96 = f32[16,512]{1,0:T(8,128)} custom-call(s32[8]{0:T(128)} %gather_fusion.1, bf16[512,192]{1,0:T(8,128)(2,1)} %multiply_bitcast_fusion.xo_ref, f32[512,1]{1,0:T(8,128)} %copy.42.no_ref, f32[512,1]{1,0:T(8,128)} %copy.43.ro_ref, bf16[8,224,512]{2,1,0:T(8,128)(2,1)} %collective-permute-done.11.x_ref.w_ref, ...), custom_call_target="tpu_custom_call" | custom-call | tf_op jit(solution)/shard_map/pallas_call | solution.py:59
  68.4 0.9 %convolution_bitcast_fusion = f32[16,16]{0,1:T(8,128)S(1)} fusion(f32[16,512]{1,0:T(8,128)S(1)} %copy-done.4, f32[16,512]{1,0:T(8,128)S(1)} %copy-done.3, f32[16,512]{1,0:T(8,128)} %shard_map.96, f32[512]{0:T(512)S(1)} %broadcast_multiply_fusion), kind=kOutput, calls=%fused_computation.4 | convolution fusion | flops 1589248 | bytes 101376 | tf_op jit(solution)/shard_map/dot_general | solution.py:177
  69.3 0.2 collective-permute-start.12
  69.4 1.0 %collective-permute-done.12 = f32[16,16]{0,1:T(8,128)S(1)} collective-permute-done((f32[16,16]{0,1:T(8,128)S(1)}, f32[16,16]{0,1:T(8,128)S(1)}, u32[]{:S(2)}, u32[]{:S(2)}) %collective-permute-start.12) | collective-permute-done | bytes 1056 | tf_op jit(solution)/shard_map/ppermute | solution.py:119
  70.5 0.4 collective-permute-start.13
  70.9 3.2 %collective-permute-done.13 = f32[16,16]{0,1:T(8,128)S(1)} collective-permute-done((f32[16,16]{0,1:T(8,128)S(1)}, f32[16,16]{0,1:T(8,128)S(1)}, u32[]{:S(2)}, u32[]{:S(2)}) %collective-permute-start.13) | collective-permute-done | bytes 1056 | tf_op jit(solution)/shard_map/ppermute | solution.py:119
  74.1 3.6 %collective-permute-start.14 = (f32[16,16]{0,1:T(8,128)S(1)}, f32[16,16]{0,1:T(8,128)S(1)}, u32[]{:S(2)}, u32[]{:S(2)}) collective-permute-start(f32[16,16]{0,1:T(8,128)S(1)} %add.95), channel_id=1, source_target_pairs={{0,4},{1,5},{2,6},{3,7},{4,0},{5,1},{6,2},{7,3},{8,12},{9,13},{10,... | collective-permute-start | bytes 3080 | tf_op jit(solution)/shard_map/ppermute | solution.py:119
  77.8 1.6 %collective-permute-done.14 = f32[16,16]{0,1:T(8,128)S(1)} collective-permute-done((f32[16,16]{0,1:T(8,128)S(1)}, f32[16,16]{0,1:T(8,128)S(1)}, u32[]{:S(2)}, u32[]{:S(2)}) %collective-permute-start.14) | collective-permute-done | bytes 1056 | tf_op jit(solution)/shard_map/ppermute | solution.py:119
  79.4 2.9 %collective-permute-start.15 = (f32[16,16]{0,1:T(8,128)S(1)}, f32[16,16]{0,1:T(8,128)S(1)}, u32[]{:S(2)}, u32[]{:S(2)}) collective-permute-start(f32[16,16]{0,1:T(8,128)S(1)} %add.96), channel_id=1, source_target_pairs={{0,8},{1,9},{2,10},{3,11},{4,12},{5,13},{6,14},{7,15},{8,0},{9,1},... | collective-permute-start | bytes 3080 | tf_op jit(solution)/shard_map/ppermute | solution.py:119
  82.3 0.1 fusion.20
  82.4 1.5 %collective-permute-done.15 = f32[16,16]{0,1:T(8,128)S(1)} collective-permute-done((f32[16,16]{0,1:T(8,128)S(1)}, f32[16,16]{0,1:T(8,128)S(1)}, u32[]{:S(2)}, u32[]{:S(2)}) %collective-permute-start.15) | collective-permute-done | bytes 1056 | tf_op jit(solution)/shard_map/ppermute | solution.py:119
  83.9 0.7 copy.46
  84.6 1.5 %fusion = f32[16,512]{1,0:T(8,128)} fusion(f32[16,512]{1,0:T(8,128)S(1)} %fusion.20, f32[16,16]{0,1:T(8,128)S(1)} %add_multiply_fusion.2, f32[16,512]{1,0:T(8,128)S(1)} %copy-done.4, f32[512]{0:T(512)S(1)} %broadcast_multiply_fusion, f32[16,512]{1,0:T(8,128)S(1)} %copy-done.3, f32[16,512]{1,0:T(8,128)} %shard_map.96), kind=kOutput, calls=%fused_computation.3 | convolution fusion | flops 1605632 | bytes 166912 | tf_op jit(solution)/shard_map/dot_general | solution.py:181
  (55 shorter events, 1.4 us)
Async XLA Ops:
  0.6 81.7 %copy-start = (f32[16,512]{1,0:T(8,128)S(1)}, f32[16,512]{1,0:T(8,128)}, u32[]{:S(2)}) copy-start(f32[16,512]{1,0:T(8,128)} %param.12) | copy-start | bytes 98308
  0.6 17.5 %copy-start.2 = (bf16[192,512]{1,0:T(8,128)(2,1)S(1)}, bf16[192,512]{1,0:T(8,128)(2,1)}, u32[]{:S(2)}) copy-start(bf16[192,512]{1,0:T(8,128)(2,1)} %param.8) | copy-start | bytes 589828
  4.7 13.5 %collective-permute-start.1 = (bf16[224,512]{1,0:T(8,128)(2,1)S(1)}, bf16[224,512]{1,0:T(8,128)(2,1)S(1)}, u32[]{:S(2)}, u32[]{:S(2)}) collective-permute-start(bf16[224,512]{1,0:T(8,128)(2,1)S(1)} %fusion.7), channel_id=1, source_target_pairs={{4,0},{5,1},{6,2},{7,3},{8,4},{9,5},{10,6},{11,7},{12,8},{13,9},{1... | collective-permute-start | bytes 688136 | tf_op jit(solution)/shard_map/ppermute | solution.py:80
  6.0 12.2 %collective-permute-start = (bf16[224,512]{1,0:T(8,128)(2,1)S(1)}, bf16[224,512]{1,0:T(8,128)(2,1)S(1)}, u32[]{:S(2)}, u32[]{:S(2)}) collective-permute-start(bf16[224,512]{1,0:T(8,128)(2,1)S(1)} %fusion.7), channel_id=1, source_target_pairs={{0,4},{1,5},{2,6},{3,7},{4,8},{5,9},{6,10},{7,11},{8,12},{9,13},{1... | collective-permute-start | bytes 688136 | tf_op jit(solution)/shard_map/ppermute | solution.py:79
  11.6 28.6 %collective-permute-start.6 = (bf16[224,512]{1,0:T(8,128)(2,1)S(1)}, bf16[224,512]{1,0:T(8,128)(2,1)S(1)}, u32[]{:S(2)}, u32[]{:S(2)}) collective-permute-start(bf16[224,512]{1,0:T(8,128)(2,1)S(1)} %fusion.7), channel_id=1, source_target_pairs={{0,2},{1,3},{2,0},{3,1},{4,6},{5,7},{6,4},{7,5},{8,10},{9,11},{10,... | collective-permute-start | bytes 688136 | tf_op jit(solution)/shard_map/ppermute | solution.py:81
  18.3 22.0 %collective-permute-start.8 = (bf16[2,224,512]{2,1,0:T(8,128)(2,1)S(1)}, bf16[2,224,512]{2,1,0:T(8,128)(2,1)S(1)}, u32[]{:S(2)}, u32[]{:S(2)}) collective-permute-start(bf16[2,224,512]{2,1,0:T(8,128)(2,1)S(1)} %pad_maximum_fusion), channel_id=1, source_target_pairs={{0,2},{1,3},{2,0},{3,1},{4,6},{5,7},{6,4},{7,5},{8,10},{9,11},{10,... | collective-permute-start | bytes 1376264 | tf_op jit(solution)/shard_map/ppermute | solution.py:84
  18.4 8.4 %collective-permute-start.3 = (bf16[224,512]{1,0:T(8,128)(2,1)S(1)}, bf16[224,512]{1,0:T(8,128)(2,1)S(1)}, u32[]{:S(2)}, u32[]{:S(2)}) collective-permute-start(bf16[224,512]{1,0:T(8,128)(2,1)S(1)} %collective-permute-done.1), channel_id=1, source_target_pairs={{4,0},{5,1},{6,2},{7,3},{8,4},{9,5},{10,6},{11,7},{12,8},{13,9},{1... | collective-permute-start | bytes 688136 | tf_op jit(solution)/shard_map/ppermute | solution.py:83
  19.7 8.3 %collective-permute-start.2 = (bf16[224,512]{1,0:T(8,128)(2,1)S(1)}, bf16[224,512]{1,0:T(8,128)(2,1)S(1)}, u32[]{:S(2)}, u32[]{:S(2)}) collective-permute-start(bf16[224,512]{1,0:T(8,128)(2,1)S(1)} %collective-permute-done), channel_id=1, source_target_pairs={{0,4},{1,5},{2,6},{3,7},{4,8},{5,9},{6,10},{7,11},{8,12},{9,13},{1... | collective-permute-start | bytes 688136 | tf_op jit(solution)/shard_map/ppermute | solution.py:82
  28.1 12.2 %collective-permute-start.7 = (bf16[224,512]{1,0:T(8,128)(2,1)S(1)}, bf16[224,512]{1,0:T(8,128)(2,1)S(1)}, u32[]{:S(2)}, u32[]{:S(2)}) collective-permute-start(bf16[224,512]{1,0:T(8,128)(2,1)S(1)} %broadcast_select_fusion.1), channel_id=1, source_target_pairs={{0,2},{1,3},{2,0},{3,1},{4,6},{5,7},{6,4},{7,5},{8,10},{9,11},{10,... | collective-permute-start | bytes 688136 | tf_op jit(solution)/shard_map/ppermute | solution.py:88
  29.8 8.4 %collective-permute-start.5 = (bf16[224,512]{1,0:T(8,128)(2,1)S(1)}, bf16[224,512]{1,0:T(8,128)(2,1)S(1)}, u32[]{:S(2)}, u32[]{:S(2)}) collective-permute-start(bf16[224,512]{1,0:T(8,128)(2,1)S(1)} %collective-permute-done.3), channel_id=1, source_target_pairs={{4,0},{5,1},{6,2},{7,3},{8,4},{9,5},{10,6},{11,7},{12,8},{13,9},{1... | collective-permute-start | bytes 688136 | tf_op jit(solution)/shard_map/ppermute | solution.py:87
  31.1 8.5 %collective-permute-start.4 = (bf16[224,512]{1,0:T(8,128)(2,1)S(1)}, bf16[224,512]{1,0:T(8,128)(2,1)S(1)}, u32[]{:S(2)}, u32[]{:S(2)}) collective-permute-start(bf16[224,512]{1,0:T(8,128)(2,1)S(1)} %collective-permute-done.2), channel_id=1, source_target_pairs={{0,4},{1,5},{2,6},{3,7},{4,8},{5,9},{6,10},{7,11},{8,12},{9,13},{1... | collective-permute-start | bytes 688136 | tf_op jit(solution)/shard_map/ppermute | solution.py:86
  39.7 6.3 %copy-start.6 = (f32[512]{0:T(512)S(1)}, f32[512]{0:T(512)}, u32[]{:S(2)}) copy-start(f32[512]{0:T(512)} %param.10) | copy-start | bytes 6148
  39.7 6.1 %collective-permute-start.9 = (bf16[224,512]{1,0:T(8,128)(2,1)S(1)}, bf16[224,512]{1,0:T(8,128)(2,1)S(1)}, u32[]{:S(2)}, u32[]{:S(2)}) collective-permute-start(bf16[224,512]{1,0:T(8,128)(2,1)S(1)} %broadcast_select_fusion), channel_id=1, source_target_pairs={{0,2},{1,3},{2,0},{3,1},{4,6},{5,7},{6,4},{7,5},{8,10},{9,11},{10,... | collective-permute-start | bytes 688136 | tf_op jit(solution)/shard_map/ppermute | solution.py:90
  45.9 7.2 %copy-start.1 = (bf16[8,224,512]{2,1,0:T(8,128)(2,1)}, bf16[8,224,512]{2,1,0:T(8,128)(2,1)S(1)}, u32[]{:S(2)}) copy-start(bf16[8,224,512]{2,1,0:T(8,128)(2,1)S(1)} %bitcast_dynamic-update-slice_fusion.x_ref.w_ref) | copy-start | bytes 5505028
  45.9 14.8 %collective-permute-start.11 = (bf16[8,224,512]{2,1,0:T(8,128)(2,1)S(1)}, bf16[8,224,512]{2,1,0:T(8,128)(2,1)}, u32[]{:S(2)}, u32[]{:S(2)}) collective-permute-start(bf16[8,224,512]{2,1,0:T(8,128)(2,1)S(1)} %bitcast_dynamic-update-slice_fusion.x_ref.w_ref), channel_id=1, source_target_pairs={{0,1},{1,0},{2,3},{3,2},{4,5},{5,4},{6,7},{7,6},{8,9},{9,8},{10,11... | collective-permute-start | bytes 5505032 | tf_op jit(solution)/shard_map/ppermute | solution.py:109
  46.9 2.8 %collective-permute-start.10 = (bf16[8,9]{1,0:T(8,128)(2,1)S(1)}, bf16[8,9]{1,0:T(8,128)(2,1)S(1)}, u32[]{:S(2)}, u32[]{:S(2)}) collective-permute-start(bf16[8,9]{1,0:T(8,128)(2,1)S(1)} %bitcast.58), channel_id=1, source_target_pairs={{0,1},{1,0},{2,3},{3,2},{4,5},{5,4},{6,7},{7,6},{8,9},{9,8},{10,11... | collective-permute-start | bytes 440 | tf_op jit(solution)/shard_map/ppermute | solution.py:151
  60.6 7.7 %copy-start.3 = (f32[16,512]{1,0:T(8,128)S(1)}, f32[16,512]{1,0:T(8,128)}, u32[]{:S(2)}) copy-start(f32[16,512]{1,0:T(8,128)} %shard_map.95) | copy-start | bytes 98308
  60.6 7.7 %copy-start.4 = (f32[16,512]{1,0:T(8,128)S(1)}, f32[16,512]{1,0:T(8,128)}, u32[]{:S(2)}) copy-start(f32[16,512]{1,0:T(8,128)} %param.11) | copy-start | bytes 98308
  60.6 21.7 %copy-start.5 = (f32[16,16]{1,0:T(8,128)S(1)}, f32[16,16]{1,0:T(8,128)}, u32[]{:S(2)}) copy-start(f32[16,16]{1,0:T(8,128)} %param.13) | copy-start | bytes 3076
  69.3 1.2 %collective-permute-start.12 = (f32[16,16]{0,1:T(8,128)S(1)}, f32[16,16]{0,1:T(8,128)S(1)}, u32[]{:S(2)}, u32[]{:S(2)}) collective-permute-start(f32[16,16]{0,1:T(8,128)S(1)} %convolution_bitcast_fusion), channel_id=1, source_target_pairs={{0,1},{1,0},{2,3},{3,2},{4,5},{5,4},{6,7},{7,6},{8,9},{9,8},{10,11... | collective-permute-start | bytes 3080 | tf_op jit(solution)/shard_map/ppermute | solution.py:119
  70.5 3.7 %collective-permute-start.13 = (f32[16,16]{0,1:T(8,128)S(1)}, f32[16,16]{0,1:T(8,128)S(1)}, u32[]{:S(2)}, u32[]{:S(2)}) collective-permute-start(f32[16,16]{0,1:T(8,128)S(1)} %add.94), channel_id=1, source_target_pairs={{0,2},{1,3},{2,0},{3,1},{4,6},{5,7},{6,4},{7,5},{8,10},{9,11},{10,... | collective-permute-start | bytes 3080 | tf_op jit(solution)/shard_map/ppermute | solution.py:119
  74.1 5.3 %collective-permute-start.14 = (f32[16,16]{0,1:T(8,128)S(1)}, f32[16,16]{0,1:T(8,128)S(1)}, u32[]{:S(2)}, u32[]{:S(2)}) collective-permute-start(f32[16,16]{0,1:T(8,128)S(1)} %add.95), channel_id=1, source_target_pairs={{0,4},{1,5},{2,6},{3,7},{4,0},{5,1},{6,2},{7,3},{8,12},{9,13},{10,... | collective-permute-start | bytes 3080 | tf_op jit(solution)/shard_map/ppermute | solution.py:119
  79.4 4.5 %collective-permute-start.15 = (f32[16,16]{0,1:T(8,128)S(1)}, f32[16,16]{0,1:T(8,128)S(1)}, u32[]{:S(2)}, u32[]{:S(2)}) collective-permute-start(f32[16,16]{0,1:T(8,128)S(1)} %add.96), channel_id=1, source_target_pairs={{0,8},{1,9},{2,10},{3,11},{4,12},{5,13},{6,14},{7,15},{8,0},{9,1},... | collective-permute-start | bytes 3080 | tf_op jit(solution)/shard_map/ppermute | solution.py:119

commit v7 on v6

--- a/solution.py
+++ b/solution.py
@@ -15,39 +15,41 @@
 HIGHEST = lax.Precision.HIGHEST
 
 
-def affinity_kernel(width, flag_ref, xo_ref, no_ref, ro_ref, x_ref, w_ref, out_ref):
+def affinity_kernel(width, per, flag_ref, xo_ref, no_ref, ro_ref, x_ref, w_ref, out_ref):
     s = pl.program_id(0)
 
     @pl.when(s == 0)
     def _():
         out_ref[...] = jnp.zeros_like(out_ref)
 
-    @pl.when(flag_ref[s] != 0)
-    def _():
-        x_cols = x_ref[0, :width, :]
-        x_wide = x_cols.astype(jnp.float32)
-        norm_cols = jnp.sum(x_wide * x_wide, axis=0, keepdims=True)
-        recip_cols = 1.0 / w_ref[0, LANCZOS : LANCZOS + 1, :].astype(jnp.float32)
-        twice_inner = jnp.dot(xo_ref[...], x_cols, preferred_element_type=jnp.float32)
-        distance = (no_ref[...] + norm_cols) - twice_inner
-        weights = jnp.exp2(distance * (ro_ref[...] * recip_cols)).astype(jnp.bfloat16)
-        out_ref[...] += lax.dot_general(
-            w_ref[0, :LANCZOS, :], weights, (((1,), (1,)), ((), ())),
-            preferred_element_type=jnp.float32,
-        )
+    for k in range(per):
+
+        @pl.when(flag_ref[s * per + k] != 0)
+        def _():
+            x_cols = x_ref[k, :width, :]
+            x_wide = x_cols.astype(jnp.float32)
+            norm_cols = jnp.sum(x_wide * x_wide, axis=0, keepdims=True)
+            recip_cols = 1.0 / w_ref[k, LANCZOS : LANCZOS + 1, :].astype(jnp.float32)
+            twice_inner = jnp.dot(xo_ref[...], x_cols, preferred_element_type=jnp.float32)
+            distance = (no_ref[...] + norm_cols) - twice_inner
+            weights = jnp.exp2(distance * (ro_ref[...] * recip_cols)).astype(jnp.bfloat16)
+            out_ref[...] += lax.dot_general(
+                w_ref[k, :LANCZOS, :], weights, (((1,), (1,)), ((), ())),
+                preferred_element_type=jnp.float32,
+            )
 
 
 def own_rows_product(flags, own_terms, mine, width):
     twice_own_t, norm_own, recip_own = own_terms
     own = twice_own_t.shape[0]
-    rows = mine.shape[1]
-    half = mine.shape[0]
+    slots, rows = mine.shape[0], mine.shape[1]
+    per = 2 if slots % 2 == 0 else 1
     lanes_row = width // LANCZOS
-    x_spec = pl.BlockSpec((1, rows, own), lambda s, m: (s, 0, 0))
-    w_spec = pl.BlockSpec((1, 2 * LANCZOS, own), lambda s, m: (s, lanes_row // 2, 0))
+    x_spec = pl.BlockSpec((per, rows, own), lambda s, m: (s, 0, 0))
+    w_spec = pl.BlockSpec((per, 2 * LANCZOS, own), lambda s, m: (s, lanes_row // 2, 0))
     grid_spec = pltpu.PrefetchScalarGridSpec(
         num_scalar_prefetch=1,
-        grid=(half,),
+        grid=(slots // per,),
         in_specs=[
             pl.BlockSpec((own, width), lambda s, m: (0, 0)),
             pl.BlockSpec((own, 1), lambda s, m: (0, 0)),
@@ -57,7 +59,7 @@
         out_specs=pl.BlockSpec((LANCZOS, own), lambda s, m: (0, 0)),
     )
     return pl.pallas_call(
-        functools.partial(affinity_kernel, width),
+        functools.partial(affinity_kernel, width, per),
         grid_spec=grid_spec,
         out_shape=jax.ShapeDtypeStruct((LANCZOS, own), jnp.float32),
     )(flags, twice_own_t, norm_own, recip_own, mine, mine)

time: 87.1 us -> 84.3 us (0.968)
  Pallas kernels: 15.3 us -> 12.9 us
    pallas_call x2, Pallas kernels: 15.3 us -> 12.9 us  [own_rows_product(): pl.pallas_call(functools.partial(affinity_kernel, width, per), grid_spec=...]
  transfers between devices with their start and end apart: 16 -> 16, of which waited for: 10 -> 10; matrix products, arithmetic and copies ran while one was open for 11% -> 11% of each run, Pallas kernels for 9% -> 8%
where the time goes in v7:
time: 84.3 us; the launch traced here: 83.8 us
  starting transfers between devices  30.9 us (37%)
  waiting for transfers between devices  22.5 us (27%)
  Pallas kernels  12.9 us (15%)
  local copies, waits for them, and re-layouts  7.59 us (9%)
  other arithmetic  5.85 us (7%)
  matrix products  2.58 us (3%)
  between operations  1.6 us (2%)
    pallas_call x2, Pallas kernels, own_rows_product(): pl.pallas_call(functools.partial(affinity_kernel, width, per), grid_spec=...  12.9 us
    ppermute x4, waiting for transfers between devices, sum_over_rows(): lax.ppermute(value, 'row', [(i, i ^ stride) for i in range(devices)])  7.79 us
    ppermute x4, starting transfers between devices, sum_over_rows(): lax.ppermute(value, 'row', [(i, i ^ stride) for i in range(devices)])  6.84 us
    ppermute x1, starting transfers between devices, gather_pieces(): up1 = lax.ppermute(packed, 'row', up)  5.57 us
    ppermute x1, waiting for transfers between devices, gather_pieces(): across4 = lax.ppermute(pick3, 'row', across)  5.41 us
    ppermute x1, starting transfers between devices, gather_pieces(): up3 = lax.ppermute(up2, 'row', up)  5.03 us
    ppermute x1, starting transfers between devices, gather_pieces(): up2 = lax.ppermute(up1, 'row', up)  4.83 us
    ppermute x1, waiting for transfers between devices, shards(): plans = jnp.concatenate([plans, lax.ppermute(plans, 'row', twin)])  2.39 us
  transfers between devices with their start and end apart: 16, of which 10 were waited for; matrix products, arithmetic and copies ran while one was open for 11% of the time, Pallas kernels for 8%

profile of v7, /device:TPU:0, one launch (start us, length us, event | category | flops | bytes accessed | tf_op | source)
XLA Modules:
  0.0 83.8 jit_solution(6309619387675494544)
XLA Ops:
  0.7 0.7 convert.7
  1.4 0.1 copy.36
  2.3 0.7 broadcast_in_dim.8
  3.0 0.8 multiply_convert_fusion
  3.8 0.9 %fusion.7 = bf16[224,512]{1,0:T(8,128)(2,1)S(1)} fusion(bf16[1,512]{1,0:T(2,128)(2,1)S(1)} %broadcast_in_dim.9, bf16[1,512]{1,0:T(2,128)(2,1)S(1)} %broadcast_in_dim.8, bf16[16,512]{1,0:T(8,128)(2,1)S(1)} %multiply_convert_fusion, bf16[192,512]{1,0:T(8,128)(2,1)} %param.8), kind=kLoop, calls=%fused_computation.15 | loop fusion | flops 1490944 | bytes 444416 | tf_op jit(solution)/shard_map/concatenate | solution.py:143
  4.7 1.3 %collective-permute-start.1 = (bf16[224,512]{1,0:T(8,128)(2,1)S(1)}, bf16[224,512]{1,0:T(8,128)(2,1)S(1)}, u32[]{:S(2)}, u32[]{:S(2)}) collective-permute-start(bf16[224,512]{1,0:T(8,128)(2,1)S(1)} %fusion.7), channel_id=1, source_target_pairs={{4,0},{5,1},{6,2},{7,3},{8,4},{9,5},{10,6},{11,7},{12,8},{13,9},{1... | collective-permute-start | bytes 688136 | tf_op jit(solution)/shard_map/ppermute | solution.py:82
  6.0 5.6 %collective-permute-start = (bf16[224,512]{1,0:T(8,128)(2,1)S(1)}, bf16[224,512]{1,0:T(8,128)(2,1)S(1)}, u32[]{:S(2)}, u32[]{:S(2)}) collective-permute-start(bf16[224,512]{1,0:T(8,128)(2,1)S(1)} %fusion.7), channel_id=1, source_target_pairs={{0,4},{1,5},{2,6},{3,7},{4,8},{5,9},{6,10},{7,11},{8,12},{9,13},{1... | collective-permute-start | bytes 688136 | tf_op jit(solution)/shard_map/ppermute | solution.py:81
  11.6 2.0 %collective-permute-start.6 = (bf16[224,512]{1,0:T(8,128)(2,1)S(1)}, bf16[224,512]{1,0:T(8,128)(2,1)S(1)}, u32[]{:S(2)}, u32[]{:S(2)}) collective-permute-start(bf16[224,512]{1,0:T(8,128)(2,1)S(1)} %fusion.7), channel_id=1, source_target_pairs={{0,2},{1,3},{2,0},{3,1},{4,6},{5,7},{6,4},{7,5},{8,10},{9,11},{10,... | collective-permute-start | bytes 688136 | tf_op jit(solution)/shard_map/ppermute | solution.py:83
  13.6 1.1 %copy.40 = bf16[192,512]{0,1:T(8,128)(2,1)S(1)} copy(bf16[192,512]{1,0:T(8,128)(2,1)} %param.8) | data formatting | bytes 393216 | tf_op args[0]
  14.7 0.7 convert_divide_fusion
  15.4 1.0 %multiply_reduce_fusion = f32[512]{0:T(512)S(1)} fusion(bf16[192,512]{1,0:T(8,128)(2,1)} %param.8), kind=kLoop, calls=%fused_computation.11 | loop fusion | flops 294400 | bytes 198656 | tf_op jit(solution)/shard_map/reduce_sum | solution.py:169
  16.4 0.9 %copy.42.no_ref = f32[512,1]{1,0:T(8,128)} copy(f32[512,1]{0,1:T(1,128)S(1)} %bitcast.56) | data formatting | bytes 4096 | tf_op jit(solution)/shard_map/broadcast_in_dim | solution.py:169
  17.2 0.9 %copy.43.ro_ref = f32[512,1]{1,0:T(8,128)} copy(f32[512,1]{0,1:T(1,128)S(1)} %bitcast.57) | data formatting | bytes 4096 | tf_op jit(solution)/shard_map/broadcast_in_dim | solution.py:171
  18.1 0.1 stack.80
  18.3 0.1 collective-permute-start.8
  18.4 1.3 %collective-permute-start.3 = (bf16[224,512]{1,0:T(8,128)(2,1)S(1)}, bf16[224,512]{1,0:T(8,128)(2,1)S(1)}, u32[]{:S(2)}, u32[]{:S(2)}) collective-permute-start(bf16[224,512]{1,0:T(8,128)(2,1)S(1)} %collective-permute-done.1), channel_id=1, source_target_pairs={{4,0},{5,1},{6,2},{7,3},{8,4},{9,5},{10,6},{11,7},{12,8},{13,9},{1... | collective-permute-start | bytes 688136 | tf_op jit(solution)/shard_map/ppermute | solution.py:85
  19.7 4.8 %collective-permute-start.2 = (bf16[224,512]{1,0:T(8,128)(2,1)S(1)}, bf16[224,512]{1,0:T(8,128)(2,1)S(1)}, u32[]{:S(2)}, u32[]{:S(2)}) collective-permute-start(bf16[224,512]{1,0:T(8,128)(2,1)S(1)} %collective-permute-done), channel_id=1, source_target_pairs={{0,4},{1,5},{2,6},{3,7},{4,8},{5,9},{6,10},{7,11},{8,12},{9,13},{1... | collective-permute-start | bytes 688136 | tf_op jit(solution)/shard_map/ppermute | solution.py:84
  24.6 2.2 %collective-permute-done.3 = bf16[224,512]{1,0:T(8,128)(2,1)S(1)} collective-permute-done((bf16[224,512]{1,0:T(8,128)(2,1)S(1)}, bf16[224,512]{1,0:T(8,128)(2,1)S(1)}, u32[]{:S(2)}, u32[]{:S(2)}) %collective-permute-start.3) | collective-permute-done | bytes 229408 | tf_op jit(solution)/shard_map/ppermute | solution.py:85
  26.8 1.2 %collective-permute-done.2 = bf16[224,512]{1,0:T(8,128)(2,1)S(1)} collective-permute-done((bf16[224,512]{1,0:T(8,128)(2,1)S(1)}, bf16[224,512]{1,0:T(8,128)(2,1)S(1)}, u32[]{:S(2)}, u32[]{:S(2)}) %collective-permute-start.2) | collective-permute-done | bytes 229408 | tf_op jit(solution)/shard_map/ppermute | solution.py:84
  28.1 1.8 %collective-permute-start.7 = (bf16[224,512]{1,0:T(8,128)(2,1)S(1)}, bf16[224,512]{1,0:T(8,128)(2,1)S(1)}, u32[]{:S(2)}, u32[]{:S(2)}) collective-permute-start(bf16[224,512]{1,0:T(8,128)(2,1)S(1)} %broadcast_select_fusion.1), channel_id=1, source_target_pairs={{0,2},{1,3},{2,0},{3,1},{4,6},{5,7},{6,4},{7,5},{8,10},{9,11},{10,... | collective-permute-start | bytes 688136 | tf_op jit(solution)/shard_map/ppermute | solution.py:90
  29.8 1.3 %collective-permute-start.5 = (bf16[224,512]{1,0:T(8,128)(2,1)S(1)}, bf16[224,512]{1,0:T(8,128)(2,1)S(1)}, u32[]{:S(2)}, u32[]{:S(2)}) collective-permute-start(bf16[224,512]{1,0:T(8,128)(2,1)S(1)} %collective-permute-done.3), channel_id=1, source_target_pairs={{4,0},{5,1},{6,2},{7,3},{8,4},{9,5},{10,6},{11,7},{12,8},{13,9},{1... | collective-permute-start | bytes 688136 | tf_op jit(solution)/shard_map/ppermute | solution.py:89
  31.1 5.0 %collective-permute-start.4 = (bf16[224,512]{1,0:T(8,128)(2,1)S(1)}, bf16[224,512]{1,0:T(8,128)(2,1)S(1)}, u32[]{:S(2)}, u32[]{:S(2)}) collective-permute-start(bf16[224,512]{1,0:T(8,128)(2,1)S(1)} %collective-permute-done.2), channel_id=1, source_target_pairs={{0,4},{1,5},{2,6},{3,7},{4,8},{5,9},{6,10},{7,11},{8,12},{9,13},{1... | collective-permute-start | bytes 688136 | tf_op jit(solution)/shard_map/ppermute | solution.py:88
  36.2 1.9 %collective-permute-done.5 = bf16[224,512]{1,0:T(8,128)(2,1)S(1)} collective-permute-done((bf16[224,512]{1,0:T(8,128)(2,1)S(1)}, bf16[224,512]{1,0:T(8,128)(2,1)S(1)}, u32[]{:S(2)}, u32[]{:S(2)}) %collective-permute-start.5) | collective-permute-done | bytes 229408 | tf_op jit(solution)/shard_map/ppermute | solution.py:89
  38.2 1.5 %collective-permute-done.4 = bf16[224,512]{1,0:T(8,128)(2,1)S(1)} collective-permute-done((bf16[224,512]{1,0:T(8,128)(2,1)S(1)}, bf16[224,512]{1,0:T(8,128)(2,1)S(1)}, u32[]{:S(2)}, u32[]{:S(2)}) %collective-permute-start.4) | collective-permute-done | bytes 229408 | tf_op jit(solution)/shard_map/ppermute | solution.py:88
  39.7 0.4 collective-permute-start.9
  40.1 0.1 bitcast_dynamic-update-slice_fusion.3
  40.4 5.4 %collective-permute-done.9 = bf16[224,512]{1,0:T(8,128)(2,1)S(1)} collective-permute-done((bf16[224,512]{1,0:T(8,128)(2,1)S(1)}, bf16[224,512]{1,0:T(8,128)(2,1)S(1)}, u32[]{:S(2)}, u32[]{:S(2)}) %collective-permute-start.9) | collective-permute-done | bytes 229408 | tf_op jit(solution)/shard_map/ppermute | solution.py:92
  46.0 0.9 %multiply_bitcast_fusion.xo_ref = bf16[512,192]{1,0:T(8,128)(2,1)} fusion(bf16[192,512]{0,1:T(8,128)(2,1)S(1)} %copy.40), kind=kLoop, calls=%fused_computation.12 | loop fusion | flops 98304 | bytes 393216 | tf_op jit(solution)/shard_map/transpose | solution.py:172
  46.9 0.4 collective-permute-start.10
  47.3 2.4 %collective-permute-done.10 = bf16[8,9]{1,0:T(8,128)(2,1)S(1)} collective-permute-done((bf16[8,9]{1,0:T(8,128)(2,1)S(1)}, bf16[8,9]{1,0:T(8,128)(2,1)S(1)}, u32[]{:S(2)}, u32[]{:S(2)}) %collective-permute-start.10) | collective-permute-done | bytes 176 | tf_op jit(solution)/shard_map/ppermute | solution.py:153
  50.1 0.2 slice_reduce_fusion
  50.4 0.1 lt.46
  50.5 0.1 fusion.13
  50.7 1.2 %gather_fusion.1 = s32[8]{0:T(128)} fusion(s32[8]{0:T(128)S(1)} %convert_element_type.22, s32[1024]{0:T(1024)S(1)} %pad_clamp_fusion), kind=kCustom, calls=%fused_computation.1 | custom fusion | bytes 96 | tf_op jit(solution)/shard_map/gather | solution.py:176
  51.9 1.2 %gather_fusion = s32[8]{0:T(128)} fusion(s32[8]{0:T(128)S(1)} %convert_element_type.22, s32[1024]{0:T(1024)S(1)} %pad_clamp_fusion.1), kind=kCustom, calls=%fused_computation | custom fusion | bytes 96 | tf_op jit(solution)/shard_map/gather | solution.py:173
  53.0 6.4 %shard_map.95 = f32[16,512]{1,0:T(8,128)} custom-call(s32[8]{0:T(128)} %gather_fusion, bf16[512,192]{1,0:T(8,128)(2,1)} %multiply_bitcast_fusion.xo_ref, f32[512,1]{1,0:T(8,128)} %copy.42.no_ref, f32[512,1]{1,0:T(8,128)} %copy.43.ro_ref, bf16[8,224,512]{2,1,0:T(8,128)(2,1)} %copy-done.1, bf16[8,224,512]{2,1,0:T(8,128)(2,1)} %copy-done.1), custom_call_target="tpu_custom_call" | custom-call | tf_op jit(solution)/shard_map/pallas_call | solution.py:61
  59.4 6.5 %shard_map.96 = f32[16,512]{1,0:T(8,128)} custom-call(s32[8]{0:T(128)} %gather_fusion.1, bf16[512,192]{1,0:T(8,128)(2,1)} %multiply_bitcast_fusion.xo_ref, f32[512,1]{1,0:T(8,128)} %copy.42.no_ref, f32[512,1]{1,0:T(8,128)} %copy.43.ro_ref, bf16[8,224,512]{2,1,0:T(8,128)(2,1)} %collective-permute-done.11.x_ref.w_ref, ...), custom_call_target="tpu_custom_call" | custom-call | tf_op jit(solution)/shard_map/pallas_call | solution.py:61
  65.9 0.9 %convolution_bitcast_fusion = f32[16,16]{0,1:T(8,128)S(1)} fusion(f32[16,512]{1,0:T(8,128)S(1)} %copy-done.4, f32[16,512]{1,0:T(8,128)S(1)} %copy-done.3, f32[16,512]{1,0:T(8,128)} %shard_map.96, f32[512]{0:T(512)S(1)} %broadcast_multiply_fusion), kind=kOutput, calls=%fused_computation.4 | convolution fusion | flops 1589248 | bytes 101376 | tf_op jit(solution)/shard_map/dot_general | solution.py:179
  66.8 0.2 collective-permute-start.12
  67.0 1.0 %collective-permute-done.12 = f32[16,16]{0,1:T(8,128)S(1)} collective-permute-done((f32[16,16]{0,1:T(8,128)S(1)}, f32[16,16]{0,1:T(8,128)S(1)}, u32[]{:S(2)}, u32[]{:S(2)}) %collective-permute-start.12) | collective-permute-done | bytes 1056 | tf_op jit(solution)/shard_map/ppermute | solution.py:121
  68.0 3.6 %collective-permute-done.13 = f32[16,16]{0,1:T(8,128)S(1)} collective-permute-done((f32[16,16]{0,1:T(8,128)S(1)}, f32[16,16]{0,1:T(8,128)S(1)}, u32[]{:S(2)}, u32[]{:S(2)}) %collective-permute-start.13) | collective-permute-done | bytes 1056 | tf_op jit(solution)/shard_map/ppermute | solution.py:121
  71.7 3.5 %collective-permute-start.14 = (f32[16,16]{0,1:T(8,128)S(1)}, f32[16,16]{0,1:T(8,128)S(1)}, u32[]{:S(2)}, u32[]{:S(2)}) collective-permute-start(f32[16,16]{0,1:T(8,128)S(1)} %add.95), channel_id=1, source_target_pairs={{0,4},{1,5},{2,6},{3,7},{4,0},{5,1},{6,2},{7,3},{8,12},{9,13},{10,... | collective-permute-start | bytes 3080 | tf_op jit(solution)/shard_map/ppermute | solution.py:121
  75.2 1.6 %collective-permute-done.14 = f32[16,16]{0,1:T(8,128)S(1)} collective-permute-done((f32[16,16]{0,1:T(8,128)S(1)}, f32[16,16]{0,1:T(8,128)S(1)}, u32[]{:S(2)}, u32[]{:S(2)}) %collective-permute-start.14) | collective-permute-done | bytes 1056 | tf_op jit(solution)/shard_map/ppermute | solution.py:121
  76.8 3.2 %collective-permute-start.15 = (f32[16,16]{0,1:T(8,128)S(1)}, f32[16,16]{0,1:T(8,128)S(1)}, u32[]{:S(2)}, u32[]{:S(2)}) collective-permute-start(f32[16,16]{0,1:T(8,128)S(1)} %add.96), channel_id=1, source_target_pairs={{0,8},{1,9},{2,10},{3,11},{4,12},{5,13},{6,14},{7,15},{8,0},{9,1},... | collective-permute-start | bytes 3080 | tf_op jit(solution)/shard_map/ppermute | solution.py:121
  80.0 0.1 fusion.20
  80.2 1.5 %collective-permute-done.15 = f32[16,16]{0,1:T(8,128)S(1)} collective-permute-done((f32[16,16]{0,1:T(8,128)S(1)}, f32[16,16]{0,1:T(8,128)S(1)}, u32[]{:S(2)}, u32[]{:S(2)}) %collective-permute-start.15) | collective-permute-done | bytes 1056 | tf_op jit(solution)/shard_map/ppermute | solution.py:121
  81.6 0.7 copy.46
  82.3 1.5 %fusion = f32[16,512]{1,0:T(8,128)} fusion(f32[16,512]{1,0:T(8,128)S(1)} %fusion.20, f32[16,16]{0,1:T(8,128)S(1)} %add_multiply_fusion.2, f32[16,512]{1,0:T(8,128)S(1)} %copy-done.4, f32[512]{0:T(512)S(1)} %broadcast_multiply_fusion, f32[16,512]{1,0:T(8,128)S(1)} %copy-done.3, f32[16,512]{1,0:T(8,128)} %shard_map.96), kind=kOutput, calls=%fused_computation.3 | convolution fusion | flops 1605632 | bytes 166912 | tf_op jit(solution)/shard_map/dot_general | solution.py:183
  (55 shorter events, 1.3 us)
Async XLA Ops:
  0.6 79.4 %copy-start = (f32[16,512]{1,0:T(8,128)S(1)}, f32[16,512]{1,0:T(8,128)}, u32[]{:S(2)}) copy-start(f32[16,512]{1,0:T(8,128)} %param.12) | copy-start | bytes 98308
  0.6 17.5 %copy-start.2 = (bf16[192,512]{1,0:T(8,128)(2,1)S(1)}, bf16[192,512]{1,0:T(8,128)(2,1)}, u32[]{:S(2)}) copy-start(bf16[192,512]{1,0:T(8,128)(2,1)} %param.8) | copy-start | bytes 589828
  4.7 13.5 %collective-permute-start.1 = (bf16[224,512]{1,0:T(8,128)(2,1)S(1)}, bf16[224,512]{1,0:T(8,128)(2,1)S(1)}, u32[]{:S(2)}, u32[]{:S(2)}) collective-permute-start(bf16[224,512]{1,0:T(8,128)(2,1)S(1)} %fusion.7), channel_id=1, source_target_pairs={{4,0},{5,1},{6,2},{7,3},{8,4},{9,5},{10,6},{11,7},{12,8},{13,9},{1... | collective-permute-start | bytes 688136 | tf_op jit(solution)/shard_map/ppermute | solution.py:82
  6.0 12.2 %collective-permute-start = (bf16[224,512]{1,0:T(8,128)(2,1)S(1)}, bf16[224,512]{1,0:T(8,128)(2,1)S(1)}, u32[]{:S(2)}, u32[]{:S(2)}) collective-permute-start(bf16[224,512]{1,0:T(8,128)(2,1)S(1)} %fusion.7), channel_id=1, source_target_pairs={{0,4},{1,5},{2,6},{3,7},{4,8},{5,9},{6,10},{7,11},{8,12},{9,13},{1... | collective-permute-start | bytes 688136 | tf_op jit(solution)/shard_map/ppermute | solution.py:81
  11.6 28.6 %collective-permute-start.6 = (bf16[224,512]{1,0:T(8,128)(2,1)S(1)}, bf16[224,512]{1,0:T(8,128)(2,1)S(1)}, u32[]{:S(2)}, u32[]{:S(2)}) collective-permute-start(bf16[224,512]{1,0:T(8,128)(2,1)S(1)} %fusion.7), channel_id=1, source_target_pairs={{0,2},{1,3},{2,0},{3,1},{4,6},{5,7},{6,4},{7,5},{8,10},{9,11},{10,... | collective-permute-start | bytes 688136 | tf_op jit(solution)/shard_map/ppermute | solution.py:83
  18.3 22.0 %collective-permute-start.8 = (bf16[2,224,512]{2,1,0:T(8,128)(2,1)S(1)}, bf16[2,224,512]{2,1,0:T(8,128)(2,1)S(1)}, u32[]{:S(2)}, u32[]{:S(2)}) collective-permute-start(bf16[2,224,512]{2,1,0:T(8,128)(2,1)S(1)} %pad_maximum_fusion), channel_id=1, source_target_pairs={{0,2},{1,3},{2,0},{3,1},{4,6},{5,7},{6,4},{7,5},{8,10},{9,11},{10,... | collective-permute-start | bytes 1376264 | tf_op jit(solution)/shard_map/ppermute | solution.py:86
  18.4 8.4 %collective-permute-start.3 = (bf16[224,512]{1,0:T(8,128)(2,1)S(1)}, bf16[224,512]{1,0:T(8,128)(2,1)S(1)}, u32[]{:S(2)}, u32[]{:S(2)}) collective-permute-start(bf16[224,512]{1,0:T(8,128)(2,1)S(1)} %collective-permute-done.1), channel_id=1, source_target_pairs={{4,0},{5,1},{6,2},{7,3},{8,4},{9,5},{10,6},{11,7},{12,8},{13,9},{1... | collective-permute-start | bytes 688136 | tf_op jit(solution)/shard_map/ppermute | solution.py:85
  19.7 8.3 %collective-permute-start.2 = (bf16[224,512]{1,0:T(8,128)(2,1)S(1)}, bf16[224,512]{1,0:T(8,128)(2,1)S(1)}, u32[]{:S(2)}, u32[]{:S(2)}) collective-permute-start(bf16[224,512]{1,0:T(8,128)(2,1)S(1)} %collective-permute-done), channel_id=1, source_target_pairs={{0,4},{1,5},{2,6},{3,7},{4,8},{5,9},{6,10},{7,11},{8,12},{9,13},{1... | collective-permute-start | bytes 688136 | tf_op jit(solution)/shard_map/ppermute | solution.py:84
  28.1 12.2 %collective-permute-start.7 = (bf16[224,512]{1,0:T(8,128)(2,1)S(1)}, bf16[224,512]{1,0:T(8,128)(2,1)S(1)}, u32[]{:S(2)}, u32[]{:S(2)}) collective-permute-start(bf16[224,512]{1,0:T(8,128)(2,1)S(1)} %broadcast_select_fusion.1), channel_id=1, source_target_pairs={{0,2},{1,3},{2,0},{3,1},{4,6},{5,7},{6,4},{7,5},{8,10},{9,11},{10,... | collective-permute-start | bytes 688136 | tf_op jit(solution)/shard_map/ppermute | solution.py:90
  29.8 8.4 %collective-permute-start.5 = (bf16[224,512]{1,0:T(8,128)(2,1)S(1)}, bf16[224,512]{1,0:T(8,128)(2,1)S(1)}, u32[]{:S(2)}, u32[]{:S(2)}) collective-permute-start(bf16[224,512]{1,0:T(8,128)(2,1)S(1)} %collective-permute-done.3), channel_id=1, source_target_pairs={{4,0},{5,1},{6,2},{7,3},{8,4},{9,5},{10,6},{11,7},{12,8},{13,9},{1... | collective-permute-start | bytes 688136 | tf_op jit(solution)/shard_map/ppermute | solution.py:89
  31.1 8.5 %collective-permute-start.4 = (bf16[224,512]{1,0:T(8,128)(2,1)S(1)}, bf16[224,512]{1,0:T(8,128)(2,1)S(1)}, u32[]{:S(2)}, u32[]{:S(2)}) collective-permute-start(bf16[224,512]{1,0:T(8,128)(2,1)S(1)} %collective-permute-done.2), channel_id=1, source_target_pairs={{0,4},{1,5},{2,6},{3,7},{4,8},{5,9},{6,10},{7,11},{8,12},{9,13},{1... | collective-permute-start | bytes 688136 | tf_op jit(solution)/shard_map/ppermute | solution.py:88
  39.7 6.3 %copy-start.6 = (f32[512]{0:T(512)S(1)}, f32[512]{0:T(512)}, u32[]{:S(2)}) copy-start(f32[512]{0:T(512)} %param.10) | copy-start | bytes 6148
  39.7 6.1 %collective-permute-start.9 = (bf16[224,512]{1,0:T(8,128)(2,1)S(1)}, bf16[224,512]{1,0:T(8,128)(2,1)S(1)}, u32[]{:S(2)}, u32[]{:S(2)}) collective-permute-start(bf16[224,512]{1,0:T(8,128)(2,1)S(1)} %broadcast_select_fusion), channel_id=1, source_target_pairs={{0,2},{1,3},{2,0},{3,1},{4,6},{5,7},{6,4},{7,5},{8,10},{9,11},{10,... | collective-permute-start | bytes 688136 | tf_op jit(solution)/shard_map/ppermute | solution.py:92
  45.9 7.2 %copy-start.1 = (bf16[8,224,512]{2,1,0:T(8,128)(2,1)}, bf16[8,224,512]{2,1,0:T(8,128)(2,1)S(1)}, u32[]{:S(2)}) copy-start(bf16[8,224,512]{2,1,0:T(8,128)(2,1)S(1)} %bitcast_dynamic-update-slice_fusion.x_ref.w_ref) | copy-start | bytes 5505028
  45.9 13.6 %collective-permute-start.11 = (bf16[8,224,512]{2,1,0:T(8,128)(2,1)S(1)}, bf16[8,224,512]{2,1,0:T(8,128)(2,1)}, u32[]{:S(2)}, u32[]{:S(2)}) collective-permute-start(bf16[8,224,512]{2,1,0:T(8,128)(2,1)S(1)} %bitcast_dynamic-update-slice_fusion.x_ref.w_ref), channel_id=1, source_target_pairs={{0,1},{1,0},{2,3},{3,2},{4,5},{5,4},{6,7},{7,6},{8,9},{9,8},{10,11... | collective-permute-start | bytes 5505032 | tf_op jit(solution)/shard_map/ppermute | solution.py:111
  46.9 2.8 %collective-permute-start.10 = (bf16[8,9]{1,0:T(8,128)(2,1)S(1)}, bf16[8,9]{1,0:T(8,128)(2,1)S(1)}, u32[]{:S(2)}, u32[]{:S(2)}) collective-permute-start(bf16[8,9]{1,0:T(8,128)(2,1)S(1)} %bitcast.58), channel_id=1, source_target_pairs={{0,1},{1,0},{2,3},{3,2},{4,5},{5,4},{6,7},{7,6},{8,9},{9,8},{10,11... | collective-permute-start | bytes 440 | tf_op jit(solution)/shard_map/ppermute | solution.py:153
  59.4 6.5 %copy-start.3 = (f32[16,512]{1,0:T(8,128)S(1)}, f32[16,512]{1,0:T(8,128)}, u32[]{:S(2)}) copy-start(f32[16,512]{1,0:T(8,128)} %shard_map.95) | copy-start | bytes 98308
  59.4 6.5 %copy-start.4 = (f32[16,512]{1,0:T(8,128)S(1)}, f32[16,512]{1,0:T(8,128)}, u32[]{:S(2)}) copy-start(f32[16,512]{1,0:T(8,128)} %param.11) | copy-start | bytes 98308
  59.4 20.6 %copy-start.5 = (f32[16,16]{1,0:T(8,128)S(1)}, f32[16,16]{1,0:T(8,128)}, u32[]{:S(2)}) copy-start(f32[16,16]{1,0:T(8,128)} %param.13) | copy-start | bytes 3076
  66.8 1.2 %collective-permute-start.12 = (f32[16,16]{0,1:T(8,128)S(1)}, f32[16,16]{0,1:T(8,128)S(1)}, u32[]{:S(2)}, u32[]{:S(2)}) collective-permute-start(f32[16,16]{0,1:T(8,128)S(1)} %convolution_bitcast_fusion), channel_id=1, source_target_pairs={{0,1},{1,0},{2,3},{3,2},{4,5},{5,4},{6,7},{7,6},{8,9},{9,8},{10,11... | collective-permute-start | bytes 3080 | tf_op jit(solution)/shard_map/ppermute | solution.py:121
  68.0 3.7 %collective-permute-start.13 = (f32[16,16]{0,1:T(8,128)S(1)}, f32[16,16]{0,1:T(8,128)S(1)}, u32[]{:S(2)}, u32[]{:S(2)}) collective-permute-start(f32[16,16]{0,1:T(8,128)S(1)} %add.94), channel_id=1, source_target_pairs={{0,2},{1,3},{2,0},{3,1},{4,6},{5,7},{6,4},{7,5},{8,10},{9,11},{10,... | collective-permute-start | bytes 3080 | tf_op jit(solution)/shard_map/ppermute | solution.py:121
  71.7 5.1 %collective-permute-start.14 = (f32[16,16]{0,1:T(8,128)S(1)}, f32[16,16]{0,1:T(8,128)S(1)}, u32[]{:S(2)}, u32[]{:S(2)}) collective-permute-start(f32[16,16]{0,1:T(8,128)S(1)} %add.95), channel_id=1, source_target_pairs={{0,4},{1,5},{2,6},{3,7},{4,0},{5,1},{6,2},{7,3},{8,12},{9,13},{10,... | collective-permute-start | bytes 3080 | tf_op jit(solution)/shard_map/ppermute | solution.py:121
  76.8 4.8 %collective-permute-start.15 = (f32[16,16]{0,1:T(8,128)S(1)}, f32[16,16]{0,1:T(8,128)S(1)}, u32[]{:S(2)}, u32[]{:S(2)}) collective-permute-start(f32[16,16]{0,1:T(8,128)S(1)} %add.96), channel_id=1, source_target_pairs={{0,8},{1,9},{2,10},{3,11},{4,12},{5,13},{6,14},{7,15},{8,0},{9,1},... | collective-permute-start | bytes 3080 | tf_op jit(solution)/shard_map/ppermute | solution.py:121

commit v8 on v7

--- a/solution.py
+++ b/solution.py
@@ -42,11 +42,11 @@
 def own_rows_product(flags, own_terms, mine, width):
     twice_own_t, norm_own, recip_own = own_terms
     own = twice_own_t.shape[0]
-    slots, rows = mine.shape[0], mine.shape[1]
+    slots, rows, cols = mine.shape
     per = 2 if slots % 2 == 0 else 1
     lanes_row = width // LANCZOS
-    x_spec = pl.BlockSpec((per, rows, own), lambda s, m: (s, 0, 0))
-    w_spec = pl.BlockSpec((per, 2 * LANCZOS, own), lambda s, m: (s, lanes_row // 2, 0))
+    x_spec = pl.BlockSpec((per, rows, cols), lambda s, m: (s, 0, 0))
+    w_spec = pl.BlockSpec((per, 2 * LANCZOS, cols), lambda s, m: (s, lanes_row // 2, 0))
     grid_spec = pltpu.PrefetchScalarGridSpec(
         num_scalar_prefetch=1,
         grid=(slots // per,),
@@ -70,11 +70,10 @@
     me = lax.axis_index("row")
     if devices != 16:
         pieces = lax.all_gather(packed, "row", axis=0, tiled=False)
-        return pieces, None, jnp.arange(devices, dtype=jnp.int32), None
+        return pieces, jnp.arange(devices, dtype=jnp.int32)
     up = [(r, r + 4) for r in range(12)]
     down = [(r, r - 4) for r in range(4, 16)]
     across = [(r, r ^ 2) for r in range(16)]
-    twin = [(r, r ^ 1) for r in range(16)]
     z = me // 4
     partner = me ^ 2
 
@@ -108,8 +107,7 @@
         jnp.where(z >= 1, partner - 4, partner + 4),
         jnp.where(z == 3, partner - 12, jnp.where(z == 0, partner + 12, partner + 4)),
     ]).astype(jnp.int32)
-    theirs = lax.ppermute(mine, "row", twin)
-    return mine, theirs, origin, origin ^ 1
+    return mine, origin
 
 
 def sum_over_rows(value):
@@ -137,44 +135,50 @@
     devices = lax.axis_size("row")
     total_rows = devices * own
     slots = tile_plan.shape[0]
+    chip_split = devices == 16
+    twin = [(r, r ^ 1) for r in range(devices)]
     weighted = (degree_scale[None, :] * lanczos_block).astype(jnp.bfloat16)
+    plan_len = 2 * slots + 1
     plan_row = jnp.concatenate([tile_plan.reshape(-1), tile_counts]).astype(jnp.bfloat16)
+    if chip_split:
+        plan_row = jnp.concatenate([plan_row, lax.ppermute(plan_row, "row", twin)])
     plan_row = jnp.pad(plan_row, (0, own - plan_row.shape[0]))
     packed = jnp.concatenate(
         [embeddings, weighted, local_scale[None, :], plan_row[None, :]], axis=0
     )
     packed = jnp.pad(packed, ((0, -packed.shape[0] % (2 * LANCZOS)), (0, 0)))
-    mine, theirs, origin, their_origin = gather_pieces(packed)
+    mine, origin = gather_pieces(packed)
 
     plan_at = width + LANCZOS + 1
-    plans = mine[:, plan_at, : 2 * slots + 1]
-    if theirs is not None:
-        twin = [(r, r ^ 1) for r in range(devices)]
-        plans = jnp.concatenate([plans, lax.ppermute(plans, "row", twin)])
-    plans = plans.astype(jnp.int32)
+    copies = 2 if chip_split else 1
+    plans = mine[:, plan_at, : copies * plan_len].astype(jnp.int32).reshape(devices, plan_len)
     counts = plans[:, 2 * slots]
     pairs = plans[:, : 2 * slots].reshape(devices, slots, 2)
     live = jnp.arange(slots, dtype=jnp.int32)[None, :] < counts[:, None]
-    row_block = pairs[..., 0].reshape(-1)
-    col_block = pairs[..., 1].reshape(-1)
-    live = live.reshape(-1)
+    row_block = pairs[..., 0].reshape(-1)[:, None]
+    col_block = pairs[..., 1].reshape(-1)[:, None]
+    live = live.reshape(-1)[:, None]
     my_block = (lax.axis_index("row") * own) // BLK
-    block_ids = jnp.arange(total_rows // BLK, dtype=jnp.int32)
-    hit = live[:, None] & (
-        ((row_block[:, None] == my_block) & (col_block[:, None] == block_ids[None, :]))
-        | ((col_block[:, None] == my_block) & (row_block[:, None] == block_ids[None, :]))
-    )
-    mask_row = jnp.any(hit, axis=0).astype(jnp.int32)
-
-    norm_own = jnp.sum(jnp.square(embeddings.astype(jnp.float32)), axis=0)[:, None]
+    piece_block = ((origin * own) // BLK)[None, :]
+    hit = live & (
+        ((row_block == my_block) & (col_block == piece_block))
+        | ((col_block == my_block) & (row_block == piece_block))
+    )
+    flags = jnp.any(hit, axis=0).astype(jnp.int32)
+
+    if chip_split:
+        twin_piece = lax.ppermute(packed, "row", twin)
+        rows_x = jnp.concatenate([embeddings, twin_piece[:width]], axis=1)
+        rows_scale = jnp.concatenate([local_scale, twin_piece[width + LANCZOS]])
+    else:
+        rows_x, rows_scale = embeddings, local_scale
+    norm_rows = jnp.sum(jnp.square(rows_x.astype(jnp.float32)), axis=0)[:, None]
     log2e = 1.0 / math.log(2.0)
-    recip_own = (-log2e / local_scale.astype(jnp.float32))[:, None]
-    own_terms = ((embeddings * 2).T, norm_own, recip_own)
-    summed = own_rows_product(mask_row[(origin * own) // BLK], own_terms, mine, width)
-    if theirs is not None:
-        summed = summed + own_rows_product(
-            mask_row[(their_origin * own) // BLK], own_terms, theirs, width
-        )
+    recip_rows = (-log2e / rows_scale.astype(jnp.float32))[:, None]
+    own_terms = ((rows_x * 2).T, norm_rows, recip_rows)
+    summed = own_rows_product(flags, own_terms, mine, width)
+    if chip_split:
+        summed = summed[:, :own] + lax.ppermute(summed[:, own:], "row", twin)
     scaled = summed * (degree_scale[None, :] / math.sqrt(total_rows))
     partial_value = lax.dot_general(
         lanczos_block, scaled, (((1,), (1,)), ((), ())), precision=HIGHEST

time: 84.3 us -> 82.2 us (0.975)
  Pallas kernels: 12.9 us -> 8.65 us
  other arithmetic: 5.85 us -> 8.35 us
  waiting for transfers between devices: 22.5 us -> 20.4 us
  starting transfers between devices: 30.9 us -> 32 us
    pallas_call x2 -> x1, Pallas kernels: 12.9 us -> 8.65 us  [own_rows_product(): pl.pallas_call(functools.partial(affinity_kernel, width, per), grid_spec=...]
    gather x2 -> x0, local copies, waits for them, and re-layouts: 2.37 us -> none  [the longest x1 1.21 us: shards(): mask_row[their_origin * own // BLK]]
    ppermute x1, waiting for transfers between devices: 5.41 us -> 3.46 us  [gather_pieces(): across4 = lax.ppermute(pick3, 'row', across)]
    ppermute x1, starting transfers between devices: 0.13 us -> 1.68 us  [gather_pieces(): across2 = lax.ppermute(jnp.stack([up1, down1]), 'row', across)]
    concatenate x0 -> x2, local copies, waits for them, and re-layouts: none -> 1.38 us  [shards(): rows_scale = jnp.concatenate([local_scale, twin_piece[width + LANCZOS]])]
    ppermute x2 -> x3, waiting for transfers between devices: 2.4 us -> 1.2 us  [the longest x1 1.2 us: shards(): summed = summed[:, :own] + lax.ppermute(summed[:, own:], 'row', twin)]
    ppermute x1, waiting for transfers between devices: 0.01 us -> 1.15 us  [gather_pieces(): up1 = lax.ppermute(packed, 'row', up)]
    ppermute x1, starting transfers between devices: 0.4 us -> 1.42 us  [gather_pieces(): across4 = lax.ppermute(pick3, 'row', across)]
  transfers between devices with their start and end apart: 16 -> 17, of which waited for: 10 -> 11; matrix products, arithmetic and copies ran while one was open for 11% -> 13% of each run, Pallas kernels for 8% -> 0%
where the time goes in v8:
time: 82.2 us; the launch traced here: 81.3 us
  starting transfers between devices  32 us (39%)
  waiting for transfers between devices  20.4 us (25%)
  Pallas kernels  8.65 us (11%)
  other arithmetic  8.35 us (10%)
  local copies, waits for them, and re-layouts  7.81 us (10%)
  matrix products  2.58 us (3%)
  between operations  1.56 us (2%)
    pallas_call x1, Pallas kernels, own_rows_product(): pl.pallas_call(functools.partial(affinity_kernel, width, per), grid_spec=...  8.65 us
    ppermute x4, waiting for transfers between devices, sum_over_rows(): lax.ppermute(value, 'row', [(i, i ^ stride) for i in range(devices)])  7.5 us
    ppermute x4, starting transfers between devices, sum_over_rows(): lax.ppermute(value, 'row', [(i, i ^ stride) for i in range(devices)])  6.26 us
    ppermute x1, starting transfers between devices, gather_pieces(): up1 = lax.ppermute(packed, 'row', up)  5.57 us
    ppermute x1, starting transfers between devices, gather_pieces(): up3 = lax.ppermute(up2, 'row', up)  5.03 us
    ppermute x1, starting transfers between devices, gather_pieces(): up2 = lax.ppermute(up1, 'row', up)  4.92 us
    ppermute x1, waiting for transfers between devices, gather_pieces(): across4 = lax.ppermute(pick3, 'row', across)  3.46 us
    ppermute x1, waiting for transfers between devices, gather_pieces(): down2 = lax.ppermute(down1, 'row', down)  2.46 us
  transfers between devices with their start and end apart: 17, of which 11 were waited for; matrix products, arithmetic and copies ran while one was open for 13% of the time, Pallas kernels for 0%

profile of v8, /device:TPU:0, one launch (start us, length us, event | category | flops | bytes accessed | tf_op | source)
XLA Modules:
  0.0 81.3 jit_solution(9446905138495712857)
XLA Ops:
  0.7 0.7 convert.8
  2.3 0.5 collective-permute-start
  2.8 0.7 broadcast_in_dim.6
  3.5 0.8 multiply_convert_fusion
  4.4 1.6 %fusion.7 = bf16[224,512]{1,0:T(8,128)(2,1)} fusion(bf16[1,512]{1,0:T(2,128)(2,1)S(1)} %broadcast_in_dim.7, bf16[1,512]{1,0:T(2,128)(2,1)S(1)} %broadcast_in_dim.6, bf16[16,512]{1,0:T(8,128)(2,1)S(1)} %multiply_convert_fusion, bf16[192,512]{1,0:T(8,128)(2,1)} %param.8), kind=kLoop, calls=%fused_computation.15 | loop fusion | flops 1490944 | bytes 444416 | tf_op jit(solution)/shard_map/concatenate | solution.py:146
  6.1 0.7 concatenate.36
  6.8 1.3 %collective-permute-start.2 = (bf16[224,512]{1,0:T(8,128)(2,1)}, bf16[224,512]{1,0:T(8,128)(2,1)S(1)}, u32[]{:S(2)}, u32[]{:S(2)}) collective-permute-start(bf16[224,512]{1,0:T(8,128)(2,1)} %fusion.7), channel_id=1, source_target_pairs={{4,0},{5,1},{6,2},{7,3},{8,4},{9,5},{10,6},{11,7},{12,8},{13,9},{1... | collective-permute-start | bytes 688136 | tf_op jit(solution)/shard_map/ppermute | solution.py:81
  8.1 5.6 %collective-permute-start.1 = (bf16[224,512]{1,0:T(8,128)(2,1)}, bf16[224,512]{1,0:T(8,128)(2,1)S(1)}, u32[]{:S(2)}, u32[]{:S(2)}) collective-permute-start(bf16[224,512]{1,0:T(8,128)(2,1)} %fusion.7), channel_id=1, source_target_pairs={{0,4},{1,5},{2,6},{3,7},{4,8},{5,9},{6,10},{7,11},{8,12},{9,13},{1... | collective-permute-start | bytes 688136 | tf_op jit(solution)/shard_map/ppermute | solution.py:80
  13.7 2.0 %collective-permute-start.7 = (bf16[224,512]{1,0:T(8,128)(2,1)}, bf16[224,512]{1,0:T(8,128)(2,1)}, u32[]{:S(2)}, u32[]{:S(2)}) collective-permute-start(bf16[224,512]{1,0:T(8,128)(2,1)} %fusion.7), channel_id=1, source_target_pairs={{0,2},{1,3},{2,0},{3,1},{4,6},{5,7},{6,4},{7,5},{8,10},{9,11},{10,... | collective-permute-start | bytes 688136 | tf_op jit(solution)/shard_map/ppermute | solution.py:82
  15.7 0.9 %bitcast_dynamic-update-slice_fusion.6 = bf16[8,224,512]{2,1,0:T(8,128)(2,1)S(1)} fusion(bf16[1,512]{1,0:T(2,128)(2,1)S(1)} %broadcast_in_dim.7, bf16[1,512]{1,0:T(2,128)(2,1)S(1)} %broadcast_in_dim.6, bf16[16,512]{1,0:T(8,128)(2,1)S(1)} %multiply_convert_fusion, bf16[192,512]{1,0:T(8,128)(2,1)} %param.8), kind=kLoop, calls=%fused_computation.25 | loop fusion | flops 1490943 | bytes 444416
  16.7 1.1 %multiply_reduce_fusion = f32[1024]{0:T(1024)S(1)} fusion(bf16[192,512]{1,0:T(8,128)(2,1)S(1)} %slice.52, bf16[192,512]{1,0:T(8,128)(2,1)} %param.8), kind=kLoop, calls=%fused_computation.3 | loop fusion | flops 1178624 | bytes 397312 | tf_op jit(solution)/shard_map/reduce_sum | solution.py:175
  17.9 1.1 %collective-permute-done.1 = bf16[224,512]{1,0:T(8,128)(2,1)S(1)} collective-permute-done((bf16[224,512]{1,0:T(8,128)(2,1)}, bf16[224,512]{1,0:T(8,128)(2,1)S(1)}, u32[]{:S(2)}, u32[]{:S(2)}) %collective-permute-start.1) | collective-permute-done | bytes 229408 | tf_op jit(solution)/shard_map/ppermute | solution.py:80
  19.0 0.8 pad_maximum_fusion
  19.8 1.7 %collective-permute-start.9 = (bf16[2,224,512]{2,1,0:T(8,128)(2,1)}, bf16[2,224,512]{2,1,0:T(8,128)(2,1)S(1)}, u32[]{:S(2)}, u32[]{:S(2)}) collective-permute-start(bf16[2,224,512]{2,1,0:T(8,128)(2,1)} %pad_maximum_fusion), channel_id=1, source_target_pairs={{0,2},{1,3},{2,0},{3,1},{4,6},{5,7},{6,4},{7,5},{8,10},{9,11},{10,... | collective-permute-start | bytes 1376264 | tf_op jit(solution)/shard_map/ppermute | solution.py:85
  21.5 1.0 %copy.52.xo_ref = bf16[1024,192]{1,0:T(8,128)(2,1)} copy(bf16[1024,192]{0,1:T(8,128)(2,1)S(1)} %multiply_bitcast_fusion) | data formatting | bytes 786432 | tf_op jit(solution)/shard_map/transpose | solution.py:178
  22.5 1.0 %copy.53.no_ref = f32[1024,1]{1,0:T(8,128)} copy(f32[1024,1]{0,1:T(1,128)S(1)} %bitcast.50) | data formatting | bytes 8192 | tf_op jit(solution)/shard_map/broadcast_in_dim | solution.py:175
  23.5 0.7 slice_bitcast_fusion
  24.2 0.2 copy.51
  24.5 0.9 %broadcast_divide_fusion.ro_ref = f32[1024,1]{1,0:T(8,128)} fusion(f32[1024,1]{1,0:T(8,128)S(1)} %copy.51), kind=kLoop, calls=%fused_computation.12 | loop fusion | flops 1024 | bytes 8192 | tf_op jit(solution)/shard_map/div | solution.py:177
  25.4 1.3 %collective-permute-start.4 = (bf16[224,512]{1,0:T(8,128)(2,1)S(1)}, bf16[224,512]{1,0:T(8,128)(2,1)S(1)}, u32[]{:S(2)}, u32[]{:S(2)}) collective-permute-start(bf16[224,512]{1,0:T(8,128)(2,1)S(1)} %collective-permute-done.2), channel_id=1, source_target_pairs={{4,0},{5,1},{6,2},{7,3},{8,4},{9,5},{10,6},{11,7},{12,8},{13,9},{1... | collective-permute-start | bytes 688136 | tf_op jit(solution)/shard_map/ppermute | solution.py:84
  26.6 4.9 %collective-permute-start.3 = (bf16[224,512]{1,0:T(8,128)(2,1)S(1)}, bf16[224,512]{1,0:T(8,128)(2,1)S(1)}, u32[]{:S(2)}, u32[]{:S(2)}) collective-permute-start(bf16[224,512]{1,0:T(8,128)(2,1)S(1)} %collective-permute-done.1), channel_id=1, source_target_pairs={{0,4},{1,5},{2,6},{3,7},{4,8},{5,9},{6,10},{7,11},{8,12},{9,13},{1... | collective-permute-start | bytes 688136 | tf_op jit(solution)/shard_map/ppermute | solution.py:83
  31.6 2.5 %collective-permute-done.4 = bf16[224,512]{1,0:T(8,128)(2,1)S(1)} collective-permute-done((bf16[224,512]{1,0:T(8,128)(2,1)S(1)}, bf16[224,512]{1,0:T(8,128)(2,1)S(1)}, u32[]{:S(2)}, u32[]{:S(2)}) %collective-permute-start.4) | collective-permute-done | bytes 229408 | tf_op jit(solution)/shard_map/ppermute | solution.py:84
  34.1 1.2 %collective-permute-done.3 = bf16[224,512]{1,0:T(8,128)(2,1)S(1)} collective-permute-done((bf16[224,512]{1,0:T(8,128)(2,1)S(1)}, bf16[224,512]{1,0:T(8,128)(2,1)S(1)}, u32[]{:S(2)}, u32[]{:S(2)}) %collective-permute-start.3) | collective-permute-done | bytes 229408 | tf_op jit(solution)/shard_map/ppermute | solution.py:83
  35.3 0.7 collective-permute-start.8
  36.0 1.3 %collective-permute-start.6 = (bf16[224,512]{1,0:T(8,128)(2,1)S(1)}, bf16[224,512]{1,0:T(8,128)(2,1)S(1)}, u32[]{:S(2)}, u32[]{:S(2)}) collective-permute-start(bf16[224,512]{1,0:T(8,128)(2,1)S(1)} %collective-permute-done.4), channel_id=1, source_target_pairs={{4,0},{5,1},{6,2},{7,3},{8,4},{9,5},{10,6},{11,7},{12,8},{13,9},{1... | collective-permute-start | bytes 688136 | tf_op jit(solution)/shard_map/ppermute | solution.py:88
  37.3 5.0 %collective-permute-start.5 = (bf16[224,512]{1,0:T(8,128)(2,1)S(1)}, bf16[224,512]{1,0:T(8,128)(2,1)S(1)}, u32[]{:S(2)}, u32[]{:S(2)}) collective-permute-start(bf16[224,512]{1,0:T(8,128)(2,1)S(1)} %collective-permute-done.3), channel_id=1, source_target_pairs={{0,4},{1,5},{2,6},{3,7},{4,8},{5,9},{6,10},{7,11},{8,12},{9,13},{1... | collective-permute-start | bytes 688136 | tf_op jit(solution)/shard_map/ppermute | solution.py:87
  42.5 1.9 %collective-permute-done.6 = bf16[224,512]{1,0:T(8,128)(2,1)S(1)} collective-permute-done((bf16[224,512]{1,0:T(8,128)(2,1)S(1)}, bf16[224,512]{1,0:T(8,128)(2,1)S(1)}, u32[]{:S(2)}, u32[]{:S(2)}) %collective-permute-start.6) | collective-permute-done | bytes 229408 | tf_op jit(solution)/shard_map/ppermute | solution.py:88
  44.4 1.5 %collective-permute-done.5 = bf16[224,512]{1,0:T(8,128)(2,1)S(1)} collective-permute-done((bf16[224,512]{1,0:T(8,128)(2,1)S(1)}, bf16[224,512]{1,0:T(8,128)(2,1)S(1)}, u32[]{:S(2)}, u32[]{:S(2)}) %collective-permute-start.5) | collective-permute-done | bytes 229408 | tf_op jit(solution)/shard_map/ppermute | solution.py:87
  45.9 1.4 %collective-permute-start.10 = (bf16[224,512]{1,0:T(8,128)(2,1)S(1)}, bf16[224,512]{1,0:T(8,128)(2,1)S(1)}, u32[]{:S(2)}, u32[]{:S(2)}) collective-permute-start(bf16[224,512]{1,0:T(8,128)(2,1)S(1)} %broadcast_select_fusion), channel_id=1, source_target_pairs={{0,2},{1,3},{2,0},{3,1},{4,6},{5,7},{6,4},{7,5},{8,10},{9,11},{10,... | collective-permute-start | bytes 688136 | tf_op jit(solution)/shard_map/ppermute | solution.py:91
  47.4 1.0 %bitcast_dynamic-update-slice_fusion.2 = bf16[8,224,512]{2,1,0:T(8,128)(2,1)S(1)} fusion(bf16[8,224,512]{2,1,0:T(8,128)(2,1)S(1)} %bitcast_dynamic-update-slice_fusion.3, bf16[224,512]{1,0:T(8,128)(2,1)} %collective-permute-done.7), kind=kLoop, calls=%fused_computation.21 | loop fusion | bytes 458752
  48.5 3.5 %collective-permute-done.10 = bf16[224,512]{1,0:T(8,128)(2,1)S(1)} collective-permute-done((bf16[224,512]{1,0:T(8,128)(2,1)S(1)}, bf16[224,512]{1,0:T(8,128)(2,1)S(1)}, u32[]{:S(2)}, u32[]{:S(2)}) %collective-permute-start.10) | collective-permute-done | bytes 229408 | tf_op jit(solution)/shard_map/ppermute | solution.py:91
  52.9 0.2 and_reduce_fusion
  53.1 0.5 convert_element_type.34.flag_ref
  53.7 8.6 %shard_map.95 = f32[16,1024]{1,0:T(8,128)} custom-call(s32[8]{0:T(128)} %convert_element_type.34.flag_ref, bf16[1024,192]{1,0:T(8,128)(2,1)} %copy.52.xo_ref, f32[1024,1]{1,0:T(8,128)} %copy.53.no_ref, f32[1024,1]{1,0:T(8,128)} %broadcast_divide_fusion.ro_ref, bf16[8,224,512]{2,1,0:T(8,128)(2,1)} %copy-done.1, bf16[8,224,512]{2,1,0:T(8,128)(2,1)} %copy-done.1), custom_call_target="tpu_custom_call" | custom-call | tf_op jit(solution)/shard_map/pallas_call | solution.py:61
  62.3 0.8 slice.55
  63.1 1.2 %collective-permute-done.12 = f32[16,512]{1,0:T(8,128)S(1)} collective-permute-done((f32[16,512]{1,0:T(8,128)S(1)}, f32[16,512]{1,0:T(8,128)S(1)}, u32[]{:S(2)}, u32[]{:S(2)}) %collective-permute-start.12) | collective-permute-done | bytes 32800 | tf_op jit(solution)/shard_map/ppermute | solution.py:181
  64.3 0.9 %convolution_bitcast_fusion = f32[16,16]{0,1:T(8,128)S(1)} fusion(f32[16,512]{1,0:T(8,128)S(1)} %copy-done.3, f32[16,512]{1,0:T(8,128)S(1)} %collective-permute-done.12, f32[16,1024]{1,0:T(8,128)} %shard_map.95, f32[512]{0:T(512)S(1)} %broadcast_multiply_fusion), kind=kOutput, calls=%fused_computation.2 | convolution fusion | flops 1589248 | bytes 101376 | tf_op jit(solution)/shard_map/dot_general | solution.py:183
  65.2 0.2 collective-permute-start.13
  65.4 1.0 %collective-permute-done.13 = f32[16,16]{0,1:T(8,128)S(1)} collective-permute-done((f32[16,16]{0,1:T(8,128)S(1)}, f32[16,16]{0,1:T(8,128)S(1)}, u32[]{:S(2)}, u32[]{:S(2)}) %collective-permute-start.13) | collective-permute-done | bytes 1056 | tf_op jit(solution)/shard_map/ppermute | solution.py:119
  66.4 0.6 collective-permute-start.14
  67.0 3.1 %collective-permute-done.14 = f32[16,16]{0,1:T(8,128)S(1)} collective-permute-done((f32[16,16]{0,1:T(8,128)S(1)}, f32[16,16]{0,1:T(8,128)S(1)}, u32[]{:S(2)}, u32[]{:S(2)}) %collective-permute-start.14) | collective-permute-done | bytes 1056 | tf_op jit(solution)/shard_map/ppermute | solution.py:119
  70.0 1.7 %collective-permute-start.15 = (f32[16,16]{0,1:T(8,128)S(1)}, f32[16,16]{0,1:T(8,128)S(1)}, u32[]{:S(2)}, u32[]{:S(2)}) collective-permute-start(f32[16,16]{0,1:T(8,128)S(1)} %add.62), channel_id=1, source_target_pairs={{0,4},{1,5},{2,6},{3,7},{4,0},{5,1},{6,2},{7,3},{8,12},{9,13},{10,... | collective-permute-start | bytes 3080 | tf_op jit(solution)/shard_map/ppermute | solution.py:119
  71.7 1.9 %collective-permute-done.15 = f32[16,16]{0,1:T(8,128)S(1)} collective-permute-done((f32[16,16]{0,1:T(8,128)S(1)}, f32[16,16]{0,1:T(8,128)S(1)}, u32[]{:S(2)}, u32[]{:S(2)}) %collective-permute-start.15) | collective-permute-done | bytes 1056 | tf_op jit(solution)/shard_map/ppermute | solution.py:119
  73.7 3.8 %collective-permute-start.16 = (f32[16,16]{0,1:T(8,128)S(1)}, f32[16,16]{0,1:T(8,128)S(1)}, u32[]{:S(2)}, u32[]{:S(2)}) collective-permute-start(f32[16,16]{0,1:T(8,128)S(1)} %add.63), channel_id=1, source_target_pairs={{0,8},{1,9},{2,10},{3,11},{4,12},{5,13},{6,14},{7,15},{8,0},{9,1},... | collective-permute-start | bytes 3080 | tf_op jit(solution)/shard_map/ppermute | solution.py:119
  77.5 0.1 fusion.18
  77.6 1.5 %collective-permute-done.16 = f32[16,16]{0,1:T(8,128)S(1)} collective-permute-done((f32[16,16]{0,1:T(8,128)S(1)}, f32[16,16]{0,1:T(8,128)S(1)}, u32[]{:S(2)}, u32[]{:S(2)}) %collective-permute-start.16) | collective-permute-done | bytes 1056 | tf_op jit(solution)/shard_map/ppermute | solution.py:119
  79.1 0.7 copy.54
  79.8 1.5 %fusion = f32[16,512]{1,0:T(8,128)} fusion(f32[16,512]{1,0:T(8,128)S(1)} %fusion.18, f32[16,16]{0,1:T(8,128)S(1)} %add_multiply_fusion, f32[16,512]{1,0:T(8,128)S(1)} %copy-done.3, f32[512]{0:T(512)S(1)} %broadcast_multiply_fusion, f32[16,512]{1,0:T(8,128)S(1)} %collective-permute-done.12, f32[16,1024]{1,0:T(8,128)} %shard_map.95), kind=kOutput, calls=%fused_computation.1 | convolution fusion | flops 1605632 | bytes 166912 | tf_op jit(solution)/shard_map/dot_general | solution.py:187
  (58 shorter events, 2.0 us)
Async XLA Ops:
  0.6 76.8 %copy-start = (f32[16,512]{1,0:T(8,128)S(1)}, f32[16,512]{1,0:T(8,128)}, u32[]{:S(2)}) copy-start(f32[16,512]{1,0:T(8,128)} %param.12) | copy-start | bytes 98308
  0.6 17.1 %copy-start.2 = (bf16[192,512]{1,0:T(8,128)(2,1)S(1)}, bf16[192,512]{1,0:T(8,128)(2,1)}, u32[]{:S(2)}) copy-start(bf16[192,512]{1,0:T(8,128)(2,1)} %param.8) | copy-start | bytes 589828
  2.3 2.0 %collective-permute-start = (bf16[9]{0:T(256)(128)(2,1)S(1)}, bf16[9]{0:T(256)(128)(2,1)S(1)}, u32[]{:S(2)}, u32[]{:S(2)}) collective-permute-start(bf16[9]{0:T(256)(128)(2,1)S(1)} %pad_maximum_fusion.2), channel_id=1, source_target_pairs={{0,1},{1,0},{2,3},{3,2},{4,5},{5,4},{6,7},{7,6},{8,9},{9,8},{10,11... | collective-permute-start | bytes 62 | tf_op jit(solution)/shard_map/ppermute | solution.py:144
  6.0 10.6 %collective-permute-start.11 = (bf16[224,512]{1,0:T(8,128)(2,1)}, bf16[224,512]{1,0:T(8,128)(2,1)S(1)}, u32[]{:S(2)}, u32[]{:S(2)}) collective-permute-start(bf16[224,512]{1,0:T(8,128)(2,1)} %fusion.7), channel_id=1, source_target_pairs={{0,1},{1,0},{2,3},{3,2},{4,5},{5,4},{6,7},{7,6},{8,9},{9,8},{10,11... | collective-permute-start | bytes 688136 | tf_op jit(solution)/shard_map/ppermute | solution.py:170
  6.8 11.1 %collective-permute-start.2 = (bf16[224,512]{1,0:T(8,128)(2,1)}, bf16[224,512]{1,0:T(8,128)(2,1)S(1)}, u32[]{:S(2)}, u32[]{:S(2)}) collective-permute-start(bf16[224,512]{1,0:T(8,128)(2,1)} %fusion.7), channel_id=1, source_target_pairs={{4,0},{5,1},{6,2},{7,3},{8,4},{9,5},{10,6},{11,7},{12,8},{13,9},{1... | collective-permute-start | bytes 688136 | tf_op jit(solution)/shard_map/ppermute | solution.py:81
  8.1 10.9 %collective-permute-start.1 = (bf16[224,512]{1,0:T(8,128)(2,1)}, bf16[224,512]{1,0:T(8,128)(2,1)S(1)}, u32[]{:S(2)}, u32[]{:S(2)}) collective-permute-start(bf16[224,512]{1,0:T(8,128)(2,1)} %fusion.7), channel_id=1, source_target_pairs={{0,4},{1,5},{2,6},{3,7},{4,8},{5,9},{6,10},{7,11},{8,12},{9,13},{1... | collective-permute-start | bytes 688136 | tf_op jit(solution)/shard_map/ppermute | solution.py:80
  13.7 33.8 %collective-permute-start.7 = (bf16[224,512]{1,0:T(8,128)(2,1)}, bf16[224,512]{1,0:T(8,128)(2,1)}, u32[]{:S(2)}, u32[]{:S(2)}) collective-permute-start(bf16[224,512]{1,0:T(8,128)(2,1)} %fusion.7), channel_id=1, source_target_pairs={{0,2},{1,3},{2,0},{3,1},{4,6},{5,7},{6,4},{7,5},{8,10},{9,11},{10,... | collective-permute-start | bytes 688136 | tf_op jit(solution)/shard_map/ppermute | solution.py:82
  16.6 2.4 %copy-start.4 = (bf16[224,512]{1,0:T(8,128)(2,1)}, bf16[224,512]{1,0:T(8,128)(2,1)S(1)}, u32[]{:S(2)}) copy-start(bf16[224,512]{1,0:T(8,128)(2,1)S(1)} %collective-permute-done.11) | copy-start | bytes 688132
  19.8 28.6 %collective-permute-start.9 = (bf16[2,224,512]{2,1,0:T(8,128)(2,1)}, bf16[2,224,512]{2,1,0:T(8,128)(2,1)S(1)}, u32[]{:S(2)}, u32[]{:S(2)}) collective-permute-start(bf16[2,224,512]{2,1,0:T(8,128)(2,1)} %pad_maximum_fusion), channel_id=1, source_target_pairs={{0,2},{1,3},{2,0},{3,1},{4,6},{5,7},{6,4},{7,5},{8,10},{9,11},{10,... | collective-permute-start | bytes 1376264 | tf_op jit(solution)/shard_map/ppermute | solution.py:85
  25.4 8.7 %collective-permute-start.4 = (bf16[224,512]{1,0:T(8,128)(2,1)S(1)}, bf16[224,512]{1,0:T(8,128)(2,1)S(1)}, u32[]{:S(2)}, u32[]{:S(2)}) collective-permute-start(bf16[224,512]{1,0:T(8,128)(2,1)S(1)} %collective-permute-done.2), channel_id=1, source_target_pairs={{4,0},{5,1},{6,2},{7,3},{8,4},{9,5},{10,6},{11,7},{12,8},{13,9},{1... | collective-permute-start | bytes 688136 | tf_op jit(solution)/shard_map/ppermute | solution.py:84
  26.6 8.6 %collective-permute-start.3 = (bf16[224,512]{1,0:T(8,128)(2,1)S(1)}, bf16[224,512]{1,0:T(8,128)(2,1)S(1)}, u32[]{:S(2)}, u32[]{:S(2)}) collective-permute-start(bf16[224,512]{1,0:T(8,128)(2,1)S(1)} %collective-permute-done.1), channel_id=1, source_target_pairs={{0,4},{1,5},{2,6},{3,7},{4,8},{5,9},{6,10},{7,11},{8,12},{9,13},{1... | collective-permute-start | bytes 688136 | tf_op jit(solution)/shard_map/ppermute | solution.py:83
  35.3 13.1 %collective-permute-start.8 = (bf16[224,512]{1,0:T(8,128)(2,1)S(1)}, bf16[224,512]{1,0:T(8,128)(2,1)S(1)}, u32[]{:S(2)}, u32[]{:S(2)}) collective-permute-start(bf16[224,512]{1,0:T(8,128)(2,1)S(1)} %broadcast_select_fusion.1), channel_id=1, source_target_pairs={{0,2},{1,3},{2,0},{3,1},{4,6},{5,7},{6,4},{7,5},{8,10},{9,11},{10,... | collective-permute-start | bytes 688136 | tf_op jit(solution)/shard_map/ppermute | solution.py:89
  36.0 8.4 %collective-permute-start.6 = (bf16[224,512]{1,0:T(8,128)(2,1)S(1)}, bf16[224,512]{1,0:T(8,128)(2,1)S(1)}, u32[]{:S(2)}, u32[]{:S(2)}) collective-permute-start(bf16[224,512]{1,0:T(8,128)(2,1)S(1)} %collective-permute-done.4), channel_id=1, source_target_pairs={{4,0},{5,1},{6,2},{7,3},{8,4},{9,5},{10,6},{11,7},{12,8},{13,9},{1... | collective-permute-start | bytes 688136 | tf_op jit(solution)/shard_map/ppermute | solution.py:88
  37.3 8.5 %collective-permute-start.5 = (bf16[224,512]{1,0:T(8,128)(2,1)S(1)}, bf16[224,512]{1,0:T(8,128)(2,1)S(1)}, u32[]{:S(2)}, u32[]{:S(2)}) collective-permute-start(bf16[224,512]{1,0:T(8,128)(2,1)S(1)} %collective-permute-done.3), channel_id=1, source_target_pairs={{0,4},{1,5},{2,6},{3,7},{4,8},{5,9},{6,10},{7,11},{8,12},{9,13},{1... | collective-permute-start | bytes 688136 | tf_op jit(solution)/shard_map/ppermute | solution.py:87
  45.9 6.1 %collective-permute-start.10 = (bf16[224,512]{1,0:T(8,128)(2,1)S(1)}, bf16[224,512]{1,0:T(8,128)(2,1)S(1)}, u32[]{:S(2)}, u32[]{:S(2)}) collective-permute-start(bf16[224,512]{1,0:T(8,128)(2,1)S(1)} %broadcast_select_fusion), channel_id=1, source_target_pairs={{0,2},{1,3},{2,0},{3,1},{4,6},{5,7},{6,4},{7,5},{8,10},{9,11},{10,... | collective-permute-start | bytes 688136 | tf_op jit(solution)/shard_map/ppermute | solution.py:91
  52.0 1.6 %copy-start.1 = (bf16[8,224,512]{2,1,0:T(8,128)(2,1)}, bf16[8,224,512]{2,1,0:T(8,128)(2,1)S(1)}, u32[]{:S(2)}) copy-start(bf16[8,224,512]{2,1,0:T(8,128)(2,1)S(1)} %bitcast_dynamic-update-slice_fusion.x_ref.w_ref) | copy-start | bytes 5505028
  53.6 9.4 %copy-start.6 = (f32[512]{0:T(512)S(1)}, f32[512]{0:T(512)}, u32[]{:S(2)}) copy-start(f32[512]{0:T(512)} %param.10) | copy-start | bytes 6148
  53.6 10.6 %copy-start.3 = (f32[16,512]{1,0:T(8,128)S(1)}, f32[16,512]{1,0:T(8,128)}, u32[]{:S(2)}) copy-start(f32[16,512]{1,0:T(8,128)} %param.11) | copy-start | bytes 98308
  53.6 23.8 %copy-start.5 = (f32[16,16]{1,0:T(8,128)S(1)}, f32[16,16]{1,0:T(8,128)}, u32[]{:S(2)}) copy-start(f32[16,16]{1,0:T(8,128)} %param.13) | copy-start | bytes 3076
  63.1 1.2 %collective-permute-start.12 = (f32[16,512]{1,0:T(8,128)S(1)}, f32[16,512]{1,0:T(8,128)S(1)}, u32[]{:S(2)}, u32[]{:S(2)}) collective-permute-start(f32[16,512]{1,0:T(8,128)S(1)} %slice.55), channel_id=1, source_target_pairs={{0,1},{1,0},{2,3},{3,2},{4,5},{5,4},{6,7},{7,6},{8,9},{9,8},{10,11... | collective-permute-start | bytes 98312 | tf_op jit(solution)/shard_map/ppermute | solution.py:181
  65.2 1.2 %collective-permute-start.13 = (f32[16,16]{0,1:T(8,128)S(1)}, f32[16,16]{0,1:T(8,128)S(1)}, u32[]{:S(2)}, u32[]{:S(2)}) collective-permute-start(f32[16,16]{0,1:T(8,128)S(1)} %convolution_bitcast_fusion), channel_id=1, source_target_pairs={{0,1},{1,0},{2,3},{3,2},{4,5},{5,4},{6,7},{7,6},{8,9},{9,8},{10,11... | collective-permute-start | bytes 3080 | tf_op jit(solution)/shard_map/ppermute | solution.py:119
  66.4 3.7 %collective-permute-start.14 = (f32[16,16]{0,1:T(8,128)S(1)}, f32[16,16]{0,1:T(8,128)S(1)}, u32[]{:S(2)}, u32[]{:S(2)}) collective-permute-start(f32[16,16]{0,1:T(8,128)S(1)} %add.61), channel_id=1, source_target_pairs={{0,2},{1,3},{2,0},{3,1},{4,6},{5,7},{6,4},{7,5},{8,10},{9,11},{10,... | collective-permute-start | bytes 3080 | tf_op jit(solution)/shard_map/ppermute | solution.py:119
  70.0 3.7 %collective-permute-start.15 = (f32[16,16]{0,1:T(8,128)S(1)}, f32[16,16]{0,1:T(8,128)S(1)}, u32[]{:S(2)}, u32[]{:S(2)}) collective-permute-start(f32[16,16]{0,1:T(8,128)S(1)} %add.62), channel_id=1, source_target_pairs={{0,4},{1,5},{2,6},{3,7},{4,0},{5,1},{6,2},{7,3},{8,12},{9,13},{10,... | collective-permute-start | bytes 3080 | tf_op jit(solution)/shard_map/ppermute | solution.py:119
  73.7 5.4 %collective-permute-start.16 = (f32[16,16]{0,1:T(8,128)S(1)}, f32[16,16]{0,1:T(8,128)S(1)}, u32[]{:S(2)}, u32[]{:S(2)}) collective-permute-start(f32[16,16]{0,1:T(8,128)S(1)} %add.63), channel_id=1, source_target_pairs={{0,8},{1,9},{2,10},{3,11},{4,12},{5,13},{6,14},{7,15},{8,0},{9,1},... | collective-permute-start | bytes 3080 | tf_op jit(solution)/shard_map/ppermute | solution.py:119

commit v9 on v8

--- a/solution.py
+++ b/solution.py
@@ -112,12 +112,27 @@
 
 def sum_over_rows(value):
     devices = lax.axis_size("row")
-    if devices & (devices - 1):
-        return lax.psum(value, "row")
-    stride = 1
-    while stride < devices:
-        value = value + lax.ppermute(value, "row", [(i, i ^ stride) for i in range(devices)])
-        stride *= 2
+    if devices != 16:
+        if devices & (devices - 1):
+            return lax.psum(value, "row")
+        stride = 1
+        while stride < devices:
+            value = value + lax.ppermute(value, "row", [(i, i ^ stride) for i in range(devices)])
+            stride *= 2
+        return value
+    me = lax.axis_index("row")
+    for shift in (0, 2):
+        got = {0: value}
+        for m in (1, 2, 3):
+            got[m] = lax.ppermute(value, "row", [(i, i ^ (m << shift)) for i in range(devices)])
+        place = (me >> shift) & 3
+        total = None
+        for k in range(4):
+            member = got[0]
+            for m in (1, 2, 3):
+                member = jnp.where((k ^ place) == m, got[m], member)
+            total = member if total is None else total + member
+        value = total
     return value
 
 

time: 82.2 us -> 81.4 us (level)
  waiting for transfers between devices: 20.4 us -> 18.8 us
    ppermute x4 -> x6, waiting for transfers between devices: 7.5 us -> 5.91 us  [sum_over_rows(): lax.ppermute(value, 'row', [(i, i ^ m << shift) for i in range(devices)])]
    ppermute x4 -> x6, starting transfers between devices: 6.26 us -> 7.06 us  [sum_over_rows(): lax.ppermute(value, 'row', [(i, i ^ m << shift) for i in range(devices)])]
  transfers between devices with their start and end apart: 17 -> 19, of which waited for: 11 -> 11; matrix products, arithmetic and copies ran while one was open for 13% -> 13% of each run, Pallas kernels for 0% -> 0%
where the time goes in v9:
time: 81.4 us; the launch traced here: 80.6 us
  starting transfers between devices  32.8 us (40%)
  waiting for transfers between devices  18.8 us (23%)
  Pallas kernels  8.64 us (11%)
  other arithmetic  8.37 us (10%)
  local copies, waits for them, and re-layouts  7.83 us (10%)
  matrix products  2.58 us (3%)
  between operations  1.57 us (2%)
    pallas_call x1, Pallas kernels, own_rows_product(): pl.pallas_call(functools.partial(affinity_kernel, width, per), grid_spec=...  8.64 us
    ppermute x6, starting transfers between devices, sum_over_rows(): lax.ppermute(value, 'row', [(i, i ^ m << shift) for i in range(devices)])  7.06 us
    ppermute x6, waiting for transfers between devices, sum_over_rows(): lax.ppermute(value, 'row', [(i, i ^ m << shift) for i in range(devices)])  5.91 us
    ppermute x1, starting transfers between devices, gather_pieces(): up1 = lax.ppermute(packed, 'row', up)  5.57 us
    ppermute x1, starting transfers between devices, gather_pieces(): up3 = lax.ppermute(up2, 'row', up)  5.03 us
    ppermute x1, starting transfers between devices, gather_pieces(): up2 = lax.ppermute(up1, 'row', up)  4.92 us
    ppermute x1, waiting for transfers between devices, gather_pieces(): across4 = lax.ppermute(pick3, 'row', across)  3.46 us
    ppermute x1, waiting for transfers between devices, gather_pieces(): down2 = lax.ppermute(down1, 'row', down)  2.46 us
  transfers between devices with their start and end apart: 19, of which 11 were waited for; matrix products, arithmetic and copies ran while one was open for 13% of the time, Pallas kernels for 0%

profile of v9, /device:TPU:0, one launch (start us, length us, event | category | flops | bytes accessed | tf_op | source)
XLA Modules:
  0.0 80.6 jit_solution(5303246871733827976)
XLA Ops:
  0.7 0.7 convert.8
  2.3 0.5 collective-permute-start
  2.8 0.7 broadcast_in_dim.6
  3.5 0.8 multiply_convert_fusion
  4.4 1.6 %fusion.7 = bf16[224,512]{1,0:T(8,128)(2,1)} fusion(bf16[1,512]{1,0:T(2,128)(2,1)S(1)} %broadcast_in_dim.7, bf16[1,512]{1,0:T(2,128)(2,1)S(1)} %broadcast_in_dim.6, bf16[16,512]{1,0:T(8,128)(2,1)S(1)} %multiply_convert_fusion, bf16[192,512]{1,0:T(8,128)(2,1)} %param.8), kind=kLoop, calls=%fused_computation.15 | loop fusion | flops 1490944 | bytes 444416 | tf_op jit(solution)/shard_map/concatenate | solution.py:161
  6.1 0.7 concatenate.36
  6.8 1.3 %collective-permute-start.2 = (bf16[224,512]{1,0:T(8,128)(2,1)}, bf16[224,512]{1,0:T(8,128)(2,1)S(1)}, u32[]{:S(2)}, u32[]{:S(2)}) collective-permute-start(bf16[224,512]{1,0:T(8,128)(2,1)} %fusion.7), channel_id=1, source_target_pairs={{4,0},{5,1},{6,2},{7,3},{8,4},{9,5},{10,6},{11,7},{12,8},{13,9},{1... | collective-permute-start | bytes 688136 | tf_op jit(solution)/shard_map/ppermute | solution.py:81
  8.1 5.6 %collective-permute-start.1 = (bf16[224,512]{1,0:T(8,128)(2,1)}, bf16[224,512]{1,0:T(8,128)(2,1)S(1)}, u32[]{:S(2)}, u32[]{:S(2)}) collective-permute-start(bf16[224,512]{1,0:T(8,128)(2,1)} %fusion.7), channel_id=1, source_target_pairs={{0,4},{1,5},{2,6},{3,7},{4,8},{5,9},{6,10},{7,11},{8,12},{9,13},{1... | collective-permute-start | bytes 688136 | tf_op jit(solution)/shard_map/ppermute | solution.py:80
  13.7 2.0 %collective-permute-start.7 = (bf16[224,512]{1,0:T(8,128)(2,1)}, bf16[224,512]{1,0:T(8,128)(2,1)}, u32[]{:S(2)}, u32[]{:S(2)}) collective-permute-start(bf16[224,512]{1,0:T(8,128)(2,1)} %fusion.7), channel_id=1, source_target_pairs={{0,2},{1,3},{2,0},{3,1},{4,6},{5,7},{6,4},{7,5},{8,10},{9,11},{10,... | collective-permute-start | bytes 688136 | tf_op jit(solution)/shard_map/ppermute | solution.py:82
  15.7 0.9 %bitcast_dynamic-update-slice_fusion.6 = bf16[8,224,512]{2,1,0:T(8,128)(2,1)S(1)} fusion(bf16[1,512]{1,0:T(2,128)(2,1)S(1)} %broadcast_in_dim.7, bf16[1,512]{1,0:T(2,128)(2,1)S(1)} %broadcast_in_dim.6, bf16[16,512]{1,0:T(8,128)(2,1)S(1)} %multiply_convert_fusion, bf16[192,512]{1,0:T(8,128)(2,1)} %param.8), kind=kLoop, calls=%fused_computation.25 | loop fusion | flops 1490943 | bytes 444416
  16.7 1.1 %multiply_reduce_fusion = f32[1024]{0:T(1024)S(1)} fusion(bf16[192,512]{1,0:T(8,128)(2,1)S(1)} %slice.52, bf16[192,512]{1,0:T(8,128)(2,1)} %param.8), kind=kLoop, calls=%fused_computation.3 | loop fusion | flops 1178624 | bytes 397312 | tf_op jit(solution)/shard_map/reduce_sum | solution.py:190
  17.9 1.1 %collective-permute-done.1 = bf16[224,512]{1,0:T(8,128)(2,1)S(1)} collective-permute-done((bf16[224,512]{1,0:T(8,128)(2,1)}, bf16[224,512]{1,0:T(8,128)(2,1)S(1)}, u32[]{:S(2)}, u32[]{:S(2)}) %collective-permute-start.1) | collective-permute-done | bytes 229408 | tf_op jit(solution)/shard_map/ppermute | solution.py:80
  19.0 0.8 %pad_maximum_fusion = bf16[2,224,512]{2,1,0:T(8,128)(2,1)} fusion(bf16[1,224,512]{2,1,0:T(8,128)(2,1)S(1)} %bitcast.47, bf16[1,224,512]{2,1,0:T(8,128)(2,1)S(1)} %bitcast.48), kind=kLoop, calls=%fused_computation.9 | loop fusion | flops 229376 | bytes 917504 | tf_op jit(solution)/shard_map/stack | solution.py:85
  19.8 1.7 %collective-permute-start.9 = (bf16[2,224,512]{2,1,0:T(8,128)(2,1)}, bf16[2,224,512]{2,1,0:T(8,128)(2,1)S(1)}, u32[]{:S(2)}, u32[]{:S(2)}) collective-permute-start(bf16[2,224,512]{2,1,0:T(8,128)(2,1)} %pad_maximum_fusion), channel_id=1, source_target_pairs={{0,2},{1,3},{2,0},{3,1},{4,6},{5,7},{6,4},{7,5},{8,10},{9,11},{10,... | collective-permute-start | bytes 1376264 | tf_op jit(solution)/shard_map/ppermute | solution.py:85
  21.5 1.0 %copy.52.xo_ref = bf16[1024,192]{1,0:T(8,128)(2,1)} copy(bf16[1024,192]{0,1:T(8,128)(2,1)S(1)} %multiply_bitcast_fusion) | data formatting | bytes 786432 | tf_op jit(solution)/shard_map/transpose | solution.py:193
  22.5 1.0 %copy.53.no_ref = f32[1024,1]{1,0:T(8,128)} copy(f32[1024,1]{0,1:T(1,128)S(1)} %bitcast.50) | data formatting | bytes 8192 | tf_op jit(solution)/shard_map/broadcast_in_dim | solution.py:190
  23.6 0.7 slice_bitcast_fusion
  24.3 0.2 copy.51
  24.5 0.9 %broadcast_divide_fusion.ro_ref = f32[1024,1]{1,0:T(8,128)} fusion(f32[1024,1]{1,0:T(8,128)S(1)} %copy.51), kind=kLoop, calls=%fused_computation.12 | loop fusion | flops 1024 | bytes 8192 | tf_op jit(solution)/shard_map/div | solution.py:192
  25.4 1.3 %collective-permute-start.4 = (bf16[224,512]{1,0:T(8,128)(2,1)S(1)}, bf16[224,512]{1,0:T(8,128)(2,1)S(1)}, u32[]{:S(2)}, u32[]{:S(2)}) collective-permute-start(bf16[224,512]{1,0:T(8,128)(2,1)S(1)} %collective-permute-done.2), channel_id=1, source_target_pairs={{4,0},{5,1},{6,2},{7,3},{8,4},{9,5},{10,6},{11,7},{12,8},{13,9},{1... | collective-permute-start | bytes 688136 | tf_op jit(solution)/shard_map/ppermute | solution.py:84
  26.7 4.9 %collective-permute-start.3 = (bf16[224,512]{1,0:T(8,128)(2,1)S(1)}, bf16[224,512]{1,0:T(8,128)(2,1)S(1)}, u32[]{:S(2)}, u32[]{:S(2)}) collective-permute-start(bf16[224,512]{1,0:T(8,128)(2,1)S(1)} %collective-permute-done.1), channel_id=1, source_target_pairs={{0,4},{1,5},{2,6},{3,7},{4,8},{5,9},{6,10},{7,11},{8,12},{9,13},{1... | collective-permute-start | bytes 688136 | tf_op jit(solution)/shard_map/ppermute | solution.py:83
  31.7 2.5 %collective-permute-done.4 = bf16[224,512]{1,0:T(8,128)(2,1)S(1)} collective-permute-done((bf16[224,512]{1,0:T(8,128)(2,1)S(1)}, bf16[224,512]{1,0:T(8,128)(2,1)S(1)}, u32[]{:S(2)}, u32[]{:S(2)}) %collective-permute-start.4) | collective-permute-done | bytes 229408 | tf_op jit(solution)/shard_map/ppermute | solution.py:84
  34.1 1.2 %collective-permute-done.3 = bf16[224,512]{1,0:T(8,128)(2,1)S(1)} collective-permute-done((bf16[224,512]{1,0:T(8,128)(2,1)S(1)}, bf16[224,512]{1,0:T(8,128)(2,1)S(1)}, u32[]{:S(2)}, u32[]{:S(2)}) %collective-permute-start.3) | collective-permute-done | bytes 229408 | tf_op jit(solution)/shard_map/ppermute | solution.py:83
  35.3 0.7 collective-permute-start.8
  36.1 1.3 %collective-permute-start.6 = (bf16[224,512]{1,0:T(8,128)(2,1)S(1)}, bf16[224,512]{1,0:T(8,128)(2,1)S(1)}, u32[]{:S(2)}, u32[]{:S(2)}) collective-permute-start(bf16[224,512]{1,0:T(8,128)(2,1)S(1)} %collective-permute-done.4), channel_id=1, source_target_pairs={{4,0},{5,1},{6,2},{7,3},{8,4},{9,5},{10,6},{11,7},{12,8},{13,9},{1... | collective-permute-start | bytes 688136 | tf_op jit(solution)/shard_map/ppermute | solution.py:88
  37.3 5.0 %collective-permute-start.5 = (bf16[224,512]{1,0:T(8,128)(2,1)S(1)}, bf16[224,512]{1,0:T(8,128)(2,1)S(1)}, u32[]{:S(2)}, u32[]{:S(2)}) collective-permute-start(bf16[224,512]{1,0:T(8,128)(2,1)S(1)} %collective-permute-done.3), channel_id=1, source_target_pairs={{0,4},{1,5},{2,6},{3,7},{4,8},{5,9},{6,10},{7,11},{8,12},{9,13},{1... | collective-permute-start | bytes 688136 | tf_op jit(solution)/shard_map/ppermute | solution.py:87
  42.5 1.9 %collective-permute-done.6 = bf16[224,512]{1,0:T(8,128)(2,1)S(1)} collective-permute-done((bf16[224,512]{1,0:T(8,128)(2,1)S(1)}, bf16[224,512]{1,0:T(8,128)(2,1)S(1)}, u32[]{:S(2)}, u32[]{:S(2)}) %collective-permute-start.6) | collective-permute-done | bytes 229408 | tf_op jit(solution)/shard_map/ppermute | solution.py:88
  44.4 1.5 %collective-permute-done.5 = bf16[224,512]{1,0:T(8,128)(2,1)S(1)} collective-permute-done((bf16[224,512]{1,0:T(8,128)(2,1)S(1)}, bf16[224,512]{1,0:T(8,128)(2,1)S(1)}, u32[]{:S(2)}, u32[]{:S(2)}) %collective-permute-start.5) | collective-permute-done | bytes 229408 | tf_op jit(solution)/shard_map/ppermute | solution.py:87
  45.9 1.4 %collective-permute-start.10 = (bf16[224,512]{1,0:T(8,128)(2,1)S(1)}, bf16[224,512]{1,0:T(8,128)(2,1)S(1)}, u32[]{:S(2)}, u32[]{:S(2)}) collective-permute-start(bf16[224,512]{1,0:T(8,128)(2,1)S(1)} %broadcast_select_fusion), channel_id=1, source_target_pairs={{0,2},{1,3},{2,0},{3,1},{4,6},{5,7},{6,4},{7,5},{8,10},{9,11},{10,... | collective-permute-start | bytes 688136 | tf_op jit(solution)/shard_map/ppermute | solution.py:91
  47.5 1.0 %bitcast_dynamic-update-slice_fusion.2 = bf16[8,224,512]{2,1,0:T(8,128)(2,1)S(1)} fusion(bf16[8,224,512]{2,1,0:T(8,128)(2,1)S(1)} %bitcast_dynamic-update-slice_fusion.3, bf16[224,512]{1,0:T(8,128)(2,1)} %collective-permute-done.7), kind=kLoop, calls=%fused_computation.21 | loop fusion | bytes 458752
  48.5 3.5 %collective-permute-done.10 = bf16[224,512]{1,0:T(8,128)(2,1)S(1)} collective-permute-done((bf16[224,512]{1,0:T(8,128)(2,1)S(1)}, bf16[224,512]{1,0:T(8,128)(2,1)S(1)}, u32[]{:S(2)}, u32[]{:S(2)}) %collective-permute-start.10) | collective-permute-done | bytes 229408 | tf_op jit(solution)/shard_map/ppermute | solution.py:91
  53.0 0.2 and_reduce_fusion
  53.1 0.5 convert_element_type.34.flag_ref
  53.7 8.6 %shard_map.95 = f32[16,1024]{1,0:T(8,128)} custom-call(s32[8]{0:T(128)} %convert_element_type.34.flag_ref, bf16[1024,192]{1,0:T(8,128)(2,1)} %copy.52.xo_ref, f32[1024,1]{1,0:T(8,128)} %copy.53.no_ref, f32[1024,1]{1,0:T(8,128)} %broadcast_divide_fusion.ro_ref, bf16[8,224,512]{2,1,0:T(8,128)(2,1)} %copy-done.1, bf16[8,224,512]{2,1,0:T(8,128)(2,1)} %copy-done.1), custom_call_target="tpu_custom_call" | custom-call | tf_op jit(solution)/shard_map/pallas_call | solution.py:61
  62.3 0.8 slice.55
  63.1 1.2 %collective-permute-done.12 = f32[16,512]{1,0:T(8,128)S(1)} collective-permute-done((f32[16,512]{1,0:T(8,128)S(1)}, f32[16,512]{1,0:T(8,128)S(1)}, u32[]{:S(2)}, u32[]{:S(2)}) %collective-permute-start.12) | collective-permute-done | bytes 32800 | tf_op jit(solution)/shard_map/ppermute | solution.py:196
  64.3 0.9 %convolution_bitcast_fusion = f32[16,16]{0,1:T(8,128)S(1)} fusion(f32[16,512]{1,0:T(8,128)S(1)} %copy-done.3, f32[16,512]{1,0:T(8,128)S(1)} %collective-permute-done.12, f32[16,1024]{1,0:T(8,128)} %shard_map.95, f32[512]{0:T(512)S(1)} %broadcast_multiply_fusion), kind=kOutput, calls=%fused_computation.2 | convolution fusion | flops 1589248 | bytes 101376 | tf_op jit(solution)/shard_map/dot_general | solution.py:198
  65.2 0.4 collective-permute-start.13
  65.6 1.4 %collective-permute-start.14 = (f32[16,16]{0,1:T(8,128)S(1)}, f32[16,16]{0,1:T(8,128)S(1)}, u32[]{:S(2)}, u32[]{:S(2)}) collective-permute-start(f32[16,16]{0,1:T(8,128)S(1)} %convolution_bitcast_fusion), channel_id=1, source_target_pairs={{0,2},{1,3},{2,0},{3,1},{4,6},{5,7},{6,4},{7,5},{8,10},{9,11},{10,... | collective-permute-start | bytes 3080 | tf_op jit(solution)/shard_map/ppermute | solution.py:127
  67.1 1.2 %collective-permute-done.13 = f32[16,16]{0,1:T(8,128)S(1)} collective-permute-done((f32[16,16]{0,1:T(8,128)S(1)}, f32[16,16]{0,1:T(8,128)S(1)}, u32[]{:S(2)}, u32[]{:S(2)}) %collective-permute-start.13) | collective-permute-done | bytes 1056 | tf_op jit(solution)/shard_map/ppermute | solution.py:127
  68.3 0.9 %collective-permute-done.14 = f32[16,16]{0,1:T(8,128)S(1)} collective-permute-done((f32[16,16]{0,1:T(8,128)S(1)}, f32[16,16]{0,1:T(8,128)S(1)}, u32[]{:S(2)}, u32[]{:S(2)}) %collective-permute-start.14) | collective-permute-done | bytes 1056 | tf_op jit(solution)/shard_map/ppermute | solution.py:127
  69.2 4.5 %collective-permute-start.16 = (f32[16,16]{0,1:T(8,128)S(1)}, f32[16,16]{0,1:T(8,128)S(1)}, u32[]{:S(2)}, u32[]{:S(2)}) collective-permute-start(f32[16,16]{0,1:T(8,128)S(1)} %select_add_fusion), channel_id=1, source_target_pairs={{0,12},{1,13},{2,14},{3,15},{4,8},{5,9},{6,10},{7,11},{8,4},{9,5},... | collective-permute-start | bytes 3080 | tf_op jit(solution)/shard_map/ppermute | solution.py:127
  73.8 0.3 collective-permute-start.17
  74.0 0.4 collective-permute-start.18
  74.6 0.8 %collective-permute-done.16 = f32[16,16]{0,1:T(8,128)S(1)} collective-permute-done((f32[16,16]{0,1:T(8,128)S(1)}, f32[16,16]{0,1:T(8,128)S(1)}, u32[]{:S(2)}, u32[]{:S(2)}) %collective-permute-start.16) | collective-permute-done | bytes 1056 | tf_op jit(solution)/shard_map/ppermute | solution.py:127
  75.4 2.9 %collective-permute-done.17 = f32[16,16]{0,1:T(8,128)S(1)} collective-permute-done((f32[16,16]{0,1:T(8,128)S(1)}, f32[16,16]{0,1:T(8,128)S(1)}, u32[]{:S(2)}, u32[]{:S(2)}) %collective-permute-start.17) | collective-permute-done | bytes 1056 | tf_op jit(solution)/shard_map/ppermute | solution.py:127
  78.3 0.7 copy.54
  79.0 1.5 %fusion = f32[16,512]{1,0:T(8,128)} fusion(f32[16,512]{1,0:T(8,128)S(1)} %fusion.18, f32[16,16]{0,1:T(8,128)S(1)} %add_multiply_fusion, f32[16,512]{1,0:T(8,128)S(1)} %copy-done.3, f32[512]{0:T(512)S(1)} %broadcast_multiply_fusion, f32[16,512]{1,0:T(8,128)S(1)} %collective-permute-done.12, f32[16,1024]{1,0:T(8,128)} %shard_map.95), kind=kOutput, calls=%fused_computation.1 | convolution fusion | flops 1605632 | bytes 166912 | tf_op jit(solution)/shard_map/dot_general | solution.py:202
  (60 shorter events, 2.2 us)
Async XLA Ops:
  0.6 73.8 %copy-start = (f32[16,512]{1,0:T(8,128)S(1)}, f32[16,512]{1,0:T(8,128)}, u32[]{:S(2)}) copy-start(f32[16,512]{1,0:T(8,128)} %param.12) | copy-start | bytes 98308
  0.6 17.1 %copy-start.2 = (bf16[192,512]{1,0:T(8,128)(2,1)S(1)}, bf16[192,512]{1,0:T(8,128)(2,1)}, u32[]{:S(2)}) copy-start(bf16[192,512]{1,0:T(8,128)(2,1)} %param.8) | copy-start | bytes 589828
  2.3 2.0 %collective-permute-start = (bf16[9]{0:T(256)(128)(2,1)S(1)}, bf16[9]{0:T(256)(128)(2,1)S(1)}, u32[]{:S(2)}, u32[]{:S(2)}) collective-permute-start(bf16[9]{0:T(256)(128)(2,1)S(1)} %pad_maximum_fusion.2), channel_id=1, source_target_pairs={{0,1},{1,0},{2,3},{3,2},{4,5},{5,4},{6,7},{7,6},{8,9},{9,8},{10,11... | collective-permute-start | bytes 62 | tf_op jit(solution)/shard_map/ppermute | solution.py:159
  6.0 10.6 %collective-permute-start.11 = (bf16[224,512]{1,0:T(8,128)(2,1)}, bf16[224,512]{1,0:T(8,128)(2,1)S(1)}, u32[]{:S(2)}, u32[]{:S(2)}) collective-permute-start(bf16[224,512]{1,0:T(8,128)(2,1)} %fusion.7), channel_id=1, source_target_pairs={{0,1},{1,0},{2,3},{3,2},{4,5},{5,4},{6,7},{7,6},{8,9},{9,8},{10,11... | collective-permute-start | bytes 688136 | tf_op jit(solution)/shard_map/ppermute | solution.py:185
  6.8 11.1 %collective-permute-start.2 = (bf16[224,512]{1,0:T(8,128)(2,1)}, bf16[224,512]{1,0:T(8,128)(2,1)S(1)}, u32[]{:S(2)}, u32[]{:S(2)}) collective-permute-start(bf16[224,512]{1,0:T(8,128)(2,1)} %fusion.7), channel_id=1, source_target_pairs={{4,0},{5,1},{6,2},{7,3},{8,4},{9,5},{10,6},{11,7},{12,8},{13,9},{1... | collective-permute-start | bytes 688136 | tf_op jit(solution)/shard_map/ppermute | solution.py:81
  8.1 10.9 %collective-permute-start.1 = (bf16[224,512]{1,0:T(8,128)(2,1)}, bf16[224,512]{1,0:T(8,128)(2,1)S(1)}, u32[]{:S(2)}, u32[]{:S(2)}) collective-permute-start(bf16[224,512]{1,0:T(8,128)(2,1)} %fusion.7), channel_id=1, source_target_pairs={{0,4},{1,5},{2,6},{3,7},{4,8},{5,9},{6,10},{7,11},{8,12},{9,13},{1... | collective-permute-start | bytes 688136 | tf_op jit(solution)/shard_map/ppermute | solution.py:80
  13.7 33.8 %collective-permute-start.7 = (bf16[224,512]{1,0:T(8,128)(2,1)}, bf16[224,512]{1,0:T(8,128)(2,1)}, u32[]{:S(2)}, u32[]{:S(2)}) collective-permute-start(bf16[224,512]{1,0:T(8,128)(2,1)} %fusion.7), channel_id=1, source_target_pairs={{0,2},{1,3},{2,0},{3,1},{4,6},{5,7},{6,4},{7,5},{8,10},{9,11},{10,... | collective-permute-start | bytes 688136 | tf_op jit(solution)/shard_map/ppermute | solution.py:82
  16.6 2.4 %copy-start.4 = (bf16[224,512]{1,0:T(8,128)(2,1)}, bf16[224,512]{1,0:T(8,128)(2,1)S(1)}, u32[]{:S(2)}) copy-start(bf16[224,512]{1,0:T(8,128)(2,1)S(1)} %collective-permute-done.11) | copy-start | bytes 688132
  19.8 28.6 %collective-permute-start.9 = (bf16[2,224,512]{2,1,0:T(8,128)(2,1)}, bf16[2,224,512]{2,1,0:T(8,128)(2,1)S(1)}, u32[]{:S(2)}, u32[]{:S(2)}) collective-permute-start(bf16[2,224,512]{2,1,0:T(8,128)(2,1)} %pad_maximum_fusion), channel_id=1, source_target_pairs={{0,2},{1,3},{2,0},{3,1},{4,6},{5,7},{6,4},{7,5},{8,10},{9,11},{10,... | collective-permute-start | bytes 1376264 | tf_op jit(solution)/shard_map/ppermute | solution.py:85
  25.4 8.7 %collective-permute-start.4 = (bf16[224,512]{1,0:T(8,128)(2,1)S(1)}, bf16[224,512]{1,0:T(8,128)(2,1)S(1)}, u32[]{:S(2)}, u32[]{:S(2)}) collective-permute-start(bf16[224,512]{1,0:T(8,128)(2,1)S(1)} %collective-permute-done.2), channel_id=1, source_target_pairs={{4,0},{5,1},{6,2},{7,3},{8,4},{9,5},{10,6},{11,7},{12,8},{13,9},{1... | collective-permute-start | bytes 688136 | tf_op jit(solution)/shard_map/ppermute | solution.py:84
  26.7 8.6 %collective-permute-start.3 = (bf16[224,512]{1,0:T(8,128)(2,1)S(1)}, bf16[224,512]{1,0:T(8,128)(2,1)S(1)}, u32[]{:S(2)}, u32[]{:S(2)}) collective-permute-start(bf16[224,512]{1,0:T(8,128)(2,1)S(1)} %collective-permute-done.1), channel_id=1, source_target_pairs={{0,4},{1,5},{2,6},{3,7},{4,8},{5,9},{6,10},{7,11},{8,12},{9,13},{1... | collective-permute-start | bytes 688136 | tf_op jit(solution)/shard_map/ppermute | solution.py:83
  35.3 13.1 %collective-permute-start.8 = (bf16[224,512]{1,0:T(8,128)(2,1)S(1)}, bf16[224,512]{1,0:T(8,128)(2,1)S(1)}, u32[]{:S(2)}, u32[]{:S(2)}) collective-permute-start(bf16[224,512]{1,0:T(8,128)(2,1)S(1)} %broadcast_select_fusion.1), channel_id=1, source_target_pairs={{0,2},{1,3},{2,0},{3,1},{4,6},{5,7},{6,4},{7,5},{8,10},{9,11},{10,... | collective-permute-start | bytes 688136 | tf_op jit(solution)/shard_map/ppermute | solution.py:89
  36.1 8.4 %collective-permute-start.6 = (bf16[224,512]{1,0:T(8,128)(2,1)S(1)}, bf16[224,512]{1,0:T(8,128)(2,1)S(1)}, u32[]{:S(2)}, u32[]{:S(2)}) collective-permute-start(bf16[224,512]{1,0:T(8,128)(2,1)S(1)} %collective-permute-done.4), channel_id=1, source_target_pairs={{4,0},{5,1},{6,2},{7,3},{8,4},{9,5},{10,6},{11,7},{12,8},{13,9},{1... | collective-permute-start | bytes 688136 | tf_op jit(solution)/shard_map/ppermute | solution.py:88
  37.3 8.5 %collective-permute-start.5 = (bf16[224,512]{1,0:T(8,128)(2,1)S(1)}, bf16[224,512]{1,0:T(8,128)(2,1)S(1)}, u32[]{:S(2)}, u32[]{:S(2)}) collective-permute-start(bf16[224,512]{1,0:T(8,128)(2,1)S(1)} %collective-permute-done.3), channel_id=1, source_target_pairs={{0,4},{1,5},{2,6},{3,7},{4,8},{5,9},{6,10},{7,11},{8,12},{9,13},{1... | collective-permute-start | bytes 688136 | tf_op jit(solution)/shard_map/ppermute | solution.py:87
  45.9 6.1 %collective-permute-start.10 = (bf16[224,512]{1,0:T(8,128)(2,1)S(1)}, bf16[224,512]{1,0:T(8,128)(2,1)S(1)}, u32[]{:S(2)}, u32[]{:S(2)}) collective-permute-start(bf16[224,512]{1,0:T(8,128)(2,1)S(1)} %broadcast_select_fusion), channel_id=1, source_target_pairs={{0,2},{1,3},{2,0},{3,1},{4,6},{5,7},{6,4},{7,5},{8,10},{9,11},{10,... | collective-permute-start | bytes 688136 | tf_op jit(solution)/shard_map/ppermute | solution.py:91
  52.1 1.6 %copy-start.1 = (bf16[8,224,512]{2,1,0:T(8,128)(2,1)}, bf16[8,224,512]{2,1,0:T(8,128)(2,1)S(1)}, u32[]{:S(2)}) copy-start(bf16[8,224,512]{2,1,0:T(8,128)(2,1)S(1)} %bitcast_dynamic-update-slice_fusion.x_ref.w_ref) | copy-start | bytes 5505028
  53.7 9.4 %copy-start.6 = (f32[512]{0:T(512)S(1)}, f32[512]{0:T(512)}, u32[]{:S(2)}) copy-start(f32[512]{0:T(512)} %param.10) | copy-start | bytes 6148
  53.7 10.6 %copy-start.3 = (f32[16,512]{1,0:T(8,128)S(1)}, f32[16,512]{1,0:T(8,128)}, u32[]{:S(2)}) copy-start(f32[16,512]{1,0:T(8,128)} %param.11) | copy-start | bytes 98308
  53.7 20.7 %copy-start.5 = (f32[16,16]{1,0:T(8,128)S(1)}, f32[16,16]{1,0:T(8,128)}, u32[]{:S(2)}) copy-start(f32[16,16]{1,0:T(8,128)} %param.13) | copy-start | bytes 3076
  63.1 1.2 %collective-permute-start.12 = (f32[16,512]{1,0:T(8,128)S(1)}, f32[16,512]{1,0:T(8,128)S(1)}, u32[]{:S(2)}, u32[]{:S(2)}) collective-permute-start(f32[16,512]{1,0:T(8,128)S(1)} %slice.55), channel_id=1, source_target_pairs={{0,1},{1,0},{2,3},{3,2},{4,5},{5,4},{6,7},{7,6},{8,9},{9,8},{10,11... | collective-permute-start | bytes 98312 | tf_op jit(solution)/shard_map/ppermute | solution.py:196
  65.2 3.1 %collective-permute-start.13 = (f32[16,16]{0,1:T(8,128)S(1)}, f32[16,16]{0,1:T(8,128)S(1)}, u32[]{:S(2)}, u32[]{:S(2)}) collective-permute-start(f32[16,16]{0,1:T(8,128)S(1)} %convolution_bitcast_fusion), channel_id=1, source_target_pairs={{0,3},{1,2},{2,1},{3,0},{4,7},{5,6},{6,5},{7,4},{8,11},{9,10},{10,... | collective-permute-start | bytes 3080 | tf_op jit(solution)/shard_map/ppermute | solution.py:127
  65.6 3.7 %collective-permute-start.14 = (f32[16,16]{0,1:T(8,128)S(1)}, f32[16,16]{0,1:T(8,128)S(1)}, u32[]{:S(2)}, u32[]{:S(2)}) collective-permute-start(f32[16,16]{0,1:T(8,128)S(1)} %convolution_bitcast_fusion), channel_id=1, source_target_pairs={{0,2},{1,3},{2,0},{3,1},{4,6},{5,7},{6,4},{7,5},{8,10},{9,11},{10,... | collective-permute-start | bytes 3080 | tf_op jit(solution)/shard_map/ppermute | solution.py:127
  67.0 2.2 %collective-permute-start.15 = (f32[16,16]{0,1:T(8,128)S(1)}, f32[16,16]{0,1:T(8,128)S(1)}, u32[]{:S(2)}, u32[]{:S(2)}) collective-permute-start(f32[16,16]{0,1:T(8,128)S(1)} %convolution_bitcast_fusion), channel_id=1, source_target_pairs={{0,1},{1,0},{2,3},{3,2},{4,5},{5,4},{6,7},{7,6},{8,9},{9,8},{10,11... | collective-permute-start | bytes 3080 | tf_op jit(solution)/shard_map/ppermute | solution.py:127
  69.2 6.2 %collective-permute-start.16 = (f32[16,16]{0,1:T(8,128)S(1)}, f32[16,16]{0,1:T(8,128)S(1)}, u32[]{:S(2)}, u32[]{:S(2)}) collective-permute-start(f32[16,16]{0,1:T(8,128)S(1)} %select_add_fusion), channel_id=1, source_target_pairs={{0,12},{1,13},{2,14},{3,15},{4,8},{5,9},{6,10},{7,11},{8,4},{9,5},... | collective-permute-start | bytes 3080 | tf_op jit(solution)/shard_map/ppermute | solution.py:127
  73.8 4.6 %collective-permute-start.17 = (f32[16,16]{0,1:T(8,128)S(1)}, f32[16,16]{0,1:T(8,128)S(1)}, u32[]{:S(2)}, u32[]{:S(2)}) collective-permute-start(f32[16,16]{0,1:T(8,128)S(1)} %select_add_fusion), channel_id=1, source_target_pairs={{0,8},{1,9},{2,10},{3,11},{4,12},{5,13},{6,14},{7,15},{8,0},{9,1},... | collective-permute-start | bytes 3080 | tf_op jit(solution)/shard_map/ppermute | solution.py:127
  74.0 4.3 %collective-permute-start.18 = (f32[16,16]{0,1:T(8,128)S(1)}, f32[16,16]{0,1:T(8,128)S(1)}, u32[]{:S(2)}, u32[]{:S(2)}) collective-permute-start(f32[16,16]{0,1:T(8,128)S(1)} %select_add_fusion), channel_id=1, source_target_pairs={{0,4},{1,5},{2,6},{3,7},{4,0},{5,1},{6,2},{7,3},{8,12},{9,13},{10,... | collective-permute-start | bytes 3080 | tf_op jit(solution)/shard_map/ppermute | solution.py:127

commit v10 on v9

--- a/solution.py
+++ b/solution.py
@@ -15,6 +15,19 @@
 HIGHEST = lax.Precision.HIGHEST
 
 
+def piece_terms(width, x_cols, w_cols, xo_ref, no_ref, ro_ref):
+    x_wide = x_cols.astype(jnp.float32)
+    norm_cols = jnp.sum(x_wide * x_wide, axis=0, keepdims=True)
+    recip_cols = 1.0 / w_cols[LANCZOS : LANCZOS + 1, :].astype(jnp.float32)
+    twice_inner = jnp.dot(xo_ref[...], x_cols, preferred_element_type=jnp.float32)
+    distance = (no_ref[...] + norm_cols) - twice_inner
+    weights = jnp.exp2(distance * (ro_ref[...] * recip_cols)).astype(jnp.bfloat16)
+    return lax.dot_general(
+        w_cols[:LANCZOS, :], weights, (((1,), (1,)), ((), ())),
+        preferred_element_type=jnp.float32,
+    )
+
+
 def affinity_kernel(width, per, flag_ref, xo_ref, no_ref, ro_ref, x_ref, w_ref, out_ref):
     s = pl.program_id(0)
 
@@ -26,17 +39,43 @@
 
         @pl.when(flag_ref[s * per + k] != 0)
         def _():
-            x_cols = x_ref[k, :width, :]
-            x_wide = x_cols.astype(jnp.float32)
-            norm_cols = jnp.sum(x_wide * x_wide, axis=0, keepdims=True)
-            recip_cols = 1.0 / w_ref[k, LANCZOS : LANCZOS + 1, :].astype(jnp.float32)
-            twice_inner = jnp.dot(xo_ref[...], x_cols, preferred_element_type=jnp.float32)
-            distance = (no_ref[...] + norm_cols) - twice_inner
-            weights = jnp.exp2(distance * (ro_ref[...] * recip_cols)).astype(jnp.bfloat16)
-            out_ref[...] += lax.dot_general(
-                w_ref[k, :LANCZOS, :], weights, (((1,), (1,)), ((), ())),
-                preferred_element_type=jnp.float32,
+            out_ref[...] += piece_terms(
+                width, x_ref[k, :width, :], w_ref[k],
+                xo_ref, no_ref, ro_ref,
             )
+
+
+def list_kernel(width, rows, counts, flag_ref, xo_ref, no_ref, ro_ref, *refs):
+    out_ref = refs[-1]
+    out_ref[...] = jnp.zeros_like(out_ref)
+    slot = 0
+    for ref, count in zip(refs[:-1], counts):
+        for k in range(count):
+
+            @pl.when(flag_ref[slot] != 0)
+            def _():
+                base = k * rows
+                out_ref[...] += piece_terms(
+                    width,
+                    ref[base : base + width, :],
+                    ref[base + width : base + width + 2 * LANCZOS, :],
+                    xo_ref, no_ref, ro_ref,
+                )
+
+            slot += 1
+
+
+def list_product(flags, own_terms, pieces, width, rows):
+    twice_own_t, norm_own, recip_own = own_terms
+    own = twice_own_t.shape[0]
+    counts = [p.shape[0] // rows for p in pieces]
+    vmem = pl.BlockSpec(memory_space=pltpu.VMEM)
+    return pl.pallas_call(
+        functools.partial(list_kernel, width, rows, counts),
+        in_specs=[pl.BlockSpec(memory_space=pltpu.SMEM)] + [vmem] * (3 + len(pieces)),
+        out_specs=vmem,
+        out_shape=jax.ShapeDtypeStruct((LANCZOS, own), jnp.float32),
+    )(flags, twice_own_t, norm_own, recip_own, *pieces)
 
 
 def own_rows_product(flags, own_terms, mine, width):
@@ -70,7 +109,7 @@
     me = lax.axis_index("row")
     if devices != 16:
         pieces = lax.all_gather(packed, "row", axis=0, tiled=False)
-        return pieces, jnp.arange(devices, dtype=jnp.int32)
+        return [pieces], None, jnp.arange(devices, dtype=jnp.int32)
     up = [(r, r + 4) for r in range(12)]
     down = [(r, r - 4) for r in range(4, 16)]
     across = [(r, r ^ 2) for r in range(16)]
@@ -82,7 +121,7 @@
     across1 = lax.ppermute(packed, "row", across)
     up2 = lax.ppermute(up1, "row", up)
     down2 = lax.ppermute(down1, "row", down)
-    across2 = lax.ppermute(jnp.stack([up1, down1]), "row", across)
+    across2 = lax.ppermute(jnp.concatenate([up1, down1]), "row", across)
     pick2 = jnp.where(z >= 2, up2, down2)
     up3 = lax.ppermute(up2, "row", up)
     down3 = lax.ppermute(down2, "row", down)
@@ -91,23 +130,14 @@
     across4 = lax.ppermute(pick3, "row", across)
 
     ends = (z == 0) | (z == 3)
-    line1 = jnp.where(z >= 1, up1, down1)
-    line2 = jnp.where(z >= 2, up2, jnp.where(z == 1, down1, down2))
-    line3 = jnp.where(z == 3, up3, jnp.where(z == 2, down1, jnp.where(z == 1, down2, down3)))
-    other2 = jnp.where(z >= 1, across2[0], across2[1])
-    other3 = jnp.where(ends, across4, across2[1])
-    mine = jnp.stack([packed, line1, line2, line3, across1, across3, other2, other3])
-    origin = jnp.stack([
-        me,
-        jnp.where(z >= 1, me - 4, me + 4),
-        jnp.where(z >= 2, me - 8, jnp.where(z == 1, me + 4, me + 8)),
-        jnp.where(z == 3, me - 12, jnp.where(z == 2, me + 4, jnp.where(z == 1, me + 8, me + 12))),
-        partner,
-        jnp.where(z >= 2, partner - 8, partner + 8),
-        jnp.where(z >= 1, partner - 4, partner + 4),
-        jnp.where(z == 3, partner - 12, jnp.where(z == 0, partner + 12, partner + 4)),
-    ]).astype(jnp.int32)
-    return mine, origin
+    one = jnp.ones((), bool)
+    pieces = [packed, up1, down1, across1, up2, down2, across2, up3, down3, across3, across4]
+    valid = [one, z >= 1, z <= 2, one, z >= 2, z <= 1, z >= 1, z <= 2, z == 3, z == 0, one, ends]
+    origin = [
+        me, me - 4, me + 4, partner, me - 8, me + 8, partner - 4, partner + 4, me - 12, me + 12,
+        jnp.where(z >= 2, partner - 8, partner + 8), jnp.where(z == 3, partner - 12, partner + 12),
+    ]
+    return pieces, jnp.stack(valid), jnp.clip(jnp.stack(origin), 0, devices - 1).astype(jnp.int32)
 
 
 def sum_over_rows(value):
@@ -162,13 +192,15 @@
         [embeddings, weighted, local_scale[None, :], plan_row[None, :]], axis=0
     )
     packed = jnp.pad(packed, ((0, -packed.shape[0] % (2 * LANCZOS)), (0, 0)))
-    mine, origin = gather_pieces(packed)
+    pieces, valid, origin = gather_pieces(packed)
+    rows = packed.shape[0]
 
     plan_at = width + LANCZOS + 1
     copies = 2 if chip_split else 1
-    plans = mine[:, plan_at, : copies * plan_len].astype(jnp.int32).reshape(devices, plan_len)
+    plans = jnp.concatenate([p.reshape(-1, rows, own)[:, plan_at, : copies * plan_len] for p in pieces])
+    plans = plans.astype(jnp.int32).reshape(-1, plan_len)
     counts = plans[:, 2 * slots]
-    pairs = plans[:, : 2 * slots].reshape(devices, slots, 2)
+    pairs = plans[:, : 2 * slots].reshape(-1, slots, 2)
     live = jnp.arange(slots, dtype=jnp.int32)[None, :] < counts[:, None]
     row_block = pairs[..., 0].reshape(-1)[:, None]
     col_block = pairs[..., 1].reshape(-1)[:, None]
@@ -179,7 +211,10 @@
         ((row_block == my_block) & (col_block == piece_block))
         | ((col_block == my_block) & (row_block == piece_block))
     )
-    flags = jnp.any(hit, axis=0).astype(jnp.int32)
+    flags = jnp.any(hit, axis=0)
+    if valid is not None:
+        flags = flags & valid
+    flags = flags.astype(jnp.int32)
 
     if chip_split:
         twin_piece = lax.ppermute(packed, "row", twin)
@@ -191,7 +226,10 @@
     log2e = 1.0 / math.log(2.0)
     recip_rows = (-log2e / rows_scale.astype(jnp.float32))[:, None]
     own_terms = ((rows_x * 2).T, norm_rows, recip_rows)
-    summed = own_rows_product(flags, own_terms, mine, width)
+    if chip_split:
+        summed = list_product(flags, own_terms, pieces, width, rows)
+    else:
+        summed = own_rows_product(flags, own_terms, pieces[0].reshape(devices, rows, own), width)
     if chip_split:
         summed = summed[:, :own] + lax.ppermute(summed[:, own:], "row", twin)
     scaled = summed * (degree_scale[None, :] / math.sqrt(total_rows))

time: 81.4 us -> 77.1 us (0.947)
  waiting for transfers between devices: 18.8 us -> 27.9 us
  starting transfers between devices: 32.8 us -> 27.5 us
  other arithmetic: 8.37 us -> 3.67 us
  matrix products: 2.58 us -> 1.07 us
  local copies, waits for them, and re-layouts: 7.83 us -> 6.58 us
    ppermute x1, waiting for transfers between devices: 0.01 us -> 4.12 us  [gather_pieces(): down1 = lax.ppermute(packed, 'row', down)]
    ppermute x1, waiting for transfers between devices: 1.95 us -> 4.4 us  [gather_pieces(): down3 = lax.ppermute(down2, 'row', down)]
    ppermute x1, waiting for transfers between devices: 2.46 us -> 4.13 us  [gather_pieces(): down2 = lax.ppermute(down1, 'row', down)]
    concatenate x1, other arithmetic: 1.64 us -> 0.02 us  [shards(): jnp.concatenate([embeddings, weighted, local_scale[None, :], plan_row[Non...]
    ppermute x1, starting transfers between devices: 5.03 us -> 3.47 us  [gather_pieces(): up3 = lax.ppermute(up2, 'row', up)]
    ppermute x1, starting transfers between devices: 4.92 us -> 3.47 us  [gather_pieces(): up2 = lax.ppermute(up1, 'row', up)]
    ppermute x6, waiting for transfers between devices: 5.91 us -> 4.56 us  [sum_over_rows(): lax.ppermute(value, 'row', [(i, i ^ m << shift) for i in range(devices)])]
    ppermute x1, waiting for transfers between devices: 1.15 us -> 2.46 us  [gather_pieces(): up1 = lax.ppermute(packed, 'row', up)]
  transfers between devices with their start and end apart: 19 -> 19, of which waited for: 11 -> 12; matrix products, arithmetic and copies ran while one was open for 13% -> 8% of each run, Pallas kernels for 0% -> 0%
where the time goes in v10:
time: 77.1 us; the launch traced here: 76.7 us
  waiting for transfers between devices  27.9 us (36%)
  starting transfers between devices  27.5 us (36%)
  Pallas kernels  8.21 us (11%)
  local copies, waits for them, and re-layouts  6.58 us (9%)
  other arithmetic  3.67 us (5%)
  between operations  1.65 us (2%)
  matrix products  1.07 us (1%)
    pallas_call x1, Pallas kernels, list_product(): pl.pallas_call(functools.partial(list_kernel, width, rows, counts), in_sp...  8.21 us
    ppermute x6, starting transfers between devices, sum_over_rows(): lax.ppermute(value, 'row', [(i, i ^ m << shift) for i in range(devices)])  6.33 us
    ppermute x6, waiting for transfers between devices, sum_over_rows(): lax.ppermute(value, 'row', [(i, i ^ m << shift) for i in range(devices)])  4.56 us
    ppermute x1, starting transfers between devices, gather_pieces(): up1 = lax.ppermute(packed, 'row', up)  4.54 us
    ppermute x1, waiting for transfers between devices, gather_pieces(): down3 = lax.ppermute(down2, 'row', down)  4.4 us
    ppermute x1, waiting for transfers between devices, gather_pieces(): across4 = lax.ppermute(pick3, 'row', across)  4.4 us
    ppermute x1, waiting for transfers between devices, gather_pieces(): down2 = lax.ppermute(down1, 'row', down)  4.13 us
    ppermute x1, waiting for transfers between devices, gather_pieces(): down1 = lax.ppermute(packed, 'row', down)  4.12 us
  transfers between devices with their start and end apart: 19, of which 12 were waited for; matrix products, arithmetic and copies ran while one was open for 8% of the time, Pallas kernels for 0%

profile of v10, /device:TPU:0, one launch (start us, length us, event | category | flops | bytes accessed | tf_op | source)
XLA Modules:
  0.0 76.7 jit_solution(11651309166557960596)
XLA Ops:
  0.7 0.7 convert.8
  1.4 0.1 copy.53
  2.3 0.5 collective-permute-start
  2.8 0.7 broadcast_in_dim.6
  3.5 0.7 concatenate.44
  4.2 0.8 %multiply_convert_fusion = bf16[16,512]{1,0:T(8,128)(2,1)S(1)} fusion(f32[16,512]{1,0:T(8,128)} %param.11, f32[512]{0:T(512)} %param.10), kind=kLoop, calls=%fused_computation.20 | loop fusion | flops 16384 | bytes 51200 | tf_op jit(solution)/shard_map/convert_element_type | solution.py:185
  5.0 0.1 stack.85
  5.3 4.5 %collective-permute-start.1 = (bf16[224,512]{1,0:T(8,128)(2,1)S(1)}, bf16[224,512]{1,0:T(8,128)(2,1)S(1)}, u32[]{:S(2)}, u32[]{:S(2)}) collective-permute-start(bf16[224,512]{1,0:T(8,128)(2,1)S(1)} %fusion.7.refs_0_), channel_id=1, source_target_pairs={{0,4},{1,5},{2,6},{3,7},{4,8},{5,9},{6,10},{7,11},{8,12},{9,13},{1... | collective-permute-start | bytes 688136 | tf_op jit(solution)/shard_map/ppermute | solution.py:119
  9.8 1.3 %collective-permute-start.2 = (bf16[224,512]{1,0:T(8,128)(2,1)S(1)}, bf16[224,512]{1,0:T(8,128)(2,1)S(1)}, u32[]{:S(2)}, u32[]{:S(2)}) collective-permute-start(bf16[224,512]{1,0:T(8,128)(2,1)S(1)} %fusion.7.refs_0_), channel_id=1, source_target_pairs={{4,0},{5,1},{6,2},{7,3},{8,4},{9,5},{10,6},{11,7},{12,8},{13,9},{1... | collective-permute-start | bytes 688136 | tf_op jit(solution)/shard_map/ppermute | solution.py:120
  11.1 1.6 %collective-permute-start.3 = (bf16[224,512]{1,0:T(8,128)(2,1)S(1)}, bf16[224,512]{1,0:T(8,128)(2,1)S(1)}, u32[]{:S(2)}, u32[]{:S(2)}) collective-permute-start(bf16[224,512]{1,0:T(8,128)(2,1)S(1)} %fusion.7.refs_0_), channel_id=1, source_target_pairs={{0,2},{1,3},{2,0},{3,1},{4,6},{5,7},{6,4},{7,5},{8,10},{9,11},{10,... | collective-permute-start | bytes 688136 | tf_op jit(solution)/shard_map/ppermute | solution.py:121
  12.8 2.5 %collective-permute-done.1.refs_1_ = bf16[224,512]{1,0:T(8,128)(2,1)S(1)} collective-permute-done((bf16[224,512]{1,0:T(8,128)(2,1)S(1)}, bf16[224,512]{1,0:T(8,128)(2,1)S(1)}, u32[]{:S(2)}, u32[]{:S(2)}) %collective-permute-start.1) | collective-permute-done | bytes 229408 | tf_op jit(solution)/shard_map/ppermute | solution.py:119
  15.3 4.1 %collective-permute-done.2.refs_2_ = bf16[224,512]{1,0:T(8,128)(2,1)S(1)} collective-permute-done((bf16[224,512]{1,0:T(8,128)(2,1)S(1)}, bf16[224,512]{1,0:T(8,128)(2,1)S(1)}, u32[]{:S(2)}, u32[]{:S(2)}) %collective-permute-start.2) | collective-permute-done | bytes 229408 | tf_op jit(solution)/shard_map/ppermute | solution.py:120
  19.4 1.6 %collective-permute-start.6 = (bf16[448,512]{1,0:T(8,128)(2,1)S(1)}, bf16[448,512]{1,0:T(8,128)(2,1)S(1)}, u32[]{:S(2)}, u32[]{:S(2)}) collective-permute-start(bf16[448,512]{1,0:T(8,128)(2,1)S(1)} %pad_maximum_fusion), channel_id=1, source_target_pairs={{0,2},{1,3},{2,0},{3,1},{4,6},{5,7},{6,4},{7,5},{8,10},{9,11},{10,... | collective-permute-start | bytes 1376264 | tf_op jit(solution)/shard_map/ppermute | solution.py:124
  21.0 0.2 copy.59
  21.3 0.9 %broadcast_divide_fusion.ro_ref = f32[1024,1]{1,0:T(8,128)} fusion(f32[1024,1]{1,0:T(8,128)S(1)} %copy.59), kind=kLoop, calls=%fused_computation.12 | loop fusion | flops 1024 | bytes 8192 | tf_op jit(solution)/shard_map/div | solution.py:227
  22.2 3.5 %collective-permute-start.4 = (bf16[224,512]{1,0:T(8,128)(2,1)S(1)}, bf16[224,512]{1,0:T(8,128)(2,1)S(1)}, u32[]{:S(2)}, u32[]{:S(2)}) collective-permute-start(bf16[224,512]{1,0:T(8,128)(2,1)S(1)} %collective-permute-done.1.refs_1_), channel_id=1, source_target_pairs={{0,4},{1,5},{2,6},{3,7},{4,8},{5,9},{6,10},{7,11},{8,12},{9,13},{1... | collective-permute-start | bytes 688136 | tf_op jit(solution)/shard_map/ppermute | solution.py:122
  25.7 1.3 %collective-permute-start.5 = (bf16[224,512]{1,0:T(8,128)(2,1)S(1)}, bf16[224,512]{1,0:T(8,128)(2,1)S(1)}, u32[]{:S(2)}, u32[]{:S(2)}) collective-permute-start(bf16[224,512]{1,0:T(8,128)(2,1)S(1)} %collective-permute-done.2.refs_2_), channel_id=1, source_target_pairs={{4,0},{5,1},{6,2},{7,3},{8,4},{9,5},{10,6},{11,7},{12,8},{13,9},{1... | collective-permute-start | bytes 688136 | tf_op jit(solution)/shard_map/ppermute | solution.py:123
  27.2 1.0 %copy.60.xo_ref = bf16[1024,192]{1,0:T(8,128)(2,1)} copy(bf16[1024,192]{0,1:T(8,128)(2,1)S(1)} %multiply_bitcast_fusion) | data formatting | bytes 786432 | tf_op jit(solution)/shard_map/transpose | solution.py:228
  28.2 1.0 %copy.61.no_ref = f32[1024,1]{1,0:T(8,128)} copy(f32[1024,1]{0,1:T(1,128)S(1)} %bitcast.83) | data formatting | bytes 8192 | tf_op jit(solution)/shard_map/broadcast_in_dim | solution.py:225
  29.2 0.5 collective-permute-done.4.refs_4_
  29.7 4.1 %collective-permute-done.5.refs_5_ = bf16[224,512]{1,0:T(8,128)(2,1)S(1)} collective-permute-done((bf16[224,512]{1,0:T(8,128)(2,1)S(1)}, bf16[224,512]{1,0:T(8,128)(2,1)S(1)}, u32[]{:S(2)}, u32[]{:S(2)}) %collective-permute-start.5) | collective-permute-done | bytes 229408 | tf_op jit(solution)/shard_map/ppermute | solution.py:123
  33.9 0.6 collective-permute-start.9
  34.5 3.5 %collective-permute-start.7 = (bf16[224,512]{1,0:T(8,128)(2,1)S(1)}, bf16[224,512]{1,0:T(8,128)(2,1)S(1)}, u32[]{:S(2)}, u32[]{:S(2)}) collective-permute-start(bf16[224,512]{1,0:T(8,128)(2,1)S(1)} %collective-permute-done.4.refs_4_), channel_id=1, source_target_pairs={{0,4},{1,5},{2,6},{3,7},{4,8},{5,9},{6,10},{7,11},{8,12},{9,13},{1... | collective-permute-start | bytes 688136 | tf_op jit(solution)/shard_map/ppermute | solution.py:126
  38.0 1.3 %collective-permute-start.8 = (bf16[224,512]{1,0:T(8,128)(2,1)S(1)}, bf16[224,512]{1,0:T(8,128)(2,1)S(1)}, u32[]{:S(2)}, u32[]{:S(2)}) collective-permute-start(bf16[224,512]{1,0:T(8,128)(2,1)S(1)} %collective-permute-done.5.refs_5_), channel_id=1, source_target_pairs={{4,0},{5,1},{6,2},{7,3},{8,4},{9,5},{10,6},{11,7},{12,8},{13,9},{1... | collective-permute-start | bytes 688136 | tf_op jit(solution)/shard_map/ppermute | solution.py:127
  39.3 2.2 %collective-permute-done.7.refs_7_ = bf16[224,512]{1,0:T(8,128)(2,1)S(1)} collective-permute-done((bf16[224,512]{1,0:T(8,128)(2,1)S(1)}, bf16[224,512]{1,0:T(8,128)(2,1)S(1)}, u32[]{:S(2)}, u32[]{:S(2)}) %collective-permute-start.7) | collective-permute-done | bytes 229408 | tf_op jit(solution)/shard_map/ppermute | solution.py:126
  41.5 4.4 %collective-permute-done.8.refs_8_ = bf16[224,512]{1,0:T(8,128)(2,1)S(1)} collective-permute-done((bf16[224,512]{1,0:T(8,128)(2,1)S(1)}, bf16[224,512]{1,0:T(8,128)(2,1)S(1)}, u32[]{:S(2)}, u32[]{:S(2)}) %collective-permute-start.8) | collective-permute-done | bytes 229408 | tf_op jit(solution)/shard_map/ppermute | solution.py:127
  45.9 1.6 %collective-permute-start.10 = (bf16[224,512]{1,0:T(8,128)(2,1)S(1)}, bf16[224,512]{1,0:T(8,128)(2,1)S(1)}, u32[]{:S(2)}, u32[]{:S(2)}) collective-permute-start(bf16[224,512]{1,0:T(8,128)(2,1)S(1)} %broadcast_select_fusion), channel_id=1, source_target_pairs={{0,2},{1,3},{2,0},{3,1},{4,6},{5,7},{6,4},{7,5},{8,10},{9,11},{10,... | collective-permute-start | bytes 688136 | tf_op jit(solution)/shard_map/ppermute | solution.py:130
  47.6 4.4 %collective-permute-done.10.refs_10_ = bf16[224,512]{1,0:T(8,128)(2,1)S(1)} collective-permute-done((bf16[224,512]{1,0:T(8,128)(2,1)S(1)}, bf16[224,512]{1,0:T(8,128)(2,1)S(1)}, u32[]{:S(2)}, u32[]{:S(2)}) %collective-permute-start.10) | collective-permute-done | bytes 229408 | tf_op jit(solution)/shard_map/ppermute | solution.py:130
  52.1 0.2 slice_reduce_fusion
  52.5 0.1 broadcast_in_dim_reshape_squeeze.4
  52.9 0.1 lt.26
  53.0 0.2 and_reduce_fusion
  53.2 0.5 and_convert_fusion.flag_ref
  53.7 8.2 %shard_map.95 = f32[16,1024]{1,0:T(8,128)} custom-call(s32[12]{0:T(128)} %and_convert_fusion.flag_ref, bf16[1024,192]{1,0:T(8,128)(2,1)} %copy.60.xo_ref, f32[1024,1]{1,0:T(8,128)} %copy.61.no_ref, f32[1024,1]{1,0:T(8,128)} %broadcast_divide_fusion.ro_ref, bf16[224,512]{1,0:T(8,128)(2,1)} %copy-done.4, bf16[224,512]{1,0:T(8,128)(2,1)} %copy-done.2, ...), custom_call_target="tpu_custom_call" | custom-call | tf_op jit(solution)/shard_map/pallas_call | solution.py:73
  61.9 0.8 %slice.94 = f32[16,512]{1,0:T(8,128)S(1)} slice(f32[16,1024]{1,0:T(8,128)} %shard_map.95), slice={[0:16], [512:1024]} | slice | bytes 65536 | tf_op jit(solution)/shard_map/slice | solution.py:234
  62.8 1.2 %collective-permute-done.12 = f32[16,512]{1,0:T(8,128)S(1)} collective-permute-done((f32[16,512]{1,0:T(8,128)S(1)}, f32[16,512]{1,0:T(8,128)S(1)}, u32[]{:S(2)}, u32[]{:S(2)}) %collective-permute-start.12) | collective-permute-done | bytes 32800 | tf_op jit(solution)/shard_map/ppermute | solution.py:234
  64.0 0.1 convolution_bitcast_fusion
  64.1 1.3 %collective-permute-start.13 = (f32[16,16]{0,1:T(8,128)S(1)}, f32[16,16]{0,1:T(8,128)S(1)}, u32[]{:S(2)}, u32[]{:S(2)}) collective-permute-start(f32[16,16]{0,1:T(8,128)S(1)} %convolution_bitcast_fusion), channel_id=1, source_target_pairs={{0,3},{1,2},{2,1},{3,0},{4,7},{5,6},{6,5},{7,4},{8,11},{9,10},{10,... | collective-permute-start | bytes 3080 | tf_op jit(solution)/shard_map/ppermute | solution.py:157
  65.4 0.5 collective-permute-start.14
  66.0 1.2 %collective-permute-done.13 = f32[16,16]{0,1:T(8,128)S(1)} collective-permute-done((f32[16,16]{0,1:T(8,128)S(1)}, f32[16,16]{0,1:T(8,128)S(1)}, u32[]{:S(2)}, u32[]{:S(2)}) %collective-permute-start.13) | collective-permute-done | bytes 1056 | tf_op jit(solution)/shard_map/ppermute | solution.py:157
  67.2 1.9 %collective-permute-done.14 = f32[16,16]{0,1:T(8,128)S(1)} collective-permute-done((f32[16,16]{0,1:T(8,128)S(1)}, f32[16,16]{0,1:T(8,128)S(1)}, u32[]{:S(2)}, u32[]{:S(2)}) %collective-permute-start.14) | collective-permute-done | bytes 1056 | tf_op jit(solution)/shard_map/ppermute | solution.py:157
  69.2 0.2 collective-permute-start.17
  69.4 4.2 %collective-permute-start.18 = (f32[16,16]{0,1:T(8,128)S(1)}, f32[16,16]{0,1:T(8,128)S(1)}, u32[]{:S(2)}, u32[]{:S(2)}) collective-permute-start(f32[16,16]{0,1:T(8,128)S(1)} %select_add_fusion), channel_id=1, source_target_pairs={{0,4},{1,5},{2,6},{3,7},{4,0},{5,1},{6,2},{7,3},{8,12},{9,13},{10,... | collective-permute-start | bytes 3080 | tf_op jit(solution)/shard_map/ppermute | solution.py:157
  73.6 0.1 fusion.16
  73.7 0.9 %collective-permute-done.16 = f32[16,16]{0,1:T(8,128)S(1)} collective-permute-done((f32[16,16]{0,1:T(8,128)S(1)}, f32[16,16]{0,1:T(8,128)S(1)}, u32[]{:S(2)}, u32[]{:S(2)}) %collective-permute-start.16) | collective-permute-done | bytes 1056 | tf_op jit(solution)/shard_map/ppermute | solution.py:157
  74.6 0.6 collective-permute-done.18
  75.2 0.7 copy.62
  75.9 0.8 %fusion = f32[16,512]{1,0:T(8,128)} fusion(f32[16,512]{1,0:T(8,128)S(1)} %fusion.16, f32[16,16]{0,1:T(8,128)S(1)} %add_multiply_fusion, f32[16,512]{1,0:T(8,128)S(1)} %copy-done.11, f32[512]{0:T(512)S(1)} %broadcast_multiply_fusion, f32[16,512]{1,0:T(8,128)S(1)} %collective-permute-done.12, f32[16,1024]{1,0:T(8,128)S(1)} %copy-done.10), kind=kOutput, calls=%fused_computation.1 | convolution fusion | flops 1605632 | bytes 166912 | tf_op jit(solution)/shard_map/dot_general | solution.py:240
  (86 shorter events, 1.6 us)
Async XLA Ops:
  0.6 72.9 %copy-start = (f32[16,512]{1,0:T(8,128)S(1)}, f32[16,512]{1,0:T(8,128)}, u32[]{:S(2)}) copy-start(f32[16,512]{1,0:T(8,128)} %param.12) | copy-start | bytes 98308
  0.6 4.6 %copy-start.1 = (bf16[192,512]{1,0:T(8,128)(2,1)S(1)}, bf16[192,512]{1,0:T(8,128)(2,1)}, u32[]{:S(2)}) copy-start(bf16[192,512]{1,0:T(8,128)(2,1)} %param.8) | copy-start | bytes 589828
  2.3 2.8 %collective-permute-start = (bf16[9]{0:T(256)(128)(2,1)S(1)}, bf16[9]{0:T(256)(128)(2,1)S(1)}, u32[]{:S(2)}, u32[]{:S(2)}) collective-permute-start(bf16[9]{0:T(256)(128)(2,1)S(1)} %pad_maximum_fusion.2), channel_id=1, source_target_pairs={{0,1},{1,0},{2,3},{3,2},{4,5},{5,4},{6,7},{7,6},{8,9},{9,8},{10,11... | collective-permute-start | bytes 62 | tf_op jit(solution)/shard_map/ppermute | solution.py:189
  5.2 14.2 %copy-start.4 = (bf16[224,512]{1,0:T(8,128)(2,1)}, bf16[224,512]{1,0:T(8,128)(2,1)S(1)}, u32[]{:S(2)}) copy-start(bf16[224,512]{1,0:T(8,128)(2,1)S(1)} %fusion.7.refs_0_) | copy-start | bytes 688132
  5.3 10.0 %collective-permute-start.1 = (bf16[224,512]{1,0:T(8,128)(2,1)S(1)}, bf16[224,512]{1,0:T(8,128)(2,1)S(1)}, u32[]{:S(2)}, u32[]{:S(2)}) collective-permute-start(bf16[224,512]{1,0:T(8,128)(2,1)S(1)} %fusion.7.refs_0_), channel_id=1, source_target_pairs={{0,4},{1,5},{2,6},{3,7},{4,8},{5,9},{6,10},{7,11},{8,12},{9,13},{1... | collective-permute-start | bytes 688136 | tf_op jit(solution)/shard_map/ppermute | solution.py:119
  9.8 9.6 %collective-permute-start.2 = (bf16[224,512]{1,0:T(8,128)(2,1)S(1)}, bf16[224,512]{1,0:T(8,128)(2,1)S(1)}, u32[]{:S(2)}, u32[]{:S(2)}) collective-permute-start(bf16[224,512]{1,0:T(8,128)(2,1)S(1)} %fusion.7.refs_0_), channel_id=1, source_target_pairs={{4,0},{5,1},{6,2},{7,3},{8,4},{9,5},{10,6},{11,7},{12,8},{13,9},{1... | collective-permute-start | bytes 688136 | tf_op jit(solution)/shard_map/ppermute | solution.py:120
  11.1 18.1 %collective-permute-start.3 = (bf16[224,512]{1,0:T(8,128)(2,1)S(1)}, bf16[224,512]{1,0:T(8,128)(2,1)S(1)}, u32[]{:S(2)}, u32[]{:S(2)}) collective-permute-start(bf16[224,512]{1,0:T(8,128)(2,1)S(1)} %fusion.7.refs_0_), channel_id=1, source_target_pairs={{0,2},{1,3},{2,0},{3,1},{4,6},{5,7},{6,4},{7,5},{8,10},{9,11},{10,... | collective-permute-start | bytes 688136 | tf_op jit(solution)/shard_map/ppermute | solution.py:121
  12.7 8.3 %collective-permute-start.11 = (bf16[224,512]{1,0:T(8,128)(2,1)S(1)}, bf16[224,512]{1,0:T(8,128)(2,1)S(1)}, u32[]{:S(2)}, u32[]{:S(2)}) collective-permute-start(bf16[224,512]{1,0:T(8,128)(2,1)S(1)} %fusion.7.refs_0_), channel_id=1, source_target_pairs={{0,1},{1,0},{2,3},{3,2},{4,5},{5,4},{6,7},{7,6},{8,9},{9,8},{10,11... | collective-permute-start | bytes 688136 | tf_op jit(solution)/shard_map/ppermute | solution.py:220
  15.3 6.9 %copy-start.2 = (bf16[224,512]{1,0:T(8,128)(2,1)}, bf16[224,512]{1,0:T(8,128)(2,1)S(1)}, u32[]{:S(2)}) copy-start(bf16[224,512]{1,0:T(8,128)(2,1)S(1)} %collective-permute-done.1.refs_1_) | copy-start | bytes 688132
  19.4 6.3 %copy-start.3 = (bf16[224,512]{1,0:T(8,128)(2,1)}, bf16[224,512]{1,0:T(8,128)(2,1)S(1)}, u32[]{:S(2)}) copy-start(bf16[224,512]{1,0:T(8,128)(2,1)S(1)} %collective-permute-done.2.refs_2_) | copy-start | bytes 688132
  19.4 28.1 %collective-permute-start.6 = (bf16[448,512]{1,0:T(8,128)(2,1)S(1)}, bf16[448,512]{1,0:T(8,128)(2,1)S(1)}, u32[]{:S(2)}, u32[]{:S(2)}) collective-permute-start(bf16[448,512]{1,0:T(8,128)(2,1)S(1)} %pad_maximum_fusion), channel_id=1, source_target_pairs={{0,2},{1,3},{2,0},{3,1},{4,6},{5,7},{6,4},{7,5},{8,10},{9,11},{10,... | collective-permute-start | bytes 1376264 | tf_op jit(solution)/shard_map/ppermute | solution.py:124
  22.2 7.6 %collective-permute-start.4 = (bf16[224,512]{1,0:T(8,128)(2,1)S(1)}, bf16[224,512]{1,0:T(8,128)(2,1)S(1)}, u32[]{:S(2)}, u32[]{:S(2)}) collective-permute-start(bf16[224,512]{1,0:T(8,128)(2,1)S(1)} %collective-permute-done.1.refs_1_), channel_id=1, source_target_pairs={{0,4},{1,5},{2,6},{3,7},{4,8},{5,9},{6,10},{7,11},{8,12},{9,13},{1... | collective-permute-start | bytes 688136 | tf_op jit(solution)/shard_map/ppermute | solution.py:122
  25.7 8.2 %collective-permute-start.5 = (bf16[224,512]{1,0:T(8,128)(2,1)S(1)}, bf16[224,512]{1,0:T(8,128)(2,1)S(1)}, u32[]{:S(2)}, u32[]{:S(2)}) collective-permute-start(bf16[224,512]{1,0:T(8,128)(2,1)S(1)} %collective-permute-done.2.refs_2_), channel_id=1, source_target_pairs={{4,0},{5,1},{6,2},{7,3},{8,4},{9,5},{10,6},{11,7},{12,8},{13,9},{1... | collective-permute-start | bytes 688136 | tf_op jit(solution)/shard_map/ppermute | solution.py:123
  29.2 4.7 %copy-start.12 = (bf16[224,512]{1,0:T(8,128)(2,1)}, bf16[224,512]{1,0:T(8,128)(2,1)S(1)}, u32[]{:S(2)}) copy-start(bf16[224,512]{1,0:T(8,128)(2,1)S(1)} %collective-permute-done.3.refs_3_) | copy-start | bytes 688132
  29.7 9.6 %copy-start.5 = (bf16[224,512]{1,0:T(8,128)(2,1)}, bf16[224,512]{1,0:T(8,128)(2,1)S(1)}, u32[]{:S(2)}) copy-start(bf16[224,512]{1,0:T(8,128)(2,1)S(1)} %collective-permute-done.4.refs_4_) | copy-start | bytes 688132
  33.9 5.4 %copy-start.6 = (bf16[224,512]{1,0:T(8,128)(2,1)}, bf16[224,512]{1,0:T(8,128)(2,1)S(1)}, u32[]{:S(2)}) copy-start(bf16[224,512]{1,0:T(8,128)(2,1)S(1)} %collective-permute-done.5.refs_5_) | copy-start | bytes 688132
  33.9 13.6 %collective-permute-start.9 = (bf16[224,512]{1,0:T(8,128)(2,1)S(1)}, bf16[224,512]{1,0:T(8,128)(2,1)S(1)}, u32[]{:S(2)}, u32[]{:S(2)}) collective-permute-start(bf16[224,512]{1,0:T(8,128)(2,1)S(1)} %broadcast_select_fusion.1), channel_id=1, source_target_pairs={{0,2},{1,3},{2,0},{3,1},{4,6},{5,7},{6,4},{7,5},{8,10},{9,11},{10,... | collective-permute-start | bytes 688136 | tf_op jit(solution)/shard_map/ppermute | solution.py:128
  34.5 7.0 %collective-permute-start.7 = (bf16[224,512]{1,0:T(8,128)(2,1)S(1)}, bf16[224,512]{1,0:T(8,128)(2,1)S(1)}, u32[]{:S(2)}, u32[]{:S(2)}) collective-permute-start(bf16[224,512]{1,0:T(8,128)(2,1)S(1)} %collective-permute-done.4.refs_4_), channel_id=1, source_target_pairs={{0,4},{1,5},{2,6},{3,7},{4,8},{5,9},{6,10},{7,11},{8,12},{9,13},{1... | collective-permute-start | bytes 688136 | tf_op jit(solution)/shard_map/ppermute | solution.py:126
  38.0 7.9 %collective-permute-start.8 = (bf16[224,512]{1,0:T(8,128)(2,1)S(1)}, bf16[224,512]{1,0:T(8,128)(2,1)S(1)}, u32[]{:S(2)}, u32[]{:S(2)}) collective-permute-start(bf16[224,512]{1,0:T(8,128)(2,1)S(1)} %collective-permute-done.5.refs_5_), channel_id=1, source_target_pairs={{4,0},{5,1},{6,2},{7,3},{8,4},{9,5},{10,6},{11,7},{12,8},{13,9},{1... | collective-permute-start | bytes 688136 | tf_op jit(solution)/shard_map/ppermute | solution.py:127
  41.5 6.1 %copy-start.7 = (bf16[224,512]{1,0:T(8,128)(2,1)}, bf16[224,512]{1,0:T(8,128)(2,1)S(1)}, u32[]{:S(2)}) copy-start(bf16[224,512]{1,0:T(8,128)(2,1)S(1)} %collective-permute-done.7.refs_7_) | copy-start | bytes 688132
  45.9 1.6 %copy-start.8 = (bf16[224,512]{1,0:T(8,128)(2,1)}, bf16[224,512]{1,0:T(8,128)(2,1)S(1)}, u32[]{:S(2)}) copy-start(bf16[224,512]{1,0:T(8,128)(2,1)S(1)} %collective-permute-done.8.refs_8_) | copy-start | bytes 688132
  45.9 6.1 %collective-permute-start.10 = (bf16[224,512]{1,0:T(8,128)(2,1)S(1)}, bf16[224,512]{1,0:T(8,128)(2,1)S(1)}, u32[]{:S(2)}, u32[]{:S(2)}) collective-permute-start(bf16[224,512]{1,0:T(8,128)(2,1)S(1)} %broadcast_select_fusion), channel_id=1, source_target_pairs={{0,2},{1,3},{2,0},{3,1},{4,6},{5,7},{6,4},{7,5},{8,10},{9,11},{10,... | collective-permute-start | bytes 688136 | tf_op jit(solution)/shard_map/ppermute | solution.py:130
  47.5 6.2 %copy-start.13 = (bf16[224,512]{1,0:T(8,128)(2,1)}, bf16[224,512]{1,0:T(8,128)(2,1)S(1)}, u32[]{:S(2)}) copy-start(bf16[224,512]{1,0:T(8,128)(2,1)S(1)} %collective-permute-done.9.refs_9_) | copy-start | bytes 688132
  47.5 6.2 %copy-start.9 = (bf16[448,512]{1,0:T(8,128)(2,1)}, bf16[448,512]{1,0:T(8,128)(2,1)S(1)}, u32[]{:S(2)}) copy-start(bf16[448,512]{1,0:T(8,128)(2,1)S(1)} %collective-permute-done.6.refs_6_) | copy-start | bytes 1376260
  52.0 1.7 %copy-start.14 = (bf16[224,512]{1,0:T(8,128)(2,1)}, bf16[224,512]{1,0:T(8,128)(2,1)S(1)}, u32[]{:S(2)}) copy-start(bf16[224,512]{1,0:T(8,128)(2,1)S(1)} %collective-permute-done.10.refs_10_) | copy-start | bytes 688132
  53.7 9.1 %copy-start.16 = (f32[512]{0:T(512)S(1)}, f32[512]{0:T(512)}, u32[]{:S(2)}) copy-start(f32[512]{0:T(512)} %param.10) | copy-start | bytes 6148
  53.7 10.3 %copy-start.11 = (f32[16,512]{1,0:T(8,128)S(1)}, f32[16,512]{1,0:T(8,128)}, u32[]{:S(2)}) copy-start(f32[16,512]{1,0:T(8,128)} %param.11) | copy-start | bytes 98308
  61.9 2.0 %copy-start.10 = (f32[16,1024]{1,0:T(8,128)S(1)}, f32[16,1024]{1,0:T(8,128)}, u32[]{:S(2)}) copy-start(f32[16,1024]{1,0:T(8,128)} %shard_map.95) | copy-start | bytes 196612
  62.8 1.2 %collective-permute-start.12 = (f32[16,512]{1,0:T(8,128)S(1)}, f32[16,512]{1,0:T(8,128)S(1)}, u32[]{:S(2)}, u32[]{:S(2)}) collective-permute-start(f32[16,512]{1,0:T(8,128)S(1)} %slice.94), channel_id=1, source_target_pairs={{0,1},{1,0},{2,3},{3,2},{4,5},{5,4},{6,7},{7,6},{8,9},{9,8},{10,11... | collective-permute-start | bytes 98312 | tf_op jit(solution)/shard_map/ppermute | solution.py:234
  64.1 3.1 %collective-permute-start.13 = (f32[16,16]{0,1:T(8,128)S(1)}, f32[16,16]{0,1:T(8,128)S(1)}, u32[]{:S(2)}, u32[]{:S(2)}) collective-permute-start(f32[16,16]{0,1:T(8,128)S(1)} %convolution_bitcast_fusion), channel_id=1, source_target_pairs={{0,3},{1,2},{2,1},{3,0},{4,7},{5,6},{6,5},{7,4},{8,11},{9,10},{10,... | collective-permute-start | bytes 3080 | tf_op jit(solution)/shard_map/ppermute | solution.py:157
  65.4 3.7 %collective-permute-start.14 = (f32[16,16]{0,1:T(8,128)S(1)}, f32[16,16]{0,1:T(8,128)S(1)}, u32[]{:S(2)}, u32[]{:S(2)}) collective-permute-start(f32[16,16]{0,1:T(8,128)S(1)} %convolution_bitcast_fusion), channel_id=1, source_target_pairs={{0,2},{1,3},{2,0},{3,1},{4,6},{5,7},{6,4},{7,5},{8,10},{9,11},{10,... | collective-permute-start | bytes 3080 | tf_op jit(solution)/shard_map/ppermute | solution.py:157
  65.9 3.2 %collective-permute-start.15 = (f32[16,16]{0,1:T(8,128)S(1)}, f32[16,16]{0,1:T(8,128)S(1)}, u32[]{:S(2)}, u32[]{:S(2)}) collective-permute-start(f32[16,16]{0,1:T(8,128)S(1)} %convolution_bitcast_fusion), channel_id=1, source_target_pairs={{0,1},{1,0},{2,3},{3,2},{4,5},{5,4},{6,7},{7,6},{8,9},{9,8},{10,11... | collective-permute-start | bytes 3080 | tf_op jit(solution)/shard_map/ppermute | solution.py:157
  66.0 7.6 %copy-start.15 = (f32[16,16]{1,0:T(8,128)S(1)}, f32[16,16]{1,0:T(8,128)}, u32[]{:S(2)}) copy-start(f32[16,16]{1,0:T(8,128)} %param.13) | copy-start | bytes 3076
  69.1 5.5 %collective-permute-start.16 = (f32[16,16]{0,1:T(8,128)S(1)}, f32[16,16]{0,1:T(8,128)S(1)}, u32[]{:S(2)}, u32[]{:S(2)}) collective-permute-start(f32[16,16]{0,1:T(8,128)S(1)} %select_add_fusion), channel_id=1, source_target_pairs={{0,12},{1,13},{2,14},{3,15},{4,8},{5,9},{6,10},{7,11},{8,4},{9,5},... | collective-permute-start | bytes 3080 | tf_op jit(solution)/shard_map/ppermute | solution.py:157
  69.2 5.4 %collective-permute-start.17 = (f32[16,16]{0,1:T(8,128)S(1)}, f32[16,16]{0,1:T(8,128)S(1)}, u32[]{:S(2)}, u32[]{:S(2)}) collective-permute-start(f32[16,16]{0,1:T(8,128)S(1)} %select_add_fusion), channel_id=1, source_target_pairs={{0,8},{1,9},{2,10},{3,11},{4,12},{5,13},{6,14},{7,15},{8,0},{9,1},... | collective-permute-start | bytes 3080 | tf_op jit(solution)/shard_map/ppermute | solution.py:157
  69.4 5.8 %collective-permute-start.18 = (f32[16,16]{0,1:T(8,128)S(1)}, f32[16,16]{0,1:T(8,128)S(1)}, u32[]{:S(2)}, u32[]{:S(2)}) collective-permute-start(f32[16,16]{0,1:T(8,128)S(1)} %select_add_fusion), channel_id=1, source_target_pairs={{0,4},{1,5},{2,6},{3,7},{4,0},{5,1},{6,2},{7,3},{8,12},{9,13},{10,... | collective-permute-start | bytes 3080 | tf_op jit(solution)/shard_map/ppermute | solution.py:157

commit v11 on v10

--- a/solution.py
+++ b/solution.py
@@ -116,26 +116,27 @@
     z = me // 4
     partner = me ^ 2
 
+    ends = (z == 0) | (z == 3)
     up1 = lax.ppermute(packed, "row", up)
     down1 = lax.ppermute(packed, "row", down)
     across1 = lax.ppermute(packed, "row", across)
     up2 = lax.ppermute(up1, "row", up)
     down2 = lax.ppermute(down1, "row", down)
-    across2 = lax.ppermute(jnp.concatenate([up1, down1]), "row", across)
-    pick2 = jnp.where(z >= 2, up2, down2)
+    across2 = lax.ppermute(jnp.where(z <= 2, down1, up1), "row", across)
     up3 = lax.ppermute(up2, "row", up)
     down3 = lax.ppermute(down2, "row", down)
-    across3 = lax.ppermute(pick2, "row", across)
-    pick3 = jnp.where(z == 3, up3, down3)
-    across4 = lax.ppermute(pick3, "row", across)
-
-    ends = (z == 0) | (z == 3)
+    across3 = lax.ppermute(jnp.where(z >= 2, up2, down2), "row", across)
+    last = jnp.where(ends, jnp.where(z == 3, up3, down3), up1)
+    across4 = lax.ppermute(last, "row", across)
+
     one = jnp.ones((), bool)
     pieces = [packed, up1, down1, across1, up2, down2, across2, up3, down3, across3, across4]
-    valid = [one, z >= 1, z <= 2, one, z >= 2, z <= 1, z >= 1, z <= 2, z == 3, z == 0, one, ends]
+    valid = [one, z >= 1, z <= 2, one, z >= 2, z <= 1, one, z == 3, z == 0, one, one]
     origin = [
-        me, me - 4, me + 4, partner, me - 8, me + 8, partner - 4, partner + 4, me - 12, me + 12,
-        jnp.where(z >= 2, partner - 8, partner + 8), jnp.where(z == 3, partner - 12, partner + 12),
+        me, me - 4, me + 4, partner, me - 8, me + 8,
+        jnp.where(z <= 2, partner + 4, partner - 4), me - 12, me + 12,
+        jnp.where(z >= 2, partner - 8, partner + 8),
+        jnp.where(ends, jnp.where(z == 3, partner - 12, partner + 12), partner - 4),
     ]
     return pieces, jnp.stack(valid), jnp.clip(jnp.stack(origin), 0, devices - 1).astype(jnp.int32)
 

time: 77.1 us -> 76.5 us (level)
  Pallas kernels: 8.21 us -> 7.4 us
    ppermute x1, waiting for transfers between devices: 4.12 us -> 0.01 us  [gather_pieces(): down1 = lax.ppermute(packed, 'row', down)]
    ppermute x3, waiting for transfers between devices: 4.4 us -> 7.22 us  [the longest x1 4.77 us: gather_pieces(): across4 = lax.ppermute(last, 'row', across)]
    ppermute x1, waiting for transfers between devices: 2.46 us -> 0.01 us  [gather_pieces(): up1 = lax.ppermute(packed, 'row', up)]
    ppermute x1, waiting for transfers between devices: 0.01 us -> 1.45 us  [shards(): twin_piece = lax.ppermute(packed, 'row', twin)]
    ppermute x1, waiting for transfers between devices: 0.48 us -> 1.6 us  [gather_pieces(): up2 = lax.ppermute(up1, 'row', up)]
    ppermute x1, starting transfers between devices: 3.47 us -> 4.56 us  [gather_pieces(): up2 = lax.ppermute(up1, 'row', up)]
    ppermute x3, starting transfers between devices: 3.74 us -> 2.84 us  [the longest x1 1.39 us: gather_pieces(): across4 = lax.ppermute(last, 'row', across)]
    ppermute x6, waiting for transfers between devices: 4.56 us -> 5.44 us  [sum_over_rows(): lax.ppermute(value, 'row', [(i, i ^ m << shift) for i in range(devices)])]
  transfers between devices with their start and end apart: 19 -> 19, of which waited for: 12 -> 13; matrix products, arithmetic and copies ran while one was open for 8% -> 8% of each run, Pallas kernels for 0% -> 0%
where the time goes in v11:
time: 76.5 us; the launch traced here: 75.7 us
  starting transfers between devices  27.7 us (36%)
  waiting for transfers between devices  27.6 us (36%)
  Pallas kernels  7.4 us (10%)
  local copies, waits for them, and re-layouts  6.62 us (9%)
  other arithmetic  3.68 us (5%)
  between operations  1.62 us (2%)
  matrix products  1.07 us (1%)
    pallas_call x1, Pallas kernels, list_product(): pl.pallas_call(functools.partial(list_kernel, width, rows, counts), in_sp...  7.4 us
    ppermute x6, starting transfers between devices, sum_over_rows(): lax.ppermute(value, 'row', [(i, i ^ m << shift) for i in range(devices)])  6.34 us
    ppermute x6, waiting for transfers between devices, sum_over_rows(): lax.ppermute(value, 'row', [(i, i ^ m << shift) for i in range(devices)])  5.44 us
    ppermute x1, waiting for transfers between devices, gather_pieces(): across4 = lax.ppermute(last, 'row', across)  4.77 us
    ppermute x1, starting transfers between devices, gather_pieces(): up2 = lax.ppermute(up1, 'row', up)  4.56 us
    ppermute x1, starting transfers between devices, gather_pieces(): up1 = lax.ppermute(packed, 'row', up)  4.54 us
    ppermute x1, waiting for transfers between devices, gather_pieces(): down3 = lax.ppermute(down2, 'row', down)  4.4 us
    ppermute x1, waiting for transfers between devices, gather_pieces(): down2 = lax.ppermute(down1, 'row', down)  4.16 us
  transfers between devices with their start and end apart: 19, of which 13 were waited for; matrix products, arithmetic and copies ran while one was open for 8% of the time, Pallas kernels for 0%

profile of v11, /device:TPU:0, one launch (start us, length us, event | category | flops | bytes accessed | tf_op | source)
XLA Modules:
  0.0 75.7 jit_solution(13640900758643101743)
XLA Ops:
  0.7 0.7 convert.8
  1.4 0.1 copy.48
  2.3 0.5 collective-permute-start
  2.8 0.7 broadcast_in_dim.6
  3.5 0.7 concatenate.40
  4.2 0.8 %multiply_convert_fusion = bf16[16,512]{1,0:T(8,128)(2,1)S(1)} fusion(f32[16,512]{1,0:T(8,128)} %param.11, f32[512]{0:T(512)} %param.10), kind=kLoop, calls=%fused_computation.20 | loop fusion | flops 16384 | bytes 51200 | tf_op jit(solution)/shard_map/convert_element_type | solution.py:186
  5.0 0.1 stack.75
  5.3 4.5 %collective-permute-start.1 = (bf16[224,512]{1,0:T(8,128)(2,1)S(1)}, bf16[224,512]{1,0:T(8,128)(2,1)S(1)}, u32[]{:S(2)}, u32[]{:S(2)}) collective-permute-start(bf16[224,512]{1,0:T(8,128)(2,1)S(1)} %fusion.7.refs_0_), channel_id=1, source_target_pairs={{0,4},{1,5},{2,6},{3,7},{4,8},{5,9},{6,10},{7,11},{8,12},{9,13},{1... | collective-permute-start | bytes 688136 | tf_op jit(solution)/shard_map/ppermute | solution.py:120
  9.8 1.3 %collective-permute-start.2 = (bf16[224,512]{1,0:T(8,128)(2,1)S(1)}, bf16[224,512]{1,0:T(8,128)(2,1)S(1)}, u32[]{:S(2)}, u32[]{:S(2)}) collective-permute-start(bf16[224,512]{1,0:T(8,128)(2,1)S(1)} %fusion.7.refs_0_), channel_id=1, source_target_pairs={{4,0},{5,1},{6,2},{7,3},{8,4},{9,5},{10,6},{11,7},{12,8},{13,9},{1... | collective-permute-start | bytes 688136 | tf_op jit(solution)/shard_map/ppermute | solution.py:121
  11.1 1.6 %collective-permute-start.3 = (bf16[224,512]{1,0:T(8,128)(2,1)S(1)}, bf16[224,512]{1,0:T(8,128)(2,1)S(1)}, u32[]{:S(2)}, u32[]{:S(2)}) collective-permute-start(bf16[224,512]{1,0:T(8,128)(2,1)S(1)} %fusion.7.refs_0_), channel_id=1, source_target_pairs={{0,2},{1,3},{2,0},{3,1},{4,6},{5,7},{6,4},{7,5},{8,10},{9,11},{10,... | collective-permute-start | bytes 688136 | tf_op jit(solution)/shard_map/ppermute | solution.py:122
  12.7 1.5 %collective-permute-done.11 = bf16[224,512]{1,0:T(8,128)(2,1)S(1)} collective-permute-done((bf16[224,512]{1,0:T(8,128)(2,1)S(1)}, bf16[224,512]{1,0:T(8,128)(2,1)S(1)}, u32[]{:S(2)}, u32[]{:S(2)}) %collective-permute-start.11) | collective-permute-done | bytes 229408 | tf_op jit(solution)/shard_map/ppermute | solution.py:221
  14.2 0.2 copy.53
  14.4 0.9 %broadcast_divide_fusion.ro_ref = f32[1024,1]{1,0:T(8,128)} fusion(f32[1024,1]{1,0:T(8,128)S(1)} %copy.53), kind=kLoop, calls=%fused_computation.11 | loop fusion | flops 1024 | bytes 8192 | tf_op jit(solution)/shard_map/div | solution.py:228
  15.5 4.6 %collective-permute-start.4 = (bf16[224,512]{1,0:T(8,128)(2,1)S(1)}, bf16[224,512]{1,0:T(8,128)(2,1)S(1)}, u32[]{:S(2)}, u32[]{:S(2)}) collective-permute-start(bf16[224,512]{1,0:T(8,128)(2,1)S(1)} %collective-permute-done.1.refs_1_), channel_id=1, source_target_pairs={{0,4},{1,5},{2,6},{3,7},{4,8},{5,9},{6,10},{7,11},{8,12},{9,13},{1... | collective-permute-start | bytes 688136 | tf_op jit(solution)/shard_map/ppermute | solution.py:123
  20.1 1.3 %collective-permute-start.5 = (bf16[224,512]{1,0:T(8,128)(2,1)S(1)}, bf16[224,512]{1,0:T(8,128)(2,1)S(1)}, u32[]{:S(2)}, u32[]{:S(2)}) collective-permute-start(bf16[224,512]{1,0:T(8,128)(2,1)S(1)} %collective-permute-done.2.refs_2_), channel_id=1, source_target_pairs={{4,0},{5,1},{6,2},{7,3},{8,4},{9,5},{10,6},{11,7},{12,8},{13,9},{1... | collective-permute-start | bytes 688136 | tf_op jit(solution)/shard_map/ppermute | solution.py:124
  21.5 1.0 %copy.54.xo_ref = bf16[1024,192]{1,0:T(8,128)(2,1)} copy(bf16[1024,192]{0,1:T(8,128)(2,1)S(1)} %multiply_bitcast_fusion) | data formatting | bytes 786432 | tf_op jit(solution)/shard_map/transpose | solution.py:229
  22.5 1.0 %copy.55.no_ref = f32[1024,1]{1,0:T(8,128)} copy(f32[1024,1]{0,1:T(1,128)S(1)} %bitcast.80) | data formatting | bytes 8192 | tf_op jit(solution)/shard_map/broadcast_in_dim | solution.py:226
  23.5 1.6 %collective-permute-done.4.refs_4_ = bf16[224,512]{1,0:T(8,128)(2,1)S(1)} collective-permute-done((bf16[224,512]{1,0:T(8,128)(2,1)S(1)}, bf16[224,512]{1,0:T(8,128)(2,1)S(1)}, u32[]{:S(2)}, u32[]{:S(2)}) %collective-permute-start.4) | collective-permute-done | bytes 229408 | tf_op jit(solution)/shard_map/ppermute | solution.py:123
  25.2 4.2 %collective-permute-done.5.refs_5_ = bf16[224,512]{1,0:T(8,128)(2,1)S(1)} collective-permute-done((bf16[224,512]{1,0:T(8,128)(2,1)S(1)}, bf16[224,512]{1,0:T(8,128)(2,1)S(1)}, u32[]{:S(2)}, u32[]{:S(2)}) %collective-permute-start.5) | collective-permute-done | bytes 229408 | tf_op jit(solution)/shard_map/ppermute | solution.py:124
  29.4 0.8 collective-permute-start.9
  30.1 3.5 %collective-permute-start.7 = (bf16[224,512]{1,0:T(8,128)(2,1)S(1)}, bf16[224,512]{1,0:T(8,128)(2,1)S(1)}, u32[]{:S(2)}, u32[]{:S(2)}) collective-permute-start(bf16[224,512]{1,0:T(8,128)(2,1)S(1)} %collective-permute-done.4.refs_4_), channel_id=1, source_target_pairs={{0,4},{1,5},{2,6},{3,7},{4,8},{5,9},{6,10},{7,11},{8,12},{9,13},{1... | collective-permute-start | bytes 688136 | tf_op jit(solution)/shard_map/ppermute | solution.py:126
  33.6 1.3 %collective-permute-start.8 = (bf16[224,512]{1,0:T(8,128)(2,1)S(1)}, bf16[224,512]{1,0:T(8,128)(2,1)S(1)}, u32[]{:S(2)}, u32[]{:S(2)}) collective-permute-start(bf16[224,512]{1,0:T(8,128)(2,1)S(1)} %collective-permute-done.5.refs_5_), channel_id=1, source_target_pairs={{4,0},{5,1},{6,2},{7,3},{8,4},{9,5},{10,6},{11,7},{12,8},{13,9},{1... | collective-permute-start | bytes 688136 | tf_op jit(solution)/shard_map/ppermute | solution.py:127
  34.9 2.2 %collective-permute-done.7.refs_7_ = bf16[224,512]{1,0:T(8,128)(2,1)S(1)} collective-permute-done((bf16[224,512]{1,0:T(8,128)(2,1)S(1)}, bf16[224,512]{1,0:T(8,128)(2,1)S(1)}, u32[]{:S(2)}, u32[]{:S(2)}) %collective-permute-start.7) | collective-permute-done | bytes 229408 | tf_op jit(solution)/shard_map/ppermute | solution.py:126
  37.1 4.4 %collective-permute-done.8.refs_8_ = bf16[224,512]{1,0:T(8,128)(2,1)S(1)} collective-permute-done((bf16[224,512]{1,0:T(8,128)(2,1)S(1)}, bf16[224,512]{1,0:T(8,128)(2,1)S(1)}, u32[]{:S(2)}, u32[]{:S(2)}) %collective-permute-start.8) | collective-permute-done | bytes 229408 | tf_op jit(solution)/shard_map/ppermute | solution.py:127
  41.6 1.4 %collective-permute-start.10 = (bf16[224,512]{1,0:T(8,128)(2,1)S(1)}, bf16[224,512]{1,0:T(8,128)(2,1)S(1)}, u32[]{:S(2)}, u32[]{:S(2)}) collective-permute-start(bf16[224,512]{1,0:T(8,128)(2,1)S(1)} %get-tuple-element.14), channel_id=1, source_target_pairs={{0,2},{1,3},{2,0},{3,1},{4,6},{5,7},{6,4},{7,5},{8,10},{9,11},{10,... | collective-permute-start | bytes 688136 | tf_op jit(solution)/shard_map/ppermute | solution.py:130
  43.0 0.7 collective-permute-start.6
  43.7 4.8 %collective-permute-done.10.refs_10_ = bf16[224,512]{1,0:T(8,128)(2,1)S(1)} collective-permute-done((bf16[224,512]{1,0:T(8,128)(2,1)S(1)}, bf16[224,512]{1,0:T(8,128)(2,1)S(1)}, u32[]{:S(2)}, u32[]{:S(2)}) %collective-permute-start.10) | collective-permute-done | bytes 229408 | tf_op jit(solution)/shard_map/ppermute | solution.py:130
  48.5 2.4 %collective-permute-done.6.refs_6_ = bf16[224,512]{1,0:T(8,128)(2,1)S(1)} collective-permute-done((bf16[224,512]{1,0:T(8,128)(2,1)S(1)}, bf16[224,512]{1,0:T(8,128)(2,1)S(1)}, u32[]{:S(2)}, u32[]{:S(2)}) %collective-permute-start.6) | collective-permute-done | bytes 229408 | tf_op jit(solution)/shard_map/ppermute | solution.py:125
  51.1 0.2 slice_reduce_fusion
  52.0 0.2 and_reduce_fusion
  52.2 0.5 and_convert_fusion.flag_ref
  52.7 7.4 %shard_map.95 = f32[16,1024]{1,0:T(8,128)} custom-call(s32[11]{0:T(128)} %and_convert_fusion.flag_ref, bf16[1024,192]{1,0:T(8,128)(2,1)} %copy.54.xo_ref, f32[1024,1]{1,0:T(8,128)} %copy.55.no_ref, f32[1024,1]{1,0:T(8,128)} %broadcast_divide_fusion.ro_ref, bf16[224,512]{1,0:T(8,128)(2,1)} %copy-done.2, bf16[224,512]{1,0:T(8,128)(2,1)} %copy-done.5, ...), custom_call_target="tpu_custom_call" | custom-call | tf_op jit(solution)/shard_map/pallas_call | solution.py:73
  60.1 0.8 %slice.94 = f32[16,512]{1,0:T(8,128)S(1)} slice(f32[16,1024]{1,0:T(8,128)} %shard_map.95), slice={[0:16], [512:1024]} | slice | bytes 65536 | tf_op jit(solution)/shard_map/slice | solution.py:235
  60.9 1.2 %collective-permute-done.12 = f32[16,512]{1,0:T(8,128)S(1)} collective-permute-done((f32[16,512]{1,0:T(8,128)S(1)}, f32[16,512]{1,0:T(8,128)S(1)}, u32[]{:S(2)}, u32[]{:S(2)}) %collective-permute-start.12) | collective-permute-done | bytes 32800 | tf_op jit(solution)/shard_map/ppermute | solution.py:235
  62.1 0.1 convolution_bitcast_fusion
  62.3 0.7 collective-permute-start.13
  63.0 1.1 %collective-permute-start.14 = (f32[16,16]{0,1:T(8,128)S(1)}, f32[16,16]{0,1:T(8,128)S(1)}, u32[]{:S(2)}, u32[]{:S(2)}) collective-permute-start(f32[16,16]{0,1:T(8,128)S(1)} %convolution_bitcast_fusion), channel_id=1, source_target_pairs={{0,2},{1,3},{2,0},{3,1},{4,6},{5,7},{6,4},{7,5},{8,10},{9,11},{10,... | collective-permute-start | bytes 3080 | tf_op jit(solution)/shard_map/ppermute | solution.py:158
  64.2 1.2 %collective-permute-done.13 = f32[16,16]{0,1:T(8,128)S(1)} collective-permute-done((f32[16,16]{0,1:T(8,128)S(1)}, f32[16,16]{0,1:T(8,128)S(1)}, u32[]{:S(2)}, u32[]{:S(2)}) %collective-permute-start.13) | collective-permute-done | bytes 1056 | tf_op jit(solution)/shard_map/ppermute | solution.py:158
  65.4 1.3 %collective-permute-done.14 = f32[16,16]{0,1:T(8,128)S(1)} collective-permute-done((f32[16,16]{0,1:T(8,128)S(1)}, f32[16,16]{0,1:T(8,128)S(1)}, u32[]{:S(2)}, u32[]{:S(2)}) %collective-permute-start.14) | collective-permute-done | bytes 1056 | tf_op jit(solution)/shard_map/ppermute | solution.py:158
  66.7 1.4 %collective-permute-start.16 = (f32[16,16]{0,1:T(8,128)S(1)}, f32[16,16]{0,1:T(8,128)S(1)}, u32[]{:S(2)}, u32[]{:S(2)}) collective-permute-start(f32[16,16]{0,1:T(8,128)S(1)} %select_add_fusion), channel_id=1, source_target_pairs={{0,12},{1,13},{2,14},{3,15},{4,8},{5,9},{6,10},{7,11},{8,4},{9,5},... | collective-permute-start | bytes 3080 | tf_op jit(solution)/shard_map/ppermute | solution.py:158
  68.1 2.5 %collective-permute-start.17 = (f32[16,16]{0,1:T(8,128)S(1)}, f32[16,16]{0,1:T(8,128)S(1)}, u32[]{:S(2)}, u32[]{:S(2)}) collective-permute-start(f32[16,16]{0,1:T(8,128)S(1)} %select_add_fusion), channel_id=1, source_target_pairs={{0,8},{1,9},{2,10},{3,11},{4,12},{5,13},{6,14},{7,15},{8,0},{9,1},... | collective-permute-start | bytes 3080 | tf_op jit(solution)/shard_map/ppermute | solution.py:158
  70.6 0.6 collective-permute-start.18
  71.2 0.1 fusion.16
  71.3 0.9 %collective-permute-done.16 = f32[16,16]{0,1:T(8,128)S(1)} collective-permute-done((f32[16,16]{0,1:T(8,128)S(1)}, f32[16,16]{0,1:T(8,128)S(1)}, u32[]{:S(2)}, u32[]{:S(2)}) %collective-permute-start.16) | collective-permute-done | bytes 1056 | tf_op jit(solution)/shard_map/ppermute | solution.py:158
  72.2 0.4 collective-permute-done.17
  72.7 1.6 %collective-permute-done.18 = f32[16,16]{0,1:T(8,128)S(1)} collective-permute-done((f32[16,16]{0,1:T(8,128)S(1)}, f32[16,16]{0,1:T(8,128)S(1)}, u32[]{:S(2)}, u32[]{:S(2)}) %collective-permute-start.18) | collective-permute-done | bytes 1056 | tf_op jit(solution)/shard_map/ppermute | solution.py:158
  74.3 0.7 copy.56
  74.9 0.8 %fusion = f32[16,512]{1,0:T(8,128)} fusion(f32[16,512]{1,0:T(8,128)S(1)} %fusion.16, f32[16,16]{0,1:T(8,128)S(1)} %add_multiply_fusion, f32[16,512]{1,0:T(8,128)S(1)} %copy-done.10, f32[512]{0:T(512)S(1)} %broadcast_multiply_fusion, f32[16,512]{1,0:T(8,128)S(1)} %collective-permute-done.12, f32[16,1024]{1,0:T(8,128)S(1)} %copy-done.9), kind=kOutput, calls=%fused_computation.1 | convolution fusion | flops 1605632 | bytes 166912 | tf_op jit(solution)/shard_map/dot_general | solution.py:241
  (85 shorter events, 1.7 us)
Async XLA Ops:
  0.6 70.5 %copy-start = (f32[16,512]{1,0:T(8,128)S(1)}, f32[16,512]{1,0:T(8,128)}, u32[]{:S(2)}) copy-start(f32[16,512]{1,0:T(8,128)} %param.12) | copy-start | bytes 98308
  0.6 4.6 %copy-start.1 = (bf16[192,512]{1,0:T(8,128)(2,1)S(1)}, bf16[192,512]{1,0:T(8,128)(2,1)}, u32[]{:S(2)}) copy-start(bf16[192,512]{1,0:T(8,128)(2,1)} %param.8) | copy-start | bytes 589828
  2.3 2.8 %collective-permute-start = (bf16[9]{0:T(256)(128)(2,1)S(1)}, bf16[9]{0:T(256)(128)(2,1)S(1)}, u32[]{:S(2)}, u32[]{:S(2)}) collective-permute-start(bf16[9]{0:T(256)(128)(2,1)S(1)} %pad_maximum_fusion.1), channel_id=1, source_target_pairs={{0,1},{1,0},{2,3},{3,2},{4,5},{5,4},{6,7},{7,6},{8,9},{9,8},{10,11... | collective-permute-start | bytes 62 | tf_op jit(solution)/shard_map/ppermute | solution.py:190
  5.2 8.9 %copy-start.2 = (bf16[224,512]{1,0:T(8,128)(2,1)}, bf16[224,512]{1,0:T(8,128)(2,1)S(1)}, u32[]{:S(2)}) copy-start(bf16[224,512]{1,0:T(8,128)(2,1)S(1)} %fusion.7.refs_0_) | copy-start | bytes 688132
  5.3 10.2 %collective-permute-start.1 = (bf16[224,512]{1,0:T(8,128)(2,1)S(1)}, bf16[224,512]{1,0:T(8,128)(2,1)S(1)}, u32[]{:S(2)}, u32[]{:S(2)}) collective-permute-start(bf16[224,512]{1,0:T(8,128)(2,1)S(1)} %fusion.7.refs_0_), channel_id=1, source_target_pairs={{0,4},{1,5},{2,6},{3,7},{4,8},{5,9},{6,10},{7,11},{8,12},{9,13},{1... | collective-permute-start | bytes 688136 | tf_op jit(solution)/shard_map/ppermute | solution.py:120
  9.8 10.2 %collective-permute-start.2 = (bf16[224,512]{1,0:T(8,128)(2,1)S(1)}, bf16[224,512]{1,0:T(8,128)(2,1)S(1)}, u32[]{:S(2)}, u32[]{:S(2)}) collective-permute-start(bf16[224,512]{1,0:T(8,128)(2,1)S(1)} %fusion.7.refs_0_), channel_id=1, source_target_pairs={{4,0},{5,1},{6,2},{7,3},{8,4},{9,5},{10,6},{11,7},{12,8},{13,9},{1... | collective-permute-start | bytes 688136 | tf_op jit(solution)/shard_map/ppermute | solution.py:121
  11.1 12.4 %collective-permute-start.3 = (bf16[224,512]{1,0:T(8,128)(2,1)S(1)}, bf16[224,512]{1,0:T(8,128)(2,1)S(1)}, u32[]{:S(2)}, u32[]{:S(2)}) collective-permute-start(bf16[224,512]{1,0:T(8,128)(2,1)S(1)} %fusion.7.refs_0_), channel_id=1, source_target_pairs={{0,2},{1,3},{2,0},{3,1},{4,6},{5,7},{6,4},{7,5},{8,10},{9,11},{10,... | collective-permute-start | bytes 688136 | tf_op jit(solution)/shard_map/ppermute | solution.py:122
  12.7 1.5 %collective-permute-start.11 = (bf16[224,512]{1,0:T(8,128)(2,1)S(1)}, bf16[224,512]{1,0:T(8,128)(2,1)S(1)}, u32[]{:S(2)}, u32[]{:S(2)}) collective-permute-start(bf16[224,512]{1,0:T(8,128)(2,1)S(1)} %fusion.7.refs_0_), channel_id=1, source_target_pairs={{0,1},{1,0},{2,3},{3,2},{4,5},{5,4},{6,7},{7,6},{8,9},{9,8},{10,11... | collective-permute-start | bytes 688136 | tf_op jit(solution)/shard_map/ppermute | solution.py:221
  15.4 26.1 %copy-start.5 = (bf16[224,512]{1,0:T(8,128)(2,1)}, bf16[224,512]{1,0:T(8,128)(2,1)S(1)}, u32[]{:S(2)}) copy-start(bf16[224,512]{1,0:T(8,128)(2,1)S(1)} %collective-permute-done.1.refs_1_) | copy-start | bytes 688132
  15.5 9.7 %collective-permute-start.4 = (bf16[224,512]{1,0:T(8,128)(2,1)S(1)}, bf16[224,512]{1,0:T(8,128)(2,1)S(1)}, u32[]{:S(2)}, u32[]{:S(2)}) collective-permute-start(bf16[224,512]{1,0:T(8,128)(2,1)S(1)} %collective-permute-done.1.refs_1_), channel_id=1, source_target_pairs={{0,4},{1,5},{2,6},{3,7},{4,8},{5,9},{6,10},{7,11},{8,12},{9,13},{1... | collective-permute-start | bytes 688136 | tf_op jit(solution)/shard_map/ppermute | solution.py:123
  20.0 21.5 %copy-start.6 = (bf16[224,512]{1,0:T(8,128)(2,1)}, bf16[224,512]{1,0:T(8,128)(2,1)S(1)}, u32[]{:S(2)}) copy-start(bf16[224,512]{1,0:T(8,128)(2,1)S(1)} %collective-permute-done.2.refs_2_) | copy-start | bytes 688132
  20.1 9.3 %collective-permute-start.5 = (bf16[224,512]{1,0:T(8,128)(2,1)S(1)}, bf16[224,512]{1,0:T(8,128)(2,1)S(1)}, u32[]{:S(2)}, u32[]{:S(2)}) collective-permute-start(bf16[224,512]{1,0:T(8,128)(2,1)S(1)} %collective-permute-done.2.refs_2_), channel_id=1, source_target_pairs={{4,0},{5,1},{6,2},{7,3},{8,4},{9,5},{10,6},{11,7},{12,8},{13,9},{1... | collective-permute-start | bytes 688136 | tf_op jit(solution)/shard_map/ppermute | solution.py:124
  23.5 5.8 %copy-start.11 = (bf16[224,512]{1,0:T(8,128)(2,1)}, bf16[224,512]{1,0:T(8,128)(2,1)S(1)}, u32[]{:S(2)}) copy-start(bf16[224,512]{1,0:T(8,128)(2,1)S(1)} %collective-permute-done.3.refs_3_) | copy-start | bytes 688132
  25.2 9.8 %copy-start.3 = (bf16[224,512]{1,0:T(8,128)(2,1)}, bf16[224,512]{1,0:T(8,128)(2,1)S(1)}, u32[]{:S(2)}) copy-start(bf16[224,512]{1,0:T(8,128)(2,1)S(1)} %collective-permute-done.4.refs_4_) | copy-start | bytes 688132
  29.3 5.6 %copy-start.4 = (bf16[224,512]{1,0:T(8,128)(2,1)}, bf16[224,512]{1,0:T(8,128)(2,1)S(1)}, u32[]{:S(2)}) copy-start(bf16[224,512]{1,0:T(8,128)(2,1)S(1)} %collective-permute-done.5.refs_5_) | copy-start | bytes 688132
  29.4 14.3 %collective-permute-start.9 = (bf16[224,512]{1,0:T(8,128)(2,1)S(1)}, bf16[224,512]{1,0:T(8,128)(2,1)S(1)}, u32[]{:S(2)}, u32[]{:S(2)}) collective-permute-start(bf16[224,512]{1,0:T(8,128)(2,1)S(1)} %broadcast_select_fusion), channel_id=1, source_target_pairs={{0,2},{1,3},{2,0},{3,1},{4,6},{5,7},{6,4},{7,5},{8,10},{9,11},{10,... | collective-permute-start | bytes 688136 | tf_op jit(solution)/shard_map/ppermute | solution.py:128
  30.1 7.0 %collective-permute-start.7 = (bf16[224,512]{1,0:T(8,128)(2,1)S(1)}, bf16[224,512]{1,0:T(8,128)(2,1)S(1)}, u32[]{:S(2)}, u32[]{:S(2)}) collective-permute-start(bf16[224,512]{1,0:T(8,128)(2,1)S(1)} %collective-permute-done.4.refs_4_), channel_id=1, source_target_pairs={{0,4},{1,5},{2,6},{3,7},{4,8},{5,9},{6,10},{7,11},{8,12},{9,13},{1... | collective-permute-start | bytes 688136 | tf_op jit(solution)/shard_map/ppermute | solution.py:126
  33.6 7.9 %collective-permute-start.8 = (bf16[224,512]{1,0:T(8,128)(2,1)S(1)}, bf16[224,512]{1,0:T(8,128)(2,1)S(1)}, u32[]{:S(2)}, u32[]{:S(2)}) collective-permute-start(bf16[224,512]{1,0:T(8,128)(2,1)S(1)} %collective-permute-done.5.refs_5_), channel_id=1, source_target_pairs={{4,0},{5,1},{6,2},{7,3},{8,4},{9,5},{10,6},{11,7},{12,8},{13,9},{1... | collective-permute-start | bytes 688136 | tf_op jit(solution)/shard_map/ppermute | solution.py:127
  37.1 6.6 %copy-start.7 = (bf16[224,512]{1,0:T(8,128)(2,1)}, bf16[224,512]{1,0:T(8,128)(2,1)S(1)}, u32[]{:S(2)}) copy-start(bf16[224,512]{1,0:T(8,128)(2,1)S(1)} %collective-permute-done.7.refs_7_) | copy-start | bytes 688132
  41.5 2.2 %copy-start.8 = (bf16[224,512]{1,0:T(8,128)(2,1)}, bf16[224,512]{1,0:T(8,128)(2,1)S(1)}, u32[]{:S(2)}) copy-start(bf16[224,512]{1,0:T(8,128)(2,1)S(1)} %collective-permute-done.8.refs_8_) | copy-start | bytes 688132
  41.6 6.9 %collective-permute-start.10 = (bf16[224,512]{1,0:T(8,128)(2,1)S(1)}, bf16[224,512]{1,0:T(8,128)(2,1)S(1)}, u32[]{:S(2)}, u32[]{:S(2)}) collective-permute-start(bf16[224,512]{1,0:T(8,128)(2,1)S(1)} %get-tuple-element.14), channel_id=1, source_target_pairs={{0,2},{1,3},{2,0},{3,1},{4,6},{5,7},{6,4},{7,5},{8,10},{9,11},{10,... | collective-permute-start | bytes 688136 | tf_op jit(solution)/shard_map/ppermute | solution.py:130
  43.0 8.0 %collective-permute-start.6 = (bf16[224,512]{1,0:T(8,128)(2,1)S(1)}, bf16[224,512]{1,0:T(8,128)(2,1)S(1)}, u32[]{:S(2)}, u32[]{:S(2)}) collective-permute-start(bf16[224,512]{1,0:T(8,128)(2,1)S(1)} %get-tuple-element.15), channel_id=1, source_target_pairs={{0,2},{1,3},{2,0},{3,1},{4,6},{5,7},{6,4},{7,5},{8,10},{9,11},{10,... | collective-permute-start | bytes 688136 | tf_op jit(solution)/shard_map/ppermute | solution.py:125
  43.7 9.0 %copy-start.12 = (bf16[224,512]{1,0:T(8,128)(2,1)}, bf16[224,512]{1,0:T(8,128)(2,1)S(1)}, u32[]{:S(2)}) copy-start(bf16[224,512]{1,0:T(8,128)(2,1)S(1)} %collective-permute-done.9.refs_9_) | copy-start | bytes 688132
  48.5 4.2 %copy-start.13 = (bf16[224,512]{1,0:T(8,128)(2,1)}, bf16[224,512]{1,0:T(8,128)(2,1)S(1)}, u32[]{:S(2)}) copy-start(bf16[224,512]{1,0:T(8,128)(2,1)S(1)} %collective-permute-done.10.refs_10_) | copy-start | bytes 688132
  50.9 1.7 %copy-start.14 = (bf16[224,512]{1,0:T(8,128)(2,1)}, bf16[224,512]{1,0:T(8,128)(2,1)S(1)}, u32[]{:S(2)}) copy-start(bf16[224,512]{1,0:T(8,128)(2,1)S(1)} %collective-permute-done.6.refs_6_) | copy-start | bytes 688132
  52.7 8.3 %copy-start.16 = (f32[512]{0:T(512)S(1)}, f32[512]{0:T(512)}, u32[]{:S(2)}) copy-start(f32[512]{0:T(512)} %param.10) | copy-start | bytes 6148
  52.7 9.5 %copy-start.10 = (f32[16,512]{1,0:T(8,128)S(1)}, f32[16,512]{1,0:T(8,128)}, u32[]{:S(2)}) copy-start(f32[16,512]{1,0:T(8,128)} %param.11) | copy-start | bytes 98308
  60.1 2.0 %copy-start.9 = (f32[16,1024]{1,0:T(8,128)S(1)}, f32[16,1024]{1,0:T(8,128)}, u32[]{:S(2)}) copy-start(f32[16,1024]{1,0:T(8,128)} %shard_map.95) | copy-start | bytes 196612
  60.9 1.2 %collective-permute-start.12 = (f32[16,512]{1,0:T(8,128)S(1)}, f32[16,512]{1,0:T(8,128)S(1)}, u32[]{:S(2)}, u32[]{:S(2)}) collective-permute-start(f32[16,512]{1,0:T(8,128)S(1)} %slice.94), channel_id=1, source_target_pairs={{0,1},{1,0},{2,3},{3,2},{4,5},{5,4},{6,7},{7,6},{8,9},{9,8},{10,11... | collective-permute-start | bytes 98312 | tf_op jit(solution)/shard_map/ppermute | solution.py:235
  62.3 3.1 %collective-permute-start.13 = (f32[16,16]{0,1:T(8,128)S(1)}, f32[16,16]{0,1:T(8,128)S(1)}, u32[]{:S(2)}, u32[]{:S(2)}) collective-permute-start(f32[16,16]{0,1:T(8,128)S(1)} %convolution_bitcast_fusion), channel_id=1, source_target_pairs={{0,3},{1,2},{2,1},{3,0},{4,7},{5,6},{6,5},{7,4},{8,11},{9,10},{10,... | collective-permute-start | bytes 3080 | tf_op jit(solution)/shard_map/ppermute | solution.py:158
  63.0 3.7 %collective-permute-start.14 = (f32[16,16]{0,1:T(8,128)S(1)}, f32[16,16]{0,1:T(8,128)S(1)}, u32[]{:S(2)}, u32[]{:S(2)}) collective-permute-start(f32[16,16]{0,1:T(8,128)S(1)} %convolution_bitcast_fusion), channel_id=1, source_target_pairs={{0,2},{1,3},{2,0},{3,1},{4,6},{5,7},{6,4},{7,5},{8,10},{9,11},{10,... | collective-permute-start | bytes 3080 | tf_op jit(solution)/shard_map/ppermute | solution.py:158
  64.1 2.6 %collective-permute-start.15 = (f32[16,16]{0,1:T(8,128)S(1)}, f32[16,16]{0,1:T(8,128)S(1)}, u32[]{:S(2)}, u32[]{:S(2)}) collective-permute-start(f32[16,16]{0,1:T(8,128)S(1)} %convolution_bitcast_fusion), channel_id=1, source_target_pairs={{0,1},{1,0},{2,3},{3,2},{4,5},{5,4},{6,7},{7,6},{8,9},{9,8},{10,11... | collective-permute-start | bytes 3080 | tf_op jit(solution)/shard_map/ppermute | solution.py:158
  64.2 7.0 %copy-start.15 = (f32[16,16]{1,0:T(8,128)S(1)}, f32[16,16]{1,0:T(8,128)}, u32[]{:S(2)}) copy-start(f32[16,16]{1,0:T(8,128)} %param.13) | copy-start | bytes 3076
  66.7 5.5 %collective-permute-start.16 = (f32[16,16]{0,1:T(8,128)S(1)}, f32[16,16]{0,1:T(8,128)S(1)}, u32[]{:S(2)}, u32[]{:S(2)}) collective-permute-start(f32[16,16]{0,1:T(8,128)S(1)} %select_add_fusion), channel_id=1, source_target_pairs={{0,12},{1,13},{2,14},{3,15},{4,8},{5,9},{6,10},{7,11},{8,4},{9,5},... | collective-permute-start | bytes 3080 | tf_op jit(solution)/shard_map/ppermute | solution.py:158
  68.1 4.5 %collective-permute-start.17 = (f32[16,16]{0,1:T(8,128)S(1)}, f32[16,16]{0,1:T(8,128)S(1)}, u32[]{:S(2)}, u32[]{:S(2)}) collective-permute-start(f32[16,16]{0,1:T(8,128)S(1)} %select_add_fusion), channel_id=1, source_target_pairs={{0,8},{1,9},{2,10},{3,11},{4,12},{5,13},{6,14},{7,15},{8,0},{9,1},... | collective-permute-start | bytes 3080 | tf_op jit(solution)/shard_map/ppermute | solution.py:158
  70.6 3.7 %collective-permute-start.18 = (f32[16,16]{0,1:T(8,128)S(1)}, f32[16,16]{0,1:T(8,128)S(1)}, u32[]{:S(2)}, u32[]{:S(2)}) collective-permute-start(f32[16,16]{0,1:T(8,128)S(1)} %select_add_fusion), channel_id=1, source_target_pairs={{0,4},{1,5},{2,6},{3,7},{4,0},{5,1},{6,2},{7,3},{8,12},{9,13},{10,... | collective-permute-start | bytes 3080 | tf_op jit(solution)/shard_map/ppermute | solution.py:158

commit v12 on v11

--- a/solution.py
+++ b/solution.py
@@ -45,36 +45,61 @@
             )
 
 
-def list_kernel(width, rows, counts, flag_ref, xo_ref, no_ref, ro_ref, *refs):
+def list_kernel(width, rows, counts, split, flag_ref, xo_ref, no_ref, ro_ref, *refs):
     out_ref = refs[-1]
-    out_ref[...] = jnp.zeros_like(out_ref)
+    if not split:
+        out_ref[...] = jnp.zeros_like(out_ref)
     slot = 0
     for ref, count in zip(refs[:-1], counts):
         for k in range(count):
-
-            @pl.when(flag_ref[slot] != 0)
-            def _():
-                base = k * rows
-                out_ref[...] += piece_terms(
+            base = k * rows
+
+            def term(ref=ref, base=base):
+                return piece_terms(
                     width,
                     ref[base : base + width, :],
                     ref[base + width : base + width + 2 * LANCZOS, :],
                     xo_ref, no_ref, ro_ref,
                 )
 
+            if split:
+
+                @pl.when(flag_ref[slot] != 0)
+                def _(term=term, slot=slot):
+                    out_ref[slot] = term()
+
+                @pl.when(flag_ref[slot] == 0)
+                def _(slot=slot):
+                    out_ref[slot] = jnp.zeros(out_ref.shape[1:], jnp.float32)
+
+            else:
+
+                @pl.when(flag_ref[slot] != 0)
+                def _(term=term):
+                    out_ref[...] += term()
+
             slot += 1
 
 
-def list_product(flags, own_terms, pieces, width, rows):
+def list_product(flags, own_terms, pieces, width, rows, split=False):
     twice_own_t, norm_own, recip_own = own_terms
     own = twice_own_t.shape[0]
     counts = [p.shape[0] // rows for p in pieces]
+    shape = (sum(counts), LANCZOS, own) if split else (LANCZOS, own)
     vmem = pl.BlockSpec(memory_space=pltpu.VMEM)
+    cols = pieces[0].shape[1]
+    slots = sum(counts)
+    cost = pl.CostEstimate(
+        flops=slots * 2 * own * cols * (width + LANCZOS),
+        transcendentals=slots * own * cols,
+        bytes_accessed=sum(p.size * 2 for p in pieces) + int(math.prod(shape)) * 4,
+    )
     return pl.pallas_call(
-        functools.partial(list_kernel, width, rows, counts),
+        functools.partial(list_kernel, width, rows, counts, split),
+        cost_estimate=cost,
         in_specs=[pl.BlockSpec(memory_space=pltpu.SMEM)] + [vmem] * (3 + len(pieces)),
         out_specs=vmem,
-        out_shape=jax.ShapeDtypeStruct((LANCZOS, own), jnp.float32),
+        out_shape=jax.ShapeDtypeStruct(shape, jnp.float32),
     )(flags, twice_own_t, norm_own, recip_own, *pieces)
 
 
@@ -104,7 +129,7 @@
     )(flags, twice_own_t, norm_own, recip_own, mine, mine)
 
 
-def gather_pieces(packed):
+def gather_pieces(packed, early_work=None):
     devices = lax.axis_size("row")
     me = lax.axis_index("row")
     if devices != 16:
@@ -127,9 +152,14 @@
     down3 = lax.ppermute(down2, "row", down)
     across3 = lax.ppermute(jnp.where(z >= 2, up2, down2), "row", across)
     last = jnp.where(ends, jnp.where(z == 3, up3, down3), up1)
+    one = jnp.ones((), bool)
+    early = None
+    if early_work is not None:
+        early = early_work([packed, up1, down1, across1, up2, down2],
+                           jnp.stack([one, z >= 1, z <= 2, one, z >= 2, z <= 1]))
+        last, early = lax.optimization_barrier((last, early))
     across4 = lax.ppermute(last, "row", across)
 
-    one = jnp.ones((), bool)
     pieces = [packed, up1, down1, across1, up2, down2, across2, up3, down3, across3, across4]
     valid = [one, z >= 1, z <= 2, one, z >= 2, z <= 1, one, z == 3, z == 0, one, one]
     origin = [
@@ -138,7 +168,10 @@
         jnp.where(z >= 2, partner - 8, partner + 8),
         jnp.where(ends, jnp.where(z == 3, partner - 12, partner + 12), partner - 4),
     ]
-    return pieces, jnp.stack(valid), jnp.clip(jnp.stack(origin), 0, devices - 1).astype(jnp.int32)
+    origin = jnp.clip(jnp.stack(origin), 0, devices - 1).astype(jnp.int32)
+    if early_work is not None:
+        return pieces, jnp.stack(valid), origin, early
+    return pieces, jnp.stack(valid), origin
 
 
 def sum_over_rows(value):
@@ -193,8 +226,24 @@
         [embeddings, weighted, local_scale[None, :], plan_row[None, :]], axis=0
     )
     packed = jnp.pad(packed, ((0, -packed.shape[0] % (2 * LANCZOS)), (0, 0)))
-    pieces, valid, origin = gather_pieces(packed)
     rows = packed.shape[0]
+    if chip_split:
+        twin_piece = lax.ppermute(packed, "row", twin)
+        rows_x = jnp.concatenate([embeddings, twin_piece[:width]], axis=1)
+        rows_scale = jnp.concatenate([local_scale, twin_piece[width + LANCZOS]])
+    else:
+        rows_x, rows_scale = embeddings, local_scale
+    norm_rows = jnp.sum(jnp.square(rows_x.astype(jnp.float32)), axis=0)[:, None]
+    log2e = 1.0 / math.log(2.0)
+    recip_rows = (-log2e / rows_scale.astype(jnp.float32))[:, None]
+    own_terms = ((rows_x * 2).T, norm_rows, recip_rows)
+    if chip_split:
+        def early_work(first, first_valid):
+            return list_product(first_valid, own_terms, first, width, rows, split=True)
+
+        pieces, valid, origin, early = gather_pieces(packed, early_work)
+    else:
+        pieces, valid, origin = gather_pieces(packed)
 
     plan_at = width + LANCZOS + 1
     copies = 2 if chip_split else 1
@@ -218,17 +267,9 @@
     flags = flags.astype(jnp.int32)
 
     if chip_split:
-        twin_piece = lax.ppermute(packed, "row", twin)
-        rows_x = jnp.concatenate([embeddings, twin_piece[:width]], axis=1)
-        rows_scale = jnp.concatenate([local_scale, twin_piece[width + LANCZOS]])
-    else:
-        rows_x, rows_scale = embeddings, local_scale
-    norm_rows = jnp.sum(jnp.square(rows_x.astype(jnp.float32)), axis=0)[:, None]
-    log2e = 1.0 / math.log(2.0)
-    recip_rows = (-log2e / rows_scale.astype(jnp.float32))[:, None]
-    own_terms = ((rows_x * 2).T, norm_rows, recip_rows)
-    if chip_split:
-        summed = list_product(flags, own_terms, pieces, width, rows)
+        head = early.shape[0]
+        summed = list_product(flags[head:], own_terms, pieces[head:], width, rows)
+        summed = summed + jnp.sum(jnp.where(flags[:head, None, None] != 0, early, 0.0), axis=0)
     else:
         summed = own_rows_product(flags, own_terms, pieces[0].reshape(devices, rows, own), width)
     if chip_split:

time: 76.5 us -> 75.5 us (0.987)
  waiting for transfers between devices: 27.6 us -> 19.7 us
  Pallas kernels: 7.4 us -> 11.1 us
  local copies, waits for them, and re-layouts: 6.62 us -> 7.7 us
  starting transfers between devices: 27.7 us -> 28.7 us
  other arithmetic: 3.68 us -> 4.64 us
    ppermute x1, waiting for transfers between devices: 4.4 us -> 0.28 us  [gather_pieces(): down3 = lax.ppermute(down2, 'row', down)]
    pallas_call x1 -> x2, Pallas kernels: 7.4 us -> 11.1 us  [list_product(): pl.pallas_call(functools.partial(list_kernel, width, rows, counts, split)...]
    ppermute x1, waiting for transfers between devices: 2.16 us -> 0.01 us  [gather_pieces(): up3 = lax.ppermute(up2, 'row', up)]
    ppermute x1, waiting for transfers between devices: 1.45 us -> 0.01 us  [shards(): twin_piece = lax.ppermute(packed, 'row', twin)]
    ppermute x1, waiting for transfers between devices: 0.01 us -> 1.09 us  [gather_pieces(): up1 = lax.ppermute(packed, 'row', up)]
    ppermute x6, waiting for transfers between devices: 5.44 us -> 4.41 us  [sum_over_rows(): lax.ppermute(value, 'row', [(i, i ^ m << shift) for i in range(devices)])]
    add x0 -> x1, other arithmetic: none -> 0.85 us  [shards(): summed + jnp.sum(jnp.where(flags[:head, None, None] != 0, early, 0.0), ax...]
    ppermute x1, starting transfers between devices: 0.75 us -> 1.58 us  [gather_pieces(): across3 = lax.ppermute(jnp.where(z >= 2, up2, down2), 'row', across)]
  transfers between devices with their start and end apart: 19 -> 19, of which waited for: 13 -> 11; matrix products, arithmetic and copies ran while one was open for 8% -> 10% of each run, Pallas kernels for 0% -> 8%
where the time goes in v12:
time: 75.5 us; the launch traced here: 74.6 us
  starting transfers between devices  28.7 us (38%)
  waiting for transfers between devices  19.7 us (26%)
  Pallas kernels  11.1 us (15%)
  local copies, waits for them, and re-layouts  7.7 us (10%)
  other arithmetic  4.64 us (6%)
  between operations  1.67 us (2%)
  matrix products  1.07 us (1%)
    pallas_call x2, Pallas kernels, list_product(): pl.pallas_call(functools.partial(list_kernel, width, rows, counts, split)...  11.1 us
    ppermute x6, starting transfers between devices, sum_over_rows(): lax.ppermute(value, 'row', [(i, i ^ m << shift) for i in range(devices)])  6.33 us
    ppermute x1, waiting for transfers between devices, gather_pieces(): across4 = lax.ppermute(last, 'row', across)  5.55 us
    ppermute x1, starting transfers between devices, gather_pieces(): up1 = lax.ppermute(packed, 'row', up)  4.53 us
    ppermute x6, waiting for transfers between devices, sum_over_rows(): lax.ppermute(value, 'row', [(i, i ^ m << shift) for i in range(devices)])  4.41 us
    ppermute x1, starting transfers between devices, gather_pieces(): up2 = lax.ppermute(up1, 'row', up)  4.39 us
    ppermute x1, waiting for transfers between devices, gather_pieces(): down2 = lax.ppermute(down1, 'row', down)  4.16 us
    ppermute x1, starting transfers between devices, gather_pieces(): up3 = lax.ppermute(up2, 'row', up)  3.62 us
  transfers between devices with their start and end apart: 19, of which 11 were waited for; matrix products, arithmetic and copies ran while one was open for 10% of the time, Pallas kernels for 8%

profile of v12, /device:TPU:0, one launch (start us, length us, event | category | flops | bytes accessed | tf_op | source)
XLA Modules:
  0.0 74.6 jit_solution(2303427252357074475)
XLA Ops:
  0.7 0.7 convert.8
  2.3 0.5 collective-permute-start
  2.8 0.7 broadcast_in_dim.27
  3.5 0.7 concatenate.39
  4.2 0.5 convert_element_type.35.flag_ref
  4.9 0.8 %multiply_convert_fusion = bf16[16,512]{1,0:T(8,128)(2,1)S(1)} fusion(f32[16,512]{1,0:T(8,128)} %param.11, f32[512]{0:T(512)} %param.10), kind=kLoop, calls=%fused_computation.21 | loop fusion | flops 16384 | bytes 51200 | tf_op jit(solution)/shard_map/convert_element_type | solution.py:219
  5.9 4.5 %collective-permute-start.1 = (bf16[224,512]{1,0:T(8,128)(2,1)S(1)}, bf16[224,512]{1,0:T(8,128)(2,1)S(1)}, u32[]{:S(2)}, u32[]{:S(2)}) collective-permute-start(bf16[224,512]{1,0:T(8,128)(2,1)S(1)} %fusion.7.refs_0_), channel_id=1, source_target_pairs={{0,4},{1,5},{2,6},{3,7},{4,8},{5,9},{6,10},{7,11},{8,12},{9,13},{1... | collective-permute-start | bytes 688136 | tf_op jit(solution)/shard_map/ppermute | solution.py:145
  10.4 1.3 %collective-permute-start.2 = (bf16[224,512]{1,0:T(8,128)(2,1)S(1)}, bf16[224,512]{1,0:T(8,128)(2,1)S(1)}, u32[]{:S(2)}, u32[]{:S(2)}) collective-permute-start(bf16[224,512]{1,0:T(8,128)(2,1)S(1)} %fusion.7.refs_0_), channel_id=1, source_target_pairs={{4,0},{5,1},{6,2},{7,3},{8,4},{9,5},{10,6},{11,7},{12,8},{13,9},{1... | collective-permute-start | bytes 688136 | tf_op jit(solution)/shard_map/ppermute | solution.py:146
  11.7 0.3 collective-permute-start.10
  12.0 1.5 %collective-permute-start.3 = (bf16[224,512]{1,0:T(8,128)(2,1)S(1)}, bf16[224,512]{1,0:T(8,128)(2,1)S(1)}, u32[]{:S(2)}, u32[]{:S(2)}) collective-permute-start(bf16[224,512]{1,0:T(8,128)(2,1)S(1)} %fusion.7.refs_0_), channel_id=1, source_target_pairs={{0,2},{1,3},{2,0},{3,1},{4,6},{5,7},{6,4},{7,5},{8,10},{9,11},{10,... | collective-permute-start | bytes 688136 | tf_op jit(solution)/shard_map/ppermute | solution.py:147
  13.6 0.2 copy.48
  13.8 0.9 %broadcast_divide_fusion.ro_ref = f32[1024,1]{1,0:T(8,128)} fusion(f32[1024,1]{1,0:T(8,128)S(1)} %copy.48), kind=kLoop, calls=%fused_computation.12 | loop fusion | flops 1024 | bytes 8192 | tf_op jit(solution)/shard_map/div | solution.py:238
  14.8 1.1 %collective-permute-done.1.refs_1_ = bf16[224,512]{1,0:T(8,128)(2,1)S(1)} collective-permute-done((bf16[224,512]{1,0:T(8,128)(2,1)S(1)}, bf16[224,512]{1,0:T(8,128)(2,1)S(1)}, u32[]{:S(2)}, u32[]{:S(2)}) %collective-permute-start.1) | collective-permute-done | bytes 229408 | tf_op jit(solution)/shard_map/ppermute | solution.py:145
  15.9 4.4 %collective-permute-start.4 = (bf16[224,512]{1,0:T(8,128)(2,1)S(1)}, bf16[224,512]{1,0:T(8,128)(2,1)S(1)}, u32[]{:S(2)}, u32[]{:S(2)}) collective-permute-start(bf16[224,512]{1,0:T(8,128)(2,1)S(1)} %collective-permute-done.1.refs_1_), channel_id=1, source_target_pairs={{0,4},{1,5},{2,6},{3,7},{4,8},{5,9},{6,10},{7,11},{8,12},{9,13},{1... | collective-permute-start | bytes 688136 | tf_op jit(solution)/shard_map/ppermute | solution.py:148
  20.3 1.3 %collective-permute-start.5 = (bf16[224,512]{1,0:T(8,128)(2,1)S(1)}, bf16[224,512]{1,0:T(8,128)(2,1)S(1)}, u32[]{:S(2)}, u32[]{:S(2)}) collective-permute-start(bf16[224,512]{1,0:T(8,128)(2,1)S(1)} %collective-permute-done.2.refs_2_), channel_id=1, source_target_pairs={{4,0},{5,1},{6,2},{7,3},{8,4},{9,5},{10,6},{11,7},{12,8},{13,9},{1... | collective-permute-start | bytes 688136 | tf_op jit(solution)/shard_map/ppermute | solution.py:149
  21.7 1.0 %copy.49.xo_ref = bf16[1024,192]{1,0:T(8,128)(2,1)} copy(bf16[1024,192]{0,1:T(8,128)(2,1)S(1)} %multiply_bitcast_fusion) | data formatting | bytes 786432 | tf_op jit(solution)/shard_map/transpose | solution.py:239
  22.8 1.0 %copy.50.no_ref = f32[1024,1]{1,0:T(8,128)} copy(f32[1024,1]{0,1:T(1,128)S(1)} %bitcast.76) | data formatting | bytes 8192 | tf_op jit(solution)/shard_map/broadcast_in_dim | solution.py:236
  23.8 1.2 %collective-permute-done.4.refs_4_ = bf16[224,512]{1,0:T(8,128)(2,1)S(1)} collective-permute-done((bf16[224,512]{1,0:T(8,128)(2,1)S(1)}, bf16[224,512]{1,0:T(8,128)(2,1)S(1)}, u32[]{:S(2)}, u32[]{:S(2)}) %collective-permute-start.4) | collective-permute-done | bytes 229408 | tf_op jit(solution)/shard_map/ppermute | solution.py:148
  25.0 4.2 %collective-permute-done.5.refs_5_ = bf16[224,512]{1,0:T(8,128)(2,1)S(1)} collective-permute-done((bf16[224,512]{1,0:T(8,128)(2,1)S(1)}, bf16[224,512]{1,0:T(8,128)(2,1)S(1)}, u32[]{:S(2)}, u32[]{:S(2)}) %collective-permute-start.5) | collective-permute-done | bytes 229408 | tf_op jit(solution)/shard_map/ppermute | solution.py:149
  29.2 1.6 %collective-permute-start.9 = (bf16[224,512]{1,0:T(8,128)(2,1)S(1)}, bf16[224,512]{1,0:T(8,128)(2,1)S(1)}, u32[]{:S(2)}, u32[]{:S(2)}) collective-permute-start(bf16[224,512]{1,0:T(8,128)(2,1)S(1)} %broadcast_select_fusion), channel_id=1, source_target_pairs={{0,2},{1,3},{2,0},{3,1},{4,6},{5,7},{6,4},{7,5},{8,10},{9,11},{10,... | collective-permute-start | bytes 688136 | tf_op jit(solution)/shard_map/ppermute | solution.py:153
  30.8 3.6 %collective-permute-start.7 = (bf16[224,512]{1,0:T(8,128)(2,1)S(1)}, bf16[224,512]{1,0:T(8,128)(2,1)S(1)}, u32[]{:S(2)}, u32[]{:S(2)}) collective-permute-start(bf16[224,512]{1,0:T(8,128)(2,1)S(1)} %collective-permute-done.4.refs_4_), channel_id=1, source_target_pairs={{0,4},{1,5},{2,6},{3,7},{4,8},{5,9},{6,10},{7,11},{8,12},{9,13},{1... | collective-permute-start | bytes 688136 | tf_op jit(solution)/shard_map/ppermute | solution.py:151
  34.4 1.3 %collective-permute-start.8 = (bf16[224,512]{1,0:T(8,128)(2,1)S(1)}, bf16[224,512]{1,0:T(8,128)(2,1)S(1)}, u32[]{:S(2)}, u32[]{:S(2)}) collective-permute-start(bf16[224,512]{1,0:T(8,128)(2,1)S(1)} %collective-permute-done.5.refs_5_), channel_id=1, source_target_pairs={{4,0},{5,1},{6,2},{7,3},{8,4},{9,5},{10,6},{11,7},{12,8},{13,9},{1... | collective-permute-start | bytes 688136 | tf_op jit(solution)/shard_map/ppermute | solution.py:152
  35.7 5.7 %shard_map.95 = f32[6,16,1024]{2,1,0:T(8,128)} custom-call(s32[6]{0:T(128)} %convert_element_type.35.flag_ref, bf16[1024,192]{1,0:T(8,128)(2,1)} %copy.49.xo_ref, f32[1024,1]{1,0:T(8,128)} %copy.50.no_ref, f32[1024,1]{1,0:T(8,128)} %broadcast_divide_fusion.ro_ref, bf16[224,512]{1,0:T(8,128)(2,1)} %copy-done.4, bf16[224,512]{1,0:T(8,128)(2,1)} %copy-done.9, ...), custom_call_target="tpu_custom_call" | custom-call | flops 1308622848 | bytes 1769472 | tf_op jit(solution)/shard_map/pallas_call | solution.py:97
  41.4 0.7 slice_bitcast_fusion.7
  42.0 0.3 collective-permute-done.8.refs_2_
  42.4 0.6 collective-permute-start.11
  43.0 1.5 %collective-permute-start.6 = (bf16[224,512]{1,0:T(8,128)(2,1)S(1)}, bf16[224,512]{1,0:T(8,128)(2,1)S(1)}, u32[]{:S(2)}, u32[]{:S(2)}) collective-permute-start(bf16[224,512]{1,0:T(8,128)(2,1)S(1)} %get-tuple-element.17), channel_id=1, source_target_pairs={{0,2},{1,3},{2,0},{3,1},{4,6},{5,7},{6,4},{7,5},{8,10},{9,11},{10,... | collective-permute-start | bytes 688136 | tf_op jit(solution)/shard_map/ppermute | solution.py:150
  44.5 5.6 %collective-permute-done.11.refs_4_ = bf16[224,512]{1,0:T(8,128)(2,1)S(1)} collective-permute-done((bf16[224,512]{1,0:T(8,128)(2,1)S(1)}, bf16[224,512]{1,0:T(8,128)(2,1)S(1)}, u32[]{:S(2)}, u32[]{:S(2)}) %collective-permute-start.11) | collective-permute-done | bytes 229408 | tf_op jit(solution)/shard_map/ppermute | solution.py:161
  50.1 2.4 %collective-permute-done.6.refs_0_ = bf16[224,512]{1,0:T(8,128)(2,1)S(1)} collective-permute-done((bf16[224,512]{1,0:T(8,128)(2,1)S(1)}, bf16[224,512]{1,0:T(8,128)(2,1)S(1)}, u32[]{:S(2)}, u32[]{:S(2)}) %collective-permute-start.6) | collective-permute-done | bytes 229408 | tf_op jit(solution)/shard_map/ppermute | solution.py:150
  52.7 0.2 slice_reduce_fusion
  53.6 0.2 and_reduce_fusion
  53.8 0.6 slice.80.flag_ref
  54.5 5.4 %shard_map.96 = f32[16,1024]{1,0:T(8,128)} custom-call(s32[5]{0:T(128)} %slice.80.flag_ref, bf16[1024,192]{1,0:T(8,128)(2,1)} %copy.49.xo_ref, f32[1024,1]{1,0:T(8,128)} %copy.50.no_ref, f32[1024,1]{1,0:T(8,128)} %broadcast_divide_fusion.ro_ref, bf16[224,512]{1,0:T(8,128)(2,1)} %copy-done.17, bf16[224,512]{1,0:T(8,128)(2,1)} %copy-done.7, ...), custom_call_target="tpu_custom_call" | custom-call | flops 1090519040 | bytes 1212416 | tf_op jit(solution)/shard_map/pallas_call | solution.py:97
  59.9 0.8 %add.65 = f32[16,1024]{1,0:T(8,128)S(1)} add(f32[16,1024]{1,0:T(8,128)} %shard_map.96, f32[16,1024]{1,0:T(8,128)S(1)} %select_reduce_fusion) | non-fusion elementwise | flops 16384 | bytes 196608 | tf_op jit(solution)/shard_map/add | solution.py:272
  60.9 0.6 copy-done.14
  61.5 0.6 collective-permute-done.12
  62.1 0.1 convolution_bitcast_fusion
  62.2 1.8 %collective-permute-start.14 = (f32[16,16]{0,1:T(8,128)S(1)}, f32[16,16]{0,1:T(8,128)S(1)}, u32[]{:S(2)}, u32[]{:S(2)}) collective-permute-start(f32[16,16]{0,1:T(8,128)S(1)} %convolution_bitcast_fusion), channel_id=1, source_target_pairs={{0,2},{1,3},{2,0},{3,1},{4,6},{5,7},{6,4},{7,5},{8,10},{9,11},{10,... | collective-permute-start | bytes 3080 | tf_op jit(solution)/shard_map/ppermute | solution.py:191
  64.1 1.2 %collective-permute-done.13 = f32[16,16]{0,1:T(8,128)S(1)} collective-permute-done((f32[16,16]{0,1:T(8,128)S(1)}, f32[16,16]{0,1:T(8,128)S(1)}, u32[]{:S(2)}, u32[]{:S(2)}) %collective-permute-start.13) | collective-permute-done | bytes 1056 | tf_op jit(solution)/shard_map/ppermute | solution.py:191
  65.3 0.6 collective-permute-done.14
  66.0 2.6 %collective-permute-start.16 = (f32[16,16]{0,1:T(8,128)S(1)}, f32[16,16]{0,1:T(8,128)S(1)}, u32[]{:S(2)}, u32[]{:S(2)}) collective-permute-start(f32[16,16]{0,1:T(8,128)S(1)} %select_add_fusion), channel_id=1, source_target_pairs={{0,12},{1,13},{2,14},{3,15},{4,8},{5,9},{6,10},{7,11},{8,4},{9,5},... | collective-permute-start | bytes 3080 | tf_op jit(solution)/shard_map/ppermute | solution.py:191
  68.6 0.7 collective-permute-start.17
  69.3 1.1 %collective-permute-start.18 = (f32[16,16]{0,1:T(8,128)S(1)}, f32[16,16]{0,1:T(8,128)S(1)}, u32[]{:S(2)}, u32[]{:S(2)}) collective-permute-start(f32[16,16]{0,1:T(8,128)S(1)} %select_add_fusion), channel_id=1, source_target_pairs={{0,4},{1,5},{2,6},{3,7},{4,0},{5,1},{6,2},{7,3},{8,12},{9,13},{10,... | collective-permute-start | bytes 3080 | tf_op jit(solution)/shard_map/ppermute | solution.py:191
  70.4 0.1 fusion.16
  70.6 0.9 %collective-permute-done.16 = f32[16,16]{0,1:T(8,128)S(1)} collective-permute-done((f32[16,16]{0,1:T(8,128)S(1)}, f32[16,16]{0,1:T(8,128)S(1)}, u32[]{:S(2)}, u32[]{:S(2)}) %collective-permute-start.16) | collective-permute-done | bytes 1056 | tf_op jit(solution)/shard_map/ppermute | solution.py:191
  71.5 1.7 %collective-permute-done.17 = f32[16,16]{0,1:T(8,128)S(1)} collective-permute-done((f32[16,16]{0,1:T(8,128)S(1)}, f32[16,16]{0,1:T(8,128)S(1)}, u32[]{:S(2)}, u32[]{:S(2)}) %collective-permute-start.17) | collective-permute-done | bytes 1056 | tf_op jit(solution)/shard_map/ppermute | solution.py:191
  73.2 0.7 copy.56
  73.8 0.8 %fusion = f32[16,512]{1,0:T(8,128)} fusion(f32[16,512]{1,0:T(8,128)S(1)} %fusion.16, f32[16,16]{0,1:T(8,128)S(1)} %add_multiply_fusion, f32[16,512]{1,0:T(8,128)S(1)} %copy-done.3, f32[512]{0:T(512)S(1)} %broadcast_multiply_fusion, f32[16,512]{1,0:T(8,128)S(1)} %collective-permute-done.12, f32[16,1024]{1,0:T(8,128)S(1)} %add.65), kind=kOutput, calls=%fused_computation.1 | convolution fusion | flops 1605632 | bytes 166912 | tf_op jit(solution)/shard_map/dot_general | solution.py:282
  (96 shorter events, 2.3 us)
Async XLA Ops:
  0.6 69.8 %copy-start = (f32[16,512]{1,0:T(8,128)S(1)}, f32[16,512]{1,0:T(8,128)}, u32[]{:S(2)}) copy-start(f32[16,512]{1,0:T(8,128)} %param.12) | copy-start | bytes 98308
  0.6 5.2 %copy-start.1 = (bf16[192,512]{1,0:T(8,128)(2,1)S(1)}, bf16[192,512]{1,0:T(8,128)(2,1)}, u32[]{:S(2)}) copy-start(bf16[192,512]{1,0:T(8,128)(2,1)} %param.8) | copy-start | bytes 589828
  2.3 3.4 %collective-permute-start = (bf16[9]{0:T(256)(128)(2,1)S(1)}, bf16[9]{0:T(256)(128)(2,1)S(1)}, u32[]{:S(2)}, u32[]{:S(2)}) collective-permute-start(bf16[9]{0:T(256)(128)(2,1)S(1)} %pad_maximum_fusion.1), channel_id=1, source_target_pairs={{0,1},{1,0},{2,3},{3,2},{4,5},{5,4},{6,7},{7,6},{8,9},{9,8},{10,11... | collective-permute-start | bytes 62 | tf_op jit(solution)/shard_map/ppermute | solution.py:223
  5.9 7.7 %copy-start.4 = (bf16[224,512]{1,0:T(8,128)(2,1)}, bf16[224,512]{1,0:T(8,128)(2,1)S(1)}, u32[]{:S(2)}) copy-start(bf16[224,512]{1,0:T(8,128)(2,1)S(1)} %fusion.7.refs_0_) | copy-start | bytes 688132
  5.9 10.0 %collective-permute-start.1 = (bf16[224,512]{1,0:T(8,128)(2,1)S(1)}, bf16[224,512]{1,0:T(8,128)(2,1)S(1)}, u32[]{:S(2)}, u32[]{:S(2)}) collective-permute-start(bf16[224,512]{1,0:T(8,128)(2,1)S(1)} %fusion.7.refs_0_), channel_id=1, source_target_pairs={{0,4},{1,5},{2,6},{3,7},{4,8},{5,9},{6,10},{7,11},{8,12},{9,13},{1... | collective-permute-start | bytes 688136 | tf_op jit(solution)/shard_map/ppermute | solution.py:145
  10.4 9.9 %collective-permute-start.2 = (bf16[224,512]{1,0:T(8,128)(2,1)S(1)}, bf16[224,512]{1,0:T(8,128)(2,1)S(1)}, u32[]{:S(2)}, u32[]{:S(2)}) collective-permute-start(bf16[224,512]{1,0:T(8,128)(2,1)S(1)} %fusion.7.refs_0_), channel_id=1, source_target_pairs={{4,0},{5,1},{6,2},{7,3},{8,4},{9,5},{10,6},{11,7},{12,8},{13,9},{1... | collective-permute-start | bytes 688136 | tf_op jit(solution)/shard_map/ppermute | solution.py:146
  11.7 1.8 %collective-permute-start.10 = (bf16[224,512]{1,0:T(8,128)(2,1)S(1)}, bf16[224,512]{1,0:T(8,128)(2,1)S(1)}, u32[]{:S(2)}, u32[]{:S(2)}) collective-permute-start(bf16[224,512]{1,0:T(8,128)(2,1)S(1)} %fusion.7.refs_0_), channel_id=1, source_target_pairs={{0,1},{1,0},{2,3},{3,2},{4,5},{5,4},{6,7},{7,6},{8,9},{9,8},{10,11... | collective-permute-start | bytes 688136 | tf_op jit(solution)/shard_map/ppermute | solution.py:231
  12.0 11.8 %collective-permute-start.3 = (bf16[224,512]{1,0:T(8,128)(2,1)S(1)}, bf16[224,512]{1,0:T(8,128)(2,1)S(1)}, u32[]{:S(2)}, u32[]{:S(2)}) collective-permute-start(bf16[224,512]{1,0:T(8,128)(2,1)S(1)} %fusion.7.refs_0_), channel_id=1, source_target_pairs={{0,2},{1,3},{2,0},{3,1},{4,6},{5,7},{6,4},{7,5},{8,10},{9,11},{10,... | collective-permute-start | bytes 688136 | tf_op jit(solution)/shard_map/ppermute | solution.py:147
  15.9 6.9 %copy-start.9 = (bf16[224,512]{1,0:T(8,128)(2,1)}, bf16[224,512]{1,0:T(8,128)(2,1)S(1)}, u32[]{:S(2)}) copy-start(bf16[224,512]{1,0:T(8,128)(2,1)S(1)} %collective-permute-done.1.refs_1_) | copy-start | bytes 688132
  15.9 9.1 %collective-permute-start.4 = (bf16[224,512]{1,0:T(8,128)(2,1)S(1)}, bf16[224,512]{1,0:T(8,128)(2,1)S(1)}, u32[]{:S(2)}, u32[]{:S(2)}) collective-permute-start(bf16[224,512]{1,0:T(8,128)(2,1)S(1)} %collective-permute-done.1.refs_1_), channel_id=1, source_target_pairs={{0,4},{1,5},{2,6},{3,7},{4,8},{5,9},{6,10},{7,11},{8,12},{9,13},{1... | collective-permute-start | bytes 688136 | tf_op jit(solution)/shard_map/ppermute | solution.py:148
  20.3 2.4 %copy-start.11 = (bf16[224,512]{1,0:T(8,128)(2,1)}, bf16[224,512]{1,0:T(8,128)(2,1)S(1)}, u32[]{:S(2)}) copy-start(bf16[224,512]{1,0:T(8,128)(2,1)S(1)} %collective-permute-done.2.refs_2_) | copy-start | bytes 688132
  20.3 8.8 %collective-permute-start.5 = (bf16[224,512]{1,0:T(8,128)(2,1)S(1)}, bf16[224,512]{1,0:T(8,128)(2,1)S(1)}, u32[]{:S(2)}, u32[]{:S(2)}) collective-permute-start(bf16[224,512]{1,0:T(8,128)(2,1)S(1)} %collective-permute-done.2.refs_2_), channel_id=1, source_target_pairs={{4,0},{5,1},{6,2},{7,3},{8,4},{9,5},{10,6},{11,7},{12,8},{13,9},{1... | collective-permute-start | bytes 688136 | tf_op jit(solution)/shard_map/ppermute | solution.py:149
  23.8 5.4 %copy-start.18 = (bf16[224,512]{1,0:T(8,128)(2,1)}, bf16[224,512]{1,0:T(8,128)(2,1)S(1)}, u32[]{:S(2)}) copy-start(bf16[224,512]{1,0:T(8,128)(2,1)S(1)} %collective-permute-done.3.refs_3_) | copy-start | bytes 688132
  25.0 5.8 %copy-start.5 = (bf16[224,512]{1,0:T(8,128)(2,1)}, bf16[224,512]{1,0:T(8,128)(2,1)S(1)}, u32[]{:S(2)}) copy-start(bf16[224,512]{1,0:T(8,128)(2,1)S(1)} %collective-permute-done.4.refs_4_) | copy-start | bytes 688132
  29.1 5.3 %copy-start.6 = (bf16[224,512]{1,0:T(8,128)(2,1)}, bf16[224,512]{1,0:T(8,128)(2,1)S(1)}, u32[]{:S(2)}) copy-start(bf16[224,512]{1,0:T(8,128)(2,1)S(1)} %collective-permute-done.5.refs_5_) | copy-start | bytes 688132
  29.2 15.3 %collective-permute-start.9 = (bf16[224,512]{1,0:T(8,128)(2,1)S(1)}, bf16[224,512]{1,0:T(8,128)(2,1)S(1)}, u32[]{:S(2)}, u32[]{:S(2)}) collective-permute-start(bf16[224,512]{1,0:T(8,128)(2,1)S(1)} %broadcast_select_fusion), channel_id=1, source_target_pairs={{0,2},{1,3},{2,0},{3,1},{4,6},{5,7},{6,4},{7,5},{8,10},{9,11},{10,... | collective-permute-start | bytes 688136 | tf_op jit(solution)/shard_map/ppermute | solution.py:153
  30.8 11.6 %copy-start.10 = (bf16[224,512]{1,0:T(8,128)(2,1)S(1)}, bf16[224,512]{1,0:T(8,128)(2,1)}, u32[]{:S(2)}) copy-start(bf16[224,512]{1,0:T(8,128)(2,1)} %copy-done.9) | copy-start | bytes 688132
  30.8 11.6 %copy-start.12 = (bf16[224,512]{1,0:T(8,128)(2,1)S(1)}, bf16[224,512]{1,0:T(8,128)(2,1)}, u32[]{:S(2)}) copy-start(bf16[224,512]{1,0:T(8,128)(2,1)} %copy-done.11) | copy-start | bytes 688132
  30.8 11.3 %collective-permute-start.7 = (bf16[224,512]{1,0:T(8,128)(2,1)S(1)}, bf16[224,512]{1,0:T(8,128)(2,1)S(1)}, u32[]{:S(2)}, u32[]{:S(2)}) collective-permute-start(bf16[224,512]{1,0:T(8,128)(2,1)S(1)} %collective-permute-done.4.refs_4_), channel_id=1, source_target_pairs={{0,4},{1,5},{2,6},{3,7},{4,8},{5,9},{6,10},{7,11},{8,12},{9,13},{1... | collective-permute-start | bytes 688136 | tf_op jit(solution)/shard_map/ppermute | solution.py:151
  34.4 7.9 %collective-permute-start.8 = (bf16[224,512]{1,0:T(8,128)(2,1)S(1)}, bf16[224,512]{1,0:T(8,128)(2,1)S(1)}, u32[]{:S(2)}, u32[]{:S(2)}) collective-permute-start(bf16[224,512]{1,0:T(8,128)(2,1)S(1)} %collective-permute-done.5.refs_5_), channel_id=1, source_target_pairs={{4,0},{5,1},{6,2},{7,3},{8,4},{9,5},{10,6},{11,7},{12,8},{13,9},{1... | collective-permute-start | bytes 688136 | tf_op jit(solution)/shard_map/ppermute | solution.py:152
  42.0 2.5 %copy-start.7 = (bf16[224,512]{1,0:T(8,128)(2,1)}, bf16[224,512]{1,0:T(8,128)(2,1)S(1)}, u32[]{:S(2)}) copy-start(bf16[224,512]{1,0:T(8,128)(2,1)S(1)} %collective-permute-done.7.refs_1_) | copy-start | bytes 688132
  42.3 2.2 %copy-start.8 = (bf16[224,512]{1,0:T(8,128)(2,1)}, bf16[224,512]{1,0:T(8,128)(2,1)S(1)}, u32[]{:S(2)}) copy-start(bf16[224,512]{1,0:T(8,128)(2,1)S(1)} %collective-permute-done.8.refs_2_) | copy-start | bytes 688132
  42.3 12.0 %copy-start.2 = (f32[6,16,1024]{2,1,0:T(8,128)S(1)}, f32[6,16,1024]{2,1,0:T(8,128)}, u32[]{:S(2)}) copy-start(f32[6,16,1024]{2,1,0:T(8,128)} %shard_map.95) | copy-start | bytes 1179652
  42.4 7.7 %collective-permute-start.11 = (bf16[224,512]{1,0:T(8,128)(2,1)S(1)}, bf16[224,512]{1,0:T(8,128)(2,1)S(1)}, u32[]{:S(2)}, u32[]{:S(2)}) collective-permute-start(bf16[224,512]{1,0:T(8,128)(2,1)S(1)} %get-tuple-element.4), channel_id=1, source_target_pairs={{0,2},{1,3},{2,0},{3,1},{4,6},{5,7},{6,4},{7,5},{8,10},{9,11},{10,... | collective-permute-start | bytes 688136 | tf_op jit(solution)/shard_map/ppermute | solution.py:161
  43.0 9.6 %collective-permute-start.6 = (bf16[224,512]{1,0:T(8,128)(2,1)S(1)}, bf16[224,512]{1,0:T(8,128)(2,1)S(1)}, u32[]{:S(2)}, u32[]{:S(2)}) collective-permute-start(bf16[224,512]{1,0:T(8,128)(2,1)S(1)} %get-tuple-element.17), channel_id=1, source_target_pairs={{0,2},{1,3},{2,0},{3,1},{4,6},{5,7},{6,4},{7,5},{8,10},{9,11},{10,... | collective-permute-start | bytes 688136 | tf_op jit(solution)/shard_map/ppermute | solution.py:150
  44.5 10.0 %copy-start.15 = (bf16[224,512]{1,0:T(8,128)(2,1)}, bf16[224,512]{1,0:T(8,128)(2,1)S(1)}, u32[]{:S(2)}) copy-start(bf16[224,512]{1,0:T(8,128)(2,1)S(1)} %collective-permute-done.9.refs_3_) | copy-start | bytes 688132
  50.1 4.4 %copy-start.16 = (bf16[224,512]{1,0:T(8,128)(2,1)}, bf16[224,512]{1,0:T(8,128)(2,1)S(1)}, u32[]{:S(2)}) copy-start(bf16[224,512]{1,0:T(8,128)(2,1)S(1)} %collective-permute-done.11.refs_4_) | copy-start | bytes 688132
  52.6 1.9 %copy-start.17 = (bf16[224,512]{1,0:T(8,128)(2,1)}, bf16[224,512]{1,0:T(8,128)(2,1)S(1)}, u32[]{:S(2)}) copy-start(bf16[224,512]{1,0:T(8,128)(2,1)S(1)} %collective-permute-done.6.refs_0_) | copy-start | bytes 688132
  60.8 0.7 copy-start.14
  60.8 1.3 %copy-start.3 = (f32[16,512]{1,0:T(8,128)S(1)}, f32[16,512]{1,0:T(8,128)}, u32[]{:S(2)}) copy-start(f32[16,512]{1,0:T(8,128)} %param.11) | copy-start | bytes 98308
  60.8 1.3 %collective-permute-start.12 = (f32[16,512]{1,0:T(8,128)S(1)}, f32[16,512]{1,0:T(8,128)S(1)}, u32[]{:S(2)}, u32[]{:S(2)}) collective-permute-start(f32[16,512]{1,0:T(8,128)S(1)} %slice.102), channel_id=1, source_target_pairs={{0,1},{1,0},{2,3},{3,2},{4,5},{5,4},{6,7},{7,6},{8,9},{9,8},{10,11... | collective-permute-start | bytes 98312 | tf_op jit(solution)/shard_map/ppermute | solution.py:276
  62.2 3.1 %collective-permute-start.13 = (f32[16,16]{0,1:T(8,128)S(1)}, f32[16,16]{0,1:T(8,128)S(1)}, u32[]{:S(2)}, u32[]{:S(2)}) collective-permute-start(f32[16,16]{0,1:T(8,128)S(1)} %convolution_bitcast_fusion), channel_id=1, source_target_pairs={{0,3},{1,2},{2,1},{3,0},{4,7},{5,6},{6,5},{7,4},{8,11},{9,10},{10,... | collective-permute-start | bytes 3080 | tf_op jit(solution)/shard_map/ppermute | solution.py:191
  62.2 3.7 %collective-permute-start.14 = (f32[16,16]{0,1:T(8,128)S(1)}, f32[16,16]{0,1:T(8,128)S(1)}, u32[]{:S(2)}, u32[]{:S(2)}) collective-permute-start(f32[16,16]{0,1:T(8,128)S(1)} %convolution_bitcast_fusion), channel_id=1, source_target_pairs={{0,2},{1,3},{2,0},{3,1},{4,6},{5,7},{6,4},{7,5},{8,10},{9,11},{10,... | collective-permute-start | bytes 3080 | tf_op jit(solution)/shard_map/ppermute | solution.py:191
  64.0 1.9 %collective-permute-start.15 = (f32[16,16]{0,1:T(8,128)S(1)}, f32[16,16]{0,1:T(8,128)S(1)}, u32[]{:S(2)}, u32[]{:S(2)}) collective-permute-start(f32[16,16]{0,1:T(8,128)S(1)} %convolution_bitcast_fusion), channel_id=1, source_target_pairs={{0,1},{1,0},{2,3},{3,2},{4,5},{5,4},{6,7},{7,6},{8,9},{9,8},{10,11... | collective-permute-start | bytes 3080 | tf_op jit(solution)/shard_map/ppermute | solution.py:191
  64.1 6.3 %copy-start.13 = (f32[16,16]{1,0:T(8,128)S(1)}, f32[16,16]{1,0:T(8,128)}, u32[]{:S(2)}) copy-start(f32[16,16]{1,0:T(8,128)} %param.13) | copy-start | bytes 3076
  66.0 5.5 %collective-permute-start.16 = (f32[16,16]{0,1:T(8,128)S(1)}, f32[16,16]{0,1:T(8,128)S(1)}, u32[]{:S(2)}, u32[]{:S(2)}) collective-permute-start(f32[16,16]{0,1:T(8,128)S(1)} %select_add_fusion), channel_id=1, source_target_pairs={{0,12},{1,13},{2,14},{3,15},{4,8},{5,9},{6,10},{7,11},{8,4},{9,5},... | collective-permute-start | bytes 3080 | tf_op jit(solution)/shard_map/ppermute | solution.py:191
  68.6 4.5 %collective-permute-start.17 = (f32[16,16]{0,1:T(8,128)S(1)}, f32[16,16]{0,1:T(8,128)S(1)}, u32[]{:S(2)}, u32[]{:S(2)}) collective-permute-start(f32[16,16]{0,1:T(8,128)S(1)} %select_add_fusion), channel_id=1, source_target_pairs={{0,8},{1,9},{2,10},{3,11},{4,12},{5,13},{6,14},{7,15},{8,0},{9,1},... | collective-permute-start | bytes 3080 | tf_op jit(solution)/shard_map/ppermute | solution.py:191
  69.3 3.8 %collective-permute-start.18 = (f32[16,16]{0,1:T(8,128)S(1)}, f32[16,16]{0,1:T(8,128)S(1)}, u32[]{:S(2)}, u32[]{:S(2)}) collective-permute-start(f32[16,16]{0,1:T(8,128)S(1)} %select_add_fusion), channel_id=1, source_target_pairs={{0,4},{1,5},{2,6},{3,7},{4,0},{5,1},{6,2},{7,3},{8,12},{9,13},{10,... | collective-permute-start | bytes 3080 | tf_op jit(solution)/shard_map/ppermute | solution.py:191

commit v13 on v12

--- a/solution.py
+++ b/solution.py
@@ -145,9 +145,11 @@
     up1 = lax.ppermute(packed, "row", up)
     down1 = lax.ppermute(packed, "row", down)
     across1 = lax.ppermute(packed, "row", across)
+    second = jnp.where(z <= 2, down1, up1)
+    up1, down1, second = lax.optimization_barrier((up1, down1, second))
     up2 = lax.ppermute(up1, "row", up)
     down2 = lax.ppermute(down1, "row", down)
-    across2 = lax.ppermute(jnp.where(z <= 2, down1, up1), "row", across)
+    across2 = lax.ppermute(second, "row", across)
     up3 = lax.ppermute(up2, "row", up)
     down3 = lax.ppermute(down2, "row", down)
     across3 = lax.ppermute(jnp.where(z >= 2, up2, down2), "row", across)
@@ -155,8 +157,8 @@
     one = jnp.ones((), bool)
     early = None
     if early_work is not None:
-        early = early_work([packed, up1, down1, across1, up2, down2],
-                           jnp.stack([one, z >= 1, z <= 2, one, z >= 2, z <= 1]))
+        early = early_work([packed, up1, down1, across1, up2, down2, across2],
+                           jnp.stack([one, z >= 1, z <= 2, one, z >= 2, z <= 1, one]))
         last, early = lax.optimization_barrier((last, early))
     across4 = lax.ppermute(last, "row", across)
 

time: 75.5 us -> 74.7 us (0.989)
  waiting for transfers between devices: 19.7 us -> 20.7 us
  starting transfers between devices: 28.7 us -> 27.9 us
  Pallas kernels: 11.1 us -> 10.3 us
    ppermute x1, waiting for transfers between devices: 0.01 us -> 4.12 us  [gather_pieces(): down1 = lax.ppermute(packed, 'row', down)]
    ppermute x1, waiting for transfers between devices: 2.45 us -> 0.01 us  [gather_pieces(): across2 = lax.ppermute(second, 'row', across)]
    ppermute x1, waiting for transfers between devices: 4.16 us -> 2.15 us  [gather_pieces(): down2 = lax.ppermute(down1, 'row', down)]
    ppermute x6, waiting for transfers between devices: 4.41 us -> 6.06 us  [sum_over_rows(): lax.ppermute(value, 'row', [(i, i ^ m << shift) for i in range(devices)])]
    ppermute x1, waiting for transfers between devices: 1.09 us -> 2.36 us  [gather_pieces(): up1 = lax.ppermute(packed, 'row', up)]
    ppermute x1, waiting for transfers between devices: 1.15 us -> 0.01 us  [gather_pieces(): up2 = lax.ppermute(up1, 'row', up)]
    ppermute x1, starting transfers between devices: 4.39 us -> 3.48 us  [gather_pieces(): up2 = lax.ppermute(up1, 'row', up)]
    pallas_call x2, Pallas kernels: 11.1 us -> 10.3 us  [list_product(): pl.pallas_call(functools.partial(list_kernel, width, rows, counts, split)...]
  transfers between devices with their start and end apart: 19 -> 19, of which waited for: 11 -> 10; matrix products, arithmetic and copies ran while one was open for 10% -> 10% of each run, Pallas kernels for 8% -> 9%
where the time goes in v13:
time: 74.7 us; the launch traced here: 74.1 us
  starting transfers between devices  27.9 us (37%)
  waiting for transfers between devices  20.7 us (28%)
  Pallas kernels  10.3 us (14%)
  local copies, waits for them, and re-layouts  7.75 us (10%)
  other arithmetic  4.72 us (6%)
  between operations  1.66 us (2%)
  matrix products  1.07 us (1%)
    pallas_call x2, Pallas kernels, list_product(): pl.pallas_call(functools.partial(list_kernel, width, rows, counts, split)...  10.3 us
    ppermute x6, starting transfers between devices, sum_over_rows(): lax.ppermute(value, 'row', [(i, i ^ m << shift) for i in range(devices)])  6.34 us
    ppermute x6, waiting for transfers between devices, sum_over_rows(): lax.ppermute(value, 'row', [(i, i ^ m << shift) for i in range(devices)])  6.06 us
    ppermute x1, waiting for transfers between devices, gather_pieces(): across4 = lax.ppermute(last, 'row', across)  5.4 us
    ppermute x1, starting transfers between devices, gather_pieces(): up1 = lax.ppermute(packed, 'row', up)  4.53 us
    ppermute x1, waiting for transfers between devices, gather_pieces(): down1 = lax.ppermute(packed, 'row', down)  4.12 us
    ppermute x1, starting transfers between devices, gather_pieces(): up3 = lax.ppermute(up2, 'row', up)  3.62 us
    ppermute x1, starting transfers between devices, gather_pieces(): up2 = lax.ppermute(up1, 'row', up)  3.48 us
  transfers between devices with their start and end apart: 19, of which 10 were waited for; matrix products, arithmetic and copies ran while one was open for 10% of the time, Pallas kernels for 9%

profile of v13, /device:TPU:0, one launch (start us, length us, event | category | flops | bytes accessed | tf_op | source)
XLA Modules:
  0.0 74.1 jit_solution(15794994672759791552)
XLA Ops:
  0.7 0.7 convert.8
  2.3 0.5 collective-permute-start
  2.8 0.7 broadcast_in_dim.27
  3.5 0.7 concatenate.39
  4.2 0.6 convert_element_type.35.flag_ref
  4.9 0.8 %multiply_convert_fusion = bf16[16,512]{1,0:T(8,128)(2,1)S(1)} fusion(f32[16,512]{1,0:T(8,128)} %param.11, f32[512]{0:T(512)} %param.10), kind=kLoop, calls=%fused_computation.21 | loop fusion | flops 16384 | bytes 51200 | tf_op jit(solution)/shard_map/convert_element_type | solution.py:221
  5.9 4.5 %collective-permute-start.1 = (bf16[224,512]{1,0:T(8,128)(2,1)S(1)}, bf16[224,512]{1,0:T(8,128)(2,1)S(1)}, u32[]{:S(2)}, u32[]{:S(2)}) collective-permute-start(bf16[224,512]{1,0:T(8,128)(2,1)S(1)} %fusion.7.refs_0_), channel_id=1, source_target_pairs={{0,4},{1,5},{2,6},{3,7},{4,8},{5,9},{6,10},{7,11},{8,12},{9,13},{1... | collective-permute-start | bytes 688136 | tf_op jit(solution)/shard_map/ppermute | solution.py:145
  10.5 1.3 %collective-permute-start.2 = (bf16[224,512]{1,0:T(8,128)(2,1)S(1)}, bf16[224,512]{1,0:T(8,128)(2,1)S(1)}, u32[]{:S(2)}, u32[]{:S(2)}) collective-permute-start(bf16[224,512]{1,0:T(8,128)(2,1)S(1)} %fusion.7.refs_0_), channel_id=1, source_target_pairs={{4,0},{5,1},{6,2},{7,3},{8,4},{9,5},{10,6},{11,7},{12,8},{13,9},{1... | collective-permute-start | bytes 688136 | tf_op jit(solution)/shard_map/ppermute | solution.py:146
  11.8 0.3 collective-permute-start.10
  12.0 1.5 %collective-permute-start.3 = (bf16[224,512]{1,0:T(8,128)(2,1)S(1)}, bf16[224,512]{1,0:T(8,128)(2,1)S(1)}, u32[]{:S(2)}, u32[]{:S(2)}) collective-permute-start(bf16[224,512]{1,0:T(8,128)(2,1)S(1)} %fusion.7.refs_0_), channel_id=1, source_target_pairs={{0,2},{1,3},{2,0},{3,1},{4,6},{5,7},{6,4},{7,5},{8,10},{9,11},{10,... | collective-permute-start | bytes 688136 | tf_op jit(solution)/shard_map/ppermute | solution.py:147
  13.6 2.4 %collective-permute-done.1.refs_1_ = bf16[224,512]{1,0:T(8,128)(2,1)S(1)} collective-permute-done((bf16[224,512]{1,0:T(8,128)(2,1)S(1)}, bf16[224,512]{1,0:T(8,128)(2,1)S(1)}, u32[]{:S(2)}, u32[]{:S(2)}) %collective-permute-start.1) | collective-permute-done | bytes 229408 | tf_op jit(solution)/shard_map/ppermute | solution.py:145
  15.9 4.1 %collective-permute-done.2.refs_2_ = bf16[224,512]{1,0:T(8,128)(2,1)S(1)} collective-permute-done((bf16[224,512]{1,0:T(8,128)(2,1)S(1)}, bf16[224,512]{1,0:T(8,128)(2,1)S(1)}, u32[]{:S(2)}, u32[]{:S(2)}) %collective-permute-start.2) | collective-permute-done | bytes 229408 | tf_op jit(solution)/shard_map/ppermute | solution.py:146
  20.1 3.5 %collective-permute-start.4 = (bf16[224,512]{1,0:T(8,128)(2,1)S(1)}, bf16[224,512]{1,0:T(8,128)(2,1)S(1)}, u32[]{:S(2)}, u32[]{:S(2)}) collective-permute-start(bf16[224,512]{1,0:T(8,128)(2,1)S(1)} %collective-permute-done.1.refs_1_), channel_id=1, source_target_pairs={{0,4},{1,5},{2,6},{3,7},{4,8},{5,9},{6,10},{7,11},{8,12},{9,13},{1... | collective-permute-start | bytes 688136 | tf_op jit(solution)/shard_map/ppermute | solution.py:150
  23.6 1.3 %collective-permute-start.5 = (bf16[224,512]{1,0:T(8,128)(2,1)S(1)}, bf16[224,512]{1,0:T(8,128)(2,1)S(1)}, u32[]{:S(2)}, u32[]{:S(2)}) collective-permute-start(bf16[224,512]{1,0:T(8,128)(2,1)S(1)} %collective-permute-done.2.refs_2_), channel_id=1, source_target_pairs={{4,0},{5,1},{6,2},{7,3},{8,4},{9,5},{10,6},{11,7},{12,8},{13,9},{1... | collective-permute-start | bytes 688136 | tf_op jit(solution)/shard_map/ppermute | solution.py:151
  24.9 1.6 %collective-permute-start.6 = (bf16[224,512]{1,0:T(8,128)(2,1)S(1)}, bf16[224,512]{1,0:T(8,128)(2,1)S(1)}, u32[]{:S(2)}, u32[]{:S(2)}) collective-permute-start(bf16[224,512]{1,0:T(8,128)(2,1)S(1)} %broadcast_select_fusion.1), channel_id=1, source_target_pairs={{0,2},{1,3},{2,0},{3,1},{4,6},{5,7},{6,4},{7,5},{8,10},{9,11},{10,... | collective-permute-start | bytes 688136 | tf_op jit(solution)/shard_map/ppermute | solution.py:152
  26.6 0.2 copy.48
  26.9 0.9 %broadcast_divide_fusion.ro_ref = f32[1024,1]{1,0:T(8,128)} fusion(f32[1024,1]{1,0:T(8,128)S(1)} %copy.48), kind=kLoop, calls=%fused_computation.12 | loop fusion | flops 1024 | bytes 8192 | tf_op jit(solution)/shard_map/div | solution.py:240
  27.9 1.0 %copy.49.xo_ref = bf16[1024,192]{1,0:T(8,128)(2,1)} copy(bf16[1024,192]{0,1:T(8,128)(2,1)S(1)} %multiply_bitcast_fusion) | data formatting | bytes 786432 | tf_op jit(solution)/shard_map/transpose | solution.py:241
  28.9 1.0 %copy.50.no_ref = f32[1024,1]{1,0:T(8,128)} copy(f32[1024,1]{0,1:T(1,128)S(1)} %bitcast.76) | data formatting | bytes 8192 | tf_op jit(solution)/shard_map/broadcast_in_dim | solution.py:238
  29.9 2.1 %collective-permute-done.5.refs_5_ = bf16[224,512]{1,0:T(8,128)(2,1)S(1)} collective-permute-done((bf16[224,512]{1,0:T(8,128)(2,1)S(1)}, bf16[224,512]{1,0:T(8,128)(2,1)S(1)}, u32[]{:S(2)}, u32[]{:S(2)}) %collective-permute-start.5) | collective-permute-done | bytes 229408 | tf_op jit(solution)/shard_map/ppermute | solution.py:151
  32.1 1.6 %collective-permute-start.9 = (bf16[224,512]{1,0:T(8,128)(2,1)S(1)}, bf16[224,512]{1,0:T(8,128)(2,1)S(1)}, u32[]{:S(2)}, u32[]{:S(2)}) collective-permute-start(bf16[224,512]{1,0:T(8,128)(2,1)S(1)} %broadcast_select_fusion), channel_id=1, source_target_pairs={{0,2},{1,3},{2,0},{3,1},{4,6},{5,7},{6,4},{7,5},{8,10},{9,11},{10,... | collective-permute-start | bytes 688136 | tf_op jit(solution)/shard_map/ppermute | solution.py:155
  33.8 3.6 %collective-permute-start.7 = (bf16[224,512]{1,0:T(8,128)(2,1)S(1)}, bf16[224,512]{1,0:T(8,128)(2,1)S(1)}, u32[]{:S(2)}, u32[]{:S(2)}) collective-permute-start(bf16[224,512]{1,0:T(8,128)(2,1)S(1)} %collective-permute-done.4.refs_4_), channel_id=1, source_target_pairs={{0,4},{1,5},{2,6},{3,7},{4,8},{5,9},{6,10},{7,11},{8,12},{9,13},{1... | collective-permute-start | bytes 688136 | tf_op jit(solution)/shard_map/ppermute | solution.py:153
  37.4 1.3 %collective-permute-start.8 = (bf16[224,512]{1,0:T(8,128)(2,1)S(1)}, bf16[224,512]{1,0:T(8,128)(2,1)S(1)}, u32[]{:S(2)}, u32[]{:S(2)}) collective-permute-start(bf16[224,512]{1,0:T(8,128)(2,1)S(1)} %collective-permute-done.5.refs_5_), channel_id=1, source_target_pairs={{4,0},{5,1},{6,2},{7,3},{8,4},{9,5},{10,6},{11,7},{12,8},{13,9},{1... | collective-permute-start | bytes 688136 | tf_op jit(solution)/shard_map/ppermute | solution.py:154
  38.7 6.5 %shard_map.95 = f32[7,16,1024]{2,1,0:T(8,128)} custom-call(s32[7]{0:T(128)} %convert_element_type.35.flag_ref, bf16[1024,192]{1,0:T(8,128)(2,1)} %copy.49.xo_ref, f32[1024,1]{1,0:T(8,128)} %copy.50.no_ref, f32[1024,1]{1,0:T(8,128)} %broadcast_divide_fusion.ro_ref, bf16[224,512]{1,0:T(8,128)(2,1)} %copy-done.7, bf16[224,512]{1,0:T(8,128)(2,1)} %copy-done.2, ...), custom_call_target="tpu_custom_call" | custom-call | flops 1526726656 | bytes 2064384 | tf_op jit(solution)/shard_map/pallas_call | solution.py:97
  45.2 0.7 slice_bitcast_fusion.7
  46.0 0.6 collective-permute-start.11
  46.6 5.4 %collective-permute-done.11.refs_3_ = bf16[224,512]{1,0:T(8,128)(2,1)S(1)} collective-permute-done((bf16[224,512]{1,0:T(8,128)(2,1)S(1)}, bf16[224,512]{1,0:T(8,128)(2,1)S(1)}, u32[]{:S(2)}, u32[]{:S(2)}) %collective-permute-start.11) | collective-permute-done | bytes 229408 | tf_op jit(solution)/shard_map/ppermute | solution.py:163
  52.2 0.2 slice_reduce_fusion
  53.1 0.2 and_reduce_fusion
  53.3 0.6 slice.80.flag_ref
  54.0 3.8 %shard_map.96 = f32[16,1024]{1,0:T(8,128)} custom-call(s32[4]{0:T(128)} %slice.80.flag_ref, bf16[1024,192]{1,0:T(8,128)(2,1)} %copy.49.xo_ref, f32[1024,1]{1,0:T(8,128)} %copy.50.no_ref, f32[1024,1]{1,0:T(8,128)} %broadcast_divide_fusion.ro_ref, bf16[224,512]{1,0:T(8,128)(2,1)} %copy-done.8, bf16[224,512]{1,0:T(8,128)(2,1)} %copy-done.9, ...), custom_call_target="tpu_custom_call" | custom-call | flops 872415232 | bytes 983040 | tf_op jit(solution)/shard_map/pallas_call | solution.py:97
  57.8 0.8 %add.65 = f32[16,1024]{1,0:T(8,128)S(1)} add(f32[16,1024]{1,0:T(8,128)} %shard_map.96, f32[16,1024]{1,0:T(8,128)S(1)} %select_reduce_fusion) | non-fusion elementwise | flops 16384 | bytes 196608 | tf_op jit(solution)/shard_map/add | solution.py:274
  58.8 0.6 copy-done.13
  59.3 0.6 collective-permute-done.12
  60.0 0.1 convolution_bitcast_fusion
  60.1 1.1 %collective-permute-start.13 = (f32[16,16]{0,1:T(8,128)S(1)}, f32[16,16]{0,1:T(8,128)S(1)}, u32[]{:S(2)}, u32[]{:S(2)}) collective-permute-start(f32[16,16]{0,1:T(8,128)S(1)} %convolution_bitcast_fusion), channel_id=1, source_target_pairs={{0,3},{1,2},{2,1},{3,0},{4,7},{5,6},{6,5},{7,4},{8,11},{9,10},{10,... | collective-permute-start | bytes 3080 | tf_op jit(solution)/shard_map/ppermute | solution.py:193
  61.2 0.7 %collective-permute-start.14 = (f32[16,16]{0,1:T(8,128)S(1)}, f32[16,16]{0,1:T(8,128)S(1)}, u32[]{:S(2)}, u32[]{:S(2)}) collective-permute-start(f32[16,16]{0,1:T(8,128)S(1)} %convolution_bitcast_fusion), channel_id=1, source_target_pairs={{0,2},{1,3},{2,0},{3,1},{4,6},{5,7},{6,4},{7,5},{8,10},{9,11},{10,... | collective-permute-start | bytes 3080 | tf_op jit(solution)/shard_map/ppermute | solution.py:193
  62.0 1.2 %collective-permute-done.13 = f32[16,16]{0,1:T(8,128)S(1)} collective-permute-done((f32[16,16]{0,1:T(8,128)S(1)}, f32[16,16]{0,1:T(8,128)S(1)}, u32[]{:S(2)}, u32[]{:S(2)}) %collective-permute-start.13) | collective-permute-done | bytes 1056 | tf_op jit(solution)/shard_map/ppermute | solution.py:193
  63.2 1.6 %collective-permute-done.14 = f32[16,16]{0,1:T(8,128)S(1)} collective-permute-done((f32[16,16]{0,1:T(8,128)S(1)}, f32[16,16]{0,1:T(8,128)S(1)}, u32[]{:S(2)}, u32[]{:S(2)}) %collective-permute-start.14) | collective-permute-done | bytes 1056 | tf_op jit(solution)/shard_map/ppermute | solution.py:193
  64.8 2.6 %collective-permute-start.16 = (f32[16,16]{0,1:T(8,128)S(1)}, f32[16,16]{0,1:T(8,128)S(1)}, u32[]{:S(2)}, u32[]{:S(2)}) collective-permute-start(f32[16,16]{0,1:T(8,128)S(1)} %select_add_fusion), channel_id=1, source_target_pairs={{0,12},{1,13},{2,14},{3,15},{4,8},{5,9},{6,10},{7,11},{8,4},{9,5},... | collective-permute-start | bytes 3080 | tf_op jit(solution)/shard_map/ppermute | solution.py:193
  67.4 1.6 %collective-permute-start.17 = (f32[16,16]{0,1:T(8,128)S(1)}, f32[16,16]{0,1:T(8,128)S(1)}, u32[]{:S(2)}, u32[]{:S(2)}) collective-permute-start(f32[16,16]{0,1:T(8,128)S(1)} %select_add_fusion), channel_id=1, source_target_pairs={{0,8},{1,9},{2,10},{3,11},{4,12},{5,13},{6,14},{7,15},{8,0},{9,1},... | collective-permute-start | bytes 3080 | tf_op jit(solution)/shard_map/ppermute | solution.py:193
  69.0 0.3 collective-permute-start.18
  69.3 0.1 fusion.16
  69.5 1.0 %collective-permute-done.16 = f32[16,16]{0,1:T(8,128)S(1)} collective-permute-done((f32[16,16]{0,1:T(8,128)S(1)}, f32[16,16]{0,1:T(8,128)S(1)}, u32[]{:S(2)}, u32[]{:S(2)}) %collective-permute-start.16) | collective-permute-done | bytes 1056 | tf_op jit(solution)/shard_map/ppermute | solution.py:193
  70.4 1.6 %collective-permute-done.17 = f32[16,16]{0,1:T(8,128)S(1)} collective-permute-done((f32[16,16]{0,1:T(8,128)S(1)}, f32[16,16]{0,1:T(8,128)S(1)}, u32[]{:S(2)}, u32[]{:S(2)}) %collective-permute-start.17) | collective-permute-done | bytes 1056 | tf_op jit(solution)/shard_map/ppermute | solution.py:193
  72.0 0.7 collective-permute-done.18
  72.7 0.7 copy.56
  73.4 0.8 %fusion = f32[16,512]{1,0:T(8,128)} fusion(f32[16,512]{1,0:T(8,128)S(1)} %fusion.16, f32[16,16]{0,1:T(8,128)S(1)} %add_multiply_fusion, f32[16,512]{1,0:T(8,128)S(1)} %copy-done.5, f32[512]{0:T(512)S(1)} %broadcast_multiply_fusion, f32[16,512]{1,0:T(8,128)S(1)} %collective-permute-done.12, f32[16,1024]{1,0:T(8,128)S(1)} %add.65), kind=kOutput, calls=%fused_computation.1 | convolution fusion | flops 1605632 | bytes 166912 | tf_op jit(solution)/shard_map/dot_general | solution.py:284
  (95 shorter events, 2.3 us)
Async XLA Ops:
  0.6 68.7 %copy-start = (f32[16,512]{1,0:T(8,128)S(1)}, f32[16,512]{1,0:T(8,128)}, u32[]{:S(2)}) copy-start(f32[16,512]{1,0:T(8,128)} %param.12) | copy-start | bytes 98308
  0.6 5.3 %copy-start.1 = (bf16[192,512]{1,0:T(8,128)(2,1)S(1)}, bf16[192,512]{1,0:T(8,128)(2,1)}, u32[]{:S(2)}) copy-start(bf16[192,512]{1,0:T(8,128)(2,1)} %param.8) | copy-start | bytes 589828
  2.3 3.5 %collective-permute-start = (bf16[9]{0:T(256)(128)(2,1)S(1)}, bf16[9]{0:T(256)(128)(2,1)S(1)}, u32[]{:S(2)}, u32[]{:S(2)}) collective-permute-start(bf16[9]{0:T(256)(128)(2,1)S(1)} %pad_maximum_fusion.1), channel_id=1, source_target_pairs={{0,1},{1,0},{2,3},{3,2},{4,5},{5,4},{6,7},{7,6},{8,9},{9,8},{10,11... | collective-permute-start | bytes 62 | tf_op jit(solution)/shard_map/ppermute | solution.py:225
  5.9 14.2 %copy-start.7 = (bf16[224,512]{1,0:T(8,128)(2,1)}, bf16[224,512]{1,0:T(8,128)(2,1)S(1)}, u32[]{:S(2)}) copy-start(bf16[224,512]{1,0:T(8,128)(2,1)S(1)} %fusion.7.refs_0_) | copy-start | bytes 688132
  5.9 10.0 %collective-permute-start.1 = (bf16[224,512]{1,0:T(8,128)(2,1)S(1)}, bf16[224,512]{1,0:T(8,128)(2,1)S(1)}, u32[]{:S(2)}, u32[]{:S(2)}) collective-permute-start(bf16[224,512]{1,0:T(8,128)(2,1)S(1)} %fusion.7.refs_0_), channel_id=1, source_target_pairs={{0,4},{1,5},{2,6},{3,7},{4,8},{5,9},{6,10},{7,11},{8,12},{9,13},{1... | collective-permute-start | bytes 688136 | tf_op jit(solution)/shard_map/ppermute | solution.py:145
  10.5 9.6 %collective-permute-start.2 = (bf16[224,512]{1,0:T(8,128)(2,1)S(1)}, bf16[224,512]{1,0:T(8,128)(2,1)S(1)}, u32[]{:S(2)}, u32[]{:S(2)}) collective-permute-start(bf16[224,512]{1,0:T(8,128)(2,1)S(1)} %fusion.7.refs_0_), channel_id=1, source_target_pairs={{4,0},{5,1},{6,2},{7,3},{8,4},{9,5},{10,6},{11,7},{12,8},{13,9},{1... | collective-permute-start | bytes 688136 | tf_op jit(solution)/shard_map/ppermute | solution.py:146
  11.8 14.7 %collective-permute-start.10 = (bf16[224,512]{1,0:T(8,128)(2,1)S(1)}, bf16[224,512]{1,0:T(8,128)(2,1)S(1)}, u32[]{:S(2)}, u32[]{:S(2)}) collective-permute-start(bf16[224,512]{1,0:T(8,128)(2,1)S(1)} %fusion.7.refs_0_), channel_id=1, source_target_pairs={{0,1},{1,0},{2,3},{3,2},{4,5},{5,4},{6,7},{7,6},{8,9},{9,8},{10,11... | collective-permute-start | bytes 688136 | tf_op jit(solution)/shard_map/ppermute | solution.py:233
  12.0 15.7 %collective-permute-start.3 = (bf16[224,512]{1,0:T(8,128)(2,1)S(1)}, bf16[224,512]{1,0:T(8,128)(2,1)S(1)}, u32[]{:S(2)}, u32[]{:S(2)}) collective-permute-start(bf16[224,512]{1,0:T(8,128)(2,1)S(1)} %fusion.7.refs_0_), channel_id=1, source_target_pairs={{0,2},{1,3},{2,0},{3,1},{4,6},{5,7},{6,4},{7,5},{8,10},{9,11},{10,... | collective-permute-start | bytes 688136 | tf_op jit(solution)/shard_map/ppermute | solution.py:147
  15.9 14.0 %copy-start.2 = (bf16[224,512]{1,0:T(8,128)(2,1)}, bf16[224,512]{1,0:T(8,128)(2,1)S(1)}, u32[]{:S(2)}) copy-start(bf16[224,512]{1,0:T(8,128)(2,1)S(1)} %collective-permute-done.1.refs_1_) | copy-start | bytes 688132
  20.1 9.8 %copy-start.6 = (bf16[224,512]{1,0:T(8,128)(2,1)}, bf16[224,512]{1,0:T(8,128)(2,1)S(1)}, u32[]{:S(2)}) copy-start(bf16[224,512]{1,0:T(8,128)(2,1)S(1)} %collective-permute-done.2.refs_2_) | copy-start | bytes 688132
  20.1 9.8 %collective-permute-start.4 = (bf16[224,512]{1,0:T(8,128)(2,1)S(1)}, bf16[224,512]{1,0:T(8,128)(2,1)S(1)}, u32[]{:S(2)}, u32[]{:S(2)}) collective-permute-start(bf16[224,512]{1,0:T(8,128)(2,1)S(1)} %collective-permute-done.1.refs_1_), channel_id=1, source_target_pairs={{0,4},{1,5},{2,6},{3,7},{4,8},{5,9},{6,10},{7,11},{8,12},{9,13},{1... | collective-permute-start | bytes 688136 | tf_op jit(solution)/shard_map/ppermute | solution.py:150
  23.6 8.5 %collective-permute-start.5 = (bf16[224,512]{1,0:T(8,128)(2,1)S(1)}, bf16[224,512]{1,0:T(8,128)(2,1)S(1)}, u32[]{:S(2)}, u32[]{:S(2)}) collective-permute-start(bf16[224,512]{1,0:T(8,128)(2,1)S(1)} %collective-permute-done.2.refs_2_), channel_id=1, source_target_pairs={{4,0},{5,1},{6,2},{7,3},{8,4},{9,5},{10,6},{11,7},{12,8},{13,9},{1... | collective-permute-start | bytes 688136 | tf_op jit(solution)/shard_map/ppermute | solution.py:151
  24.9 8.8 %collective-permute-start.6 = (bf16[224,512]{1,0:T(8,128)(2,1)S(1)}, bf16[224,512]{1,0:T(8,128)(2,1)S(1)}, u32[]{:S(2)}, u32[]{:S(2)}) collective-permute-start(bf16[224,512]{1,0:T(8,128)(2,1)S(1)} %broadcast_select_fusion.1), channel_id=1, source_target_pairs={{0,2},{1,3},{2,0},{3,1},{4,6},{5,7},{6,4},{7,5},{8,10},{9,11},{10,... | collective-permute-start | bytes 688136 | tf_op jit(solution)/shard_map/ppermute | solution.py:152
  27.7 1.1 %copy-start.15 = (bf16[224,512]{1,0:T(8,128)(2,1)}, bf16[224,512]{1,0:T(8,128)(2,1)S(1)}, u32[]{:S(2)}) copy-start(bf16[224,512]{1,0:T(8,128)(2,1)S(1)} %collective-permute-done.3.refs_3_) | copy-start | bytes 688132
  29.9 3.8 %copy-start.10 = (bf16[224,512]{1,0:T(8,128)(2,1)}, bf16[224,512]{1,0:T(8,128)(2,1)S(1)}, u32[]{:S(2)}) copy-start(bf16[224,512]{1,0:T(8,128)(2,1)S(1)} %collective-permute-done.4.refs_4_) | copy-start | bytes 688132
  32.1 5.3 %copy-start.11 = (bf16[224,512]{1,0:T(8,128)(2,1)}, bf16[224,512]{1,0:T(8,128)(2,1)S(1)}, u32[]{:S(2)}) copy-start(bf16[224,512]{1,0:T(8,128)(2,1)S(1)} %collective-permute-done.5.refs_5_) | copy-start | bytes 688132
  32.1 14.4 %collective-permute-start.9 = (bf16[224,512]{1,0:T(8,128)(2,1)S(1)}, bf16[224,512]{1,0:T(8,128)(2,1)S(1)}, u32[]{:S(2)}, u32[]{:S(2)}) collective-permute-start(bf16[224,512]{1,0:T(8,128)(2,1)S(1)} %broadcast_select_fusion), channel_id=1, source_target_pairs={{0,2},{1,3},{2,0},{3,1},{4,6},{5,7},{6,4},{7,5},{8,10},{9,11},{10,... | collective-permute-start | bytes 688136 | tf_op jit(solution)/shard_map/ppermute | solution.py:155
  33.7 5.0 %copy-start.17 = (bf16[224,512]{1,0:T(8,128)(2,1)}, bf16[224,512]{1,0:T(8,128)(2,1)S(1)}, u32[]{:S(2)}) copy-start(bf16[224,512]{1,0:T(8,128)(2,1)S(1)} %collective-permute-done.6.refs_6_) | copy-start | bytes 688132
  33.7 12.1 %copy-start.3 = (bf16[224,512]{1,0:T(8,128)(2,1)S(1)}, bf16[224,512]{1,0:T(8,128)(2,1)}, u32[]{:S(2)}) copy-start(bf16[224,512]{1,0:T(8,128)(2,1)} %copy-done.2) | copy-start | bytes 688132
  33.8 12.1 %collective-permute-start.7 = (bf16[224,512]{1,0:T(8,128)(2,1)S(1)}, bf16[224,512]{1,0:T(8,128)(2,1)S(1)}, u32[]{:S(2)}, u32[]{:S(2)}) collective-permute-start(bf16[224,512]{1,0:T(8,128)(2,1)S(1)} %collective-permute-done.4.refs_4_), channel_id=1, source_target_pairs={{0,4},{1,5},{2,6},{3,7},{4,8},{5,9},{6,10},{7,11},{8,12},{9,13},{1... | collective-permute-start | bytes 688136 | tf_op jit(solution)/shard_map/ppermute | solution.py:153
  37.4 8.5 %collective-permute-start.8 = (bf16[224,512]{1,0:T(8,128)(2,1)S(1)}, bf16[224,512]{1,0:T(8,128)(2,1)S(1)}, u32[]{:S(2)}, u32[]{:S(2)}) collective-permute-start(bf16[224,512]{1,0:T(8,128)(2,1)S(1)} %collective-permute-done.5.refs_5_), channel_id=1, source_target_pairs={{4,0},{5,1},{6,2},{7,3},{8,4},{9,5},{10,6},{11,7},{12,8},{13,9},{1... | collective-permute-start | bytes 688136 | tf_op jit(solution)/shard_map/ppermute | solution.py:154
  45.9 8.0 %copy-start.4 = (f32[7,16,1024]{2,1,0:T(8,128)S(1)}, f32[7,16,1024]{2,1,0:T(8,128)}, u32[]{:S(2)}) copy-start(f32[7,16,1024]{2,1,0:T(8,128)} %shard_map.95) | copy-start | bytes 1376260
  45.9 0.8 %copy-start.8 = (bf16[224,512]{1,0:T(8,128)(2,1)}, bf16[224,512]{1,0:T(8,128)(2,1)S(1)}, u32[]{:S(2)}) copy-start(bf16[224,512]{1,0:T(8,128)(2,1)S(1)} %collective-permute-done.7.refs_0_) | copy-start | bytes 688132
  45.9 0.7 copy-start.9
  46.0 6.1 %collective-permute-start.11 = (bf16[224,512]{1,0:T(8,128)(2,1)S(1)}, bf16[224,512]{1,0:T(8,128)(2,1)S(1)}, u32[]{:S(2)}, u32[]{:S(2)}) collective-permute-start(bf16[224,512]{1,0:T(8,128)(2,1)S(1)} %select_select_fusion), channel_id=1, source_target_pairs={{0,2},{1,3},{2,0},{3,1},{4,6},{5,7},{6,4},{7,5},{8,10},{9,11},{10,... | collective-permute-start | bytes 688136 | tf_op jit(solution)/shard_map/ppermute | solution.py:163
  46.5 7.4 %copy-start.14 = (bf16[224,512]{1,0:T(8,128)(2,1)}, bf16[224,512]{1,0:T(8,128)(2,1)S(1)}, u32[]{:S(2)}) copy-start(bf16[224,512]{1,0:T(8,128)(2,1)S(1)} %collective-permute-done.9.refs_2_) | copy-start | bytes 688132
  52.0 1.9 %copy-start.16 = (bf16[224,512]{1,0:T(8,128)(2,1)}, bf16[224,512]{1,0:T(8,128)(2,1)S(1)}, u32[]{:S(2)}) copy-start(bf16[224,512]{1,0:T(8,128)(2,1)S(1)} %collective-permute-done.11.refs_3_) | copy-start | bytes 688132
  58.6 0.7 copy-start.13
  58.7 1.3 %copy-start.5 = (f32[16,512]{1,0:T(8,128)S(1)}, f32[16,512]{1,0:T(8,128)}, u32[]{:S(2)}) copy-start(f32[16,512]{1,0:T(8,128)} %param.11) | copy-start | bytes 98308
  58.7 1.3 %collective-permute-start.12 = (f32[16,512]{1,0:T(8,128)S(1)}, f32[16,512]{1,0:T(8,128)S(1)}, u32[]{:S(2)}, u32[]{:S(2)}) collective-permute-start(f32[16,512]{1,0:T(8,128)S(1)} %slice.102), channel_id=1, source_target_pairs={{0,1},{1,0},{2,3},{3,2},{4,5},{5,4},{6,7},{7,6},{8,9},{9,8},{10,11... | collective-permute-start | bytes 98312 | tf_op jit(solution)/shard_map/ppermute | solution.py:278
  60.1 3.1 %collective-permute-start.13 = (f32[16,16]{0,1:T(8,128)S(1)}, f32[16,16]{0,1:T(8,128)S(1)}, u32[]{:S(2)}, u32[]{:S(2)}) collective-permute-start(f32[16,16]{0,1:T(8,128)S(1)} %convolution_bitcast_fusion), channel_id=1, source_target_pairs={{0,3},{1,2},{2,1},{3,0},{4,7},{5,6},{6,5},{7,4},{8,11},{9,10},{10,... | collective-permute-start | bytes 3080 | tf_op jit(solution)/shard_map/ppermute | solution.py:193
  61.2 3.7 %collective-permute-start.14 = (f32[16,16]{0,1:T(8,128)S(1)}, f32[16,16]{0,1:T(8,128)S(1)}, u32[]{:S(2)}, u32[]{:S(2)}) collective-permute-start(f32[16,16]{0,1:T(8,128)S(1)} %convolution_bitcast_fusion), channel_id=1, source_target_pairs={{0,2},{1,3},{2,0},{3,1},{4,6},{5,7},{6,4},{7,5},{8,10},{9,11},{10,... | collective-permute-start | bytes 3080 | tf_op jit(solution)/shard_map/ppermute | solution.py:193
  61.9 2.9 %collective-permute-start.15 = (f32[16,16]{0,1:T(8,128)S(1)}, f32[16,16]{0,1:T(8,128)S(1)}, u32[]{:S(2)}, u32[]{:S(2)}) collective-permute-start(f32[16,16]{0,1:T(8,128)S(1)} %convolution_bitcast_fusion), channel_id=1, source_target_pairs={{0,1},{1,0},{2,3},{3,2},{4,5},{5,4},{6,7},{7,6},{8,9},{9,8},{10,11... | collective-permute-start | bytes 3080 | tf_op jit(solution)/shard_map/ppermute | solution.py:193
  62.0 7.3 %copy-start.12 = (f32[16,16]{1,0:T(8,128)S(1)}, f32[16,16]{1,0:T(8,128)}, u32[]{:S(2)}) copy-start(f32[16,16]{1,0:T(8,128)} %param.13) | copy-start | bytes 3076
  64.8 5.6 %collective-permute-start.16 = (f32[16,16]{0,1:T(8,128)S(1)}, f32[16,16]{0,1:T(8,128)S(1)}, u32[]{:S(2)}, u32[]{:S(2)}) collective-permute-start(f32[16,16]{0,1:T(8,128)S(1)} %select_add_fusion), channel_id=1, source_target_pairs={{0,12},{1,13},{2,14},{3,15},{4,8},{5,9},{6,10},{7,11},{8,4},{9,5},... | collective-permute-start | bytes 3080 | tf_op jit(solution)/shard_map/ppermute | solution.py:193
  67.4 4.5 %collective-permute-start.17 = (f32[16,16]{0,1:T(8,128)S(1)}, f32[16,16]{0,1:T(8,128)S(1)}, u32[]{:S(2)}, u32[]{:S(2)}) collective-permute-start(f32[16,16]{0,1:T(8,128)S(1)} %select_add_fusion), channel_id=1, source_target_pairs={{0,8},{1,9},{2,10},{3,11},{4,12},{5,13},{6,14},{7,15},{8,0},{9,1},... | collective-permute-start | bytes 3080 | tf_op jit(solution)/shard_map/ppermute | solution.py:193
  69.0 3.7 %collective-permute-start.18 = (f32[16,16]{0,1:T(8,128)S(1)}, f32[16,16]{0,1:T(8,128)S(1)}, u32[]{:S(2)}, u32[]{:S(2)}) collective-permute-start(f32[16,16]{0,1:T(8,128)S(1)} %select_add_fusion), channel_id=1, source_target_pairs={{0,4},{1,5},{2,6},{3,7},{4,0},{5,1},{6,2},{7,3},{8,12},{9,13},{10,... | collective-permute-start | bytes 3080 | tf_op jit(solution)/shard_map/ppermute | solution.py:193

commit v14 on v13

--- a/solution.py
+++ b/solution.py
@@ -270,8 +270,11 @@
 
     if chip_split:
         head = early.shape[0]
-        summed = list_product(flags[head:], own_terms, pieces[head:], width, rows)
-        summed = summed + jnp.sum(jnp.where(flags[:head, None, None] != 0, early, 0.0), axis=0)
+        tail = len(pieces) - 1
+        middle = list_product(valid[head:tail], own_terms, pieces[head:tail], width, rows, split=True)
+        parts = jnp.concatenate([early, middle])
+        summed = list_product(flags[tail:], own_terms, pieces[tail:], width, rows)
+        summed = summed + jnp.sum(jnp.where(flags[:tail, None, None] != 0, parts, 0.0), axis=0)
     else:
         summed = own_rows_product(flags, own_terms, pieces[0].reshape(devices, rows, own), width)
     if chip_split:

time: 74.7 us -> 77.1 us (1.032)
  waiting for transfers between devices: 20.7 us -> 14.7 us
  Pallas kernels: 10.3 us -> 13.8 us
  local copies, waits for them, and re-layouts: 7.75 us -> 10.9 us
  other arithmetic: 4.72 us -> 6.25 us
    ppermute x1, waiting for transfers between devices: 5.4 us -> 0.26 us  [gather_pieces(): across4 = lax.ppermute(last, 'row', across)]
    pallas_call x2 -> x3, Pallas kernels: 10.3 us -> 13.8 us  [list_product(): pl.pallas_call(functools.partial(list_kernel, width, rows, counts, split)...]
    unnamed x37, local copies, waits for them, and re-layouts: 1.4 us -> 3.86 us
    reduce_sum x1, other arithmetic: 0.1 us -> 1.05 us  [shards(): jnp.sum(jnp.where(flags[:tail, None, None] != 0, parts, 0.0), axis=0)]
  transfers between devices with their start and end apart: 19 -> 19, of which waited for: 10 -> 10; matrix products, arithmetic and copies ran while one was open for 10% -> 11% of each run, Pallas kernels for 9% -> 14%
where the time goes in v14:
time: 77.1 us; the launch traced here: 76.4 us
  starting transfers between devices  28 us (36%)
  waiting for transfers between devices  14.7 us (19%)
  Pallas kernels  13.8 us (18%)
  local copies, waits for them, and re-layouts  10.9 us (14%)
  other arithmetic  6.25 us (8%)
  between operations  1.72 us (2%)
  matrix products  1.07 us (1%)
    pallas_call x3, Pallas kernels, list_product(): pl.pallas_call(functools.partial(list_kernel, width, rows, counts, split)...  13.8 us
    ppermute x6, starting transfers between devices, sum_over_rows(): lax.ppermute(value, 'row', [(i, i ^ m << shift) for i in range(devices)])  6.84 us
    ppermute x6, waiting for transfers between devices, sum_over_rows(): lax.ppermute(value, 'row', [(i, i ^ m << shift) for i in range(devices)])  5.54 us
    ppermute x1, starting transfers between devices, gather_pieces(): up1 = lax.ppermute(packed, 'row', up)  4.53 us
    ppermute x1, waiting for transfers between devices, gather_pieces(): down1 = lax.ppermute(packed, 'row', down)  4.12 us
    unnamed x37, local copies, waits for them, and re-layouts  3.86 us
    ppermute x1, starting transfers between devices, gather_pieces(): up2 = lax.ppermute(up1, 'row', up)  3.48 us
    ppermute x1, starting transfers between devices, gather_pieces(): up3 = lax.ppermute(up2, 'row', up)  3.47 us
  transfers between devices with their start and end apart: 19, of which 10 were waited for; matrix products, arithmetic and copies ran while one was open for 11% of the time, Pallas kernels for 14%

profile of v14, /device:TPU:0, one launch (start us, length us, event | category | flops | bytes accessed | tf_op | source)
XLA Modules:
  0.0 76.4 jit_solution(13120395524482378278)
XLA Ops:
  1.3 0.7 convert.8
  2.3 0.5 collective-permute-start
  2.8 0.7 broadcast_in_dim.27
  3.4 0.7 concatenate.43
  4.4 0.6 convert_element_type.38.flag_ref
  5.1 0.6 slice_convert_fusion.flag_ref
  5.7 0.8 %multiply_convert_fusion = bf16[16,512]{1,0:T(8,128)(2,1)S(1)} fusion(f32[16,512]{1,0:T(8,128)} %param.11, f32[512]{0:T(512)} %param.10), kind=kLoop, calls=%fused_computation.22 | loop fusion | flops 16384 | bytes 51200 | tf_op jit(solution)/shard_map/convert_element_type | solution.py:221
  6.6 4.5 %collective-permute-start.1 = (bf16[224,512]{1,0:T(8,128)(2,1)S(1)}, bf16[224,512]{1,0:T(8,128)(2,1)S(1)}, u32[]{:S(2)}, u32[]{:S(2)}) collective-permute-start(bf16[224,512]{1,0:T(8,128)(2,1)S(1)} %fusion.8.refs_0_), channel_id=1, source_target_pairs={{0,4},{1,5},{2,6},{3,7},{4,8},{5,9},{6,10},{7,11},{8,12},{9,13},{1... | collective-permute-start | bytes 688136 | tf_op jit(solution)/shard_map/ppermute | solution.py:145
  11.1 1.3 %collective-permute-start.2 = (bf16[224,512]{1,0:T(8,128)(2,1)S(1)}, bf16[224,512]{1,0:T(8,128)(2,1)S(1)}, u32[]{:S(2)}, u32[]{:S(2)}) collective-permute-start(bf16[224,512]{1,0:T(8,128)(2,1)S(1)} %fusion.8.refs_0_), channel_id=1, source_target_pairs={{4,0},{5,1},{6,2},{7,3},{8,4},{9,5},{10,6},{11,7},{12,8},{13,9},{1... | collective-permute-start | bytes 688136 | tf_op jit(solution)/shard_map/ppermute | solution.py:146
  12.4 1.6 %collective-permute-start.3 = (bf16[224,512]{1,0:T(8,128)(2,1)S(1)}, bf16[224,512]{1,0:T(8,128)(2,1)S(1)}, u32[]{:S(2)}, u32[]{:S(2)}) collective-permute-start(bf16[224,512]{1,0:T(8,128)(2,1)S(1)} %fusion.8.refs_0_), channel_id=1, source_target_pairs={{0,2},{1,3},{2,0},{3,1},{4,6},{5,7},{6,4},{7,5},{8,10},{9,11},{10,... | collective-permute-start | bytes 688136 | tf_op jit(solution)/shard_map/ppermute | solution.py:147
  14.0 2.5 %collective-permute-done.1.refs_1_ = bf16[224,512]{1,0:T(8,128)(2,1)S(1)} collective-permute-done((bf16[224,512]{1,0:T(8,128)(2,1)S(1)}, bf16[224,512]{1,0:T(8,128)(2,1)S(1)}, u32[]{:S(2)}, u32[]{:S(2)}) %collective-permute-start.1) | collective-permute-done | bytes 229408 | tf_op jit(solution)/shard_map/ppermute | solution.py:145
  16.6 4.1 %collective-permute-done.2.refs_2_ = bf16[224,512]{1,0:T(8,128)(2,1)S(1)} collective-permute-done((bf16[224,512]{1,0:T(8,128)(2,1)S(1)}, bf16[224,512]{1,0:T(8,128)(2,1)S(1)}, u32[]{:S(2)}, u32[]{:S(2)}) %collective-permute-start.2) | collective-permute-done | bytes 229408 | tf_op jit(solution)/shard_map/ppermute | solution.py:146
  20.8 3.5 %collective-permute-start.4 = (bf16[224,512]{1,0:T(8,128)(2,1)S(1)}, bf16[224,512]{1,0:T(8,128)(2,1)S(1)}, u32[]{:S(2)}, u32[]{:S(2)}) collective-permute-start(bf16[224,512]{1,0:T(8,128)(2,1)S(1)} %collective-permute-done.1.refs_1_), channel_id=1, source_target_pairs={{0,4},{1,5},{2,6},{3,7},{4,8},{5,9},{6,10},{7,11},{8,12},{9,13},{1... | collective-permute-start | bytes 688136 | tf_op jit(solution)/shard_map/ppermute | solution.py:150
  24.2 1.3 %collective-permute-start.5 = (bf16[224,512]{1,0:T(8,128)(2,1)S(1)}, bf16[224,512]{1,0:T(8,128)(2,1)S(1)}, u32[]{:S(2)}, u32[]{:S(2)}) collective-permute-start(bf16[224,512]{1,0:T(8,128)(2,1)S(1)} %collective-permute-done.2.refs_2_), channel_id=1, source_target_pairs={{4,0},{5,1},{6,2},{7,3},{8,4},{9,5},{10,6},{11,7},{12,8},{13,9},{1... | collective-permute-start | bytes 688136 | tf_op jit(solution)/shard_map/ppermute | solution.py:151
  25.7 0.6 copy-done.15
  26.5 0.9 %broadcast_divide_fusion.ro_ref = f32[1024,1]{1,0:T(8,128)} fusion(f32[1024,1]{1,0:T(8,128)S(1)} %copy.55), kind=kLoop, calls=%fused_computation.13 | loop fusion | flops 1024 | bytes 8192 | tf_op jit(solution)/shard_map/div | solution.py:240
  27.5 1.6 %collective-permute-start.6 = (bf16[224,512]{1,0:T(8,128)(2,1)S(1)}, bf16[224,512]{1,0:T(8,128)(2,1)S(1)}, u32[]{:S(2)}, u32[]{:S(2)}) collective-permute-start(bf16[224,512]{1,0:T(8,128)(2,1)S(1)} %broadcast_select_fusion.1), channel_id=1, source_target_pairs={{0,2},{1,3},{2,0},{3,1},{4,6},{5,7},{6,4},{7,5},{8,10},{9,11},{10,... | collective-permute-start | bytes 688136 | tf_op jit(solution)/shard_map/ppermute | solution.py:152
  29.1 1.0 %copy.56.xo_ref = bf16[1024,192]{1,0:T(8,128)(2,1)} copy(bf16[1024,192]{0,1:T(8,128)(2,1)S(1)} %multiply_bitcast_fusion) | data formatting | bytes 786432 | tf_op jit(solution)/shard_map/transpose | solution.py:241
  30.1 1.0 %copy.57.no_ref = f32[1024,1]{1,0:T(8,128)} copy(f32[1024,1]{0,1:T(1,128)S(1)} %bitcast.77) | data formatting | bytes 8192 | tf_op jit(solution)/shard_map/broadcast_in_dim | solution.py:238
  31.2 1.6 %collective-permute-done.5.refs_5_ = bf16[224,512]{1,0:T(8,128)(2,1)S(1)} collective-permute-done((bf16[224,512]{1,0:T(8,128)(2,1)S(1)}, bf16[224,512]{1,0:T(8,128)(2,1)S(1)}, u32[]{:S(2)}, u32[]{:S(2)}) %collective-permute-start.5) | collective-permute-done | bytes 229408 | tf_op jit(solution)/shard_map/ppermute | solution.py:151
  32.8 1.6 %collective-permute-start.9 = (bf16[224,512]{1,0:T(8,128)(2,1)S(1)}, bf16[224,512]{1,0:T(8,128)(2,1)S(1)}, u32[]{:S(2)}, u32[]{:S(2)}) collective-permute-start(bf16[224,512]{1,0:T(8,128)(2,1)S(1)} %broadcast_select_fusion), channel_id=1, source_target_pairs={{0,2},{1,3},{2,0},{3,1},{4,6},{5,7},{6,4},{7,5},{8,10},{9,11},{10,... | collective-permute-start | bytes 688136 | tf_op jit(solution)/shard_map/ppermute | solution.py:155
  34.4 3.5 %collective-permute-start.7 = (bf16[224,512]{1,0:T(8,128)(2,1)S(1)}, bf16[224,512]{1,0:T(8,128)(2,1)S(1)}, u32[]{:S(2)}, u32[]{:S(2)}) collective-permute-start(bf16[224,512]{1,0:T(8,128)(2,1)S(1)} %collective-permute-done.4.refs_4_), channel_id=1, source_target_pairs={{0,4},{1,5},{2,6},{3,7},{4,8},{5,9},{6,10},{7,11},{8,12},{9,13},{1... | collective-permute-start | bytes 688136 | tf_op jit(solution)/shard_map/ppermute | solution.py:153
  37.8 1.3 %collective-permute-start.8 = (bf16[224,512]{1,0:T(8,128)(2,1)S(1)}, bf16[224,512]{1,0:T(8,128)(2,1)S(1)}, u32[]{:S(2)}, u32[]{:S(2)}) collective-permute-start(bf16[224,512]{1,0:T(8,128)(2,1)S(1)} %collective-permute-done.5.refs_5_), channel_id=1, source_target_pairs={{4,0},{5,1},{6,2},{7,3},{8,4},{9,5},{10,6},{11,7},{12,8},{13,9},{1... | collective-permute-start | bytes 688136 | tf_op jit(solution)/shard_map/ppermute | solution.py:154
  39.2 0.7 copy-done.17
  39.9 6.5 %shard_map.95 = f32[7,16,1024]{2,1,0:T(8,128)} custom-call(s32[7]{0:T(128)} %convert_element_type.38.flag_ref, bf16[1024,192]{1,0:T(8,128)(2,1)} %copy.56.xo_ref, f32[1024,1]{1,0:T(8,128)} %copy.57.no_ref, f32[1024,1]{1,0:T(8,128)} %broadcast_divide_fusion.ro_ref, bf16[224,512]{1,0:T(8,128)(2,1)} %copy-done.7, bf16[224,512]{1,0:T(8,128)(2,1)} %copy-done.2, ...), custom_call_target="tpu_custom_call" | custom-call | flops 1526726656 | bytes 2064384 | tf_op jit(solution)/shard_map/pallas_call | solution.py:97
  46.4 0.7 slice_bitcast_fusion.5
  47.1 0.6 copy-done.10
  47.8 0.5 collective-permute-start.11
  48.3 0.7 copy-done.16
  49.0 3.9 %shard_map.97 = f32[3,16,1024]{2,1,0:T(8,128)} custom-call(s32[3]{0:T(128)} %slice_convert_fusion.flag_ref, bf16[1024,192]{1,0:T(8,128)(2,1)} %copy.56.xo_ref, f32[1024,1]{1,0:T(8,128)} %copy.57.no_ref, f32[1024,1]{1,0:T(8,128)} %broadcast_divide_fusion.ro_ref, bf16[224,512]{1,0:T(8,128)(2,1)} %copy-done.10, bf16[224,512]{1,0:T(8,128)(2,1)} %copy-done.11, ...), custom_call_target="tpu_custom_call" | custom-call | flops 654311424 | bytes 884736 | tf_op jit(solution)/shard_map/pallas_call | solution.py:97
  52.8 0.7 slice_bitcast_fusion.2
  55.0 0.6 slice.84.flag_ref
  55.6 1.0 %fusion.1 = f32[16,1024]{1,0:T(8,128)S(1)} fusion(f32[3,16,1024]{2,1,0:T(8,128)} %shard_map.97, f32[7,16,1024]{2,1,0:T(8,128)S(1)} %copy-done.4, pred[10]{0:T(512)(128)(4,1)S(1)} %slice_compare_fusion), kind=kLoop, calls=%fused_computation.5 | loop fusion | flops 475136 | bytes 720906 | tf_op jit(solution)/shard_map/reduce_sum | solution.py:277
  56.7 3.5 %shard_map.96 = f32[16,1024]{1,0:T(8,128)} custom-call(s32[1]{0:T(128)} %slice.84.flag_ref, bf16[1024,192]{1,0:T(8,128)(2,1)} %copy.56.xo_ref, f32[1024,1]{1,0:T(8,128)} %copy.57.no_ref, f32[1024,1]{1,0:T(8,128)} %broadcast_divide_fusion.ro_ref, bf16[224,512]{1,0:T(8,128)(2,1)} %copy-done.12), custom_call_target="tpu_custom_call" | custom-call | flops 218103808 | bytes 294912 | tf_op jit(solution)/shard_map/pallas_call | solution.py:97
  60.1 0.8 %add.65 = f32[16,1024]{1,0:T(8,128)S(1)} add(f32[16,1024]{1,0:T(8,128)} %shard_map.96, f32[16,1024]{1,0:T(8,128)S(1)} %fusion.1) | non-fusion elementwise | flops 16384 | bytes 196608 | tf_op jit(solution)/shard_map/add | solution.py:277
  61.1 0.6 copy-done.14
  61.7 0.6 collective-permute-done.12
  62.4 0.3 collective-permute-start.13
  62.7 1.5 %collective-permute-start.14 = (f32[16,16]{0,1:T(8,128)S(1)}, f32[16,16]{0,1:T(8,128)S(1)}, u32[]{:S(2)}, u32[]{:S(2)}) collective-permute-start(f32[16,16]{0,1:T(8,128)S(1)} %convolution_bitcast_fusion), channel_id=1, source_target_pairs={{0,2},{1,3},{2,0},{3,1},{4,6},{5,7},{6,4},{7,5},{8,10},{9,11},{10,... | collective-permute-start | bytes 3080 | tf_op jit(solution)/shard_map/ppermute | solution.py:193
  64.3 1.2 %collective-permute-done.13 = f32[16,16]{0,1:T(8,128)S(1)} collective-permute-done((f32[16,16]{0,1:T(8,128)S(1)}, f32[16,16]{0,1:T(8,128)S(1)}, u32[]{:S(2)}, u32[]{:S(2)}) %collective-permute-start.13) | collective-permute-done | bytes 1056 | tf_op jit(solution)/shard_map/ppermute | solution.py:193
  65.5 0.8 %collective-permute-done.14 = f32[16,16]{0,1:T(8,128)S(1)} collective-permute-done((f32[16,16]{0,1:T(8,128)S(1)}, f32[16,16]{0,1:T(8,128)S(1)}, u32[]{:S(2)}, u32[]{:S(2)}) %collective-permute-start.14) | collective-permute-done | bytes 1056 | tf_op jit(solution)/shard_map/ppermute | solution.py:193
  66.4 2.7 %collective-permute-start.16 = (f32[16,16]{0,1:T(8,128)S(1)}, f32[16,16]{0,1:T(8,128)S(1)}, u32[]{:S(2)}, u32[]{:S(2)}) collective-permute-start(f32[16,16]{0,1:T(8,128)S(1)} %select_add_fusion), channel_id=1, source_target_pairs={{0,12},{1,13},{2,14},{3,15},{4,8},{5,9},{6,10},{7,11},{8,4},{9,5},... | collective-permute-start | bytes 3080 | tf_op jit(solution)/shard_map/ppermute | solution.py:193
  69.1 2.2 %collective-permute-start.17 = (f32[16,16]{0,1:T(8,128)S(1)}, f32[16,16]{0,1:T(8,128)S(1)}, u32[]{:S(2)}, u32[]{:S(2)}) collective-permute-start(f32[16,16]{0,1:T(8,128)S(1)} %select_add_fusion), channel_id=1, source_target_pairs={{0,8},{1,9},{2,10},{3,11},{4,12},{5,13},{6,14},{7,15},{8,0},{9,1},... | collective-permute-start | bytes 3080 | tf_op jit(solution)/shard_map/ppermute | solution.py:193
  71.5 0.4 collective-permute-done.16
  71.9 1.7 %collective-permute-done.17 = f32[16,16]{0,1:T(8,128)S(1)} collective-permute-done((f32[16,16]{0,1:T(8,128)S(1)}, f32[16,16]{0,1:T(8,128)S(1)}, u32[]{:S(2)}, u32[]{:S(2)}) %collective-permute-start.17) | collective-permute-done | bytes 1056 | tf_op jit(solution)/shard_map/ppermute | solution.py:193
  73.6 1.3 %collective-permute-done.18 = f32[16,16]{0,1:T(8,128)S(1)} collective-permute-done((f32[16,16]{0,1:T(8,128)S(1)}, f32[16,16]{0,1:T(8,128)S(1)}, u32[]{:S(2)}, u32[]{:S(2)}) %collective-permute-start.18) | collective-permute-done | bytes 1056 | tf_op jit(solution)/shard_map/ppermute | solution.py:193
  75.0 0.7 copy.65
  75.7 0.8 %fusion = f32[16,512]{1,0:T(8,128)} fusion(f32[16,512]{1,0:T(8,128)S(1)} %fusion.17, f32[16,16]{0,1:T(8,128)S(1)} %add_multiply_fusion, f32[16,512]{1,0:T(8,128)S(1)} %copy-done.5, f32[512]{0:T(512)S(1)} %broadcast_multiply_fusion, f32[16,512]{1,0:T(8,128)S(1)} %collective-permute-done.12, f32[16,1024]{1,0:T(8,128)S(1)} %add.65), kind=kOutput, calls=%fused_computation.1 | convolution fusion | flops 1605632 | bytes 166912 | tf_op jit(solution)/shard_map/dot_general | solution.py:287
  (98 shorter events, 3.4 us)
Async XLA Ops:
  0.6 70.7 %copy-start = (f32[16,512]{1,0:T(8,128)S(1)}, f32[16,512]{1,0:T(8,128)}, u32[]{:S(2)}) copy-start(f32[16,512]{1,0:T(8,128)} %param.12) | copy-start | bytes 98308
  0.6 5.9 %copy-start.1 = (bf16[192,512]{1,0:T(8,128)(2,1)S(1)}, bf16[192,512]{1,0:T(8,128)(2,1)}, u32[]{:S(2)}) copy-start(bf16[192,512]{1,0:T(8,128)(2,1)} %param.8) | copy-start | bytes 589828
  2.3 4.1 %collective-permute-start = (bf16[9]{0:T(256)(128)(2,1)S(1)}, bf16[9]{0:T(256)(128)(2,1)S(1)}, u32[]{:S(2)}, u32[]{:S(2)}) collective-permute-start(bf16[9]{0:T(256)(128)(2,1)S(1)} %pad_maximum_fusion.1), channel_id=1, source_target_pairs={{0,1},{1,0},{2,3},{3,2},{4,5},{5,4},{6,7},{7,6},{8,9},{9,8},{10,11... | collective-permute-start | bytes 62 | tf_op jit(solution)/shard_map/ppermute | solution.py:225
  6.6 14.2 %copy-start.7 = (bf16[224,512]{1,0:T(8,128)(2,1)}, bf16[224,512]{1,0:T(8,128)(2,1)S(1)}, u32[]{:S(2)}) copy-start(bf16[224,512]{1,0:T(8,128)(2,1)S(1)} %fusion.8.refs_0_) | copy-start | bytes 688132
  6.6 10.0 %collective-permute-start.1 = (bf16[224,512]{1,0:T(8,128)(2,1)S(1)}, bf16[224,512]{1,0:T(8,128)(2,1)S(1)}, u32[]{:S(2)}, u32[]{:S(2)}) collective-permute-start(bf16[224,512]{1,0:T(8,128)(2,1)S(1)} %fusion.8.refs_0_), channel_id=1, source_target_pairs={{0,4},{1,5},{2,6},{3,7},{4,8},{5,9},{6,10},{7,11},{8,12},{9,13},{1... | collective-permute-start | bytes 688136 | tf_op jit(solution)/shard_map/ppermute | solution.py:145
  11.1 9.6 %collective-permute-start.2 = (bf16[224,512]{1,0:T(8,128)(2,1)S(1)}, bf16[224,512]{1,0:T(8,128)(2,1)S(1)}, u32[]{:S(2)}, u32[]{:S(2)}) collective-permute-start(bf16[224,512]{1,0:T(8,128)(2,1)S(1)} %fusion.8.refs_0_), channel_id=1, source_target_pairs={{4,0},{5,1},{6,2},{7,3},{8,4},{9,5},{10,6},{11,7},{12,8},{13,9},{1... | collective-permute-start | bytes 688136 | tf_op jit(solution)/shard_map/ppermute | solution.py:146
  12.4 13.1 %collective-permute-start.3 = (bf16[224,512]{1,0:T(8,128)(2,1)S(1)}, bf16[224,512]{1,0:T(8,128)(2,1)S(1)}, u32[]{:S(2)}, u32[]{:S(2)}) collective-permute-start(bf16[224,512]{1,0:T(8,128)(2,1)S(1)} %fusion.8.refs_0_), channel_id=1, source_target_pairs={{0,2},{1,3},{2,0},{3,1},{4,6},{5,7},{6,4},{7,5},{8,10},{9,11},{10,... | collective-permute-start | bytes 688136 | tf_op jit(solution)/shard_map/ppermute | solution.py:147
  14.0 11.5 %collective-permute-start.10 = (bf16[224,512]{1,0:T(8,128)(2,1)S(1)}, bf16[224,512]{1,0:T(8,128)(2,1)S(1)}, u32[]{:S(2)}, u32[]{:S(2)}) collective-permute-start(bf16[224,512]{1,0:T(8,128)(2,1)S(1)} %fusion.8.refs_0_), channel_id=1, source_target_pairs={{0,1},{1,0},{2,3},{3,2},{4,5},{5,4},{6,7},{7,6},{8,9},{9,8},{10,11... | collective-permute-start | bytes 688136 | tf_op jit(solution)/shard_map/ppermute | solution.py:233
  16.6 14.5 %copy-start.2 = (bf16[224,512]{1,0:T(8,128)(2,1)}, bf16[224,512]{1,0:T(8,128)(2,1)S(1)}, u32[]{:S(2)}) copy-start(bf16[224,512]{1,0:T(8,128)(2,1)S(1)} %collective-permute-done.1.refs_1_) | copy-start | bytes 688132
  20.7 10.4 %copy-start.6 = (bf16[224,512]{1,0:T(8,128)(2,1)}, bf16[224,512]{1,0:T(8,128)(2,1)S(1)}, u32[]{:S(2)}) copy-start(bf16[224,512]{1,0:T(8,128)(2,1)S(1)} %collective-permute-done.2.refs_2_) | copy-start | bytes 688132
  20.8 10.4 %collective-permute-start.4 = (bf16[224,512]{1,0:T(8,128)(2,1)S(1)}, bf16[224,512]{1,0:T(8,128)(2,1)S(1)}, u32[]{:S(2)}, u32[]{:S(2)}) collective-permute-start(bf16[224,512]{1,0:T(8,128)(2,1)S(1)} %collective-permute-done.1.refs_1_), channel_id=1, source_target_pairs={{0,4},{1,5},{2,6},{3,7},{4,8},{5,9},{6,10},{7,11},{8,12},{9,13},{1... | collective-permute-start | bytes 688136 | tf_op jit(solution)/shard_map/ppermute | solution.py:150
  24.2 8.5 %collective-permute-start.5 = (bf16[224,512]{1,0:T(8,128)(2,1)S(1)}, bf16[224,512]{1,0:T(8,128)(2,1)S(1)}, u32[]{:S(2)}, u32[]{:S(2)}) collective-permute-start(bf16[224,512]{1,0:T(8,128)(2,1)S(1)} %collective-permute-done.2.refs_2_), channel_id=1, source_target_pairs={{4,0},{5,1},{6,2},{7,3},{8,4},{9,5},{10,6},{11,7},{12,8},{13,9},{1... | collective-permute-start | bytes 688136 | tf_op jit(solution)/shard_map/ppermute | solution.py:151
  25.6 0.7 copy-start.15
  27.5 11.7 %collective-permute-start.6 = (bf16[224,512]{1,0:T(8,128)(2,1)S(1)}, bf16[224,512]{1,0:T(8,128)(2,1)S(1)}, u32[]{:S(2)}, u32[]{:S(2)}) collective-permute-start(bf16[224,512]{1,0:T(8,128)(2,1)S(1)} %broadcast_select_fusion.1), channel_id=1, source_target_pairs={{0,2},{1,3},{2,0},{3,1},{4,6},{5,7},{6,4},{7,5},{8,10},{9,11},{10,... | collective-permute-start | bytes 688136 | tf_op jit(solution)/shard_map/ppermute | solution.py:152
  31.2 3.2 %copy-start.8 = (bf16[224,512]{1,0:T(8,128)(2,1)}, bf16[224,512]{1,0:T(8,128)(2,1)S(1)}, u32[]{:S(2)}) copy-start(bf16[224,512]{1,0:T(8,128)(2,1)S(1)} %collective-permute-done.4.refs_4_) | copy-start | bytes 688132
  32.7 6.4 %copy-start.9 = (bf16[224,512]{1,0:T(8,128)(2,1)}, bf16[224,512]{1,0:T(8,128)(2,1)S(1)}, u32[]{:S(2)}) copy-start(bf16[224,512]{1,0:T(8,128)(2,1)S(1)} %collective-permute-done.5.refs_5_) | copy-start | bytes 688132
  32.8 15.5 %collective-permute-start.9 = (bf16[224,512]{1,0:T(8,128)(2,1)S(1)}, bf16[224,512]{1,0:T(8,128)(2,1)S(1)}, u32[]{:S(2)}, u32[]{:S(2)}) collective-permute-start(bf16[224,512]{1,0:T(8,128)(2,1)S(1)} %broadcast_select_fusion), channel_id=1, source_target_pairs={{0,2},{1,3},{2,0},{3,1},{4,6},{5,7},{6,4},{7,5},{8,10},{9,11},{10,... | collective-permute-start | bytes 688136 | tf_op jit(solution)/shard_map/ppermute | solution.py:155
  34.4 12.7 %collective-permute-start.7 = (bf16[224,512]{1,0:T(8,128)(2,1)S(1)}, bf16[224,512]{1,0:T(8,128)(2,1)S(1)}, u32[]{:S(2)}, u32[]{:S(2)}) collective-permute-start(bf16[224,512]{1,0:T(8,128)(2,1)S(1)} %collective-permute-done.4.refs_4_), channel_id=1, source_target_pairs={{0,4},{1,5},{2,6},{3,7},{4,8},{5,9},{6,10},{7,11},{8,12},{9,13},{1... | collective-permute-start | bytes 688136 | tf_op jit(solution)/shard_map/ppermute | solution.py:153
  37.8 9.2 %collective-permute-start.8 = (bf16[224,512]{1,0:T(8,128)(2,1)S(1)}, bf16[224,512]{1,0:T(8,128)(2,1)S(1)}, u32[]{:S(2)}, u32[]{:S(2)}) collective-permute-start(bf16[224,512]{1,0:T(8,128)(2,1)S(1)} %collective-permute-done.5.refs_5_), channel_id=1, source_target_pairs={{4,0},{5,1},{6,2},{7,3},{8,4},{9,5},{10,6},{11,7},{12,8},{13,9},{1... | collective-permute-start | bytes 688136 | tf_op jit(solution)/shard_map/ppermute | solution.py:154
  39.2 7.9 %copy-start.3 = (bf16[224,512]{1,0:T(8,128)(2,1)S(1)}, bf16[224,512]{1,0:T(8,128)(2,1)}, u32[]{:S(2)}) copy-start(bf16[224,512]{1,0:T(8,128)(2,1)} %copy-done.2) | copy-start | bytes 688132
  39.2 0.7 copy-start.17
  47.1 0.7 copy-start.10
  47.1 1.2 %copy-start.11 = (bf16[224,512]{1,0:T(8,128)(2,1)}, bf16[224,512]{1,0:T(8,128)(2,1)S(1)}, u32[]{:S(2)}) copy-start(bf16[224,512]{1,0:T(8,128)(2,1)S(1)} %collective-permute-done.8.refs_1_) | copy-start | bytes 688132
  47.8 6.0 %collective-permute-start.11 = (bf16[224,512]{1,0:T(8,128)(2,1)S(1)}, bf16[224,512]{1,0:T(8,128)(2,1)S(1)}, u32[]{:S(2)}, u32[]{:S(2)}) collective-permute-start(bf16[224,512]{1,0:T(8,128)(2,1)S(1)} %select_select_fusion), channel_id=1, source_target_pairs={{0,2},{1,3},{2,0},{3,1},{4,6},{5,7},{6,4},{7,5},{8,10},{9,11},{10,... | collective-permute-start | bytes 688136 | tf_op jit(solution)/shard_map/ppermute | solution.py:163
  48.3 0.7 copy-start.16
  49.0 6.6 %copy-start.4 = (f32[7,16,1024]{2,1,0:T(8,128)S(1)}, f32[7,16,1024]{2,1,0:T(8,128)}, u32[]{:S(2)}) copy-start(f32[7,16,1024]{2,1,0:T(8,128)} %shard_map.95) | copy-start | bytes 1376260
  53.8 2.9 %copy-start.12 = (bf16[224,512]{1,0:T(8,128)(2,1)}, bf16[224,512]{1,0:T(8,128)(2,1)S(1)}, u32[]{:S(2)}) copy-start(bf16[224,512]{1,0:T(8,128)(2,1)S(1)} %collective-permute-done.11.refs_0_) | copy-start | bytes 688132
  61.0 0.7 copy-start.14
  61.0 1.3 %copy-start.5 = (f32[16,512]{1,0:T(8,128)S(1)}, f32[16,512]{1,0:T(8,128)}, u32[]{:S(2)}) copy-start(f32[16,512]{1,0:T(8,128)} %param.11) | copy-start | bytes 98308
  61.0 1.3 %collective-permute-start.12 = (f32[16,512]{1,0:T(8,128)S(1)}, f32[16,512]{1,0:T(8,128)S(1)}, u32[]{:S(2)}, u32[]{:S(2)}) collective-permute-start(f32[16,512]{1,0:T(8,128)S(1)} %slice.107), channel_id=1, source_target_pairs={{0,1},{1,0},{2,3},{3,2},{4,5},{5,4},{6,7},{7,6},{8,9},{9,8},{10,11... | collective-permute-start | bytes 98312 | tf_op jit(solution)/shard_map/ppermute | solution.py:281
  62.4 3.1 %collective-permute-start.13 = (f32[16,16]{0,1:T(8,128)S(1)}, f32[16,16]{0,1:T(8,128)S(1)}, u32[]{:S(2)}, u32[]{:S(2)}) collective-permute-start(f32[16,16]{0,1:T(8,128)S(1)} %convolution_bitcast_fusion), channel_id=1, source_target_pairs={{0,3},{1,2},{2,1},{3,0},{4,7},{5,6},{6,5},{7,4},{8,11},{9,10},{10,... | collective-permute-start | bytes 3080 | tf_op jit(solution)/shard_map/ppermute | solution.py:193
  62.7 3.7 %collective-permute-start.14 = (f32[16,16]{0,1:T(8,128)S(1)}, f32[16,16]{0,1:T(8,128)S(1)}, u32[]{:S(2)}, u32[]{:S(2)}) collective-permute-start(f32[16,16]{0,1:T(8,128)S(1)} %convolution_bitcast_fusion), channel_id=1, source_target_pairs={{0,2},{1,3},{2,0},{3,1},{4,6},{5,7},{6,4},{7,5},{8,10},{9,11},{10,... | collective-permute-start | bytes 3080 | tf_op jit(solution)/shard_map/ppermute | solution.py:193
  64.2 2.1 %collective-permute-start.15 = (f32[16,16]{0,1:T(8,128)S(1)}, f32[16,16]{0,1:T(8,128)S(1)}, u32[]{:S(2)}, u32[]{:S(2)}) collective-permute-start(f32[16,16]{0,1:T(8,128)S(1)} %convolution_bitcast_fusion), channel_id=1, source_target_pairs={{0,1},{1,0},{2,3},{3,2},{4,5},{5,4},{6,7},{7,6},{8,9},{9,8},{10,11... | collective-permute-start | bytes 3080 | tf_op jit(solution)/shard_map/ppermute | solution.py:193
  64.3 7.0 %copy-start.13 = (f32[16,16]{1,0:T(8,128)S(1)}, f32[16,16]{1,0:T(8,128)}, u32[]{:S(2)}) copy-start(f32[16,16]{1,0:T(8,128)} %param.13) | copy-start | bytes 3076
  66.4 5.5 %collective-permute-start.16 = (f32[16,16]{0,1:T(8,128)S(1)}, f32[16,16]{0,1:T(8,128)S(1)}, u32[]{:S(2)}, u32[]{:S(2)}) collective-permute-start(f32[16,16]{0,1:T(8,128)S(1)} %select_add_fusion), channel_id=1, source_target_pairs={{0,12},{1,13},{2,14},{3,15},{4,8},{5,9},{6,10},{7,11},{8,4},{9,5},... | collective-permute-start | bytes 3080 | tf_op jit(solution)/shard_map/ppermute | solution.py:193
  69.1 4.5 %collective-permute-start.17 = (f32[16,16]{0,1:T(8,128)S(1)}, f32[16,16]{0,1:T(8,128)S(1)}, u32[]{:S(2)}, u32[]{:S(2)}) collective-permute-start(f32[16,16]{0,1:T(8,128)S(1)} %select_add_fusion), channel_id=1, source_target_pairs={{0,8},{1,9},{2,10},{3,11},{4,12},{5,13},{6,14},{7,15},{8,0},{9,1},... | collective-permute-start | bytes 3080 | tf_op jit(solution)/shard_map/ppermute | solution.py:193
  71.3 3.7 %collective-permute-start.18 = (f32[16,16]{0,1:T(8,128)S(1)}, f32[16,16]{0,1:T(8,128)S(1)}, u32[]{:S(2)}, u32[]{:S(2)}) collective-permute-start(f32[16,16]{0,1:T(8,128)S(1)} %select_add_fusion), channel_id=1, source_target_pairs={{0,4},{1,5},{2,6},{3,7},{4,0},{5,1},{6,2},{7,3},{8,12},{9,13},{10,... | collective-permute-start | bytes 3080 | tf_op jit(solution)/shard_map/ppermute | solution.py:193

commit v15 on v12

--- a/solution.py
+++ b/solution.py
@@ -135,38 +135,46 @@
     if devices != 16:
         pieces = lax.all_gather(packed, "row", axis=0, tiled=False)
         return [pieces], None, jnp.arange(devices, dtype=jnp.int32)
-    up = [(r, r + 4) for r in range(12)]
-    down = [(r, r - 4) for r in range(4, 16)]
+    zone = [r // 4 for r in range(16)]
+    pairs_swap = [(r, r ^ 4) for r in range(16)]
+    inner_swap = [(r, r + 4) for r in range(16) if zone[r] == 1] + [
+        (r, r - 4) for r in range(16) if zone[r] == 2
+    ]
+    outward = [(r, r - 4) for r in range(16) if zone[r] == 1] + [
+        (r, r + 4) for r in range(16) if zone[r] == 2
+    ]
     across = [(r, r ^ 2) for r in range(16)]
     z = me // 4
     partner = me ^ 2
-
-    ends = (z == 0) | (z == 3)
-    up1 = lax.ppermute(packed, "row", up)
-    down1 = lax.ppermute(packed, "row", down)
+    mid = (z == 1) | (z == 2)
+    low = z <= 1
+
+    swap1 = lax.ppermute(packed, "row", pairs_swap)
+    inner1 = lax.ppermute(packed, "row", inner_swap)
     across1 = lax.ppermute(packed, "row", across)
-    up2 = lax.ppermute(up1, "row", up)
-    down2 = lax.ppermute(down1, "row", down)
-    across2 = lax.ppermute(jnp.where(z <= 2, down1, up1), "row", across)
-    up3 = lax.ppermute(up2, "row", up)
-    down3 = lax.ppermute(down2, "row", down)
-    across3 = lax.ppermute(jnp.where(z >= 2, up2, down2), "row", across)
-    last = jnp.where(ends, jnp.where(z == 3, up3, down3), up1)
+    swap1, inner1 = lax.optimization_barrier((swap1, inner1))
+    inner2 = lax.ppermute(swap1, "row", inner_swap)
+    out2 = lax.ppermute(inner1, "row", outward)
+    across2 = lax.ppermute(swap1, "row", across)
+    out3 = lax.ppermute(inner2, "row", outward)
+    across3 = lax.ppermute(jnp.where(mid, inner1, out2), "row", across)
+    last = jnp.where(mid, inner2, out3)
     one = jnp.ones((), bool)
     early = None
     if early_work is not None:
-        early = early_work([packed, up1, down1, across1, up2, down2],
-                           jnp.stack([one, z >= 1, z <= 2, one, z >= 2, z <= 1]))
+        early = early_work([packed, swap1, inner1, across1, inner2, out2, across2],
+                           jnp.stack([one, one, mid, one, mid, ~mid, one]))
         last, early = lax.optimization_barrier((last, early))
     across4 = lax.ppermute(last, "row", across)
 
-    pieces = [packed, up1, down1, across1, up2, down2, across2, up3, down3, across3, across4]
-    valid = [one, z >= 1, z <= 2, one, z >= 2, z <= 1, one, z == 3, z == 0, one, one]
+    pieces = [packed, swap1, inner1, across1, inner2, out2, across2, out3, across3, across4]
+    valid = [one, one, mid, one, mid, ~mid, one, ~mid, one, one]
     origin = [
-        me, me - 4, me + 4, partner, me - 8, me + 8,
-        jnp.where(z <= 2, partner + 4, partner - 4), me - 12, me + 12,
-        jnp.where(z >= 2, partner - 8, partner + 8),
-        jnp.where(ends, jnp.where(z == 3, partner - 12, partner + 12), partner - 4),
+        me, me ^ 4, jnp.where(low, me + 4, me - 4), partner,
+        jnp.where(low, me + 8, me - 8), jnp.where(low, me + 8, me - 8), partner ^ 4,
+        jnp.where(low, me + 12, me - 12),
+        jnp.where(mid, jnp.where(low, partner + 4, partner - 4), jnp.where(low, partner + 8, partner - 8)),
+        jnp.where(mid, jnp.where(low, partner + 8, partner - 8), jnp.where(low, partner + 12, partner - 12)),
     ]
     origin = jnp.clip(jnp.stack(origin), 0, devices - 1).astype(jnp.int32)
     if early_work is not None:

time: 75.5 us -> 70.9 us (0.939)
  starting transfers between devices: 28.7 us -> 19.7 us
  waiting for transfers between devices: 19.7 us -> 24.3 us
  Pallas kernels: 11.1 us -> 10.3 us
    ppermute x8 -> x7, starting transfers between devices: 19.5 us -> 8.9 us  [the longest x1 2.67 us: gather_pieces(): swap1 = lax.ppermute(packed, 'row', pairs_swap)]
    ppermute x8 -> x7, waiting for transfers between devices: 9.14 us -> 12.4 us  [the longest x1 8.66 us: gather_pieces(): out2 = lax.ppermute(inner1, 'row', outward)]
    ppermute x6, waiting for transfers between devices: 4.41 us -> 6.78 us  [sum_over_rows(): lax.ppermute(value, 'row', [(i, i ^ m << shift) for i in range(devices)])]
    ppermute x1, waiting for transfers between devices: 5.55 us -> 4.47 us  [gather_pieces(): across4 = lax.ppermute(last, 'row', across)]
    ppermute x1, starting transfers between devices: 0.57 us -> 1.58 us  [gather_pieces(): across4 = lax.ppermute(last, 'row', across)]
    pallas_call x2, Pallas kernels: 11.1 us -> 10.3 us  [list_product(): pl.pallas_call(functools.partial(list_kernel, width, rows, counts, split)...]
    unnamed x39 -> x33, local copies, waits for them, and re-layouts: 1.32 us -> 1.98 us
  transfers between devices with their start and end apart: 19 -> 18, of which waited for: 11 -> 9; matrix products, arithmetic and copies ran while one was open for 10% -> 11% of each run, Pallas kernels for 8% -> 9%
where the time goes in v15:
time: 70.9 us; the launch traced here: 70 us
  waiting for transfers between devices  24.3 us (34%)
  starting transfers between devices  19.7 us (28%)
  Pallas kernels  10.3 us (15%)
  local copies, waits for them, and re-layouts  8.38 us (12%)
  other arithmetic  4.67 us (7%)
  between operations  1.62 us (2%)
  matrix products  1.07 us (2%)
    pallas_call x2, Pallas kernels, list_product(): pl.pallas_call(functools.partial(list_kernel, width, rows, counts, split)...  10.3 us
    ppermute x1, waiting for transfers between devices, gather_pieces(): out2 = lax.ppermute(inner1, 'row', outward)  8.66 us
    ppermute x6, starting transfers between devices, sum_over_rows(): lax.ppermute(value, 'row', [(i, i ^ m << shift) for i in range(devices)])  6.87 us
    ppermute x6, waiting for transfers between devices, sum_over_rows(): lax.ppermute(value, 'row', [(i, i ^ m << shift) for i in range(devices)])  6.78 us
    ppermute x1, waiting for transfers between devices, gather_pieces(): across4 = lax.ppermute(last, 'row', across)  4.47 us
    ppermute x1, waiting for transfers between devices, gather_pieces(): swap1 = lax.ppermute(packed, 'row', pairs_swap)  3.76 us
    ppermute x1, starting transfers between devices, gather_pieces(): swap1 = lax.ppermute(packed, 'row', pairs_swap)  2.67 us
    unnamed x33, local copies, waits for them, and re-layouts  1.98 us
  transfers between devices with their start and end apart: 18, of which 9 were waited for; matrix products, arithmetic and copies ran while one was open for 11% of the time, Pallas kernels for 9%

profile of v15, /device:TPU:0, one launch (start us, length us, event | category | flops | bytes accessed | tf_op | source)
XLA Modules:
  0.0 70.0 jit_solution(9238477639482124364)
XLA Ops:
  0.7 0.7 %convert.8 = bf16[4,2]{0,1:T(2,128)(2,1)S(1)} convert(s32[4,2]{0,1:T(2,128)} %param.14) | non-fusion elementwise | flops 8 | bytes 48 | tf_op jit(solution)/shard_map/convert.3
  1.4 0.1 copy.47
  2.3 0.5 collective-permute-start
  2.8 0.7 broadcast_in_dim.27
  3.5 0.7 concatenate.39
  4.1 0.1 stack.50
  4.3 0.6 convert_element_type.35.flag_ref
  5.0 0.8 %multiply_convert_fusion = bf16[16,512]{1,0:T(8,128)(2,1)S(1)} fusion(f32[16,512]{1,0:T(8,128)} %param.11, f32[512]{0:T(512)} %param.10), kind=kLoop, calls=%fused_computation.20 | loop fusion | flops 16384 | bytes 51200 | tf_op jit(solution)/shard_map/convert_element_type | solution.py:227
  5.9 2.7 %collective-permute-start.1 = (bf16[224,512]{1,0:T(8,128)(2,1)S(1)}, bf16[224,512]{1,0:T(8,128)(2,1)S(1)}, u32[]{:S(2)}, u32[]{:S(2)}) collective-permute-start(bf16[224,512]{1,0:T(8,128)(2,1)S(1)} %fusion.7.refs_0_), channel_id=1, source_target_pairs={{0,4},{1,5},{2,6},{3,7},{4,0},{5,1},{6,2},{7,3},{8,12},{9,13},{10,... | collective-permute-start | bytes 688136 | tf_op jit(solution)/shard_map/ppermute | solution.py:152
  8.6 0.7 collective-permute-start.2
  9.3 0.3 collective-permute-start.9
  9.5 1.5 %collective-permute-start.3 = (bf16[224,512]{1,0:T(8,128)(2,1)S(1)}, bf16[224,512]{1,0:T(8,128)(2,1)S(1)}, u32[]{:S(2)}, u32[]{:S(2)}) collective-permute-start(bf16[224,512]{1,0:T(8,128)(2,1)S(1)} %fusion.7.refs_0_), channel_id=1, source_target_pairs={{0,2},{1,3},{2,0},{3,1},{4,6},{5,7},{6,4},{7,5},{8,10},{9,11},{10,... | collective-permute-start | bytes 688136 | tf_op jit(solution)/shard_map/ppermute | solution.py:154
  11.1 3.8 %collective-permute-done.1.refs_1_ = bf16[224,512]{1,0:T(8,128)(2,1)S(1)} collective-permute-done((bf16[224,512]{1,0:T(8,128)(2,1)S(1)}, bf16[224,512]{1,0:T(8,128)(2,1)S(1)}, u32[]{:S(2)}, u32[]{:S(2)}) %collective-permute-start.1) | collective-permute-done | bytes 229408 | tf_op jit(solution)/shard_map/ppermute | solution.py:152
  14.8 0.7 collective-permute-start.4
  15.5 1.7 %collective-permute-start.6 = (bf16[224,512]{1,0:T(8,128)(2,1)S(1)}, bf16[224,512]{1,0:T(8,128)(2,1)S(1)}, u32[]{:S(2)}, u32[]{:S(2)}) collective-permute-start(bf16[224,512]{1,0:T(8,128)(2,1)S(1)} %collective-permute-done.1.refs_1_), channel_id=1, source_target_pairs={{0,2},{1,3},{2,0},{3,1},{4,6},{5,7},{6,4},{7,5},{8,10},{9,11},{10,... | collective-permute-start | bytes 688136 | tf_op jit(solution)/shard_map/ppermute | solution.py:158
  17.3 1.3 %collective-permute-start.5 = (bf16[224,512]{1,0:T(8,128)(2,1)S(1)}, bf16[224,512]{1,0:T(8,128)(2,1)S(1)}, u32[]{:S(2)}, u32[]{:S(2)}) collective-permute-start(bf16[224,512]{1,0:T(8,128)(2,1)S(1)} %collective-permute-done.2.refs_2_), channel_id=1, source_target_pairs={{4,0},{5,1},{6,2},{7,3},{8,12},{9,13},{10,14},{11,15},{20,16},{21,... | collective-permute-start | bytes 688136 | tf_op jit(solution)/shard_map/ppermute | solution.py:157
  18.7 0.2 copy.48
  18.9 0.9 %broadcast_divide_fusion.ro_ref = f32[1024,1]{1,0:T(8,128)} fusion(f32[1024,1]{1,0:T(8,128)S(1)} %copy.48), kind=kLoop, calls=%fused_computation.12 | loop fusion | flops 1024 | bytes 8192 | tf_op jit(solution)/shard_map/div | solution.py:246
  20.0 1.0 %copy.49.xo_ref = bf16[1024,192]{1,0:T(8,128)(2,1)} copy(bf16[1024,192]{0,1:T(8,128)(2,1)S(1)} %multiply_bitcast_fusion) | data formatting | bytes 786432 | tf_op jit(solution)/shard_map/transpose | solution.py:247
  21.0 1.0 %copy.50.no_ref = f32[1024,1]{1,0:T(8,128)} copy(f32[1024,1]{0,1:T(1,128)S(1)} %bitcast.65) | data formatting | bytes 8192 | tf_op jit(solution)/shard_map/broadcast_in_dim | solution.py:244
  22.0 8.7 %collective-permute-done.5.refs_5_ = bf16[224,512]{1,0:T(8,128)(2,1)S(1)} collective-permute-done((bf16[224,512]{1,0:T(8,128)(2,1)S(1)}, bf16[224,512]{1,0:T(8,128)(2,1)S(1)}, u32[]{:S(2)}, u32[]{:S(2)}) %collective-permute-start.5) | collective-permute-done | bytes 229408 | tf_op jit(solution)/shard_map/ppermute | solution.py:157
  30.7 0.6 collective-permute-start.8
  31.3 1.3 %collective-permute-start.7 = (bf16[224,512]{1,0:T(8,128)(2,1)S(1)}, bf16[224,512]{1,0:T(8,128)(2,1)S(1)}, u32[]{:S(2)}, u32[]{:S(2)}) collective-permute-start(bf16[224,512]{1,0:T(8,128)(2,1)S(1)} %collective-permute-done.4.refs_4_), channel_id=1, source_target_pairs={{4,0},{5,1},{6,2},{7,3},{8,12},{9,13},{10,14},{11,15},{20,16},{21,... | collective-permute-start | bytes 688136 | tf_op jit(solution)/shard_map/ppermute | solution.py:159
  32.6 0.7 copy-done.15
  33.3 6.5 %shard_map.95 = f32[7,16,1024]{2,1,0:T(8,128)} custom-call(s32[7]{0:T(128)} %convert_element_type.35.flag_ref, bf16[1024,192]{1,0:T(8,128)(2,1)} %copy.49.xo_ref, f32[1024,1]{1,0:T(8,128)} %copy.50.no_ref, f32[1024,1]{1,0:T(8,128)} %broadcast_divide_fusion.ro_ref, bf16[224,512]{1,0:T(8,128)(2,1)} %copy-done.5, bf16[224,512]{1,0:T(8,128)(2,1)} %copy-done.11, ...), custom_call_target="tpu_custom_call" | custom-call | flops 1526726656 | bytes 2064384 | tf_op jit(solution)/shard_map/pallas_call | solution.py:97
  39.8 0.7 %slice_bitcast_fusion.4 = bf16[1,18]{1,0:T(2,128)(2,1)S(1)} fusion(bf16[1,224,512]{2,1,0:T(8,128)(2,1)} %bitcast.71), kind=kLoop, calls=%fused_computation.43 | loop fusion | bytes 72 | tf_op jit(solution)/shard_map/squeeze | solution.py:258
  40.6 1.6 %collective-permute-start.10 = (bf16[224,512]{1,0:T(8,128)(2,1)S(1)}, bf16[224,512]{1,0:T(8,128)(2,1)S(1)}, u32[]{:S(2)}, u32[]{:S(2)}) collective-permute-start(bf16[224,512]{1,0:T(8,128)(2,1)S(1)} %broadcast_select_fusion), channel_id=1, source_target_pairs={{0,2},{1,3},{2,0},{3,1},{4,6},{5,7},{6,4},{7,5},{8,10},{9,11},{10,... | collective-permute-start | bytes 688136 | tf_op jit(solution)/shard_map/ppermute | solution.py:168
  42.2 4.5 %collective-permute-done.10.refs_2_ = bf16[224,512]{1,0:T(8,128)(2,1)S(1)} collective-permute-done((bf16[224,512]{1,0:T(8,128)(2,1)S(1)}, bf16[224,512]{1,0:T(8,128)(2,1)S(1)}, u32[]{:S(2)}, u32[]{:S(2)}) %collective-permute-start.10) | collective-permute-done | bytes 229408 | tf_op jit(solution)/shard_map/ppermute | solution.py:168
  46.9 0.2 slice_reduce_fusion
  47.7 0.2 and_reduce_fusion
  47.9 0.6 slice.76.flag_ref
  48.6 3.7 %shard_map.96 = f32[16,1024]{1,0:T(8,128)} custom-call(s32[3]{0:T(128)} %slice.76.flag_ref, bf16[1024,192]{1,0:T(8,128)(2,1)} %copy.49.xo_ref, f32[1024,1]{1,0:T(8,128)} %copy.50.no_ref, f32[1024,1]{1,0:T(8,128)} %broadcast_divide_fusion.ro_ref, bf16[224,512]{1,0:T(8,128)(2,1)} %copy-done.6, bf16[224,512]{1,0:T(8,128)(2,1)} %copy-done.12, ...), custom_call_target="tpu_custom_call" | custom-call | flops 654311424 | bytes 753664 | tf_op jit(solution)/shard_map/pallas_call | solution.py:97
  52.4 0.8 %add.67 = f32[16,1024]{1,0:T(8,128)S(1)} add(f32[16,1024]{1,0:T(8,128)} %shard_map.96, f32[16,1024]{1,0:T(8,128)S(1)} %select_reduce_fusion) | non-fusion elementwise | flops 16384 | bytes 196608 | tf_op jit(solution)/shard_map/add | solution.py:280
  53.3 0.6 copy-done.10
  53.9 0.6 collective-permute-done.11
  54.5 0.1 convolution_bitcast_fusion
  54.7 2.1 %collective-permute-start.12 = (f32[16,16]{0,1:T(8,128)S(1)}, f32[16,16]{0,1:T(8,128)S(1)}, u32[]{:S(2)}, u32[]{:S(2)}) collective-permute-start(f32[16,16]{0,1:T(8,128)S(1)} %convolution_bitcast_fusion), channel_id=1, source_target_pairs={{0,3},{1,2},{2,1},{3,0},{4,7},{5,6},{6,5},{7,4},{8,11},{9,10},{10,... | collective-permute-start | bytes 3080 | tf_op jit(solution)/shard_map/ppermute | solution.py:199
  56.8 0.3 collective-permute-start.13
  57.1 1.0 %collective-permute-done.12 = f32[16,16]{0,1:T(8,128)S(1)} collective-permute-done((f32[16,16]{0,1:T(8,128)S(1)}, f32[16,16]{0,1:T(8,128)S(1)}, u32[]{:S(2)}, u32[]{:S(2)}) %collective-permute-start.12) | collective-permute-done | bytes 1056 | tf_op jit(solution)/shard_map/ppermute | solution.py:199
  58.1 2.3 %collective-permute-done.13 = f32[16,16]{0,1:T(8,128)S(1)} collective-permute-done((f32[16,16]{0,1:T(8,128)S(1)}, f32[16,16]{0,1:T(8,128)S(1)}, u32[]{:S(2)}, u32[]{:S(2)}) %collective-permute-start.13) | collective-permute-done | bytes 1056 | tf_op jit(solution)/shard_map/ppermute | solution.py:199
  60.4 0.8 %collective-permute-start.15 = (f32[16,16]{0,1:T(8,128)S(1)}, f32[16,16]{0,1:T(8,128)S(1)}, u32[]{:S(2)}, u32[]{:S(2)}) collective-permute-start(f32[16,16]{0,1:T(8,128)S(1)} %select_add_fusion), channel_id=1, source_target_pairs={{0,12},{1,13},{2,14},{3,15},{4,8},{5,9},{6,10},{7,11},{8,4},{9,5},... | collective-permute-start | bytes 3080 | tf_op jit(solution)/shard_map/ppermute | solution.py:199
  61.2 3.6 %collective-permute-start.16 = (f32[16,16]{0,1:T(8,128)S(1)}, f32[16,16]{0,1:T(8,128)S(1)}, u32[]{:S(2)}, u32[]{:S(2)}) collective-permute-start(f32[16,16]{0,1:T(8,128)S(1)} %select_add_fusion), channel_id=1, source_target_pairs={{0,8},{1,9},{2,10},{3,11},{4,12},{5,13},{6,14},{7,15},{8,0},{9,1},... | collective-permute-start | bytes 3080 | tf_op jit(solution)/shard_map/ppermute | solution.py:199
  64.9 0.1 fusion.16
  65.0 0.9 %collective-permute-done.15 = f32[16,16]{0,1:T(8,128)S(1)} collective-permute-done((f32[16,16]{0,1:T(8,128)S(1)}, f32[16,16]{0,1:T(8,128)S(1)}, u32[]{:S(2)}, u32[]{:S(2)}) %collective-permute-start.15) | collective-permute-done | bytes 1056 | tf_op jit(solution)/shard_map/ppermute | solution.py:199
  65.9 0.6 collective-permute-done.16
  66.6 1.9 %collective-permute-done.17 = f32[16,16]{0,1:T(8,128)S(1)} collective-permute-done((f32[16,16]{0,1:T(8,128)S(1)}, f32[16,16]{0,1:T(8,128)S(1)}, u32[]{:S(2)}, u32[]{:S(2)}) %collective-permute-start.17) | collective-permute-done | bytes 1056 | tf_op jit(solution)/shard_map/ppermute | solution.py:199
  68.5 0.7 copy.56
  69.2 0.8 %fusion = f32[16,512]{1,0:T(8,128)} fusion(f32[16,512]{1,0:T(8,128)S(1)} %fusion.16, f32[16,16]{0,1:T(8,128)S(1)} %add_multiply_fusion, f32[16,512]{1,0:T(8,128)S(1)} %copy-done.3, f32[512]{0:T(512)S(1)} %broadcast_multiply_fusion, f32[16,512]{1,0:T(8,128)S(1)} %collective-permute-done.11, f32[16,1024]{1,0:T(8,128)S(1)} %add.67), kind=kOutput, calls=%fused_computation.1 | convolution fusion | flops 1605632 | bytes 166912 | tf_op jit(solution)/shard_map/dot_general | solution.py:290
  (87 shorter events, 2.0 us)
Async XLA Ops:
  0.6 64.3 %copy-start = (f32[16,512]{1,0:T(8,128)S(1)}, f32[16,512]{1,0:T(8,128)}, u32[]{:S(2)}) copy-start(f32[16,512]{1,0:T(8,128)} %param.12) | copy-start | bytes 98308
  0.6 5.2 %copy-start.1 = (bf16[192,512]{1,0:T(8,128)(2,1)S(1)}, bf16[192,512]{1,0:T(8,128)(2,1)}, u32[]{:S(2)}) copy-start(bf16[192,512]{1,0:T(8,128)(2,1)} %param.8) | copy-start | bytes 589828
  2.3 3.5 %collective-permute-start = (bf16[9]{0:T(256)(128)(2,1)S(1)}, bf16[9]{0:T(256)(128)(2,1)S(1)}, u32[]{:S(2)}, u32[]{:S(2)}) collective-permute-start(bf16[9]{0:T(256)(128)(2,1)S(1)} %pad_maximum_fusion.1), channel_id=1, source_target_pairs={{0,1},{1,0},{2,3},{3,2},{4,5},{5,4},{6,7},{7,6},{8,9},{9,8},{10,11... | collective-permute-start | bytes 62 | tf_op jit(solution)/shard_map/ppermute | solution.py:231
  5.9 12.7 %copy-start.5 = (bf16[224,512]{1,0:T(8,128)(2,1)}, bf16[224,512]{1,0:T(8,128)(2,1)S(1)}, u32[]{:S(2)}) copy-start(bf16[224,512]{1,0:T(8,128)(2,1)S(1)} %fusion.7.refs_0_) | copy-start | bytes 688132
  5.9 8.9 %collective-permute-start.1 = (bf16[224,512]{1,0:T(8,128)(2,1)S(1)}, bf16[224,512]{1,0:T(8,128)(2,1)S(1)}, u32[]{:S(2)}, u32[]{:S(2)}) collective-permute-start(bf16[224,512]{1,0:T(8,128)(2,1)S(1)} %fusion.7.refs_0_), channel_id=1, source_target_pairs={{0,4},{1,5},{2,6},{3,7},{4,0},{5,1},{6,2},{7,3},{8,12},{9,13},{10,... | collective-permute-start | bytes 688136 | tf_op jit(solution)/shard_map/ppermute | solution.py:152
  8.6 6.2 %collective-permute-start.2 = (bf16[224,512]{1,0:T(8,128)(2,1)S(1)}, bf16[224,512]{1,0:T(8,128)(2,1)S(1)}, u32[]{:S(2)}, u32[]{:S(2)}) collective-permute-start(bf16[224,512]{1,0:T(8,128)(2,1)S(1)} %fusion.7.refs_0_), channel_id=1, source_target_pairs={{4,8},{5,9},{6,10},{7,11},{8,4},{9,5},{10,6},{11,7},{20,24},{21,25... | collective-permute-start | bytes 688136 | tf_op jit(solution)/shard_map/ppermute | solution.py:153
  9.3 9.3 %collective-permute-start.9 = (bf16[224,512]{1,0:T(8,128)(2,1)S(1)}, bf16[224,512]{1,0:T(8,128)(2,1)S(1)}, u32[]{:S(2)}, u32[]{:S(2)}) collective-permute-start(bf16[224,512]{1,0:T(8,128)(2,1)S(1)} %fusion.7.refs_0_), channel_id=1, source_target_pairs={{0,1},{1,0},{2,3},{3,2},{4,5},{5,4},{6,7},{7,6},{8,9},{9,8},{10,11... | collective-permute-start | bytes 688136 | tf_op jit(solution)/shard_map/ppermute | solution.py:239
  9.5 10.3 %collective-permute-start.3 = (bf16[224,512]{1,0:T(8,128)(2,1)S(1)}, bf16[224,512]{1,0:T(8,128)(2,1)S(1)}, u32[]{:S(2)}, u32[]{:S(2)}) collective-permute-start(bf16[224,512]{1,0:T(8,128)(2,1)S(1)} %fusion.7.refs_0_), channel_id=1, source_target_pairs={{0,2},{1,3},{2,0},{3,1},{4,6},{5,7},{6,4},{7,5},{8,10},{9,11},{10,... | collective-permute-start | bytes 688136 | tf_op jit(solution)/shard_map/ppermute | solution.py:154
  14.8 7.2 %copy-start.11 = (bf16[224,512]{1,0:T(8,128)(2,1)}, bf16[224,512]{1,0:T(8,128)(2,1)S(1)}, u32[]{:S(2)}) copy-start(bf16[224,512]{1,0:T(8,128)(2,1)S(1)} %collective-permute-done.1.refs_1_) | copy-start | bytes 688132
  14.8 15.8 %copy-start.4 = (bf16[224,512]{1,0:T(8,128)(2,1)}, bf16[224,512]{1,0:T(8,128)(2,1)S(1)}, u32[]{:S(2)}) copy-start(bf16[224,512]{1,0:T(8,128)(2,1)S(1)} %collective-permute-done.2.refs_2_) | copy-start | bytes 688132
  14.8 16.4 %collective-permute-start.4 = (bf16[224,512]{1,0:T(8,128)(2,1)S(1)}, bf16[224,512]{1,0:T(8,128)(2,1)S(1)}, u32[]{:S(2)}, u32[]{:S(2)}) collective-permute-start(bf16[224,512]{1,0:T(8,128)(2,1)S(1)} %collective-permute-done.1.refs_1_), channel_id=1, source_target_pairs={{4,8},{5,9},{6,10},{7,11},{8,4},{9,5},{10,6},{11,7},{20,24},{21,25... | collective-permute-start | bytes 688136 | tf_op jit(solution)/shard_map/ppermute | solution.py:156
  15.5 17.1 %collective-permute-start.6 = (bf16[224,512]{1,0:T(8,128)(2,1)S(1)}, bf16[224,512]{1,0:T(8,128)(2,1)S(1)}, u32[]{:S(2)}, u32[]{:S(2)}) collective-permute-start(bf16[224,512]{1,0:T(8,128)(2,1)S(1)} %collective-permute-done.1.refs_1_), channel_id=1, source_target_pairs={{0,2},{1,3},{2,0},{3,1},{4,6},{5,7},{6,4},{7,5},{8,10},{9,11},{10,... | collective-permute-start | bytes 688136 | tf_op jit(solution)/shard_map/ppermute | solution.py:158
  17.3 13.4 %collective-permute-start.5 = (bf16[224,512]{1,0:T(8,128)(2,1)S(1)}, bf16[224,512]{1,0:T(8,128)(2,1)S(1)}, u32[]{:S(2)}, u32[]{:S(2)}) collective-permute-start(bf16[224,512]{1,0:T(8,128)(2,1)S(1)} %collective-permute-done.2.refs_2_), channel_id=1, source_target_pairs={{4,0},{5,1},{6,2},{7,3},{8,12},{9,13},{10,14},{11,15},{20,16},{21,... | collective-permute-start | bytes 688136 | tf_op jit(solution)/shard_map/ppermute | solution.py:157
  19.8 1.1 %copy-start.13 = (bf16[224,512]{1,0:T(8,128)(2,1)}, bf16[224,512]{1,0:T(8,128)(2,1)S(1)}, u32[]{:S(2)}) copy-start(bf16[224,512]{1,0:T(8,128)(2,1)S(1)} %collective-permute-done.3.refs_3_) | copy-start | bytes 688132
  30.7 1.9 %copy-start.8 = (bf16[224,512]{1,0:T(8,128)(2,1)}, bf16[224,512]{1,0:T(8,128)(2,1)S(1)}, u32[]{:S(2)}) copy-start(bf16[224,512]{1,0:T(8,128)(2,1)S(1)} %collective-permute-done.5.refs_5_) | copy-start | bytes 688132
  30.7 11.5 %collective-permute-start.8 = (bf16[224,512]{1,0:T(8,128)(2,1)S(1)}, bf16[224,512]{1,0:T(8,128)(2,1)S(1)}, u32[]{:S(2)}, u32[]{:S(2)}) collective-permute-start(bf16[224,512]{1,0:T(8,128)(2,1)S(1)} %broadcast_select_fusion.1), channel_id=1, source_target_pairs={{0,2},{1,3},{2,0},{3,1},{4,6},{5,7},{6,4},{7,5},{8,10},{9,11},{10,... | collective-permute-start | bytes 688136 | tf_op jit(solution)/shard_map/ppermute | solution.py:160
  31.3 1.3 %copy-start.7 = (bf16[224,512]{1,0:T(8,128)(2,1)}, bf16[224,512]{1,0:T(8,128)(2,1)S(1)}, u32[]{:S(2)}) copy-start(bf16[224,512]{1,0:T(8,128)(2,1)S(1)} %collective-permute-done.4.refs_4_) | copy-start | bytes 688132
  31.3 9.3 %collective-permute-start.7 = (bf16[224,512]{1,0:T(8,128)(2,1)S(1)}, bf16[224,512]{1,0:T(8,128)(2,1)S(1)}, u32[]{:S(2)}, u32[]{:S(2)}) collective-permute-start(bf16[224,512]{1,0:T(8,128)(2,1)S(1)} %collective-permute-done.4.refs_4_), channel_id=1, source_target_pairs={{4,0},{5,1},{6,2},{7,3},{8,12},{9,13},{10,14},{11,15},{20,16},{21,... | collective-permute-start | bytes 688136 | tf_op jit(solution)/shard_map/ppermute | solution.py:159
  32.6 0.7 copy-start.15
  39.8 8.7 %copy-start.2 = (f32[7,16,1024]{2,1,0:T(8,128)S(1)}, f32[7,16,1024]{2,1,0:T(8,128)}, u32[]{:S(2)}) copy-start(f32[7,16,1024]{2,1,0:T(8,128)} %shard_map.95) | copy-start | bytes 1376260
  40.6 1.6 %copy-start.6 = (bf16[224,512]{1,0:T(8,128)(2,1)}, bf16[224,512]{1,0:T(8,128)(2,1)S(1)}, u32[]{:S(2)}) copy-start(bf16[224,512]{1,0:T(8,128)(2,1)S(1)} %collective-permute-done.7.refs_0_) | copy-start | bytes 688132
  40.6 6.1 %collective-permute-start.10 = (bf16[224,512]{1,0:T(8,128)(2,1)S(1)}, bf16[224,512]{1,0:T(8,128)(2,1)S(1)}, u32[]{:S(2)}, u32[]{:S(2)}) collective-permute-start(bf16[224,512]{1,0:T(8,128)(2,1)S(1)} %broadcast_select_fusion), channel_id=1, source_target_pairs={{0,2},{1,3},{2,0},{3,1},{4,6},{5,7},{6,4},{7,5},{8,10},{9,11},{10,... | collective-permute-start | bytes 688136 | tf_op jit(solution)/shard_map/ppermute | solution.py:168
  42.2 6.4 %copy-start.12 = (bf16[224,512]{1,0:T(8,128)(2,1)}, bf16[224,512]{1,0:T(8,128)(2,1)S(1)}, u32[]{:S(2)}) copy-start(bf16[224,512]{1,0:T(8,128)(2,1)S(1)} %collective-permute-done.8.refs_1_) | copy-start | bytes 688132
  46.7 1.9 %copy-start.14 = (bf16[224,512]{1,0:T(8,128)(2,1)}, bf16[224,512]{1,0:T(8,128)(2,1)S(1)}, u32[]{:S(2)}) copy-start(bf16[224,512]{1,0:T(8,128)(2,1)S(1)} %collective-permute-done.10.refs_2_) | copy-start | bytes 688132
  53.2 0.7 copy-start.10
  53.2 1.3 %copy-start.3 = (f32[16,512]{1,0:T(8,128)S(1)}, f32[16,512]{1,0:T(8,128)}, u32[]{:S(2)}) copy-start(f32[16,512]{1,0:T(8,128)} %param.11) | copy-start | bytes 98308
  53.3 1.3 %collective-permute-start.11 = (f32[16,512]{1,0:T(8,128)S(1)}, f32[16,512]{1,0:T(8,128)S(1)}, u32[]{:S(2)}, u32[]{:S(2)}) collective-permute-start(f32[16,512]{1,0:T(8,128)S(1)} %slice.97), channel_id=1, source_target_pairs={{0,1},{1,0},{2,3},{3,2},{4,5},{5,4},{6,7},{7,6},{8,9},{9,8},{10,11... | collective-permute-start | bytes 98312 | tf_op jit(solution)/shard_map/ppermute | solution.py:284
  54.7 3.4 %collective-permute-start.12 = (f32[16,16]{0,1:T(8,128)S(1)}, f32[16,16]{0,1:T(8,128)S(1)}, u32[]{:S(2)}, u32[]{:S(2)}) collective-permute-start(f32[16,16]{0,1:T(8,128)S(1)} %convolution_bitcast_fusion), channel_id=1, source_target_pairs={{0,3},{1,2},{2,1},{3,0},{4,7},{5,6},{6,5},{7,4},{8,11},{9,10},{10,... | collective-permute-start | bytes 3080 | tf_op jit(solution)/shard_map/ppermute | solution.py:199
  56.8 3.7 %collective-permute-start.13 = (f32[16,16]{0,1:T(8,128)S(1)}, f32[16,16]{0,1:T(8,128)S(1)}, u32[]{:S(2)}, u32[]{:S(2)}) collective-permute-start(f32[16,16]{0,1:T(8,128)S(1)} %convolution_bitcast_fusion), channel_id=1, source_target_pairs={{0,2},{1,3},{2,0},{3,1},{4,6},{5,7},{6,4},{7,5},{8,10},{9,11},{10,... | collective-permute-start | bytes 3080 | tf_op jit(solution)/shard_map/ppermute | solution.py:199
  57.0 3.4 %collective-permute-start.14 = (f32[16,16]{0,1:T(8,128)S(1)}, f32[16,16]{0,1:T(8,128)S(1)}, u32[]{:S(2)}, u32[]{:S(2)}) collective-permute-start(f32[16,16]{0,1:T(8,128)S(1)} %convolution_bitcast_fusion), channel_id=1, source_target_pairs={{0,1},{1,0},{2,3},{3,2},{4,5},{5,4},{6,7},{7,6},{8,9},{9,8},{10,11... | collective-permute-start | bytes 3080 | tf_op jit(solution)/shard_map/ppermute | solution.py:199
  57.1 7.8 %copy-start.9 = (f32[16,16]{1,0:T(8,128)S(1)}, f32[16,16]{1,0:T(8,128)}, u32[]{:S(2)}) copy-start(f32[16,16]{1,0:T(8,128)} %param.13) | copy-start | bytes 3076
  60.4 5.5 %collective-permute-start.15 = (f32[16,16]{0,1:T(8,128)S(1)}, f32[16,16]{0,1:T(8,128)S(1)}, u32[]{:S(2)}, u32[]{:S(2)}) collective-permute-start(f32[16,16]{0,1:T(8,128)S(1)} %select_add_fusion), channel_id=1, source_target_pairs={{0,12},{1,13},{2,14},{3,15},{4,8},{5,9},{6,10},{7,11},{8,4},{9,5},... | collective-permute-start | bytes 3080 | tf_op jit(solution)/shard_map/ppermute | solution.py:199
  61.2 5.3 %collective-permute-start.16 = (f32[16,16]{0,1:T(8,128)S(1)}, f32[16,16]{0,1:T(8,128)S(1)}, u32[]{:S(2)}, u32[]{:S(2)}) collective-permute-start(f32[16,16]{0,1:T(8,128)S(1)} %select_add_fusion), channel_id=1, source_target_pairs={{0,8},{1,9},{2,10},{3,11},{4,12},{5,13},{6,14},{7,15},{8,0},{9,1},... | collective-permute-start | bytes 3080 | tf_op jit(solution)/shard_map/ppermute | solution.py:199
  64.9 3.7 %collective-permute-start.17 = (f32[16,16]{0,1:T(8,128)S(1)}, f32[16,16]{0,1:T(8,128)S(1)}, u32[]{:S(2)}, u32[]{:S(2)}) collective-permute-start(f32[16,16]{0,1:T(8,128)S(1)} %select_add_fusion), channel_id=1, source_target_pairs={{0,4},{1,5},{2,6},{3,7},{4,0},{5,1},{6,2},{7,3},{8,12},{9,13},{10,... | collective-permute-start | bytes 3080 | tf_op jit(solution)/shard_map/ppermute | solution.py:199

commit v16 on v15

--- a/solution.py
+++ b/solution.py
@@ -237,6 +237,9 @@
     rows = packed.shape[0]
     if chip_split:
         twin_piece = lax.ppermute(packed, "row", twin)
+        twin_terms = lax.ppermute(
+            jnp.concatenate([lanczos_block, degree_scale[None, :]]), "row", twin
+        )
         rows_x = jnp.concatenate([embeddings, twin_piece[:width]], axis=1)
         rows_scale = jnp.concatenate([local_scale, twin_piece[width + LANCZOS]])
     else:
@@ -281,11 +284,19 @@
     else:
         summed = own_rows_product(flags, own_terms, pieces[0].reshape(devices, rows, own), width)
     if chip_split:
+        chip_lanes = jnp.concatenate([lanczos_block, twin_terms[:LANCZOS]], axis=1)
+        chip_scale = jnp.concatenate([degree_scale, twin_terms[LANCZOS]])
+        partial_value = lax.dot_general(
+            chip_lanes, summed * (chip_scale[None, :] / math.sqrt(total_rows)),
+            (((1,), (1,)), ((), ())), precision=HIGHEST,
+        )
         summed = summed[:, :own] + lax.ppermute(summed[:, own:], "row", twin)
-    scaled = summed * (degree_scale[None, :] / math.sqrt(total_rows))
-    partial_value = lax.dot_general(
-        lanczos_block, scaled, (((1,), (1,)), ((), ())), precision=HIGHEST
-    )
+        scaled = summed * (degree_scale[None, :] / math.sqrt(total_rows))
+    else:
+        scaled = summed * (degree_scale[None, :] / math.sqrt(total_rows))
+        partial_value = lax.dot_general(
+            lanczos_block, scaled, (((1,), (1,)), ((), ())), precision=HIGHEST
+        )
     coupling = sum_over_rows(partial_value) / total_rows
     projected = lax.dot_general(
         coupling, lanczos_block, (((0,), (0,)), ((), ())), precision=HIGHEST

time: 70.9 us -> 66.9 us (0.944); the launches traced: 70 us -> 67 us
  waiting for transfers between devices: 24.3 us -> 20.9 us
  local copies, waits for them, and re-layouts: 8.38 us -> 7.4 us
    ppermute x6, waiting for transfers between devices: 6.78 us -> 5.47 us  [sum_over_rows(): lax.ppermute(value, 'row', [(i, i ^ m << shift) for i in range(devices)])]
    ppermute x1, waiting for transfers between devices: 3.76 us -> 2.79 us  [gather_pieces(): swap1 = lax.ppermute(packed, 'row', pairs_swap)]
    concatenate x0 -> x1, other arithmetic: none -> 0.76 us  [shards(): jnp.concatenate([lanczos_block, degree_scale[None, :]])]
    convert_element_type x1, other arithmetic: 0.77 us -> 0.01 us  [shards(): weighted = (degree_scale[None, :] * lanczos_block).astype(jnp.bfloat16)]
    pallas_call x2, Pallas kernels: 10.3 us -> 11 us  [list_product(): pl.pallas_call(functools.partial(list_kernel, width, rows, counts, split)...]
    unnamed x33 -> x38, local copies, waits for them, and re-layouts: 1.98 us -> 2.32 us
  transfers between devices with their start and end apart: 18 -> 19, of which waited for: 9 -> 8; matrix products, arithmetic and copies ran while one was open for 11% -> 9% of each run, Pallas kernels for 9% -> 10%
where the time goes in v16:
time: 66.9 us; the launch traced here: 67 us
  waiting for transfers between devices  20.9 us (31%)
  starting transfers between devices  20.2 us (30%)
  Pallas kernels  11 us (16%)
  local copies, waits for them, and re-layouts  7.4 us (11%)
  other arithmetic  5.25 us (8%)
  between operations  1.73 us (3%)
    pallas_call x2, Pallas kernels, list_product(): pl.pallas_call(functools.partial(list_kernel, width, rows, counts, split)...  11 us
    ppermute x1, waiting for transfers between devices, gather_pieces(): out2 = lax.ppermute(inner1, 'row', outward)  8.12 us
    ppermute x6, starting transfers between devices, sum_over_rows(): lax.ppermute(value, 'row', [(i, i ^ m << shift) for i in range(devices)])  7.11 us
    ppermute x6, waiting for transfers between devices, sum_over_rows(): lax.ppermute(value, 'row', [(i, i ^ m << shift) for i in range(devices)])  5.47 us
    ppermute x1, waiting for transfers between devices, gather_pieces(): across4 = lax.ppermute(last, 'row', across)  4.46 us
    ppermute x1, starting transfers between devices, gather_pieces(): swap1 = lax.ppermute(packed, 'row', pairs_swap)  3.09 us
    ppermute x1, waiting for transfers between devices, gather_pieces(): swap1 = lax.ppermute(packed, 'row', pairs_swap)  2.79 us
    unnamed x38, local copies, waits for them, and re-layouts  2.32 us
  transfers between devices with their start and end apart: 19, of which 8 were waited for; matrix products, arithmetic and copies ran while one was open for 9% of the time, Pallas kernels for 10%

profile of v16, /device:TPU:0, one launch (start us, length us, event | category | flops | bytes accessed | tf_op | source)
XLA Modules:
  0.0 67.0 jit_solution(5759491456187025081)
XLA Ops:
  0.6 0.7 %convert.8 = bf16[4,2]{0,1:T(2,128)(2,1)S(1)} convert(s32[4,2]{0,1:T(2,128)} %param.14) | non-fusion elementwise | flops 8 | bytes 48 | tf_op jit(solution)/shard_map/convert.3
  1.3 0.1 copy.43
  2.3 0.5 collective-permute-start
  2.7 0.8 %pad_maximum_fusion.1 = f32[17,512]{1,0:T(8,128)S(1)} fusion(f32[1,512]{1,0:T(1,128)S(1)} %bitcast.64, f32[16,512]{1,0:T(8,128)} %param.11), kind=kLoop, calls=%fused_computation.20 | loop fusion | flops 8704 | bytes 69632 | tf_op jit(solution)/shard_map/concatenate | solution.py:241
  3.6 0.1 stack.50
  3.8 0.1 stack.61
  3.9 0.5 convert_element_type.35.flag_ref
  4.5 0.6 copy-done.12
  5.1 0.1 fusion.24
  5.4 3.1 %collective-permute-start.1 = (bf16[224,512]{1,0:T(8,128)(2,1)S(1)}, bf16[224,512]{1,0:T(8,128)(2,1)S(1)}, u32[]{:S(2)}, u32[]{:S(2)}) collective-permute-start(bf16[224,512]{1,0:T(8,128)(2,1)S(1)} %fusion.6.refs_0_), channel_id=1, source_target_pairs={{0,4},{1,5},{2,6},{3,7},{4,0},{5,1},{6,2},{7,3},{8,12},{9,13},{10,... | collective-permute-start | bytes 688136 | tf_op jit(solution)/shard_map/ppermute | solution.py:152
  8.5 0.7 collective-permute-start.2
  9.2 1.6 %collective-permute-start.3 = (bf16[224,512]{1,0:T(8,128)(2,1)S(1)}, bf16[224,512]{1,0:T(8,128)(2,1)S(1)}, u32[]{:S(2)}, u32[]{:S(2)}) collective-permute-start(bf16[224,512]{1,0:T(8,128)(2,1)S(1)} %fusion.6.refs_0_), channel_id=1, source_target_pairs={{0,2},{1,3},{2,0},{3,1},{4,6},{5,7},{6,4},{7,5},{8,10},{9,11},{10,... | collective-permute-start | bytes 688136 | tf_op jit(solution)/shard_map/ppermute | solution.py:154
  10.9 0.6 copy-done.9
  11.5 2.8 %collective-permute-done.1.refs_1_ = bf16[224,512]{1,0:T(8,128)(2,1)S(1)} collective-permute-done((bf16[224,512]{1,0:T(8,128)(2,1)S(1)}, bf16[224,512]{1,0:T(8,128)(2,1)S(1)}, u32[]{:S(2)}, u32[]{:S(2)}) %collective-permute-start.1) | collective-permute-done | bytes 229408 | tf_op jit(solution)/shard_map/ppermute | solution.py:152
  14.3 0.7 %collective-permute-start.4 = (bf16[224,512]{1,0:T(8,128)(2,1)S(1)}, bf16[224,512]{1,0:T(8,128)(2,1)S(1)}, u32[]{:S(2)}, u32[]{:S(2)}) collective-permute-start(bf16[224,512]{1,0:T(8,128)(2,1)S(1)} %collective-permute-done.1.refs_1_), channel_id=1, source_target_pairs={{4,8},{5,9},{6,10},{7,11},{8,4},{9,5},{10,6},{11,7},{20,24},{21,25... | collective-permute-start | bytes 688136 | tf_op jit(solution)/shard_map/ppermute | solution.py:156
  15.0 1.7 %collective-permute-start.6 = (bf16[224,512]{1,0:T(8,128)(2,1)S(1)}, bf16[224,512]{1,0:T(8,128)(2,1)S(1)}, u32[]{:S(2)}, u32[]{:S(2)}) collective-permute-start(bf16[224,512]{1,0:T(8,128)(2,1)S(1)} %collective-permute-done.1.refs_1_), channel_id=1, source_target_pairs={{0,2},{1,3},{2,0},{3,1},{4,6},{5,7},{6,4},{7,5},{8,10},{9,11},{10,... | collective-permute-start | bytes 688136 | tf_op jit(solution)/shard_map/ppermute | solution.py:158
  16.7 1.3 %collective-permute-start.5 = (bf16[224,512]{1,0:T(8,128)(2,1)S(1)}, bf16[224,512]{1,0:T(8,128)(2,1)S(1)}, u32[]{:S(2)}, u32[]{:S(2)}) collective-permute-start(bf16[224,512]{1,0:T(8,128)(2,1)S(1)} %collective-permute-done.2.refs_2_), channel_id=1, source_target_pairs={{4,0},{5,1},{6,2},{7,3},{8,12},{9,13},{10,14},{11,15},{20,16},{21,... | collective-permute-start | bytes 688136 | tf_op jit(solution)/shard_map/ppermute | solution.py:157
  18.1 0.2 copy.44
  18.4 0.9 %broadcast_divide_fusion.ro_ref = f32[1024,1]{1,0:T(8,128)} fusion(f32[1024,1]{1,0:T(8,128)S(1)} %copy.44), kind=kLoop, calls=%fused_computation.9 | loop fusion | flops 1024 | bytes 8192 | tf_op jit(solution)/shard_map/div | solution.py:249
  19.4 1.0 %copy.45.xo_ref = bf16[1024,192]{1,0:T(8,128)(2,1)} copy(bf16[1024,192]{0,1:T(8,128)(2,1)S(1)} %multiply_bitcast_fusion) | data formatting | bytes 786432 | tf_op jit(solution)/shard_map/transpose | solution.py:250
  20.4 1.1 %copy.46.no_ref = f32[1024,1]{1,0:T(8,128)} copy(f32[1024,1]{0,1:T(1,128)S(1)} %bitcast.65) | data formatting | bytes 8192 | tf_op jit(solution)/shard_map/broadcast_in_dim | solution.py:247
  21.5 8.1 %collective-permute-done.5.refs_5_ = bf16[224,512]{1,0:T(8,128)(2,1)S(1)} collective-permute-done((bf16[224,512]{1,0:T(8,128)(2,1)S(1)}, bf16[224,512]{1,0:T(8,128)(2,1)S(1)}, u32[]{:S(2)}, u32[]{:S(2)}) %collective-permute-start.5) | collective-permute-done | bytes 229408 | tf_op jit(solution)/shard_map/ppermute | solution.py:157
  29.6 0.6 collective-permute-start.8
  30.2 1.3 %collective-permute-start.7 = (bf16[224,512]{1,0:T(8,128)(2,1)S(1)}, bf16[224,512]{1,0:T(8,128)(2,1)S(1)}, u32[]{:S(2)}, u32[]{:S(2)}) collective-permute-start(bf16[224,512]{1,0:T(8,128)(2,1)S(1)} %collective-permute-done.4.refs_4_), channel_id=1, source_target_pairs={{4,0},{5,1},{6,2},{7,3},{8,12},{9,13},{10,14},{11,15},{20,16},{21,... | collective-permute-start | bytes 688136 | tf_op jit(solution)/shard_map/ppermute | solution.py:159
  31.6 0.7 %copy-done.18 = bf16[224,512]{1,0:T(8,128)(2,1)} copy-done((bf16[224,512]{1,0:T(8,128)(2,1)}, bf16[224,512]{1,0:T(8,128)(2,1)S(1)}, u32[]{:S(2)}) %copy-start.18) | copy-done | bytes 229400
  32.3 6.5 %shard_map.95 = f32[7,16,1024]{2,1,0:T(8,128)} custom-call(s32[7]{0:T(128)} %convert_element_type.35.flag_ref, bf16[1024,192]{1,0:T(8,128)(2,1)} %copy.45.xo_ref, f32[1024,1]{1,0:T(8,128)} %copy.46.no_ref, f32[1024,1]{1,0:T(8,128)} %broadcast_divide_fusion.ro_ref, bf16[224,512]{1,0:T(8,128)(2,1)} %copy-done.5, bf16[224,512]{1,0:T(8,128)(2,1)} %copy-done.14, ...), custom_call_target="tpu_custom_call" | custom-call | flops 1526726656 | bytes 2064384 | tf_op jit(solution)/shard_map/pallas_call | solution.py:97
  38.8 0.7 %slice_bitcast_fusion.4 = bf16[1,18]{1,0:T(2,128)(2,1)S(1)} fusion(bf16[1,224,512]{2,1,0:T(8,128)(2,1)} %bitcast.72), kind=kLoop, calls=%fused_computation.50 | loop fusion | bytes 72 | tf_op jit(solution)/shard_map/squeeze | solution.py:261
  39.5 1.6 %collective-permute-start.10 = (bf16[224,512]{1,0:T(8,128)(2,1)S(1)}, bf16[224,512]{1,0:T(8,128)(2,1)S(1)}, u32[]{:S(2)}, u32[]{:S(2)}) collective-permute-start(bf16[224,512]{1,0:T(8,128)(2,1)S(1)} %broadcast_select_fusion), channel_id=1, source_target_pairs={{0,2},{1,3},{2,0},{3,1},{4,6},{5,7},{6,4},{7,5},{8,10},{9,11},{10,... | collective-permute-start | bytes 688136 | tf_op jit(solution)/shard_map/ppermute | solution.py:168
  41.2 4.5 %collective-permute-done.10.refs_2_ = bf16[224,512]{1,0:T(8,128)(2,1)S(1)} collective-permute-done((bf16[224,512]{1,0:T(8,128)(2,1)S(1)}, bf16[224,512]{1,0:T(8,128)(2,1)S(1)}, u32[]{:S(2)}, u32[]{:S(2)}) %collective-permute-start.10) | collective-permute-done | bytes 229408 | tf_op jit(solution)/shard_map/ppermute | solution.py:168
  45.8 0.2 slice_reduce_fusion
  46.5 0.1 lt.26
  46.6 0.2 and_reduce_fusion
  46.9 0.6 slice.82.flag_ref
  47.6 4.5 %shard_map.96 = f32[16,1024]{1,0:T(8,128)} custom-call(s32[3]{0:T(128)} %slice.82.flag_ref, bf16[1024,192]{1,0:T(8,128)(2,1)} %copy.45.xo_ref, f32[1024,1]{1,0:T(8,128)} %copy.46.no_ref, f32[1024,1]{1,0:T(8,128)} %broadcast_divide_fusion.ro_ref, bf16[224,512]{1,0:T(8,128)(2,1)} %copy-done.6, bf16[224,512]{1,0:T(8,128)(2,1)} %copy-done.15, ...), custom_call_target="tpu_custom_call" | custom-call | flops 654311424 | bytes 753664 | tf_op jit(solution)/shard_map/pallas_call | solution.py:97
  52.1 0.9 %add.67 = f32[16,1024]{1,0:T(8,128)S(1)} add(f32[16,1024]{1,0:T(8,128)} %shard_map.96, f32[16,1024]{1,0:T(8,128)S(1)} %select_reduce_fusion) | non-fusion elementwise | flops 16384 | bytes 196608 | tf_op jit(solution)/shard_map/add | solution.py:283
  52.9 0.2 fusion.7
  53.1 1.6 %collective-permute-start.14 = (f32[16,16]{1,0:T(8,128)S(1)}, f32[16,16]{1,0:T(8,128)S(1)}, u32[]{:S(2)}, u32[]{:S(2)}) collective-permute-start(f32[16,16]{1,0:T(8,128)S(1)} %fusion.7), channel_id=1, source_target_pairs={{0,2},{1,3},{2,0},{3,1},{4,6},{5,7},{6,4},{7,5},{8,10},{9,11},{10,... | collective-permute-start | bytes 3080 | tf_op jit(solution)/shard_map/ppermute | solution.py:199
  54.7 0.3 collective-permute-start.15
  55.0 1.2 %collective-permute-done.13 = f32[16,16]{1,0:T(8,128)S(1)} collective-permute-done((f32[16,16]{1,0:T(8,128)S(1)}, f32[16,16]{1,0:T(8,128)S(1)}, u32[]{:S(2)}, u32[]{:S(2)}) %collective-permute-start.13) | collective-permute-done | bytes 1056 | tf_op jit(solution)/shard_map/ppermute | solution.py:199
  56.2 0.6 collective-permute-done.14
  56.9 1.6 %collective-permute-start.16 = (f32[16,16]{1,0:T(8,128)S(1)}, f32[16,16]{1,0:T(8,128)S(1)}, u32[]{:S(2)}, u32[]{:S(2)}) collective-permute-start(f32[16,16]{1,0:T(8,128)S(1)} %select_add_fusion), channel_id=1, source_target_pairs={{0,12},{1,13},{2,14},{3,15},{4,8},{5,9},{6,10},{7,11},{8,4},{9,5},... | collective-permute-start | bytes 3080 | tf_op jit(solution)/shard_map/ppermute | solution.py:199
  58.4 3.6 %collective-permute-start.17 = (f32[16,16]{1,0:T(8,128)S(1)}, f32[16,16]{1,0:T(8,128)S(1)}, u32[]{:S(2)}, u32[]{:S(2)}) collective-permute-start(f32[16,16]{1,0:T(8,128)S(1)} %select_add_fusion), channel_id=1, source_target_pairs={{0,8},{1,9},{2,10},{3,11},{4,12},{5,13},{6,14},{7,15},{8,0},{9,1},... | collective-permute-start | bytes 3080 | tf_op jit(solution)/shard_map/ppermute | solution.py:199
  62.1 0.3 collective-permute-done.16
  62.4 1.4 %collective-permute-done.17 = f32[16,16]{1,0:T(8,128)S(1)} collective-permute-done((f32[16,16]{1,0:T(8,128)S(1)}, f32[16,16]{1,0:T(8,128)S(1)}, u32[]{:S(2)}, u32[]{:S(2)}) %collective-permute-start.17) | collective-permute-done | bytes 1056 | tf_op jit(solution)/shard_map/ppermute | solution.py:199
  63.8 1.9 %collective-permute-done.18 = f32[16,16]{1,0:T(8,128)S(1)} collective-permute-done((f32[16,16]{1,0:T(8,128)S(1)}, f32[16,16]{1,0:T(8,128)S(1)}, u32[]{:S(2)}, u32[]{:S(2)}) %collective-permute-start.18) | collective-permute-done | bytes 1056 | tf_op jit(solution)/shard_map/ppermute | solution.py:199
  65.7 0.2 fusion.23
  66.0 0.4 copy-done.10
  66.3 0.6 fusion.14
  (100 shorter events, 1.8 us)
Async XLA Ops:
  0.6 3.9 %copy-start = (f32[16,512]{1,0:T(8,128)S(1)}, f32[16,512]{1,0:T(8,128)}, u32[]{:S(2)}) copy-start(f32[16,512]{1,0:T(8,128)} %param.12) | copy-start | bytes 98308
  1.4 1.3 %copy-start.11 = (f32[512]{0:T(512)S(1)}, f32[512]{0:T(512)}, u32[]{:S(2)}) copy-start(f32[512]{0:T(512)} %param.10) | copy-start | bytes 6148
  1.5 2.0 %copy-start.2 = (f32[16,512]{1,0:T(8,128)S(1)}, f32[16,512]{1,0:T(8,128)}, u32[]{:S(2)}) copy-start(f32[16,512]{1,0:T(8,128)} %param.11) | copy-start | bytes 98308
  1.5 2.1 %copy-start.13 = (bf16[512]{0:T(512)(128)(2,1)S(1)}, bf16[512]{0:T(512)(128)(2,1)}, u32[]{:S(2)}) copy-start(bf16[512]{0:T(512)(128)(2,1)} %param.9) | copy-start | bytes 3076
  2.2 3.2 %copy-start.1 = (bf16[192,512]{1,0:T(8,128)(2,1)S(1)}, bf16[192,512]{1,0:T(8,128)(2,1)}, u32[]{:S(2)}) copy-start(bf16[192,512]{1,0:T(8,128)(2,1)} %param.8) | copy-start | bytes 589828
  2.3 3.0 %collective-permute-start = (bf16[9]{0:T(256)(128)(2,1)S(1)}, bf16[9]{0:T(256)(128)(2,1)S(1)}, u32[]{:S(2)}, u32[]{:S(2)}) collective-permute-start(bf16[9]{0:T(256)(128)(2,1)S(1)} %pad_maximum_fusion.2), channel_id=1, source_target_pairs={{0,1},{1,0},{2,3},{3,2},{4,5},{5,4},{6,7},{7,6},{8,9},{9,8},{10,11... | collective-permute-start | bytes 62 | tf_op jit(solution)/shard_map/ppermute | solution.py:231
  3.5 7.3 %collective-permute-start.12 = (f32[17,512]{1,0:T(8,128)S(1)}, f32[17,512]{1,0:T(8,128)S(1)}, u32[]{:S(2)}, u32[]{:S(2)}) collective-permute-start(f32[17,512]{1,0:T(8,128)S(1)} %pad_maximum_fusion.1), channel_id=1, source_target_pairs={{0,1},{1,0},{2,3},{3,2},{4,5},{5,4},{6,7},{7,6},{8,9},{9,8},{10,11... | collective-permute-start | bytes 104456 | tf_op jit(solution)/shard_map/ppermute | solution.py:240
  4.4 0.7 %copy-start.12 = (f32[16,16]{1,0:T(8,128)S(1)}, f32[16,16]{1,0:T(8,128)}, u32[]{:S(2)}) copy-start(f32[16,16]{1,0:T(8,128)} %param.13) | copy-start | bytes 3076
  5.4 5.5 %copy-start.5 = (bf16[224,512]{1,0:T(8,128)(2,1)}, bf16[224,512]{1,0:T(8,128)(2,1)S(1)}, u32[]{:S(2)}) copy-start(bf16[224,512]{1,0:T(8,128)(2,1)S(1)} %fusion.6.refs_0_) | copy-start | bytes 688132
  5.4 8.9 %collective-permute-start.1 = (bf16[224,512]{1,0:T(8,128)(2,1)S(1)}, bf16[224,512]{1,0:T(8,128)(2,1)S(1)}, u32[]{:S(2)}, u32[]{:S(2)}) collective-permute-start(bf16[224,512]{1,0:T(8,128)(2,1)S(1)} %fusion.6.refs_0_), channel_id=1, source_target_pairs={{0,4},{1,5},{2,6},{3,7},{4,0},{5,1},{6,2},{7,3},{8,12},{9,13},{10,... | collective-permute-start | bytes 688136 | tf_op jit(solution)/shard_map/ppermute | solution.py:152
  8.5 5.8 %collective-permute-start.2 = (bf16[224,512]{1,0:T(8,128)(2,1)S(1)}, bf16[224,512]{1,0:T(8,128)(2,1)S(1)}, u32[]{:S(2)}, u32[]{:S(2)}) collective-permute-start(bf16[224,512]{1,0:T(8,128)(2,1)S(1)} %fusion.6.refs_0_), channel_id=1, source_target_pairs={{4,8},{5,9},{6,10},{7,11},{8,4},{9,5},{10,6},{11,7},{20,24},{21,25... | collective-permute-start | bytes 688136 | tf_op jit(solution)/shard_map/ppermute | solution.py:153
  9.1 8.8 %collective-permute-start.9 = (bf16[224,512]{1,0:T(8,128)(2,1)S(1)}, bf16[224,512]{1,0:T(8,128)(2,1)S(1)}, u32[]{:S(2)}, u32[]{:S(2)}) collective-permute-start(bf16[224,512]{1,0:T(8,128)(2,1)S(1)} %fusion.6.refs_0_), channel_id=1, source_target_pairs={{0,1},{1,0},{2,3},{3,2},{4,5},{5,4},{6,7},{7,6},{8,9},{9,8},{10,11... | collective-permute-start | bytes 688136 | tf_op jit(solution)/shard_map/ppermute | solution.py:239
  9.2 10.0 %collective-permute-start.3 = (bf16[224,512]{1,0:T(8,128)(2,1)S(1)}, bf16[224,512]{1,0:T(8,128)(2,1)S(1)}, u32[]{:S(2)}, u32[]{:S(2)}) collective-permute-start(bf16[224,512]{1,0:T(8,128)(2,1)S(1)} %fusion.6.refs_0_), channel_id=1, source_target_pairs={{0,2},{1,3},{2,0},{3,1},{4,6},{5,7},{6,4},{7,5},{8,10},{9,11},{10,... | collective-permute-start | bytes 688136 | tf_op jit(solution)/shard_map/ppermute | solution.py:154
  10.9 0.6 copy-start.9
  14.3 7.2 %copy-start.14 = (bf16[224,512]{1,0:T(8,128)(2,1)}, bf16[224,512]{1,0:T(8,128)(2,1)S(1)}, u32[]{:S(2)}) copy-start(bf16[224,512]{1,0:T(8,128)(2,1)S(1)} %collective-permute-done.1.refs_1_) | copy-start | bytes 688132
  14.3 15.3 %copy-start.4 = (bf16[224,512]{1,0:T(8,128)(2,1)}, bf16[224,512]{1,0:T(8,128)(2,1)S(1)}, u32[]{:S(2)}) copy-start(bf16[224,512]{1,0:T(8,128)(2,1)S(1)} %collective-permute-done.2.refs_2_) | copy-start | bytes 688132
  14.3 15.9 %collective-permute-start.4 = (bf16[224,512]{1,0:T(8,128)(2,1)S(1)}, bf16[224,512]{1,0:T(8,128)(2,1)S(1)}, u32[]{:S(2)}, u32[]{:S(2)}) collective-permute-start(bf16[224,512]{1,0:T(8,128)(2,1)S(1)} %collective-permute-done.1.refs_1_), channel_id=1, source_target_pairs={{4,8},{5,9},{6,10},{7,11},{8,4},{9,5},{10,6},{11,7},{20,24},{21,25... | collective-permute-start | bytes 688136 | tf_op jit(solution)/shard_map/ppermute | solution.py:156
  15.0 16.6 %collective-permute-start.6 = (bf16[224,512]{1,0:T(8,128)(2,1)S(1)}, bf16[224,512]{1,0:T(8,128)(2,1)S(1)}, u32[]{:S(2)}, u32[]{:S(2)}) collective-permute-start(bf16[224,512]{1,0:T(8,128)(2,1)S(1)} %collective-permute-done.1.refs_1_), channel_id=1, source_target_pairs={{0,2},{1,3},{2,0},{3,1},{4,6},{5,7},{6,4},{7,5},{8,10},{9,11},{10,... | collective-permute-start | bytes 688136 | tf_op jit(solution)/shard_map/ppermute | solution.py:158
  16.7 12.9 %collective-permute-start.5 = (bf16[224,512]{1,0:T(8,128)(2,1)S(1)}, bf16[224,512]{1,0:T(8,128)(2,1)S(1)}, u32[]{:S(2)}, u32[]{:S(2)}) collective-permute-start(bf16[224,512]{1,0:T(8,128)(2,1)S(1)} %collective-permute-done.2.refs_2_), channel_id=1, source_target_pairs={{4,0},{5,1},{6,2},{7,3},{8,12},{9,13},{10,14},{11,15},{20,16},{21,... | collective-permute-start | bytes 688136 | tf_op jit(solution)/shard_map/ppermute | solution.py:157
  19.3 1.1 %copy-start.16 = (bf16[224,512]{1,0:T(8,128)(2,1)}, bf16[224,512]{1,0:T(8,128)(2,1)S(1)}, u32[]{:S(2)}) copy-start(bf16[224,512]{1,0:T(8,128)(2,1)S(1)} %collective-permute-done.3.refs_3_) | copy-start | bytes 688132
  29.6 1.9 %copy-start.8 = (bf16[224,512]{1,0:T(8,128)(2,1)}, bf16[224,512]{1,0:T(8,128)(2,1)S(1)}, u32[]{:S(2)}) copy-start(bf16[224,512]{1,0:T(8,128)(2,1)S(1)} %collective-permute-done.5.refs_5_) | copy-start | bytes 688132
  29.6 11.5 %collective-permute-start.8 = (bf16[224,512]{1,0:T(8,128)(2,1)S(1)}, bf16[224,512]{1,0:T(8,128)(2,1)S(1)}, u32[]{:S(2)}, u32[]{:S(2)}) collective-permute-start(bf16[224,512]{1,0:T(8,128)(2,1)S(1)} %broadcast_select_fusion.1), channel_id=1, source_target_pairs={{0,2},{1,3},{2,0},{3,1},{4,6},{5,7},{6,4},{7,5},{8,10},{9,11},{10,... | collective-permute-start | bytes 688136 | tf_op jit(solution)/shard_map/ppermute | solution.py:160
  30.2 1.3 %copy-start.7 = (bf16[224,512]{1,0:T(8,128)(2,1)}, bf16[224,512]{1,0:T(8,128)(2,1)S(1)}, u32[]{:S(2)}) copy-start(bf16[224,512]{1,0:T(8,128)(2,1)S(1)} %collective-permute-done.4.refs_4_) | copy-start | bytes 688132
  30.2 9.3 %collective-permute-start.7 = (bf16[224,512]{1,0:T(8,128)(2,1)S(1)}, bf16[224,512]{1,0:T(8,128)(2,1)S(1)}, u32[]{:S(2)}, u32[]{:S(2)}) collective-permute-start(bf16[224,512]{1,0:T(8,128)(2,1)S(1)} %collective-permute-done.4.refs_4_), channel_id=1, source_target_pairs={{4,0},{5,1},{6,2},{7,3},{8,12},{9,13},{10,14},{11,15},{20,16},{21,... | collective-permute-start | bytes 688136 | tf_op jit(solution)/shard_map/ppermute | solution.py:159
  31.5 0.7 %copy-start.18 = (bf16[224,512]{1,0:T(8,128)(2,1)}, bf16[224,512]{1,0:T(8,128)(2,1)S(1)}, u32[]{:S(2)}) copy-start(bf16[224,512]{1,0:T(8,128)(2,1)S(1)} %collective-permute-done.6.refs_6_) | copy-start | bytes 688132
  38.8 8.7 %copy-start.3 = (f32[7,16,1024]{2,1,0:T(8,128)S(1)}, f32[7,16,1024]{2,1,0:T(8,128)}, u32[]{:S(2)}) copy-start(f32[7,16,1024]{2,1,0:T(8,128)} %shard_map.95) | copy-start | bytes 1376260
  39.5 1.6 %copy-start.6 = (bf16[224,512]{1,0:T(8,128)(2,1)}, bf16[224,512]{1,0:T(8,128)(2,1)S(1)}, u32[]{:S(2)}) copy-start(bf16[224,512]{1,0:T(8,128)(2,1)S(1)} %collective-permute-done.7.refs_0_) | copy-start | bytes 688132
  39.5 6.1 %collective-permute-start.10 = (bf16[224,512]{1,0:T(8,128)(2,1)S(1)}, bf16[224,512]{1,0:T(8,128)(2,1)S(1)}, u32[]{:S(2)}, u32[]{:S(2)}) collective-permute-start(bf16[224,512]{1,0:T(8,128)(2,1)S(1)} %broadcast_select_fusion), channel_id=1, source_target_pairs={{0,2},{1,3},{2,0},{3,1},{4,6},{5,7},{6,4},{7,5},{8,10},{9,11},{10,... | collective-permute-start | bytes 688136 | tf_op jit(solution)/shard_map/ppermute | solution.py:168
  41.1 6.4 %copy-start.15 = (bf16[224,512]{1,0:T(8,128)(2,1)}, bf16[224,512]{1,0:T(8,128)(2,1)S(1)}, u32[]{:S(2)}) copy-start(bf16[224,512]{1,0:T(8,128)(2,1)S(1)} %collective-permute-done.8.refs_1_) | copy-start | bytes 688132
  45.6 1.9 %copy-start.17 = (bf16[224,512]{1,0:T(8,128)(2,1)}, bf16[224,512]{1,0:T(8,128)(2,1)S(1)}, u32[]{:S(2)}) copy-start(bf16[224,512]{1,0:T(8,128)(2,1)S(1)} %collective-permute-done.10.refs_2_) | copy-start | bytes 688132
  52.1 0.9 %slice-start = ((f32[17,512]{1,0:T(8,128)}), f32[16,512]{1,0:T(8,128)S(1)}, s32[]{:S(2)}) async-start(f32[17,512]{1,0:T(8,128)} %copy-done.9), calls=%async_computation | async-start | bytes 65536 | tf_op jit(solution)/shard_map/slice | solution.py:287
  53.1 3.1 %collective-permute-start.13 = (f32[16,16]{1,0:T(8,128)S(1)}, f32[16,16]{1,0:T(8,128)S(1)}, u32[]{:S(2)}, u32[]{:S(2)}) collective-permute-start(f32[16,16]{1,0:T(8,128)S(1)} %fusion.7), channel_id=1, source_target_pairs={{0,3},{1,2},{2,1},{3,0},{4,7},{5,6},{6,5},{7,4},{8,11},{9,10},{10,... | collective-permute-start | bytes 3080 | tf_op jit(solution)/shard_map/ppermute | solution.py:199
  53.1 3.7 %collective-permute-start.14 = (f32[16,16]{1,0:T(8,128)S(1)}, f32[16,16]{1,0:T(8,128)S(1)}, u32[]{:S(2)}, u32[]{:S(2)}) collective-permute-start(f32[16,16]{1,0:T(8,128)S(1)} %fusion.7), channel_id=1, source_target_pairs={{0,2},{1,3},{2,0},{3,1},{4,6},{5,7},{6,4},{7,5},{8,10},{9,11},{10,... | collective-permute-start | bytes 3080 | tf_op jit(solution)/shard_map/ppermute | solution.py:199
  54.7 2.1 %collective-permute-start.15 = (f32[16,16]{1,0:T(8,128)S(1)}, f32[16,16]{1,0:T(8,128)S(1)}, u32[]{:S(2)}, u32[]{:S(2)}) collective-permute-start(f32[16,16]{1,0:T(8,128)S(1)} %fusion.7), channel_id=1, source_target_pairs={{0,1},{1,0},{2,3},{3,2},{4,5},{5,4},{6,7},{7,6},{8,9},{9,8},{10,11... | collective-permute-start | bytes 3080 | tf_op jit(solution)/shard_map/ppermute | solution.py:199
  56.9 5.5 %collective-permute-start.16 = (f32[16,16]{1,0:T(8,128)S(1)}, f32[16,16]{1,0:T(8,128)S(1)}, u32[]{:S(2)}, u32[]{:S(2)}) collective-permute-start(f32[16,16]{1,0:T(8,128)S(1)} %select_add_fusion), channel_id=1, source_target_pairs={{0,12},{1,13},{2,14},{3,15},{4,8},{5,9},{6,10},{7,11},{8,4},{9,5},... | collective-permute-start | bytes 3080 | tf_op jit(solution)/shard_map/ppermute | solution.py:199
  58.4 5.3 %collective-permute-start.17 = (f32[16,16]{1,0:T(8,128)S(1)}, f32[16,16]{1,0:T(8,128)S(1)}, u32[]{:S(2)}, u32[]{:S(2)}) collective-permute-start(f32[16,16]{1,0:T(8,128)S(1)} %select_add_fusion), channel_id=1, source_target_pairs={{0,8},{1,9},{2,10},{3,11},{4,12},{5,13},{6,14},{7,15},{8,0},{9,1},... | collective-permute-start | bytes 3080 | tf_op jit(solution)/shard_map/ppermute | solution.py:199
  62.1 3.7 %collective-permute-start.18 = (f32[16,16]{1,0:T(8,128)S(1)}, f32[16,16]{1,0:T(8,128)S(1)}, u32[]{:S(2)}, u32[]{:S(2)}) collective-permute-start(f32[16,16]{1,0:T(8,128)S(1)} %select_add_fusion), channel_id=1, source_target_pairs={{0,4},{1,5},{2,6},{3,7},{4,0},{5,1},{6,2},{7,3},{8,12},{9,13},{10,... | collective-permute-start | bytes 3080 | tf_op jit(solution)/shard_map/ppermute | solution.py:199
  62.1 4.3 %collective-permute-start.11 = (f32[16,512]{1,0:T(8,128)S(1)}, f32[16,512]{1,0:T(8,128)S(1)}, u32[]{:S(2)}, u32[]{:S(2)}) collective-permute-start(f32[16,512]{1,0:T(8,128)S(1)} %slice.105), channel_id=1, source_target_pairs={{0,1},{1,0},{2,3},{3,2},{4,5},{5,4},{6,7},{7,6},{8,9},{9,8},{10,11... | collective-permute-start | bytes 98312 | tf_op jit(solution)/shard_map/ppermute | solution.py:293
  65.7 0.6 copy-start.10

commit v17 on v16

--- a/solution.py
+++ b/solution.py
@@ -45,11 +45,19 @@
             )
 
 
-def list_kernel(width, rows, counts, split, flag_ref, xo_ref, no_ref, ro_ref, *refs):
+def list_kernel(width, rows, counts, split, head, flag_ref, xo_ref, no_ref, ro_ref, *refs):
     out_ref = refs[-1]
     if not split:
         out_ref[...] = jnp.zeros_like(out_ref)
-    slot = 0
+    if head:
+        early_ref, refs = refs[0], refs[1:]
+        for k in range(head):
+
+            @pl.when(flag_ref[k] != 0)
+            def _(k=k):
+                out_ref[...] += early_ref[k]
+
+    slot = head
     for ref, count in zip(refs[:-1], counts):
         for k in range(count):
             base = k * rows
@@ -81,7 +89,7 @@
             slot += 1
 
 
-def list_product(flags, own_terms, pieces, width, rows, split=False):
+def list_product(flags, own_terms, pieces, width, rows, split=False, early=None):
     twice_own_t, norm_own, recip_own = own_terms
     own = twice_own_t.shape[0]
     counts = [p.shape[0] // rows for p in pieces]
@@ -94,13 +102,15 @@
         transcendentals=slots * own * cols,
         bytes_accessed=sum(p.size * 2 for p in pieces) + int(math.prod(shape)) * 4,
     )
+    head = 0 if early is None else early.shape[0]
+    extra = [] if early is None else [early]
     return pl.pallas_call(
-        functools.partial(list_kernel, width, rows, counts, split),
+        functools.partial(list_kernel, width, rows, counts, split, head),
         cost_estimate=cost,
-        in_specs=[pl.BlockSpec(memory_space=pltpu.SMEM)] + [vmem] * (3 + len(pieces)),
+        in_specs=[pl.BlockSpec(memory_space=pltpu.SMEM)] + [vmem] * (3 + len(extra) + len(pieces)),
         out_specs=vmem,
         out_shape=jax.ShapeDtypeStruct(shape, jnp.float32),
-    )(flags, twice_own_t, norm_own, recip_own, *pieces)
+    )(flags, twice_own_t, norm_own, recip_own, *extra, *pieces)
 
 
 def own_rows_product(flags, own_terms, mine, width):
@@ -279,8 +289,7 @@
 
     if chip_split:
         head = early.shape[0]
-        summed = list_product(flags[head:], own_terms, pieces[head:], width, rows)
-        summed = summed + jnp.sum(jnp.where(flags[:head, None, None] != 0, early, 0.0), axis=0)
+        summed = list_product(flags, own_terms, pieces[head:], width, rows, early=early)
     else:
         summed = own_rows_product(flags, own_terms, pieces[0].reshape(devices, rows, own), width)
     if chip_split:

time: 66.9 us -> 67.5 us (level)
  matrix products: 0.52 us -> 1.37 us
  starting transfers between devices: 20.2 us -> 21 us
    add x1 -> x0, other arithmetic: 0.85 us -> none  [shards(): summed + jnp.sum(jnp.where(flags[:head, None, None] != 0, early, 0.0), ax...]
    dot_general x1, matrix products: 0.16 us -> 1.01 us  [shards(): lax.dot_general(chip_lanes, summed * (chip_scale[None, :] / math.sqrt(tot...]
    ppermute x6, starting transfers between devices: 7.11 us -> 7.89 us  [sum_over_rows(): lax.ppermute(value, 'row', [(i, i ^ m << shift) for i in range(devices)])]
  transfers between devices with their start and end apart: 19 -> 19, of which waited for: 8 -> 7; matrix products, arithmetic and copies ran while one was open for 9% -> 9% of each run, Pallas kernels for 10% -> 10%
where the time goes in v17:
time: 67.5 us; the launch traced here: 66.9 us
  starting transfers between devices  21 us (31%)
  waiting for transfers between devices  20.9 us (31%)
  Pallas kernels  10.4 us (15%)
  local copies, waits for them, and re-layouts  6.76 us (10%)
  other arithmetic  4.76 us (7%)
  between operations  1.72 us (3%)
  matrix products  1.37 us (2%)
    pallas_call x2, Pallas kernels, list_product(): pl.pallas_call(functools.partial(list_kernel, width, rows, counts, split,...  10.4 us
    ppermute x1, waiting for transfers between devices, gather_pieces(): out2 = lax.ppermute(inner1, 'row', outward)  8.17 us
    ppermute x6, starting transfers between devices, sum_over_rows(): lax.ppermute(value, 'row', [(i, i ^ m << shift) for i in range(devices)])  7.89 us
    ppermute x6, waiting for transfers between devices, sum_over_rows(): lax.ppermute(value, 'row', [(i, i ^ m << shift) for i in range(devices)])  5.42 us
    ppermute x1, waiting for transfers between devices, gather_pieces(): across4 = lax.ppermute(last, 'row', across)  4.46 us
    ppermute x1, starting transfers between devices, gather_pieces(): swap1 = lax.ppermute(packed, 'row', pairs_swap)  3.09 us
    ppermute x1, waiting for transfers between devices, gather_pieces(): swap1 = lax.ppermute(packed, 'row', pairs_swap)  2.76 us
    unnamed x38, local copies, waits for them, and re-layouts  2.34 us
  transfers between devices with their start and end apart: 19, of which 7 were waited for; matrix products, arithmetic and copies ran while one was open for 9% of the time, Pallas kernels for 10%

profile of v17, /device:TPU:0, one launch (start us, length us, event | category | flops | bytes accessed | tf_op | source)
XLA Modules:
  0.0 66.9 jit_solution(13826614143148125502)
XLA Ops:
  0.6 0.7 %convert.8 = bf16[4,2]{0,1:T(2,128)(2,1)S(1)} convert(s32[4,2]{0,1:T(2,128)} %param.14) | non-fusion elementwise | flops 8 | bytes 48 | tf_op jit(solution)/shard_map/convert.3
  1.3 0.1 copy.43
  2.3 0.5 collective-permute-start
  2.7 0.8 %pad_maximum_fusion.1 = f32[17,512]{1,0:T(8,128)S(1)} fusion(f32[1,512]{1,0:T(1,128)S(1)} %bitcast.64, f32[16,512]{1,0:T(8,128)} %param.11), kind=kLoop, calls=%fused_computation.19 | loop fusion | flops 8704 | bytes 69632 | tf_op jit(solution)/shard_map/concatenate | solution.py:251
  3.6 0.1 stack.50
  3.8 0.1 stack.61
  3.9 0.5 convert_element_type.35.flag_ref
  4.5 0.6 copy-done.12
  5.1 0.1 fusion.24
  5.4 3.1 %collective-permute-start.1 = (bf16[224,512]{1,0:T(8,128)(2,1)S(1)}, bf16[224,512]{1,0:T(8,128)(2,1)S(1)}, u32[]{:S(2)}, u32[]{:S(2)}) collective-permute-start(bf16[224,512]{1,0:T(8,128)(2,1)S(1)} %fusion.6.refs_0_), channel_id=1, source_target_pairs={{0,4},{1,5},{2,6},{3,7},{4,0},{5,1},{6,2},{7,3},{8,12},{9,13},{10,... | collective-permute-start | bytes 688136 | tf_op jit(solution)/shard_map/ppermute | solution.py:162
  8.5 0.7 collective-permute-start.2
  9.2 1.6 %collective-permute-start.3 = (bf16[224,512]{1,0:T(8,128)(2,1)S(1)}, bf16[224,512]{1,0:T(8,128)(2,1)S(1)}, u32[]{:S(2)}, u32[]{:S(2)}) collective-permute-start(bf16[224,512]{1,0:T(8,128)(2,1)S(1)} %fusion.6.refs_0_), channel_id=1, source_target_pairs={{0,2},{1,3},{2,0},{3,1},{4,6},{5,7},{6,4},{7,5},{8,10},{9,11},{10,... | collective-permute-start | bytes 688136 | tf_op jit(solution)/shard_map/ppermute | solution.py:164
  10.9 0.6 copy-done.9
  11.5 2.8 %collective-permute-done.1.refs_1_ = bf16[224,512]{1,0:T(8,128)(2,1)S(1)} collective-permute-done((bf16[224,512]{1,0:T(8,128)(2,1)S(1)}, bf16[224,512]{1,0:T(8,128)(2,1)S(1)}, u32[]{:S(2)}, u32[]{:S(2)}) %collective-permute-start.1) | collective-permute-done | bytes 229408 | tf_op jit(solution)/shard_map/ppermute | solution.py:162
  14.3 0.7 %collective-permute-start.4 = (bf16[224,512]{1,0:T(8,128)(2,1)S(1)}, bf16[224,512]{1,0:T(8,128)(2,1)S(1)}, u32[]{:S(2)}, u32[]{:S(2)}) collective-permute-start(bf16[224,512]{1,0:T(8,128)(2,1)S(1)} %collective-permute-done.1.refs_1_), channel_id=1, source_target_pairs={{4,8},{5,9},{6,10},{7,11},{8,4},{9,5},{10,6},{11,7},{20,24},{21,25... | collective-permute-start | bytes 688136 | tf_op jit(solution)/shard_map/ppermute | solution.py:166
  14.9 1.7 %collective-permute-start.6 = (bf16[224,512]{1,0:T(8,128)(2,1)S(1)}, bf16[224,512]{1,0:T(8,128)(2,1)S(1)}, u32[]{:S(2)}, u32[]{:S(2)}) collective-permute-start(bf16[224,512]{1,0:T(8,128)(2,1)S(1)} %collective-permute-done.1.refs_1_), channel_id=1, source_target_pairs={{0,2},{1,3},{2,0},{3,1},{4,6},{5,7},{6,4},{7,5},{8,10},{9,11},{10,... | collective-permute-start | bytes 688136 | tf_op jit(solution)/shard_map/ppermute | solution.py:168
  16.7 1.3 %collective-permute-start.5 = (bf16[224,512]{1,0:T(8,128)(2,1)S(1)}, bf16[224,512]{1,0:T(8,128)(2,1)S(1)}, u32[]{:S(2)}, u32[]{:S(2)}) collective-permute-start(bf16[224,512]{1,0:T(8,128)(2,1)S(1)} %collective-permute-done.2.refs_2_), channel_id=1, source_target_pairs={{4,0},{5,1},{6,2},{7,3},{8,12},{9,13},{10,14},{11,15},{20,16},{21,... | collective-permute-start | bytes 688136 | tf_op jit(solution)/shard_map/ppermute | solution.py:167
  18.1 0.2 copy.44
  18.3 0.9 %broadcast_divide_fusion.ro_ref = f32[1024,1]{1,0:T(8,128)} fusion(f32[1024,1]{1,0:T(8,128)S(1)} %copy.44), kind=kLoop, calls=%fused_computation.8 | loop fusion | flops 1024 | bytes 8192 | tf_op jit(solution)/shard_map/div | solution.py:259
  19.3 1.0 %copy.45.xo_ref = bf16[1024,192]{1,0:T(8,128)(2,1)} copy(bf16[1024,192]{0,1:T(8,128)(2,1)S(1)} %multiply_bitcast_fusion) | data formatting | bytes 786432 | tf_op jit(solution)/shard_map/transpose | solution.py:260
  20.4 1.0 %copy.46.no_ref = f32[1024,1]{1,0:T(8,128)} copy(f32[1024,1]{0,1:T(1,128)S(1)} %bitcast.65) | data formatting | bytes 8192 | tf_op jit(solution)/shard_map/broadcast_in_dim | solution.py:257
  21.4 8.2 %collective-permute-done.5.refs_5_ = bf16[224,512]{1,0:T(8,128)(2,1)S(1)} collective-permute-done((bf16[224,512]{1,0:T(8,128)(2,1)S(1)}, bf16[224,512]{1,0:T(8,128)(2,1)S(1)}, u32[]{:S(2)}, u32[]{:S(2)}) %collective-permute-start.5) | collective-permute-done | bytes 229408 | tf_op jit(solution)/shard_map/ppermute | solution.py:167
  29.6 0.6 collective-permute-start.8
  30.2 1.3 %collective-permute-start.7 = (bf16[224,512]{1,0:T(8,128)(2,1)S(1)}, bf16[224,512]{1,0:T(8,128)(2,1)S(1)}, u32[]{:S(2)}, u32[]{:S(2)}) collective-permute-start(bf16[224,512]{1,0:T(8,128)(2,1)S(1)} %collective-permute-done.4.refs_4_), channel_id=1, source_target_pairs={{4,0},{5,1},{6,2},{7,3},{8,12},{9,13},{10,14},{11,15},{20,16},{21,... | collective-permute-start | bytes 688136 | tf_op jit(solution)/shard_map/ppermute | solution.py:169
  31.5 0.7 %copy-done.18 = bf16[224,512]{1,0:T(8,128)(2,1)} copy-done((bf16[224,512]{1,0:T(8,128)(2,1)}, bf16[224,512]{1,0:T(8,128)(2,1)S(1)}, u32[]{:S(2)}) %copy-start.18) | copy-done | bytes 229400
  32.2 6.5 %shard_map.95.refs_0_ = f32[7,16,1024]{2,1,0:T(8,128)} custom-call(s32[7]{0:T(128)} %convert_element_type.35.flag_ref, bf16[1024,192]{1,0:T(8,128)(2,1)} %copy.45.xo_ref, f32[1024,1]{1,0:T(8,128)} %copy.46.no_ref, f32[1024,1]{1,0:T(8,128)} %broadcast_divide_fusion.ro_ref, bf16[224,512]{1,0:T(8,128)(2,1)} %copy-done.5, bf16[224,512]{1,0:T(8,128)(2,1)} %copy-done.14, ...), custom_call_target="tpu_custom_call" | custom-call | flops 1526726656 | bytes 2064384 | tf_op jit(solution)/shard_map/pallas_call | solution.py:107
  38.7 0.7 %slice_bitcast_fusion.4 = bf16[1,18]{1,0:T(2,128)(2,1)S(1)} fusion(bf16[1,224,512]{2,1,0:T(8,128)(2,1)} %bitcast.72), kind=kLoop, calls=%fused_computation.49 | loop fusion | bytes 72 | tf_op jit(solution)/shard_map/squeeze | solution.py:271
  39.4 1.6 %collective-permute-start.10 = (bf16[224,512]{1,0:T(8,128)(2,1)S(1)}, bf16[224,512]{1,0:T(8,128)(2,1)S(1)}, u32[]{:S(2)}, u32[]{:S(2)}) collective-permute-start(bf16[224,512]{1,0:T(8,128)(2,1)S(1)} %broadcast_select_fusion), channel_id=1, source_target_pairs={{0,2},{1,3},{2,0},{3,1},{4,6},{5,7},{6,4},{7,5},{8,10},{9,11},{10,... | collective-permute-start | bytes 688136 | tf_op jit(solution)/shard_map/ppermute | solution.py:178
  41.1 4.5 %collective-permute-done.10.refs_3_ = bf16[224,512]{1,0:T(8,128)(2,1)S(1)} collective-permute-done((bf16[224,512]{1,0:T(8,128)(2,1)S(1)}, bf16[224,512]{1,0:T(8,128)(2,1)S(1)}, u32[]{:S(2)}, u32[]{:S(2)}) %collective-permute-start.10) | collective-permute-done | bytes 229408 | tf_op jit(solution)/shard_map/ppermute | solution.py:178
  45.7 0.2 slice_reduce_fusion
  45.9 0.1 copy.48
  46.0 0.1 broadcast_in_dim_reshape_squeeze.4
  46.4 0.1 lt.26
  46.5 0.2 and_reduce_fusion
  46.7 0.5 and_convert_fusion.flag_ref
  47.3 4.0 %shard_map.96 = f32[16,1024]{1,0:T(8,128)} custom-call(s32[10]{0:T(128)} %and_convert_fusion.flag_ref, bf16[1024,192]{1,0:T(8,128)(2,1)} %copy.45.xo_ref, f32[1024,1]{1,0:T(8,128)} %copy.46.no_ref, f32[1024,1]{1,0:T(8,128)} %broadcast_divide_fusion.ro_ref, f32[7,16,1024]{2,1,0:T(8,128)} %shard_map.95.refs_0_, bf16[224,512]{1,0:T(8,128)(2,1)} %copy-done.6, ...), custom_call_target="tpu_custom_call" | custom-call | flops 654311424 | bytes 753664 | tf_op jit(solution)/shard_map/pallas_call | solution.py:107
  51.2 1.0 %fusion.7 = f32[16,16]{1,0:T(8,128)S(1)} fusion(f32[16,512]{1,0:T(8,128)S(1)} %slice-done, f32[16,512]{1,0:T(8,128)S(1)} %copy-done.2, f32[16,1024]{1,0:T(8,128)} %shard_map.96, f32[1024]{0:T(1024)S(1)} %maximum_multiply_fusion), kind=kOutput, calls=%fused_computation.14 | convolution fusion | flops 3178496 | bytes 136192 | tf_op jit(solution)/shard_map/dot_general | solution.py:298
  52.3 1.6 %collective-permute-start.14 = (f32[16,16]{1,0:T(8,128)S(1)}, f32[16,16]{1,0:T(8,128)S(1)}, u32[]{:S(2)}, u32[]{:S(2)}) collective-permute-start(f32[16,16]{1,0:T(8,128)S(1)} %fusion.7), channel_id=1, source_target_pairs={{0,2},{1,3},{2,0},{3,1},{4,6},{5,7},{6,4},{7,5},{8,10},{9,11},{10,... | collective-permute-start | bytes 3080 | tf_op jit(solution)/shard_map/ppermute | solution.py:209
  53.9 0.3 collective-permute-start.15
  54.2 1.2 %collective-permute-done.13 = f32[16,16]{1,0:T(8,128)S(1)} collective-permute-done((f32[16,16]{1,0:T(8,128)S(1)}, f32[16,16]{1,0:T(8,128)S(1)}, u32[]{:S(2)}, u32[]{:S(2)}) %collective-permute-start.13) | collective-permute-done | bytes 1056 | tf_op jit(solution)/shard_map/ppermute | solution.py:209
  55.4 0.6 collective-permute-done.14
  56.1 2.3 %collective-permute-start.16 = (f32[16,16]{1,0:T(8,128)S(1)}, f32[16,16]{1,0:T(8,128)S(1)}, u32[]{:S(2)}, u32[]{:S(2)}) collective-permute-start(f32[16,16]{1,0:T(8,128)S(1)} %select_add_fusion), channel_id=1, source_target_pairs={{0,12},{1,13},{2,14},{3,15},{4,8},{5,9},{6,10},{7,11},{8,4},{9,5},... | collective-permute-start | bytes 3080 | tf_op jit(solution)/shard_map/ppermute | solution.py:209
  58.4 3.6 %collective-permute-start.17 = (f32[16,16]{1,0:T(8,128)S(1)}, f32[16,16]{1,0:T(8,128)S(1)}, u32[]{:S(2)}, u32[]{:S(2)}) collective-permute-start(f32[16,16]{1,0:T(8,128)S(1)} %select_add_fusion), channel_id=1, source_target_pairs={{0,8},{1,9},{2,10},{3,11},{4,12},{5,13},{6,14},{7,15},{8,0},{9,1},... | collective-permute-start | bytes 3080 | tf_op jit(solution)/shard_map/ppermute | solution.py:209
  62.1 1.6 %collective-permute-done.17 = f32[16,16]{1,0:T(8,128)S(1)} collective-permute-done((f32[16,16]{1,0:T(8,128)S(1)}, f32[16,16]{1,0:T(8,128)S(1)}, u32[]{:S(2)}, u32[]{:S(2)}) %collective-permute-start.17) | collective-permute-done | bytes 1056 | tf_op jit(solution)/shard_map/ppermute | solution.py:209
  63.8 1.9 %collective-permute-done.18 = f32[16,16]{1,0:T(8,128)S(1)} collective-permute-done((f32[16,16]{1,0:T(8,128)S(1)}, f32[16,16]{1,0:T(8,128)S(1)}, u32[]{:S(2)}, u32[]{:S(2)}) %collective-permute-start.18) | collective-permute-done | bytes 1056 | tf_op jit(solution)/shard_map/ppermute | solution.py:209
  65.7 0.2 fusion.23
  65.9 0.4 copy-done.10
  66.3 0.6 fusion.14
  (96 shorter events, 1.7 us)
Async XLA Ops:
  0.6 3.9 %copy-start = (f32[16,512]{1,0:T(8,128)S(1)}, f32[16,512]{1,0:T(8,128)}, u32[]{:S(2)}) copy-start(f32[16,512]{1,0:T(8,128)} %param.12) | copy-start | bytes 98308
  1.4 1.3 %copy-start.11 = (f32[512]{0:T(512)S(1)}, f32[512]{0:T(512)}, u32[]{:S(2)}) copy-start(f32[512]{0:T(512)} %param.10) | copy-start | bytes 6148
  1.5 2.0 %copy-start.2 = (f32[16,512]{1,0:T(8,128)S(1)}, f32[16,512]{1,0:T(8,128)}, u32[]{:S(2)}) copy-start(f32[16,512]{1,0:T(8,128)} %param.11) | copy-start | bytes 98308
  1.5 2.1 %copy-start.13 = (bf16[512]{0:T(512)(128)(2,1)S(1)}, bf16[512]{0:T(512)(128)(2,1)}, u32[]{:S(2)}) copy-start(bf16[512]{0:T(512)(128)(2,1)} %param.9) | copy-start | bytes 3076
  2.2 3.1 %copy-start.1 = (bf16[192,512]{1,0:T(8,128)(2,1)S(1)}, bf16[192,512]{1,0:T(8,128)(2,1)}, u32[]{:S(2)}) copy-start(bf16[192,512]{1,0:T(8,128)(2,1)} %param.8) | copy-start | bytes 589828
  2.3 2.9 %collective-permute-start = (bf16[9]{0:T(256)(128)(2,1)S(1)}, bf16[9]{0:T(256)(128)(2,1)S(1)}, u32[]{:S(2)}, u32[]{:S(2)}) collective-permute-start(bf16[9]{0:T(256)(128)(2,1)S(1)} %pad_maximum_fusion.2), channel_id=1, source_target_pairs={{0,1},{1,0},{2,3},{3,2},{4,5},{5,4},{6,7},{7,6},{8,9},{9,8},{10,11... | collective-permute-start | bytes 62 | tf_op jit(solution)/shard_map/ppermute | solution.py:241
  3.5 7.3 %collective-permute-start.12 = (f32[17,512]{1,0:T(8,128)S(1)}, f32[17,512]{1,0:T(8,128)S(1)}, u32[]{:S(2)}, u32[]{:S(2)}) collective-permute-start(f32[17,512]{1,0:T(8,128)S(1)} %pad_maximum_fusion.1), channel_id=1, source_target_pairs={{0,1},{1,0},{2,3},{3,2},{4,5},{5,4},{6,7},{7,6},{8,9},{9,8},{10,11... | collective-permute-start | bytes 104456 | tf_op jit(solution)/shard_map/ppermute | solution.py:250
  4.4 0.7 %copy-start.12 = (f32[16,16]{1,0:T(8,128)S(1)}, f32[16,16]{1,0:T(8,128)}, u32[]{:S(2)}) copy-start(f32[16,16]{1,0:T(8,128)} %param.13) | copy-start | bytes 3076
  5.4 5.5 %copy-start.5 = (bf16[224,512]{1,0:T(8,128)(2,1)}, bf16[224,512]{1,0:T(8,128)(2,1)S(1)}, u32[]{:S(2)}) copy-start(bf16[224,512]{1,0:T(8,128)(2,1)S(1)} %fusion.6.refs_0_) | copy-start | bytes 688132
  5.4 8.9 %collective-permute-start.1 = (bf16[224,512]{1,0:T(8,128)(2,1)S(1)}, bf16[224,512]{1,0:T(8,128)(2,1)S(1)}, u32[]{:S(2)}, u32[]{:S(2)}) collective-permute-start(bf16[224,512]{1,0:T(8,128)(2,1)S(1)} %fusion.6.refs_0_), channel_id=1, source_target_pairs={{0,4},{1,5},{2,6},{3,7},{4,0},{5,1},{6,2},{7,3},{8,12},{9,13},{10,... | collective-permute-start | bytes 688136 | tf_op jit(solution)/shard_map/ppermute | solution.py:162
  8.5 5.8 %collective-permute-start.2 = (bf16[224,512]{1,0:T(8,128)(2,1)S(1)}, bf16[224,512]{1,0:T(8,128)(2,1)S(1)}, u32[]{:S(2)}, u32[]{:S(2)}) collective-permute-start(bf16[224,512]{1,0:T(8,128)(2,1)S(1)} %fusion.6.refs_0_), channel_id=1, source_target_pairs={{4,8},{5,9},{6,10},{7,11},{8,4},{9,5},{10,6},{11,7},{20,24},{21,25... | collective-permute-start | bytes 688136 | tf_op jit(solution)/shard_map/ppermute | solution.py:163
  9.1 8.8 %collective-permute-start.9 = (bf16[224,512]{1,0:T(8,128)(2,1)S(1)}, bf16[224,512]{1,0:T(8,128)(2,1)S(1)}, u32[]{:S(2)}, u32[]{:S(2)}) collective-permute-start(bf16[224,512]{1,0:T(8,128)(2,1)S(1)} %fusion.6.refs_0_), channel_id=1, source_target_pairs={{0,1},{1,0},{2,3},{3,2},{4,5},{5,4},{6,7},{7,6},{8,9},{9,8},{10,11... | collective-permute-start | bytes 688136 | tf_op jit(solution)/shard_map/ppermute | solution.py:249
  9.2 10.0 %collective-permute-start.3 = (bf16[224,512]{1,0:T(8,128)(2,1)S(1)}, bf16[224,512]{1,0:T(8,128)(2,1)S(1)}, u32[]{:S(2)}, u32[]{:S(2)}) collective-permute-start(bf16[224,512]{1,0:T(8,128)(2,1)S(1)} %fusion.6.refs_0_), channel_id=1, source_target_pairs={{0,2},{1,3},{2,0},{3,1},{4,6},{5,7},{6,4},{7,5},{8,10},{9,11},{10,... | collective-permute-start | bytes 688136 | tf_op jit(solution)/shard_map/ppermute | solution.py:164
  10.8 0.6 copy-start.9
  14.3 7.1 %copy-start.14 = (bf16[224,512]{1,0:T(8,128)(2,1)}, bf16[224,512]{1,0:T(8,128)(2,1)S(1)}, u32[]{:S(2)}) copy-start(bf16[224,512]{1,0:T(8,128)(2,1)S(1)} %collective-permute-done.1.refs_1_) | copy-start | bytes 688132
  14.3 15.3 %copy-start.4 = (bf16[224,512]{1,0:T(8,128)(2,1)}, bf16[224,512]{1,0:T(8,128)(2,1)S(1)}, u32[]{:S(2)}) copy-start(bf16[224,512]{1,0:T(8,128)(2,1)S(1)} %collective-permute-done.2.refs_2_) | copy-start | bytes 688132
  14.3 15.9 %collective-permute-start.4 = (bf16[224,512]{1,0:T(8,128)(2,1)S(1)}, bf16[224,512]{1,0:T(8,128)(2,1)S(1)}, u32[]{:S(2)}, u32[]{:S(2)}) collective-permute-start(bf16[224,512]{1,0:T(8,128)(2,1)S(1)} %collective-permute-done.1.refs_1_), channel_id=1, source_target_pairs={{4,8},{5,9},{6,10},{7,11},{8,4},{9,5},{10,6},{11,7},{20,24},{21,25... | collective-permute-start | bytes 688136 | tf_op jit(solution)/shard_map/ppermute | solution.py:166
  14.9 16.6 %collective-permute-start.6 = (bf16[224,512]{1,0:T(8,128)(2,1)S(1)}, bf16[224,512]{1,0:T(8,128)(2,1)S(1)}, u32[]{:S(2)}, u32[]{:S(2)}) collective-permute-start(bf16[224,512]{1,0:T(8,128)(2,1)S(1)} %collective-permute-done.1.refs_1_), channel_id=1, source_target_pairs={{0,2},{1,3},{2,0},{3,1},{4,6},{5,7},{6,4},{7,5},{8,10},{9,11},{10,... | collective-permute-start | bytes 688136 | tf_op jit(solution)/shard_map/ppermute | solution.py:168
  16.7 12.9 %collective-permute-start.5 = (bf16[224,512]{1,0:T(8,128)(2,1)S(1)}, bf16[224,512]{1,0:T(8,128)(2,1)S(1)}, u32[]{:S(2)}, u32[]{:S(2)}) collective-permute-start(bf16[224,512]{1,0:T(8,128)(2,1)S(1)} %collective-permute-done.2.refs_2_), channel_id=1, source_target_pairs={{4,0},{5,1},{6,2},{7,3},{8,12},{9,13},{10,14},{11,15},{20,16},{21,... | collective-permute-start | bytes 688136 | tf_op jit(solution)/shard_map/ppermute | solution.py:167
  19.2 1.1 %copy-start.16 = (bf16[224,512]{1,0:T(8,128)(2,1)}, bf16[224,512]{1,0:T(8,128)(2,1)S(1)}, u32[]{:S(2)}) copy-start(bf16[224,512]{1,0:T(8,128)(2,1)S(1)} %collective-permute-done.3.refs_3_) | copy-start | bytes 688132
  29.6 1.9 %copy-start.8 = (bf16[224,512]{1,0:T(8,128)(2,1)}, bf16[224,512]{1,0:T(8,128)(2,1)S(1)}, u32[]{:S(2)}) copy-start(bf16[224,512]{1,0:T(8,128)(2,1)S(1)} %collective-permute-done.5.refs_5_) | copy-start | bytes 688132
  29.6 11.4 %collective-permute-start.8 = (bf16[224,512]{1,0:T(8,128)(2,1)S(1)}, bf16[224,512]{1,0:T(8,128)(2,1)S(1)}, u32[]{:S(2)}, u32[]{:S(2)}) collective-permute-start(bf16[224,512]{1,0:T(8,128)(2,1)S(1)} %broadcast_select_fusion.1), channel_id=1, source_target_pairs={{0,2},{1,3},{2,0},{3,1},{4,6},{5,7},{6,4},{7,5},{8,10},{9,11},{10,... | collective-permute-start | bytes 688136 | tf_op jit(solution)/shard_map/ppermute | solution.py:170
  30.2 1.3 %copy-start.7 = (bf16[224,512]{1,0:T(8,128)(2,1)}, bf16[224,512]{1,0:T(8,128)(2,1)S(1)}, u32[]{:S(2)}) copy-start(bf16[224,512]{1,0:T(8,128)(2,1)S(1)} %collective-permute-done.4.refs_4_) | copy-start | bytes 688132
  30.2 9.2 %collective-permute-start.7 = (bf16[224,512]{1,0:T(8,128)(2,1)S(1)}, bf16[224,512]{1,0:T(8,128)(2,1)S(1)}, u32[]{:S(2)}, u32[]{:S(2)}) collective-permute-start(bf16[224,512]{1,0:T(8,128)(2,1)S(1)} %collective-permute-done.4.refs_4_), channel_id=1, source_target_pairs={{4,0},{5,1},{6,2},{7,3},{8,12},{9,13},{10,14},{11,15},{20,16},{21,... | collective-permute-start | bytes 688136 | tf_op jit(solution)/shard_map/ppermute | solution.py:169
  31.5 0.7 %copy-start.18 = (bf16[224,512]{1,0:T(8,128)(2,1)}, bf16[224,512]{1,0:T(8,128)(2,1)S(1)}, u32[]{:S(2)}) copy-start(bf16[224,512]{1,0:T(8,128)(2,1)S(1)} %collective-permute-done.6.refs_6_) | copy-start | bytes 688132
  39.4 1.6 %copy-start.6 = (bf16[224,512]{1,0:T(8,128)(2,1)}, bf16[224,512]{1,0:T(8,128)(2,1)S(1)}, u32[]{:S(2)}) copy-start(bf16[224,512]{1,0:T(8,128)(2,1)S(1)} %collective-permute-done.7.refs_1_) | copy-start | bytes 688132
  39.4 6.1 %collective-permute-start.10 = (bf16[224,512]{1,0:T(8,128)(2,1)S(1)}, bf16[224,512]{1,0:T(8,128)(2,1)S(1)}, u32[]{:S(2)}, u32[]{:S(2)}) collective-permute-start(bf16[224,512]{1,0:T(8,128)(2,1)S(1)} %broadcast_select_fusion), channel_id=1, source_target_pairs={{0,2},{1,3},{2,0},{3,1},{4,6},{5,7},{6,4},{7,5},{8,10},{9,11},{10,... | collective-permute-start | bytes 688136 | tf_op jit(solution)/shard_map/ppermute | solution.py:178
  41.0 6.2 %copy-start.15 = (bf16[224,512]{1,0:T(8,128)(2,1)}, bf16[224,512]{1,0:T(8,128)(2,1)S(1)}, u32[]{:S(2)}) copy-start(bf16[224,512]{1,0:T(8,128)(2,1)S(1)} %collective-permute-done.8.refs_2_) | copy-start | bytes 688132
  45.5 1.7 %copy-start.17 = (bf16[224,512]{1,0:T(8,128)(2,1)}, bf16[224,512]{1,0:T(8,128)(2,1)S(1)}, u32[]{:S(2)}) copy-start(bf16[224,512]{1,0:T(8,128)(2,1)S(1)} %collective-permute-done.10.refs_3_) | copy-start | bytes 688132
  47.3 4.0 %slice-start = ((f32[17,512]{1,0:T(8,128)}), f32[16,512]{1,0:T(8,128)S(1)}, s32[]{:S(2)}) async-start(f32[17,512]{1,0:T(8,128)} %copy-done.9), calls=%async_computation | async-start | bytes 65536 | tf_op jit(solution)/shard_map/slice | solution.py:296
  52.2 9.8 %copy-start.3 = (f32[16,1024]{1,0:T(8,128)S(1)}, f32[16,1024]{1,0:T(8,128)}, u32[]{:S(2)}) copy-start(f32[16,1024]{1,0:T(8,128)} %shard_map.96) | copy-start | bytes 196612
  52.3 3.2 %collective-permute-start.13 = (f32[16,16]{1,0:T(8,128)S(1)}, f32[16,16]{1,0:T(8,128)S(1)}, u32[]{:S(2)}, u32[]{:S(2)}) collective-permute-start(f32[16,16]{1,0:T(8,128)S(1)} %fusion.7), channel_id=1, source_target_pairs={{0,3},{1,2},{2,1},{3,0},{4,7},{5,6},{6,5},{7,4},{8,11},{9,10},{10,... | collective-permute-start | bytes 3080 | tf_op jit(solution)/shard_map/ppermute | solution.py:209
  52.3 3.7 %collective-permute-start.14 = (f32[16,16]{1,0:T(8,128)S(1)}, f32[16,16]{1,0:T(8,128)S(1)}, u32[]{:S(2)}, u32[]{:S(2)}) collective-permute-start(f32[16,16]{1,0:T(8,128)S(1)} %fusion.7), channel_id=1, source_target_pairs={{0,2},{1,3},{2,0},{3,1},{4,6},{5,7},{6,4},{7,5},{8,10},{9,11},{10,... | collective-permute-start | bytes 3080 | tf_op jit(solution)/shard_map/ppermute | solution.py:209
  53.9 2.1 %collective-permute-start.15 = (f32[16,16]{1,0:T(8,128)S(1)}, f32[16,16]{1,0:T(8,128)S(1)}, u32[]{:S(2)}, u32[]{:S(2)}) collective-permute-start(f32[16,16]{1,0:T(8,128)S(1)} %fusion.7), channel_id=1, source_target_pairs={{0,1},{1,0},{2,3},{3,2},{4,5},{5,4},{6,7},{7,6},{8,9},{9,8},{10,11... | collective-permute-start | bytes 3080 | tf_op jit(solution)/shard_map/ppermute | solution.py:209
  56.1 6.1 %collective-permute-start.16 = (f32[16,16]{1,0:T(8,128)S(1)}, f32[16,16]{1,0:T(8,128)S(1)}, u32[]{:S(2)}, u32[]{:S(2)}) collective-permute-start(f32[16,16]{1,0:T(8,128)S(1)} %select_add_fusion), channel_id=1, source_target_pairs={{0,12},{1,13},{2,14},{3,15},{4,8},{5,9},{6,10},{7,11},{8,4},{9,5},... | collective-permute-start | bytes 3080 | tf_op jit(solution)/shard_map/ppermute | solution.py:209
  58.4 5.3 %collective-permute-start.17 = (f32[16,16]{1,0:T(8,128)S(1)}, f32[16,16]{1,0:T(8,128)S(1)}, u32[]{:S(2)}, u32[]{:S(2)}) collective-permute-start(f32[16,16]{1,0:T(8,128)S(1)} %select_add_fusion), channel_id=1, source_target_pairs={{0,8},{1,9},{2,10},{3,11},{4,12},{5,13},{6,14},{7,15},{8,0},{9,1},... | collective-permute-start | bytes 3080 | tf_op jit(solution)/shard_map/ppermute | solution.py:209
  62.0 3.7 %collective-permute-start.18 = (f32[16,16]{1,0:T(8,128)S(1)}, f32[16,16]{1,0:T(8,128)S(1)}, u32[]{:S(2)}, u32[]{:S(2)}) collective-permute-start(f32[16,16]{1,0:T(8,128)S(1)} %select_add_fusion), channel_id=1, source_target_pairs={{0,4},{1,5},{2,6},{3,7},{4,0},{5,1},{6,2},{7,3},{8,12},{9,13},{10,... | collective-permute-start | bytes 3080 | tf_op jit(solution)/shard_map/ppermute | solution.py:209
  62.1 4.3 %collective-permute-start.11 = (f32[16,512]{1,0:T(8,128)S(1)}, f32[16,512]{1,0:T(8,128)S(1)}, u32[]{:S(2)}, u32[]{:S(2)}) collective-permute-start(f32[16,512]{1,0:T(8,128)S(1)} %slice.97), channel_id=1, source_target_pairs={{0,1},{1,0},{2,3},{3,2},{4,5},{5,4},{6,7},{7,6},{8,9},{9,8},{10,11... | collective-permute-start | bytes 98312 | tf_op jit(solution)/shard_map/ppermute | solution.py:302
  65.7 0.6 copy-start.10

commit v18 on v16

--- a/solution.py
+++ b/solution.py
@@ -58,7 +58,7 @@
                 return piece_terms(
                     width,
                     ref[base : base + width, :],
-                    ref[base + width : base + width + 2 * LANCZOS, :],
+                    ref[base + width : base + width + LANCZOS + 1, :],
                     xo_ref, no_ref, ro_ref,
                 )
 
@@ -233,7 +233,7 @@
     packed = jnp.concatenate(
         [embeddings, weighted, local_scale[None, :], plan_row[None, :]], axis=0
     )
-    packed = jnp.pad(packed, ((0, -packed.shape[0] % (2 * LANCZOS)), (0, 0)))
+    packed = jnp.pad(packed, ((0, -packed.shape[0] % (8 if chip_split else 2 * LANCZOS)), (0, 0)))
     rows = packed.shape[0]
     if chip_split:
         twin_piece = lax.ppermute(packed, "row", twin)

time: 66.9 us -> 66.9 us (level)
  Pallas kernels: 11 us -> 10.2 us
  starting transfers between devices: 20.2 us -> 20.9 us
    pallas_call x2, Pallas kernels: 11 us -> 10.2 us  [list_product(): pl.pallas_call(functools.partial(list_kernel, width, rows, counts, split)...]
    ppermute x6, starting transfers between devices: 7.11 us -> 7.86 us  [sum_over_rows(): lax.ppermute(value, 'row', [(i, i ^ m << shift) for i in range(devices)])]
  transfers between devices with their start and end apart: 19 -> 19, of which waited for: 8 -> 7; matrix products, arithmetic and copies ran while one was open for 9% -> 10% of each run, Pallas kernels for 10% -> 10%
where the time goes in v18:
time: 66.9 us; the launch traced here: 66.7 us
  starting transfers between devices  20.9 us (31%)
  waiting for transfers between devices  20.7 us (31%)
  Pallas kernels  10.2 us (15%)
  local copies, waits for them, and re-layouts  7.38 us (11%)
  other arithmetic  5.25 us (8%)
  between operations  1.74 us (3%)
    pallas_call x2, Pallas kernels, list_product(): pl.pallas_call(functools.partial(list_kernel, width, rows, counts, split)...  10.2 us
    ppermute x1, waiting for transfers between devices, gather_pieces(): out2 = lax.ppermute(inner1, 'row', outward)  8.18 us
    ppermute x6, starting transfers between devices, sum_over_rows(): lax.ppermute(value, 'row', [(i, i ^ m << shift) for i in range(devices)])  7.86 us
    ppermute x6, waiting for transfers between devices, sum_over_rows(): lax.ppermute(value, 'row', [(i, i ^ m << shift) for i in range(devices)])  5.46 us
    ppermute x1, waiting for transfers between devices, gather_pieces(): across4 = lax.ppermute(last, 'row', across)  4.38 us
    ppermute x1, starting transfers between devices, gather_pieces(): swap1 = lax.ppermute(packed, 'row', pairs_swap)  3.09 us
    ppermute x1, waiting for transfers between devices, gather_pieces(): swap1 = lax.ppermute(packed, 'row', pairs_swap)  2.62 us
    unnamed x38, local copies, waits for them, and re-layouts  2.3 us
  transfers between devices with their start and end apart: 19, of which 7 were waited for; matrix products, arithmetic and copies ran while one was open for 10% of the time, Pallas kernels for 10%

profile of v18, /device:TPU:0, one launch (start us, length us, event | category | flops | bytes accessed | tf_op | source)
XLA Modules:
  0.0 66.7 jit_solution(15261113852285993770)
XLA Ops:
  0.6 0.7 %convert.8 = bf16[4,2]{0,1:T(2,128)(2,1)S(1)} convert(s32[4,2]{0,1:T(2,128)} %param.14) | non-fusion elementwise | flops 8 | bytes 48 | tf_op jit(solution)/shard_map/convert.3
  1.3 0.1 copy.43
  2.3 0.5 collective-permute-start
  2.7 0.8 %pad_maximum_fusion.1 = f32[17,512]{1,0:T(8,128)S(1)} fusion(f32[1,512]{1,0:T(1,128)S(1)} %bitcast.64, f32[16,512]{1,0:T(8,128)} %param.11), kind=kLoop, calls=%fused_computation.20 | loop fusion | flops 8704 | bytes 69632 | tf_op jit(solution)/shard_map/concatenate | solution.py:241
  3.6 0.1 stack.50
  3.8 0.1 stack.61
  3.9 0.5 convert_element_type.35.flag_ref
  4.5 0.6 copy-done.12
  5.1 0.1 fusion.24
  5.4 3.1 %collective-permute-start.1 = (bf16[216,512]{1,0:T(8,128)(2,1)S(1)}, bf16[216,512]{1,0:T(8,128)(2,1)S(1)}, u32[]{:S(2)}, u32[]{:S(2)}) collective-permute-start(bf16[216,512]{1,0:T(8,128)(2,1)S(1)} %fusion.6.refs_0_), channel_id=1, source_target_pairs={{0,4},{1,5},{2,6},{3,7},{4,0},{5,1},{6,2},{7,3},{8,12},{9,13},{10,... | collective-permute-start | bytes 663560 | tf_op jit(solution)/shard_map/ppermute | solution.py:152
  8.5 0.7 collective-permute-start.2
  9.2 1.6 %collective-permute-start.3 = (bf16[216,512]{1,0:T(8,128)(2,1)S(1)}, bf16[216,512]{1,0:T(8,128)(2,1)S(1)}, u32[]{:S(2)}, u32[]{:S(2)}) collective-permute-start(bf16[216,512]{1,0:T(8,128)(2,1)S(1)} %fusion.6.refs_0_), channel_id=1, source_target_pairs={{0,2},{1,3},{2,0},{3,1},{4,6},{5,7},{6,4},{7,5},{8,10},{9,11},{10,... | collective-permute-start | bytes 663560 | tf_op jit(solution)/shard_map/ppermute | solution.py:154
  10.9 0.6 copy-done.9
  11.5 2.6 %collective-permute-done.1.refs_1_ = bf16[216,512]{1,0:T(8,128)(2,1)S(1)} collective-permute-done((bf16[216,512]{1,0:T(8,128)(2,1)S(1)}, bf16[216,512]{1,0:T(8,128)(2,1)S(1)}, u32[]{:S(2)}, u32[]{:S(2)}) %collective-permute-start.1) | collective-permute-done | bytes 221216 | tf_op jit(solution)/shard_map/ppermute | solution.py:152
  14.1 0.7 %collective-permute-start.4 = (bf16[216,512]{1,0:T(8,128)(2,1)S(1)}, bf16[216,512]{1,0:T(8,128)(2,1)S(1)}, u32[]{:S(2)}, u32[]{:S(2)}) collective-permute-start(bf16[216,512]{1,0:T(8,128)(2,1)S(1)} %collective-permute-done.1.refs_1_), channel_id=1, source_target_pairs={{4,8},{5,9},{6,10},{7,11},{8,4},{9,5},{10,6},{11,7},{20,24},{21,25... | collective-permute-start | bytes 663560 | tf_op jit(solution)/shard_map/ppermute | solution.py:156
  14.8 1.7 %collective-permute-start.6 = (bf16[216,512]{1,0:T(8,128)(2,1)S(1)}, bf16[216,512]{1,0:T(8,128)(2,1)S(1)}, u32[]{:S(2)}, u32[]{:S(2)}) collective-permute-start(bf16[216,512]{1,0:T(8,128)(2,1)S(1)} %collective-permute-done.1.refs_1_), channel_id=1, source_target_pairs={{0,2},{1,3},{2,0},{3,1},{4,6},{5,7},{6,4},{7,5},{8,10},{9,11},{10,... | collective-permute-start | bytes 663560 | tf_op jit(solution)/shard_map/ppermute | solution.py:158
  16.7 1.3 %collective-permute-start.5 = (bf16[216,512]{1,0:T(8,128)(2,1)S(1)}, bf16[216,512]{1,0:T(8,128)(2,1)S(1)}, u32[]{:S(2)}, u32[]{:S(2)}) collective-permute-start(bf16[216,512]{1,0:T(8,128)(2,1)S(1)} %collective-permute-done.2.refs_2_), channel_id=1, source_target_pairs={{4,0},{5,1},{6,2},{7,3},{8,12},{9,13},{10,14},{11,15},{20,16},{21,... | collective-permute-start | bytes 663560 | tf_op jit(solution)/shard_map/ppermute | solution.py:157
  18.0 1.0 %copy.45.xo_ref = bf16[1024,192]{1,0:T(8,128)(2,1)} copy(bf16[1024,192]{0,1:T(8,128)(2,1)S(1)} %multiply_bitcast_fusion) | data formatting | bytes 786432 | tf_op jit(solution)/shard_map/transpose | solution.py:250
  19.1 1.0 %copy.46.no_ref = f32[1024,1]{1,0:T(8,128)} copy(f32[1024,1]{0,1:T(1,128)S(1)} %bitcast.65) | data formatting | bytes 8192 | tf_op jit(solution)/shard_map/broadcast_in_dim | solution.py:247
  20.1 0.2 copy.44
  20.3 0.9 %broadcast_divide_fusion.ro_ref = f32[1024,1]{1,0:T(8,128)} fusion(f32[1024,1]{1,0:T(8,128)S(1)} %copy.44), kind=kLoop, calls=%fused_computation.9 | loop fusion | flops 1024 | bytes 8192 | tf_op jit(solution)/shard_map/div | solution.py:249
  21.3 8.2 %collective-permute-done.5.refs_5_ = bf16[216,512]{1,0:T(8,128)(2,1)S(1)} collective-permute-done((bf16[216,512]{1,0:T(8,128)(2,1)S(1)}, bf16[216,512]{1,0:T(8,128)(2,1)S(1)}, u32[]{:S(2)}, u32[]{:S(2)}) %collective-permute-start.5) | collective-permute-done | bytes 221216 | tf_op jit(solution)/shard_map/ppermute | solution.py:157
  29.5 0.6 collective-permute-start.8
  30.1 1.3 %collective-permute-start.7 = (bf16[216,512]{1,0:T(8,128)(2,1)S(1)}, bf16[216,512]{1,0:T(8,128)(2,1)S(1)}, u32[]{:S(2)}, u32[]{:S(2)}) collective-permute-start(bf16[216,512]{1,0:T(8,128)(2,1)S(1)} %collective-permute-done.4.refs_4_), channel_id=1, source_target_pairs={{4,0},{5,1},{6,2},{7,3},{8,12},{9,13},{10,14},{11,15},{20,16},{21,... | collective-permute-start | bytes 663560 | tf_op jit(solution)/shard_map/ppermute | solution.py:159
  31.5 0.7 %copy-done.18 = bf16[216,512]{1,0:T(8,128)(2,1)} copy-done((bf16[216,512]{1,0:T(8,128)(2,1)}, bf16[216,512]{1,0:T(8,128)(2,1)S(1)}, u32[]{:S(2)}) %copy-start.18) | copy-done | bytes 221208
  32.1 6.5 %shard_map.95 = f32[7,16,1024]{2,1,0:T(8,128)} custom-call(s32[7]{0:T(128)} %convert_element_type.35.flag_ref, bf16[1024,192]{1,0:T(8,128)(2,1)} %copy.45.xo_ref, f32[1024,1]{1,0:T(8,128)} %copy.46.no_ref, f32[1024,1]{1,0:T(8,128)} %broadcast_divide_fusion.ro_ref, bf16[216,512]{1,0:T(8,128)(2,1)} %copy-done.8, bf16[216,512]{1,0:T(8,128)(2,1)} %copy-done.14, ...), custom_call_target="tpu_custom_call" | custom-call | flops 1526726656 | bytes 2007040 | tf_op jit(solution)/shard_map/pallas_call | solution.py:97
  38.6 0.7 %slice_bitcast_fusion.4 = bf16[1,18]{1,0:T(2,128)(2,1)S(1)} fusion(bf16[1,216,512]{2,1,0:T(8,128)(2,1)} %bitcast.72), kind=kLoop, calls=%fused_computation.50 | loop fusion | bytes 72 | tf_op jit(solution)/shard_map/squeeze | solution.py:261
  39.4 1.6 %collective-permute-start.10 = (bf16[216,512]{1,0:T(8,128)(2,1)S(1)}, bf16[216,512]{1,0:T(8,128)(2,1)S(1)}, u32[]{:S(2)}, u32[]{:S(2)}) collective-permute-start(bf16[216,512]{1,0:T(8,128)(2,1)S(1)} %broadcast_select_fusion), channel_id=1, source_target_pairs={{0,2},{1,3},{2,0},{3,1},{4,6},{5,7},{6,4},{7,5},{8,10},{9,11},{10,... | collective-permute-start | bytes 663560 | tf_op jit(solution)/shard_map/ppermute | solution.py:168
  41.0 4.4 %collective-permute-done.10.refs_2_ = bf16[216,512]{1,0:T(8,128)(2,1)S(1)} collective-permute-done((bf16[216,512]{1,0:T(8,128)(2,1)S(1)}, bf16[216,512]{1,0:T(8,128)(2,1)S(1)}, u32[]{:S(2)}, u32[]{:S(2)}) %collective-permute-start.10) | collective-permute-done | bytes 221216 | tf_op jit(solution)/shard_map/ppermute | solution.py:168
  45.6 0.2 slice_reduce_fusion
  45.8 0.1 copy.48
  46.3 0.1 lt.26
  46.4 0.2 and_reduce_fusion
  46.6 0.6 slice.82.flag_ref
  47.3 3.7 %shard_map.96 = f32[16,1024]{1,0:T(8,128)} custom-call(s32[3]{0:T(128)} %slice.82.flag_ref, bf16[1024,192]{1,0:T(8,128)(2,1)} %copy.45.xo_ref, f32[1024,1]{1,0:T(8,128)} %copy.46.no_ref, f32[1024,1]{1,0:T(8,128)} %broadcast_divide_fusion.ro_ref, bf16[216,512]{1,0:T(8,128)(2,1)} %copy-done.5, bf16[216,512]{1,0:T(8,128)(2,1)} %copy-done.15, ...), custom_call_target="tpu_custom_call" | custom-call | flops 654311424 | bytes 729088 | tf_op jit(solution)/shard_map/pallas_call | solution.py:97
  51.1 0.9 %add.67 = f32[16,1024]{1,0:T(8,128)S(1)} add(f32[16,1024]{1,0:T(8,128)} %shard_map.96, f32[16,1024]{1,0:T(8,128)S(1)} %select_reduce_fusion) | non-fusion elementwise | flops 16384 | bytes 196608 | tf_op jit(solution)/shard_map/add | solution.py:283
  51.9 0.2 fusion.7
  52.1 0.8 %collective-permute-start.14 = (f32[16,16]{1,0:T(8,128)S(1)}, f32[16,16]{1,0:T(8,128)S(1)}, u32[]{:S(2)}, u32[]{:S(2)}) collective-permute-start(f32[16,16]{1,0:T(8,128)S(1)} %fusion.7), channel_id=1, source_target_pairs={{0,2},{1,3},{2,0},{3,1},{4,6},{5,7},{6,4},{7,5},{8,10},{9,11},{10,... | collective-permute-start | bytes 3080 | tf_op jit(solution)/shard_map/ppermute | solution.py:199
  52.9 1.1 %collective-permute-start.15 = (f32[16,16]{1,0:T(8,128)S(1)}, f32[16,16]{1,0:T(8,128)S(1)}, u32[]{:S(2)}, u32[]{:S(2)}) collective-permute-start(f32[16,16]{1,0:T(8,128)S(1)} %fusion.7), channel_id=1, source_target_pairs={{0,1},{1,0},{2,3},{3,2},{4,5},{5,4},{6,7},{7,6},{8,9},{9,8},{10,11... | collective-permute-start | bytes 3080 | tf_op jit(solution)/shard_map/ppermute | solution.py:199
  54.0 1.2 %collective-permute-done.13 = f32[16,16]{1,0:T(8,128)S(1)} collective-permute-done((f32[16,16]{1,0:T(8,128)S(1)}, f32[16,16]{1,0:T(8,128)S(1)}, u32[]{:S(2)}, u32[]{:S(2)}) %collective-permute-start.13) | collective-permute-done | bytes 1056 | tf_op jit(solution)/shard_map/ppermute | solution.py:199
  55.2 0.6 collective-permute-done.14
  55.9 1.1 %collective-permute-start.16 = (f32[16,16]{1,0:T(8,128)S(1)}, f32[16,16]{1,0:T(8,128)S(1)}, u32[]{:S(2)}, u32[]{:S(2)}) collective-permute-start(f32[16,16]{1,0:T(8,128)S(1)} %select_add_fusion), channel_id=1, source_target_pairs={{0,12},{1,13},{2,14},{3,15},{4,8},{5,9},{6,10},{7,11},{8,4},{9,5},... | collective-permute-start | bytes 3080 | tf_op jit(solution)/shard_map/ppermute | solution.py:199
  57.0 4.9 %collective-permute-start.17 = (f32[16,16]{1,0:T(8,128)S(1)}, f32[16,16]{1,0:T(8,128)S(1)}, u32[]{:S(2)}, u32[]{:S(2)}) collective-permute-start(f32[16,16]{1,0:T(8,128)S(1)} %select_add_fusion), channel_id=1, source_target_pairs={{0,8},{1,9},{2,10},{3,11},{4,12},{5,13},{6,14},{7,15},{8,0},{9,1},... | collective-permute-start | bytes 3080 | tf_op jit(solution)/shard_map/ppermute | solution.py:199
  61.8 1.7 %collective-permute-done.17 = f32[16,16]{1,0:T(8,128)S(1)} collective-permute-done((f32[16,16]{1,0:T(8,128)S(1)}, f32[16,16]{1,0:T(8,128)S(1)}, u32[]{:S(2)}, u32[]{:S(2)}) %collective-permute-start.17) | collective-permute-done | bytes 1056 | tf_op jit(solution)/shard_map/ppermute | solution.py:199
  63.5 1.9 %collective-permute-done.18 = f32[16,16]{1,0:T(8,128)S(1)} collective-permute-done((f32[16,16]{1,0:T(8,128)S(1)}, f32[16,16]{1,0:T(8,128)S(1)}, u32[]{:S(2)}, u32[]{:S(2)}) %collective-permute-start.18) | collective-permute-done | bytes 1056 | tf_op jit(solution)/shard_map/ppermute | solution.py:199
  65.5 0.2 fusion.23
  65.7 0.4 copy-done.10
  66.1 0.6 fusion.14
  (100 shorter events, 1.8 us)
Async XLA Ops:
  0.6 3.9 %copy-start = (f32[16,512]{1,0:T(8,128)S(1)}, f32[16,512]{1,0:T(8,128)}, u32[]{:S(2)}) copy-start(f32[16,512]{1,0:T(8,128)} %param.12) | copy-start | bytes 98308
  1.4 1.3 %copy-start.11 = (f32[512]{0:T(512)S(1)}, f32[512]{0:T(512)}, u32[]{:S(2)}) copy-start(f32[512]{0:T(512)} %param.10) | copy-start | bytes 6148
  1.5 2.0 %copy-start.2 = (f32[16,512]{1,0:T(8,128)S(1)}, f32[16,512]{1,0:T(8,128)}, u32[]{:S(2)}) copy-start(f32[16,512]{1,0:T(8,128)} %param.11) | copy-start | bytes 98308
  1.5 2.1 %copy-start.13 = (bf16[512]{0:T(512)(128)(2,1)S(1)}, bf16[512]{0:T(512)(128)(2,1)}, u32[]{:S(2)}) copy-start(bf16[512]{0:T(512)(128)(2,1)} %param.9) | copy-start | bytes 3076
  2.2 3.2 %copy-start.1 = (bf16[192,512]{1,0:T(8,128)(2,1)S(1)}, bf16[192,512]{1,0:T(8,128)(2,1)}, u32[]{:S(2)}) copy-start(bf16[192,512]{1,0:T(8,128)(2,1)} %param.8) | copy-start | bytes 589828
  2.3 3.0 %collective-permute-start = (bf16[9]{0:T(256)(128)(2,1)S(1)}, bf16[9]{0:T(256)(128)(2,1)S(1)}, u32[]{:S(2)}, u32[]{:S(2)}) collective-permute-start(bf16[9]{0:T(256)(128)(2,1)S(1)} %pad_maximum_fusion.2), channel_id=1, source_target_pairs={{0,1},{1,0},{2,3},{3,2},{4,5},{5,4},{6,7},{7,6},{8,9},{9,8},{10,11... | collective-permute-start | bytes 62 | tf_op jit(solution)/shard_map/ppermute | solution.py:231
  3.5 7.3 %collective-permute-start.12 = (f32[17,512]{1,0:T(8,128)S(1)}, f32[17,512]{1,0:T(8,128)S(1)}, u32[]{:S(2)}, u32[]{:S(2)}) collective-permute-start(f32[17,512]{1,0:T(8,128)S(1)} %pad_maximum_fusion.1), channel_id=1, source_target_pairs={{0,1},{1,0},{2,3},{3,2},{4,5},{5,4},{6,7},{7,6},{8,9},{9,8},{10,11... | collective-permute-start | bytes 104456 | tf_op jit(solution)/shard_map/ppermute | solution.py:240
  4.4 0.7 %copy-start.12 = (f32[16,16]{1,0:T(8,128)S(1)}, f32[16,16]{1,0:T(8,128)}, u32[]{:S(2)}) copy-start(f32[16,16]{1,0:T(8,128)} %param.13) | copy-start | bytes 3076
  5.4 5.5 %copy-start.8 = (bf16[216,512]{1,0:T(8,128)(2,1)}, bf16[216,512]{1,0:T(8,128)(2,1)S(1)}, u32[]{:S(2)}) copy-start(bf16[216,512]{1,0:T(8,128)(2,1)S(1)} %fusion.6.refs_0_) | copy-start | bytes 663556
  5.4 8.7 %collective-permute-start.1 = (bf16[216,512]{1,0:T(8,128)(2,1)S(1)}, bf16[216,512]{1,0:T(8,128)(2,1)S(1)}, u32[]{:S(2)}, u32[]{:S(2)}) collective-permute-start(bf16[216,512]{1,0:T(8,128)(2,1)S(1)} %fusion.6.refs_0_), channel_id=1, source_target_pairs={{0,4},{1,5},{2,6},{3,7},{4,0},{5,1},{6,2},{7,3},{8,12},{9,13},{10,... | collective-permute-start | bytes 663560 | tf_op jit(solution)/shard_map/ppermute | solution.py:152
  8.5 5.6 %collective-permute-start.2 = (bf16[216,512]{1,0:T(8,128)(2,1)S(1)}, bf16[216,512]{1,0:T(8,128)(2,1)S(1)}, u32[]{:S(2)}, u32[]{:S(2)}) collective-permute-start(bf16[216,512]{1,0:T(8,128)(2,1)S(1)} %fusion.6.refs_0_), channel_id=1, source_target_pairs={{4,8},{5,9},{6,10},{7,11},{8,4},{9,5},{10,6},{11,7},{20,24},{21,25... | collective-permute-start | bytes 663560 | tf_op jit(solution)/shard_map/ppermute | solution.py:153
  9.1 7.4 %collective-permute-start.9 = (bf16[216,512]{1,0:T(8,128)(2,1)S(1)}, bf16[216,512]{1,0:T(8,128)(2,1)S(1)}, u32[]{:S(2)}, u32[]{:S(2)}) collective-permute-start(bf16[216,512]{1,0:T(8,128)(2,1)S(1)} %fusion.6.refs_0_), channel_id=1, source_target_pairs={{0,1},{1,0},{2,3},{3,2},{4,5},{5,4},{6,7},{7,6},{8,9},{9,8},{10,11... | collective-permute-start | bytes 663560 | tf_op jit(solution)/shard_map/ppermute | solution.py:239
  9.2 12.0 %collective-permute-start.3 = (bf16[216,512]{1,0:T(8,128)(2,1)S(1)}, bf16[216,512]{1,0:T(8,128)(2,1)S(1)}, u32[]{:S(2)}, u32[]{:S(2)}) collective-permute-start(bf16[216,512]{1,0:T(8,128)(2,1)S(1)} %fusion.6.refs_0_), channel_id=1, source_target_pairs={{0,2},{1,3},{2,0},{3,1},{4,6},{5,7},{6,4},{7,5},{8,10},{9,11},{10,... | collective-permute-start | bytes 663560 | tf_op jit(solution)/shard_map/ppermute | solution.py:154
  10.9 0.6 copy-start.9
  14.1 7.2 %copy-start.14 = (bf16[216,512]{1,0:T(8,128)(2,1)}, bf16[216,512]{1,0:T(8,128)(2,1)S(1)}, u32[]{:S(2)}) copy-start(bf16[216,512]{1,0:T(8,128)(2,1)S(1)} %collective-permute-done.1.refs_1_) | copy-start | bytes 663556
  14.1 15.4 %copy-start.4 = (bf16[216,512]{1,0:T(8,128)(2,1)}, bf16[216,512]{1,0:T(8,128)(2,1)S(1)}, u32[]{:S(2)}) copy-start(bf16[216,512]{1,0:T(8,128)(2,1)S(1)} %collective-permute-done.2.refs_2_) | copy-start | bytes 663556
  14.1 16.0 %collective-permute-start.4 = (bf16[216,512]{1,0:T(8,128)(2,1)S(1)}, bf16[216,512]{1,0:T(8,128)(2,1)S(1)}, u32[]{:S(2)}, u32[]{:S(2)}) collective-permute-start(bf16[216,512]{1,0:T(8,128)(2,1)S(1)} %collective-permute-done.1.refs_1_), channel_id=1, source_target_pairs={{4,8},{5,9},{6,10},{7,11},{8,4},{9,5},{10,6},{11,7},{20,24},{21,25... | collective-permute-start | bytes 663560 | tf_op jit(solution)/shard_map/ppermute | solution.py:156
  14.8 16.6 %collective-permute-start.6 = (bf16[216,512]{1,0:T(8,128)(2,1)S(1)}, bf16[216,512]{1,0:T(8,128)(2,1)S(1)}, u32[]{:S(2)}, u32[]{:S(2)}) collective-permute-start(bf16[216,512]{1,0:T(8,128)(2,1)S(1)} %collective-permute-done.1.refs_1_), channel_id=1, source_target_pairs={{0,2},{1,3},{2,0},{3,1},{4,6},{5,7},{6,4},{7,5},{8,10},{9,11},{10,... | collective-permute-start | bytes 663560 | tf_op jit(solution)/shard_map/ppermute | solution.py:158
  16.7 12.7 %collective-permute-start.5 = (bf16[216,512]{1,0:T(8,128)(2,1)S(1)}, bf16[216,512]{1,0:T(8,128)(2,1)S(1)}, u32[]{:S(2)}, u32[]{:S(2)}) collective-permute-start(bf16[216,512]{1,0:T(8,128)(2,1)S(1)} %collective-permute-done.2.refs_2_), channel_id=1, source_target_pairs={{4,0},{5,1},{6,2},{7,3},{8,12},{9,13},{10,14},{11,15},{20,16},{21,... | collective-permute-start | bytes 663560 | tf_op jit(solution)/shard_map/ppermute | solution.py:157
  21.3 8.2 %copy-start.16 = (bf16[216,512]{1,0:T(8,128)(2,1)}, bf16[216,512]{1,0:T(8,128)(2,1)S(1)}, u32[]{:S(2)}) copy-start(bf16[216,512]{1,0:T(8,128)(2,1)S(1)} %collective-permute-done.3.refs_3_) | copy-start | bytes 663556
  29.5 1.9 %copy-start.7 = (bf16[216,512]{1,0:T(8,128)(2,1)}, bf16[216,512]{1,0:T(8,128)(2,1)S(1)}, u32[]{:S(2)}) copy-start(bf16[216,512]{1,0:T(8,128)(2,1)S(1)} %collective-permute-done.5.refs_5_) | copy-start | bytes 663556
  29.5 11.5 %collective-permute-start.8 = (bf16[216,512]{1,0:T(8,128)(2,1)S(1)}, bf16[216,512]{1,0:T(8,128)(2,1)S(1)}, u32[]{:S(2)}, u32[]{:S(2)}) collective-permute-start(bf16[216,512]{1,0:T(8,128)(2,1)S(1)} %broadcast_select_fusion.1), channel_id=1, source_target_pairs={{0,2},{1,3},{2,0},{3,1},{4,6},{5,7},{6,4},{7,5},{8,10},{9,11},{10,... | collective-permute-start | bytes 663560 | tf_op jit(solution)/shard_map/ppermute | solution.py:160
  30.1 1.3 %copy-start.6 = (bf16[216,512]{1,0:T(8,128)(2,1)}, bf16[216,512]{1,0:T(8,128)(2,1)S(1)}, u32[]{:S(2)}) copy-start(bf16[216,512]{1,0:T(8,128)(2,1)S(1)} %collective-permute-done.4.refs_4_) | copy-start | bytes 663556
  30.1 9.3 %collective-permute-start.7 = (bf16[216,512]{1,0:T(8,128)(2,1)S(1)}, bf16[216,512]{1,0:T(8,128)(2,1)S(1)}, u32[]{:S(2)}, u32[]{:S(2)}) collective-permute-start(bf16[216,512]{1,0:T(8,128)(2,1)S(1)} %collective-permute-done.4.refs_4_), channel_id=1, source_target_pairs={{4,0},{5,1},{6,2},{7,3},{8,12},{9,13},{10,14},{11,15},{20,16},{21,... | collective-permute-start | bytes 663560 | tf_op jit(solution)/shard_map/ppermute | solution.py:159
  31.4 0.7 %copy-start.18 = (bf16[216,512]{1,0:T(8,128)(2,1)}, bf16[216,512]{1,0:T(8,128)(2,1)S(1)}, u32[]{:S(2)}) copy-start(bf16[216,512]{1,0:T(8,128)(2,1)S(1)} %collective-permute-done.6.refs_6_) | copy-start | bytes 663556
  38.6 8.6 %copy-start.3 = (f32[7,16,1024]{2,1,0:T(8,128)S(1)}, f32[7,16,1024]{2,1,0:T(8,128)}, u32[]{:S(2)}) copy-start(f32[7,16,1024]{2,1,0:T(8,128)} %shard_map.95) | copy-start | bytes 1376260
  39.4 1.6 %copy-start.5 = (bf16[216,512]{1,0:T(8,128)(2,1)}, bf16[216,512]{1,0:T(8,128)(2,1)S(1)}, u32[]{:S(2)}) copy-start(bf16[216,512]{1,0:T(8,128)(2,1)S(1)} %collective-permute-done.7.refs_0_) | copy-start | bytes 663556
  39.4 6.0 %collective-permute-start.10 = (bf16[216,512]{1,0:T(8,128)(2,1)S(1)}, bf16[216,512]{1,0:T(8,128)(2,1)S(1)}, u32[]{:S(2)}, u32[]{:S(2)}) collective-permute-start(bf16[216,512]{1,0:T(8,128)(2,1)S(1)} %broadcast_select_fusion), channel_id=1, source_target_pairs={{0,2},{1,3},{2,0},{3,1},{4,6},{5,7},{6,4},{7,5},{8,10},{9,11},{10,... | collective-permute-start | bytes 663560 | tf_op jit(solution)/shard_map/ppermute | solution.py:168
  41.0 6.3 %copy-start.15 = (bf16[216,512]{1,0:T(8,128)(2,1)}, bf16[216,512]{1,0:T(8,128)(2,1)S(1)}, u32[]{:S(2)}) copy-start(bf16[216,512]{1,0:T(8,128)(2,1)S(1)} %collective-permute-done.8.refs_1_) | copy-start | bytes 663556
  45.4 1.9 %copy-start.17 = (bf16[216,512]{1,0:T(8,128)(2,1)}, bf16[216,512]{1,0:T(8,128)(2,1)S(1)}, u32[]{:S(2)}) copy-start(bf16[216,512]{1,0:T(8,128)(2,1)S(1)} %collective-permute-done.10.refs_2_) | copy-start | bytes 663556
  51.1 0.9 %slice-start = ((f32[17,512]{1,0:T(8,128)}), f32[16,512]{1,0:T(8,128)S(1)}, s32[]{:S(2)}) async-start(f32[17,512]{1,0:T(8,128)} %copy-done.9), calls=%async_computation | async-start | bytes 65536 | tf_op jit(solution)/shard_map/slice | solution.py:287
  52.1 3.1 %collective-permute-start.13 = (f32[16,16]{1,0:T(8,128)S(1)}, f32[16,16]{1,0:T(8,128)S(1)}, u32[]{:S(2)}, u32[]{:S(2)}) collective-permute-start(f32[16,16]{1,0:T(8,128)S(1)} %fusion.7), channel_id=1, source_target_pairs={{0,3},{1,2},{2,1},{3,0},{4,7},{5,6},{6,5},{7,4},{8,11},{9,10},{10,... | collective-permute-start | bytes 3080 | tf_op jit(solution)/shard_map/ppermute | solution.py:199
  52.1 3.7 %collective-permute-start.14 = (f32[16,16]{1,0:T(8,128)S(1)}, f32[16,16]{1,0:T(8,128)S(1)}, u32[]{:S(2)}, u32[]{:S(2)}) collective-permute-start(f32[16,16]{1,0:T(8,128)S(1)} %fusion.7), channel_id=1, source_target_pairs={{0,2},{1,3},{2,0},{3,1},{4,6},{5,7},{6,4},{7,5},{8,10},{9,11},{10,... | collective-permute-start | bytes 3080 | tf_op jit(solution)/shard_map/ppermute | solution.py:199
  52.9 2.9 %collective-permute-start.15 = (f32[16,16]{1,0:T(8,128)S(1)}, f32[16,16]{1,0:T(8,128)S(1)}, u32[]{:S(2)}, u32[]{:S(2)}) collective-permute-start(f32[16,16]{1,0:T(8,128)S(1)} %fusion.7), channel_id=1, source_target_pairs={{0,1},{1,0},{2,3},{3,2},{4,5},{5,4},{6,7},{7,6},{8,9},{9,8},{10,11... | collective-permute-start | bytes 3080 | tf_op jit(solution)/shard_map/ppermute | solution.py:199
  55.9 6.0 %collective-permute-start.16 = (f32[16,16]{1,0:T(8,128)S(1)}, f32[16,16]{1,0:T(8,128)S(1)}, u32[]{:S(2)}, u32[]{:S(2)}) collective-permute-start(f32[16,16]{1,0:T(8,128)S(1)} %select_add_fusion), channel_id=1, source_target_pairs={{0,12},{1,13},{2,14},{3,15},{4,8},{5,9},{6,10},{7,11},{8,4},{9,5},... | collective-permute-start | bytes 3080 | tf_op jit(solution)/shard_map/ppermute | solution.py:199
  57.0 6.6 %collective-permute-start.17 = (f32[16,16]{1,0:T(8,128)S(1)}, f32[16,16]{1,0:T(8,128)S(1)}, u32[]{:S(2)}, u32[]{:S(2)}) collective-permute-start(f32[16,16]{1,0:T(8,128)S(1)} %select_add_fusion), channel_id=1, source_target_pairs={{0,8},{1,9},{2,10},{3,11},{4,12},{5,13},{6,14},{7,15},{8,0},{9,1},... | collective-permute-start | bytes 3080 | tf_op jit(solution)/shard_map/ppermute | solution.py:199
  61.8 3.7 %collective-permute-start.18 = (f32[16,16]{1,0:T(8,128)S(1)}, f32[16,16]{1,0:T(8,128)S(1)}, u32[]{:S(2)}, u32[]{:S(2)}) collective-permute-start(f32[16,16]{1,0:T(8,128)S(1)} %select_add_fusion), channel_id=1, source_target_pairs={{0,4},{1,5},{2,6},{3,7},{4,0},{5,1},{6,2},{7,3},{8,12},{9,13},{10,... | collective-permute-start | bytes 3080 | tf_op jit(solution)/shard_map/ppermute | solution.py:199
  61.8 4.3 %collective-permute-start.11 = (f32[16,512]{1,0:T(8,128)S(1)}, f32[16,512]{1,0:T(8,128)S(1)}, u32[]{:S(2)}, u32[]{:S(2)}) collective-permute-start(f32[16,512]{1,0:T(8,128)S(1)} %slice.105), channel_id=1, source_target_pairs={{0,1},{1,0},{2,3},{3,2},{4,5},{5,4},{6,7},{7,6},{8,9},{9,8},{10,11... | collective-permute-start | bytes 98312 | tf_op jit(solution)/shard_map/ppermute | solution.py:293
  65.5 0.6 copy-start.10

commit v19 on v18

--- a/solution.py
+++ b/solution.py
@@ -15,13 +15,13 @@
 HIGHEST = lax.Precision.HIGHEST
 
 
-def piece_terms(width, x_cols, w_cols, xo_ref, no_ref, ro_ref):
+def piece_terms(width, x_cols, w_cols, xo_ref, norm_rows, recip_rows):
     x_wide = x_cols.astype(jnp.float32)
     norm_cols = jnp.sum(x_wide * x_wide, axis=0, keepdims=True)
     recip_cols = 1.0 / w_cols[LANCZOS : LANCZOS + 1, :].astype(jnp.float32)
     twice_inner = jnp.dot(xo_ref[...], x_cols, preferred_element_type=jnp.float32)
-    distance = (no_ref[...] + norm_cols) - twice_inner
-    weights = jnp.exp2(distance * (ro_ref[...] * recip_cols)).astype(jnp.bfloat16)
+    distance = (norm_rows + norm_cols) - twice_inner
+    weights = jnp.exp2(distance * (recip_rows * recip_cols)).astype(jnp.bfloat16)
     return lax.dot_general(
         w_cols[:LANCZOS, :], weights, (((1,), (1,)), ((), ())),
         preferred_element_type=jnp.float32,
@@ -41,12 +41,14 @@
         def _():
             out_ref[...] += piece_terms(
                 width, x_ref[k, :width, :], w_ref[k],
-                xo_ref, no_ref, ro_ref,
+                xo_ref, no_ref[...], ro_ref[...],
             )
 
 
-def list_kernel(width, rows, counts, split, flag_ref, xo_ref, no_ref, ro_ref, *refs):
+def list_kernel(width, rows, counts, split, flag_ref, xo_ref, terms_ref, *refs):
     out_ref = refs[-1]
+    row_terms = jnp.transpose(terms_ref[...])
+    norm_rows, recip_rows = row_terms[:, 0:1], row_terms[:, 1:2]
     if not split:
         out_ref[...] = jnp.zeros_like(out_ref)
     slot = 0
@@ -59,7 +61,7 @@
                     width,
                     ref[base : base + width, :],
                     ref[base + width : base + width + LANCZOS + 1, :],
-                    xo_ref, no_ref, ro_ref,
+                    xo_ref, norm_rows, recip_rows,
                 )
 
             if split:
@@ -87,6 +89,9 @@
     counts = [p.shape[0] // rows for p in pieces]
     shape = (sum(counts), LANCZOS, own) if split else (LANCZOS, own)
     vmem = pl.BlockSpec(memory_space=pltpu.VMEM)
+    row_terms = jnp.concatenate(
+        [norm_own.reshape(1, own), recip_own.reshape(1, own), jnp.zeros((6, own), jnp.float32)]
+    )
     cols = pieces[0].shape[1]
     slots = sum(counts)
     cost = pl.CostEstimate(
@@ -97,10 +102,10 @@
     return pl.pallas_call(
         functools.partial(list_kernel, width, rows, counts, split),
         cost_estimate=cost,
-        in_specs=[pl.BlockSpec(memory_space=pltpu.SMEM)] + [vmem] * (3 + len(pieces)),
+        in_specs=[pl.BlockSpec(memory_space=pltpu.SMEM)] + [vmem] * (2 + len(pieces)),
         out_specs=vmem,
         out_shape=jax.ShapeDtypeStruct(shape, jnp.float32),
-    )(flags, twice_own_t, norm_own, recip_own, *pieces)
+    )(flags, twice_own_t, row_terms, *pieces)
 
 
 def own_rows_product(flags, own_terms, mine, width):

time: 66.9 us -> 67 us (level)
  waiting for transfers between devices: 20.7 us -> 22.2 us
  local copies, waits for them, and re-layouts: 7.38 us -> 6.29 us
  starting transfers between devices: 20.9 us -> 20.2 us
    ppermute x1, waiting for transfers between devices: 8.18 us -> 9.68 us  [gather_pieces(): out2 = lax.ppermute(inner1, 'row', outward)]
    broadcast_in_dim x1 -> x0, local copies, waits for them, and re-layouts: 1.04 us -> none  [shards(): norm_rows = jnp.sum(jnp.square(rows_x.astype(jnp.float32)), axis=0)[:, None]]
    div x1, other arithmetic: 0.9 us -> 0.01 us  [shards(): recip_rows = (-log2e / rows_scale.astype(jnp.float32))[:, None]]
    ppermute x6, starting transfers between devices: 7.86 us -> 7.08 us  [sum_over_rows(): lax.ppermute(value, 'row', [(i, i ^ m << shift) for i in range(devices)])]
    concatenate x0 -> x1, other arithmetic: none -> 0.68 us  [list_product(): jnp.concatenate([norm_own.reshape(1, own), recip_own.reshape(1, own), jnp...]
  transfers between devices with their start and end apart: 19 -> 19, of which waited for: 7 -> 8; matrix products, arithmetic and copies ran while one was open for 10% -> 7% of each run, Pallas kernels for 10% -> 9%
where the time goes in v19:
time: 67 us; the launch traced here: 66.5 us
  waiting for transfers between devices  22.2 us (33%)
  starting transfers between devices  20.2 us (30%)
  Pallas kernels  10.6 us (16%)
  local copies, waits for them, and re-layouts  6.29 us (9%)
  other arithmetic  5.04 us (8%)
  between operations  1.73 us (3%)
    pallas_call x2, Pallas kernels, list_product(): pl.pallas_call(functools.partial(list_kernel, width, rows, counts, split)...  10.6 us
    ppermute x1, waiting for transfers between devices, gather_pieces(): out2 = lax.ppermute(inner1, 'row', outward)  9.68 us
    ppermute x6, starting transfers between devices, sum_over_rows(): lax.ppermute(value, 'row', [(i, i ^ m << shift) for i in range(devices)])  7.08 us
    ppermute x6, waiting for transfers between devices, sum_over_rows(): lax.ppermute(value, 'row', [(i, i ^ m << shift) for i in range(devices)])  5.47 us
    ppermute x1, waiting for transfers between devices, gather_pieces(): across4 = lax.ppermute(last, 'row', across)  4.38 us
    ppermute x1, starting transfers between devices, gather_pieces(): swap1 = lax.ppermute(packed, 'row', pairs_swap)  3.09 us
    ppermute x1, waiting for transfers between devices, gather_pieces(): swap1 = lax.ppermute(packed, 'row', pairs_swap)  2.61 us
    unnamed x38, local copies, waits for them, and re-layouts  2.38 us
  transfers between devices with their start and end apart: 19, of which 8 were waited for; matrix products, arithmetic and copies ran while one was open for 7% of the time, Pallas kernels for 9%

profile of v19, /device:TPU:0, one launch (start us, length us, event | category | flops | bytes accessed | tf_op | source)
XLA Modules:
  0.0 66.5 jit_solution(5872044533579134803)
XLA Ops:
  0.6 0.7 %convert.8 = bf16[4,2]{0,1:T(2,128)(2,1)S(1)} convert(s32[4,2]{0,1:T(2,128)} %param.14) | non-fusion elementwise | flops 8 | bytes 48 | tf_op jit(solution)/shard_map/convert.3
  1.3 0.1 copy.26
  2.3 0.5 collective-permute-start
  2.8 0.8 %pad_maximum_fusion.1 = f32[17,512]{1,0:T(8,128)S(1)} fusion(f32[1,512]{1,0:T(1,128)S(1)} %bitcast.62, f32[16,512]{1,0:T(8,128)} %param.11), kind=kLoop, calls=%fused_computation.19 | loop fusion | flops 8704 | bytes 69632 | tf_op jit(solution)/shard_map/concatenate | solution.py:246
  3.6 0.1 stack.50
  3.7 0.1 stack.61
  3.9 0.5 convert_element_type.35.flag_ref
  4.4 0.1 copy-done.13
  4.7 0.5 copy-done.12
  5.2 0.1 fusion.25
  5.5 3.1 %collective-permute-start.1 = (bf16[216,512]{1,0:T(8,128)(2,1)S(1)}, bf16[216,512]{1,0:T(8,128)(2,1)S(1)}, u32[]{:S(2)}, u32[]{:S(2)}) collective-permute-start(bf16[216,512]{1,0:T(8,128)(2,1)S(1)} %fusion.6.refs_0_), channel_id=1, source_target_pairs={{0,4},{1,5},{2,6},{3,7},{4,0},{5,1},{6,2},{7,3},{8,12},{9,13},{10,... | collective-permute-start | bytes 663560 | tf_op jit(solution)/shard_map/ppermute | solution.py:157
  8.6 0.7 collective-permute-start.2
  9.4 1.6 %collective-permute-start.3 = (bf16[216,512]{1,0:T(8,128)(2,1)S(1)}, bf16[216,512]{1,0:T(8,128)(2,1)S(1)}, u32[]{:S(2)}, u32[]{:S(2)}) collective-permute-start(bf16[216,512]{1,0:T(8,128)(2,1)S(1)} %fusion.6.refs_0_), channel_id=1, source_target_pairs={{0,2},{1,3},{2,0},{3,1},{4,6},{5,7},{6,4},{7,5},{8,10},{9,11},{10,... | collective-permute-start | bytes 663560 | tf_op jit(solution)/shard_map/ppermute | solution.py:159
  11.0 0.6 copy-done.9
  11.6 2.6 %collective-permute-done.1.refs_1_ = bf16[216,512]{1,0:T(8,128)(2,1)S(1)} collective-permute-done((bf16[216,512]{1,0:T(8,128)(2,1)S(1)}, bf16[216,512]{1,0:T(8,128)(2,1)S(1)}, u32[]{:S(2)}, u32[]{:S(2)}) %collective-permute-start.1) | collective-permute-done | bytes 221216 | tf_op jit(solution)/shard_map/ppermute | solution.py:157
  14.3 0.7 %collective-permute-start.4 = (bf16[216,512]{1,0:T(8,128)(2,1)S(1)}, bf16[216,512]{1,0:T(8,128)(2,1)S(1)}, u32[]{:S(2)}, u32[]{:S(2)}) collective-permute-start(bf16[216,512]{1,0:T(8,128)(2,1)S(1)} %collective-permute-done.1.refs_1_), channel_id=1, source_target_pairs={{4,8},{5,9},{6,10},{7,11},{8,4},{9,5},{10,6},{11,7},{20,24},{21,25... | collective-permute-start | bytes 663560 | tf_op jit(solution)/shard_map/ppermute | solution.py:161
  14.9 1.7 %collective-permute-start.6 = (bf16[216,512]{1,0:T(8,128)(2,1)S(1)}, bf16[216,512]{1,0:T(8,128)(2,1)S(1)}, u32[]{:S(2)}, u32[]{:S(2)}) collective-permute-start(bf16[216,512]{1,0:T(8,128)(2,1)S(1)} %collective-permute-done.1.refs_1_), channel_id=1, source_target_pairs={{0,2},{1,3},{2,0},{3,1},{4,6},{5,7},{6,4},{7,5},{8,10},{9,11},{10,... | collective-permute-start | bytes 663560 | tf_op jit(solution)/shard_map/ppermute | solution.py:163
  16.9 1.3 %collective-permute-start.5 = (bf16[216,512]{1,0:T(8,128)(2,1)S(1)}, bf16[216,512]{1,0:T(8,128)(2,1)S(1)}, u32[]{:S(2)}, u32[]{:S(2)}) collective-permute-start(bf16[216,512]{1,0:T(8,128)(2,1)S(1)} %collective-permute-done.2.refs_2_), channel_id=1, source_target_pairs={{4,0},{5,1},{6,2},{7,3},{8,12},{9,13},{10,14},{11,15},{20,16},{21,... | collective-permute-start | bytes 663560 | tf_op jit(solution)/shard_map/ppermute | solution.py:162
  18.2 1.0 %copy.27.xo_ref = bf16[1024,192]{1,0:T(8,128)(2,1)} copy(bf16[1024,192]{0,1:T(8,128)(2,1)S(1)} %multiply_bitcast_fusion) | data formatting | bytes 786432 | tf_op jit(solution)/shard_map/transpose | solution.py:255
  19.2 0.7 %maximum_maximum_fusion.terms_ref = f32[8,1024]{1,0:T(8,128)} fusion(f32[1,1024]{1,0:T(1,128)S(1)} %fusion.16, f32[1,1024]{1,0:T(1,128)S(1)} %bitcast.63, f32[8]{0:T(128)S(1)} %pad.18.clone), kind=kLoop, calls=%fused_computation.24 | loop fusion | flops 16384 | bytes 40992 | tf_op jit(solution)/shard_map/concatenate | solution.py:92
  20.0 9.7 %collective-permute-done.5.refs_5_ = bf16[216,512]{1,0:T(8,128)(2,1)S(1)} collective-permute-done((bf16[216,512]{1,0:T(8,128)(2,1)S(1)}, bf16[216,512]{1,0:T(8,128)(2,1)S(1)}, u32[]{:S(2)}, u32[]{:S(2)}) %collective-permute-start.5) | collective-permute-done | bytes 221216 | tf_op jit(solution)/shard_map/ppermute | solution.py:162
  29.7 0.6 collective-permute-start.8
  30.3 1.3 %collective-permute-start.7 = (bf16[216,512]{1,0:T(8,128)(2,1)S(1)}, bf16[216,512]{1,0:T(8,128)(2,1)S(1)}, u32[]{:S(2)}, u32[]{:S(2)}) collective-permute-start(bf16[216,512]{1,0:T(8,128)(2,1)S(1)} %collective-permute-done.4.refs_4_), channel_id=1, source_target_pairs={{4,0},{5,1},{6,2},{7,3},{8,12},{9,13},{10,14},{11,15},{20,16},{21,... | collective-permute-start | bytes 663560 | tf_op jit(solution)/shard_map/ppermute | solution.py:164
  31.6 0.7 %copy-done.18 = bf16[216,512]{1,0:T(8,128)(2,1)} copy-done((bf16[216,512]{1,0:T(8,128)(2,1)}, bf16[216,512]{1,0:T(8,128)(2,1)S(1)}, u32[]{:S(2)}) %copy-start.18) | copy-done | bytes 221208
  32.3 6.3 %shard_map.95 = f32[7,16,1024]{2,1,0:T(8,128)} custom-call(s32[7]{0:T(128)} %convert_element_type.35.flag_ref, bf16[1024,192]{1,0:T(8,128)(2,1)} %copy.27.xo_ref, f32[8,1024]{1,0:T(8,128)} %maximum_maximum_fusion.terms_ref, bf16[216,512]{1,0:T(8,128)(2,1)} %copy-done.8, bf16[216,512]{1,0:T(8,128)(2,1)} %copy-done.14, bf16[216,512]{1,0:T(8,128)(2,1)} %copy-done.4, ...), custom_call_target="tpu_custom_call" | custom-call | flops 1526726656 | bytes 2007040 | tf_op jit(solution)/shard_map/pallas_call | solution.py:102
  38.6 0.7 %slice_bitcast_fusion.3 = bf16[1,18]{1,0:T(2,128)(2,1)S(1)} fusion(bf16[1,216,512]{2,1,0:T(8,128)(2,1)} %bitcast.70), kind=kLoop, calls=%fused_computation.50 | loop fusion | bytes 72 | tf_op jit(solution)/shard_map/squeeze | solution.py:266
  39.4 1.6 %collective-permute-start.10 = (bf16[216,512]{1,0:T(8,128)(2,1)S(1)}, bf16[216,512]{1,0:T(8,128)(2,1)S(1)}, u32[]{:S(2)}, u32[]{:S(2)}) collective-permute-start(bf16[216,512]{1,0:T(8,128)(2,1)S(1)} %broadcast_select_fusion), channel_id=1, source_target_pairs={{0,2},{1,3},{2,0},{3,1},{4,6},{5,7},{6,4},{7,5},{8,10},{9,11},{10,... | collective-permute-start | bytes 663560 | tf_op jit(solution)/shard_map/ppermute | solution.py:173
  41.0 4.4 %collective-permute-done.10.refs_2_ = bf16[216,512]{1,0:T(8,128)(2,1)S(1)} collective-permute-done((bf16[216,512]{1,0:T(8,128)(2,1)S(1)}, bf16[216,512]{1,0:T(8,128)(2,1)S(1)}, u32[]{:S(2)}, u32[]{:S(2)}) %collective-permute-start.10) | collective-permute-done | bytes 221216 | tf_op jit(solution)/shard_map/ppermute | solution.py:173
  45.5 0.2 slice_reduce_fusion
  45.8 0.1 copy.29
  46.3 0.1 lt.26
  46.4 0.2 and_reduce_fusion
  46.6 0.6 slice.82.flag_ref
  47.3 4.3 %shard_map.96 = f32[16,1024]{1,0:T(8,128)} custom-call(s32[3]{0:T(128)} %slice.82.flag_ref, bf16[1024,192]{1,0:T(8,128)(2,1)} %copy.27.xo_ref, f32[8,1024]{1,0:T(8,128)} %maximum_maximum_fusion.terms_ref, bf16[216,512]{1,0:T(8,128)(2,1)} %copy-done.5, bf16[216,512]{1,0:T(8,128)(2,1)} %copy-done.15, bf16[216,512]{1,0:T(8,128)(2,1)} %copy-done.17), custom_call_target="tpu_custom_call" | custom-call | flops 654311424 | bytes 729088 | tf_op jit(solution)/shard_map/pallas_call | solution.py:102
  51.7 0.9 %add.67 = f32[16,1024]{1,0:T(8,128)S(1)} add(f32[16,1024]{1,0:T(8,128)} %shard_map.96, f32[16,1024]{1,0:T(8,128)S(1)} %select_reduce_fusion) | non-fusion elementwise | flops 16384 | bytes 196608 | tf_op jit(solution)/shard_map/add | solution.py:288
  52.5 0.2 fusion.7
  52.7 0.9 %collective-permute-start.14 = (f32[16,16]{1,0:T(8,128)S(1)}, f32[16,16]{1,0:T(8,128)S(1)}, u32[]{:S(2)}, u32[]{:S(2)}) collective-permute-start(f32[16,16]{1,0:T(8,128)S(1)} %fusion.7), channel_id=1, source_target_pairs={{0,2},{1,3},{2,0},{3,1},{4,6},{5,7},{6,4},{7,5},{8,10},{9,11},{10,... | collective-permute-start | bytes 3080 | tf_op jit(solution)/shard_map/ppermute | solution.py:204
  53.6 1.0 %collective-permute-start.15 = (f32[16,16]{1,0:T(8,128)S(1)}, f32[16,16]{1,0:T(8,128)S(1)}, u32[]{:S(2)}, u32[]{:S(2)}) collective-permute-start(f32[16,16]{1,0:T(8,128)S(1)} %fusion.7), channel_id=1, source_target_pairs={{0,1},{1,0},{2,3},{3,2},{4,5},{5,4},{6,7},{7,6},{8,9},{9,8},{10,11... | collective-permute-start | bytes 3080 | tf_op jit(solution)/shard_map/ppermute | solution.py:204
  54.6 1.2 %collective-permute-done.13 = f32[16,16]{1,0:T(8,128)S(1)} collective-permute-done((f32[16,16]{1,0:T(8,128)S(1)}, f32[16,16]{1,0:T(8,128)S(1)}, u32[]{:S(2)}, u32[]{:S(2)}) %collective-permute-start.13) | collective-permute-done | bytes 1056 | tf_op jit(solution)/shard_map/ppermute | solution.py:204
  55.8 0.6 collective-permute-done.14
  56.4 1.1 %collective-permute-start.16 = (f32[16,16]{1,0:T(8,128)S(1)}, f32[16,16]{1,0:T(8,128)S(1)}, u32[]{:S(2)}, u32[]{:S(2)}) collective-permute-start(f32[16,16]{1,0:T(8,128)S(1)} %select_add_fusion), channel_id=1, source_target_pairs={{0,12},{1,13},{2,14},{3,15},{4,8},{5,9},{6,10},{7,11},{8,4},{9,5},... | collective-permute-start | bytes 3080 | tf_op jit(solution)/shard_map/ppermute | solution.py:204
  57.5 4.1 %collective-permute-start.17 = (f32[16,16]{1,0:T(8,128)S(1)}, f32[16,16]{1,0:T(8,128)S(1)}, u32[]{:S(2)}, u32[]{:S(2)}) collective-permute-start(f32[16,16]{1,0:T(8,128)S(1)} %select_add_fusion), channel_id=1, source_target_pairs={{0,8},{1,9},{2,10},{3,11},{4,12},{5,13},{6,14},{7,15},{8,0},{9,1},... | collective-permute-start | bytes 3080 | tf_op jit(solution)/shard_map/ppermute | solution.py:204
  61.6 0.3 collective-permute-done.16
  62.0 1.4 %collective-permute-done.17 = f32[16,16]{1,0:T(8,128)S(1)} collective-permute-done((f32[16,16]{1,0:T(8,128)S(1)}, f32[16,16]{1,0:T(8,128)S(1)}, u32[]{:S(2)}, u32[]{:S(2)}) %collective-permute-start.17) | collective-permute-done | bytes 1056 | tf_op jit(solution)/shard_map/ppermute | solution.py:204
  63.3 1.9 %collective-permute-done.18 = f32[16,16]{1,0:T(8,128)S(1)} collective-permute-done((f32[16,16]{1,0:T(8,128)S(1)}, f32[16,16]{1,0:T(8,128)S(1)}, u32[]{:S(2)}, u32[]{:S(2)}) %collective-permute-start.18) | collective-permute-done | bytes 1056 | tf_op jit(solution)/shard_map/ppermute | solution.py:204
  65.3 0.2 fusion.24
  65.5 0.4 copy-done.10
  65.9 0.6 fusion.14
  (99 shorter events, 1.8 us)
Async XLA Ops:
  0.6 4.1 %copy-start = (f32[16,512]{1,0:T(8,128)S(1)}, f32[16,512]{1,0:T(8,128)}, u32[]{:S(2)}) copy-start(f32[16,512]{1,0:T(8,128)} %param.12) | copy-start | bytes 98308
  1.5 1.2 %copy-start.11 = (f32[512]{0:T(512)S(1)}, f32[512]{0:T(512)}, u32[]{:S(2)}) copy-start(f32[512]{0:T(512)} %param.10) | copy-start | bytes 6148
  2.2 1.4 %copy-start.2 = (f32[16,512]{1,0:T(8,128)S(1)}, f32[16,512]{1,0:T(8,128)}, u32[]{:S(2)}) copy-start(f32[16,512]{1,0:T(8,128)} %param.11) | copy-start | bytes 98308
  2.2 3.3 %copy-start.1 = (bf16[192,512]{1,0:T(8,128)(2,1)S(1)}, bf16[192,512]{1,0:T(8,128)(2,1)}, u32[]{:S(2)}) copy-start(bf16[192,512]{1,0:T(8,128)(2,1)} %param.8) | copy-start | bytes 589828
  2.3 3.1 %collective-permute-start = (bf16[9]{0:T(256)(128)(2,1)S(1)}, bf16[9]{0:T(256)(128)(2,1)S(1)}, u32[]{:S(2)}, u32[]{:S(2)}) collective-permute-start(bf16[9]{0:T(256)(128)(2,1)S(1)} %pad_maximum_fusion.2), channel_id=1, source_target_pairs={{0,1},{1,0},{2,3},{3,2},{4,5},{5,4},{6,7},{7,6},{8,9},{9,8},{10,11... | collective-permute-start | bytes 62 | tf_op jit(solution)/shard_map/ppermute | solution.py:236
  3.5 7.5 %collective-permute-start.12 = (f32[17,512]{1,0:T(8,128)S(1)}, f32[17,512]{1,0:T(8,128)S(1)}, u32[]{:S(2)}, u32[]{:S(2)}) collective-permute-start(f32[17,512]{1,0:T(8,128)S(1)} %pad_maximum_fusion.1), channel_id=1, source_target_pairs={{0,1},{1,0},{2,3},{3,2},{4,5},{5,4},{6,7},{7,6},{8,9},{9,8},{10,11... | collective-permute-start | bytes 104456 | tf_op jit(solution)/shard_map/ppermute | solution.py:245
  3.9 0.7 %copy-start.13 = (bf16[512]{0:T(512)(128)(2,1)S(1)}, bf16[512]{0:T(512)(128)(2,1)}, u32[]{:S(2)}) copy-start(bf16[512]{0:T(512)(128)(2,1)} %param.9) | copy-start | bytes 3076
  4.5 0.7 %copy-start.12 = (f32[16,16]{1,0:T(8,128)S(1)}, f32[16,16]{1,0:T(8,128)}, u32[]{:S(2)}) copy-start(f32[16,16]{1,0:T(8,128)} %param.13) | copy-start | bytes 3076
  5.5 5.5 %copy-start.8 = (bf16[216,512]{1,0:T(8,128)(2,1)}, bf16[216,512]{1,0:T(8,128)(2,1)S(1)}, u32[]{:S(2)}) copy-start(bf16[216,512]{1,0:T(8,128)(2,1)S(1)} %fusion.6.refs_0_) | copy-start | bytes 663556
  5.5 8.7 %collective-permute-start.1 = (bf16[216,512]{1,0:T(8,128)(2,1)S(1)}, bf16[216,512]{1,0:T(8,128)(2,1)S(1)}, u32[]{:S(2)}, u32[]{:S(2)}) collective-permute-start(bf16[216,512]{1,0:T(8,128)(2,1)S(1)} %fusion.6.refs_0_), channel_id=1, source_target_pairs={{0,4},{1,5},{2,6},{3,7},{4,0},{5,1},{6,2},{7,3},{8,12},{9,13},{10,... | collective-permute-start | bytes 663560 | tf_op jit(solution)/shard_map/ppermute | solution.py:157
  8.6 5.6 %collective-permute-start.2 = (bf16[216,512]{1,0:T(8,128)(2,1)S(1)}, bf16[216,512]{1,0:T(8,128)(2,1)S(1)}, u32[]{:S(2)}, u32[]{:S(2)}) collective-permute-start(bf16[216,512]{1,0:T(8,128)(2,1)S(1)} %fusion.6.refs_0_), channel_id=1, source_target_pairs={{4,8},{5,9},{6,10},{7,11},{8,4},{9,5},{10,6},{11,7},{20,24},{21,25... | collective-permute-start | bytes 663560 | tf_op jit(solution)/shard_map/ppermute | solution.py:158
  9.3 7.4 %collective-permute-start.9 = (bf16[216,512]{1,0:T(8,128)(2,1)S(1)}, bf16[216,512]{1,0:T(8,128)(2,1)S(1)}, u32[]{:S(2)}, u32[]{:S(2)}) collective-permute-start(bf16[216,512]{1,0:T(8,128)(2,1)S(1)} %fusion.6.refs_0_), channel_id=1, source_target_pairs={{0,1},{1,0},{2,3},{3,2},{4,5},{5,4},{6,7},{7,6},{8,9},{9,8},{10,11... | collective-permute-start | bytes 663560 | tf_op jit(solution)/shard_map/ppermute | solution.py:244
  9.4 10.6 %collective-permute-start.3 = (bf16[216,512]{1,0:T(8,128)(2,1)S(1)}, bf16[216,512]{1,0:T(8,128)(2,1)S(1)}, u32[]{:S(2)}, u32[]{:S(2)}) collective-permute-start(bf16[216,512]{1,0:T(8,128)(2,1)S(1)} %fusion.6.refs_0_), channel_id=1, source_target_pairs={{0,2},{1,3},{2,0},{3,1},{4,6},{5,7},{6,4},{7,5},{8,10},{9,11},{10,... | collective-permute-start | bytes 663560 | tf_op jit(solution)/shard_map/ppermute | solution.py:159
  11.0 0.6 copy-start.9
  14.2 5.7 %copy-start.14 = (bf16[216,512]{1,0:T(8,128)(2,1)}, bf16[216,512]{1,0:T(8,128)(2,1)S(1)}, u32[]{:S(2)}) copy-start(bf16[216,512]{1,0:T(8,128)(2,1)S(1)} %collective-permute-done.1.refs_1_) | copy-start | bytes 663556
  14.2 15.4 %copy-start.4 = (bf16[216,512]{1,0:T(8,128)(2,1)}, bf16[216,512]{1,0:T(8,128)(2,1)S(1)}, u32[]{:S(2)}) copy-start(bf16[216,512]{1,0:T(8,128)(2,1)S(1)} %collective-permute-done.2.refs_2_) | copy-start | bytes 663556
  14.3 16.0 %collective-permute-start.4 = (bf16[216,512]{1,0:T(8,128)(2,1)S(1)}, bf16[216,512]{1,0:T(8,128)(2,1)S(1)}, u32[]{:S(2)}, u32[]{:S(2)}) collective-permute-start(bf16[216,512]{1,0:T(8,128)(2,1)S(1)} %collective-permute-done.1.refs_1_), channel_id=1, source_target_pairs={{4,8},{5,9},{6,10},{7,11},{8,4},{9,5},{10,6},{11,7},{20,24},{21,25... | collective-permute-start | bytes 663560 | tf_op jit(solution)/shard_map/ppermute | solution.py:161
  14.9 16.7 %collective-permute-start.6 = (bf16[216,512]{1,0:T(8,128)(2,1)S(1)}, bf16[216,512]{1,0:T(8,128)(2,1)S(1)}, u32[]{:S(2)}, u32[]{:S(2)}) collective-permute-start(bf16[216,512]{1,0:T(8,128)(2,1)S(1)} %collective-permute-done.1.refs_1_), channel_id=1, source_target_pairs={{0,2},{1,3},{2,0},{3,1},{4,6},{5,7},{6,4},{7,5},{8,10},{9,11},{10,... | collective-permute-start | bytes 663560 | tf_op jit(solution)/shard_map/ppermute | solution.py:163
  16.9 12.7 %collective-permute-start.5 = (bf16[216,512]{1,0:T(8,128)(2,1)S(1)}, bf16[216,512]{1,0:T(8,128)(2,1)S(1)}, u32[]{:S(2)}, u32[]{:S(2)}) collective-permute-start(bf16[216,512]{1,0:T(8,128)(2,1)S(1)} %collective-permute-done.2.refs_2_), channel_id=1, source_target_pairs={{4,0},{5,1},{6,2},{7,3},{8,12},{9,13},{10,14},{11,15},{20,16},{21,... | collective-permute-start | bytes 663560 | tf_op jit(solution)/shard_map/ppermute | solution.py:162
  20.0 9.7 %copy-start.16 = (bf16[216,512]{1,0:T(8,128)(2,1)}, bf16[216,512]{1,0:T(8,128)(2,1)S(1)}, u32[]{:S(2)}) copy-start(bf16[216,512]{1,0:T(8,128)(2,1)S(1)} %collective-permute-done.3.refs_3_) | copy-start | bytes 663556
  29.7 1.9 %copy-start.7 = (bf16[216,512]{1,0:T(8,128)(2,1)}, bf16[216,512]{1,0:T(8,128)(2,1)S(1)}, u32[]{:S(2)}) copy-start(bf16[216,512]{1,0:T(8,128)(2,1)S(1)} %collective-permute-done.5.refs_5_) | copy-start | bytes 663556
  29.7 11.3 %collective-permute-start.8 = (bf16[216,512]{1,0:T(8,128)(2,1)S(1)}, bf16[216,512]{1,0:T(8,128)(2,1)S(1)}, u32[]{:S(2)}, u32[]{:S(2)}) collective-permute-start(bf16[216,512]{1,0:T(8,128)(2,1)S(1)} %broadcast_select_fusion.1), channel_id=1, source_target_pairs={{0,2},{1,3},{2,0},{3,1},{4,6},{5,7},{6,4},{7,5},{8,10},{9,11},{10,... | collective-permute-start | bytes 663560 | tf_op jit(solution)/shard_map/ppermute | solution.py:165
  30.3 1.3 %copy-start.6 = (bf16[216,512]{1,0:T(8,128)(2,1)}, bf16[216,512]{1,0:T(8,128)(2,1)S(1)}, u32[]{:S(2)}) copy-start(bf16[216,512]{1,0:T(8,128)(2,1)S(1)} %collective-permute-done.4.refs_4_) | copy-start | bytes 663556
  30.3 9.1 %collective-permute-start.7 = (bf16[216,512]{1,0:T(8,128)(2,1)S(1)}, bf16[216,512]{1,0:T(8,128)(2,1)S(1)}, u32[]{:S(2)}, u32[]{:S(2)}) collective-permute-start(bf16[216,512]{1,0:T(8,128)(2,1)S(1)} %collective-permute-done.4.refs_4_), channel_id=1, source_target_pairs={{4,0},{5,1},{6,2},{7,3},{8,12},{9,13},{10,14},{11,15},{20,16},{21,... | collective-permute-start | bytes 663560 | tf_op jit(solution)/shard_map/ppermute | solution.py:164
  31.6 0.7 %copy-start.18 = (bf16[216,512]{1,0:T(8,128)(2,1)}, bf16[216,512]{1,0:T(8,128)(2,1)S(1)}, u32[]{:S(2)}) copy-start(bf16[216,512]{1,0:T(8,128)(2,1)S(1)} %collective-permute-done.6.refs_6_) | copy-start | bytes 663556
  38.6 8.6 %copy-start.3 = (f32[7,16,1024]{2,1,0:T(8,128)S(1)}, f32[7,16,1024]{2,1,0:T(8,128)}, u32[]{:S(2)}) copy-start(f32[7,16,1024]{2,1,0:T(8,128)} %shard_map.95) | copy-start | bytes 1376260
  39.3 1.6 %copy-start.5 = (bf16[216,512]{1,0:T(8,128)(2,1)}, bf16[216,512]{1,0:T(8,128)(2,1)S(1)}, u32[]{:S(2)}) copy-start(bf16[216,512]{1,0:T(8,128)(2,1)S(1)} %collective-permute-done.7.refs_0_) | copy-start | bytes 663556
  39.4 6.0 %collective-permute-start.10 = (bf16[216,512]{1,0:T(8,128)(2,1)S(1)}, bf16[216,512]{1,0:T(8,128)(2,1)S(1)}, u32[]{:S(2)}, u32[]{:S(2)}) collective-permute-start(bf16[216,512]{1,0:T(8,128)(2,1)S(1)} %broadcast_select_fusion), channel_id=1, source_target_pairs={{0,2},{1,3},{2,0},{3,1},{4,6},{5,7},{6,4},{7,5},{8,10},{9,11},{10,... | collective-permute-start | bytes 663560 | tf_op jit(solution)/shard_map/ppermute | solution.py:173
  41.0 6.3 %copy-start.15 = (bf16[216,512]{1,0:T(8,128)(2,1)}, bf16[216,512]{1,0:T(8,128)(2,1)S(1)}, u32[]{:S(2)}) copy-start(bf16[216,512]{1,0:T(8,128)(2,1)S(1)} %collective-permute-done.8.refs_1_) | copy-start | bytes 663556
  45.4 1.9 %copy-start.17 = (bf16[216,512]{1,0:T(8,128)(2,1)}, bf16[216,512]{1,0:T(8,128)(2,1)S(1)}, u32[]{:S(2)}) copy-start(bf16[216,512]{1,0:T(8,128)(2,1)S(1)} %collective-permute-done.10.refs_2_) | copy-start | bytes 663556
  51.7 0.9 %slice-start = ((f32[17,512]{1,0:T(8,128)}), f32[16,512]{1,0:T(8,128)S(1)}, s32[]{:S(2)}) async-start(f32[17,512]{1,0:T(8,128)} %copy-done.9), calls=%async_computation | async-start | bytes 65536 | tf_op jit(solution)/shard_map/slice | solution.py:292
  52.7 3.1 %collective-permute-start.13 = (f32[16,16]{1,0:T(8,128)S(1)}, f32[16,16]{1,0:T(8,128)S(1)}, u32[]{:S(2)}, u32[]{:S(2)}) collective-permute-start(f32[16,16]{1,0:T(8,128)S(1)} %fusion.7), channel_id=1, source_target_pairs={{0,3},{1,2},{2,1},{3,0},{4,7},{5,6},{6,5},{7,4},{8,11},{9,10},{10,... | collective-permute-start | bytes 3080 | tf_op jit(solution)/shard_map/ppermute | solution.py:204
  52.7 3.7 %collective-permute-start.14 = (f32[16,16]{1,0:T(8,128)S(1)}, f32[16,16]{1,0:T(8,128)S(1)}, u32[]{:S(2)}, u32[]{:S(2)}) collective-permute-start(f32[16,16]{1,0:T(8,128)S(1)} %fusion.7), channel_id=1, source_target_pairs={{0,2},{1,3},{2,0},{3,1},{4,6},{5,7},{6,4},{7,5},{8,10},{9,11},{10,... | collective-permute-start | bytes 3080 | tf_op jit(solution)/shard_map/ppermute | solution.py:204
  53.6 2.9 %collective-permute-start.15 = (f32[16,16]{1,0:T(8,128)S(1)}, f32[16,16]{1,0:T(8,128)S(1)}, u32[]{:S(2)}, u32[]{:S(2)}) collective-permute-start(f32[16,16]{1,0:T(8,128)S(1)} %fusion.7), channel_id=1, source_target_pairs={{0,1},{1,0},{2,3},{3,2},{4,5},{5,4},{6,7},{7,6},{8,9},{9,8},{10,11... | collective-permute-start | bytes 3080 | tf_op jit(solution)/shard_map/ppermute | solution.py:204
  56.4 5.5 %collective-permute-start.16 = (f32[16,16]{1,0:T(8,128)S(1)}, f32[16,16]{1,0:T(8,128)S(1)}, u32[]{:S(2)}, u32[]{:S(2)}) collective-permute-start(f32[16,16]{1,0:T(8,128)S(1)} %select_add_fusion), channel_id=1, source_target_pairs={{0,12},{1,13},{2,14},{3,15},{4,8},{5,9},{6,10},{7,11},{8,4},{9,5},... | collective-permute-start | bytes 3080 | tf_op jit(solution)/shard_map/ppermute | solution.py:204
  57.5 5.8 %collective-permute-start.17 = (f32[16,16]{1,0:T(8,128)S(1)}, f32[16,16]{1,0:T(8,128)S(1)}, u32[]{:S(2)}, u32[]{:S(2)}) collective-permute-start(f32[16,16]{1,0:T(8,128)S(1)} %select_add_fusion), channel_id=1, source_target_pairs={{0,8},{1,9},{2,10},{3,11},{4,12},{5,13},{6,14},{7,15},{8,0},{9,1},... | collective-permute-start | bytes 3080 | tf_op jit(solution)/shard_map/ppermute | solution.py:204
  61.6 3.7 %collective-permute-start.18 = (f32[16,16]{1,0:T(8,128)S(1)}, f32[16,16]{1,0:T(8,128)S(1)}, u32[]{:S(2)}, u32[]{:S(2)}) collective-permute-start(f32[16,16]{1,0:T(8,128)S(1)} %select_add_fusion), channel_id=1, source_target_pairs={{0,4},{1,5},{2,6},{3,7},{4,0},{5,1},{6,2},{7,3},{8,12},{9,13},{10,... | collective-permute-start | bytes 3080 | tf_op jit(solution)/shard_map/ppermute | solution.py:204
  61.6 4.3 %collective-permute-start.11 = (f32[16,512]{1,0:T(8,128)S(1)}, f32[16,512]{1,0:T(8,128)S(1)}, u32[]{:S(2)}, u32[]{:S(2)}) collective-permute-start(f32[16,512]{1,0:T(8,128)S(1)} %slice.105), channel_id=1, source_target_pairs={{0,1},{1,0},{2,3},{3,2},{4,5},{5,4},{6,7},{7,6},{8,9},{9,8},{10,11... | collective-permute-start | bytes 98312 | tf_op jit(solution)/shard_map/ppermute | solution.py:298
  65.3 0.6 copy-start.10

commit v20 on v19

--- a/solution.py
+++ b/solution.py
@@ -45,13 +45,21 @@
             )
 
 
-def list_kernel(width, rows, counts, split, flag_ref, xo_ref, terms_ref, *refs):
+def list_kernel(width, rows, counts, split, head, flag_ref, xo_ref, terms_ref, *refs):
     out_ref = refs[-1]
     row_terms = jnp.transpose(terms_ref[...])
     norm_rows, recip_rows = row_terms[:, 0:1], row_terms[:, 1:2]
     if not split:
         out_ref[...] = jnp.zeros_like(out_ref)
-    slot = 0
+    if head:
+        early_ref, refs = refs[0], refs[1:]
+        for k in range(head):
+
+            @pl.when(flag_ref[k] != 0)
+            def _(k=k):
+                out_ref[...] += early_ref[k]
+
+    slot = head
     for ref, count in zip(refs[:-1], counts):
         for k in range(count):
             base = k * rows
@@ -83,7 +91,7 @@
             slot += 1
 
 
-def list_product(flags, own_terms, pieces, width, rows, split=False):
+def list_product(flags, own_terms, pieces, width, rows, split=False, early=None):
     twice_own_t, norm_own, recip_own = own_terms
     own = twice_own_t.shape[0]
     counts = [p.shape[0] // rows for p in pieces]
@@ -99,13 +107,15 @@
         transcendentals=slots * own * cols,
         bytes_accessed=sum(p.size * 2 for p in pieces) + int(math.prod(shape)) * 4,
     )
+    head = 0 if early is None else early.shape[0]
+    extra = [] if early is None else [early]
     return pl.pallas_call(
-        functools.partial(list_kernel, width, rows, counts, split),
+        functools.partial(list_kernel, width, rows, counts, split, head),
         cost_estimate=cost,
-        in_specs=[pl.BlockSpec(memory_space=pltpu.SMEM)] + [vmem] * (2 + len(pieces)),
+        in_specs=[pl.BlockSpec(memory_space=pltpu.SMEM)] + [vmem] * (2 + len(extra) + len(pieces)),
         out_specs=vmem,
         out_shape=jax.ShapeDtypeStruct(shape, jnp.float32),
-    )(flags, twice_own_t, row_terms, *pieces)
+    )(flags, twice_own_t, row_terms, *extra, *pieces)
 
 
 def own_rows_product(flags, own_terms, mine, width):
@@ -284,8 +294,7 @@
 
     if chip_split:
         head = early.shape[0]
-        summed = list_product(flags[head:], own_terms, pieces[head:], width, rows)
-        summed = summed + jnp.sum(jnp.where(flags[:head, None, None] != 0, early, 0.0), axis=0)
+        summed = list_product(flags, own_terms, pieces[head:], width, rows, early=early)
     else:
         summed = own_rows_product(flags, own_terms, pieces[0].reshape(devices, rows, own), width)
     if chip_split:

time: 67 us -> 66.6 us (level)
  matrix products: 0.52 us -> 1.36 us
    add x1 -> x0, other arithmetic: 0.85 us -> none  [shards(): summed + jnp.sum(jnp.where(flags[:head, None, None] != 0, early, 0.0), ax...]
    dot_general x1, matrix products: 0.16 us -> 1.01 us  [shards(): lax.dot_general(chip_lanes, summed * (chip_scale[None, :] / math.sqrt(tot...]
  transfers between devices with their start and end apart: 19 -> 19, of which waited for: 8 -> 8; matrix products, arithmetic and copies ran while one was open for 7% -> 7% of each run, Pallas kernels for 9% -> 10%
where the time goes in v20:
time: 66.6 us; the launch traced here: 66.1 us
  waiting for transfers between devices  21.8 us (33%)
  starting transfers between devices  20.1 us (30%)
  Pallas kernels  10.8 us (16%)
  local copies, waits for them, and re-layouts  5.68 us (9%)
  other arithmetic  4.62 us (7%)
  between operations  1.7 us (3%)
  matrix products  1.36 us (2%)
    pallas_call x2, Pallas kernels, list_product(): pl.pallas_call(functools.partial(list_kernel, width, rows, counts, split,...  10.8 us
    ppermute x1, waiting for transfers between devices, gather_pieces(): out2 = lax.ppermute(inner1, 'row', outward)  9.71 us
    ppermute x6, starting transfers between devices, sum_over_rows(): lax.ppermute(value, 'row', [(i, i ^ m << shift) for i in range(devices)])  6.64 us
    ppermute x6, waiting for transfers between devices, sum_over_rows(): lax.ppermute(value, 'row', [(i, i ^ m << shift) for i in range(devices)])  5.1 us
    ppermute x1, waiting for transfers between devices, gather_pieces(): across4 = lax.ppermute(last, 'row', across)  4.37 us
    ppermute x1, starting transfers between devices, gather_pieces(): swap1 = lax.ppermute(packed, 'row', pairs_swap)  3.09 us
    ppermute x1, waiting for transfers between devices, gather_pieces(): swap1 = lax.ppermute(packed, 'row', pairs_swap)  2.61 us
    unnamed x38, local copies, waits for them, and re-layouts  2.45 us
  transfers between devices with their start and end apart: 19, of which 8 were waited for; matrix products, arithmetic and copies ran while one was open for 7% of the time, Pallas kernels for 10%

profile of v20, /device:TPU:0, one launch (start us, length us, event | category | flops | bytes accessed | tf_op | source)
XLA Modules:
  0.0 66.1 jit_solution(58011468325418635)
XLA Ops:
  0.6 0.7 %convert.8 = bf16[4,2]{0,1:T(2,128)(2,1)S(1)} convert(s32[4,2]{0,1:T(2,128)} %param.14) | non-fusion elementwise | flops 8 | bytes 48 | tf_op jit(solution)/shard_map/convert.3
  1.3 0.1 copy.26
  2.3 0.5 collective-permute-start
  2.8 0.8 %pad_maximum_fusion.1 = f32[17,512]{1,0:T(8,128)S(1)} fusion(f32[1,512]{1,0:T(1,128)S(1)} %bitcast.62, f32[16,512]{1,0:T(8,128)} %param.11), kind=kLoop, calls=%fused_computation.18 | loop fusion | flops 8704 | bytes 69632 | tf_op jit(solution)/shard_map/concatenate | solution.py:256
  3.6 0.1 stack.50
  3.7 0.1 stack.61
  3.9 0.5 convert_element_type.35.flag_ref
  4.3 0.2 copy-done.13
  4.7 0.5 copy-done.12
  5.2 0.1 fusion.25
  5.5 3.1 %collective-permute-start.1 = (bf16[216,512]{1,0:T(8,128)(2,1)S(1)}, bf16[216,512]{1,0:T(8,128)(2,1)S(1)}, u32[]{:S(2)}, u32[]{:S(2)}) collective-permute-start(bf16[216,512]{1,0:T(8,128)(2,1)S(1)} %fusion.6.refs_0_), channel_id=1, source_target_pairs={{0,4},{1,5},{2,6},{3,7},{4,0},{5,1},{6,2},{7,3},{8,12},{9,13},{10,... | collective-permute-start | bytes 663560 | tf_op jit(solution)/shard_map/ppermute | solution.py:167
  8.6 0.7 %collective-permute-start.2 = (bf16[216,512]{1,0:T(8,128)(2,1)S(1)}, bf16[216,512]{1,0:T(8,128)(2,1)S(1)}, u32[]{:S(2)}, u32[]{:S(2)}) collective-permute-start(bf16[216,512]{1,0:T(8,128)(2,1)S(1)} %fusion.6.refs_0_), channel_id=1, source_target_pairs={{4,8},{5,9},{6,10},{7,11},{8,4},{9,5},{10,6},{11,7},{20,24},{21,25... | collective-permute-start | bytes 663560 | tf_op jit(solution)/shard_map/ppermute | solution.py:168
  9.4 1.6 %collective-permute-start.3 = (bf16[216,512]{1,0:T(8,128)(2,1)S(1)}, bf16[216,512]{1,0:T(8,128)(2,1)S(1)}, u32[]{:S(2)}, u32[]{:S(2)}) collective-permute-start(bf16[216,512]{1,0:T(8,128)(2,1)S(1)} %fusion.6.refs_0_), channel_id=1, source_target_pairs={{0,2},{1,3},{2,0},{3,1},{4,6},{5,7},{6,4},{7,5},{8,10},{9,11},{10,... | collective-permute-start | bytes 663560 | tf_op jit(solution)/shard_map/ppermute | solution.py:169
  11.0 0.6 copy-done.9
  11.6 2.6 %collective-permute-done.1.refs_1_ = bf16[216,512]{1,0:T(8,128)(2,1)S(1)} collective-permute-done((bf16[216,512]{1,0:T(8,128)(2,1)S(1)}, bf16[216,512]{1,0:T(8,128)(2,1)S(1)}, u32[]{:S(2)}, u32[]{:S(2)}) %collective-permute-start.1) | collective-permute-done | bytes 221216 | tf_op jit(solution)/shard_map/ppermute | solution.py:167
  14.3 0.7 %collective-permute-start.4 = (bf16[216,512]{1,0:T(8,128)(2,1)S(1)}, bf16[216,512]{1,0:T(8,128)(2,1)S(1)}, u32[]{:S(2)}, u32[]{:S(2)}) collective-permute-start(bf16[216,512]{1,0:T(8,128)(2,1)S(1)} %collective-permute-done.1.refs_1_), channel_id=1, source_target_pairs={{4,8},{5,9},{6,10},{7,11},{8,4},{9,5},{10,6},{11,7},{20,24},{21,25... | collective-permute-start | bytes 663560 | tf_op jit(solution)/shard_map/ppermute | solution.py:171
  14.9 1.7 %collective-permute-start.6 = (bf16[216,512]{1,0:T(8,128)(2,1)S(1)}, bf16[216,512]{1,0:T(8,128)(2,1)S(1)}, u32[]{:S(2)}, u32[]{:S(2)}) collective-permute-start(bf16[216,512]{1,0:T(8,128)(2,1)S(1)} %collective-permute-done.1.refs_1_), channel_id=1, source_target_pairs={{0,2},{1,3},{2,0},{3,1},{4,6},{5,7},{6,4},{7,5},{8,10},{9,11},{10,... | collective-permute-start | bytes 663560 | tf_op jit(solution)/shard_map/ppermute | solution.py:173
  16.9 1.3 %collective-permute-start.5 = (bf16[216,512]{1,0:T(8,128)(2,1)S(1)}, bf16[216,512]{1,0:T(8,128)(2,1)S(1)}, u32[]{:S(2)}, u32[]{:S(2)}) collective-permute-start(bf16[216,512]{1,0:T(8,128)(2,1)S(1)} %collective-permute-done.2.refs_2_), channel_id=1, source_target_pairs={{4,0},{5,1},{6,2},{7,3},{8,12},{9,13},{10,14},{11,15},{20,16},{21,... | collective-permute-start | bytes 663560 | tf_op jit(solution)/shard_map/ppermute | solution.py:172
  18.2 1.0 %copy.27.xo_ref = bf16[1024,192]{1,0:T(8,128)(2,1)} copy(bf16[1024,192]{0,1:T(8,128)(2,1)S(1)} %multiply_bitcast_fusion) | data formatting | bytes 786432 | tf_op jit(solution)/shard_map/transpose | solution.py:265
  19.2 0.7 %maximum_maximum_fusion.terms_ref = f32[8,1024]{1,0:T(8,128)} fusion(f32[1,1024]{1,0:T(1,128)S(1)} %fusion.16, f32[1,1024]{1,0:T(1,128)S(1)} %bitcast.63, f32[8]{0:T(128)S(1)} %pad.18.clone), kind=kLoop, calls=%fused_computation.23 | loop fusion | flops 16384 | bytes 40992 | tf_op jit(solution)/shard_map/concatenate | solution.py:100
  19.9 9.7 %collective-permute-done.5.refs_5_ = bf16[216,512]{1,0:T(8,128)(2,1)S(1)} collective-permute-done((bf16[216,512]{1,0:T(8,128)(2,1)S(1)}, bf16[216,512]{1,0:T(8,128)(2,1)S(1)}, u32[]{:S(2)}, u32[]{:S(2)}) %collective-permute-start.5) | collective-permute-done | bytes 221216 | tf_op jit(solution)/shard_map/ppermute | solution.py:172
  29.7 0.6 collective-permute-start.8
  30.3 1.3 %collective-permute-start.7 = (bf16[216,512]{1,0:T(8,128)(2,1)S(1)}, bf16[216,512]{1,0:T(8,128)(2,1)S(1)}, u32[]{:S(2)}, u32[]{:S(2)}) collective-permute-start(bf16[216,512]{1,0:T(8,128)(2,1)S(1)} %collective-permute-done.4.refs_4_), channel_id=1, source_target_pairs={{4,0},{5,1},{6,2},{7,3},{8,12},{9,13},{10,14},{11,15},{20,16},{21,... | collective-permute-start | bytes 663560 | tf_op jit(solution)/shard_map/ppermute | solution.py:174
  31.6 0.7 %copy-done.18 = bf16[216,512]{1,0:T(8,128)(2,1)} copy-done((bf16[216,512]{1,0:T(8,128)(2,1)}, bf16[216,512]{1,0:T(8,128)(2,1)S(1)}, u32[]{:S(2)}) %copy-start.18) | copy-done | bytes 221208
  32.3 6.3 %shard_map.95.refs_0_ = f32[7,16,1024]{2,1,0:T(8,128)} custom-call(s32[7]{0:T(128)} %convert_element_type.35.flag_ref, bf16[1024,192]{1,0:T(8,128)(2,1)} %copy.27.xo_ref, f32[8,1024]{1,0:T(8,128)} %maximum_maximum_fusion.terms_ref, bf16[216,512]{1,0:T(8,128)(2,1)} %copy-done.8, bf16[216,512]{1,0:T(8,128)(2,1)} %copy-done.14, bf16[216,512]{1,0:T(8,128)(2,1)} %copy-done.4, ...), custom_call_target="tpu_custom_call" | custom-call | flops 1526726656 | bytes 2007040 | tf_op jit(solution)/shard_map/pallas_call | solution.py:112
  38.6 0.7 %slice_bitcast_fusion.3 = bf16[1,18]{1,0:T(2,128)(2,1)S(1)} fusion(bf16[1,216,512]{2,1,0:T(8,128)(2,1)} %bitcast.70), kind=kLoop, calls=%fused_computation.49 | loop fusion | bytes 72 | tf_op jit(solution)/shard_map/squeeze | solution.py:276
  39.4 1.6 %collective-permute-start.10 = (bf16[216,512]{1,0:T(8,128)(2,1)S(1)}, bf16[216,512]{1,0:T(8,128)(2,1)S(1)}, u32[]{:S(2)}, u32[]{:S(2)}) collective-permute-start(bf16[216,512]{1,0:T(8,128)(2,1)S(1)} %broadcast_select_fusion), channel_id=1, source_target_pairs={{0,2},{1,3},{2,0},{3,1},{4,6},{5,7},{6,4},{7,5},{8,10},{9,11},{10,... | collective-permute-start | bytes 663560 | tf_op jit(solution)/shard_map/ppermute | solution.py:183
  41.0 4.4 %collective-permute-done.10.refs_3_ = bf16[216,512]{1,0:T(8,128)(2,1)S(1)} collective-permute-done((bf16[216,512]{1,0:T(8,128)(2,1)S(1)}, bf16[216,512]{1,0:T(8,128)(2,1)S(1)}, u32[]{:S(2)}, u32[]{:S(2)}) %collective-permute-start.10) | collective-permute-done | bytes 221216 | tf_op jit(solution)/shard_map/ppermute | solution.py:183
  45.5 0.2 slice_reduce_fusion
  45.8 0.1 copy.29
  46.3 0.1 lt.26
  46.4 0.2 and_reduce_fusion
  46.6 0.6 and_convert_fusion.flag_ref
  47.2 4.5 %shard_map.96 = f32[16,1024]{1,0:T(8,128)} custom-call(s32[10]{0:T(128)} %and_convert_fusion.flag_ref, bf16[1024,192]{1,0:T(8,128)(2,1)} %copy.27.xo_ref, f32[8,1024]{1,0:T(8,128)} %maximum_maximum_fusion.terms_ref, f32[7,16,1024]{2,1,0:T(8,128)} %shard_map.95.refs_0_, bf16[216,512]{1,0:T(8,128)(2,1)} %copy-done.5, bf16[216,512]{1,0:T(8,128)(2,1)} %copy-done.15, ...), custom_call_target="tpu_custom_call" | custom-call | flops 654311424 | bytes 729088 | tf_op jit(solution)/shard_map/pallas_call | solution.py:112
  51.7 1.0 %fusion.7 = f32[16,16]{1,0:T(8,128)S(1)} fusion(f32[16,512]{1,0:T(8,128)S(1)} %slice-done, f32[16,512]{1,0:T(8,128)S(1)} %copy-done.2, f32[16,1024]{1,0:T(8,128)} %shard_map.96, f32[1024]{0:T(1024)S(1)} %maximum_multiply_fusion), kind=kOutput, calls=%fused_computation.13 | convolution fusion | flops 3178496 | bytes 136192 | tf_op jit(solution)/shard_map/dot_general | solution.py:303
  52.8 0.1 collective-permute-start.14
  52.9 1.7 %collective-permute-start.15 = (f32[16,16]{1,0:T(8,128)S(1)}, f32[16,16]{1,0:T(8,128)S(1)}, u32[]{:S(2)}, u32[]{:S(2)}) collective-permute-start(f32[16,16]{1,0:T(8,128)S(1)} %fusion.7), channel_id=1, source_target_pairs={{0,1},{1,0},{2,3},{3,2},{4,5},{5,4},{6,7},{7,6},{8,9},{9,8},{10,11... | collective-permute-start | bytes 3080 | tf_op jit(solution)/shard_map/ppermute | solution.py:214
  54.6 1.2 %collective-permute-done.13 = f32[16,16]{1,0:T(8,128)S(1)} collective-permute-done((f32[16,16]{1,0:T(8,128)S(1)}, f32[16,16]{1,0:T(8,128)S(1)}, u32[]{:S(2)}, u32[]{:S(2)}) %collective-permute-start.13) | collective-permute-done | bytes 1056 | tf_op jit(solution)/shard_map/ppermute | solution.py:214
  55.9 0.7 collective-permute-done.14
  56.5 0.8 %collective-permute-start.16 = (f32[16,16]{1,0:T(8,128)S(1)}, f32[16,16]{1,0:T(8,128)S(1)}, u32[]{:S(2)}, u32[]{:S(2)}) collective-permute-start(f32[16,16]{1,0:T(8,128)S(1)} %select_add_fusion), channel_id=1, source_target_pairs={{0,12},{1,13},{2,14},{3,15},{4,8},{5,9},{6,10},{7,11},{8,4},{9,5},... | collective-permute-start | bytes 3080 | tf_op jit(solution)/shard_map/ppermute | solution.py:214
  57.4 3.9 %collective-permute-start.17 = (f32[16,16]{1,0:T(8,128)S(1)}, f32[16,16]{1,0:T(8,128)S(1)}, u32[]{:S(2)}, u32[]{:S(2)}) collective-permute-start(f32[16,16]{1,0:T(8,128)S(1)} %select_add_fusion), channel_id=1, source_target_pairs={{0,8},{1,9},{2,10},{3,11},{4,12},{5,13},{6,14},{7,15},{8,0},{9,1},... | collective-permute-start | bytes 3080 | tf_op jit(solution)/shard_map/ppermute | solution.py:214
  61.2 0.4 collective-permute-start.11
  61.7 0.4 collective-permute-done.16
  62.0 1.0 %collective-permute-done.17 = f32[16,16]{1,0:T(8,128)S(1)} collective-permute-done((f32[16,16]{1,0:T(8,128)S(1)}, f32[16,16]{1,0:T(8,128)S(1)}, u32[]{:S(2)}, u32[]{:S(2)}) %collective-permute-start.17) | collective-permute-done | bytes 1056 | tf_op jit(solution)/shard_map/ppermute | solution.py:214
  63.1 1.8 %collective-permute-done.18 = f32[16,16]{1,0:T(8,128)S(1)} collective-permute-done((f32[16,16]{1,0:T(8,128)S(1)}, f32[16,16]{1,0:T(8,128)S(1)}, u32[]{:S(2)}, u32[]{:S(2)}) %collective-permute-start.18) | collective-permute-done | bytes 1056 | tf_op jit(solution)/shard_map/ppermute | solution.py:214
  64.9 0.2 fusion.24
  65.1 0.4 copy-done.10
  65.5 0.6 fusion.14
  (95 shorter events, 1.8 us)
Async XLA Ops:
  0.6 4.1 %copy-start = (f32[16,512]{1,0:T(8,128)S(1)}, f32[16,512]{1,0:T(8,128)}, u32[]{:S(2)}) copy-start(f32[16,512]{1,0:T(8,128)} %param.12) | copy-start | bytes 98308
  1.5 1.2 %copy-start.11 = (f32[512]{0:T(512)S(1)}, f32[512]{0:T(512)}, u32[]{:S(2)}) copy-start(f32[512]{0:T(512)} %param.10) | copy-start | bytes 6148
  2.2 1.4 %copy-start.2 = (f32[16,512]{1,0:T(8,128)S(1)}, f32[16,512]{1,0:T(8,128)}, u32[]{:S(2)}) copy-start(f32[16,512]{1,0:T(8,128)} %param.11) | copy-start | bytes 98308
  2.2 3.3 %copy-start.1 = (bf16[192,512]{1,0:T(8,128)(2,1)S(1)}, bf16[192,512]{1,0:T(8,128)(2,1)}, u32[]{:S(2)}) copy-start(bf16[192,512]{1,0:T(8,128)(2,1)} %param.8) | copy-start | bytes 589828
  2.3 3.1 %collective-permute-start = (bf16[9]{0:T(256)(128)(2,1)S(1)}, bf16[9]{0:T(256)(128)(2,1)S(1)}, u32[]{:S(2)}, u32[]{:S(2)}) collective-permute-start(bf16[9]{0:T(256)(128)(2,1)S(1)} %pad_maximum_fusion.2), channel_id=1, source_target_pairs={{0,1},{1,0},{2,3},{3,2},{4,5},{5,4},{6,7},{7,6},{8,9},{9,8},{10,11... | collective-permute-start | bytes 62 | tf_op jit(solution)/shard_map/ppermute | solution.py:246
  3.5 7.5 %collective-permute-start.12 = (f32[17,512]{1,0:T(8,128)S(1)}, f32[17,512]{1,0:T(8,128)S(1)}, u32[]{:S(2)}, u32[]{:S(2)}) collective-permute-start(f32[17,512]{1,0:T(8,128)S(1)} %pad_maximum_fusion.1), channel_id=1, source_target_pairs={{0,1},{1,0},{2,3},{3,2},{4,5},{5,4},{6,7},{7,6},{8,9},{9,8},{10,11... | collective-permute-start | bytes 104456 | tf_op jit(solution)/shard_map/ppermute | solution.py:255
  3.9 0.7 %copy-start.13 = (bf16[512]{0:T(512)(128)(2,1)S(1)}, bf16[512]{0:T(512)(128)(2,1)}, u32[]{:S(2)}) copy-start(bf16[512]{0:T(512)(128)(2,1)} %param.9) | copy-start | bytes 3076
  4.5 0.7 %copy-start.12 = (f32[16,16]{1,0:T(8,128)S(1)}, f32[16,16]{1,0:T(8,128)}, u32[]{:S(2)}) copy-start(f32[16,16]{1,0:T(8,128)} %param.13) | copy-start | bytes 3076
  5.5 5.5 %copy-start.8 = (bf16[216,512]{1,0:T(8,128)(2,1)}, bf16[216,512]{1,0:T(8,128)(2,1)S(1)}, u32[]{:S(2)}) copy-start(bf16[216,512]{1,0:T(8,128)(2,1)S(1)} %fusion.6.refs_0_) | copy-start | bytes 663556
  5.5 8.7 %collective-permute-start.1 = (bf16[216,512]{1,0:T(8,128)(2,1)S(1)}, bf16[216,512]{1,0:T(8,128)(2,1)S(1)}, u32[]{:S(2)}, u32[]{:S(2)}) collective-permute-start(bf16[216,512]{1,0:T(8,128)(2,1)S(1)} %fusion.6.refs_0_), channel_id=1, source_target_pairs={{0,4},{1,5},{2,6},{3,7},{4,0},{5,1},{6,2},{7,3},{8,12},{9,13},{10,... | collective-permute-start | bytes 663560 | tf_op jit(solution)/shard_map/ppermute | solution.py:167
  8.6 5.6 %collective-permute-start.2 = (bf16[216,512]{1,0:T(8,128)(2,1)S(1)}, bf16[216,512]{1,0:T(8,128)(2,1)S(1)}, u32[]{:S(2)}, u32[]{:S(2)}) collective-permute-start(bf16[216,512]{1,0:T(8,128)(2,1)S(1)} %fusion.6.refs_0_), channel_id=1, source_target_pairs={{4,8},{5,9},{6,10},{7,11},{8,4},{9,5},{10,6},{11,7},{20,24},{21,25... | collective-permute-start | bytes 663560 | tf_op jit(solution)/shard_map/ppermute | solution.py:168
  9.3 7.4 %collective-permute-start.9 = (bf16[216,512]{1,0:T(8,128)(2,1)S(1)}, bf16[216,512]{1,0:T(8,128)(2,1)S(1)}, u32[]{:S(2)}, u32[]{:S(2)}) collective-permute-start(bf16[216,512]{1,0:T(8,128)(2,1)S(1)} %fusion.6.refs_0_), channel_id=1, source_target_pairs={{0,1},{1,0},{2,3},{3,2},{4,5},{5,4},{6,7},{7,6},{8,9},{9,8},{10,11... | collective-permute-start | bytes 663560 | tf_op jit(solution)/shard_map/ppermute | solution.py:254
  9.4 10.5 %collective-permute-start.3 = (bf16[216,512]{1,0:T(8,128)(2,1)S(1)}, bf16[216,512]{1,0:T(8,128)(2,1)S(1)}, u32[]{:S(2)}, u32[]{:S(2)}) collective-permute-start(bf16[216,512]{1,0:T(8,128)(2,1)S(1)} %fusion.6.refs_0_), channel_id=1, source_target_pairs={{0,2},{1,3},{2,0},{3,1},{4,6},{5,7},{6,4},{7,5},{8,10},{9,11},{10,... | collective-permute-start | bytes 663560 | tf_op jit(solution)/shard_map/ppermute | solution.py:169
  11.0 0.6 copy-start.9
  14.2 5.7 %copy-start.14 = (bf16[216,512]{1,0:T(8,128)(2,1)}, bf16[216,512]{1,0:T(8,128)(2,1)S(1)}, u32[]{:S(2)}) copy-start(bf16[216,512]{1,0:T(8,128)(2,1)S(1)} %collective-permute-done.1.refs_1_) | copy-start | bytes 663556
  14.2 15.4 %copy-start.4 = (bf16[216,512]{1,0:T(8,128)(2,1)}, bf16[216,512]{1,0:T(8,128)(2,1)S(1)}, u32[]{:S(2)}) copy-start(bf16[216,512]{1,0:T(8,128)(2,1)S(1)} %collective-permute-done.2.refs_2_) | copy-start | bytes 663556
  14.3 16.0 %collective-permute-start.4 = (bf16[216,512]{1,0:T(8,128)(2,1)S(1)}, bf16[216,512]{1,0:T(8,128)(2,1)S(1)}, u32[]{:S(2)}, u32[]{:S(2)}) collective-permute-start(bf16[216,512]{1,0:T(8,128)(2,1)S(1)} %collective-permute-done.1.refs_1_), channel_id=1, source_target_pairs={{4,8},{5,9},{6,10},{7,11},{8,4},{9,5},{10,6},{11,7},{20,24},{21,25... | collective-permute-start | bytes 663560 | tf_op jit(solution)/shard_map/ppermute | solution.py:171
  14.9 16.7 %collective-permute-start.6 = (bf16[216,512]{1,0:T(8,128)(2,1)S(1)}, bf16[216,512]{1,0:T(8,128)(2,1)S(1)}, u32[]{:S(2)}, u32[]{:S(2)}) collective-permute-start(bf16[216,512]{1,0:T(8,128)(2,1)S(1)} %collective-permute-done.1.refs_1_), channel_id=1, source_target_pairs={{0,2},{1,3},{2,0},{3,1},{4,6},{5,7},{6,4},{7,5},{8,10},{9,11},{10,... | collective-permute-start | bytes 663560 | tf_op jit(solution)/shard_map/ppermute | solution.py:173
  16.9 12.7 %collective-permute-start.5 = (bf16[216,512]{1,0:T(8,128)(2,1)S(1)}, bf16[216,512]{1,0:T(8,128)(2,1)S(1)}, u32[]{:S(2)}, u32[]{:S(2)}) collective-permute-start(bf16[216,512]{1,0:T(8,128)(2,1)S(1)} %collective-permute-done.2.refs_2_), channel_id=1, source_target_pairs={{4,0},{5,1},{6,2},{7,3},{8,12},{9,13},{10,14},{11,15},{20,16},{21,... | collective-permute-start | bytes 663560 | tf_op jit(solution)/shard_map/ppermute | solution.py:172
  19.9 9.8 %copy-start.16 = (bf16[216,512]{1,0:T(8,128)(2,1)}, bf16[216,512]{1,0:T(8,128)(2,1)S(1)}, u32[]{:S(2)}) copy-start(bf16[216,512]{1,0:T(8,128)(2,1)S(1)} %collective-permute-done.3.refs_3_) | copy-start | bytes 663556
  29.7 1.9 %copy-start.7 = (bf16[216,512]{1,0:T(8,128)(2,1)}, bf16[216,512]{1,0:T(8,128)(2,1)S(1)}, u32[]{:S(2)}) copy-start(bf16[216,512]{1,0:T(8,128)(2,1)S(1)} %collective-permute-done.5.refs_5_) | copy-start | bytes 663556
  29.7 11.2 %collective-permute-start.8 = (bf16[216,512]{1,0:T(8,128)(2,1)S(1)}, bf16[216,512]{1,0:T(8,128)(2,1)S(1)}, u32[]{:S(2)}, u32[]{:S(2)}) collective-permute-start(bf16[216,512]{1,0:T(8,128)(2,1)S(1)} %broadcast_select_fusion.1), channel_id=1, source_target_pairs={{0,2},{1,3},{2,0},{3,1},{4,6},{5,7},{6,4},{7,5},{8,10},{9,11},{10,... | collective-permute-start | bytes 663560 | tf_op jit(solution)/shard_map/ppermute | solution.py:175
  30.3 1.3 %copy-start.6 = (bf16[216,512]{1,0:T(8,128)(2,1)}, bf16[216,512]{1,0:T(8,128)(2,1)S(1)}, u32[]{:S(2)}) copy-start(bf16[216,512]{1,0:T(8,128)(2,1)S(1)} %collective-permute-done.4.refs_4_) | copy-start | bytes 663556
  30.3 9.0 %collective-permute-start.7 = (bf16[216,512]{1,0:T(8,128)(2,1)S(1)}, bf16[216,512]{1,0:T(8,128)(2,1)S(1)}, u32[]{:S(2)}, u32[]{:S(2)}) collective-permute-start(bf16[216,512]{1,0:T(8,128)(2,1)S(1)} %collective-permute-done.4.refs_4_), channel_id=1, source_target_pairs={{4,0},{5,1},{6,2},{7,3},{8,12},{9,13},{10,14},{11,15},{20,16},{21,... | collective-permute-start | bytes 663560 | tf_op jit(solution)/shard_map/ppermute | solution.py:174
  31.6 0.7 %copy-start.18 = (bf16[216,512]{1,0:T(8,128)(2,1)}, bf16[216,512]{1,0:T(8,128)(2,1)S(1)}, u32[]{:S(2)}) copy-start(bf16[216,512]{1,0:T(8,128)(2,1)S(1)} %collective-permute-done.6.refs_6_) | copy-start | bytes 663556
  39.3 1.6 %copy-start.5 = (bf16[216,512]{1,0:T(8,128)(2,1)}, bf16[216,512]{1,0:T(8,128)(2,1)S(1)}, u32[]{:S(2)}) copy-start(bf16[216,512]{1,0:T(8,128)(2,1)S(1)} %collective-permute-done.7.refs_1_) | copy-start | bytes 663556
  39.4 6.0 %collective-permute-start.10 = (bf16[216,512]{1,0:T(8,128)(2,1)S(1)}, bf16[216,512]{1,0:T(8,128)(2,1)S(1)}, u32[]{:S(2)}, u32[]{:S(2)}) collective-permute-start(bf16[216,512]{1,0:T(8,128)(2,1)S(1)} %broadcast_select_fusion), channel_id=1, source_target_pairs={{0,2},{1,3},{2,0},{3,1},{4,6},{5,7},{6,4},{7,5},{8,10},{9,11},{10,... | collective-permute-start | bytes 663560 | tf_op jit(solution)/shard_map/ppermute | solution.py:183
  40.9 6.2 %copy-start.15 = (bf16[216,512]{1,0:T(8,128)(2,1)}, bf16[216,512]{1,0:T(8,128)(2,1)S(1)}, u32[]{:S(2)}) copy-start(bf16[216,512]{1,0:T(8,128)(2,1)S(1)} %collective-permute-done.8.refs_2_) | copy-start | bytes 663556
  45.4 1.8 %copy-start.17 = (bf16[216,512]{1,0:T(8,128)(2,1)}, bf16[216,512]{1,0:T(8,128)(2,1)S(1)}, u32[]{:S(2)}) copy-start(bf16[216,512]{1,0:T(8,128)(2,1)S(1)} %collective-permute-done.10.refs_3_) | copy-start | bytes 663556
  47.2 4.5 %slice-start = ((f32[17,512]{1,0:T(8,128)}), f32[16,512]{1,0:T(8,128)S(1)}, s32[]{:S(2)}) async-start(f32[17,512]{1,0:T(8,128)} %copy-done.9), calls=%async_computation | async-start | bytes 65536 | tf_op jit(solution)/shard_map/slice | solution.py:301
  52.7 8.6 %copy-start.3 = (f32[16,1024]{1,0:T(8,128)S(1)}, f32[16,1024]{1,0:T(8,128)}, u32[]{:S(2)}) copy-start(f32[16,1024]{1,0:T(8,128)} %shard_map.96) | copy-start | bytes 196612
  52.7 3.1 %collective-permute-start.13 = (f32[16,16]{1,0:T(8,128)S(1)}, f32[16,16]{1,0:T(8,128)S(1)}, u32[]{:S(2)}, u32[]{:S(2)}) collective-permute-start(f32[16,16]{1,0:T(8,128)S(1)} %fusion.7), channel_id=1, source_target_pairs={{0,3},{1,2},{2,1},{3,0},{4,7},{5,6},{6,5},{7,4},{8,11},{9,10},{10,... | collective-permute-start | bytes 3080 | tf_op jit(solution)/shard_map/ppermute | solution.py:214
  52.8 3.7 %collective-permute-start.14 = (f32[16,16]{1,0:T(8,128)S(1)}, f32[16,16]{1,0:T(8,128)S(1)}, u32[]{:S(2)}, u32[]{:S(2)}) collective-permute-start(f32[16,16]{1,0:T(8,128)S(1)} %fusion.7), channel_id=1, source_target_pairs={{0,2},{1,3},{2,0},{3,1},{4,6},{5,7},{6,4},{7,5},{8,10},{9,11},{10,... | collective-permute-start | bytes 3080 | tf_op jit(solution)/shard_map/ppermute | solution.py:214
  52.9 3.6 %collective-permute-start.15 = (f32[16,16]{1,0:T(8,128)S(1)}, f32[16,16]{1,0:T(8,128)S(1)}, u32[]{:S(2)}, u32[]{:S(2)}) collective-permute-start(f32[16,16]{1,0:T(8,128)S(1)} %fusion.7), channel_id=1, source_target_pairs={{0,1},{1,0},{2,3},{3,2},{4,5},{5,4},{6,7},{7,6},{8,9},{9,8},{10,11... | collective-permute-start | bytes 3080 | tf_op jit(solution)/shard_map/ppermute | solution.py:214
  56.5 5.5 %collective-permute-start.16 = (f32[16,16]{1,0:T(8,128)S(1)}, f32[16,16]{1,0:T(8,128)S(1)}, u32[]{:S(2)}, u32[]{:S(2)}) collective-permute-start(f32[16,16]{1,0:T(8,128)S(1)} %select_add_fusion), channel_id=1, source_target_pairs={{0,12},{1,13},{2,14},{3,15},{4,8},{5,9},{6,10},{7,11},{8,4},{9,5},... | collective-permute-start | bytes 3080 | tf_op jit(solution)/shard_map/ppermute | solution.py:214
  57.4 5.7 %collective-permute-start.17 = (f32[16,16]{1,0:T(8,128)S(1)}, f32[16,16]{1,0:T(8,128)S(1)}, u32[]{:S(2)}, u32[]{:S(2)}) collective-permute-start(f32[16,16]{1,0:T(8,128)S(1)} %select_add_fusion), channel_id=1, source_target_pairs={{0,8},{1,9},{2,10},{3,11},{4,12},{5,13},{6,14},{7,15},{8,0},{9,1},... | collective-permute-start | bytes 3080 | tf_op jit(solution)/shard_map/ppermute | solution.py:214
  61.2 3.7 %collective-permute-start.18 = (f32[16,16]{1,0:T(8,128)S(1)}, f32[16,16]{1,0:T(8,128)S(1)}, u32[]{:S(2)}, u32[]{:S(2)}) collective-permute-start(f32[16,16]{1,0:T(8,128)S(1)} %select_add_fusion), channel_id=1, source_target_pairs={{0,4},{1,5},{2,6},{3,7},{4,0},{5,1},{6,2},{7,3},{8,12},{9,13},{10,... | collective-permute-start | bytes 3080 | tf_op jit(solution)/shard_map/ppermute | solution.py:214
  61.2 4.3 %collective-permute-start.11 = (f32[16,512]{1,0:T(8,128)S(1)}, f32[16,512]{1,0:T(8,128)S(1)}, u32[]{:S(2)}, u32[]{:S(2)}) collective-permute-start(f32[16,512]{1,0:T(8,128)S(1)} %slice.97), channel_id=1, source_target_pairs={{0,1},{1,0},{2,3},{3,2},{4,5},{5,4},{6,7},{7,6},{8,9},{9,8},{10,11... | collective-permute-start | bytes 98312 | tf_op jit(solution)/shard_map/ppermute | solution.py:307
  64.9 0.6 copy-start.10

commit v21 on v19

--- a/solution.py
+++ b/solution.py
@@ -198,18 +198,19 @@
             stride *= 2
         return value
     me = lax.axis_index("row")
-    for shift in (0, 2):
-        got = {0: value}
+    got = {0: value}
+    for m in (1, 2, 3):
+        got[m] = lax.ppermute(value, "row", [(i, i ^ m) for i in range(devices)])
+    place = me & 3
+    total = None
+    for k in range(4):
+        member = got[0]
         for m in (1, 2, 3):
-            got[m] = lax.ppermute(value, "row", [(i, i ^ (m << shift)) for i in range(devices)])
-        place = (me >> shift) & 3
-        total = None
-        for k in range(4):
-            member = got[0]
-            for m in (1, 2, 3):
-                member = jnp.where((k ^ place) == m, got[m], member)
-            total = member if total is None else total + member
-        value = total
+            member = jnp.where((k ^ place) == m, got[m], member)
+        total = member if total is None else total + member
+    value = total
+    for stride in (4, 8):
+        value = value + lax.ppermute(value, "row", [(i, i ^ stride) for i in range(devices)])
     return value
 
 

time: 67 us -> 67.8 us (1.012)
  starting transfers between devices: 20.2 us -> 21.5 us
  Pallas kernels: 10.6 us -> 9.86 us
  other arithmetic: 5.04 us -> 5.72 us
    ppermute x6 -> x5, starting transfers between devices: 7.08 us -> 8.42 us  [the longest x2 6.51 us: sum_over_rows(): lax.ppermute(value, 'row', [(i, i ^ stride) for i in range(devices)])]
    pallas_call x2, Pallas kernels: 10.6 us -> 9.86 us  [list_product(): pl.pallas_call(functools.partial(list_kernel, width, rows, counts, split)...]
    convert_element_type x1, other arithmetic: 0.01 us -> 0.69 us  [shards(): weighted = (degree_scale[None, :] * lanczos_block).astype(jnp.bfloat16)]
    ppermute x6 -> x5, waiting for transfers between devices: 5.47 us -> 5.79 us  [the longest x2 3.96 us: sum_over_rows(): lax.ppermute(value, 'row', [(i, i ^ stride) for i in range(devices)])]
  transfers between devices with their start and end apart: 19 -> 18, of which waited for: 8 -> 7; matrix products, arithmetic and copies ran while one was open for 7% -> 8% of each run, Pallas kernels for 9% -> 9%
where the time goes in v21:
time: 67.8 us; the launch traced here: 67.6 us
  waiting for transfers between devices  21.8 us (32%)
  starting transfers between devices  21.5 us (32%)
  Pallas kernels  9.86 us (15%)
  local copies, waits for them, and re-layouts  6.55 us (10%)
  other arithmetic  5.72 us (8%)
  between operations  1.66 us (2%)
    pallas_call x2, Pallas kernels, list_product(): pl.pallas_call(functools.partial(list_kernel, width, rows, counts, split)...  9.86 us
    ppermute x1, waiting for transfers between devices, gather_pieces(): out2 = lax.ppermute(inner1, 'row', outward)  9.69 us
    ppermute x2, starting transfers between devices, sum_over_rows(): lax.ppermute(value, 'row', [(i, i ^ stride) for i in range(devices)])  6.51 us
    ppermute x1, waiting for transfers between devices, gather_pieces(): across4 = lax.ppermute(last, 'row', across)  4.38 us
    ppermute x2, waiting for transfers between devices, sum_over_rows(): lax.ppermute(value, 'row', [(i, i ^ stride) for i in range(devices)])  3.96 us
    ppermute x1, starting transfers between devices, gather_pieces(): swap1 = lax.ppermute(packed, 'row', pairs_swap)  3.09 us
    unnamed x38, local copies, waits for them, and re-layouts  2.61 us
    ppermute x1, waiting for transfers between devices, gather_pieces(): swap1 = lax.ppermute(packed, 'row', pairs_swap)  1.94 us
  transfers between devices with their start and end apart: 18, of which 7 were waited for; matrix products, arithmetic and copies ran while one was open for 8% of the time, Pallas kernels for 9%

profile of v21, /device:TPU:0, one launch (start us, length us, event | category | flops | bytes accessed | tf_op | source)
XLA Modules:
  0.0 67.6 jit_solution(112794156178682312)
XLA Ops:
  0.7 0.7 %convert.8 = bf16[4,2]{0,1:T(2,128)(2,1)S(1)} convert(s32[4,2]{0,1:T(2,128)} %param.14) | non-fusion elementwise | flops 8 | bytes 48 | tf_op jit(solution)/shard_map/convert.3
  1.4 0.1 copy.26
  2.3 0.5 collective-permute-start
  2.8 0.8 %pad_maximum_fusion.1 = f32[17,512]{1,0:T(8,128)S(1)} fusion(f32[1,512]{1,0:T(1,128)} %bitcast.62, f32[16,512]{1,0:T(8,128)} %param.11), kind=kLoop, calls=%fused_computation.19 | loop fusion | flops 8704 | bytes 69632 | tf_op jit(solution)/shard_map/concatenate | solution.py:247
  3.6 0.7 %multiply_convert_fusion = bf16[16,512]{1,0:T(8,128)(2,1)S(1)} fusion(f32[16,512]{1,0:T(8,128)S(1)} %copy-done.2, f32[512]{0:T(512)} %param.10), kind=kLoop, calls=%fused_computation.26 | loop fusion | flops 16384 | bytes 51200 | tf_op jit(solution)/shard_map/convert_element_type | solution.py:233
  4.3 0.1 stack.50
  4.4 0.1 stack.61
  4.5 0.5 convert_element_type.35.flag_ref
  5.0 0.2 copy-done.13
  5.5 3.1 %collective-permute-start.1 = (bf16[216,512]{1,0:T(8,128)(2,1)S(1)}, bf16[216,512]{1,0:T(8,128)(2,1)S(1)}, u32[]{:S(2)}, u32[]{:S(2)}) collective-permute-start(bf16[216,512]{1,0:T(8,128)(2,1)S(1)} %fusion.6.refs_0_), channel_id=1, source_target_pairs={{0,4},{1,5},{2,6},{3,7},{4,0},{5,1},{6,2},{7,3},{8,12},{9,13},{10,... | collective-permute-start | bytes 663560 | tf_op jit(solution)/shard_map/ppermute | solution.py:157
  8.6 0.7 collective-permute-start.2
  9.4 1.6 %collective-permute-start.3 = (bf16[216,512]{1,0:T(8,128)(2,1)S(1)}, bf16[216,512]{1,0:T(8,128)(2,1)S(1)}, u32[]{:S(2)}, u32[]{:S(2)}) collective-permute-start(bf16[216,512]{1,0:T(8,128)(2,1)S(1)} %fusion.6.refs_0_), channel_id=1, source_target_pairs={{0,2},{1,3},{2,0},{3,1},{4,6},{5,7},{6,4},{7,5},{8,10},{9,11},{10,... | collective-permute-start | bytes 663560 | tf_op jit(solution)/shard_map/ppermute | solution.py:159
  11.0 0.6 copy-done.9
  11.6 0.7 %copy-done.11 = f32[512]{0:T(512)S(1)} copy-done((f32[512]{0:T(512)S(1)}, f32[512]{0:T(512)}, u32[]{:S(2)}) %copy-start.11) | copy-done | bytes 2072
  12.3 1.9 %collective-permute-done.1.refs_1_ = bf16[216,512]{1,0:T(8,128)(2,1)S(1)} collective-permute-done((bf16[216,512]{1,0:T(8,128)(2,1)S(1)}, bf16[216,512]{1,0:T(8,128)(2,1)S(1)}, u32[]{:S(2)}, u32[]{:S(2)}) %collective-permute-start.1) | collective-permute-done | bytes 221216 | tf_op jit(solution)/shard_map/ppermute | solution.py:157
  14.3 0.7 collective-permute-start.4
  14.9 1.7 %collective-permute-start.6 = (bf16[216,512]{1,0:T(8,128)(2,1)S(1)}, bf16[216,512]{1,0:T(8,128)(2,1)S(1)}, u32[]{:S(2)}, u32[]{:S(2)}) collective-permute-start(bf16[216,512]{1,0:T(8,128)(2,1)S(1)} %collective-permute-done.1.refs_1_), channel_id=1, source_target_pairs={{0,2},{1,3},{2,0},{3,1},{4,6},{5,7},{6,4},{7,5},{8,10},{9,11},{10,... | collective-permute-start | bytes 663560 | tf_op jit(solution)/shard_map/ppermute | solution.py:163
  16.9 1.3 %collective-permute-start.5 = (bf16[216,512]{1,0:T(8,128)(2,1)S(1)}, bf16[216,512]{1,0:T(8,128)(2,1)S(1)}, u32[]{:S(2)}, u32[]{:S(2)}) collective-permute-start(bf16[216,512]{1,0:T(8,128)(2,1)S(1)} %collective-permute-done.2.refs_2_), channel_id=1, source_target_pairs={{4,0},{5,1},{6,2},{7,3},{8,12},{9,13},{10,14},{11,15},{20,16},{21,... | collective-permute-start | bytes 663560 | tf_op jit(solution)/shard_map/ppermute | solution.py:162
  18.2 1.0 %copy.27.xo_ref = bf16[1024,192]{1,0:T(8,128)(2,1)} copy(bf16[1024,192]{0,1:T(8,128)(2,1)S(1)} %multiply_bitcast_fusion) | data formatting | bytes 786432 | tf_op jit(solution)/shard_map/transpose | solution.py:256
  19.2 0.7 %maximum_maximum_fusion.terms_ref = f32[8,1024]{1,0:T(8,128)} fusion(f32[1,1024]{1,0:T(1,128)S(1)} %fusion.16, f32[1,1024]{1,0:T(1,128)S(1)} %bitcast.63, f32[8]{0:T(128)S(1)} %pad.18.clone), kind=kLoop, calls=%fused_computation.24 | loop fusion | flops 16384 | bytes 40992 | tf_op jit(solution)/shard_map/concatenate | solution.py:92
  20.0 9.7 %collective-permute-done.5.refs_5_ = bf16[216,512]{1,0:T(8,128)(2,1)S(1)} collective-permute-done((bf16[216,512]{1,0:T(8,128)(2,1)S(1)}, bf16[216,512]{1,0:T(8,128)(2,1)S(1)}, u32[]{:S(2)}, u32[]{:S(2)}) %collective-permute-start.5) | collective-permute-done | bytes 221216 | tf_op jit(solution)/shard_map/ppermute | solution.py:162
  29.7 0.6 collective-permute-start.8
  30.3 1.3 %collective-permute-start.7 = (bf16[216,512]{1,0:T(8,128)(2,1)S(1)}, bf16[216,512]{1,0:T(8,128)(2,1)S(1)}, u32[]{:S(2)}, u32[]{:S(2)}) collective-permute-start(bf16[216,512]{1,0:T(8,128)(2,1)S(1)} %collective-permute-done.4.refs_4_), channel_id=1, source_target_pairs={{4,0},{5,1},{6,2},{7,3},{8,12},{9,13},{10,14},{11,15},{20,16},{21,... | collective-permute-start | bytes 663560 | tf_op jit(solution)/shard_map/ppermute | solution.py:164
  31.7 0.7 %copy-done.18 = bf16[216,512]{1,0:T(8,128)(2,1)} copy-done((bf16[216,512]{1,0:T(8,128)(2,1)}, bf16[216,512]{1,0:T(8,128)(2,1)S(1)}, u32[]{:S(2)}) %copy-start.18) | copy-done | bytes 221208
  32.3 6.3 %shard_map.95 = f32[7,16,1024]{2,1,0:T(8,128)} custom-call(s32[7]{0:T(128)} %convert_element_type.35.flag_ref, bf16[1024,192]{1,0:T(8,128)(2,1)} %copy.27.xo_ref, f32[8,1024]{1,0:T(8,128)} %maximum_maximum_fusion.terms_ref, bf16[216,512]{1,0:T(8,128)(2,1)} %copy-done.8, bf16[216,512]{1,0:T(8,128)(2,1)} %copy-done.14, bf16[216,512]{1,0:T(8,128)(2,1)} %copy-done.4, ...), custom_call_target="tpu_custom_call" | custom-call | flops 1526726656 | bytes 2007040 | tf_op jit(solution)/shard_map/pallas_call | solution.py:102
  38.6 0.7 %slice_bitcast_fusion.3 = bf16[1,18]{1,0:T(2,128)(2,1)S(1)} fusion(bf16[1,216,512]{2,1,0:T(8,128)(2,1)} %bitcast.70), kind=kLoop, calls=%fused_computation.50 | loop fusion | bytes 72 | tf_op jit(solution)/shard_map/squeeze | solution.py:267
  39.4 1.6 %collective-permute-start.10 = (bf16[216,512]{1,0:T(8,128)(2,1)S(1)}, bf16[216,512]{1,0:T(8,128)(2,1)S(1)}, u32[]{:S(2)}, u32[]{:S(2)}) collective-permute-start(bf16[216,512]{1,0:T(8,128)(2,1)S(1)} %broadcast_select_fusion), channel_id=1, source_target_pairs={{0,2},{1,3},{2,0},{3,1},{4,6},{5,7},{6,4},{7,5},{8,10},{9,11},{10,... | collective-permute-start | bytes 663560 | tf_op jit(solution)/shard_map/ppermute | solution.py:173
  41.0 4.4 %collective-permute-done.10.refs_2_ = bf16[216,512]{1,0:T(8,128)(2,1)S(1)} collective-permute-done((bf16[216,512]{1,0:T(8,128)(2,1)S(1)}, bf16[216,512]{1,0:T(8,128)(2,1)S(1)}, u32[]{:S(2)}, u32[]{:S(2)}) %collective-permute-start.10) | collective-permute-done | bytes 221216 | tf_op jit(solution)/shard_map/ppermute | solution.py:173
  45.6 0.2 slice_reduce_fusion
  45.8 0.1 copy.29
  46.3 0.1 lt.26
  46.4 0.2 and_reduce_fusion
  46.6 0.6 slice.82.flag_ref
  47.4 3.6 %shard_map.96 = f32[16,1024]{1,0:T(8,128)} custom-call(s32[3]{0:T(128)} %slice.82.flag_ref, bf16[1024,192]{1,0:T(8,128)(2,1)} %copy.27.xo_ref, f32[8,1024]{1,0:T(8,128)} %maximum_maximum_fusion.terms_ref, bf16[216,512]{1,0:T(8,128)(2,1)} %copy-done.5, bf16[216,512]{1,0:T(8,128)(2,1)} %copy-done.15, bf16[216,512]{1,0:T(8,128)(2,1)} %copy-done.17), custom_call_target="tpu_custom_call" | custom-call | flops 654311424 | bytes 729088 | tf_op jit(solution)/shard_map/pallas_call | solution.py:102
  51.0 0.9 %add.64 = f32[16,1024]{1,0:T(8,128)S(1)} add(f32[16,1024]{1,0:T(8,128)} %shard_map.96, f32[16,1024]{1,0:T(8,128)S(1)} %select_reduce_fusion) | non-fusion elementwise | flops 16384 | bytes 196608 | tf_op jit(solution)/shard_map/add | solution.py:289
  51.8 0.2 fusion.7
  52.0 1.6 %collective-permute-start.14 = (f32[16,16]{1,0:T(8,128)S(1)}, f32[16,16]{1,0:T(8,128)S(1)}, u32[]{:S(2)}, u32[]{:S(2)}) collective-permute-start(f32[16,16]{1,0:T(8,128)S(1)} %fusion.7), channel_id=1, source_target_pairs={{0,2},{1,3},{2,0},{3,1},{4,6},{5,7},{6,4},{7,5},{8,10},{9,11},{10,... | collective-permute-start | bytes 3080 | tf_op jit(solution)/shard_map/ppermute | solution.py:203
  53.6 0.3 collective-permute-start.15
  53.9 1.2 %collective-permute-done.13 = f32[16,16]{1,0:T(8,128)S(1)} collective-permute-done((f32[16,16]{1,0:T(8,128)S(1)}, f32[16,16]{1,0:T(8,128)S(1)}, u32[]{:S(2)}, u32[]{:S(2)}) %collective-permute-start.13) | collective-permute-done | bytes 1056 | tf_op jit(solution)/shard_map/ppermute | solution.py:203
  55.1 0.6 collective-permute-done.14
  55.8 4.5 %collective-permute-start.16 = (f32[16,16]{1,0:T(8,128)S(1)}, f32[16,16]{1,0:T(8,128)S(1)}, u32[]{:S(2)}, u32[]{:S(2)}) collective-permute-start(f32[16,16]{1,0:T(8,128)S(1)} %select_add_fusion), channel_id=1, source_target_pairs={{0,4},{1,5},{2,6},{3,7},{4,0},{5,1},{6,2},{7,3},{8,12},{9,13},{10,... | collective-permute-start | bytes 3080 | tf_op jit(solution)/shard_map/ppermute | solution.py:213
  60.2 0.1 fusion.25
  60.4 1.5 %collective-permute-done.16 = f32[16,16]{1,0:T(8,128)S(1)} collective-permute-done((f32[16,16]{1,0:T(8,128)S(1)}, f32[16,16]{1,0:T(8,128)S(1)}, u32[]{:S(2)}, u32[]{:S(2)}) %collective-permute-start.16) | collective-permute-done | bytes 1056 | tf_op jit(solution)/shard_map/ppermute | solution.py:213
  61.9 2.1 %collective-permute-start.17 = (f32[16,16]{1,0:T(8,128)S(1)}, f32[16,16]{1,0:T(8,128)S(1)}, u32[]{:S(2)}, u32[]{:S(2)}) collective-permute-start(f32[16,16]{1,0:T(8,128)S(1)} %add.69), channel_id=1, source_target_pairs={{0,8},{1,9},{2,10},{3,11},{4,12},{5,13},{6,14},{7,15},{8,0},{9,1},... | collective-permute-start | bytes 3080 | tf_op jit(solution)/shard_map/ppermute | solution.py:213
  63.9 2.5 %collective-permute-done.17 = f32[16,16]{1,0:T(8,128)S(1)} collective-permute-done((f32[16,16]{1,0:T(8,128)S(1)}, f32[16,16]{1,0:T(8,128)S(1)}, u32[]{:S(2)}, u32[]{:S(2)}) %collective-permute-start.17) | collective-permute-done | bytes 1056 | tf_op jit(solution)/shard_map/ppermute | solution.py:213
  66.4 0.2 fusion.24
  66.6 0.4 copy-done.10
  67.0 0.6 fusion.14
  (98 shorter events, 1.8 us)
Async XLA Ops:
  0.6 59.6 %copy-start = (f32[16,512]{1,0:T(8,128)S(1)}, f32[16,512]{1,0:T(8,128)}, u32[]{:S(2)}) copy-start(f32[16,512]{1,0:T(8,128)} %param.12) | copy-start | bytes 98308
  0.6 3.0 %copy-start.2 = (f32[16,512]{1,0:T(8,128)S(1)}, f32[16,512]{1,0:T(8,128)}, u32[]{:S(2)}) copy-start(f32[16,512]{1,0:T(8,128)} %param.11) | copy-start | bytes 98308
  0.7 4.8 %copy-start.1 = (bf16[192,512]{1,0:T(8,128)(2,1)S(1)}, bf16[192,512]{1,0:T(8,128)(2,1)}, u32[]{:S(2)}) copy-start(bf16[192,512]{1,0:T(8,128)(2,1)} %param.8) | copy-start | bytes 589828
  2.3 3.1 %collective-permute-start = (bf16[9]{0:T(256)(128)(2,1)S(1)}, bf16[9]{0:T(256)(128)(2,1)S(1)}, u32[]{:S(2)}, u32[]{:S(2)}) collective-permute-start(bf16[9]{0:T(256)(128)(2,1)S(1)} %pad_maximum_fusion.2), channel_id=1, source_target_pairs={{0,1},{1,0},{2,3},{3,2},{4,5},{5,4},{6,7},{7,6},{8,9},{9,8},{10,11... | collective-permute-start | bytes 62 | tf_op jit(solution)/shard_map/ppermute | solution.py:237
  3.6 7.4 %collective-permute-start.12 = (f32[17,512]{1,0:T(8,128)S(1)}, f32[17,512]{1,0:T(8,128)S(1)}, u32[]{:S(2)}, u32[]{:S(2)}) collective-permute-start(f32[17,512]{1,0:T(8,128)S(1)} %pad_maximum_fusion.1), channel_id=1, source_target_pairs={{0,1},{1,0},{2,3},{3,2},{4,5},{5,4},{6,7},{7,6},{8,9},{9,8},{10,11... | collective-permute-start | bytes 104456 | tf_op jit(solution)/shard_map/ppermute | solution.py:246
  4.5 0.7 %copy-start.13 = (bf16[512]{0:T(512)(128)(2,1)S(1)}, bf16[512]{0:T(512)(128)(2,1)}, u32[]{:S(2)}) copy-start(bf16[512]{0:T(512)(128)(2,1)} %param.9) | copy-start | bytes 3076
  5.5 5.5 %copy-start.8 = (bf16[216,512]{1,0:T(8,128)(2,1)}, bf16[216,512]{1,0:T(8,128)(2,1)S(1)}, u32[]{:S(2)}) copy-start(bf16[216,512]{1,0:T(8,128)(2,1)S(1)} %fusion.6.refs_0_) | copy-start | bytes 663556
  5.5 8.7 %collective-permute-start.1 = (bf16[216,512]{1,0:T(8,128)(2,1)S(1)}, bf16[216,512]{1,0:T(8,128)(2,1)S(1)}, u32[]{:S(2)}, u32[]{:S(2)}) collective-permute-start(bf16[216,512]{1,0:T(8,128)(2,1)S(1)} %fusion.6.refs_0_), channel_id=1, source_target_pairs={{0,4},{1,5},{2,6},{3,7},{4,0},{5,1},{6,2},{7,3},{8,12},{9,13},{10,... | collective-permute-start | bytes 663560 | tf_op jit(solution)/shard_map/ppermute | solution.py:157
  8.6 5.6 %collective-permute-start.2 = (bf16[216,512]{1,0:T(8,128)(2,1)S(1)}, bf16[216,512]{1,0:T(8,128)(2,1)S(1)}, u32[]{:S(2)}, u32[]{:S(2)}) collective-permute-start(bf16[216,512]{1,0:T(8,128)(2,1)S(1)} %fusion.6.refs_0_), channel_id=1, source_target_pairs={{4,8},{5,9},{6,10},{7,11},{8,4},{9,5},{10,6},{11,7},{20,24},{21,25... | collective-permute-start | bytes 663560 | tf_op jit(solution)/shard_map/ppermute | solution.py:158
  9.3 7.4 %collective-permute-start.9 = (bf16[216,512]{1,0:T(8,128)(2,1)S(1)}, bf16[216,512]{1,0:T(8,128)(2,1)S(1)}, u32[]{:S(2)}, u32[]{:S(2)}) collective-permute-start(bf16[216,512]{1,0:T(8,128)(2,1)S(1)} %fusion.6.refs_0_), channel_id=1, source_target_pairs={{0,1},{1,0},{2,3},{3,2},{4,5},{5,4},{6,7},{7,6},{8,9},{9,8},{10,11... | collective-permute-start | bytes 663560 | tf_op jit(solution)/shard_map/ppermute | solution.py:245
  9.4 10.6 %collective-permute-start.3 = (bf16[216,512]{1,0:T(8,128)(2,1)S(1)}, bf16[216,512]{1,0:T(8,128)(2,1)S(1)}, u32[]{:S(2)}, u32[]{:S(2)}) collective-permute-start(bf16[216,512]{1,0:T(8,128)(2,1)S(1)} %fusion.6.refs_0_), channel_id=1, source_target_pairs={{0,2},{1,3},{2,0},{3,1},{4,6},{5,7},{6,4},{7,5},{8,10},{9,11},{10,... | collective-permute-start | bytes 663560 | tf_op jit(solution)/shard_map/ppermute | solution.py:159
  11.0 0.6 copy-start.9
  11.6 0.7 %copy-start.11 = (f32[512]{0:T(512)S(1)}, f32[512]{0:T(512)}, u32[]{:S(2)}) copy-start(f32[512]{0:T(512)} %param.10) | copy-start | bytes 6148
  14.3 5.7 %copy-start.14 = (bf16[216,512]{1,0:T(8,128)(2,1)}, bf16[216,512]{1,0:T(8,128)(2,1)S(1)}, u32[]{:S(2)}) copy-start(bf16[216,512]{1,0:T(8,128)(2,1)S(1)} %collective-permute-done.1.refs_1_) | copy-start | bytes 663556
  14.3 15.4 %copy-start.4 = (bf16[216,512]{1,0:T(8,128)(2,1)}, bf16[216,512]{1,0:T(8,128)(2,1)S(1)}, u32[]{:S(2)}) copy-start(bf16[216,512]{1,0:T(8,128)(2,1)S(1)} %collective-permute-done.2.refs_2_) | copy-start | bytes 663556
  14.3 16.0 %collective-permute-start.4 = (bf16[216,512]{1,0:T(8,128)(2,1)S(1)}, bf16[216,512]{1,0:T(8,128)(2,1)S(1)}, u32[]{:S(2)}, u32[]{:S(2)}) collective-permute-start(bf16[216,512]{1,0:T(8,128)(2,1)S(1)} %collective-permute-done.1.refs_1_), channel_id=1, source_target_pairs={{4,8},{5,9},{6,10},{7,11},{8,4},{9,5},{10,6},{11,7},{20,24},{21,25... | collective-permute-start | bytes 663560 | tf_op jit(solution)/shard_map/ppermute | solution.py:161
  14.9 16.7 %collective-permute-start.6 = (bf16[216,512]{1,0:T(8,128)(2,1)S(1)}, bf16[216,512]{1,0:T(8,128)(2,1)S(1)}, u32[]{:S(2)}, u32[]{:S(2)}) collective-permute-start(bf16[216,512]{1,0:T(8,128)(2,1)S(1)} %collective-permute-done.1.refs_1_), channel_id=1, source_target_pairs={{0,2},{1,3},{2,0},{3,1},{4,6},{5,7},{6,4},{7,5},{8,10},{9,11},{10,... | collective-permute-start | bytes 663560 | tf_op jit(solution)/shard_map/ppermute | solution.py:163
  16.9 12.7 %collective-permute-start.5 = (bf16[216,512]{1,0:T(8,128)(2,1)S(1)}, bf16[216,512]{1,0:T(8,128)(2,1)S(1)}, u32[]{:S(2)}, u32[]{:S(2)}) collective-permute-start(bf16[216,512]{1,0:T(8,128)(2,1)S(1)} %collective-permute-done.2.refs_2_), channel_id=1, source_target_pairs={{4,0},{5,1},{6,2},{7,3},{8,12},{9,13},{10,14},{11,15},{20,16},{21,... | collective-permute-start | bytes 663560 | tf_op jit(solution)/shard_map/ppermute | solution.py:162
  20.0 9.8 %copy-start.16 = (bf16[216,512]{1,0:T(8,128)(2,1)}, bf16[216,512]{1,0:T(8,128)(2,1)S(1)}, u32[]{:S(2)}) copy-start(bf16[216,512]{1,0:T(8,128)(2,1)S(1)} %collective-permute-done.3.refs_3_) | copy-start | bytes 663556
  29.7 1.9 %copy-start.7 = (bf16[216,512]{1,0:T(8,128)(2,1)}, bf16[216,512]{1,0:T(8,128)(2,1)S(1)}, u32[]{:S(2)}) copy-start(bf16[216,512]{1,0:T(8,128)(2,1)S(1)} %collective-permute-done.5.refs_5_) | copy-start | bytes 663556
  29.7 11.3 %collective-permute-start.8 = (bf16[216,512]{1,0:T(8,128)(2,1)S(1)}, bf16[216,512]{1,0:T(8,128)(2,1)S(1)}, u32[]{:S(2)}, u32[]{:S(2)}) collective-permute-start(bf16[216,512]{1,0:T(8,128)(2,1)S(1)} %broadcast_select_fusion.1), channel_id=1, source_target_pairs={{0,2},{1,3},{2,0},{3,1},{4,6},{5,7},{6,4},{7,5},{8,10},{9,11},{10,... | collective-permute-start | bytes 663560 | tf_op jit(solution)/shard_map/ppermute | solution.py:165
  30.3 1.3 %copy-start.6 = (bf16[216,512]{1,0:T(8,128)(2,1)}, bf16[216,512]{1,0:T(8,128)(2,1)S(1)}, u32[]{:S(2)}) copy-start(bf16[216,512]{1,0:T(8,128)(2,1)S(1)} %collective-permute-done.4.refs_4_) | copy-start | bytes 663556
  30.3 9.1 %collective-permute-start.7 = (bf16[216,512]{1,0:T(8,128)(2,1)S(1)}, bf16[216,512]{1,0:T(8,128)(2,1)S(1)}, u32[]{:S(2)}, u32[]{:S(2)}) collective-permute-start(bf16[216,512]{1,0:T(8,128)(2,1)S(1)} %collective-permute-done.4.refs_4_), channel_id=1, source_target_pairs={{4,0},{5,1},{6,2},{7,3},{8,12},{9,13},{10,14},{11,15},{20,16},{21,... | collective-permute-start | bytes 663560 | tf_op jit(solution)/shard_map/ppermute | solution.py:164
  31.6 0.7 %copy-start.18 = (bf16[216,512]{1,0:T(8,128)(2,1)}, bf16[216,512]{1,0:T(8,128)(2,1)S(1)}, u32[]{:S(2)}) copy-start(bf16[216,512]{1,0:T(8,128)(2,1)S(1)} %collective-permute-done.6.refs_6_) | copy-start | bytes 663556
  38.6 8.7 %copy-start.3 = (f32[7,16,1024]{2,1,0:T(8,128)S(1)}, f32[7,16,1024]{2,1,0:T(8,128)}, u32[]{:S(2)}) copy-start(f32[7,16,1024]{2,1,0:T(8,128)} %shard_map.95) | copy-start | bytes 1376260
  39.4 1.6 %copy-start.5 = (bf16[216,512]{1,0:T(8,128)(2,1)}, bf16[216,512]{1,0:T(8,128)(2,1)S(1)}, u32[]{:S(2)}) copy-start(bf16[216,512]{1,0:T(8,128)(2,1)S(1)} %collective-permute-done.7.refs_0_) | copy-start | bytes 663556
  39.4 6.0 %collective-permute-start.10 = (bf16[216,512]{1,0:T(8,128)(2,1)S(1)}, bf16[216,512]{1,0:T(8,128)(2,1)S(1)}, u32[]{:S(2)}, u32[]{:S(2)}) collective-permute-start(bf16[216,512]{1,0:T(8,128)(2,1)S(1)} %broadcast_select_fusion), channel_id=1, source_target_pairs={{0,2},{1,3},{2,0},{3,1},{4,6},{5,7},{6,4},{7,5},{8,10},{9,11},{10,... | collective-permute-start | bytes 663560 | tf_op jit(solution)/shard_map/ppermute | solution.py:173
  41.0 6.4 %copy-start.15 = (bf16[216,512]{1,0:T(8,128)(2,1)}, bf16[216,512]{1,0:T(8,128)(2,1)S(1)}, u32[]{:S(2)}) copy-start(bf16[216,512]{1,0:T(8,128)(2,1)S(1)} %collective-permute-done.8.refs_1_) | copy-start | bytes 663556
  45.4 2.0 %copy-start.17 = (bf16[216,512]{1,0:T(8,128)(2,1)}, bf16[216,512]{1,0:T(8,128)(2,1)S(1)}, u32[]{:S(2)}) copy-start(bf16[216,512]{1,0:T(8,128)(2,1)S(1)} %collective-permute-done.10.refs_2_) | copy-start | bytes 663556
  51.0 0.9 %slice-start = ((f32[17,512]{1,0:T(8,128)}), f32[16,512]{1,0:T(8,128)S(1)}, s32[]{:S(2)}) async-start(f32[17,512]{1,0:T(8,128)} %copy-done.9), calls=%async_computation | async-start | bytes 65536 | tf_op jit(solution)/shard_map/slice | solution.py:293
  52.0 3.1 %collective-permute-start.13 = (f32[16,16]{1,0:T(8,128)S(1)}, f32[16,16]{1,0:T(8,128)S(1)}, u32[]{:S(2)}, u32[]{:S(2)}) collective-permute-start(f32[16,16]{1,0:T(8,128)S(1)} %fusion.7), channel_id=1, source_target_pairs={{0,3},{1,2},{2,1},{3,0},{4,7},{5,6},{6,5},{7,4},{8,11},{9,10},{10,... | collective-permute-start | bytes 3080 | tf_op jit(solution)/shard_map/ppermute | solution.py:203
  52.0 3.7 %collective-permute-start.14 = (f32[16,16]{1,0:T(8,128)S(1)}, f32[16,16]{1,0:T(8,128)S(1)}, u32[]{:S(2)}, u32[]{:S(2)}) collective-permute-start(f32[16,16]{1,0:T(8,128)S(1)} %fusion.7), channel_id=1, source_target_pairs={{0,2},{1,3},{2,0},{3,1},{4,6},{5,7},{6,4},{7,5},{8,10},{9,11},{10,... | collective-permute-start | bytes 3080 | tf_op jit(solution)/shard_map/ppermute | solution.py:203
  53.6 2.1 %collective-permute-start.15 = (f32[16,16]{1,0:T(8,128)S(1)}, f32[16,16]{1,0:T(8,128)S(1)}, u32[]{:S(2)}, u32[]{:S(2)}) collective-permute-start(f32[16,16]{1,0:T(8,128)S(1)} %fusion.7), channel_id=1, source_target_pairs={{0,1},{1,0},{2,3},{3,2},{4,5},{5,4},{6,7},{7,6},{8,9},{9,8},{10,11... | collective-permute-start | bytes 3080 | tf_op jit(solution)/shard_map/ppermute | solution.py:203
  53.9 6.3 %copy-start.12 = (f32[16,16]{1,0:T(8,128)S(1)}, f32[16,16]{1,0:T(8,128)}, u32[]{:S(2)}) copy-start(f32[16,16]{1,0:T(8,128)} %param.13) | copy-start | bytes 3076
  55.8 6.1 %collective-permute-start.16 = (f32[16,16]{1,0:T(8,128)S(1)}, f32[16,16]{1,0:T(8,128)S(1)}, u32[]{:S(2)}, u32[]{:S(2)}) collective-permute-start(f32[16,16]{1,0:T(8,128)S(1)} %select_add_fusion), channel_id=1, source_target_pairs={{0,4},{1,5},{2,6},{3,7},{4,0},{5,1},{6,2},{7,3},{8,12},{9,13},{10,... | collective-permute-start | bytes 3080 | tf_op jit(solution)/shard_map/ppermute | solution.py:213
  61.9 4.5 %collective-permute-start.17 = (f32[16,16]{1,0:T(8,128)S(1)}, f32[16,16]{1,0:T(8,128)S(1)}, u32[]{:S(2)}, u32[]{:S(2)}) collective-permute-start(f32[16,16]{1,0:T(8,128)S(1)} %add.69), channel_id=1, source_target_pairs={{0,8},{1,9},{2,10},{3,11},{4,12},{5,13},{6,14},{7,15},{8,0},{9,1},... | collective-permute-start | bytes 3080 | tf_op jit(solution)/shard_map/ppermute | solution.py:213
  63.9 3.1 %collective-permute-start.11 = (f32[16,512]{1,0:T(8,128)S(1)}, f32[16,512]{1,0:T(8,128)S(1)}, u32[]{:S(2)}, u32[]{:S(2)}) collective-permute-start(f32[16,512]{1,0:T(8,128)S(1)} %slice.105), channel_id=1, source_target_pairs={{0,1},{1,0},{2,3},{3,2},{4,5},{5,4},{6,7},{7,6},{8,9},{9,8},{10,11... | collective-permute-start | bytes 98312 | tf_op jit(solution)/shard_map/ppermute | solution.py:299
  66.4 0.6 copy-start.10

commit v22 on v19

--- a/solution.py
+++ b/solution.py
@@ -65,12 +65,16 @@
                 )
 
             if split:
-
-                @pl.when(flag_ref[slot] != 0)
+                z = lax.axis_index("row") // 4
+                middle = (z == 1) | (z == 2)
+                keep = [True, True, middle, True, middle, ~middle, True][slot]
+                keep = jnp.asarray(keep)
+
+                @pl.when(keep)
                 def _(term=term, slot=slot):
                     out_ref[slot] = term()
 
-                @pl.when(flag_ref[slot] == 0)
+                @pl.when(jnp.logical_not(keep))
                 def _(slot=slot):
                     out_ref[slot] = jnp.zeros(out_ref.shape[1:], jnp.float32)
 
@@ -255,7 +259,7 @@
     own_terms = ((rows_x * 2).T, norm_rows, recip_rows)
     if chip_split:
         def early_work(first, first_valid):
-            return list_product(first_valid, own_terms, first, width, rows, split=True)
+            return list_product(jnp.ones((len(first),), jnp.int32), own_terms, first, width, rows, split=True)
 
         pieces, valid, origin, early = gather_pieces(packed, early_work)
     else:

time: 67 us -> 66 us (0.985)
  Pallas kernels: 10.6 us -> 9.62 us
  starting transfers between devices: 20.2 us -> 20.9 us
    pallas_call x2, Pallas kernels: 10.6 us -> 9.62 us  [list_product(): pl.pallas_call(functools.partial(list_kernel, width, rows, counts, split)...]
    unnamed x38, local copies, waits for them, and re-layouts: 2.38 us -> 1.64 us
    ppermute x6, starting transfers between devices: 7.08 us -> 7.77 us  [sum_over_rows(): lax.ppermute(value, 'row', [(i, i ^ m << shift) for i in range(devices)])]
  transfers between devices with their start and end apart: 19 -> 19, of which waited for: 8 -> 7; matrix products, arithmetic and copies ran while one was open for 7% -> 8% of each run, Pallas kernels for 9% -> 9%
where the time goes in v22:
time: 66 us; the launch traced here: 65.5 us
  waiting for transfers between devices  22.1 us (33%)
  starting transfers between devices  20.9 us (32%)
  Pallas kernels  9.62 us (15%)
  local copies, waits for them, and re-layouts  6.04 us (9%)
  other arithmetic  4.52 us (7%)
  between operations  1.79 us (3%)
    ppermute x1, waiting for transfers between devices, gather_pieces(): out2 = lax.ppermute(inner1, 'row', outward)  9.68 us
    pallas_call x2, Pallas kernels, list_product(): pl.pallas_call(functools.partial(list_kernel, width, rows, counts, split)...  9.62 us
    ppermute x6, starting transfers between devices, sum_over_rows(): lax.ppermute(value, 'row', [(i, i ^ m << shift) for i in range(devices)])  7.77 us
    ppermute x6, waiting for transfers between devices, sum_over_rows(): lax.ppermute(value, 'row', [(i, i ^ m << shift) for i in range(devices)])  5.46 us
    ppermute x1, waiting for transfers between devices, gather_pieces(): across4 = lax.ppermute(last, 'row', across)  4.37 us
    ppermute x1, starting transfers between devices, gather_pieces(): swap1 = lax.ppermute(packed, 'row', pairs_swap)  3.09 us
    ppermute x1, waiting for transfers between devices, gather_pieces(): swap1 = lax.ppermute(packed, 'row', pairs_swap)  2.6 us
    ppermute x1, starting transfers between devices, gather_pieces(): across2 = lax.ppermute(swap1, 'row', across)  1.75 us
  transfers between devices with their start and end apart: 19, of which 7 were waited for; matrix products, arithmetic and copies ran while one was open for 8% of the time, Pallas kernels for 9%

profile of v22, /device:TPU:0, one launch (start us, length us, event | category | flops | bytes accessed | tf_op | source)
XLA Modules:
  0.0 65.5 jit_solution(6399486652115107995)
XLA Ops:
  0.7 0.7 %convert.8 = bf16[4,2]{0,1:T(2,128)(2,1)S(1)} convert(s32[4,2]{0,1:T(2,128)} %param.14) | non-fusion elementwise | flops 8 | bytes 48 | tf_op jit(solution)/shard_map/convert.3
  1.4 0.1 copy.26
  2.3 0.5 collective-permute-start
  2.8 0.8 %pad_maximum_fusion.1 = f32[17,512]{1,0:T(8,128)S(1)} fusion(f32[1,512]{1,0:T(1,128)S(1)} %bitcast.62, f32[16,512]{1,0:T(8,128)} %param.11), kind=kLoop, calls=%fused_computation.19 | loop fusion | flops 8704 | bytes 69632 | tf_op jit(solution)/shard_map/concatenate | solution.py:250
  3.9 0.5 copy-done.12
  4.4 0.1 fusion.25
  4.6 0.1 stack.54
  4.8 3.1 %collective-permute-start.1 = (bf16[216,512]{1,0:T(8,128)(2,1)S(1)}, bf16[216,512]{1,0:T(8,128)(2,1)S(1)}, u32[]{:S(2)}, u32[]{:S(2)}) collective-permute-start(bf16[216,512]{1,0:T(8,128)(2,1)S(1)} %fusion.6.refs_0_), channel_id=1, source_target_pairs={{0,4},{1,5},{2,6},{3,7},{4,0},{5,1},{6,2},{7,3},{8,12},{9,13},{10,... | collective-permute-start | bytes 663560 | tf_op jit(solution)/shard_map/ppermute | solution.py:161
  7.9 0.7 %collective-permute-start.2 = (bf16[216,512]{1,0:T(8,128)(2,1)S(1)}, bf16[216,512]{1,0:T(8,128)(2,1)S(1)}, u32[]{:S(2)}, u32[]{:S(2)}) collective-permute-start(bf16[216,512]{1,0:T(8,128)(2,1)S(1)} %fusion.6.refs_0_), channel_id=1, source_target_pairs={{4,8},{5,9},{6,10},{7,11},{8,4},{9,5},{10,6},{11,7},{20,24},{21,25... | collective-permute-start | bytes 663560 | tf_op jit(solution)/shard_map/ppermute | solution.py:162
  8.7 1.6 %collective-permute-start.3 = (bf16[216,512]{1,0:T(8,128)(2,1)S(1)}, bf16[216,512]{1,0:T(8,128)(2,1)S(1)}, u32[]{:S(2)}, u32[]{:S(2)}) collective-permute-start(bf16[216,512]{1,0:T(8,128)(2,1)S(1)} %fusion.6.refs_0_), channel_id=1, source_target_pairs={{0,2},{1,3},{2,0},{3,1},{4,6},{5,7},{6,4},{7,5},{8,10},{9,11},{10,... | collective-permute-start | bytes 663560 | tf_op jit(solution)/shard_map/ppermute | solution.py:163
  10.3 0.6 copy-done.9
  10.9 2.6 %collective-permute-done.1.refs_1_ = bf16[216,512]{1,0:T(8,128)(2,1)S(1)} collective-permute-done((bf16[216,512]{1,0:T(8,128)(2,1)S(1)}, bf16[216,512]{1,0:T(8,128)(2,1)S(1)}, u32[]{:S(2)}, u32[]{:S(2)}) %collective-permute-start.1) | collective-permute-done | bytes 221216 | tf_op jit(solution)/shard_map/ppermute | solution.py:161
  13.5 0.7 %collective-permute-start.4 = (bf16[216,512]{1,0:T(8,128)(2,1)S(1)}, bf16[216,512]{1,0:T(8,128)(2,1)S(1)}, u32[]{:S(2)}, u32[]{:S(2)}) collective-permute-start(bf16[216,512]{1,0:T(8,128)(2,1)S(1)} %collective-permute-done.1.refs_1_), channel_id=1, source_target_pairs={{4,8},{5,9},{6,10},{7,11},{8,4},{9,5},{10,6},{11,7},{20,24},{21,25... | collective-permute-start | bytes 663560 | tf_op jit(solution)/shard_map/ppermute | solution.py:165
  14.2 1.7 %collective-permute-start.6 = (bf16[216,512]{1,0:T(8,128)(2,1)S(1)}, bf16[216,512]{1,0:T(8,128)(2,1)S(1)}, u32[]{:S(2)}, u32[]{:S(2)}) collective-permute-start(bf16[216,512]{1,0:T(8,128)(2,1)S(1)} %collective-permute-done.1.refs_1_), channel_id=1, source_target_pairs={{0,2},{1,3},{2,0},{3,1},{4,6},{5,7},{6,4},{7,5},{8,10},{9,11},{10,... | collective-permute-start | bytes 663560 | tf_op jit(solution)/shard_map/ppermute | solution.py:167
  16.0 0.1 multiply_reduce_fusion
  16.2 1.3 %collective-permute-start.5 = (bf16[216,512]{1,0:T(8,128)(2,1)S(1)}, bf16[216,512]{1,0:T(8,128)(2,1)S(1)}, u32[]{:S(2)}, u32[]{:S(2)}) collective-permute-start(bf16[216,512]{1,0:T(8,128)(2,1)S(1)} %collective-permute-done.2.refs_2_), channel_id=1, source_target_pairs={{4,0},{5,1},{6,2},{7,3},{8,12},{9,13},{10,14},{11,15},{20,16},{21,... | collective-permute-start | bytes 663560 | tf_op jit(solution)/shard_map/ppermute | solution.py:166
  17.5 1.0 %copy.27.xo_ref = bf16[1024,192]{1,0:T(8,128)(2,1)} copy(bf16[1024,192]{0,1:T(8,128)(2,1)S(1)} %multiply_bitcast_fusion) | data formatting | bytes 786432 | tf_op jit(solution)/shard_map/transpose | solution.py:259
  18.5 0.7 %maximum_maximum_fusion.terms_ref = f32[8,1024]{1,0:T(8,128)} fusion(f32[1,1024]{1,0:T(1,128)S(1)} %fusion.16, f32[1,1024]{1,0:T(1,128)S(1)} %bitcast.63, f32[8]{0:T(128)S(1)} %pad.18.clone), kind=kLoop, calls=%fused_computation.24 | loop fusion | flops 16384 | bytes 40992 | tf_op jit(solution)/shard_map/concatenate | solution.py:96
  19.3 9.7 %collective-permute-done.5.refs_5_ = bf16[216,512]{1,0:T(8,128)(2,1)S(1)} collective-permute-done((bf16[216,512]{1,0:T(8,128)(2,1)S(1)}, bf16[216,512]{1,0:T(8,128)(2,1)S(1)}, u32[]{:S(2)}, u32[]{:S(2)}) %collective-permute-start.5) | collective-permute-done | bytes 221216 | tf_op jit(solution)/shard_map/ppermute | solution.py:166
  29.0 0.6 collective-permute-start.8
  29.6 1.3 %collective-permute-start.7 = (bf16[216,512]{1,0:T(8,128)(2,1)S(1)}, bf16[216,512]{1,0:T(8,128)(2,1)S(1)}, u32[]{:S(2)}, u32[]{:S(2)}) collective-permute-start(bf16[216,512]{1,0:T(8,128)(2,1)S(1)} %collective-permute-done.4.refs_4_), channel_id=1, source_target_pairs={{4,0},{5,1},{6,2},{7,3},{8,12},{9,13},{10,14},{11,15},{20,16},{21,... | collective-permute-start | bytes 663560 | tf_op jit(solution)/shard_map/ppermute | solution.py:168
  30.9 0.6 broadcast_13_flag_ref.2.flag_ref
  31.5 0.1 copy-done.18
  31.6 6.0 %shard_map.95 = f32[7,16,1024]{2,1,0:T(8,128)} custom-call(s32[7]{0:T(128)} %broadcast_13_flag_ref.2.flag_ref, bf16[1024,192]{1,0:T(8,128)(2,1)} %copy.27.xo_ref, f32[8,1024]{1,0:T(8,128)} %maximum_maximum_fusion.terms_ref, bf16[216,512]{1,0:T(8,128)(2,1)} %copy-done.8, bf16[216,512]{1,0:T(8,128)(2,1)} %copy-done.14, bf16[216,512]{1,0:T(8,128)(2,1)} %copy-done.4, ...), custom_call_target="tpu_custom_call" | custom-call | flops 1526726656 | bytes 2007040 | tf_op jit(solution)/shard_map/pallas_call | solution.py:106
  37.6 0.7 %slice_bitcast_fusion.3 = bf16[1,18]{1,0:T(2,128)(2,1)S(1)} fusion(bf16[1,216,512]{2,1,0:T(8,128)(2,1)} %bitcast.70), kind=kLoop, calls=%fused_computation.50 | loop fusion | bytes 72 | tf_op jit(solution)/shard_map/squeeze | solution.py:270
  38.4 1.6 %collective-permute-start.10 = (bf16[216,512]{1,0:T(8,128)(2,1)S(1)}, bf16[216,512]{1,0:T(8,128)(2,1)S(1)}, u32[]{:S(2)}, u32[]{:S(2)}) collective-permute-start(bf16[216,512]{1,0:T(8,128)(2,1)S(1)} %broadcast_select_fusion), channel_id=1, source_target_pairs={{0,2},{1,3},{2,0},{3,1},{4,6},{5,7},{6,4},{7,5},{8,10},{9,11},{10,... | collective-permute-start | bytes 663560 | tf_op jit(solution)/shard_map/ppermute | solution.py:177
  40.0 4.4 %collective-permute-done.10.refs_2_ = bf16[216,512]{1,0:T(8,128)(2,1)S(1)} collective-permute-done((bf16[216,512]{1,0:T(8,128)(2,1)S(1)}, bf16[216,512]{1,0:T(8,128)(2,1)S(1)}, u32[]{:S(2)}, u32[]{:S(2)}) %collective-permute-start.10) | collective-permute-done | bytes 221216 | tf_op jit(solution)/shard_map/ppermute | solution.py:177
  44.5 0.2 slice_reduce_fusion
  44.8 0.1 copy.29
  44.9 0.1 broadcast_in_dim_reshape_squeeze.4
  45.3 0.1 lt.26
  45.4 0.2 and_reduce_fusion
  45.6 0.6 slice.82.flag_ref
  46.2 0.1 select_reduce_fusion
  46.3 3.6 %shard_map.96 = f32[16,1024]{1,0:T(8,128)} custom-call(s32[3]{0:T(128)} %slice.82.flag_ref, bf16[1024,192]{1,0:T(8,128)(2,1)} %copy.27.xo_ref, f32[8,1024]{1,0:T(8,128)} %maximum_maximum_fusion.terms_ref, bf16[216,512]{1,0:T(8,128)(2,1)} %copy-done.5, bf16[216,512]{1,0:T(8,128)(2,1)} %copy-done.15, bf16[216,512]{1,0:T(8,128)(2,1)} %copy-done.17), custom_call_target="tpu_custom_call" | custom-call | flops 654311424 | bytes 729088 | tf_op jit(solution)/shard_map/pallas_call | solution.py:106
  49.9 0.9 %add.67 = f32[16,1024]{1,0:T(8,128)S(1)} add(f32[16,1024]{1,0:T(8,128)} %shard_map.96, f32[16,1024]{1,0:T(8,128)S(1)} %select_reduce_fusion) | non-fusion elementwise | flops 16384 | bytes 196608 | tf_op jit(solution)/shard_map/add | solution.py:292
  50.8 0.2 fusion.7
  51.0 1.6 %collective-permute-start.14 = (f32[16,16]{1,0:T(8,128)S(1)}, f32[16,16]{1,0:T(8,128)S(1)}, u32[]{:S(2)}, u32[]{:S(2)}) collective-permute-start(f32[16,16]{1,0:T(8,128)S(1)} %fusion.7), channel_id=1, source_target_pairs={{0,2},{1,3},{2,0},{3,1},{4,6},{5,7},{6,4},{7,5},{8,10},{9,11},{10,... | collective-permute-start | bytes 3080 | tf_op jit(solution)/shard_map/ppermute | solution.py:208
  52.6 0.3 collective-permute-start.15
  52.9 1.2 %collective-permute-done.13 = f32[16,16]{1,0:T(8,128)S(1)} collective-permute-done((f32[16,16]{1,0:T(8,128)S(1)}, f32[16,16]{1,0:T(8,128)S(1)}, u32[]{:S(2)}, u32[]{:S(2)}) %collective-permute-start.13) | collective-permute-done | bytes 1056 | tf_op jit(solution)/shard_map/ppermute | solution.py:208
  54.1 0.6 collective-permute-done.14
  54.7 2.3 %collective-permute-start.16 = (f32[16,16]{1,0:T(8,128)S(1)}, f32[16,16]{1,0:T(8,128)S(1)}, u32[]{:S(2)}, u32[]{:S(2)}) collective-permute-start(f32[16,16]{1,0:T(8,128)S(1)} %select_add_fusion), channel_id=1, source_target_pairs={{0,12},{1,13},{2,14},{3,15},{4,8},{5,9},{6,10},{7,11},{8,4},{9,5},... | collective-permute-start | bytes 3080 | tf_op jit(solution)/shard_map/ppermute | solution.py:208
  57.0 3.6 %collective-permute-start.17 = (f32[16,16]{1,0:T(8,128)S(1)}, f32[16,16]{1,0:T(8,128)S(1)}, u32[]{:S(2)}, u32[]{:S(2)}) collective-permute-start(f32[16,16]{1,0:T(8,128)S(1)} %select_add_fusion), channel_id=1, source_target_pairs={{0,8},{1,9},{2,10},{3,11},{4,12},{5,13},{6,14},{7,15},{8,0},{9,1},... | collective-permute-start | bytes 3080 | tf_op jit(solution)/shard_map/ppermute | solution.py:208
  60.6 1.7 %collective-permute-done.17 = f32[16,16]{1,0:T(8,128)S(1)} collective-permute-done((f32[16,16]{1,0:T(8,128)S(1)}, f32[16,16]{1,0:T(8,128)S(1)}, u32[]{:S(2)}, u32[]{:S(2)}) %collective-permute-start.17) | collective-permute-done | bytes 1056 | tf_op jit(solution)/shard_map/ppermute | solution.py:208
  62.3 1.9 %collective-permute-done.18 = f32[16,16]{1,0:T(8,128)S(1)} collective-permute-done((f32[16,16]{1,0:T(8,128)S(1)}, f32[16,16]{1,0:T(8,128)S(1)}, u32[]{:S(2)}, u32[]{:S(2)}) %collective-permute-start.18) | collective-permute-done | bytes 1056 | tf_op jit(solution)/shard_map/ppermute | solution.py:208
  64.3 0.2 fusion.24
  64.5 0.4 copy-done.10
  64.9 0.6 fusion.14
  (98 shorter events, 1.5 us)
Async XLA Ops:
  0.6 3.3 %copy-start = (f32[16,512]{1,0:T(8,128)S(1)}, f32[16,512]{1,0:T(8,128)}, u32[]{:S(2)}) copy-start(f32[16,512]{1,0:T(8,128)} %param.12) | copy-start | bytes 98308
  0.6 2.1 %copy-start.11 = (f32[512]{0:T(512)S(1)}, f32[512]{0:T(512)}, u32[]{:S(2)}) copy-start(f32[512]{0:T(512)} %param.10) | copy-start | bytes 6148
  1.4 2.2 %copy-start.2 = (f32[16,512]{1,0:T(8,128)S(1)}, f32[16,512]{1,0:T(8,128)}, u32[]{:S(2)}) copy-start(f32[16,512]{1,0:T(8,128)} %param.11) | copy-start | bytes 98308
  1.4 2.3 %copy-start.13 = (bf16[512]{0:T(512)(128)(2,1)S(1)}, bf16[512]{0:T(512)(128)(2,1)}, u32[]{:S(2)}) copy-start(bf16[512]{0:T(512)(128)(2,1)} %param.9) | copy-start | bytes 3076
  1.5 3.3 %copy-start.1 = (bf16[192,512]{1,0:T(8,128)(2,1)S(1)}, bf16[192,512]{1,0:T(8,128)(2,1)}, u32[]{:S(2)}) copy-start(bf16[192,512]{1,0:T(8,128)(2,1)} %param.8) | copy-start | bytes 589828
  2.3 2.4 %collective-permute-start = (bf16[9]{0:T(256)(128)(2,1)S(1)}, bf16[9]{0:T(256)(128)(2,1)S(1)}, u32[]{:S(2)}, u32[]{:S(2)}) collective-permute-start(bf16[9]{0:T(256)(128)(2,1)S(1)} %pad_maximum_fusion.2), channel_id=1, source_target_pairs={{0,1},{1,0},{2,3},{3,2},{4,5},{5,4},{6,7},{7,6},{8,9},{9,8},{10,11... | collective-permute-start | bytes 62 | tf_op jit(solution)/shard_map/ppermute | solution.py:240
  3.5 6.7 %collective-permute-start.12 = (f32[17,512]{1,0:T(8,128)S(1)}, f32[17,512]{1,0:T(8,128)S(1)}, u32[]{:S(2)}, u32[]{:S(2)}) collective-permute-start(f32[17,512]{1,0:T(8,128)S(1)} %pad_maximum_fusion.1), channel_id=1, source_target_pairs={{0,1},{1,0},{2,3},{3,2},{4,5},{5,4},{6,7},{7,6},{8,9},{9,8},{10,11... | collective-permute-start | bytes 104456 | tf_op jit(solution)/shard_map/ppermute | solution.py:249
  3.7 0.7 %copy-start.12 = (f32[16,16]{1,0:T(8,128)S(1)}, f32[16,16]{1,0:T(8,128)}, u32[]{:S(2)}) copy-start(f32[16,16]{1,0:T(8,128)} %param.13) | copy-start | bytes 3076
  4.8 5.5 %copy-start.8 = (bf16[216,512]{1,0:T(8,128)(2,1)}, bf16[216,512]{1,0:T(8,128)(2,1)S(1)}, u32[]{:S(2)}) copy-start(bf16[216,512]{1,0:T(8,128)(2,1)S(1)} %fusion.6.refs_0_) | copy-start | bytes 663556
  4.8 8.7 %collective-permute-start.1 = (bf16[216,512]{1,0:T(8,128)(2,1)S(1)}, bf16[216,512]{1,0:T(8,128)(2,1)S(1)}, u32[]{:S(2)}, u32[]{:S(2)}) collective-permute-start(bf16[216,512]{1,0:T(8,128)(2,1)S(1)} %fusion.6.refs_0_), channel_id=1, source_target_pairs={{0,4},{1,5},{2,6},{3,7},{4,0},{5,1},{6,2},{7,3},{8,12},{9,13},{10,... | collective-permute-start | bytes 663560 | tf_op jit(solution)/shard_map/ppermute | solution.py:161
  7.9 5.6 %collective-permute-start.2 = (bf16[216,512]{1,0:T(8,128)(2,1)S(1)}, bf16[216,512]{1,0:T(8,128)(2,1)S(1)}, u32[]{:S(2)}, u32[]{:S(2)}) collective-permute-start(bf16[216,512]{1,0:T(8,128)(2,1)S(1)} %fusion.6.refs_0_), channel_id=1, source_target_pairs={{4,8},{5,9},{6,10},{7,11},{8,4},{9,5},{10,6},{11,7},{20,24},{21,25... | collective-permute-start | bytes 663560 | tf_op jit(solution)/shard_map/ppermute | solution.py:162
  8.6 7.4 %collective-permute-start.9 = (bf16[216,512]{1,0:T(8,128)(2,1)S(1)}, bf16[216,512]{1,0:T(8,128)(2,1)S(1)}, u32[]{:S(2)}, u32[]{:S(2)}) collective-permute-start(bf16[216,512]{1,0:T(8,128)(2,1)S(1)} %fusion.6.refs_0_), channel_id=1, source_target_pairs={{0,1},{1,0},{2,3},{3,2},{4,5},{5,4},{6,7},{7,6},{8,9},{9,8},{10,11... | collective-permute-start | bytes 663560 | tf_op jit(solution)/shard_map/ppermute | solution.py:248
  8.7 10.6 %collective-permute-start.3 = (bf16[216,512]{1,0:T(8,128)(2,1)S(1)}, bf16[216,512]{1,0:T(8,128)(2,1)S(1)}, u32[]{:S(2)}, u32[]{:S(2)}) collective-permute-start(bf16[216,512]{1,0:T(8,128)(2,1)S(1)} %fusion.6.refs_0_), channel_id=1, source_target_pairs={{0,2},{1,3},{2,0},{3,1},{4,6},{5,7},{6,4},{7,5},{8,10},{9,11},{10,... | collective-permute-start | bytes 663560 | tf_op jit(solution)/shard_map/ppermute | solution.py:163
  10.3 0.6 copy-start.9
  13.5 5.7 %copy-start.14 = (bf16[216,512]{1,0:T(8,128)(2,1)}, bf16[216,512]{1,0:T(8,128)(2,1)S(1)}, u32[]{:S(2)}) copy-start(bf16[216,512]{1,0:T(8,128)(2,1)S(1)} %collective-permute-done.1.refs_1_) | copy-start | bytes 663556
  13.5 15.4 %copy-start.4 = (bf16[216,512]{1,0:T(8,128)(2,1)}, bf16[216,512]{1,0:T(8,128)(2,1)S(1)}, u32[]{:S(2)}) copy-start(bf16[216,512]{1,0:T(8,128)(2,1)S(1)} %collective-permute-done.2.refs_2_) | copy-start | bytes 663556
  13.5 16.0 %collective-permute-start.4 = (bf16[216,512]{1,0:T(8,128)(2,1)S(1)}, bf16[216,512]{1,0:T(8,128)(2,1)S(1)}, u32[]{:S(2)}, u32[]{:S(2)}) collective-permute-start(bf16[216,512]{1,0:T(8,128)(2,1)S(1)} %collective-permute-done.1.refs_1_), channel_id=1, source_target_pairs={{4,8},{5,9},{6,10},{7,11},{8,4},{9,5},{10,6},{11,7},{20,24},{21,25... | collective-permute-start | bytes 663560 | tf_op jit(solution)/shard_map/ppermute | solution.py:165
  14.2 16.7 %collective-permute-start.6 = (bf16[216,512]{1,0:T(8,128)(2,1)S(1)}, bf16[216,512]{1,0:T(8,128)(2,1)S(1)}, u32[]{:S(2)}, u32[]{:S(2)}) collective-permute-start(bf16[216,512]{1,0:T(8,128)(2,1)S(1)} %collective-permute-done.1.refs_1_), channel_id=1, source_target_pairs={{0,2},{1,3},{2,0},{3,1},{4,6},{5,7},{6,4},{7,5},{8,10},{9,11},{10,... | collective-permute-start | bytes 663560 | tf_op jit(solution)/shard_map/ppermute | solution.py:167
  16.2 12.7 %collective-permute-start.5 = (bf16[216,512]{1,0:T(8,128)(2,1)S(1)}, bf16[216,512]{1,0:T(8,128)(2,1)S(1)}, u32[]{:S(2)}, u32[]{:S(2)}) collective-permute-start(bf16[216,512]{1,0:T(8,128)(2,1)S(1)} %collective-permute-done.2.refs_2_), channel_id=1, source_target_pairs={{4,0},{5,1},{6,2},{7,3},{8,12},{9,13},{10,14},{11,15},{20,16},{21,... | collective-permute-start | bytes 663560 | tf_op jit(solution)/shard_map/ppermute | solution.py:166
  19.2 9.7 %copy-start.16 = (bf16[216,512]{1,0:T(8,128)(2,1)}, bf16[216,512]{1,0:T(8,128)(2,1)S(1)}, u32[]{:S(2)}) copy-start(bf16[216,512]{1,0:T(8,128)(2,1)S(1)} %collective-permute-done.3.refs_3_) | copy-start | bytes 663556
  28.9 1.9 %copy-start.7 = (bf16[216,512]{1,0:T(8,128)(2,1)}, bf16[216,512]{1,0:T(8,128)(2,1)S(1)}, u32[]{:S(2)}) copy-start(bf16[216,512]{1,0:T(8,128)(2,1)S(1)} %collective-permute-done.5.refs_5_) | copy-start | bytes 663556
  29.0 11.0 %collective-permute-start.8 = (bf16[216,512]{1,0:T(8,128)(2,1)S(1)}, bf16[216,512]{1,0:T(8,128)(2,1)S(1)}, u32[]{:S(2)}, u32[]{:S(2)}) collective-permute-start(bf16[216,512]{1,0:T(8,128)(2,1)S(1)} %broadcast_select_fusion.1), channel_id=1, source_target_pairs={{0,2},{1,3},{2,0},{3,1},{4,6},{5,7},{6,4},{7,5},{8,10},{9,11},{10,... | collective-permute-start | bytes 663560 | tf_op jit(solution)/shard_map/ppermute | solution.py:169
  29.6 1.9 %copy-start.6 = (bf16[216,512]{1,0:T(8,128)(2,1)}, bf16[216,512]{1,0:T(8,128)(2,1)S(1)}, u32[]{:S(2)}) copy-start(bf16[216,512]{1,0:T(8,128)(2,1)S(1)} %collective-permute-done.4.refs_4_) | copy-start | bytes 663556
  29.6 8.8 %collective-permute-start.7 = (bf16[216,512]{1,0:T(8,128)(2,1)S(1)}, bf16[216,512]{1,0:T(8,128)(2,1)S(1)}, u32[]{:S(2)}, u32[]{:S(2)}) collective-permute-start(bf16[216,512]{1,0:T(8,128)(2,1)S(1)} %collective-permute-done.4.refs_4_), channel_id=1, source_target_pairs={{4,0},{5,1},{6,2},{7,3},{8,12},{9,13},{10,14},{11,15},{20,16},{21,... | collective-permute-start | bytes 663560 | tf_op jit(solution)/shard_map/ppermute | solution.py:168
  30.9 0.7 %copy-start.18 = (bf16[216,512]{1,0:T(8,128)(2,1)}, bf16[216,512]{1,0:T(8,128)(2,1)S(1)}, u32[]{:S(2)}) copy-start(bf16[216,512]{1,0:T(8,128)(2,1)S(1)} %collective-permute-done.6.refs_6_) | copy-start | bytes 663556
  37.6 8.6 %copy-start.3 = (f32[7,16,1024]{2,1,0:T(8,128)S(1)}, f32[7,16,1024]{2,1,0:T(8,128)}, u32[]{:S(2)}) copy-start(f32[7,16,1024]{2,1,0:T(8,128)} %shard_map.95) | copy-start | bytes 1376260
  38.4 1.6 %copy-start.5 = (bf16[216,512]{1,0:T(8,128)(2,1)}, bf16[216,512]{1,0:T(8,128)(2,1)S(1)}, u32[]{:S(2)}) copy-start(bf16[216,512]{1,0:T(8,128)(2,1)S(1)} %collective-permute-done.7.refs_0_) | copy-start | bytes 663556
  38.4 6.0 %collective-permute-start.10 = (bf16[216,512]{1,0:T(8,128)(2,1)S(1)}, bf16[216,512]{1,0:T(8,128)(2,1)S(1)}, u32[]{:S(2)}, u32[]{:S(2)}) collective-permute-start(bf16[216,512]{1,0:T(8,128)(2,1)S(1)} %broadcast_select_fusion), channel_id=1, source_target_pairs={{0,2},{1,3},{2,0},{3,1},{4,6},{5,7},{6,4},{7,5},{8,10},{9,11},{10,... | collective-permute-start | bytes 663560 | tf_op jit(solution)/shard_map/ppermute | solution.py:177
  40.0 6.3 %copy-start.15 = (bf16[216,512]{1,0:T(8,128)(2,1)}, bf16[216,512]{1,0:T(8,128)(2,1)S(1)}, u32[]{:S(2)}) copy-start(bf16[216,512]{1,0:T(8,128)(2,1)S(1)} %collective-permute-done.8.refs_1_) | copy-start | bytes 663556
  44.4 1.9 %copy-start.17 = (bf16[216,512]{1,0:T(8,128)(2,1)}, bf16[216,512]{1,0:T(8,128)(2,1)S(1)}, u32[]{:S(2)}) copy-start(bf16[216,512]{1,0:T(8,128)(2,1)S(1)} %collective-permute-done.10.refs_2_) | copy-start | bytes 663556
  49.9 0.9 %slice-start = ((f32[17,512]{1,0:T(8,128)}), f32[16,512]{1,0:T(8,128)S(1)}, s32[]{:S(2)}) async-start(f32[17,512]{1,0:T(8,128)} %copy-done.9), calls=%async_computation | async-start | bytes 65536 | tf_op jit(solution)/shard_map/slice | solution.py:296
  51.0 3.1 %collective-permute-start.13 = (f32[16,16]{1,0:T(8,128)S(1)}, f32[16,16]{1,0:T(8,128)S(1)}, u32[]{:S(2)}, u32[]{:S(2)}) collective-permute-start(f32[16,16]{1,0:T(8,128)S(1)} %fusion.7), channel_id=1, source_target_pairs={{0,3},{1,2},{2,1},{3,0},{4,7},{5,6},{6,5},{7,4},{8,11},{9,10},{10,... | collective-permute-start | bytes 3080 | tf_op jit(solution)/shard_map/ppermute | solution.py:208
  51.0 3.7 %collective-permute-start.14 = (f32[16,16]{1,0:T(8,128)S(1)}, f32[16,16]{1,0:T(8,128)S(1)}, u32[]{:S(2)}, u32[]{:S(2)}) collective-permute-start(f32[16,16]{1,0:T(8,128)S(1)} %fusion.7), channel_id=1, source_target_pairs={{0,2},{1,3},{2,0},{3,1},{4,6},{5,7},{6,4},{7,5},{8,10},{9,11},{10,... | collective-permute-start | bytes 3080 | tf_op jit(solution)/shard_map/ppermute | solution.py:208
  52.6 2.1 %collective-permute-start.15 = (f32[16,16]{1,0:T(8,128)S(1)}, f32[16,16]{1,0:T(8,128)S(1)}, u32[]{:S(2)}, u32[]{:S(2)}) collective-permute-start(f32[16,16]{1,0:T(8,128)S(1)} %fusion.7), channel_id=1, source_target_pairs={{0,1},{1,0},{2,3},{3,2},{4,5},{5,4},{6,7},{7,6},{8,9},{9,8},{10,11... | collective-permute-start | bytes 3080 | tf_op jit(solution)/shard_map/ppermute | solution.py:208
  54.7 5.9 %collective-permute-start.16 = (f32[16,16]{1,0:T(8,128)S(1)}, f32[16,16]{1,0:T(8,128)S(1)}, u32[]{:S(2)}, u32[]{:S(2)}) collective-permute-start(f32[16,16]{1,0:T(8,128)S(1)} %select_add_fusion), channel_id=1, source_target_pairs={{0,12},{1,13},{2,14},{3,15},{4,8},{5,9},{6,10},{7,11},{8,4},{9,5},... | collective-permute-start | bytes 3080 | tf_op jit(solution)/shard_map/ppermute | solution.py:208
  57.0 5.3 %collective-permute-start.17 = (f32[16,16]{1,0:T(8,128)S(1)}, f32[16,16]{1,0:T(8,128)S(1)}, u32[]{:S(2)}, u32[]{:S(2)}) collective-permute-start(f32[16,16]{1,0:T(8,128)S(1)} %select_add_fusion), channel_id=1, source_target_pairs={{0,8},{1,9},{2,10},{3,11},{4,12},{5,13},{6,14},{7,15},{8,0},{9,1},... | collective-permute-start | bytes 3080 | tf_op jit(solution)/shard_map/ppermute | solution.py:208
  60.6 3.7 %collective-permute-start.18 = (f32[16,16]{1,0:T(8,128)S(1)}, f32[16,16]{1,0:T(8,128)S(1)}, u32[]{:S(2)}, u32[]{:S(2)}) collective-permute-start(f32[16,16]{1,0:T(8,128)S(1)} %select_add_fusion), channel_id=1, source_target_pairs={{0,4},{1,5},{2,6},{3,7},{4,0},{5,1},{6,2},{7,3},{8,12},{9,13},{10,... | collective-permute-start | bytes 3080 | tf_op jit(solution)/shard_map/ppermute | solution.py:208
  60.6 4.3 %collective-permute-start.11 = (f32[16,512]{1,0:T(8,128)S(1)}, f32[16,512]{1,0:T(8,128)S(1)}, u32[]{:S(2)}, u32[]{:S(2)}) collective-permute-start(f32[16,512]{1,0:T(8,128)S(1)} %slice.105), channel_id=1, source_target_pairs={{0,1},{1,0},{2,3},{3,2},{4,5},{5,4},{6,7},{7,6},{8,9},{9,8},{10,11... | collective-permute-start | bytes 98312 | tf_op jit(solution)/shard_map/ppermute | solution.py:302
  64.3 0.6 copy-start.10

commit v23 on v22

--- a/solution.py
+++ b/solution.py
@@ -45,13 +45,13 @@
             )
 
 
-def list_kernel(width, rows, counts, split, flag_ref, xo_ref, terms_ref, *refs):
+def list_kernel(width, rows, counts, split, offset, flag_ref, xo_ref, terms_ref, *refs):
     out_ref = refs[-1]
     row_terms = jnp.transpose(terms_ref[...])
     norm_rows, recip_rows = row_terms[:, 0:1], row_terms[:, 1:2]
     if not split:
         out_ref[...] = jnp.zeros_like(out_ref)
-    slot = 0
+    slot = offset
     for ref, count in zip(refs[:-1], counts):
         for k in range(count):
             base = k * rows
@@ -67,16 +67,16 @@
             if split:
                 z = lax.axis_index("row") // 4
                 middle = (z == 1) | (z == 2)
-                keep = [True, True, middle, True, middle, ~middle, True][slot]
+                keep = [True, True, middle, True, middle, ~middle, True][slot - offset]
                 keep = jnp.asarray(keep)
 
                 @pl.when(keep)
                 def _(term=term, slot=slot):
-                    out_ref[slot] = term()
+                    out_ref[slot - offset] = term()
 
                 @pl.when(jnp.logical_not(keep))
                 def _(slot=slot):
-                    out_ref[slot] = jnp.zeros(out_ref.shape[1:], jnp.float32)
+                    out_ref[slot - offset] = jnp.zeros(out_ref.shape[1:], jnp.float32)
 
             else:
 
@@ -87,7 +87,7 @@
             slot += 1
 
 
-def list_product(flags, own_terms, pieces, width, rows, split=False):
+def list_product(flags, own_terms, pieces, width, rows, split=False, offset=0):
     twice_own_t, norm_own, recip_own = own_terms
     own = twice_own_t.shape[0]
     counts = [p.shape[0] // rows for p in pieces]
@@ -104,7 +104,7 @@
         bytes_accessed=sum(p.size * 2 for p in pieces) + int(math.prod(shape)) * 4,
     )
     return pl.pallas_call(
-        functools.partial(list_kernel, width, rows, counts, split),
+        functools.partial(list_kernel, width, rows, counts, split, offset),
         cost_estimate=cost,
         in_specs=[pl.BlockSpec(memory_space=pltpu.SMEM)] + [vmem] * (2 + len(pieces)),
         out_specs=vmem,
@@ -288,7 +288,7 @@
 
     if chip_split:
         head = early.shape[0]
-        summed = list_product(flags[head:], own_terms, pieces[head:], width, rows)
+        summed = list_product(flags, own_terms, pieces[head:], width, rows, offset=head)
         summed = summed + jnp.sum(jnp.where(flags[:head, None, None] != 0, early, 0.0), axis=0)
     else:
         summed = own_rows_product(flags, own_terms, pieces[0].reshape(devices, rows, own), width)

time: 66 us -> 65.5 us (level)
  starting transfers between devices: 20.9 us -> 21.8 us
  Pallas kernels: 9.62 us -> 8.89 us
    ppermute x6, starting transfers between devices: 7.77 us -> 8.73 us  [sum_over_rows(): lax.ppermute(value, 'row', [(i, i ^ m << shift) for i in range(devices)])]
    pallas_call x2, Pallas kernels: 9.62 us -> 8.89 us  [list_product(): pl.pallas_call(functools.partial(list_kernel, width, rows, counts, split,...]
    unnamed x38 -> x40, local copies, waits for them, and re-layouts: 1.64 us -> 1.94 us
where the time goes in v23:
time: 65.5 us; the launch traced here: 65.3 us
  waiting for transfers between devices  21.9 us (33%)
  starting transfers between devices  21.8 us (33%)
  Pallas kernels  8.89 us (14%)
  local copies, waits for them, and re-layouts  5.8 us (9%)
  other arithmetic  4.52 us (7%)
  between operations  1.8 us (3%)
    ppermute x1, waiting for transfers between devices, gather_pieces(): out2 = lax.ppermute(inner1, 'row', outward)  9.69 us
    pallas_call x2, Pallas kernels, list_product(): pl.pallas_call(functools.partial(list_kernel, width, rows, counts, split,...  8.89 us
    ppermute x6, starting transfers between devices, sum_over_rows(): lax.ppermute(value, 'row', [(i, i ^ m << shift) for i in range(devices)])  8.73 us
    ppermute x6, waiting for transfers between devices, sum_over_rows(): lax.ppermute(value, 'row', [(i, i ^ m << shift) for i in range(devices)])  5.23 us
    ppermute x1, waiting for transfers between devices, gather_pieces(): across4 = lax.ppermute(last, 'row', across)  4.39 us
    ppermute x1, starting transfers between devices, gather_pieces(): swap1 = lax.ppermute(packed, 'row', pairs_swap)  3.09 us
    ppermute x1, waiting for transfers between devices, gather_pieces(): swap1 = lax.ppermute(packed, 'row', pairs_swap)  2.6 us
    unnamed x40, local copies, waits for them, and re-layouts  1.94 us
  transfers between devices with their start and end apart: 19, of which 7 were waited for; matrix products, arithmetic and copies ran while one was open for 8% of the time, Pallas kernels for 9%

profile of v23, /device:TPU:0, one launch (start us, length us, event | category | flops | bytes accessed | tf_op | source)
XLA Modules:
  0.0 65.3 jit_solution(13393606074052787476)
XLA Ops:
  0.7 0.7 %convert.8 = bf16[4,2]{0,1:T(2,128)(2,1)S(1)} convert(s32[4,2]{0,1:T(2,128)} %param.14) | non-fusion elementwise | flops 8 | bytes 48 | tf_op jit(solution)/shard_map/convert.3
  1.4 0.1 copy.26
  2.3 0.5 collective-permute-start
  2.8 0.8 %pad_maximum_fusion.1 = f32[17,512]{1,0:T(8,128)S(1)} fusion(f32[1,512]{1,0:T(1,128)S(1)} %bitcast.62, f32[16,512]{1,0:T(8,128)} %param.11), kind=kLoop, calls=%fused_computation.19 | loop fusion | flops 8704 | bytes 69632 | tf_op jit(solution)/shard_map/concatenate | solution.py:250
  3.9 0.5 copy-done.12
  4.4 0.1 fusion.25
  4.6 0.1 stack.54
  4.8 3.1 %collective-permute-start.1 = (bf16[216,512]{1,0:T(8,128)(2,1)S(1)}, bf16[216,512]{1,0:T(8,128)(2,1)S(1)}, u32[]{:S(2)}, u32[]{:S(2)}) collective-permute-start(bf16[216,512]{1,0:T(8,128)(2,1)S(1)} %fusion.6.refs_0_), channel_id=1, source_target_pairs={{0,4},{1,5},{2,6},{3,7},{4,0},{5,1},{6,2},{7,3},{8,12},{9,13},{10,... | collective-permute-start | bytes 663560 | tf_op jit(solution)/shard_map/ppermute | solution.py:161
  7.9 0.7 %collective-permute-start.2 = (bf16[216,512]{1,0:T(8,128)(2,1)S(1)}, bf16[216,512]{1,0:T(8,128)(2,1)S(1)}, u32[]{:S(2)}, u32[]{:S(2)}) collective-permute-start(bf16[216,512]{1,0:T(8,128)(2,1)S(1)} %fusion.6.refs_0_), channel_id=1, source_target_pairs={{4,8},{5,9},{6,10},{7,11},{8,4},{9,5},{10,6},{11,7},{20,24},{21,25... | collective-permute-start | bytes 663560 | tf_op jit(solution)/shard_map/ppermute | solution.py:162
  8.7 1.6 %collective-permute-start.3 = (bf16[216,512]{1,0:T(8,128)(2,1)S(1)}, bf16[216,512]{1,0:T(8,128)(2,1)S(1)}, u32[]{:S(2)}, u32[]{:S(2)}) collective-permute-start(bf16[216,512]{1,0:T(8,128)(2,1)S(1)} %fusion.6.refs_0_), channel_id=1, source_target_pairs={{0,2},{1,3},{2,0},{3,1},{4,6},{5,7},{6,4},{7,5},{8,10},{9,11},{10,... | collective-permute-start | bytes 663560 | tf_op jit(solution)/shard_map/ppermute | solution.py:163
  10.3 0.6 copy-done.9
  10.9 2.6 %collective-permute-done.1.refs_1_ = bf16[216,512]{1,0:T(8,128)(2,1)S(1)} collective-permute-done((bf16[216,512]{1,0:T(8,128)(2,1)S(1)}, bf16[216,512]{1,0:T(8,128)(2,1)S(1)}, u32[]{:S(2)}, u32[]{:S(2)}) %collective-permute-start.1) | collective-permute-done | bytes 221216 | tf_op jit(solution)/shard_map/ppermute | solution.py:161
  13.5 0.7 %collective-permute-start.4 = (bf16[216,512]{1,0:T(8,128)(2,1)S(1)}, bf16[216,512]{1,0:T(8,128)(2,1)S(1)}, u32[]{:S(2)}, u32[]{:S(2)}) collective-permute-start(bf16[216,512]{1,0:T(8,128)(2,1)S(1)} %collective-permute-done.1.refs_1_), channel_id=1, source_target_pairs={{4,8},{5,9},{6,10},{7,11},{8,4},{9,5},{10,6},{11,7},{20,24},{21,25... | collective-permute-start | bytes 663560 | tf_op jit(solution)/shard_map/ppermute | solution.py:165
  14.2 1.7 %collective-permute-start.6 = (bf16[216,512]{1,0:T(8,128)(2,1)S(1)}, bf16[216,512]{1,0:T(8,128)(2,1)S(1)}, u32[]{:S(2)}, u32[]{:S(2)}) collective-permute-start(bf16[216,512]{1,0:T(8,128)(2,1)S(1)} %collective-permute-done.1.refs_1_), channel_id=1, source_target_pairs={{0,2},{1,3},{2,0},{3,1},{4,6},{5,7},{6,4},{7,5},{8,10},{9,11},{10,... | collective-permute-start | bytes 663560 | tf_op jit(solution)/shard_map/ppermute | solution.py:167
  16.0 0.1 multiply_reduce_fusion
  16.2 1.3 %collective-permute-start.5 = (bf16[216,512]{1,0:T(8,128)(2,1)S(1)}, bf16[216,512]{1,0:T(8,128)(2,1)S(1)}, u32[]{:S(2)}, u32[]{:S(2)}) collective-permute-start(bf16[216,512]{1,0:T(8,128)(2,1)S(1)} %collective-permute-done.2.refs_2_), channel_id=1, source_target_pairs={{4,0},{5,1},{6,2},{7,3},{8,12},{9,13},{10,14},{11,15},{20,16},{21,... | collective-permute-start | bytes 663560 | tf_op jit(solution)/shard_map/ppermute | solution.py:166
  17.5 1.0 %copy.27.xo_ref = bf16[1024,192]{1,0:T(8,128)(2,1)} copy(bf16[1024,192]{0,1:T(8,128)(2,1)S(1)} %multiply_bitcast_fusion) | data formatting | bytes 786432 | tf_op jit(solution)/shard_map/transpose | solution.py:259
  18.5 0.7 %maximum_maximum_fusion.terms_ref = f32[8,1024]{1,0:T(8,128)} fusion(f32[1,1024]{1,0:T(1,128)S(1)} %fusion.16, f32[1,1024]{1,0:T(1,128)S(1)} %bitcast.63, f32[8]{0:T(128)S(1)} %pad.18.clone), kind=kLoop, calls=%fused_computation.24 | loop fusion | flops 16384 | bytes 40992 | tf_op jit(solution)/shard_map/concatenate | solution.py:96
  19.2 9.7 %collective-permute-done.5.refs_5_ = bf16[216,512]{1,0:T(8,128)(2,1)S(1)} collective-permute-done((bf16[216,512]{1,0:T(8,128)(2,1)S(1)}, bf16[216,512]{1,0:T(8,128)(2,1)S(1)}, u32[]{:S(2)}, u32[]{:S(2)}) %collective-permute-start.5) | collective-permute-done | bytes 221216 | tf_op jit(solution)/shard_map/ppermute | solution.py:166
  29.0 0.6 collective-permute-start.8
  29.6 1.3 %collective-permute-start.7 = (bf16[216,512]{1,0:T(8,128)(2,1)S(1)}, bf16[216,512]{1,0:T(8,128)(2,1)S(1)}, u32[]{:S(2)}, u32[]{:S(2)}) collective-permute-start(bf16[216,512]{1,0:T(8,128)(2,1)S(1)} %collective-permute-done.4.refs_4_), channel_id=1, source_target_pairs={{4,0},{5,1},{6,2},{7,3},{8,12},{9,13},{10,14},{11,15},{20,16},{21,... | collective-permute-start | bytes 663560 | tf_op jit(solution)/shard_map/ppermute | solution.py:168
  30.9 0.6 broadcast_13_flag_ref.2.flag_ref
  31.6 6.0 %shard_map.95 = f32[7,16,1024]{2,1,0:T(8,128)} custom-call(s32[7]{0:T(128)} %broadcast_13_flag_ref.2.flag_ref, bf16[1024,192]{1,0:T(8,128)(2,1)} %copy.27.xo_ref, f32[8,1024]{1,0:T(8,128)} %maximum_maximum_fusion.terms_ref, bf16[216,512]{1,0:T(8,128)(2,1)} %copy-done.8, bf16[216,512]{1,0:T(8,128)(2,1)} %copy-done.14, bf16[216,512]{1,0:T(8,128)(2,1)} %copy-done.4, ...), custom_call_target="tpu_custom_call" | custom-call | flops 1526726656 | bytes 2007040 | tf_op jit(solution)/shard_map/pallas_call | solution.py:106
  37.6 0.7 %slice_bitcast_fusion.3 = bf16[1,18]{1,0:T(2,128)(2,1)S(1)} fusion(bf16[1,216,512]{2,1,0:T(8,128)(2,1)} %bitcast.70), kind=kLoop, calls=%fused_computation.50 | loop fusion | bytes 72 | tf_op jit(solution)/shard_map/squeeze | solution.py:270
  38.4 1.6 %collective-permute-start.10 = (bf16[216,512]{1,0:T(8,128)(2,1)S(1)}, bf16[216,512]{1,0:T(8,128)(2,1)S(1)}, u32[]{:S(2)}, u32[]{:S(2)}) collective-permute-start(bf16[216,512]{1,0:T(8,128)(2,1)S(1)} %broadcast_select_fusion), channel_id=1, source_target_pairs={{0,2},{1,3},{2,0},{3,1},{4,6},{5,7},{6,4},{7,5},{8,10},{9,11},{10,... | collective-permute-start | bytes 663560 | tf_op jit(solution)/shard_map/ppermute | solution.py:177
  40.0 4.4 %collective-permute-done.10.refs_2_ = bf16[216,512]{1,0:T(8,128)(2,1)S(1)} collective-permute-done((bf16[216,512]{1,0:T(8,128)(2,1)S(1)}, bf16[216,512]{1,0:T(8,128)(2,1)S(1)}, u32[]{:S(2)}, u32[]{:S(2)}) %collective-permute-start.10) | collective-permute-done | bytes 221216 | tf_op jit(solution)/shard_map/ppermute | solution.py:177
  44.6 0.2 slice_reduce_fusion
  44.8 0.1 copy.29
  44.9 0.1 broadcast_in_dim_reshape_squeeze.4
  45.0 0.1 copy.30
  45.1 0.1 eq.128
  45.3 0.1 lt.26
  45.4 0.2 and_reduce_fusion
  45.7 0.1 select_reduce_fusion
  45.8 0.4 copy-done.19
  46.1 2.9 %shard_map.96 = f32[16,1024]{1,0:T(8,128)} custom-call(s32[10]{0:T(128)} %copy-done.19, bf16[1024,192]{1,0:T(8,128)(2,1)} %copy.27.xo_ref, f32[8,1024]{1,0:T(8,128)} %maximum_maximum_fusion.terms_ref, bf16[216,512]{1,0:T(8,128)(2,1)} %copy-done.5, bf16[216,512]{1,0:T(8,128)(2,1)} %copy-done.15, bf16[216,512]{1,0:T(8,128)(2,1)} %copy-done.17), custom_call_target="tpu_custom_call" | custom-call | flops 654311424 | bytes 729088 | tf_op jit(solution)/shard_map/pallas_call | solution.py:106
  49.0 0.9 %add.67 = f32[16,1024]{1,0:T(8,128)S(1)} add(f32[16,1024]{1,0:T(8,128)} %shard_map.96, f32[16,1024]{1,0:T(8,128)S(1)} %select_reduce_fusion) | non-fusion elementwise | flops 16384 | bytes 196608 | tf_op jit(solution)/shard_map/add | solution.py:292
  49.8 0.2 fusion.7
  50.0 2.3 %collective-permute-start.14 = (f32[16,16]{1,0:T(8,128)S(1)}, f32[16,16]{1,0:T(8,128)S(1)}, u32[]{:S(2)}, u32[]{:S(2)}) collective-permute-start(f32[16,16]{1,0:T(8,128)S(1)} %fusion.7), channel_id=1, source_target_pairs={{0,2},{1,3},{2,0},{3,1},{4,6},{5,7},{6,4},{7,5},{8,10},{9,11},{10,... | collective-permute-start | bytes 3080 | tf_op jit(solution)/shard_map/ppermute | solution.py:208
  52.4 0.7 %collective-permute-done.13 = f32[16,16]{1,0:T(8,128)S(1)} collective-permute-done((f32[16,16]{1,0:T(8,128)S(1)}, f32[16,16]{1,0:T(8,128)S(1)}, u32[]{:S(2)}, u32[]{:S(2)}) %collective-permute-start.13) | collective-permute-done | bytes 1056 | tf_op jit(solution)/shard_map/ppermute | solution.py:208
  53.1 0.9 %collective-permute-done.14 = f32[16,16]{1,0:T(8,128)S(1)} collective-permute-done((f32[16,16]{1,0:T(8,128)S(1)}, f32[16,16]{1,0:T(8,128)S(1)}, u32[]{:S(2)}, u32[]{:S(2)}) %collective-permute-start.14) | collective-permute-done | bytes 1056 | tf_op jit(solution)/shard_map/ppermute | solution.py:208
  54.0 2.7 %collective-permute-start.16 = (f32[16,16]{1,0:T(8,128)S(1)}, f32[16,16]{1,0:T(8,128)S(1)}, u32[]{:S(2)}, u32[]{:S(2)}) collective-permute-start(f32[16,16]{1,0:T(8,128)S(1)} %select_add_fusion), channel_id=1, source_target_pairs={{0,12},{1,13},{2,14},{3,15},{4,8},{5,9},{6,10},{7,11},{8,4},{9,5},... | collective-permute-start | bytes 3080 | tf_op jit(solution)/shard_map/ppermute | solution.py:208
  56.8 3.6 %collective-permute-start.17 = (f32[16,16]{1,0:T(8,128)S(1)}, f32[16,16]{1,0:T(8,128)S(1)}, u32[]{:S(2)}, u32[]{:S(2)}) collective-permute-start(f32[16,16]{1,0:T(8,128)S(1)} %select_add_fusion), channel_id=1, source_target_pairs={{0,8},{1,9},{2,10},{3,11},{4,12},{5,13},{6,14},{7,15},{8,0},{9,1},... | collective-permute-start | bytes 3080 | tf_op jit(solution)/shard_map/ppermute | solution.py:208
  60.4 1.7 %collective-permute-done.17 = f32[16,16]{1,0:T(8,128)S(1)} collective-permute-done((f32[16,16]{1,0:T(8,128)S(1)}, f32[16,16]{1,0:T(8,128)S(1)}, u32[]{:S(2)}, u32[]{:S(2)}) %collective-permute-start.17) | collective-permute-done | bytes 1056 | tf_op jit(solution)/shard_map/ppermute | solution.py:208
  62.1 1.9 %collective-permute-done.18 = f32[16,16]{1,0:T(8,128)S(1)} collective-permute-done((f32[16,16]{1,0:T(8,128)S(1)}, f32[16,16]{1,0:T(8,128)S(1)}, u32[]{:S(2)}, u32[]{:S(2)}) %collective-permute-start.18) | collective-permute-done | bytes 1056 | tf_op jit(solution)/shard_map/ppermute | solution.py:208
  64.0 0.2 fusion.24
  64.3 0.4 copy-done.10
  64.6 0.6 fusion.14
  (99 shorter events, 1.5 us)
Async XLA Ops:
  0.6 3.3 %copy-start = (f32[16,512]{1,0:T(8,128)S(1)}, f32[16,512]{1,0:T(8,128)}, u32[]{:S(2)}) copy-start(f32[16,512]{1,0:T(8,128)} %param.12) | copy-start | bytes 98308
  0.6 2.1 %copy-start.11 = (f32[512]{0:T(512)S(1)}, f32[512]{0:T(512)}, u32[]{:S(2)}) copy-start(f32[512]{0:T(512)} %param.10) | copy-start | bytes 6148
  1.4 2.2 %copy-start.2 = (f32[16,512]{1,0:T(8,128)S(1)}, f32[16,512]{1,0:T(8,128)}, u32[]{:S(2)}) copy-start(f32[16,512]{1,0:T(8,128)} %param.11) | copy-start | bytes 98308
  1.4 2.3 %copy-start.13 = (bf16[512]{0:T(512)(128)(2,1)S(1)}, bf16[512]{0:T(512)(128)(2,1)}, u32[]{:S(2)}) copy-start(bf16[512]{0:T(512)(128)(2,1)} %param.9) | copy-start | bytes 3076
  1.5 3.3 %copy-start.1 = (bf16[192,512]{1,0:T(8,128)(2,1)S(1)}, bf16[192,512]{1,0:T(8,128)(2,1)}, u32[]{:S(2)}) copy-start(bf16[192,512]{1,0:T(8,128)(2,1)} %param.8) | copy-start | bytes 589828
  2.3 2.4 %collective-permute-start = (bf16[9]{0:T(256)(128)(2,1)S(1)}, bf16[9]{0:T(256)(128)(2,1)S(1)}, u32[]{:S(2)}, u32[]{:S(2)}) collective-permute-start(bf16[9]{0:T(256)(128)(2,1)S(1)} %pad_maximum_fusion.2), channel_id=1, source_target_pairs={{0,1},{1,0},{2,3},{3,2},{4,5},{5,4},{6,7},{7,6},{8,9},{9,8},{10,11... | collective-permute-start | bytes 62 | tf_op jit(solution)/shard_map/ppermute | solution.py:240
  3.5 6.7 %collective-permute-start.12 = (f32[17,512]{1,0:T(8,128)S(1)}, f32[17,512]{1,0:T(8,128)S(1)}, u32[]{:S(2)}, u32[]{:S(2)}) collective-permute-start(f32[17,512]{1,0:T(8,128)S(1)} %pad_maximum_fusion.1), channel_id=1, source_target_pairs={{0,1},{1,0},{2,3},{3,2},{4,5},{5,4},{6,7},{7,6},{8,9},{9,8},{10,11... | collective-permute-start | bytes 104456 | tf_op jit(solution)/shard_map/ppermute | solution.py:249
  3.7 0.7 %copy-start.12 = (f32[16,16]{1,0:T(8,128)S(1)}, f32[16,16]{1,0:T(8,128)}, u32[]{:S(2)}) copy-start(f32[16,16]{1,0:T(8,128)} %param.13) | copy-start | bytes 3076
  4.8 5.5 %copy-start.8 = (bf16[216,512]{1,0:T(8,128)(2,1)}, bf16[216,512]{1,0:T(8,128)(2,1)S(1)}, u32[]{:S(2)}) copy-start(bf16[216,512]{1,0:T(8,128)(2,1)S(1)} %fusion.6.refs_0_) | copy-start | bytes 663556
  4.8 8.7 %collective-permute-start.1 = (bf16[216,512]{1,0:T(8,128)(2,1)S(1)}, bf16[216,512]{1,0:T(8,128)(2,1)S(1)}, u32[]{:S(2)}, u32[]{:S(2)}) collective-permute-start(bf16[216,512]{1,0:T(8,128)(2,1)S(1)} %fusion.6.refs_0_), channel_id=1, source_target_pairs={{0,4},{1,5},{2,6},{3,7},{4,0},{5,1},{6,2},{7,3},{8,12},{9,13},{10,... | collective-permute-start | bytes 663560 | tf_op jit(solution)/shard_map/ppermute | solution.py:161
  7.9 5.6 %collective-permute-start.2 = (bf16[216,512]{1,0:T(8,128)(2,1)S(1)}, bf16[216,512]{1,0:T(8,128)(2,1)S(1)}, u32[]{:S(2)}, u32[]{:S(2)}) collective-permute-start(bf16[216,512]{1,0:T(8,128)(2,1)S(1)} %fusion.6.refs_0_), channel_id=1, source_target_pairs={{4,8},{5,9},{6,10},{7,11},{8,4},{9,5},{10,6},{11,7},{20,24},{21,25... | collective-permute-start | bytes 663560 | tf_op jit(solution)/shard_map/ppermute | solution.py:162
  8.6 7.4 %collective-permute-start.9 = (bf16[216,512]{1,0:T(8,128)(2,1)S(1)}, bf16[216,512]{1,0:T(8,128)(2,1)S(1)}, u32[]{:S(2)}, u32[]{:S(2)}) collective-permute-start(bf16[216,512]{1,0:T(8,128)(2,1)S(1)} %fusion.6.refs_0_), channel_id=1, source_target_pairs={{0,1},{1,0},{2,3},{3,2},{4,5},{5,4},{6,7},{7,6},{8,9},{9,8},{10,11... | collective-permute-start | bytes 663560 | tf_op jit(solution)/shard_map/ppermute | solution.py:248
  8.7 10.6 %collective-permute-start.3 = (bf16[216,512]{1,0:T(8,128)(2,1)S(1)}, bf16[216,512]{1,0:T(8,128)(2,1)S(1)}, u32[]{:S(2)}, u32[]{:S(2)}) collective-permute-start(bf16[216,512]{1,0:T(8,128)(2,1)S(1)} %fusion.6.refs_0_), channel_id=1, source_target_pairs={{0,2},{1,3},{2,0},{3,1},{4,6},{5,7},{6,4},{7,5},{8,10},{9,11},{10,... | collective-permute-start | bytes 663560 | tf_op jit(solution)/shard_map/ppermute | solution.py:163
  10.3 0.6 copy-start.9
  13.5 5.7 %copy-start.14 = (bf16[216,512]{1,0:T(8,128)(2,1)}, bf16[216,512]{1,0:T(8,128)(2,1)S(1)}, u32[]{:S(2)}) copy-start(bf16[216,512]{1,0:T(8,128)(2,1)S(1)} %collective-permute-done.1.refs_1_) | copy-start | bytes 663556
  13.5 15.4 %copy-start.4 = (bf16[216,512]{1,0:T(8,128)(2,1)}, bf16[216,512]{1,0:T(8,128)(2,1)S(1)}, u32[]{:S(2)}) copy-start(bf16[216,512]{1,0:T(8,128)(2,1)S(1)} %collective-permute-done.2.refs_2_) | copy-start | bytes 663556
  13.5 16.0 %collective-permute-start.4 = (bf16[216,512]{1,0:T(8,128)(2,1)S(1)}, bf16[216,512]{1,0:T(8,128)(2,1)S(1)}, u32[]{:S(2)}, u32[]{:S(2)}) collective-permute-start(bf16[216,512]{1,0:T(8,128)(2,1)S(1)} %collective-permute-done.1.refs_1_), channel_id=1, source_target_pairs={{4,8},{5,9},{6,10},{7,11},{8,4},{9,5},{10,6},{11,7},{20,24},{21,25... | collective-permute-start | bytes 663560 | tf_op jit(solution)/shard_map/ppermute | solution.py:165
  14.2 16.7 %collective-permute-start.6 = (bf16[216,512]{1,0:T(8,128)(2,1)S(1)}, bf16[216,512]{1,0:T(8,128)(2,1)S(1)}, u32[]{:S(2)}, u32[]{:S(2)}) collective-permute-start(bf16[216,512]{1,0:T(8,128)(2,1)S(1)} %collective-permute-done.1.refs_1_), channel_id=1, source_target_pairs={{0,2},{1,3},{2,0},{3,1},{4,6},{5,7},{6,4},{7,5},{8,10},{9,11},{10,... | collective-permute-start | bytes 663560 | tf_op jit(solution)/shard_map/ppermute | solution.py:167
  16.2 12.7 %collective-permute-start.5 = (bf16[216,512]{1,0:T(8,128)(2,1)S(1)}, bf16[216,512]{1,0:T(8,128)(2,1)S(1)}, u32[]{:S(2)}, u32[]{:S(2)}) collective-permute-start(bf16[216,512]{1,0:T(8,128)(2,1)S(1)} %collective-permute-done.2.refs_2_), channel_id=1, source_target_pairs={{4,0},{5,1},{6,2},{7,3},{8,12},{9,13},{10,14},{11,15},{20,16},{21,... | collective-permute-start | bytes 663560 | tf_op jit(solution)/shard_map/ppermute | solution.py:166
  19.2 9.7 %copy-start.16 = (bf16[216,512]{1,0:T(8,128)(2,1)}, bf16[216,512]{1,0:T(8,128)(2,1)S(1)}, u32[]{:S(2)}) copy-start(bf16[216,512]{1,0:T(8,128)(2,1)S(1)} %collective-permute-done.3.refs_3_) | copy-start | bytes 663556
  28.9 1.9 %copy-start.7 = (bf16[216,512]{1,0:T(8,128)(2,1)}, bf16[216,512]{1,0:T(8,128)(2,1)S(1)}, u32[]{:S(2)}) copy-start(bf16[216,512]{1,0:T(8,128)(2,1)S(1)} %collective-permute-done.5.refs_5_) | copy-start | bytes 663556
  29.0 11.0 %collective-permute-start.8 = (bf16[216,512]{1,0:T(8,128)(2,1)S(1)}, bf16[216,512]{1,0:T(8,128)(2,1)S(1)}, u32[]{:S(2)}, u32[]{:S(2)}) collective-permute-start(bf16[216,512]{1,0:T(8,128)(2,1)S(1)} %broadcast_select_fusion.1), channel_id=1, source_target_pairs={{0,2},{1,3},{2,0},{3,1},{4,6},{5,7},{6,4},{7,5},{8,10},{9,11},{10,... | collective-permute-start | bytes 663560 | tf_op jit(solution)/shard_map/ppermute | solution.py:169
  29.6 2.0 %copy-start.6 = (bf16[216,512]{1,0:T(8,128)(2,1)}, bf16[216,512]{1,0:T(8,128)(2,1)S(1)}, u32[]{:S(2)}) copy-start(bf16[216,512]{1,0:T(8,128)(2,1)S(1)} %collective-permute-done.4.refs_4_) | copy-start | bytes 663556
  29.6 8.8 %collective-permute-start.7 = (bf16[216,512]{1,0:T(8,128)(2,1)S(1)}, bf16[216,512]{1,0:T(8,128)(2,1)S(1)}, u32[]{:S(2)}, u32[]{:S(2)}) collective-permute-start(bf16[216,512]{1,0:T(8,128)(2,1)S(1)} %collective-permute-done.4.refs_4_), channel_id=1, source_target_pairs={{4,0},{5,1},{6,2},{7,3},{8,12},{9,13},{10,14},{11,15},{20,16},{21,... | collective-permute-start | bytes 663560 | tf_op jit(solution)/shard_map/ppermute | solution.py:168
  30.9 0.7 %copy-start.18 = (bf16[216,512]{1,0:T(8,128)(2,1)}, bf16[216,512]{1,0:T(8,128)(2,1)S(1)}, u32[]{:S(2)}) copy-start(bf16[216,512]{1,0:T(8,128)(2,1)S(1)} %collective-permute-done.6.refs_6_) | copy-start | bytes 663556
  37.6 8.0 %copy-start.3 = (f32[7,16,1024]{2,1,0:T(8,128)S(1)}, f32[7,16,1024]{2,1,0:T(8,128)}, u32[]{:S(2)}) copy-start(f32[7,16,1024]{2,1,0:T(8,128)} %shard_map.95) | copy-start | bytes 1376260
  38.4 1.6 %copy-start.5 = (bf16[216,512]{1,0:T(8,128)(2,1)}, bf16[216,512]{1,0:T(8,128)(2,1)S(1)}, u32[]{:S(2)}) copy-start(bf16[216,512]{1,0:T(8,128)(2,1)S(1)} %collective-permute-done.7.refs_0_) | copy-start | bytes 663556
  38.4 6.0 %collective-permute-start.10 = (bf16[216,512]{1,0:T(8,128)(2,1)S(1)}, bf16[216,512]{1,0:T(8,128)(2,1)S(1)}, u32[]{:S(2)}, u32[]{:S(2)}) collective-permute-start(bf16[216,512]{1,0:T(8,128)(2,1)S(1)} %broadcast_select_fusion), channel_id=1, source_target_pairs={{0,2},{1,3},{2,0},{3,1},{4,6},{5,7},{6,4},{7,5},{8,10},{9,11},{10,... | collective-permute-start | bytes 663560 | tf_op jit(solution)/shard_map/ppermute | solution.py:177
  40.0 5.8 %copy-start.15 = (bf16[216,512]{1,0:T(8,128)(2,1)}, bf16[216,512]{1,0:T(8,128)(2,1)S(1)}, u32[]{:S(2)}) copy-start(bf16[216,512]{1,0:T(8,128)(2,1)S(1)} %collective-permute-done.8.refs_1_) | copy-start | bytes 663556
  44.4 1.4 %copy-start.17 = (bf16[216,512]{1,0:T(8,128)(2,1)}, bf16[216,512]{1,0:T(8,128)(2,1)S(1)}, u32[]{:S(2)}) copy-start(bf16[216,512]{1,0:T(8,128)(2,1)S(1)} %collective-permute-done.10.refs_2_) | copy-start | bytes 663556
  45.6 0.5 copy-start.19
  49.0 0.9 %slice-start = ((f32[17,512]{1,0:T(8,128)}), f32[16,512]{1,0:T(8,128)S(1)}, s32[]{:S(2)}) async-start(f32[17,512]{1,0:T(8,128)} %copy-done.9), calls=%async_computation | async-start | bytes 65536 | tf_op jit(solution)/shard_map/slice | solution.py:296
  50.0 3.1 %collective-permute-start.13 = (f32[16,16]{1,0:T(8,128)S(1)}, f32[16,16]{1,0:T(8,128)S(1)}, u32[]{:S(2)}, u32[]{:S(2)}) collective-permute-start(f32[16,16]{1,0:T(8,128)S(1)} %fusion.7), channel_id=1, source_target_pairs={{0,3},{1,2},{2,1},{3,0},{4,7},{5,6},{6,5},{7,4},{8,11},{9,10},{10,... | collective-permute-start | bytes 3080 | tf_op jit(solution)/shard_map/ppermute | solution.py:208
  50.0 4.0 %collective-permute-start.14 = (f32[16,16]{1,0:T(8,128)S(1)}, f32[16,16]{1,0:T(8,128)S(1)}, u32[]{:S(2)}, u32[]{:S(2)}) collective-permute-start(f32[16,16]{1,0:T(8,128)S(1)} %fusion.7), channel_id=1, source_target_pairs={{0,2},{1,3},{2,0},{3,1},{4,6},{5,7},{6,4},{7,5},{8,10},{9,11},{10,... | collective-permute-start | bytes 3080 | tf_op jit(solution)/shard_map/ppermute | solution.py:208
  52.3 1.7 %collective-permute-start.15 = (f32[16,16]{1,0:T(8,128)S(1)}, f32[16,16]{1,0:T(8,128)S(1)}, u32[]{:S(2)}, u32[]{:S(2)}) collective-permute-start(f32[16,16]{1,0:T(8,128)S(1)} %fusion.7), channel_id=1, source_target_pairs={{0,1},{1,0},{2,3},{3,2},{4,5},{5,4},{6,7},{7,6},{8,9},{9,8},{10,11... | collective-permute-start | bytes 3080 | tf_op jit(solution)/shard_map/ppermute | solution.py:208
  54.0 6.3 %collective-permute-start.16 = (f32[16,16]{1,0:T(8,128)S(1)}, f32[16,16]{1,0:T(8,128)S(1)}, u32[]{:S(2)}, u32[]{:S(2)}) collective-permute-start(f32[16,16]{1,0:T(8,128)S(1)} %select_add_fusion), channel_id=1, source_target_pairs={{0,12},{1,13},{2,14},{3,15},{4,8},{5,9},{6,10},{7,11},{8,4},{9,5},... | collective-permute-start | bytes 3080 | tf_op jit(solution)/shard_map/ppermute | solution.py:208
  56.8 5.3 %collective-permute-start.17 = (f32[16,16]{1,0:T(8,128)S(1)}, f32[16,16]{1,0:T(8,128)S(1)}, u32[]{:S(2)}, u32[]{:S(2)}) collective-permute-start(f32[16,16]{1,0:T(8,128)S(1)} %select_add_fusion), channel_id=1, source_target_pairs={{0,8},{1,9},{2,10},{3,11},{4,12},{5,13},{6,14},{7,15},{8,0},{9,1},... | collective-permute-start | bytes 3080 | tf_op jit(solution)/shard_map/ppermute | solution.py:208
  60.4 3.7 %collective-permute-start.18 = (f32[16,16]{1,0:T(8,128)S(1)}, f32[16,16]{1,0:T(8,128)S(1)}, u32[]{:S(2)}, u32[]{:S(2)}) collective-permute-start(f32[16,16]{1,0:T(8,128)S(1)} %select_add_fusion), channel_id=1, source_target_pairs={{0,4},{1,5},{2,6},{3,7},{4,0},{5,1},{6,2},{7,3},{8,12},{9,13},{10,... | collective-permute-start | bytes 3080 | tf_op jit(solution)/shard_map/ppermute | solution.py:208
  60.4 4.3 %collective-permute-start.11 = (f32[16,512]{1,0:T(8,128)S(1)}, f32[16,512]{1,0:T(8,128)S(1)}, u32[]{:S(2)}, u32[]{:S(2)}) collective-permute-start(f32[16,512]{1,0:T(8,128)S(1)} %slice.101), channel_id=1, source_target_pairs={{0,1},{1,0},{2,3},{3,2},{4,5},{5,4},{6,7},{7,6},{8,9},{9,8},{10,11... | collective-permute-start | bytes 98312 | tf_op jit(solution)/shard_map/ppermute | solution.py:302
  64.0 0.6 copy-start.10
